TPU v7x, 32 devices: a whole 2x2x4 slice. The times are simulated.
32 devices in a mesh: band: 8 (over z, core), col: 4 (over y, x).
Axes of the slice: x: 2, y: 2, z: 4, core: 2. Of those that a mesh axis runs over, the one named last changes fastest.
Arguments:
- cells: bfloat16 [32, 256, 768], P('band', 'col'), may hold values from -25 to 25
- summary: bfloat16 [8, 256, 768], P('band', 'col'), may hold values from -6 to 6
- owner: int32 [4], P('col'), may hold values from 0 to 7
- schema: int32 [32, 256], P('band', 'col'), may hold values from 0 to 15
- w_qkv: bfloat16 [768, 2304], replicated, may hold values from -0.21875 to 0.21875
- w_out: bfloat16 [768, 768], replicated, may hold values from -0.625 to 0.625
- gain_attn: float32 [768], replicated, may hold values from 0.5 to 1.5
- w_up: bfloat16 [768, 3072], replicated, may hold values from -0.21875 to 0.21875
- w_down: bfloat16 [3072, 768], replicated, may hold values from -0.109375 to 0.109375
- gain_ffn: float32 [768], replicated, may hold values from 0.5 to 1.5
Outputs:
- cells_out: bfloat16 [32, 256, 768], P('band', 'col')
- summary_out: bfloat16 [256, 768], P('col')
Inputs may be any that keep to these rules, and one draw needn't show every extreme that they name: `owner`: each entry names the band whose summary tokens its column group reads. `schema`: bit g of an entry allows the cell to attend to the row's cells of column group g; the cell's own group is allowed whatever the bits.
All inputs are finite; a program needn't handle non-finite values.
Results may differ from a plain program's by a relative error of at most 0.019.
Values may be sent and summed in bfloat16 or wider, within the bound.
No kernel may reach another device: no remote copies, remote signals or barrier semaphores. Data moves between devices by JAX's collectives and lax.ppermute only.
A program may use at most 128 MiB of HBM per device.

v0:
```python
import jax
import jax.numpy as jnp
from jax import lax
from jax.sharding import PartitionSpec as P

HEADS = 12
HEAD_DIM = 64


def spread_2(value, axis, source):
    kept = jnp.where(lax.axis_index(axis) == source, value, 0).astype(value.dtype)
    return lax.psum(kept, axis)


def layer_norm(values, gain_vec):
    center = values - jnp.mean(values, -1, keepdims=True)
    spread = jnp.mean(center * center, -1, keepdims=True)
    return center * lax.rsqrt(spread + 1e-05) * gain_vec


def finish(tokens_in, attended, w_out, gain_attn, w_up, w_down, gain_ffn):
    mixed_out = jnp.dot(attended, w_out, preferred_element_type=jnp.float32)
    hidden = layer_norm(tokens_in.astype(jnp.float32) + mixed_out, gain_attn).astype(jnp.bfloat16)
    inner_act = jax.nn.gelu(jnp.dot(hidden, w_up, preferred_element_type=jnp.float32)).astype(
        jnp.bfloat16
    )
    outer_out = jnp.dot(inner_act, w_down, preferred_element_type=jnp.float32)
    return layer_norm(hidden.astype(jnp.float32) + outer_out, gain_ffn).astype(jnp.bfloat16)


def project(values, weight):
    return jnp.dot(values, weight, preferred_element_type=jnp.float32).astype(jnp.bfloat16)


def empty_state(dims_of):
    return (
        jnp.full(dims_of, -1e30, jnp.float32),
        jnp.zeros(dims_of, jnp.float32),
        jnp.zeros(dims_of + (HEAD_DIM,), jnp.float32),
    )


def absorb(running, scores, vals_part, pattern):
    run_top, run_total, run_accum = running
    new_top = jnp.maximum(run_top, scores.max(-1))
    fade_out = jnp.exp(run_top - new_top)
    weights = jnp.exp(scores - new_top[..., None])
    added = jnp.einsum(
        pattern, weights.astype(jnp.bfloat16), vals_part, preferred_element_type=jnp.float32
    )
    return (
        new_top,
        run_total * fade_out + weights.sum(-1),
        run_accum * fade_out[..., None] + added,
    )


def local(cells, summary, owner, schema, w_qkv, w_out, gain_attn, w_up, w_down, gain_ffn):
    row_count, cols_dev, model_width = cells.shape
    own_group = lax.axis_index("col")
    score_scale = HEAD_DIM ** (-0.5)
    flat_cells = cells.reshape(row_count * cols_dev, model_width)
    qkv_cells = project(flat_cells, w_qkv).reshape(row_count, cols_dev, 3 * model_width)
    queries = qkv_cells[:, :, :model_width].reshape(row_count, cols_dev, HEADS, HEAD_DIM)
    key_values = qkv_cells[:, :, model_width:]
    own_tokens = summary[0]
    tokens = spread_2(own_tokens, "band", owner[0])
    summary_qkv = project(tokens, w_qkv)
    sum_queries = summary_qkv[:, :model_width].reshape(cols_dev, HEADS, HEAD_DIM)
    sum_keys = summary_qkv[:, model_width : 2 * model_width].reshape(cols_dev, HEADS, HEAD_DIM)
    sum_vals = summary_qkv[:, 2 * model_width :].reshape(cols_dev, HEADS, HEAD_DIM)
    sum_scores = (
        jnp.einsum("rqhd,khd->rhqk", queries, sum_keys, preferred_element_type=jnp.float32)
        * score_scale
    )
    start_row = absorb(
        empty_state((row_count, HEADS, cols_dev)), sum_scores, sum_vals, "rhqk,khd->rhqd"
    )
    portion = lax.all_gather(key_values, "col", axis=1, tiled=True)
    width_now = portion.shape[1]
    keys_part = portion[:, :, :model_width].reshape(row_count, width_now, HEADS, HEAD_DIM)
    vals_part = portion[:, :, model_width:].reshape(row_count, width_now, HEADS, HEAD_DIM)
    key_groups = jnp.arange(width_now, dtype=jnp.int32) // cols_dev
    allowed = (jnp.right_shift(schema[:, :, None], key_groups[None, None, :]) & 1 == 1) | (
        key_groups == own_group
    )[None, None, :]
    scores = (
        jnp.einsum("rqhd,rkhd->rhqk", queries, keys_part, preferred_element_type=jnp.float32)
        * score_scale
    )
    scores = jnp.where(allowed[:, None], scores, -1e30)
    row_state = absorb(start_row, scores, vals_part, "rhqk,rkhd->rhqd")
    attended = (row_state[2] / row_state[1][..., None]).transpose(0, 2, 1, 3)
    attended = attended.reshape(row_count * cols_dev, model_width).astype(jnp.bfloat16)
    cells_out = finish(flat_cells, attended, w_out, gain_attn, w_up, w_down, gain_ffn)
    cells_out = cells_out.reshape(row_count, cols_dev, model_width)
    self_scores = (
        jnp.sum(sum_queries.astype(jnp.float32) * sum_keys.astype(jnp.float32), -1) * score_scale
    )
    self_state = (
        self_scores,
        jnp.ones((cols_dev, HEADS), jnp.float32),
        sum_vals.astype(jnp.float32),
    )
    portion = lax.all_gather(key_values, "band", axis=0, tiled=True)
    depth_now = portion.shape[0]
    keys_part = portion[:, :, :model_width].reshape(depth_now, cols_dev, HEADS, HEAD_DIM)
    vals_part = portion[:, :, model_width:].reshape(depth_now, cols_dev, HEADS, HEAD_DIM)
    scores = (
        jnp.einsum("jhd,rjhd->jhr", sum_queries, keys_part, preferred_element_type=jnp.float32)
        * score_scale
    )
    column_state = absorb(self_state, scores, vals_part, "jhr,rjhd->jhd")
    summary_att = (
        (column_state[2] / column_state[1][..., None])
        .reshape(cols_dev, model_width)
        .astype(jnp.bfloat16)
    )
    summary_out = finish(tokens, summary_att, w_out, gain_attn, w_up, w_down, gain_ffn)
    return (cells_out, summary_out)


def solution(mesh):
    in_specs = (
        P("band", "col", None),
        P("band", "col", None),
        P("col"),
        P("band", "col"),
        P(),
        P(),
        P(),
        P(),
        P(),
        P(),
    )
    out_specs = (P("band", "col", None), P("col", None))
    return jax.shard_map(local, mesh=mesh, in_specs=in_specs, out_specs=out_specs, check_vma=False)
```

profile of v0, /device:TPU:0, one launch (start us, length us, event | category | flops | bytes accessed | tf_op | source)
XLA Modules:
  0.0 193.0 jit_solution(19137682196019115)
XLA Ops:
  8.0 0.0 copy-start
  8.0 0.0 all-reduce.2.cloned.1.call-start
  8.9 0.7 select_bitcast_fusion
  9.5 0.0 all-reduce.2.cloned.1.call-update
  9.5 0.0 all-gather.3.cloned.1.call-start
  9.6 0.5 copy-done
  10.1 2.1 %convolution_convert_fusion = bf16[256,2304]{1,0:T(8,128)(2,1)S(1)} fusion(bf16[256,768]{1,0:T(8,128)(2,1)} %bitcast.97, bf16[768,2304]{1,0:T(8,128)(2,1)S(1)} %copy-done), kind=kOutput, calls=%fused_computation.5 | convolution fusion | flops 906559488 | bytes 5111808 | tf_op jit(solution)/shard_map/dot_general | solution.py:32
  12.2 1.0 copy-done.8
  13.1 0.9 slice.39
  14.1 2.7 %copy.148 = bf16[4,64,1536]{2,0,1:T(4,128)(2,1)} copy(bf16[4,64,1536]{2,1,0:T(8,128)(2,1)} %slice.39) | data formatting | bytes 1572864
  16.8 0.0 all-gather.3.cloned.1.call-update
  16.8 0.0 all-gather.5.cloned.1.call-start
  16.9 0.5 all-gather.5.cloned.1.call-update
  17.4 1.8 slice.37
  19.2 2.4 %reshape.167 = bf16[4,64,12,64]{3,2,1,0:T(8,128)(2,1)} reshape(bf16[4,64,768]{2,1,0:T(8,128)(2,1)} %slice.37) | data formatting | bytes 786432 | tf_op jit(solution)/shard_map/reshape | solution.py:64
  21.6 0.8 fusion.53
  22.4 43.8 %all-reduce.2.cloned.1.call-done = bf16[64,768]{1,0:T(8,128)(2,1)} async-done(((bf16[64,768]{1,0:T(8,128)(2,1)}), bf16[64,768]{1,0:T(8,128)(2,1)}) %all-reduce.2.cloned.1.call-update) | async-done | bytes 98320 | tf_op jit(solution)/shard_map/psum | solution.py:12
  66.2 1.6 convolution_convert_fusion.1
  67.8 0.9 reshape.182
  68.8 0.2 reshape.172
  68.9 0.2 reshape.165
  69.1 0.2 reshape.168
  69.3 0.2 multiply_reduce_fusion.2
  69.5 0.1 copy.130
  69.6 2.1 %bitcast_reduce_fusion = (f32[4,12,64]{2,0,1:T(4,128)S(1)}, f32[12,64,4,64]{3,1,2,0:T(8,128)}) fusion(bf16[4,64,12,64]{3,2,1,0:T(8,128)(2,1)S(1)} %copy-done.2, bf16[64,12,64,1]{2,1,0,3:T(8,128)(2,1)S(1)} %bitcast.93), kind=kOutput, calls=%fused_computation.27 | convolution fusion | flops 25555968 | bytes 1290240 | tf_op jit(solution)/shard_map/rqhd,khd->rhqk/dot_general | solution.py:73
  71.7 3.2 %fusion.77 = (bf16[4,256,768]{2,0,1:T(4,128)(2,1)S(1)}, bf16[4,256,768]{2,0,1:T(4,128)(2,1)S(1)}) fusion(bf16[4,256,1536]{2,0,1:T(4,128)(2,1)} %all-gather.3.cloned.1.call-done), kind=kLoop, calls=%fused_computation.120 | loop fusion | bytes 6291456 | tf_op jit(solution)/shard_map/slice | solution.py:81
  74.9 0.0 copy-start.11
  74.9 2.4 %copy.149 = bf16[4,256,768]{1,2,0:T(8,128)(2,1)} copy(bf16[4,256,768]{2,0,1:T(4,128)(2,1)S(1)} %get-tuple-element.11) | data formatting | bytes 3145728
  77.3 2.4 %copy.119 = bf16[4,256,768]{1,2,0:T(8,128)(2,1)} copy(bf16[4,256,768]{2,0,1:T(4,128)(2,1)S(1)} %get-tuple-element.10) | data formatting | bytes 3145728 | tf_op jit(solution)/shard_map/slice | solution.py:81
  79.7 2.6 %fusion.12 = (f32[4,12,64]{2,1,0:T(8,128)S(1)}, f32[4,12,64,256]{3,2,1,0:T(8,128)S(1)}) fusion(pred[4,64,256]{2,1,0:T(8,128)(4,1)S(1)} %copy-done.11, bf16[4,256,12,64]{1,3,2,0:T(8,128)(2,1)} %bitcast.92, bf16[4,64,12,64]{3,2,1,0:T(8,128)(2,1)} %reshape.167), kind=kOutput, calls=%fused_computation.17 | convolution fusion | flops 103019520 | bytes 5189632 | tf_op jit(solution)/shard_map/rqhd,rkhd->rhqk/dot_general | solution.py:88
  82.3 0.4 fusion.28
  82.7 1.4 fusion.13
  84.1 0.6 fusion.21
  84.7 0.0 copy-start.12
  84.7 0.6 fusion.18
  85.3 0.0 copy-start.17
  85.3 0.6 copy.129
  86.0 0.5 convert_element_type.74
  86.5 0.6 fusion.79
  87.0 0.2 multiply_reduce_fusion.1
  87.3 6.9 %fusion.80 = (f32[256]{0:T(256)S(1)}, f32[256,768]{1,0:T(8,128)S(1)}) fusion(bf16[3072,768]{1,0:T(8,128)(2,1)} %param.18, bf16[768,3072]{1,0:T(8,128)(2,1)} %param.17, f32[256,768]{1,0:T(8,128)S(1)} %get-tuple-element.25, f32[768]{0:T(1024)S(1)} %copy-done.17, f32[256]{0:T(256)S(1)} %add_rsqrt_fusion.1, f32[256]{0:T(256)S(1)} %broadcast_multiply_fusion.1), kind=kOutput, calls=%fused_computation.123 | convolution fusion | flops 2425159424 | bytes 11016192 | tf_op jit(solution)/shard_map/dot_general | solution.py:27
  94.2 0.2 multiply_reduce_fusion
  94.5 0.9 multiply_convert_fusion
  95.4 34.3 %all-gather.5.cloned.1.call-done = bf16[32,64,1536]{2,1,0:T(8,128)(2,1)} async-done(((bf16[4,64,1536]{2,1,0:T(8,128)(2,1)}), bf16[32,64,1536]{2,1,0:T(8,128)(2,1)}) %all-gather.5.cloned.1.call-update) | async-done | bytes 6291472 | tf_op jit(solution)/shard_map/all_gather | solution.py:105
  129.7 5.3 %fusion.76 = (bf16[32,64,768]{2,1,0:T(8,128)(2,1)S(1)}, bf16[32,64,768]{2,1,0:T(8,128)(2,1)}) fusion(bf16[32,64,1536]{2,1,0:T(8,128)(2,1)} %all-gather.5.cloned.1.call-done), kind=kLoop, calls=%fused_computation.119 | loop fusion | bytes 12582912 | tf_op jit(solution)/shard_map/slice | solution.py:108
  135.1 10.6 %reshape.173 = bf16[32,64,12,64]{3,2,1,0:T(8,128)(2,1)} reshape(bf16[32,64,768]{2,1,0:T(8,128)(2,1)} %get-tuple-element.7) | data formatting | bytes 6291456 | tf_op jit(solution)/shard_map/reshape | solution.py:107
  145.7 8.0 %fusion.2 = f32[64,12,1,32]{3,2,1,0:T(1,128)} fusion(bf16[64,12,64,1]{2,3,1,0:T(2,128)(2,1)S(1)} %copy-done.13, bf16[32,64,12,64]{3,2,1,0:T(8,128)(2,1)} %reshape.173), kind=kOutput, calls=%fused_computation.2 | convolution fusion | flops 3145728 | bytes 3342336 | tf_op jit(solution)/shard_map/jhd,rjhd->jhr/dot_general | solution.py:110
  153.7 1.1 copy.140
  155.0 1.3 fusion.57
  156.2 1.1 copy.141
  157.4 7.3 %reshape.174 = bf16[32,64,12,64]{3,2,1,0:T(8,128)(2,1)} reshape(bf16[32,64,768]{2,1,0:T(8,128)(2,1)S(1)} %get-tuple-element.6) | data formatting | bytes 6291456 | tf_op jit(solution)/shard_map/reshape | solution.py:108
  164.7 0.7 fusion.74
  165.4 0.1 copy.133
  165.5 0.1 copy.132
  165.6 7.3 %fusion = f32[64,12,1,64]{3,2,1,0:T(1,128)S(1)} fusion(bf16[64,12,32,1]{2,3,1,0:T(2,128)(2,1)S(1)} %copy.141, bf16[32,64,12,64]{3,2,1,0:T(8,128)(2,1)} %reshape.174), kind=kOutput, calls=%fused_computation | convolution fusion | flops 3145728 | bytes 3391488 | tf_op jit(solution)/shard_map/jhr,rjhd->jhd/dot_general | solution.py:48
  173.0 0.3 fusion.47
  173.3 0.2 convert_element_type.85
  173.5 0.4 fusion.81
  174.0 0.7 copy-done.7
  174.6 0.2 multiply_reduce_fusion.4
  174.8 7.2 %fusion.82 = (f32[64]{0:T(128)}, f32[64,768]{1,0:T(8,128)}) fusion(bf16[3072,768]{1,0:T(8,128)(2,1)} %param.18, bf16[768,3072]{1,0:T(8,128)(2,1)} %param.17, f32[64,768]{1,0:T(8,128)} %copy-done.7, f32[768]{0:T(1024)S(1)} %copy-done.18, f32[64]{0:T(128)S(1)} %add_rsqrt_fusion.3, f32[64]{0:T(128)S(1)} %broadcast_multiply_fusion.3), kind=kOutput, calls=%fused_computation.125 | convolution fusion | flops 606289856 | bytes 9834240 | tf_op jit(solution)/shard_map/dot_general | solution.py:27
  182.1 0.7 broadcast_multiply_fusion.2
  182.7 1.1 multiply_reduce_fusion.3
  183.9 1.7 multiply_convert_fusion.2
  (49 shorter events, 0.3 us)
Async XLA Ops:
  8.0 2.1 %copy-start = (bf16[768,2304]{1,0:T(8,128)(2,1)S(1)}, bf16[768,2304]{1,0:T(8,128)(2,1)}, u32[]{:S(2)}) copy-start(bf16[768,2304]{1,0:T(8,128)(2,1)} %param.14) | copy-start | bytes 10616836
  8.0 58.1 %all-reduce.2.cloned.1.call-start = ((), (), s32[]{:S(2)}) async-start(), calls=%async_computation | async-start | bytes 196608 | tf_op jit(solution)/shard_map/psum | solution.py:12
  9.5 62.1 %all-gather.3.cloned.1.call-start = ((), (), s32[]{:S(2)}) async-start(), calls=%async_computation.1 | async-start | bytes 3932160 | tf_op jit(solution)/shard_map/all_gather | solution.py:79
  12.1 1.0 copy-start.8
  13.1 8.5 %copy-start.19 = (s32[4,64]{1,0:T(4,128)S(1)}, s32[4,64]{1,0:T(4,128)}, u32[]{:S(2)}) copy-start(s32[4,64]{1,0:T(4,128)} %param.13) | copy-start | bytes 3076
  16.8 112.9 %all-gather.5.cloned.1.call-start = ((), (), s32[]{:S(2)}) async-start(), calls=%async_computation.2 | async-start | bytes 7077888 | tf_op jit(solution)/shard_map/all_gather | solution.py:105
  67.8 1.8 copy-start.2
  69.3 15.4 %copy-start.9 = (bf16[64,12,64]{2,1,0:T(8,128)(2,1)}, bf16[64,12,64]{2,1,0:T(8,128)(2,1)S(1)}, u32[]{:S(2)}) copy-start(bf16[64,12,64]{2,1,0:T(8,128)(2,1)S(1)} %reshape.168) | copy-start | bytes 294916
  74.9 4.7 %copy-start.11 = (pred[4,64,256]{2,1,0:T(8,128)(4,1)S(1)}, pred[4,64,256]{2,1,0:T(8,128)(4,1)}, u32[]{:S(2)}) copy-start(pred[4,64,256]{2,1,0:T(8,128)(4,1)} %fusion.53) | copy-start | bytes 196612
  79.7 2.6 %copy-start.3 = (f32[12,64,4,64]{3,1,2,0:T(8,128)S(1)}, f32[12,64,4,64]{3,1,2,0:T(8,128)}, u32[]{:S(2)}) copy-start(f32[12,64,4,64]{3,1,2,0:T(8,128)} %get-tuple-element.21) | copy-start | bytes 2359300
  82.3 1.8 copy-start.4
  84.7 1.7 copy-start.5
  84.7 1.7 copy-start.12
  85.3 2.0 %copy-start.17 = (f32[768]{0:T(1024)S(1)}, f32[768]{0:T(1024)}, u32[]{:S(2)}) copy-start(f32[768]{0:T(1024)} %param.16) | copy-start | bytes 9220
  87.3 7.2 %copy-start.15 = (f32[768]{0:T(1024)S(1)}, f32[768]{0:T(1024)}, u32[]{:S(2)}) copy-start(f32[768]{0:T(1024)} %param.19) | copy-start | bytes 9220
  135.1 10.6 %copy-start.13 = (bf16[64,12,64,1]{2,3,1,0:T(2,128)(2,1)S(1)}, bf16[64,12,64,1]{2,3,1,0:T(2,128)(2,1)}, u32[]{:S(2)}) copy-start(bf16[64,12,64,1]{2,3,1,0:T(2,128)(2,1)} %reshape.182) | copy-start | bytes 294916
  165.6 7.4 %copy-start.10 = (bf16[64,12,64]{2,1,0:T(8,128)(2,1)S(1)}, bf16[64,12,64]{2,1,0:T(8,128)(2,1)}, u32[]{:S(2)}) copy-start(bf16[64,12,64]{2,1,0:T(8,128)(2,1)} %copy-done.9) | copy-start | bytes 294916
  165.6 7.9 %copy-start.6 = (bf16[768,768]{1,0:T(8,128)(2,1)S(1)}, bf16[768,768]{1,0:T(8,128)(2,1)}, u32[]{:S(2)}) copy-start(bf16[768,768]{1,0:T(8,128)(2,1)} %param.15) | copy-start | bytes 3538948
  165.6 7.9 %copy-start.14 = (bf16[64,768]{1,0:T(8,128)(2,1)S(1)}, bf16[64,768]{1,0:T(8,128)(2,1)}, u32[]{:S(2)}) copy-start(bf16[64,768]{1,0:T(8,128)(2,1)} %all-reduce.2.cloned.1.call-done) | copy-start | bytes 294916
  165.6 9.2 %copy-start.18 = (f32[768]{0:T(1024)S(1)}, f32[768]{0:T(1024)}, u32[]{:S(2)}) copy-start(f32[768]{0:T(1024)} %param.16) | copy-start | bytes 9220
  173.9 0.7 copy-start.7
  174.8 10.7 %copy-start.1 = (bf16[768,2304]{1,0:T(8,128)(2,1)S(1)}, bf16[768,2304]{1,0:T(8,128)(2,1)}, u32[]{:S(2)}) copy-start(bf16[768,2304]{1,0:T(8,128)(2,1)} %param.14) | copy-start | bytes 10616836
  174.8 9.0 %copy-start.16 = (f32[768]{0:T(1024)S(1)}, f32[768]{0:T(1024)}, u32[]{:S(2)}) copy-start(f32[768]{0:T(1024)} %param.19) | copy-start | bytes 9220
Sparse Core Ops, SparseCore 0:
  11.7 54.3 all-reduce.1
Sparse Core Ops, SparseCore 1:
  16.9 46.6 all-gather.2
  65.1 64.6 all-gather.4
where the time goes:
time: 194 us; the launch traced here: 193 us
  waiting for transfers between devices  78.7 us (41%)
  local copies, waits for them, and re-layouts  46.6 us (24%)
  matrix products  40 us (21%)
  between operations  16.7 us (9%)
  other arithmetic  10.9 us (6%)
    psum x1, waiting for transfers between devices, spread_2(): return lax.psum(kept, axis)  43.8 us
    all_gather x1, waiting for transfers between devices, local(): portion = lax.all_gather(key_values, 'band', axis=0, tiled=True)  34.3 us
    dot_general x2, matrix products, finish(): outer_out = jnp.dot(inner_act, w_down, preferred_element_type=jnp.float32)  14.1 us
    reshape x1, local copies, waits for them, and re-layouts, local(): portion[:, :, :model_width].reshape(depth_now, cols_dev, HEADS, HEAD_DIM)  10.6 us
    dot_general x3, matrix products, absorb(): jnp.einsum(pattern, weights.astype(jnp.bfloat16), vals_part, preferred_el...  8.47 us
    dot_general x1, matrix products, local(): jnp.einsum('jhd,rjhd->jhr', sum_queries, keys_part, preferred_element_typ...  8.03 us
    reshape x1, local copies, waits for them, and re-layouts, local(): portion[:, :, model_width:].reshape(depth_now, cols_dev, HEADS, HEAD_DIM)  7.32 us
    unnamed x42, local copies, waits for them, and re-layouts  7.27 us
  transfers between devices with their start and end apart: 3, of which 2 were waited for; matrix products, arithmetic and copies ran while one was open for 21% of the time, Pallas kernels for 0%

commit v1 on v0

v1 whole, which is shorter than its diff:
```python
import jax
import jax.numpy as jnp
from jax import lax
from jax.sharding import PartitionSpec as P

HEADS = 12
HEAD_DIM = 64


def spread_2(value, axis, source):
    kept = jnp.where(lax.axis_index(axis) == source, value, 0).astype(value.dtype)
    return lax.psum(kept, axis)


def layer_norm(values, gain_vec):
    center = values - jnp.mean(values, -1, keepdims=True)
    spread = jnp.mean(center * center, -1, keepdims=True)
    return center * lax.rsqrt(spread + 1e-05) * gain_vec


def finish(tokens_in, attended, w_out, gain_attn, w_up, w_down, gain_ffn):
    mixed_out = jnp.dot(attended, w_out, preferred_element_type=jnp.float32)
    hidden = layer_norm(tokens_in.astype(jnp.float32) + mixed_out, gain_attn).astype(jnp.bfloat16)
    inner_act = jax.nn.gelu(jnp.dot(hidden, w_up, preferred_element_type=jnp.float32)).astype(
        jnp.bfloat16
    )
    outer_out = jnp.dot(inner_act, w_down, preferred_element_type=jnp.float32)
    return layer_norm(hidden.astype(jnp.float32) + outer_out, gain_ffn).astype(jnp.bfloat16)


def project(values, weight):
    return jnp.dot(values, weight, preferred_element_type=jnp.float32).astype(jnp.bfloat16)


def head_sum(values):
    dims = values.shape[:-1]
    return values.reshape(dims + (HEADS, HEAD_DIM)).sum(-1)


def head_spread(values):
    dims = values.shape[:-1]
    return jnp.broadcast_to(values[..., None], dims + (HEADS, HEAD_DIM)).reshape(
        dims + (HEADS * HEAD_DIM,)
    )


def local(cells, summary, owner, schema, w_qkv, w_out, gain_attn, w_up, w_down, gain_ffn):
    row_count, cols_dev, model_width = cells.shape
    own_group = lax.axis_index("col")
    score_scale = HEAD_DIM ** (-0.5)
    flat_cells = cells.reshape(row_count * cols_dev, model_width)
    w_kv = w_qkv[:, model_width:]

    tokens = spread_2(summary[0], "band", owner[0])
    row_cells = lax.all_gather(cells, "col", axis=1, tiled=True)
    width_now = row_cells.shape[1]

    qkv_cells = project(flat_cells, w_qkv).reshape(row_count, cols_dev, 3 * model_width)
    queries = qkv_cells[:, :, :model_width]
    own_keys = qkv_cells[:, :, model_width : 2 * model_width].astype(jnp.float32)
    own_vals = qkv_cells[:, :, 2 * model_width :].astype(jnp.float32)

    summary_qkv = project(tokens, w_qkv)
    sum_queries = summary_qkv[:, :model_width]
    sum_keys = summary_qkv[:, model_width : 2 * model_width]
    sum_vals = summary_qkv[:, 2 * model_width :]

    sq = sum_queries.astype(jnp.float32)
    col_scores = head_sum(sq[None] * own_keys) * score_scale
    self_scores = head_sum(sq * sum_keys.astype(jnp.float32)) * score_scale
    col_top = jnp.maximum(lax.pmax(col_scores.max(0), "band"), self_scores)
    col_exp = jnp.exp(col_scores - col_top[None])
    self_exp = jnp.exp(self_scores - col_top)
    col_weights = head_spread(col_exp.astype(jnp.bfloat16).astype(jnp.float32))
    col_mixed = (col_weights * own_vals).sum(0)
    col_total = col_exp.sum(0)
    packed = jnp.concatenate([col_mixed, col_total], axis=-1)
    packed = lax.psum(packed, "band")
    col_mixed = packed[:, :model_width]
    col_total = packed[:, model_width:] + self_exp
    self_weights = head_spread(self_exp.astype(jnp.bfloat16).astype(jnp.float32))
    col_mixed = col_mixed + self_weights * sum_vals.astype(jnp.float32)
    summary_att = (col_mixed / head_spread(col_total)).astype(jnp.bfloat16)

    row_kv = project(row_cells.reshape(row_count * width_now, model_width), w_kv)
    row_kv = row_kv.reshape(row_count, width_now, 2 * model_width)
    q4 = queries.reshape(row_count, cols_dev, HEADS, HEAD_DIM)
    k4 = row_kv[:, :, :model_width].reshape(row_count, width_now, HEADS, HEAD_DIM)
    v4 = row_kv[:, :, model_width:].reshape(row_count, width_now, HEADS, HEAD_DIM)
    sk = sum_keys.reshape(cols_dev, HEADS, HEAD_DIM)
    sv = sum_vals.reshape(cols_dev, HEADS, HEAD_DIM)
    key_groups = jnp.arange(width_now, dtype=jnp.int32) // cols_dev
    allowed = (jnp.right_shift(schema[:, :, None], key_groups[None, None, :]) & 1 == 1) | (
        key_groups == own_group
    )[None, None, :]
    cell_scores = (
        jnp.einsum("rqhd,rkhd->rhqk", q4, k4, preferred_element_type=jnp.float32) * score_scale
    )
    cell_scores = jnp.where(allowed[:, None], cell_scores, -1e30)
    tok_scores = (
        jnp.einsum("rqhd,khd->rhqk", q4, sk, preferred_element_type=jnp.float32) * score_scale
    )
    row_top = jnp.maximum(cell_scores.max(-1), tok_scores.max(-1))
    cell_exp = jnp.exp(cell_scores - row_top[..., None])
    tok_exp = jnp.exp(tok_scores - row_top[..., None])
    row_total = cell_exp.sum(-1) + tok_exp.sum(-1)
    mixed = jnp.einsum(
        "rhqk,rkhd->rqhd", cell_exp.astype(jnp.bfloat16), v4, preferred_element_type=jnp.float32
    )
    mixed = mixed + jnp.einsum(
        "rhqk,khd->rqhd", tok_exp.astype(jnp.bfloat16), sv, preferred_element_type=jnp.float32
    )
    attended = mixed / row_total.transpose(0, 2, 1)[..., None]
    attended = attended.reshape(row_count * cols_dev, model_width).astype(jnp.bfloat16)

    all_in = jnp.concatenate([flat_cells, tokens], axis=0)
    all_att = jnp.concatenate([attended, summary_att], axis=0)
    all_out = finish(all_in, all_att, w_out, gain_attn, w_up, w_down, gain_ffn)
    cells_out = all_out[: row_count * cols_dev].reshape(row_count, cols_dev, model_width)
    summary_out = all_out[row_count * cols_dev :]
    return (cells_out, summary_out)


def solution(mesh):
    in_specs = (
        P("band", "col", None),
        P("band", "col", None),
        P("col"),
        P("band", "col"),
        P(),
        P(),
        P(),
        P(),
        P(),
        P(),
    )
    out_specs = (P("band", "col", None), P("col", None))
    return jax.shard_map(local, mesh=mesh, in_specs=in_specs, out_specs=out_specs, check_vma=False)
```

time: 194 us -> 202 us (1.041)
  blocking collectives: 0 us -> 28.4 us
  local copies, waits for them, and re-layouts: 46.6 us -> 20.1 us
  waiting for transfers between devices: 78.7 us -> 99.3 us
  matrix products: 40 us -> 25.7 us
    psum x0 -> x1, waiting for transfers between devices: none -> 45.5 us  [local(): packed = lax.psum(packed, 'band')]
    all_gather x2 -> x1, waiting for transfers between devices: 34.3 us -> 0.01 us  [local(): row_cells = lax.all_gather(cells, 'col', axis=1, tiled=True)]
    pmax x0 -> x1, blocking collectives: none -> 28.4 us  [local(): col_top = jnp.maximum(lax.pmax(col_scores.max(0), 'band'), self_scores)]
    reshape x7 -> x8, local copies, waits for them, and re-layouts: 21.8 us -> 5.82 us  [the longest x2 2.53 us: head_sum(): return values.reshape(dims + (HEADS, HEAD_DIM)).sum(-1)]
    dot_general x6 -> x4, matrix products: 21.1 us -> 5.77 us  [the longest x1 2.25 us: local(): jnp.einsum('rqhd,rkhd->rhqk', q4, k4, preferred_element_type=jnp.float32)]
    psum x1, waiting for transfers between devices: 43.8 us -> 53.3 us  [spread_2(): return lax.psum(kept, axis)]
    dot_general x2 -> x3, matrix products: 3.71 us -> 10.8 us  [project(): jnp.dot(values, weight, preferred_element_type=jnp.float32)]
    dot_general x2 -> x1, matrix products: 14.1 us -> 7.43 us  [finish(): outer_out = jnp.dot(inner_act, w_down, preferred_element_type=jnp.float32)]
  transfers between devices with their start and end apart: 3 -> 3, of which waited for: 2 -> 2; matrix products, arithmetic and copies ran while one was open for 21% -> 6% of each run, Pallas kernels for 0% -> 0%
where the time goes in v1:
time: 202 us; the launch traced here: 201 us
  waiting for transfers between devices  99.3 us (49%)
  blocking collectives  28.4 us (14%)
  matrix products  25.7 us (13%)
  local copies, waits for them, and re-layouts  20.1 us (10%)
  between operations  16.6 us (8%)
  other arithmetic  11.3 us (6%)
    psum x1, waiting for transfers between devices, spread_2(): return lax.psum(kept, axis)  53.3 us
    psum x1, waiting for transfers between devices, local(): packed = lax.psum(packed, 'band')  45.5 us
    pmax x1, blocking collectives, local(): col_top = jnp.maximum(lax.pmax(col_scores.max(0), 'band'), self_scores)  28.4 us
    dot_general x3, matrix products, project(): jnp.dot(values, weight, preferred_element_type=jnp.float32)  10.8 us
    dot_general x1, matrix products, finish(): outer_out = jnp.dot(inner_act, w_down, preferred_element_type=jnp.float32)  7.43 us
    slice x2, local copies, waits for them, and re-layouts, local(): row_kv[:, :, :model_width].reshape(row_count, width_now, HEADS, HEAD_DIM)  4.55 us
  transfers between devices with their start and end apart: 3, of which 2 were waited for; matrix products, arithmetic and copies ran while one was open for 6% of the time, Pallas kernels for 0%

profile of v1, /device:TPU:0, one launch (start us, length us, event | category | flops | bytes accessed | tf_op | source)
XLA Modules:
  0.0 201.4 jit_solution(11720248242947388714)
XLA Ops:
  8.0 0.0 copy-start
  8.0 0.0 all-reduce.3.cloned.1.call-start
  8.8 0.7 select_bitcast_fusion
  9.5 0.0 all-reduce.3.cloned.1.call-update
  9.5 0.0 all-reduce.5.cloned.1.call-start
  9.5 3.2 %convolution_convert_fusion = bf16[256,2304]{1,0:T(8,128)(2,1)S(1)} fusion(bf16[256,768]{1,0:T(8,128)(2,1)} %bitcast.54, bf16[768,2304]{1,0:T(8,128)(2,1)} %param.14), kind=kOutput, calls=%fused_computation.9 | convolution fusion | flops 906559488 | bytes 5111808 | tf_op jit(solution)/shard_map/dot_general | solution.py:32
  12.8 0.0 copy-start.4
  12.8 53.3 %all-reduce.3.cloned.1.call-done = bf16[64,768]{1,0:T(8,128)(2,1)} async-done(((bf16[64,768]{1,0:T(8,128)(2,1)}), bf16[64,768]{1,0:T(8,128)(2,1)}) %all-reduce.3.cloned.1.call-update) | async-done | bytes 98320 | tf_op jit(solution)/shard_map/psum | solution.py:12
  66.1 2.8 %convolution_convert_fusion.2 = bf16[64,2304]{1,0:T(8,128)(2,1)S(1)} fusion(bf16[64,768]{1,0:T(8,128)(2,1)} %all-reduce.3.cloned.1.call-done, bf16[768,2304]{1,0:T(8,128)(2,1)} %param.14), kind=kOutput, calls=%fused_computation.11 | convolution fusion | flops 226639872 | bytes 3932160 | tf_op jit(solution)/shard_map/dot_general | solution.py:32
  68.9 0.0 copy-start.3
  68.9 0.7 copy-done.3
  69.6 0.7 fusion.56
  70.3 0.9 reshape.128
  71.2 1.0 convert_multiply_fusion
  72.2 1.6 reshape.127
  73.8 1.3 reduce_sum.93
  75.1 0.6 reduce_sum.92
  75.7 28.4 %pmax.7 = f32[64,12]{1,0:T(8,128)S(1)} all-reduce(f32[64,12]{1,0:T(8,128)S(1)} %multiply_reduce_fusion.3), channel_id=1, replica_groups=mesh['band'=8,'col'=4] {'band'}, use_global_device_ids=true, to_apply=%region_7.8 | all-reduce | flops 768 | bytes 6144 | tf_op jit(solution)/shard_map/pmax | solution.py:71
  104.1 0.6 fusion.45
  104.7 0.0 copy-done.7
  104.7 0.6 broadcast_in_dim.21
  105.4 0.0 copy-start.13
  105.4 0.0 copy-start.6
  105.4 1.4 reshape.129
  106.8 1.3 multiply_reduce_fusion.2
  108.2 0.7 pad_maximum_fusion
  108.9 0.0 all-reduce.5.cloned.1.call-update
  108.9 0.0 all-gather.2.cloned.1.call-start
  109.0 0.5 all-gather.2.cloned.1.call-update
  109.5 1.0 slice.53
  110.5 0.6 reshape.123
  111.2 0.1 fusion.39
  111.3 0.2 reshape.125
  111.5 0.8 copy.58
  112.3 2.0 %bitcast_reduce_fusion = (f32[4,12,64]{2,0,1:T(4,128)S(1)}, f32[12,64,4,64]{3,1,2,0:T(8,128)}) fusion(bf16[4,64,12,64]{3,2,1,0:T(8,128)(2,1)S(1)} %reshape.123, bf16[64,12,64,1]{2,1,0,3:T(8,128)(2,1)S(1)} %bitcast.53), kind=kOutput, calls=%fused_computation.28 | convolution fusion | flops 25555968 | bytes 1290240 | tf_op jit(solution)/shard_map/rqhd,khd->rhqk/dot_general | solution.py:101
  114.3 45.5 %all-reduce.5.cloned.1.call-done = f32[64,780]{1,0:T(8,128)} async-done(((f32[64,780]{1,0:T(8,128)}), f32[64,780]{1,0:T(8,128)}) %all-reduce.5.cloned.1.call-update) | async-done | bytes 199696 | tf_op jit(solution)/shard_map/psum | solution.py:78
  159.8 0.8 convert_convert_fusion
  160.6 0.2 broadcast_in_dim.23
  160.8 0.1 reshape.131
  160.9 0.2 broadcast_in_dim.22
  161.1 0.1 reshape.130
  161.2 1.0 fusion.41
  162.3 0.8 copy.53
  163.1 4.7 %convolution_convert_fusion.1 = bf16[1024,1536]{1,0:T(8,128)(2,1)S(1)} fusion(bf16[1024,768]{1,0:T(8,128)(2,1)} %bitcast.58, bf16[768,2304]{1,0:T(8,128)(2,1)} %param.14), kind=kOutput, calls=%fused_computation.10 | convolution fusion | flops 2417491968 | bytes 7077888 | tf_op jit(solution)/shard_map/dot_general | solution.py:32
  167.8 1.9 fusion.55
  169.8 2.6 %copy.42 = bf16[4,256,768]{1,2,0:T(8,128)(2,1)} copy(bf16[4,256,768]{2,1,0:T(8,128)(2,1)} %get-tuple-element.3) | data formatting | bytes 3145728 | tf_op jit(solution)/shard_map/slice | solution.py:89
  172.3 2.6 %copy.43 = bf16[4,256,768]{1,2,0:T(8,128)(2,1)} copy(bf16[4,256,768]{2,1,0:T(8,128)(2,1)} %get-tuple-element.2) | data formatting | bytes 3145728 | tf_op jit(solution)/shard_map/slice | solution.py:88
  175.0 2.2 %fusion.8 = (f32[4,12,64]{2,1,0:T(8,128)S(1)}, f32[4,12,64,256]{3,2,1,0:T(8,128)S(1)}) fusion(pred[4,64,256]{2,1,0:T(8,128)(4,1)S(1)} %fusion.39, bf16[4,256,12,64]{1,3,2,0:T(8,128)(2,1)} %bitcast.48, bf16[4,64,12,64]{3,2,1,0:T(8,128)(2,1)S(1)} %reshape.123), kind=kOutput, calls=%fused_computation.14 | convolution fusion | flops 103019520 | bytes 5189632 | tf_op jit(solution)/shard_map/rqhd,rkhd->rhqk/dot_general | solution.py:97
  177.3 1.2 fusion.9
  178.5 1.1 fusion.18
  179.7 0.3 copy-done.1
  179.9 0.4 fusion.27
  180.4 0.0 copy-start.5
  180.4 0.4 fusion.21
  180.8 0.6 copy.52
  181.4 1.2 convert_element_type.83
  182.6 1.7 fusion.57
  184.3 0.3 multiply_reduce_fusion.1
  184.6 0.0 copy-start.12
  184.6 7.4 %fusion.58 = (f32[320]{0:T(512)S(1)}, f32[320,768]{1,0:T(8,128)S(1)}) fusion(bf16[3072,768]{1,0:T(8,128)(2,1)} %param.18, bf16[768,3072]{1,0:T(8,128)(2,1)} %param.17, f32[320,768]{1,0:T(8,128)S(1)} %get-tuple-element.18, f32[768]{0:T(1024)S(1)} %copy-done.14, f32[320]{0:T(512)S(1)} %add_rsqrt_fusion.1, f32[320]{0:T(512)S(1)} %broadcast_multiply_fusion.1), kind=kOutput, calls=%fused_computation.94 | convolution fusion | flops 3031449344 | bytes 11410176 | tf_op jit(solution)/shard_map/dot_general | solution.py:27
  192.1 0.3 multiply_reduce_fusion
  192.4 0.2 multiply_convert_fusion
  192.6 0.8 slice.62
  193.3 0.6 slice.63
  (33 shorter events, 0.2 us)
Async XLA Ops:
  8.0 174.6 %copy-start = (bf16[768,768]{1,0:T(8,128)(2,1)S(1)}, bf16[768,768]{1,0:T(8,128)(2,1)}, u32[]{:S(2)}) copy-start(bf16[768,768]{1,0:T(8,128)(2,1)} %param.15) | copy-start | bytes 3538948
  8.0 58.1 %all-reduce.3.cloned.1.call-start = ((), (), s32[]{:S(2)}) async-start(), calls=%async_computation | async-start | bytes 196608 | tf_op jit(solution)/shard_map/psum | solution.py:12
  9.5 150.3 %all-reduce.5.cloned.1.call-start = ((), (), s32[]{:S(2)}) async-start(), calls=%async_computation.2 | async-start | bytes 458752 | tf_op jit(solution)/shard_map/psum | solution.py:78
  12.8 58.5 %copy-start.4 = (bf16[256,2304]{1,0:T(8,128)(2,1)}, bf16[256,2304]{1,0:T(8,128)(2,1)S(1)}, u32[]{:S(2)}) copy-start(bf16[256,2304]{1,0:T(8,128)(2,1)S(1)} %convolution_convert_fusion) | copy-start | bytes 3538948
  68.9 0.7 copy-start.3
  104.1 0.6 copy-start.7
  104.7 3.4 %copy-start.11 = (f32[64,12]{1,0:T(8,128)S(1)}, f32[64,12]{1,0:T(8,128)}, u32[]{:S(2)}) copy-start(f32[64,12]{1,0:T(8,128)} %get-tuple-element.10) | copy-start | bytes 9220
  105.4 5.8 %copy-start.13 = (s32[4,64]{1,0:T(4,128)S(1)}, s32[4,64]{1,0:T(4,128)}, u32[]{:S(2)}) copy-start(s32[4,64]{1,0:T(4,128)} %param.13) | copy-start | bytes 3076
  105.4 5.9 %copy-start.6 = (bf16[64,768]{1,0:T(8,128)(2,1)S(1)}, bf16[64,768]{1,0:T(8,128)(2,1)}, u32[]{:S(2)}) copy-start(bf16[64,768]{1,0:T(8,128)(2,1)} %get-tuple-element.8) | copy-start | bytes 294916
  108.9 50.9 %copy-start.8 = (f32[64,12]{1,0:T(8,128)S(1)}, f32[64,12]{1,0:T(8,128)}, u32[]{:S(2)}) copy-start(f32[64,12]{1,0:T(8,128)} %copy-done.7) | copy-start | bytes 9220
  108.9 54.2 %all-gather.2.cloned.1.call-start = ((), (), s32[]{:S(2)}) async-start(), calls=%async_computation.1 | async-start | bytes 1966080 | tf_op jit(solution)/shard_map/all_gather | solution.py:55
  175.0 3.5 %copy-start.2 = (bf16[4,256,768]{1,2,0:T(8,128)(2,1)S(1)}, bf16[4,256,768]{1,2,0:T(8,128)(2,1)}, u32[]{:S(2)}) copy-start(bf16[4,256,768]{1,2,0:T(8,128)(2,1)} %copy.42) | copy-start | bytes 4718596
  178.5 1.4 copy-start.1
  178.5 1.8 copy-start.9
  180.4 2.3 %copy-start.5 = (bf16[4,64,768]{2,1,0:T(8,128)(2,1)S(1)}, bf16[4,64,768]{2,1,0:T(8,128)(2,1)}, u32[]{:S(2)}) copy-start(bf16[4,64,768]{2,1,0:T(8,128)(2,1)} %param.10) | copy-start | bytes 1179652
  180.4 2.2 %copy-start.10 = (bf16[64,768]{0,1:T(8,128)(2,1)S(1)}, bf16[64,768]{0,1:T(8,128)(2,1)}, u32[]{:S(2)}) copy-start(bf16[64,768]{0,1:T(8,128)(2,1)} %copy.53) | copy-start | bytes 294916
  182.6 2.0 copy-start.14
  184.6 7.7 %copy-start.12 = (f32[768]{0:T(1024)S(1)}, f32[768]{0:T(1024)}, u32[]{:S(2)}) copy-start(f32[768]{0:T(1024)} %param.19) | copy-start | bytes 9220
Sparse Core Ops, SparseCore 0:
  11.7 54.3 all-reduce.2
  109.0 50.7 all-reduce.4
Sparse Core Ops, SparseCore 1:
  111.2 28.9 all-gather.1

commit v2 on v1

--- a/solution.py
+++ b/solution.py
@@ -1,3 +1,5 @@
+import functools
+
 import jax
 import jax.numpy as jnp
 from jax import lax
@@ -44,21 +46,38 @@
     )
 
 
-def local(cells, summary, owner, schema, w_qkv, w_out, gain_attn, w_up, w_down, gain_ffn):
+def fan_out(value, axis, count):
+    here = lax.axis_index(axis)
+    got = []
+    for step in range(1, count):
+        if count & (count - 1) == 0:
+            pairs = [(i, i ^ step) for i in range(count)]
+            source = here ^ step
+        else:
+            pairs = [(i, (i + step) % count) for i in range(count)]
+            source = (here - step) % count
+        got.append((source, lax.ppermute(value, axis, pairs)))
+    return got
+
+
+def local(cells, summary, owner, schema, w_qkv, w_out, gain_attn, w_up, w_down, gain_ffn, *, n_band, n_col):
     row_count, cols_dev, model_width = cells.shape
     own_group = lax.axis_index("col")
+    own_band = lax.axis_index("band")
     score_scale = HEAD_DIM ** (-0.5)
     flat_cells = cells.reshape(row_count * cols_dev, model_width)
     w_kv = w_qkv[:, model_width:]
 
-    tokens = spread_2(summary[0], "band", owner[0])
-    row_cells = lax.all_gather(cells, "col", axis=1, tiled=True)
-    width_now = row_cells.shape[1]
+    tokens = summary[0]
+    for source, got in fan_out(summary[0], "band", n_band):
+        tokens = jnp.where(source == owner[0], got, tokens)
+    tokens = jnp.where(own_band == owner[0], summary[0], tokens)
+    row_parts = fan_out(cells, "col", n_col)
 
     qkv_cells = project(flat_cells, w_qkv).reshape(row_count, cols_dev, 3 * model_width)
     queries = qkv_cells[:, :, :model_width]
-    own_keys = qkv_cells[:, :, model_width : 2 * model_width].astype(jnp.float32)
-    own_vals = qkv_cells[:, :, 2 * model_width :].astype(jnp.float32)
+    own_keys = qkv_cells[:, :, model_width : 2 * model_width]
+    own_vals = qkv_cells[:, :, 2 * model_width :]
 
     summary_qkv = project(tokens, w_qkv)
     sum_queries = summary_qkv[:, :model_width]
@@ -66,33 +85,51 @@
     sum_vals = summary_qkv[:, 2 * model_width :]
 
     sq = sum_queries.astype(jnp.float32)
-    col_scores = head_sum(sq[None] * own_keys) * score_scale
+    col_scores = head_sum(sq[None] * own_keys.astype(jnp.float32)) * score_scale
     self_scores = head_sum(sq * sum_keys.astype(jnp.float32)) * score_scale
-    col_top = jnp.maximum(lax.pmax(col_scores.max(0), "band"), self_scores)
-    col_exp = jnp.exp(col_scores - col_top[None])
+    part_top = col_scores.max(0)
+    col_exp = jnp.exp(col_scores - part_top[None])
+    col_weights = head_spread(col_exp.astype(jnp.bfloat16).astype(jnp.float32))
+    part_mixed = (col_weights * own_vals.astype(jnp.float32)).sum(0)
+    part_total = col_exp.sum(0)
+    packed = jnp.concatenate([part_mixed, part_total, part_top], axis=-1)
+    stacked = jnp.stack([packed] + [got for _, got in fan_out(packed, "band", n_band)])
+    stacked = jnp.take(stacked, jnp.arange(n_band, dtype=jnp.int32) ^ own_band, axis=0)
+    parts = [stacked[k] for k in range(n_band)]
+    tops = [p[:, model_width + HEADS :] for p in parts]
+    col_top = self_scores
+    for t in tops:
+        col_top = jnp.maximum(col_top, t)
     self_exp = jnp.exp(self_scores - col_top)
-    col_weights = head_spread(col_exp.astype(jnp.bfloat16).astype(jnp.float32))
-    col_mixed = (col_weights * own_vals).sum(0)
-    col_total = col_exp.sum(0)
-    packed = jnp.concatenate([col_mixed, col_total], axis=-1)
-    packed = lax.psum(packed, "band")
-    col_mixed = packed[:, :model_width]
-    col_total = packed[:, model_width:] + self_exp
+    col_total = self_exp
     self_weights = head_spread(self_exp.astype(jnp.bfloat16).astype(jnp.float32))
-    col_mixed = col_mixed + self_weights * sum_vals.astype(jnp.float32)
+    col_mixed = self_weights * sum_vals.astype(jnp.float32)
+    for p, t in zip(parts, tops):
+        fade = jnp.exp(t - col_top)
+        col_total = col_total + fade * p[:, model_width : model_width + HEADS]
+        col_mixed = col_mixed + head_spread(fade) * p[:, :model_width]
     summary_att = (col_mixed / head_spread(col_total)).astype(jnp.bfloat16)
 
-    row_kv = project(row_cells.reshape(row_count * width_now, model_width), w_kv)
-    row_kv = row_kv.reshape(row_count, width_now, 2 * model_width)
+    sources = [own_group] + [s for s, _ in row_parts]
+    other_cells = jnp.concatenate([got for _, got in row_parts], axis=1)
+    width_other = other_cells.shape[1]
+    other_kv = project(other_cells.reshape(row_count * width_other, model_width), w_kv)
+    other_kv = other_kv.reshape(row_count, width_other, 2 * model_width)
+    row_keys = jnp.concatenate([own_keys, other_kv[:, :, :model_width]], axis=1)
+    row_vals = jnp.concatenate([own_vals, other_kv[:, :, model_width:]], axis=1)
+    width_now = row_keys.shape[1]
     q4 = queries.reshape(row_count, cols_dev, HEADS, HEAD_DIM)
-    k4 = row_kv[:, :, :model_width].reshape(row_count, width_now, HEADS, HEAD_DIM)
-    v4 = row_kv[:, :, model_width:].reshape(row_count, width_now, HEADS, HEAD_DIM)
+    k4 = row_keys.reshape(row_count, width_now, HEADS, HEAD_DIM)
+    v4 = row_vals.reshape(row_count, width_now, HEADS, HEAD_DIM)
     sk = sum_keys.reshape(cols_dev, HEADS, HEAD_DIM)
     sv = sum_vals.reshape(cols_dev, HEADS, HEAD_DIM)
-    key_groups = jnp.arange(width_now, dtype=jnp.int32) // cols_dev
-    allowed = (jnp.right_shift(schema[:, :, None], key_groups[None, None, :]) & 1 == 1) | (
-        key_groups == own_group
-    )[None, None, :]
+    key_groups = jnp.concatenate(
+        [jnp.full((cols_dev,), s, jnp.int32) for s in sources]
+    )
+    own_block = jnp.arange(width_now, dtype=jnp.int32) < cols_dev
+    allowed = (jnp.right_shift(schema[:, :, None], key_groups[None, None, :]) & 1 == 1) | own_block[
+        None, None, :
+    ]
     cell_scores = (
         jnp.einsum("rqhd,rkhd->rhqk", q4, k4, preferred_element_type=jnp.float32) * score_scale
     )
@@ -135,4 +172,5 @@
         P(),
     )
     out_specs = (P("band", "col", None), P("col", None))
-    return jax.shard_map(local, mesh=mesh, in_specs=in_specs, out_specs=out_specs, check_vma=False)
+    body = functools.partial(local, n_band=mesh.shape["band"], n_col=mesh.shape["col"])
+    return jax.shard_map(body, mesh=mesh, in_specs=in_specs, out_specs=out_specs, check_vma=False)

time: 202 us -> 141 us (0.70)
  the two profiles are of different devices: /device:TPU:0 before, /device:TPU:9 now
where the time goes in v2:
time: 141 us; the launch traced here: 140 us
  local copies, waits for them, and re-layouts  38.9 us (28%)
  starting transfers between devices  28.9 us (20%)
  waiting for transfers between devices  27.6 us (20%)
  matrix products  25.4 us (18%)
  other arithmetic  17.5 us (12%)
  between operations  1.81 us (1%)
    ppermute x17, starting transfers between devices, fan_out(): got.append((source, lax.ppermute(value, axis, pairs)))  28.9 us
    ppermute x17, waiting for transfers between devices, fan_out(): got.append((source, lax.ppermute(value, axis, pairs)))  27.6 us
    dot_general x3, matrix products, project(): jnp.dot(values, weight, preferred_element_type=jnp.float32)  9.66 us
    reshape x11, local copies, waits for them, and re-layouts, head_spread(): jnp.broadcast_to(values[..., None], dims + (HEADS, HEAD_DIM))  9.61 us
    unnamed x56, local copies, waits for them, and re-layouts  8.33 us
    dot_general x1, matrix products, finish(): outer_out = jnp.dot(inner_act, w_down, preferred_element_type=jnp.float32)  7.54 us
    broadcast_in_dim x11, local copies, waits for them, and re-layouts, head_spread(): jnp.broadcast_to(values[..., None], dims + (HEADS, HEAD_DIM))  4.76 us
  transfers between devices with their start and end apart: 17, of which 7 were waited for; matrix products, arithmetic and copies ran while one was open for 35% of the time, Pallas kernels for 0%

profile of v2, /device:TPU:9, one launch (start us, length us, event | category | flops | bytes accessed | tf_op | source)
XLA Modules:
  0.0 140.2 jit_solution(9550821316583459675)
XLA Ops:
  0.6 1.9 %collective-permute-start = (bf16[64,768]{1,0:T(8,128)(2,1)}, bf16[64,768]{1,0:T(8,128)(2,1)S(1)}, u32[]{:S(2)}, u32[]{:S(2)}) collective-permute-start(bf16[64,768]{1,0:T(8,128)(2,1)} %bitcast.98), channel_id=1, source_target_pairs={{0,28},{4,24},{8,20},{12,16},{16,12},{20,8},{24,4},{28,0},{1,29},{... | collective-permute-start | bytes 294920 | tf_op jit(solution)/shard_map/ppermute | solution.py:59
  2.7 4.1 %collective-permute-start.2 = (bf16[64,768]{1,0:T(8,128)(2,1)}, bf16[64,768]{1,0:T(8,128)(2,1)S(1)}, u32[]{:S(2)}, u32[]{:S(2)}) collective-permute-start(bf16[64,768]{1,0:T(8,128)(2,1)} %bitcast.100), channel_id=1, source_target_pairs={{0,20},{4,16},{8,28},{12,24},{16,4},{20,0},{24,12},{28,8},{1,21},{... | collective-permute-start | bytes 294920 | tf_op jit(solution)/shard_map/ppermute | solution.py:59
  6.9 0.8 collective-permute-start.4
  8.4 3.2 %convolution_convert_fusion = bf16[256,2304]{1,0:T(8,128)(2,1)S(1)} fusion(bf16[256,768]{1,0:T(8,128)(2,1)} %bitcast, bf16[768,2304]{1,0:T(8,128)(2,1)} %param.14), kind=kOutput, calls=%fused_computation.10 | convolution fusion | flops 906559488 | bytes 5111808 | tf_op jit(solution)/shard_map/dot_general | solution.py:34
  11.6 1.0 fusion.74
  12.6 1.6 %reshape.162 = bf16[4,64,12,64]{3,2,1,0:T(8,128)(2,1)} reshape(bf16[4,64,768]{2,1,0:T(8,128)(2,1)S(1)} %get-tuple-element.27) | data formatting | bytes 786432 | tf_op jit(solution)/shard_map/reshape | solution.py:121
  14.3 0.7 fusion.40
  15.1 1.0 collective-permute-start.5
  17.4 0.8 collective-permute-done.2
  18.1 2.2 %collective-permute-start.9 = (bf16[4,64,768]{2,1,0:T(8,128)(2,1)}, bf16[4,64,768]{2,1,0:T(8,128)(2,1)}, u32[]{:S(2)}, u32[]{:S(2)}) collective-permute-start(bf16[4,64,768]{2,1,0:T(8,128)(2,1)} %param.10), channel_id=1, source_target_pairs={{0,3},{1,2},{2,1},{3,0},{4,7},{5,6},{6,5},{7,4},{8,11},{9,10},{10,... | collective-permute-start | bytes 1179656 | tf_op jit(solution)/shard_map/ppermute | solution.py:59
  20.3 1.2 collective-permute-start.8
  21.5 1.2 collective-permute-start.7
  22.8 2.8 %convolution_convert_fusion.1 = bf16[64,2304]{1,0:T(8,128)(2,1)S(1)} fusion(bf16[64,768]{1,0:T(8,128)(2,1)S(1)} %select_select_fusion, bf16[768,2304]{1,0:T(8,128)(2,1)} %param.14), kind=kOutput, calls=%fused_computation.11 | convolution fusion | flops 226639872 | bytes 3932160 | tf_op jit(solution)/shard_map/dot_general | solution.py:34
  26.3 1.0 convert_multiply_fusion
  27.3 1.6 %reshape.167 = f32[4,64,12,64]{3,2,1,0:T(8,128)S(1)} reshape(f32[4,64,768]{2,1,0:T(8,128)} %convert_multiply_fusion) | data formatting | bytes 1572864 | tf_op jit(solution)/shard_map/reshape | solution.py:39
  30.8 1.4 reshape.168
  32.2 1.4 multiply_reduce_fusion.2
  33.6 1.7 %bitcast_dynamic-update-slice_fusion.7 = (f32[8,64,792]{2,1,0:T(8,128)}, f32[64,792]{1,0:T(8,128)}) fusion(f32[64,12]{1,0:T(8,128)S(1)} %multiply_reduce_fusion.3, f32[64,12]{1,0:T(8,128)} %get-tuple-element.34, f32[64,768]{1,0:T(8,128)S(1)} %multiply_reduce_fusion.2), kind=kLoop, calls=%fused_computation.76 | loop fusion | flops 101375 | bytes 661504
  35.3 1.0 collective-permute-start.10
  36.2 2.0 %collective-permute-start.11 = (f32[64,792]{1,0:T(8,128)}, f32[64,792]{1,0:T(8,128)}, u32[]{:S(2)}, u32[]{:S(2)}) collective-permute-start(f32[64,792]{1,0:T(8,128)} %get-tuple-element.14), channel_id=1, source_target_pairs={{0,8},{4,12},{8,0},{12,4},{16,24},{20,28},{24,16},{28,20},{1,9},{5... | collective-permute-start | bytes 608264 | tf_op jit(solution)/shard_map/ppermute | solution.py:59
  38.4 0.8 reduce_sum.92
  39.4 0.8 copy.58
  40.3 2.6 %bitcast_reduce_fusion = (f32[4,12,64]{2,0,1:T(4,128)}, f32[12,64,4,64]{3,1,2,0:T(8,128)}) fusion(bf16[4,64,12,64]{3,2,1,0:T(8,128)(2,1)S(1)} %copy-done.1, bf16[64,12,64,1]{2,1,0,3:T(8,128)(2,1)S(1)} %bitcast.95), kind=kOutput, calls=%fused_computation.31 | convolution fusion | flops 25555968 | bytes 1290240 | tf_op jit(solution)/shard_map/rqhd,khd->rhqk/dot_general | solution.py:138
  42.9 1.7 %bitcast_dynamic-update-slice_fusion.6 = f32[8,64,792]{2,1,0:T(8,128)} fusion(f32[8,64,792]{2,1,0:T(8,128)} %get-tuple-element.13, f32[64,792]{1,0:T(8,128)} %collective-permute-done.10), kind=kLoop, calls=%fused_computation.75 | loop fusion | bytes 458752
  44.6 2.6 %collective-permute-start.13 = (f32[64,792]{1,0:T(8,128)}, f32[64,792]{1,0:T(8,128)S(1)}, u32[]{:S(2)}, u32[]{:S(2)}) collective-permute-start(f32[64,792]{1,0:T(8,128)} %get-tuple-element.14), channel_id=1, source_target_pairs={{0,16},{4,20},{8,24},{12,28},{16,0},{20,4},{24,8},{28,12},{1,17},{... | collective-permute-start | bytes 608264 | tf_op jit(solution)/shard_map/ppermute | solution.py:59
  47.2 1.6 %bitcast_dynamic-update-slice_fusion.5 = f32[8,64,792]{2,1,0:T(8,128)} fusion(f32[8,64,792]{2,1,0:T(8,128)} %bitcast_dynamic-update-slice_fusion.6, f32[64,792]{1,0:T(8,128)} %collective-permute-done.11), kind=kLoop, calls=%fused_computation.74 | loop fusion | bytes 458752
  48.8 2.8 %collective-permute-done.12 = f32[64,792]{1,0:T(8,128)S(1)} collective-permute-done((f32[64,792]{1,0:T(8,128)}, f32[64,792]{1,0:T(8,128)S(1)}, u32[]{:S(2)}, u32[]{:S(2)}) %collective-permute-start.12) | collective-permute-done | bytes 202784 | tf_op jit(solution)/shard_map/ppermute | solution.py:59
  51.7 2.4 %collective-permute-start.14 = (f32[64,792]{1,0:T(8,128)}, f32[64,792]{1,0:T(8,128)S(1)}, u32[]{:S(2)}, u32[]{:S(2)}) collective-permute-start(f32[64,792]{1,0:T(8,128)} %get-tuple-element.14), channel_id=1, source_target_pairs={{0,20},{4,16},{8,28},{12,24},{16,4},{20,0},{24,12},{28,8},{1,21},{... | collective-permute-start | bytes 608264 | tf_op jit(solution)/shard_map/ppermute | solution.py:59
  54.8 6.9 %collective-permute-done.13 = f32[64,792]{1,0:T(8,128)S(1)} collective-permute-done((f32[64,792]{1,0:T(8,128)}, f32[64,792]{1,0:T(8,128)S(1)}, u32[]{:S(2)}, u32[]{:S(2)}) %collective-permute-start.13) | collective-permute-done | bytes 202784 | tf_op jit(solution)/shard_map/ppermute | solution.py:59
  62.5 4.2 %collective-permute-done.14 = f32[64,792]{1,0:T(8,128)S(1)} collective-permute-done((f32[64,792]{1,0:T(8,128)}, f32[64,792]{1,0:T(8,128)S(1)}, u32[]{:S(2)}, u32[]{:S(2)}) %collective-permute-start.14) | collective-permute-done | bytes 202784 | tf_op jit(solution)/shard_map/ppermute | solution.py:59
  66.7 7.5 %collective-permute-start.16 = (f32[64,792]{1,0:T(8,128)}, f32[64,792]{1,0:T(8,128)S(1)}, u32[]{:S(2)}, u32[]{:S(2)}) collective-permute-start(f32[64,792]{1,0:T(8,128)} %get-tuple-element.14), channel_id=1, source_target_pairs={{0,28},{4,24},{8,20},{12,16},{16,12},{20,8},{24,4},{28,0},{1,29},{... | collective-permute-start | bytes 608264 | tf_op jit(solution)/shard_map/ppermute | solution.py:59
  74.9 3.9 %collective-permute-done.15 = f32[64,792]{1,0:T(8,128)S(1)} collective-permute-done((f32[64,792]{1,0:T(8,128)}, f32[64,792]{1,0:T(8,128)S(1)}, u32[]{:S(2)}, u32[]{:S(2)}) %collective-permute-start.15) | collective-permute-done | bytes 202784 | tf_op jit(solution)/shard_map/ppermute | solution.py:59
  79.5 8.4 %collective-permute-done.16 = f32[64,792]{1,0:T(8,128)S(1)} collective-permute-done((f32[64,792]{1,0:T(8,128)}, f32[64,792]{1,0:T(8,128)S(1)}, u32[]{:S(2)}, u32[]{:S(2)}) %collective-permute-start.16) | collective-permute-done | bytes 202784 | tf_op jit(solution)/shard_map/ppermute | solution.py:59
  88.6 2.2 %gather_fusion = f32[8,64,792]{2,1,0:T(8,128)S(1)} fusion(f32[8,64,792]{2,1,0:T(8,128)} %bitcast_dynamic-update-slice_fusion, s32[1024]{0:T(1024)S(1)} %pad_clamp_fusion), kind=kCustom, calls=%fused_computation | custom fusion | bytes 3244064 | tf_op jit(solution)/shard_map/jit(_take)/gather | solution.py:97
  91.8 0.7 convert_convert_fusion
  92.5 0.8 fusion.55
  93.5 0.8 reshape.178
  94.3 1.0 broadcast_in_dim.69
  95.3 0.8 reshape.177
  96.1 0.9 broadcast_in_dim.68
  97.0 0.8 reshape.176
  97.9 0.9 broadcast_in_dim.63
  98.8 0.8 reshape.175
  99.8 0.8 reshape.174
  100.9 0.8 reshape.173
  101.9 0.8 reshape.172
  102.9 0.8 reshape.171
  103.9 0.8 reshape.170
  104.9 0.8 reshape.169
  105.7 1.9 %fusion.51 = bf16[64,768]{1,0:T(8,128)(2,1)S(1)} fusion(f32[64,768]{1,0:T(8,128)} %reshape.178, f32[64,768]{1,0:T(8,128)} %reshape.177, f32[64,792]{1,0:T(8,128)S(1)} %get-tuple-element.18, f32[64,768]{1,0:T(8,128)} %reshape.176, f32[64,792]{1,0:T(8,128)S(1)} %get-tuple-element.19, f32[64,768]{1,0:T(8,128)} %reshape.175, ...), kind=kLoop, calls=%fused_computation.96 | loop fusion | flops 983040 | bytes 3735552 | tf_op jit(solution)/shard_map/convert_element_type | solution.py:111
  107.8 1.3 pad_maximum_fusion.2
  109.1 3.7 %convolution_convert_fusion.2 = bf16[768,1536]{1,0:T(8,128)(2,1)S(1)} fusion(bf16[768,768]{1,0:T(8,128)(2,1)S(1)} %bitcast.94, bf16[768,2304]{1,0:T(8,128)(2,1)} %param.14), kind=kOutput, calls=%fused_computation.12 | convolution fusion | flops 1813118976 | bytes 5898240 | tf_op jit(solution)/shard_map/dot_general | solution.py:34
  113.0 0.8 copy-done.8
  113.9 1.4 pad_maximum_fusion
  115.3 1.6 %copy.42 = bf16[4,256,768]{1,2,0:T(8,128)(2,1)} copy(bf16[4,256,768]{2,1,0:T(8,128)(2,1)S(1)} %get-tuple-element.43) | data formatting | bytes 3145728 | tf_op jit(solution)/shard_map/concatenate | solution.py:119
  116.8 2.7 %copy.43 = bf16[4,256,768]{1,2,0:T(8,128)(2,1)} copy(bf16[4,256,768]{2,1,0:T(8,128)(2,1)} %get-tuple-element.44) | data formatting | bytes 3145728 | tf_op jit(solution)/shard_map/concatenate | solution.py:118
  119.5 2.1 %fusion.8 = (f32[4,12,64]{2,1,0:T(8,128)S(1)}, f32[4,12,64,256]{3,2,1,0:T(8,128)S(1)}) fusion(pred[4,64,256]{2,1,0:T(8,128)(4,1)S(1)} %copy-done.12, bf16[4,256,12,64]{1,3,2,0:T(8,128)(2,1)} %bitcast.89, bf16[4,64,12,64]{3,2,1,0:T(8,128)(2,1)S(1)} %copy-done.2), kind=kOutput, calls=%fused_computation.15 | convolution fusion | flops 103019520 | bytes 5189632 | tf_op jit(solution)/shard_map/rqhd,rkhd->rhqk/dot_general | solution.py:134
  121.7 1.2 fusion.9
  123.1 1.3 fusion.18
  126.4 1.2 convert_element_type.81
  127.6 1.8 %fusion.64 = (f32[320]{0:T(512)S(1)}, f32[320,768]{1,0:T(8,128)S(1)}) fusion(bf16[64,768]{1,0:T(8,128)(2,1)S(1)} %copy-done.14, bf16[256,768]{1,0:T(8,128)(2,1)} %bitcast, bf16[768,768]{1,0:T(8,128)(2,1)S(1)} %copy-done, bf16[64,768]{0,1:T(8,128)(2,1)S(1)} %copy.53, bf16[256,768]{0,1:T(8,128)(2,1)} %convert_element_type.81), kind=kOutput, calls=%fused_computation.133 | convolution fusion | flops 379944640 | bytes 3147008 | tf_op jit(solution)/shard_map/dot_general | solution.py:24
  129.4 1.3 multiply_reduce_fusion.1
  130.7 7.5 %fusion.76 = (f32[320]{0:T(512)S(1)}, f32[320,768]{1,0:T(8,128)S(1)}) fusion(bf16[3072,768]{1,0:T(8,128)(2,1)} %param.18, bf16[768,3072]{1,0:T(8,128)(2,1)} %param.17, f32[768]{0:T(1024)S(1)} %copy-done.24, f32[320]{0:T(512)S(1)} %add_rsqrt_fusion.1, f32[320]{0:T(512)S(1)} %broadcast_multiply_fusion.1, f32[320,768]{1,0:T(8,128)S(1)} %get-tuple-element.40, ...), kind=kOutput, calls=%fused_computation.156 | convolution fusion | flops 3033906944 | bytes 11901696 | tf_op jit(solution)/shard_map/dot_general | solution.py:29
  138.8 0.8 slice.214
  (112 shorter events, 14.1 us)
Async XLA Ops:
  0.6 127.0 %copy-start = (bf16[768,768]{1,0:T(8,128)(2,1)S(1)}, bf16[768,768]{1,0:T(8,128)(2,1)}, u32[]{:S(2)}) copy-start(bf16[768,768]{1,0:T(8,128)(2,1)} %param.15) | copy-start | bytes 3538948
  0.6 14.4 %collective-permute-start = (bf16[64,768]{1,0:T(8,128)(2,1)}, bf16[64,768]{1,0:T(8,128)(2,1)S(1)}, u32[]{:S(2)}, u32[]{:S(2)}) collective-permute-start(bf16[64,768]{1,0:T(8,128)(2,1)} %bitcast.98), channel_id=1, source_target_pairs={{0,28},{4,24},{8,20},{12,16},{16,12},{20,8},{24,4},{28,0},{1,29},{... | collective-permute-start | bytes 294920 | tf_op jit(solution)/shard_map/ppermute | solution.py:59
  2.6 14.1 %collective-permute-start.1 = (bf16[64,768]{1,0:T(8,128)(2,1)}, bf16[64,768]{1,0:T(8,128)(2,1)S(1)}, u32[]{:S(2)}, u32[]{:S(2)}) collective-permute-start(bf16[64,768]{1,0:T(8,128)(2,1)} %bitcast.99), channel_id=1, source_target_pairs={{0,24},{4,28},{8,16},{12,20},{16,8},{20,12},{24,0},{28,4},{1,25},{... | collective-permute-start | bytes 294920 | tf_op jit(solution)/shard_map/ppermute | solution.py:59
  2.7 15.4 %collective-permute-start.2 = (bf16[64,768]{1,0:T(8,128)(2,1)}, bf16[64,768]{1,0:T(8,128)(2,1)S(1)}, u32[]{:S(2)}, u32[]{:S(2)}) collective-permute-start(bf16[64,768]{1,0:T(8,128)(2,1)} %bitcast.100), channel_id=1, source_target_pairs={{0,20},{4,16},{8,28},{12,24},{16,4},{20,0},{24,12},{28,8},{1,21},{... | collective-permute-start | bytes 294920 | tf_op jit(solution)/shard_map/ppermute | solution.py:59
  6.8 13.4 %collective-permute-start.3 = (bf16[64,768]{1,0:T(8,128)(2,1)}, bf16[64,768]{1,0:T(8,128)(2,1)S(1)}, u32[]{:S(2)}, u32[]{:S(2)}) collective-permute-start(bf16[64,768]{1,0:T(8,128)(2,1)} %bitcast.101), channel_id=1, source_target_pairs={{0,16},{4,20},{8,24},{12,28},{16,0},{20,4},{24,8},{28,12},{1,17},{... | collective-permute-start | bytes 294920 | tf_op jit(solution)/shard_map/ppermute | solution.py:59
  6.9 14.6 %collective-permute-start.4 = (bf16[64,768]{1,0:T(8,128)(2,1)}, bf16[64,768]{1,0:T(8,128)(2,1)S(1)}, u32[]{:S(2)}, u32[]{:S(2)}) collective-permute-start(bf16[64,768]{1,0:T(8,128)(2,1)} %bitcast.102), channel_id=1, source_target_pairs={{0,12},{4,8},{8,4},{12,0},{16,28},{20,24},{24,20},{28,16},{1,13},{... | collective-permute-start | bytes 294920 | tf_op jit(solution)/shard_map/ppermute | solution.py:59
  11.6 14.7 %copy-start.5 = (bf16[256,2304]{1,0:T(8,128)(2,1)}, bf16[256,2304]{1,0:T(8,128)(2,1)S(1)}, u32[]{:S(2)}) copy-start(bf16[256,2304]{1,0:T(8,128)(2,1)S(1)} %convolution_convert_fusion) | copy-start | bytes 3538948
  11.6 2.7 %copy-start.23 = (s32[4,64]{1,0:T(4,128)S(1)}, s32[4,64]{1,0:T(4,128)}, u32[]{:S(2)}) copy-start(s32[4,64]{1,0:T(4,128)} %param.13) | copy-start | bytes 3076
  11.6 3.5 %copy-start.21 = (bf16[1,64,768]{2,1,0:T(8,128)(2,1)S(1)}, bf16[1,64,768]{2,1,0:T(8,128)(2,1)}, u32[]{:S(2)}) copy-start(bf16[1,64,768]{2,1,0:T(8,128)(2,1)} %param.11) | copy-start | bytes 294916
  15.1 7.6 %collective-permute-start.5 = (bf16[64,768]{1,0:T(8,128)(2,1)S(1)}, bf16[64,768]{1,0:T(8,128)(2,1)S(1)}, u32[]{:S(2)}, u32[]{:S(2)}) collective-permute-start(bf16[64,768]{1,0:T(8,128)(2,1)S(1)} %bitcast.103), channel_id=1, source_target_pairs={{0,8},{4,12},{8,0},{12,4},{16,24},{20,28},{24,16},{28,20},{1,9},{5... | collective-permute-start | bytes 294920 | tf_op jit(solution)/shard_map/ppermute | solution.py:59
  16.7 6.0 %collective-permute-start.6 = (bf16[64,768]{1,0:T(8,128)(2,1)S(1)}, bf16[64,768]{1,0:T(8,128)(2,1)S(1)}, u32[]{:S(2)}, u32[]{:S(2)}) collective-permute-start(bf16[64,768]{1,0:T(8,128)(2,1)S(1)} %bitcast.104), channel_id=1, source_target_pairs={{0,4},{4,0},{8,12},{12,8},{16,20},{20,16},{24,28},{28,24},{1,5},{5... | collective-permute-start | bytes 294920 | tf_op jit(solution)/shard_map/ppermute | solution.py:59
  18.1 89.7 %collective-permute-start.9 = (bf16[4,64,768]{2,1,0:T(8,128)(2,1)}, bf16[4,64,768]{2,1,0:T(8,128)(2,1)}, u32[]{:S(2)}, u32[]{:S(2)}) collective-permute-start(bf16[4,64,768]{2,1,0:T(8,128)(2,1)} %param.10), channel_id=1, source_target_pairs={{0,3},{1,2},{2,1},{3,0},{4,7},{5,6},{6,5},{7,4},{8,11},{9,10},{10,... | collective-permute-start | bytes 1179656 | tf_op jit(solution)/shard_map/ppermute | solution.py:59
  20.3 87.5 %collective-permute-start.8 = (bf16[4,64,768]{2,1,0:T(8,128)(2,1)}, bf16[4,64,768]{2,1,0:T(8,128)(2,1)}, u32[]{:S(2)}, u32[]{:S(2)}) collective-permute-start(bf16[4,64,768]{2,1,0:T(8,128)(2,1)} %param.10), channel_id=1, source_target_pairs={{0,2},{1,3},{2,0},{3,1},{4,6},{5,7},{6,4},{7,5},{8,10},{9,11},{10,... | collective-permute-start | bytes 1179656 | tf_op jit(solution)/shard_map/ppermute | solution.py:59
  21.5 86.3 %collective-permute-start.7 = (bf16[4,64,768]{2,1,0:T(8,128)(2,1)}, bf16[4,64,768]{2,1,0:T(8,128)(2,1)}, u32[]{:S(2)}, u32[]{:S(2)}) collective-permute-start(bf16[4,64,768]{2,1,0:T(8,128)(2,1)} %param.10), channel_id=1, source_target_pairs={{0,1},{1,0},{2,3},{3,2},{4,5},{5,4},{6,7},{7,6},{8,9},{9,8},{10,11... | collective-permute-start | bytes 1179656 | tf_op jit(solution)/shard_map/ppermute | solution.py:59
  22.8 2.8 %copy-start.13 = (bf16[64,768]{1,0:T(8,128)(2,1)}, bf16[64,768]{1,0:T(8,128)(2,1)S(1)}, u32[]{:S(2)}) copy-start(bf16[64,768]{1,0:T(8,128)(2,1)S(1)} %select_select_fusion) | copy-start | bytes 294916
  25.6 0.8 copy-start.6
  32.2 6.1 %copy-start.7 = (bf16[64,2304]{1,0:T(8,128)(2,1)S(1)}, bf16[64,2304]{1,0:T(8,128)(2,1)}, u32[]{:S(2)}) copy-start(bf16[64,2304]{1,0:T(8,128)(2,1)} %copy-done.6) | copy-start | bytes 884740
  32.2 7.1 %copy-start.15 = (bf16[64,768]{1,0:T(8,128)(2,1)S(1)}, bf16[64,768]{1,0:T(8,128)(2,1)}, u32[]{:S(2)}) copy-start(bf16[64,768]{1,0:T(8,128)(2,1)} %get-tuple-element.32) | copy-start | bytes 294916
  33.6 6.7 %copy-start.1 = (bf16[4,64,12,64]{3,2,1,0:T(8,128)(2,1)S(1)}, bf16[4,64,12,64]{3,2,1,0:T(8,128)(2,1)}, u32[]{:S(2)}) copy-start(bf16[4,64,12,64]{3,2,1,0:T(8,128)(2,1)} %reshape.162) | copy-start | bytes 1179652
  35.3 7.6 %collective-permute-start.10 = (f32[64,792]{1,0:T(8,128)}, f32[64,792]{1,0:T(8,128)}, u32[]{:S(2)}, u32[]{:S(2)}) collective-permute-start(f32[64,792]{1,0:T(8,128)} %get-tuple-element.14), channel_id=1, source_target_pairs={{0,4},{4,0},{8,12},{12,8},{16,20},{20,16},{24,28},{28,24},{1,5},{5... | collective-permute-start | bytes 608264 | tf_op jit(solution)/shard_map/ppermute | solution.py:59
  36.2 8.3 %collective-permute-start.11 = (f32[64,792]{1,0:T(8,128)}, f32[64,792]{1,0:T(8,128)}, u32[]{:S(2)}, u32[]{:S(2)}) collective-permute-start(f32[64,792]{1,0:T(8,128)} %get-tuple-element.14), channel_id=1, source_target_pairs={{0,8},{4,12},{8,0},{12,4},{16,24},{20,28},{24,16},{28,20},{1,9},{5... | collective-permute-start | bytes 608264 | tf_op jit(solution)/shard_map/ppermute | solution.py:59
  42.9 8.8 %collective-permute-start.12 = (f32[64,792]{1,0:T(8,128)}, f32[64,792]{1,0:T(8,128)S(1)}, u32[]{:S(2)}, u32[]{:S(2)}) collective-permute-start(f32[64,792]{1,0:T(8,128)} %get-tuple-element.14), channel_id=1, source_target_pairs={{0,12},{4,8},{8,4},{12,0},{16,28},{20,24},{24,20},{28,16},{1,13},{... | collective-permute-start | bytes 608264 | tf_op jit(solution)/shard_map/ppermute | solution.py:59
  44.6 17.2 %collective-permute-start.13 = (f32[64,792]{1,0:T(8,128)}, f32[64,792]{1,0:T(8,128)S(1)}, u32[]{:S(2)}, u32[]{:S(2)}) collective-permute-start(f32[64,792]{1,0:T(8,128)} %get-tuple-element.14), channel_id=1, source_target_pairs={{0,16},{4,20},{8,24},{12,28},{16,0},{20,4},{24,8},{28,12},{1,17},{... | collective-permute-start | bytes 608264 | tf_op jit(solution)/shard_map/ppermute | solution.py:59
  51.7 15.0 %collective-permute-start.14 = (f32[64,792]{1,0:T(8,128)}, f32[64,792]{1,0:T(8,128)S(1)}, u32[]{:S(2)}, u32[]{:S(2)}) collective-permute-start(f32[64,792]{1,0:T(8,128)} %get-tuple-element.14), channel_id=1, source_target_pairs={{0,20},{4,16},{8,28},{12,24},{16,4},{20,0},{24,12},{28,8},{1,21},{... | collective-permute-start | bytes 608264 | tf_op jit(solution)/shard_map/ppermute | solution.py:59
  61.7 17.1 %collective-permute-start.15 = (f32[64,792]{1,0:T(8,128)}, f32[64,792]{1,0:T(8,128)S(1)}, u32[]{:S(2)}, u32[]{:S(2)}) collective-permute-start(f32[64,792]{1,0:T(8,128)} %get-tuple-element.14), channel_id=1, source_target_pairs={{0,24},{4,28},{8,16},{12,20},{16,8},{20,12},{24,0},{28,4},{1,25},{... | collective-permute-start | bytes 608264 | tf_op jit(solution)/shard_map/ppermute | solution.py:59
  66.7 21.2 %collective-permute-start.16 = (f32[64,792]{1,0:T(8,128)}, f32[64,792]{1,0:T(8,128)S(1)}, u32[]{:S(2)}, u32[]{:S(2)}) collective-permute-start(f32[64,792]{1,0:T(8,128)} %get-tuple-element.14), channel_id=1, source_target_pairs={{0,28},{4,24},{8,20},{12,16},{16,12},{20,8},{24,4},{28,0},{1,29},{... | collective-permute-start | bytes 608264 | tf_op jit(solution)/shard_map/ppermute | solution.py:59
  91.0 0.8 copy-start.16
  91.2 2.1 %copy-start.10 = (f32[64,792]{1,0:T(8,128)}, f32[64,792]{1,0:T(8,128)S(1)}, u32[]{:S(2)}) copy-start(f32[64,792]{1,0:T(8,128)S(1)} %get-tuple-element.23) | copy-start | bytes 608260
  91.2 2.1 %copy-start.11 = (f32[64,792]{1,0:T(8,128)}, f32[64,792]{1,0:T(8,128)S(1)}, u32[]{:S(2)}) copy-start(f32[64,792]{1,0:T(8,128)S(1)} %get-tuple-element.24) | copy-start | bytes 608260
  94.3 5.4 %copy-start.18 = (f32[64,12]{1,0:T(8,128)S(1)}, f32[64,12]{1,0:T(8,128)}, u32[]{:S(2)}) copy-start(f32[64,12]{1,0:T(8,128)} %get-tuple-element.9) | copy-start | bytes 9220
  101.7 3.0 %copy-start.19 = (f32[64,12]{1,0:T(8,128)S(1)}, f32[64,12]{1,0:T(8,128)}, u32[]{:S(2)}) copy-start(f32[64,12]{1,0:T(8,128)} %get-tuple-element.2) | copy-start | bytes 9220
  112.8 1.0 copy-start.8
  112.8 1.1 copy-start.9
  116.8 2.7 %copy-start.2 = (bf16[4,64,12,64]{3,2,1,0:T(8,128)(2,1)S(1)}, bf16[4,64,12,64]{3,2,1,0:T(8,128)(2,1)}, u32[]{:S(2)}) copy-start(bf16[4,64,12,64]{3,2,1,0:T(8,128)(2,1)} %reshape.162) | copy-start | bytes 1179652
  116.8 2.7 %copy-start.12 = (pred[4,64,256]{2,1,0:T(8,128)(4,1)S(1)}, pred[4,64,256]{2,1,0:T(8,128)(4,1)}, u32[]{:S(2)}) copy-start(pred[4,64,256]{2,1,0:T(8,128)(4,1)} %fusion.40) | copy-start | bytes 196612
  119.5 2.2 %copy-start.20 = (f32[4,12,64]{2,0,1:T(4,128)S(1)}, f32[4,12,64]{2,0,1:T(4,128)}, u32[]{:S(2)}) copy-start(f32[4,12,64]{2,0,1:T(4,128)} %get-tuple-element.37) | copy-start | bytes 36868
  121.7 1.4 %copy-start.4 = (bf16[4,256,768]{1,2,0:T(8,128)(2,1)S(1)}, bf16[4,256,768]{1,2,0:T(8,128)(2,1)}, u32[]{:S(2)}) copy-start(bf16[4,256,768]{1,2,0:T(8,128)(2,1)} %copy.42) | copy-start | bytes 4718596
  123.1 1.4 %copy-start.3 = (f32[12,64,4,64]{3,1,2,0:T(8,128)S(1)}, f32[12,64,4,64]{3,1,2,0:T(8,128)}, u32[]{:S(2)}) copy-start(f32[12,64,4,64]{3,1,2,0:T(8,128)} %get-tuple-element.38) | copy-start | bytes 2359300
  124.4 0.9 copy-start.17
  125.7 1.9 %copy-start.14 = (bf16[64,768]{1,0:T(8,128)(2,1)S(1)}, bf16[64,768]{1,0:T(8,128)(2,1)}, u32[]{:S(2)}) copy-start(bf16[64,768]{1,0:T(8,128)(2,1)} %copy-done.13) | copy-start | bytes 294916
  127.6 3.1 %copy-start.24 = (f32[768]{0:T(1024)S(1)}, f32[768]{0:T(1024)}, u32[]{:S(2)}) copy-start(f32[768]{0:T(1024)} %param.16) | copy-start | bytes 9220
  130.7 7.8 %copy-start.22 = (f32[768]{0:T(1024)S(1)}, f32[768]{0:T(1024)}, u32[]{:S(2)}) copy-start(f32[768]{0:T(1024)} %param.19) | copy-start | bytes 9220

commit v3 on v2

--- a/solution.py
+++ b/solution.py
@@ -34,16 +34,63 @@
     return jnp.dot(values, weight, preferred_element_type=jnp.float32).astype(jnp.bfloat16)
 
 
+def head_matrix():
+    lanes = jnp.arange(HEADS * HEAD_DIM, dtype=jnp.int32) // HEAD_DIM
+    return (lanes[None, :] == jnp.arange(HEADS, dtype=jnp.int32)[:, None]).astype(jnp.float32)
+
+
 def head_sum(values):
     dims = values.shape[:-1]
-    return values.reshape(dims + (HEADS, HEAD_DIM)).sum(-1)
+    flat = values.reshape(-1, values.shape[-1])
+    out = jnp.dot(flat, head_matrix().T, precision=lax.Precision.HIGHEST,
+                  preferred_element_type=jnp.float32)
+    return out.reshape(dims + (HEADS,))
 
 
 def head_spread(values):
     dims = values.shape[:-1]
-    return jnp.broadcast_to(values[..., None], dims + (HEADS, HEAD_DIM)).reshape(
-        dims + (HEADS * HEAD_DIM,)
-    )
+    flat = values.reshape(-1, HEADS)
+    out = jnp.dot(flat, head_matrix(), precision=lax.Precision.HIGHEST,
+                  preferred_element_type=jnp.float32)
+    return out.reshape(dims + (HEADS * HEAD_DIM,))
+
+
+def partner(value, axis, step, count):
+    return lax.ppermute(value, axis, [(i, i ^ step) for i in range(count)])
+
+
+def broadcast_from(value, axis, count, source):
+    here = lax.axis_index(axis)
+    step = 1
+    while step < count:
+        got = partner(value, axis, step, count)
+        value = jnp.where(here // step == source // step, value, got)
+        step *= 2
+    return value
+
+
+def merge(lo, hi, width):
+    top = jnp.maximum(lo[:, width + HEADS :], hi[:, width + HEADS :])
+    fade_lo = jnp.exp(lo[:, width + HEADS :] - top)
+    fade_hi = jnp.exp(hi[:, width + HEADS :] - top)
+    total = lo[:, width : width + HEADS] * fade_lo + hi[:, width : width + HEADS] * fade_hi
+    fades = head_spread(jnp.concatenate([fade_lo, fade_hi], axis=0))
+    rows = lo.shape[0]
+    mixed = lo[:, :width] * fades[:rows] + hi[:, :width] * fades[rows:]
+    return jnp.concatenate([mixed, total, top], axis=-1)
+
+
+def all_merge(value, axis, count, width):
+    here = lax.axis_index(axis)
+    step = 1
+    while step < count:
+        got = partner(value, axis, step, count)
+        low_side = (here & step) == 0
+        lo = jnp.where(low_side, value, got)
+        hi = jnp.where(low_side, got, value)
+        value = merge(lo, hi, width)
+        step *= 2
+    return value
 
 
 def fan_out(value, axis, count):
@@ -68,10 +115,7 @@
     flat_cells = cells.reshape(row_count * cols_dev, model_width)
     w_kv = w_qkv[:, model_width:]
 
-    tokens = summary[0]
-    for source, got in fan_out(summary[0], "band", n_band):
-        tokens = jnp.where(source == owner[0], got, tokens)
-    tokens = jnp.where(own_band == owner[0], summary[0], tokens)
+    tokens = broadcast_from(summary[0], "band", n_band, owner[0])
     row_parts = fan_out(cells, "col", n_col)
 
     qkv_cells = project(flat_cells, w_qkv).reshape(row_count, cols_dev, 3 * model_width)
@@ -93,21 +137,13 @@
     part_mixed = (col_weights * own_vals.astype(jnp.float32)).sum(0)
     part_total = col_exp.sum(0)
     packed = jnp.concatenate([part_mixed, part_total, part_top], axis=-1)
-    stacked = jnp.stack([packed] + [got for _, got in fan_out(packed, "band", n_band)])
-    stacked = jnp.take(stacked, jnp.arange(n_band, dtype=jnp.int32) ^ own_band, axis=0)
-    parts = [stacked[k] for k in range(n_band)]
-    tops = [p[:, model_width + HEADS :] for p in parts]
-    col_top = self_scores
-    for t in tops:
-        col_top = jnp.maximum(col_top, t)
+    packed = all_merge(packed, "band", n_band, model_width)
+    col_top = jnp.maximum(packed[:, model_width + HEADS :], self_scores)
+    fade = jnp.exp(packed[:, model_width + HEADS :] - col_top)
     self_exp = jnp.exp(self_scores - col_top)
-    col_total = self_exp
-    self_weights = head_spread(self_exp.astype(jnp.bfloat16).astype(jnp.float32))
-    col_mixed = self_weights * sum_vals.astype(jnp.float32)
-    for p, t in zip(parts, tops):
-        fade = jnp.exp(t - col_top)
-        col_total = col_total + fade * p[:, model_width : model_width + HEADS]
-        col_mixed = col_mixed + head_spread(fade) * p[:, :model_width]
+    col_total = packed[:, model_width : model_width + HEADS] * fade + self_exp
+    spreads = head_spread(jnp.concatenate([fade, self_exp.astype(jnp.bfloat16).astype(jnp.float32)], axis=0))
+    col_mixed = packed[:, :model_width] * spreads[:cols_dev] + spreads[cols_dev:] * sum_vals.astype(jnp.float32)
     summary_att = (col_mixed / head_spread(col_total)).astype(jnp.bfloat16)
 
     sources = [own_group] + [s for s, _ in row_parts]

time: 141 us -> 105 us (0.74)
  the two profiles are of different devices: /device:TPU:9 before, /device:TPU:0 now
where the time goes in v3:
time: 105 us
  waiting for transfers between devices  34 us (32%)
  matrix products  29.4 us (28%)
  local copies, waits for them, and re-layouts  16.3 us (16%)
  starting transfers between devices  12.5 us (12%)
  other arithmetic  10.5 us (10%)
  between operations  1.82 us (2%)
    ppermute x6, waiting for transfers between devices, partner(): return lax.ppermute(value, axis, [(i, i ^ step) for i in range(count)])  34 us
    dot_general x3, matrix products, project(): jnp.dot(values, weight, preferred_element_type=jnp.float32)  8.73 us
    ppermute x6, starting transfers between devices, partner(): return lax.ppermute(value, axis, [(i, i ^ step) for i in range(count)])  7.9 us
    dot_general x1, matrix products, finish(): outer_out = jnp.dot(inner_act, w_down, preferred_element_type=jnp.float32)  7.54 us
    ppermute x3, starting transfers between devices, fan_out(): got.append((source, lax.ppermute(value, axis, pairs)))  4.6 us
    dot_general x6, matrix products, head_spread(): jnp.dot(flat, head_matrix(), precision=lax.Precision.HIGHEST, preferred_e...  3.66 us
    dot_general x1, matrix products, local(): jnp.einsum('rqhd,khd->rhqk', q4, sk, preferred_element_type=jnp.float32)  3.13 us
    concatenate x1, local copies, waits for them, and re-layouts, local(): row_vals = jnp.concatenate([own_vals, other_kv[:, :, model_width:]], axis=1)  2.58 us
  transfers between devices with their start and end apart: 9, of which 4 were waited for; matrix products, arithmetic and copies ran while one was open for 38% of the time, Pallas kernels for 0%

profile of v3, /device:TPU:0, one launch (start us, length us, event | category | flops | bytes accessed | tf_op | source)
XLA Modules:
  0.0 104.5 jit_solution(16571208160419595895)
XLA Ops:
  0.6 0.0 copy-start
  0.6 4.0 %collective-permute-start.5 = (bf16[4,64,768]{2,1,0:T(8,128)(2,1)}, bf16[4,64,768]{2,1,0:T(8,128)(2,1)}, u32[]{:S(2)}, u32[]{:S(2)}) collective-permute-start(bf16[4,64,768]{2,1,0:T(8,128)(2,1)} %param.10), channel_id=1, source_target_pairs={{0,3},{1,2},{2,1},{3,0},{4,7},{5,6},{6,5},{7,4},{8,11},{9,10},{10,... | collective-permute-start | bytes 1179656 | tf_op jit(solution)/shard_map/ppermute | solution.py:106
  4.6 0.5 collective-permute-start.4
  5.1 0.1 collective-permute-start.3
  5.9 3.2 %convolution_convert_fusion = bf16[256,2304]{1,0:T(8,128)(2,1)S(1)} fusion(bf16[256,768]{1,0:T(8,128)(2,1)} %bitcast.71, bf16[768,2304]{1,0:T(8,128)(2,1)} %param.14), kind=kOutput, calls=%fused_computation.9 | convolution fusion | flops 906559488 | bytes 5111808 | tf_op jit(solution)/shard_map/dot_general | solution.py:34
  9.2 1.0 fusion.111
  10.2 0.1 pad_add_fusion
  10.3 0.7 broadcast_select_fusion.6
  11.0 2.0 %collective-permute-start.1 = (bf16[64,768]{1,0:T(8,128)(2,1)}, bf16[64,768]{1,0:T(8,128)(2,1)}, u32[]{:S(2)}, u32[]{:S(2)}) collective-permute-start(bf16[64,768]{1,0:T(8,128)(2,1)} %broadcast_select_fusion.6), channel_id=1, source_target_pairs={{0,8},{4,12},{8,0},{12,4},{16,24},{20,28},{24,16},{28,20},{1,9},{5... | collective-permute-start | bytes 294920 | tf_op jit(solution)/shard_map/ppermute | solution.py:59
  12.9 0.1 fusion.51
  13.1 1.7 %reshape.106 = bf16[4,64,12,64]{3,2,1,0:T(8,128)(2,1)S(1)} reshape(bf16[4,64,768]{2,1,0:T(8,128)(2,1)} %get-tuple-element.16) | data formatting | bytes 786432 | tf_op jit(solution)/shard_map/reshape | solution.py:157
  14.8 1.9 %collective-permute-done.1 = bf16[64,768]{1,0:T(8,128)(2,1)} collective-permute-done((bf16[64,768]{1,0:T(8,128)(2,1)}, bf16[64,768]{1,0:T(8,128)(2,1)}, u32[]{:S(2)}, u32[]{:S(2)}) %collective-permute-start.1) | collective-permute-done | bytes 98336 | tf_op jit(solution)/shard_map/ppermute | solution.py:59
  16.7 0.9 broadcast_select_fusion.7
  17.6 2.8 %collective-permute-start.2 = (bf16[64,768]{1,0:T(8,128)(2,1)S(1)}, bf16[64,768]{1,0:T(8,128)(2,1)S(1)}, u32[]{:S(2)}, u32[]{:S(2)}) collective-permute-start(bf16[64,768]{1,0:T(8,128)(2,1)S(1)} %broadcast_select_fusion.7), channel_id=1, source_target_pairs={{0,16},{4,20},{8,24},{12,28},{16,0},{20,4},{24,8},{28,12},{1,17},{... | collective-permute-start | bytes 294920 | tf_op jit(solution)/shard_map/ppermute | solution.py:59
  20.5 4.8 %collective-permute-done.2 = bf16[64,768]{1,0:T(8,128)(2,1)S(1)} collective-permute-done((bf16[64,768]{1,0:T(8,128)(2,1)S(1)}, bf16[64,768]{1,0:T(8,128)(2,1)S(1)}, u32[]{:S(2)}, u32[]{:S(2)}) %collective-permute-start.2) | collective-permute-done | bytes 98336 | tf_op jit(solution)/shard_map/ppermute | solution.py:59
  25.3 3.5 %convolution_convert_fusion.1 = bf16[64,2304]{0,1:T(8,128)(2,1)S(1)} fusion(bf16[64,768]{1,0:T(8,128)(2,1)S(1)} %broadcast_select_fusion.8, bf16[768,2304]{1,0:T(8,128)(2,1)} %param.14), kind=kOutput, calls=%fused_computation.10 | convolution fusion | flops 226639872 | bytes 3932160 | tf_op jit(solution)/shard_map/dot_general | solution.py:34
  28.8 0.8 copy-done.4
  29.6 0.9 fusion.112
  30.5 1.8 %copy.118 = f32[64,768]{1,0:T(8,128)} copy(f32[64,768]{0,1:T(8,128)} %get-tuple-element.26) | data formatting | bytes 393216 | tf_op jit(solution)/shard_map/convert_element_type | solution.py:131
  32.4 1.6 %fusion.113 = (f32[64,12]{0,1:T(8,128)S(1)}, f32[4,64,12]{1,2,0:T(8,128)S(1)}) fusion(s32[768]{0:T(1024)S(1)} %add_select_fusion, f32[64,768]{1,0:T(8,128)} %copy.118, bf16[4,64,2304]{2,1,0:T(8,128)(2,1)S(1)} %bitcast.65), kind=kOutput, calls=%fused_computation.180 | convolution fusion | flops 28719360 | bytes 609280 | tf_op jit(solution)/shard_map/dot_general | solution.py:45
  34.0 1.0 fusion.32
  34.9 1.1 %copy.119 = f32[64,768]{0,1:T(8,128)S(1)} copy(f32[64,768]{1,0:T(8,128)} %fusion.32) | data formatting | bytes 393216 | tf_op jit(solution)/shard_map/reduce_sum | solution.py:137
  36.0 0.8 pad_maximum_fusion.3
  36.8 3.1 %bitcast_reduce_fusion = (f32[4,12,64]{2,0,1:T(4,128)S(1)}, f32[12,64,4,64]{3,1,2,0:T(8,128)}) fusion(bf16[64,12,64,1]{0,2,3,1:T(8,128)(2,1)} %bitcast.69, bf16[4,64,12,64]{3,2,1,0:T(8,128)(2,1)S(1)} %reshape.106), kind=kOutput, calls=%fused_computation.30 | convolution fusion | flops 25555968 | bytes 1290240 | tf_op jit(solution)/shard_map/rqhd,khd->rhqk/dot_general | solution.py:174
  40.0 1.3 %pad_maximum_fusion.2 = bf16[4,192,768]{2,1,0:T(8,128)(2,1)S(1)} fusion(bf16[4,64,768]{2,1,0:T(8,128)(2,1)} %collective-permute-done.5, bf16[4,64,768]{2,1,0:T(8,128)(2,1)} %collective-permute-done.4, bf16[4,64,768]{2,1,0:T(8,128)(2,1)} %collective-permute-done.3), kind=kLoop, calls=%fused_computation.43 | loop fusion | flops 3538944 | bytes 2359296 | tf_op jit(solution)/shard_map/concatenate | solution.py:150
  41.3 2.0 %convolution_convert_fusion.2 = bf16[768,1536]{1,0:T(8,128)(2,1)S(1)} fusion(bf16[768,768]{1,0:T(8,128)(2,1)S(1)} %bitcast.68, bf16[768,2304]{1,0:T(8,128)(2,1)S(1)} %copy-done.3), kind=kOutput, calls=%fused_computation.11 | convolution fusion | flops 1813118976 | bytes 5898240 | tf_op jit(solution)/shard_map/dot_general | solution.py:34
  43.3 0.2 fusion.110
  43.5 0.8 copy-done.6
  44.3 0.1 copy-done.7
  44.4 1.9 %pad_maximum_fusion = (bf16[4,256,768]{2,1,0:T(8,128)(2,1)}, bf16[4,256,768]{2,1,0:T(8,128)(2,1)}) fusion(bf16[4,192,768]{2,1,0:T(8,128)(2,1)S(1)} %get-tuple-element.13, bf16[4,64,768]{2,1,0:T(8,128)(2,1)S(1)} %copy-done.7, bf16[4,192,768]{2,1,0:T(8,128)(2,1)S(1)} %get-tuple-element.12, bf16[4,64,768]{2,1,0:T(8,128)(2,1)S(1)} %copy-done.6), kind=kLoop, calls=%fused_computation.24 | loop fusion | flops 6291456 | bytes 6291456 | tf_op jit(solution)/shard_map/concatenate | solution.py:155
  46.3 2.6 %copy.104 = bf16[4,256,768]{1,2,0:T(8,128)(2,1)} copy(bf16[4,256,768]{2,1,0:T(8,128)(2,1)} %get-tuple-element.42) | data formatting | bytes 3145728 | tf_op jit(solution)/shard_map/concatenate | solution.py:155
  48.9 2.6 %copy.105 = bf16[4,256,768]{1,2,0:T(8,128)(2,1)} copy(bf16[4,256,768]{2,1,0:T(8,128)(2,1)} %get-tuple-element.43) | data formatting | bytes 3145728 | tf_op jit(solution)/shard_map/concatenate | solution.py:154
  51.5 2.1 %fusion.8 = (f32[4,12,64]{2,1,0:T(8,128)S(1)}, f32[4,12,64,256]{3,2,1,0:T(8,128)S(1)}) fusion(pred[4,64,256]{2,1,0:T(8,128)(4,1)S(1)} %fusion.51, bf16[4,256,12,64]{1,3,2,0:T(8,128)(2,1)} %bitcast.63, bf16[4,64,12,64]{3,2,1,0:T(8,128)(2,1)S(1)} %reshape.106), kind=kOutput, calls=%fused_computation.14 | convolution fusion | flops 103019520 | bytes 5189632 | tf_op jit(solution)/shard_map/rqhd,rkhd->rhqk/dot_general | solution.py:170
  53.7 1.2 %fusion.9 = f32[4,12,64]{2,1,0:T(8,128)S(1)} fusion(f32[4,12,64,256]{3,2,1,0:T(8,128)S(1)} %get-tuple-element.35, f32[4,12,64]{2,1,0:T(8,128)S(1)} %copy_maximum_fusion, pred[4,64,256]{2,1,0:T(8,128)(4,1)S(1)} %fusion.51), kind=kLoop, calls=%fused_computation.15 | loop fusion | flops 3142656 | bytes 3235840 | tf_op jit(solution)/shard_map/reduce_sum | solution.py:179
  54.9 0.1 copy-done.2
  55.0 1.3 %fusion.18 = f32[4,12,64,64]{3,2,1,0:T(8,128)S(1)} fusion(bf16[4,256,12,64]{1,3,2,0:T(8,128)(2,1)S(1)} %bitcast.62, f32[4,12,64,256]{3,2,1,0:T(8,128)S(1)} %get-tuple-element.35, f32[4,12,64]{2,1,0:T(8,128)S(1)} %copy_maximum_fusion, pred[4,64,256]{2,1,0:T(8,128)(4,1)S(1)} %fusion.51), kind=kOutput, calls=%fused_computation.23 | convolution fusion | flops 103809024 | bytes 5582848 | tf_op jit(solution)/shard_map/rhqk,rkhd->rqhd/dot_general | solution.py:180
  56.3 0.1 copy-done.1
  56.4 0.4 fusion.27
  56.9 0.1 broadcast_select_fusion.1
  57.0 0.5 fusion.55
  57.5 0.2 fusion.47
  57.7 0.8 collective-permute-start.7
  58.5 11.1 %collective-permute-done.7 = f32[64,792]{0,1:T(8,128)S(1)} collective-permute-done((f32[64,792]{0,1:T(8,128)S(1)}, f32[64,792]{0,1:T(8,128)S(1)}, u32[]{:S(2)}, u32[]{:S(2)}) %collective-permute-start.7) | collective-permute-done | bytes 202784 | tf_op jit(solution)/shard_map/ppermute | solution.py:59
  69.6 0.1 broadcast_select_fusion.3
  69.6 0.5 fusion.54
  70.2 0.2 fusion.46
  70.3 0.8 pad_maximum_fusion.5
  71.1 2.3 %collective-permute-start.8 = (f32[64,792]{0,1:T(8,128)}, f32[64,792]{0,1:T(8,128)S(1)}, u32[]{:S(2)}, u32[]{:S(2)}) collective-permute-start(f32[64,792]{0,1:T(8,128)} %pad_maximum_fusion.5), channel_id=1, source_target_pairs={{0,16},{4,20},{8,24},{12,28},{16,0},{20,4},{24,8},{28,12},{1,17},{... | collective-permute-start | bytes 608264 | tf_op jit(solution)/shard_map/ppermute | solution.py:59
  73.5 0.4 fusion.21
  73.8 0.6 copy.117
  74.5 1.2 %convert_element_type.79 = bf16[256,768]{0,1:T(8,128)(2,1)} reshape(bf16[4,64,12,64]{1,0,3,2:T(4,128)(2,1)S(1)} %copy.117) | data formatting | bytes 786432 | tf_op jit(solution)/shard_map/convert_element_type | solution.py:187
  75.7 16.2 %collective-permute-done.8 = f32[64,792]{0,1:T(8,128)S(1)} collective-permute-done((f32[64,792]{0,1:T(8,128)}, f32[64,792]{0,1:T(8,128)S(1)}, u32[]{:S(2)}, u32[]{:S(2)}) %collective-permute-start.8) | collective-permute-done | bytes 202784 | tf_op jit(solution)/shard_map/ppermute | solution.py:59
  91.9 0.1 broadcast_select_fusion.4
  92.0 0.3 fusion.73
  92.3 0.5 fusion.52
  92.9 0.5 fusion.53
  93.4 0.6 fusion.33
  94.1 0.7 fusion.62
  94.8 0.3 multiply_reduce_fusion.1
  95.1 7.5 %fusion.114 = (f32[320]{0:T(512)S(1)}, f32[320,768]{1,0:T(8,128)S(1)}) fusion(bf16[3072,768]{1,0:T(8,128)(2,1)} %param.18, bf16[768,3072]{1,0:T(8,128)(2,1)} %param.17, f32[768]{0:T(1024)S(1)} %copy-done.16, f32[320]{0:T(512)S(1)} %add_rsqrt_fusion.1, f32[320]{0:T(512)S(1)} %broadcast_multiply_fusion.1, f32[320,768]{1,0:T(8,128)S(1)} %get-tuple-element.39, ...), kind=kOutput, calls=%fused_computation.181 | convolution fusion | flops 3033906944 | bytes 11901696 | tf_op jit(solution)/shard_map/dot_general | solution.py:29
  102.6 0.3 multiply_reduce_fusion
  102.9 0.2 multiply_convert_fusion
  103.1 0.8 slice.188
  103.9 0.6 slice.189
  (54 shorter events, 0.3 us)
Async XLA Ops:
  0.6 93.4 %copy-start = (bf16[768,768]{1,0:T(8,128)(2,1)S(1)}, bf16[768,768]{1,0:T(8,128)(2,1)}, u32[]{:S(2)}) copy-start(bf16[768,768]{1,0:T(8,128)(2,1)} %param.15) | copy-start | bytes 3538948
  0.6 39.3 %collective-permute-start.5 = (bf16[4,64,768]{2,1,0:T(8,128)(2,1)}, bf16[4,64,768]{2,1,0:T(8,128)(2,1)}, u32[]{:S(2)}, u32[]{:S(2)}) collective-permute-start(bf16[4,64,768]{2,1,0:T(8,128)(2,1)} %param.10), channel_id=1, source_target_pairs={{0,3},{1,2},{2,1},{3,0},{4,7},{5,6},{6,5},{7,4},{8,11},{9,10},{10,... | collective-permute-start | bytes 1179656 | tf_op jit(solution)/shard_map/ppermute | solution.py:106
  4.6 35.4 %collective-permute-start.4 = (bf16[4,64,768]{2,1,0:T(8,128)(2,1)}, bf16[4,64,768]{2,1,0:T(8,128)(2,1)}, u32[]{:S(2)}, u32[]{:S(2)}) collective-permute-start(bf16[4,64,768]{2,1,0:T(8,128)(2,1)} %param.10), channel_id=1, source_target_pairs={{0,2},{1,3},{2,0},{3,1},{4,6},{5,7},{6,4},{7,5},{8,10},{9,11},{10,... | collective-permute-start | bytes 1179656 | tf_op jit(solution)/shard_map/ppermute | solution.py:106
  5.1 34.9 %collective-permute-start.3 = (bf16[4,64,768]{2,1,0:T(8,128)(2,1)}, bf16[4,64,768]{2,1,0:T(8,128)(2,1)}, u32[]{:S(2)}, u32[]{:S(2)}) collective-permute-start(bf16[4,64,768]{2,1,0:T(8,128)(2,1)} %param.10), channel_id=1, source_target_pairs={{0,1},{1,0},{2,3},{3,2},{4,5},{5,4},{6,7},{7,6},{8,9},{9,8},{10,11... | collective-permute-start | bytes 1179656 | tf_op jit(solution)/shard_map/ppermute | solution.py:106
  5.3 5.0 %collective-permute-start = (bf16[64,768]{1,0:T(8,128)(2,1)}, bf16[64,768]{1,0:T(8,128)(2,1)S(1)}, u32[]{:S(2)}, u32[]{:S(2)}) collective-permute-start(bf16[64,768]{1,0:T(8,128)(2,1)} %bitcast.76), channel_id=1, source_target_pairs={{0,4},{4,0},{8,12},{12,8},{16,20},{20,16},{24,28},{28,24},{1,5},{5... | collective-permute-start | bytes 294920 | tf_op jit(solution)/shard_map/ppermute | solution.py:59
  9.1 1.2 %copy-start.13 = (bf16[1,64,768]{2,1,0:T(8,128)(2,1)S(1)}, bf16[1,64,768]{2,1,0:T(8,128)(2,1)}, u32[]{:S(2)}) copy-start(bf16[1,64,768]{2,1,0:T(8,128)(2,1)} %param.11) | copy-start | bytes 294916
  9.2 3.8 %copy-start.15 = (s32[4,64]{1,0:T(4,128)S(1)}, s32[4,64]{1,0:T(4,128)}, u32[]{:S(2)}) copy-start(s32[4,64]{1,0:T(4,128)} %param.13) | copy-start | bytes 3076
  11.0 5.7 %collective-permute-start.1 = (bf16[64,768]{1,0:T(8,128)(2,1)}, bf16[64,768]{1,0:T(8,128)(2,1)}, u32[]{:S(2)}, u32[]{:S(2)}) collective-permute-start(bf16[64,768]{1,0:T(8,128)(2,1)} %broadcast_select_fusion.6), channel_id=1, source_target_pairs={{0,8},{4,12},{8,0},{12,4},{16,24},{20,28},{24,16},{28,20},{1,9},{5... | collective-permute-start | bytes 294920 | tf_op jit(solution)/shard_map/ppermute | solution.py:59
  17.6 7.6 %collective-permute-start.2 = (bf16[64,768]{1,0:T(8,128)(2,1)S(1)}, bf16[64,768]{1,0:T(8,128)(2,1)S(1)}, u32[]{:S(2)}, u32[]{:S(2)}) collective-permute-start(bf16[64,768]{1,0:T(8,128)(2,1)S(1)} %broadcast_select_fusion.7), channel_id=1, source_target_pairs={{0,16},{4,20},{8,24},{12,28},{16,0},{20,4},{24,8},{28,12},{1,17},{... | collective-permute-start | bytes 294920 | tf_op jit(solution)/shard_map/ppermute | solution.py:59
  25.3 5.3 %copy-start.8 = (bf16[64,768]{1,0:T(8,128)(2,1)}, bf16[64,768]{1,0:T(8,128)(2,1)S(1)}, u32[]{:S(2)}) copy-start(bf16[64,768]{1,0:T(8,128)(2,1)S(1)} %broadcast_select_fusion.8) | copy-start | bytes 294916
  28.8 0.8 copy-start.4
  36.8 20.0 %collective-permute-start.6 = (f32[64,792]{0,1:T(8,128)}, f32[64,792]{0,1:T(8,128)S(1)}, u32[]{:S(2)}, u32[]{:S(2)}) collective-permute-start(f32[64,792]{0,1:T(8,128)} %pad_maximum_fusion.3), channel_id=1, source_target_pairs={{0,4},{4,0},{8,12},{12,8},{16,20},{20,16},{24,28},{28,24},{1,5},{5... | collective-permute-start | bytes 608264 | tf_op jit(solution)/shard_map/ppermute | solution.py:59
  36.8 4.5 %copy-start.3 = (bf16[768,2304]{1,0:T(8,128)(2,1)S(1)}, bf16[768,2304]{1,0:T(8,128)(2,1)}, u32[]{:S(2)}) copy-start(bf16[768,2304]{1,0:T(8,128)(2,1)} %param.14) | copy-start | bytes 10616836
  43.3 1.0 copy-start.6
  43.3 1.1 %copy-start.7 = (bf16[4,64,768]{2,1,0:T(8,128)(2,1)S(1)}, bf16[4,64,768]{2,1,0:T(8,128)(2,1)}, u32[]{:S(2)}) copy-start(bf16[4,64,768]{2,1,0:T(8,128)(2,1)} %get-tuple-element.18) | copy-start | bytes 1179652
  53.6 1.4 %copy-start.2 = (bf16[4,256,768]{1,2,0:T(8,128)(2,1)S(1)}, bf16[4,256,768]{1,2,0:T(8,128)(2,1)}, u32[]{:S(2)}) copy-start(bf16[4,256,768]{1,2,0:T(8,128)(2,1)} %copy.104) | copy-start | bytes 4718596
  55.0 1.4 %copy-start.1 = (f32[12,64,4,64]{3,1,2,0:T(8,128)S(1)}, f32[12,64,4,64]{3,1,2,0:T(8,128)}, u32[]{:S(2)}) copy-start(f32[12,64,4,64]{3,1,2,0:T(8,128)} %get-tuple-element.37) | copy-start | bytes 2359300
  57.7 11.8 %collective-permute-start.7 = (f32[64,792]{0,1:T(8,128)S(1)}, f32[64,792]{0,1:T(8,128)S(1)}, u32[]{:S(2)}, u32[]{:S(2)}) collective-permute-start(f32[64,792]{0,1:T(8,128)S(1)} %pad_maximum_fusion.4), channel_id=1, source_target_pairs={{0,8},{4,12},{8,0},{12,4},{16,24},{20,28},{24,16},{28,20},{1,9},{5... | collective-permute-start | bytes 608264 | tf_op jit(solution)/shard_map/ppermute | solution.py:59
  58.5 15.0 %copy-start.12 = (bf16[64,768]{0,1:T(8,128)(2,1)S(1)}, bf16[64,768]{0,1:T(8,128)(2,1)}, u32[]{:S(2)}) copy-start(bf16[64,768]{0,1:T(8,128)(2,1)} %get-tuple-element.25) | copy-start | bytes 294916
  71.1 20.8 %collective-permute-start.8 = (f32[64,792]{0,1:T(8,128)}, f32[64,792]{0,1:T(8,128)S(1)}, u32[]{:S(2)}, u32[]{:S(2)}) collective-permute-start(f32[64,792]{0,1:T(8,128)} %pad_maximum_fusion.5), channel_id=1, source_target_pairs={{0,16},{4,20},{8,24},{12,28},{16,0},{20,4},{24,8},{28,12},{1,17},{... | collective-permute-start | bytes 608264 | tf_op jit(solution)/shard_map/ppermute | solution.py:59
  73.8 18.2 %copy-start.5 = (bf16[64,2304]{0,1:T(8,128)(2,1)S(1)}, bf16[64,2304]{0,1:T(8,128)(2,1)}, u32[]{:S(2)}) copy-start(bf16[64,2304]{0,1:T(8,128)(2,1)} %copy-done.4) | copy-start | bytes 884740
  92.0 2.0 %copy-start.9 = (bf16[64,768]{1,0:T(8,128)(2,1)S(1)}, bf16[64,768]{1,0:T(8,128)(2,1)}, u32[]{:S(2)}) copy-start(bf16[64,768]{1,0:T(8,128)(2,1)} %copy-done.8) | copy-start | bytes 294916
  92.0 2.0 %copy-start.10 = (bf16[4,64,768]{2,1,0:T(8,128)(2,1)S(1)}, bf16[4,64,768]{2,1,0:T(8,128)(2,1)}, u32[]{:S(2)}) copy-start(bf16[4,64,768]{2,1,0:T(8,128)(2,1)} %param.10) | copy-start | bytes 1179652
  92.0 2.0 %copy-start.11 = (bf16[256,768]{0,1:T(8,128)(2,1)S(1)}, bf16[256,768]{0,1:T(8,128)(2,1)}, u32[]{:S(2)}) copy-start(bf16[256,768]{0,1:T(8,128)(2,1)} %convert_element_type.79) | copy-start | bytes 1179652
  94.0 1.0 copy-start.16
  95.1 7.8 %copy-start.14 = (f32[768]{0:T(1024)S(1)}, f32[768]{0:T(1024)}, u32[]{:S(2)}) copy-start(f32[768]{0:T(1024)} %param.19) | copy-start | bytes 9220

commit v4 on v3

--- a/solution.py
+++ b/solution.py
@@ -80,17 +80,36 @@
     return jnp.concatenate([mixed, total, top], axis=-1)
 
 
+def swap(value, axis, step, count, width, narrow):
+    if not narrow:
+        return value, partner(value, axis, step, count)
+    mixed = value[:, :width].astype(jnp.bfloat16)
+    stats = value[:, width:]
+    got_mixed = partner(mixed, axis, step, count)
+    got_stats = partner(stats, axis, step, count)
+    mine = jnp.concatenate([mixed.astype(jnp.float32), stats], axis=-1)
+    got = jnp.concatenate([got_mixed.astype(jnp.float32), got_stats], axis=-1)
+    return mine, got
+
+
 def all_merge(value, axis, count, width):
     here = lax.axis_index(axis)
-    step = 1
+    half = value.shape[0] // 2
+    first = (here & 1) == 0
+    mine = jnp.where(first, value[:half], value[half:])
+    sent = jnp.where(first, value[half:], value[:half])
+    got = partner(sent, axis, 1, count)
+    value = merge(jnp.where(first, mine, got), jnp.where(first, got, mine), width)
+    step = 2
     while step < count:
-        got = partner(value, axis, step, count)
+        mine, got = swap(value, axis, step, count, width, True)
         low_side = (here & step) == 0
-        lo = jnp.where(low_side, value, got)
-        hi = jnp.where(low_side, got, value)
+        lo = jnp.where(low_side, mine, got)
+        hi = jnp.where(low_side, got, mine)
         value = merge(lo, hi, width)
         step *= 2
-    return value
+    got = partner(value, axis, 1, count)
+    return jnp.where(first, jnp.concatenate([value, got]), jnp.concatenate([got, value]))
 
 
 def fan_out(value, axis, count):

time: 105 us -> 91.6 us (0.87)
  waiting for transfers between devices: 34 us -> 13.2 us
  other arithmetic: 10.5 us -> 13.2 us
  starting transfers between devices: 12.5 us -> 15.1 us
  matrix products: 29.4 us -> 31.1 us
    ppermute x6 -> x9, waiting for transfers between devices: 34 us -> 13.2 us  [partner(): return lax.ppermute(value, axis, [(i, i ^ step) for i in range(count)])]
    ppermute x6 -> x9, starting transfers between devices: 7.9 us -> 10.5 us  [partner(): return lax.ppermute(value, axis, [(i, i ^ step) for i in range(count)])]
    select_n x3 -> x5, other arithmetic: 0.18 us -> 1.68 us  [the longest x1 1.48 us: all_merge(): jnp.where(first, jnp.concatenate([value, got]), jnp.concatenate([got, val...]
    dot_general x1, matrix products: 0.35 us -> 1.76 us  [local(): jnp.einsum('rhqk,khd->rqhd', tok_exp.astype(jnp.bfloat16), sv, preferred_...]
  transfers between devices with their start and end apart: 9 -> 12, of which waited for: 4 -> 4; matrix products, arithmetic and copies ran while one was open for 38% -> 49% of each run, Pallas kernels for 0% -> 0%
where the time goes in v4:
time: 91.6 us; the launch traced here: 91 us
  matrix products  31.1 us (34%)
  local copies, waits for them, and re-layouts  16.5 us (18%)
  starting transfers between devices  15.1 us (16%)
  other arithmetic  13.2 us (14%)
  waiting for transfers between devices  13.2 us (14%)
  between operations  1.87 us (2%)
    ppermute x9, waiting for transfers between devices, partner(): return lax.ppermute(value, axis, [(i, i ^ step) for i in range(count)])  13.2 us
    ppermute x9, starting transfers between devices, partner(): return lax.ppermute(value, axis, [(i, i ^ step) for i in range(count)])  10.5 us
    dot_general x3, matrix products, project(): jnp.dot(values, weight, preferred_element_type=jnp.float32)  8.73 us
    dot_general x1, matrix products, finish(): outer_out = jnp.dot(inner_act, w_down, preferred_element_type=jnp.float32)  7.54 us
    ppermute x3, starting transfers between devices, fan_out(): got.append((source, lax.ppermute(value, axis, pairs)))  4.6 us
    dot_general x6, matrix products, head_spread(): jnp.dot(flat, head_matrix(), precision=lax.Precision.HIGHEST, preferred_e...  3.17 us
    dot_general x1, matrix products, local(): jnp.einsum('rqhd,khd->rhqk', q4, sk, preferred_element_type=jnp.float32)  3.16 us
    reduce_sum x2, other arithmetic, local(): row_total = cell_exp.sum(-1) + tok_exp.sum(-1)  2.67 us
  transfers between devices with their start and end apart: 12, of which 4 were waited for; matrix products, arithmetic and copies ran while one was open for 49% of the time, Pallas kernels for 0%

profile of v4, /device:TPU:0, one launch (start us, length us, event | category | flops | bytes accessed | tf_op | source)
XLA Modules:
  0.0 91.0 jit_solution(15015328974169677824)
XLA Ops:
  0.6 4.0 %collective-permute-start.5 = (bf16[4,64,768]{2,1,0:T(8,128)(2,1)}, bf16[4,64,768]{2,1,0:T(8,128)(2,1)}, u32[]{:S(2)}, u32[]{:S(2)}) collective-permute-start(bf16[4,64,768]{2,1,0:T(8,128)(2,1)} %param.10), channel_id=1, source_target_pairs={{0,3},{1,2},{2,1},{3,0},{4,7},{5,6},{6,5},{7,4},{8,11},{9,10},{10,... | collective-permute-start | bytes 1179656 | tf_op jit(solution)/shard_map/ppermute | solution.py:125
  4.6 0.5 collective-permute-start.4
  5.1 0.1 collective-permute-start.3
  5.9 3.2 %convolution_convert_fusion = bf16[256,2304]{1,0:T(8,128)(2,1)S(1)} fusion(bf16[256,768]{1,0:T(8,128)(2,1)} %bitcast.71, bf16[768,2304]{1,0:T(8,128)(2,1)} %param.14), kind=kOutput, calls=%fused_computation.9 | convolution fusion | flops 906559488 | bytes 5111808 | tf_op jit(solution)/shard_map/dot_general | solution.py:34
  9.2 1.0 %fusion.120 = (bf16[4,64,768]{2,1,0:T(8,128)(2,1)}, bf16[4,64,768]{2,1,0:T(8,128)(2,1)}, bf16[4,64,768]{2,1,0:T(8,128)(2,1)}) fusion(bf16[4,64,2304]{2,1,0:T(8,128)(2,1)S(1)} %bitcast.64), kind=kLoop, calls=%fused_computation.190 | loop fusion | bytes 2359296 | tf_op jit(solution)/shard_map/slice | solution.py:141
  10.3 0.7 broadcast_select_fusion
  11.0 2.0 %collective-permute-start.1 = (bf16[64,768]{1,0:T(8,128)(2,1)}, bf16[64,768]{1,0:T(8,128)(2,1)}, u32[]{:S(2)}, u32[]{:S(2)}) collective-permute-start(bf16[64,768]{1,0:T(8,128)(2,1)} %broadcast_select_fusion), channel_id=1, source_target_pairs={{0,8},{4,12},{8,0},{12,4},{16,24},{20,28},{24,16},{28,20},{1,9},{5... | collective-permute-start | bytes 294920 | tf_op jit(solution)/shard_map/ppermute | solution.py:59
  12.9 0.1 fusion.48
  13.1 1.7 %reshape.106 = bf16[4,64,12,64]{3,2,1,0:T(8,128)(2,1)S(1)} reshape(bf16[4,64,768]{2,1,0:T(8,128)(2,1)} %get-tuple-element.22) | data formatting | bytes 786432 | tf_op jit(solution)/shard_map/reshape | solution.py:176
  14.8 1.9 %collective-permute-done.1 = bf16[64,768]{1,0:T(8,128)(2,1)} collective-permute-done((bf16[64,768]{1,0:T(8,128)(2,1)}, bf16[64,768]{1,0:T(8,128)(2,1)}, u32[]{:S(2)}, u32[]{:S(2)}) %collective-permute-start.1) | collective-permute-done | bytes 98336 | tf_op jit(solution)/shard_map/ppermute | solution.py:59
  16.7 0.9 broadcast_select_fusion.1
  17.6 2.8 %collective-permute-start.2 = (bf16[64,768]{1,0:T(8,128)(2,1)S(1)}, bf16[64,768]{1,0:T(8,128)(2,1)S(1)}, u32[]{:S(2)}, u32[]{:S(2)}) collective-permute-start(bf16[64,768]{1,0:T(8,128)(2,1)S(1)} %broadcast_select_fusion.1), channel_id=1, source_target_pairs={{0,16},{4,20},{8,24},{12,28},{16,0},{20,4},{24,8},{28,12},{1,17},{... | collective-permute-start | bytes 294920 | tf_op jit(solution)/shard_map/ppermute | solution.py:59
  20.5 4.8 %collective-permute-done.2 = bf16[64,768]{1,0:T(8,128)(2,1)S(1)} collective-permute-done((bf16[64,768]{1,0:T(8,128)(2,1)S(1)}, bf16[64,768]{1,0:T(8,128)(2,1)S(1)}, u32[]{:S(2)}, u32[]{:S(2)}) %collective-permute-start.2) | collective-permute-done | bytes 98336 | tf_op jit(solution)/shard_map/ppermute | solution.py:59
  25.3 3.5 %convolution_convert_fusion.1 = bf16[64,2304]{0,1:T(8,128)(2,1)S(1)} fusion(bf16[64,768]{1,0:T(8,128)(2,1)S(1)} %broadcast_select_fusion.2, bf16[768,2304]{1,0:T(8,128)(2,1)} %param.14), kind=kOutput, calls=%fused_computation.10 | convolution fusion | flops 226639872 | bytes 3932160 | tf_op jit(solution)/shard_map/dot_general | solution.py:34
  28.8 0.8 copy-done.4
  29.6 0.9 fusion.121
  30.5 1.8 %copy.118 = f32[64,768]{1,0:T(8,128)} copy(f32[64,768]{0,1:T(8,128)} %get-tuple-element.26) | data formatting | bytes 393216 | tf_op jit(solution)/shard_map/convert_element_type | solution.py:150
  32.4 1.6 %fusion.122 = (f32[64,12]{0,1:T(8,128)S(1)}, f32[4,64,12]{1,2,0:T(8,128)S(1)}) fusion(s32[768]{0:T(1024)S(1)} %add_select_fusion, f32[64,768]{1,0:T(8,128)} %copy.118, bf16[4,64,2304]{2,1,0:T(8,128)(2,1)S(1)} %bitcast.65), kind=kOutput, calls=%fused_computation.192 | convolution fusion | flops 28719360 | bytes 609280 | tf_op jit(solution)/shard_map/dot_general | solution.py:45
  33.9 0.1 copy.120
  34.0 0.6 fusion.66
  34.6 1.0 %fusion.32 = f32[64,768]{1,0:T(8,128)} fusion(s32[768]{0:T(1024)S(1)} %add_select_fusion, f32[4,64,12]{1,2,0:T(8,128)S(1)} %get-tuple-element.37, f32[64,12]{0,1:T(8,128)S(1)} %get-tuple-element.36, bf16[4,64,2304]{2,1,0:T(8,128)(2,1)S(1)} %bitcast.66), kind=kOutput, calls=%fused_computation.41 | convolution fusion | flops 5274624 | bytes 608256 | tf_op jit(solution)/shard_map/dot_general | solution.py:53
  35.6 0.8 copy.119
  36.4 1.0 %pad_maximum_fusion.3 = f32[64,792]{1,0:T(8,128)S(1)} fusion(f32[64,12]{1,0:T(8,128)S(1)} %copy.120, f32[64,12]{1,0:T(8,128)S(1)} %copy.119, f32[64,768]{1,0:T(8,128)} %fusion.32), kind=kLoop, calls=%fused_computation.71 | loop fusion | flops 101376 | bytes 405504 | tf_op jit(solution)/shard_map/concatenate | solution.py:158
  37.5 3.2 %bitcast_reduce_fusion = (f32[4,12,64]{2,0,1:T(4,128)S(1)}, f32[12,64,4,64]{3,1,2,0:T(8,128)}) fusion(bf16[64,12,64,1]{0,2,3,1:T(8,128)(2,1)} %bitcast.69, bf16[4,64,12,64]{3,2,1,0:T(8,128)(2,1)S(1)} %reshape.106), kind=kOutput, calls=%fused_computation.30 | convolution fusion | flops 25555968 | bytes 1290240 | tf_op jit(solution)/shard_map/rqhd,khd->rhqk/dot_general | solution.py:193
  40.7 1.3 %pad_maximum_fusion.2 = bf16[4,192,768]{2,1,0:T(8,128)(2,1)S(1)} fusion(bf16[4,64,768]{2,1,0:T(8,128)(2,1)} %collective-permute-done.5, bf16[4,64,768]{2,1,0:T(8,128)(2,1)} %collective-permute-done.4, bf16[4,64,768]{2,1,0:T(8,128)(2,1)} %collective-permute-done.3), kind=kLoop, calls=%fused_computation.43 | loop fusion | flops 3538944 | bytes 2359296 | tf_op jit(solution)/shard_map/concatenate | solution.py:169
  42.0 2.0 %convolution_convert_fusion.2 = bf16[768,1536]{1,0:T(8,128)(2,1)S(1)} fusion(bf16[768,768]{1,0:T(8,128)(2,1)S(1)} %bitcast.68, bf16[768,2304]{1,0:T(8,128)(2,1)S(1)} %copy-done.3), kind=kOutput, calls=%fused_computation.11 | convolution fusion | flops 1813118976 | bytes 5898240 | tf_op jit(solution)/shard_map/dot_general | solution.py:34
  44.0 0.2 fusion.119
  44.2 0.8 copy-done.6
  45.0 0.1 copy-done.7
  45.1 1.9 %pad_maximum_fusion = (bf16[4,256,768]{2,1,0:T(8,128)(2,1)}, bf16[4,256,768]{2,1,0:T(8,128)(2,1)}) fusion(bf16[4,192,768]{2,1,0:T(8,128)(2,1)S(1)} %get-tuple-element.19, bf16[4,64,768]{2,1,0:T(8,128)(2,1)S(1)} %copy-done.7, bf16[4,192,768]{2,1,0:T(8,128)(2,1)S(1)} %get-tuple-element.18, bf16[4,64,768]{2,1,0:T(8,128)(2,1)S(1)} %copy-done.6), kind=kLoop, calls=%fused_computation.24 | loop fusion | flops 6291456 | bytes 6291456 | tf_op jit(solution)/shard_map/concatenate | solution.py:174
  47.0 2.6 %copy.104 = bf16[4,256,768]{1,2,0:T(8,128)(2,1)} copy(bf16[4,256,768]{2,1,0:T(8,128)(2,1)} %get-tuple-element.47) | data formatting | bytes 3145728 | tf_op jit(solution)/shard_map/concatenate | solution.py:174
  49.6 2.6 %copy.105 = bf16[4,256,768]{1,2,0:T(8,128)(2,1)} copy(bf16[4,256,768]{2,1,0:T(8,128)(2,1)} %get-tuple-element.48) | data formatting | bytes 3145728 | tf_op jit(solution)/shard_map/concatenate | solution.py:173
  52.2 2.2 %fusion.8 = (f32[4,12,64]{2,1,0:T(8,128)S(1)}, f32[4,12,64,256]{3,2,1,0:T(8,128)S(1)}) fusion(pred[4,64,256]{2,1,0:T(8,128)(4,1)S(1)} %fusion.48, bf16[4,256,12,64]{1,3,2,0:T(8,128)(2,1)} %bitcast.63, bf16[4,64,12,64]{3,2,1,0:T(8,128)(2,1)S(1)} %reshape.106), kind=kOutput, calls=%fused_computation.14 | convolution fusion | flops 103019520 | bytes 5189632 | tf_op jit(solution)/shard_map/rqhd,rkhd->rhqk/dot_general | solution.py:189
  54.5 2.0 %fusion.18 = f32[4,12,64,64]{3,2,1,0:T(8,128)} fusion(bf16[4,256,12,64]{1,3,2,0:T(8,128)(2,1)S(1)} %bitcast.62, f32[4,12,64,256]{3,2,1,0:T(8,128)S(1)} %get-tuple-element.40, f32[4,12,64]{2,1,0:T(8,128)S(1)} %copy_maximum_fusion, pred[4,64,256]{2,1,0:T(8,128)(4,1)S(1)} %fusion.48), kind=kOutput, calls=%fused_computation.23 | convolution fusion | flops 103809024 | bytes 5582848 | tf_op jit(solution)/shard_map/rhqk,rkhd->rqhd/dot_general | solution.py:199
  56.5 1.4 %fusion.9 = f32[4,12,64]{2,1,0:T(8,128)S(1)} fusion(f32[4,12,64,256]{3,2,1,0:T(8,128)S(1)} %get-tuple-element.40, f32[4,12,64]{2,1,0:T(8,128)S(1)} %copy_maximum_fusion, pred[4,64,256]{2,1,0:T(8,128)(4,1)S(1)} %fusion.48), kind=kLoop, calls=%fused_computation.15 | loop fusion | flops 3142656 | bytes 3235840 | tf_op jit(solution)/shard_map/reduce_sum | solution.py:198
  57.9 0.1 fusion.80
  58.1 0.7 collective-permute-start.8
  59.0 0.4 fusion.61
  59.4 1.4 %collective-permute-start.7 = (bf16[32,768]{1,0:T(8,128)(2,1)S(1)}, bf16[32,768]{1,0:T(8,128)(2,1)S(1)}, u32[]{:S(2)}, u32[]{:S(2)}) collective-permute-start(bf16[32,768]{1,0:T(8,128)(2,1)S(1)} %get-tuple-element.13), channel_id=1, source_target_pairs={{0,8},{4,12},{8,0},{12,4},{16,24},{20,28},{24,16},{28,20},{1,9},{5... | collective-permute-start | bytes 147464 | tf_op jit(solution)/shard_map/ppermute | solution.py:59
  60.8 1.3 %fusion.27 = (f32[4,12,64]{2,0,1:T(4,128)S(1)}, bf16[4,12,64,64]{2,3,0,1:T(8,128)(2,1)}) fusion(f32[12,64,4,64]{3,1,2,0:T(8,128)S(1)} %copy-done.1, f32[4,12,64]{2,0,1:T(4,128)S(1)} %copy.113), kind=kLoop, calls=%fused_computation.37 | loop fusion | flops 586752 | bytes 1204224 | tf_op jit(solution)/shard_map/reduce_sum | solution.py:198
  62.1 1.5 %collective-permute-done.7 = bf16[32,768]{1,0:T(8,128)(2,1)S(1)} collective-permute-done((bf16[32,768]{1,0:T(8,128)(2,1)S(1)}, bf16[32,768]{1,0:T(8,128)(2,1)S(1)}, u32[]{:S(2)}, u32[]{:S(2)}) %collective-permute-start.7) | collective-permute-done | bytes 49184 | tf_op jit(solution)/shard_map/ppermute | solution.py:59
  63.6 0.1 fusion.57
  63.6 0.1 fusion.79
  63.8 3.4 %collective-permute-start.10 = (f32[32,24]{1,0:T(8,128)S(1)}, f32[32,24]{1,0:T(8,128)S(1)}, u32[]{:S(2)}, u32[]{:S(2)}) collective-permute-start(f32[32,24]{1,0:T(8,128)S(1)} %pad_maximum_fusion.10), channel_id=1, source_target_pairs={{0,16},{4,20},{8,24},{12,28},{16,0},{20,4},{24,8},{28,12},{1,17},{... | collective-permute-start | bytes 9224 | tf_op jit(solution)/shard_map/ppermute | solution.py:59
  67.4 0.4 fusion.60
  67.9 5.0 %collective-permute-done.9 = bf16[32,768]{1,0:T(8,128)(2,1)S(1)} collective-permute-done((bf16[32,768]{1,0:T(8,128)(2,1)S(1)}, bf16[32,768]{1,0:T(8,128)(2,1)S(1)}, u32[]{:S(2)}, u32[]{:S(2)}) %collective-permute-start.9) | collective-permute-done | bytes 49184 | tf_op jit(solution)/shard_map/ppermute | solution.py:59
  72.9 0.1 fusion.55
  73.0 0.1 fusion.78
  73.2 0.4 fusion.59
  73.7 0.2 copy.128
  74.0 1.8 %fusion.21 = bf16[4,64,12,64]{1,3,2,0:T(8,128)(2,1)S(1)} fusion(f32[4,12,64,64]{3,2,1,0:T(8,128)} %fusion.18, bf16[64,12,64,1]{0,2,1,3:T(8,128)(2,1)S(1)} %bitcast.75, bf16[4,12,64,64]{2,3,0,1:T(8,128)(2,1)S(1)} %copy-done.10, f32[4,64,12]{1,2,0:T(8,128)S(1)} %fusion.65), kind=kOutput, calls=%fused_computation.28 | convolution fusion | flops 25755648 | bytes 1683456 | tf_op jit(solution)/shard_map/rhqk,khd->rqhd/dot_general | solution.py:202
  75.8 0.6 copy.117
  76.4 1.2 %convert_element_type.97 = bf16[256,768]{0,1:T(8,128)(2,1)} reshape(bf16[4,64,12,64]{1,0,3,2:T(4,128)(2,1)S(1)} %copy.117) | data formatting | bytes 786432 | tf_op jit(solution)/shard_map/convert_element_type | solution.py:206
  77.7 1.5 %maximum_select_fusion = f32[64,792]{0,1:T(8,128)S(1)} fusion(f32[32,792]{0,1:T(8,128)} %collective-permute-done.11, f32[32,792]{0,1:T(8,128)S(1)} %copy.128, pred[]{:T(512)S(6)} %eq.133), kind=kLoop, calls=%fused_computation.62 | loop fusion | flops 152064 | bytes 405505 | tf_op jit(solution)/shard_map/jit(_where)/select_n | solution.py:112
  79.2 0.3 fusion.82
  79.5 0.5 fusion.58
  80.0 0.5 fusion.33
  80.6 0.7 fusion.68
  81.3 0.3 multiply_reduce_fusion.1
  81.6 7.5 %fusion.123 = (f32[320]{0:T(512)S(1)}, f32[320,768]{1,0:T(8,128)S(1)}) fusion(bf16[3072,768]{1,0:T(8,128)(2,1)} %param.18, bf16[768,3072]{1,0:T(8,128)(2,1)} %param.17, f32[768]{0:T(1024)S(1)} %copy-done.17, f32[320]{0:T(512)S(1)} %add_rsqrt_fusion.1, f32[320]{0:T(512)S(1)} %broadcast_multiply_fusion.1, f32[320,768]{1,0:T(8,128)S(1)} %get-tuple-element.44, ...), kind=kOutput, calls=%fused_computation.193 | convolution fusion | flops 3033906944 | bytes 11901696 | tf_op jit(solution)/shard_map/dot_general | solution.py:29
  89.1 0.3 multiply_reduce_fusion
  89.4 0.2 multiply_convert_fusion
  89.6 0.8 slice.216
  90.4 0.6 slice.217
  (76 shorter events, 1.3 us)
Async XLA Ops:
  0.6 79.9 %copy-start = (bf16[768,768]{1,0:T(8,128)(2,1)S(1)}, bf16[768,768]{1,0:T(8,128)(2,1)}, u32[]{:S(2)}) copy-start(bf16[768,768]{1,0:T(8,128)(2,1)} %param.15) | copy-start | bytes 3538948
  0.6 40.0 %collective-permute-start.5 = (bf16[4,64,768]{2,1,0:T(8,128)(2,1)}, bf16[4,64,768]{2,1,0:T(8,128)(2,1)}, u32[]{:S(2)}, u32[]{:S(2)}) collective-permute-start(bf16[4,64,768]{2,1,0:T(8,128)(2,1)} %param.10), channel_id=1, source_target_pairs={{0,3},{1,2},{2,1},{3,0},{4,7},{5,6},{6,5},{7,4},{8,11},{9,10},{10,... | collective-permute-start | bytes 1179656 | tf_op jit(solution)/shard_map/ppermute | solution.py:125
  4.6 36.1 %collective-permute-start.4 = (bf16[4,64,768]{2,1,0:T(8,128)(2,1)}, bf16[4,64,768]{2,1,0:T(8,128)(2,1)}, u32[]{:S(2)}, u32[]{:S(2)}) collective-permute-start(bf16[4,64,768]{2,1,0:T(8,128)(2,1)} %param.10), channel_id=1, source_target_pairs={{0,2},{1,3},{2,0},{3,1},{4,6},{5,7},{6,4},{7,5},{8,10},{9,11},{10,... | collective-permute-start | bytes 1179656 | tf_op jit(solution)/shard_map/ppermute | solution.py:125
  5.1 35.6 %collective-permute-start.3 = (bf16[4,64,768]{2,1,0:T(8,128)(2,1)}, bf16[4,64,768]{2,1,0:T(8,128)(2,1)}, u32[]{:S(2)}, u32[]{:S(2)}) collective-permute-start(bf16[4,64,768]{2,1,0:T(8,128)(2,1)} %param.10), channel_id=1, source_target_pairs={{0,1},{1,0},{2,3},{3,2},{4,5},{5,4},{6,7},{7,6},{8,9},{9,8},{10,11... | collective-permute-start | bytes 1179656 | tf_op jit(solution)/shard_map/ppermute | solution.py:125
  5.3 5.1 %collective-permute-start = (bf16[64,768]{1,0:T(8,128)(2,1)}, bf16[64,768]{1,0:T(8,128)(2,1)S(1)}, u32[]{:S(2)}, u32[]{:S(2)}) collective-permute-start(bf16[64,768]{1,0:T(8,128)(2,1)} %bitcast.76), channel_id=1, source_target_pairs={{0,4},{4,0},{8,12},{12,8},{16,20},{20,16},{24,28},{28,24},{1,5},{5... | collective-permute-start | bytes 294920 | tf_op jit(solution)/shard_map/ppermute | solution.py:59
  9.1 1.2 %copy-start.14 = (bf16[1,64,768]{2,1,0:T(8,128)(2,1)S(1)}, bf16[1,64,768]{2,1,0:T(8,128)(2,1)}, u32[]{:S(2)}) copy-start(bf16[1,64,768]{2,1,0:T(8,128)(2,1)} %param.11) | copy-start | bytes 294916
  9.2 3.8 %copy-start.16 = (s32[4,64]{1,0:T(4,128)S(1)}, s32[4,64]{1,0:T(4,128)}, u32[]{:S(2)}) copy-start(s32[4,64]{1,0:T(4,128)} %param.13) | copy-start | bytes 3076
  11.0 5.7 %collective-permute-start.1 = (bf16[64,768]{1,0:T(8,128)(2,1)}, bf16[64,768]{1,0:T(8,128)(2,1)}, u32[]{:S(2)}, u32[]{:S(2)}) collective-permute-start(bf16[64,768]{1,0:T(8,128)(2,1)} %broadcast_select_fusion), channel_id=1, source_target_pairs={{0,8},{4,12},{8,0},{12,4},{16,24},{20,28},{24,16},{28,20},{1,9},{5... | collective-permute-start | bytes 294920 | tf_op jit(solution)/shard_map/ppermute | solution.py:59
  17.6 7.6 %collective-permute-start.2 = (bf16[64,768]{1,0:T(8,128)(2,1)S(1)}, bf16[64,768]{1,0:T(8,128)(2,1)S(1)}, u32[]{:S(2)}, u32[]{:S(2)}) collective-permute-start(bf16[64,768]{1,0:T(8,128)(2,1)S(1)} %broadcast_select_fusion.1), channel_id=1, source_target_pairs={{0,16},{4,20},{8,24},{12,28},{16,0},{20,4},{24,8},{28,12},{1,17},{... | collective-permute-start | bytes 294920 | tf_op jit(solution)/shard_map/ppermute | solution.py:59
  25.3 5.2 %copy-start.8 = (bf16[64,768]{1,0:T(8,128)(2,1)}, bf16[64,768]{1,0:T(8,128)(2,1)S(1)}, u32[]{:S(2)}) copy-start(bf16[64,768]{1,0:T(8,128)(2,1)S(1)} %broadcast_select_fusion.2) | copy-start | bytes 294916
  28.8 0.8 copy-start.4
  37.4 20.5 %collective-permute-start.6 = (f32[32,792]{1,0:T(8,128)S(1)}, f32[32,792]{1,0:T(8,128)S(1)}, u32[]{:S(2)}, u32[]{:S(2)}) collective-permute-start(f32[32,792]{1,0:T(8,128)S(1)} %slice_select_fusion), channel_id=1, source_target_pairs={{0,4},{4,0},{8,12},{12,8},{16,20},{20,16},{24,28},{28,24},{1,5},{5... | collective-permute-start | bytes 304136 | tf_op jit(solution)/shard_map/ppermute | solution.py:59
  37.5 4.5 %copy-start.3 = (bf16[768,2304]{1,0:T(8,128)(2,1)S(1)}, bf16[768,2304]{1,0:T(8,128)(2,1)}, u32[]{:S(2)}) copy-start(bf16[768,2304]{1,0:T(8,128)(2,1)} %param.14) | copy-start | bytes 10616836
  44.0 1.0 %copy-start.6 = (bf16[4,64,768]{2,1,0:T(8,128)(2,1)S(1)}, bf16[4,64,768]{2,1,0:T(8,128)(2,1)}, u32[]{:S(2)}) copy-start(bf16[4,64,768]{2,1,0:T(8,128)(2,1)} %get-tuple-element.23) | copy-start | bytes 1179652
  44.0 1.1 %copy-start.7 = (bf16[4,64,768]{2,1,0:T(8,128)(2,1)S(1)}, bf16[4,64,768]{2,1,0:T(8,128)(2,1)}, u32[]{:S(2)}) copy-start(bf16[4,64,768]{2,1,0:T(8,128)(2,1)} %get-tuple-element.24) | copy-start | bytes 1179652
  52.2 2.3 %copy-start.2 = (bf16[4,256,768]{1,2,0:T(8,128)(2,1)S(1)}, bf16[4,256,768]{1,2,0:T(8,128)(2,1)}, u32[]{:S(2)}) copy-start(bf16[4,256,768]{1,2,0:T(8,128)(2,1)} %copy.104) | copy-start | bytes 4718596
  56.5 4.3 %copy-start.1 = (f32[12,64,4,64]{3,1,2,0:T(8,128)S(1)}, f32[12,64,4,64]{3,1,2,0:T(8,128)}, u32[]{:S(2)}) copy-start(f32[12,64,4,64]{3,1,2,0:T(8,128)} %get-tuple-element.42) | copy-start | bytes 2359300
  58.1 5.5 %collective-permute-start.8 = (f32[32,24]{1,0:T(8,128)S(1)}, f32[32,24]{1,0:T(8,128)S(1)}, u32[]{:S(2)}, u32[]{:S(2)}) collective-permute-start(f32[32,24]{1,0:T(8,128)S(1)} %pad_maximum_fusion.9), channel_id=1, source_target_pairs={{0,8},{4,12},{8,0},{12,4},{16,24},{20,28},{24,16},{28,20},{1,9},{5... | collective-permute-start | bytes 9224 | tf_op jit(solution)/shard_map/ppermute | solution.py:59
  59.4 4.2 %collective-permute-start.7 = (bf16[32,768]{1,0:T(8,128)(2,1)S(1)}, bf16[32,768]{1,0:T(8,128)(2,1)S(1)}, u32[]{:S(2)}, u32[]{:S(2)}) collective-permute-start(bf16[32,768]{1,0:T(8,128)(2,1)S(1)} %get-tuple-element.13), channel_id=1, source_target_pairs={{0,8},{4,12},{8,0},{12,4},{16,24},{20,28},{24,16},{28,20},{1,9},{5... | collective-permute-start | bytes 147464 | tf_op jit(solution)/shard_map/ppermute | solution.py:59
  62.1 11.9 %copy-start.10 = (bf16[4,12,64,64]{2,3,0,1:T(8,128)(2,1)S(1)}, bf16[4,12,64,64]{2,3,0,1:T(8,128)(2,1)}, u32[]{:S(2)}) copy-start(bf16[4,12,64,64]{2,3,0,1:T(8,128)(2,1)} %get-tuple-element.21) | copy-start | bytes 1179652
  62.1 11.9 %copy-start.13 = (bf16[64,768]{0,1:T(8,128)(2,1)S(1)}, bf16[64,768]{0,1:T(8,128)(2,1)}, u32[]{:S(2)}) copy-start(bf16[64,768]{0,1:T(8,128)(2,1)} %get-tuple-element.25) | copy-start | bytes 294916
  63.8 9.1 %collective-permute-start.10 = (f32[32,24]{1,0:T(8,128)S(1)}, f32[32,24]{1,0:T(8,128)S(1)}, u32[]{:S(2)}, u32[]{:S(2)}) collective-permute-start(f32[32,24]{1,0:T(8,128)S(1)} %pad_maximum_fusion.10), channel_id=1, source_target_pairs={{0,16},{4,20},{8,24},{12,28},{16,0},{20,4},{24,8},{28,12},{1,17},{... | collective-permute-start | bytes 9224 | tf_op jit(solution)/shard_map/ppermute | solution.py:59
  67.8 5.1 %collective-permute-start.9 = (bf16[32,768]{1,0:T(8,128)(2,1)S(1)}, bf16[32,768]{1,0:T(8,128)(2,1)S(1)}, u32[]{:S(2)}, u32[]{:S(2)}) collective-permute-start(bf16[32,768]{1,0:T(8,128)(2,1)S(1)} %get-tuple-element.7), channel_id=1, source_target_pairs={{0,16},{4,20},{8,24},{12,28},{16,0},{20,4},{24,8},{28,12},{1,17},{... | collective-permute-start | bytes 147464 | tf_op jit(solution)/shard_map/ppermute | solution.py:59
  73.9 3.7 %collective-permute-start.11 = (f32[32,792]{0,1:T(8,128)S(1)}, f32[32,792]{0,1:T(8,128)}, u32[]{:S(2)}, u32[]{:S(2)}) collective-permute-start(f32[32,792]{0,1:T(8,128)S(1)} %copy.128), channel_id=1, source_target_pairs={{0,4},{4,0},{8,12},{12,8},{16,20},{20,16},{24,28},{28,24},{1,5},{5... | collective-permute-start | bytes 304136 | tf_op jit(solution)/shard_map/ppermute | solution.py:59
  75.8 3.4 %copy-start.5 = (bf16[64,2304]{0,1:T(8,128)(2,1)S(1)}, bf16[64,2304]{0,1:T(8,128)(2,1)}, u32[]{:S(2)}) copy-start(bf16[64,2304]{0,1:T(8,128)(2,1)} %copy-done.4) | copy-start | bytes 884740
  77.6 2.9 %copy-start.9 = (bf16[64,768]{1,0:T(8,128)(2,1)S(1)}, bf16[64,768]{1,0:T(8,128)(2,1)}, u32[]{:S(2)}) copy-start(bf16[64,768]{1,0:T(8,128)(2,1)} %copy-done.8) | copy-start | bytes 294916
  77.7 2.9 %copy-start.11 = (bf16[4,64,768]{2,1,0:T(8,128)(2,1)S(1)}, bf16[4,64,768]{2,1,0:T(8,128)(2,1)}, u32[]{:S(2)}) copy-start(bf16[4,64,768]{2,1,0:T(8,128)(2,1)} %param.10) | copy-start | bytes 1179652
  77.7 2.9 %copy-start.12 = (bf16[256,768]{0,1:T(8,128)(2,1)S(1)}, bf16[256,768]{0,1:T(8,128)(2,1)}, u32[]{:S(2)}) copy-start(bf16[256,768]{0,1:T(8,128)(2,1)} %convert_element_type.97) | copy-start | bytes 1179652
  80.6 1.0 %copy-start.17 = (f32[768]{0:T(1024)S(1)}, f32[768]{0:T(1024)}, u32[]{:S(2)}) copy-start(f32[768]{0:T(1024)} %param.16) | copy-start | bytes 9220
  81.6 7.8 %copy-start.15 = (f32[768]{0:T(1024)S(1)}, f32[768]{0:T(1024)}, u32[]{:S(2)}) copy-start(f32[768]{0:T(1024)} %param.19) | copy-start | bytes 9220

commit v5 on v3

--- a/solution.py
+++ b/solution.py
@@ -80,17 +80,45 @@
     return jnp.concatenate([mixed, total, top], axis=-1)
 
 
-def all_merge(value, axis, count, width):
+def all_merge(value, axis, count, width, fillers, state):
     here = lax.axis_index(axis)
-    step = 1
+    rounds = [0]
+
+    def exchange(sent, state):
+        k = rounds[0]
+        rounds[0] += 1
+        if k < len(fillers):
+            sent, state = lax.optimization_barrier((sent, state))
+        got = [partner(s, axis, step_of[k], count) for s in sent]
+        if k < len(fillers):
+            state = fillers[k](state)
+            got, state = lax.optimization_barrier((got, state))
+        return got, state
+
+    steps = []
+    step = 2
     while step < count:
-        got = partner(value, axis, step, count)
+        steps.append(step)
+        step *= 2
+    step_of = [1] + steps + [1]
+
+    half = value.shape[0] // 2
+    first = (here & 1) == 0
+    mine = jnp.where(first, value[:half], value[half:])
+    sent = jnp.where(first, value[half:], value[:half])
+    (got,), state = exchange([sent], state)
+    value = merge(jnp.where(first, mine, got), jnp.where(first, got, mine), width)
+    for step in steps:
+        mixed = value[:, :width].astype(jnp.bfloat16)
+        stats = value[:, width:]
+        (got_mixed, got_stats), state = exchange([mixed, stats], state)
+        mine = jnp.concatenate([mixed.astype(jnp.float32), stats], axis=-1)
+        got = jnp.concatenate([got_mixed.astype(jnp.float32), got_stats], axis=-1)
         low_side = (here & step) == 0
-        lo = jnp.where(low_side, value, got)
-        hi = jnp.where(low_side, got, value)
-        value = merge(lo, hi, width)
-        step *= 2
-    return value
+        value = merge(jnp.where(low_side, mine, got), jnp.where(low_side, got, mine), width)
+    (got,), state = exchange([value], state)
+    value = jnp.where(first, jnp.concatenate([value, got]), jnp.concatenate([got, value]))
+    return value, state
 
 
 def fan_out(value, axis, count):
@@ -137,7 +165,60 @@
     part_mixed = (col_weights * own_vals.astype(jnp.float32)).sum(0)
     part_total = col_exp.sum(0)
     packed = jnp.concatenate([part_mixed, part_total, part_top], axis=-1)
-    packed = all_merge(packed, "band", n_band, model_width)
+
+    sources = [own_group] + [s for s, _ in row_parts]
+    q4 = queries.reshape(row_count, cols_dev, HEADS, HEAD_DIM)
+    sk = sum_keys.reshape(cols_dev, HEADS, HEAD_DIM)
+    sv = sum_vals.reshape(cols_dev, HEADS, HEAD_DIM)
+
+    def scores_stage(state):
+        other_cells = jnp.concatenate(state, axis=1)
+        width_other = other_cells.shape[1]
+        other_kv = project(other_cells.reshape(row_count * width_other, model_width), w_kv)
+        other_kv = other_kv.reshape(row_count, width_other, 2 * model_width)
+        row_keys = jnp.concatenate([own_keys, other_kv[:, :, :model_width]], axis=1)
+        row_vals = jnp.concatenate([own_vals, other_kv[:, :, model_width:]], axis=1)
+        width_now = row_keys.shape[1]
+        k4 = row_keys.reshape(row_count, width_now, HEADS, HEAD_DIM)
+        v4 = row_vals.reshape(row_count, width_now, HEADS, HEAD_DIM)
+        key_groups = jnp.concatenate([jnp.full((cols_dev,), s, jnp.int32) for s in sources])
+        own_block = jnp.arange(width_now, dtype=jnp.int32) < cols_dev
+        allowed = (jnp.right_shift(schema[:, :, None], key_groups[None, None, :]) & 1 == 1) | (
+            own_block[None, None, :]
+        )
+        cell_scores = (
+            jnp.einsum("rqhd,rkhd->rhqk", q4, k4, preferred_element_type=jnp.float32) * score_scale
+        )
+        cell_scores = jnp.where(allowed[:, None], cell_scores, -1e30)
+        tok_scores = (
+            jnp.einsum("rqhd,khd->rhqk", q4, sk, preferred_element_type=jnp.float32) * score_scale
+        )
+        return cell_scores, tok_scores, v4
+
+    def weights_stage(state):
+        cell_scores, tok_scores, v4 = state
+        row_top = jnp.maximum(cell_scores.max(-1), tok_scores.max(-1))
+        cell_exp = jnp.exp(cell_scores - row_top[..., None])
+        tok_exp = jnp.exp(tok_scores - row_top[..., None])
+        row_total = cell_exp.sum(-1) + tok_exp.sum(-1)
+        mixed = jnp.einsum(
+            "rhqk,rkhd->rqhd", cell_exp.astype(jnp.bfloat16), v4, preferred_element_type=jnp.float32
+        )
+        return mixed, tok_exp.astype(jnp.bfloat16), row_total
+
+    def output_stage(state):
+        mixed, tok_weights, row_total = state
+        mixed = mixed + jnp.einsum(
+            "rhqk,khd->rqhd", tok_weights, sv, preferred_element_type=jnp.float32
+        )
+        attended = mixed / row_total.transpose(0, 2, 1)[..., None]
+        return attended.reshape(row_count * cols_dev, model_width).astype(jnp.bfloat16)
+
+    packed, attended = all_merge(
+        packed, "band", n_band, model_width,
+        [scores_stage, weights_stage, output_stage],
+        [got for _, got in row_parts],
+    )
     col_top = jnp.maximum(packed[:, model_width + HEADS :], self_scores)
     fade = jnp.exp(packed[:, model_width + HEADS :] - col_top)
     self_exp = jnp.exp(self_scores - col_top)
@@ -146,46 +227,6 @@
     col_mixed = packed[:, :model_width] * spreads[:cols_dev] + spreads[cols_dev:] * sum_vals.astype(jnp.float32)
     summary_att = (col_mixed / head_spread(col_total)).astype(jnp.bfloat16)
 
-    sources = [own_group] + [s for s, _ in row_parts]
-    other_cells = jnp.concatenate([got for _, got in row_parts], axis=1)
-    width_other = other_cells.shape[1]
-    other_kv = project(other_cells.reshape(row_count * width_other, model_width), w_kv)
-    other_kv = other_kv.reshape(row_count, width_other, 2 * model_width)
-    row_keys = jnp.concatenate([own_keys, other_kv[:, :, :model_width]], axis=1)
-    row_vals = jnp.concatenate([own_vals, other_kv[:, :, model_width:]], axis=1)
-    width_now = row_keys.shape[1]
-    q4 = queries.reshape(row_count, cols_dev, HEADS, HEAD_DIM)
-    k4 = row_keys.reshape(row_count, width_now, HEADS, HEAD_DIM)
-    v4 = row_vals.reshape(row_count, width_now, HEADS, HEAD_DIM)
-    sk = sum_keys.reshape(cols_dev, HEADS, HEAD_DIM)
-    sv = sum_vals.reshape(cols_dev, HEADS, HEAD_DIM)
-    key_groups = jnp.concatenate(
-        [jnp.full((cols_dev,), s, jnp.int32) for s in sources]
-    )
-    own_block = jnp.arange(width_now, dtype=jnp.int32) < cols_dev
-    allowed = (jnp.right_shift(schema[:, :, None], key_groups[None, None, :]) & 1 == 1) | own_block[
-        None, None, :
-    ]
-    cell_scores = (
-        jnp.einsum("rqhd,rkhd->rhqk", q4, k4, preferred_element_type=jnp.float32) * score_scale
-    )
-    cell_scores = jnp.where(allowed[:, None], cell_scores, -1e30)
-    tok_scores = (
-        jnp.einsum("rqhd,khd->rhqk", q4, sk, preferred_element_type=jnp.float32) * score_scale
-    )
-    row_top = jnp.maximum(cell_scores.max(-1), tok_scores.max(-1))
-    cell_exp = jnp.exp(cell_scores - row_top[..., None])
-    tok_exp = jnp.exp(tok_scores - row_top[..., None])
-    row_total = cell_exp.sum(-1) + tok_exp.sum(-1)
-    mixed = jnp.einsum(
-        "rhqk,rkhd->rqhd", cell_exp.astype(jnp.bfloat16), v4, preferred_element_type=jnp.float32
-    )
-    mixed = mixed + jnp.einsum(
-        "rhqk,khd->rqhd", tok_exp.astype(jnp.bfloat16), sv, preferred_element_type=jnp.float32
-    )
-    attended = mixed / row_total.transpose(0, 2, 1)[..., None]
-    attended = attended.reshape(row_count * cols_dev, model_width).astype(jnp.bfloat16)
-
     all_in = jnp.concatenate([flat_cells, tokens], axis=0)
     all_att = jnp.concatenate([attended, summary_att], axis=0)
     all_out = finish(all_in, all_att, w_out, gain_attn, w_up, w_down, gain_ffn)

time: 105 us -> 96 us (0.914)
  waiting for transfers between devices: 34 us -> 11.1 us
  other arithmetic: 10.5 us -> 21.5 us
  starting transfers between devices: 12.5 us -> 14.9 us
    ppermute x6 -> x9, waiting for transfers between devices: 34 us -> 11.1 us  [partner(): return lax.ppermute(value, axis, [(i, i ^ step) for i in range(count)])]
    convert_element_type x0 -> x4, other arithmetic: none -> 3.09 us  [the longest x2 3.08 us: all_merge(): mine = jnp.concatenate([mixed.astype(jnp.float32), stats], axis=-1)]
    reduce_max x0 -> x2, other arithmetic: none -> 2.62 us  [weights_stage(): row_top = jnp.maximum(cell_scores.max(-1), tok_scores.max(-1))]
    reduce_sum x2, other arithmetic: 1.66 us -> 4.2 us  [weights_stage(): row_total = cell_exp.sum(-1) + tok_exp.sum(-1)]
    ppermute x6 -> x9, starting transfers between devices: 7.9 us -> 10.4 us  [partner(): return lax.ppermute(value, axis, [(i, i ^ step) for i in range(count)])]
    dot_general x4, matrix products: 6.9 us -> 9.23 us  [the longest x1 3.99 us: scores_stage(): jnp.einsum('rqhd,rkhd->rhqk', q4, k4, preferred_element_type=jnp.float32)]
    convert_element_type x1, local copies, waits for them, and re-layouts: 1.83 us -> 0.14 us  [local(): sq = sum_queries.astype(jnp.float32)]
    unnamed x34 -> x50, local copies, waits for them, and re-layouts: 2.06 us -> 3.62 us
  transfers between devices with their start and end apart: 9 -> 12, of which waited for: 4 -> 5; matrix products, arithmetic and copies ran while one was open for 38% -> 27% of each run, Pallas kernels for 0% -> 0%
where the time goes in v5:
time: 96 us; the launch traced here: 95.4 us
  matrix products  30.1 us (31%)
  other arithmetic  21.5 us (22%)
  local copies, waits for them, and re-layouts  15.8 us (16%)
  starting transfers between devices  14.9 us (16%)
  waiting for transfers between devices  11.1 us (12%)
  between operations  1.83 us (2%)
    ppermute x9, waiting for transfers between devices, partner(): return lax.ppermute(value, axis, [(i, i ^ step) for i in range(count)])  11.1 us
    ppermute x9, starting transfers between devices, partner(): return lax.ppermute(value, axis, [(i, i ^ step) for i in range(count)])  10.4 us
    dot_general x3, matrix products, project(): jnp.dot(values, weight, preferred_element_type=jnp.float32)  8.68 us
    dot_general x1, matrix products, finish(): outer_out = jnp.dot(inner_act, w_down, preferred_element_type=jnp.float32)  7.43 us
    ppermute x3, starting transfers between devices, fan_out(): got.append((source, lax.ppermute(value, axis, pairs)))  4.55 us
    reduce_sum x2, other arithmetic, weights_stage(): row_total = cell_exp.sum(-1) + tok_exp.sum(-1)  4.2 us
    dot_general x1, matrix products, scores_stage(): jnp.einsum('rqhd,rkhd->rhqk', q4, k4, preferred_element_type=jnp.float32)  3.99 us
    unnamed x50, local copies, waits for them, and re-layouts  3.62 us
  transfers between devices with their start and end apart: 12, of which 5 were waited for; matrix products, arithmetic and copies ran while one was open for 27% of the time, Pallas kernels for 0%

profile of v5, /device:TPU:0, one launch (start us, length us, event | category | flops | bytes accessed | tf_op | source)
XLA Modules:
  0.0 95.4 jit_solution(18387766015964644931)
XLA Ops:
  0.6 3.0 %collective-permute-start.3 = (bf16[4,64,768]{2,1,0:T(8,128)(2,1)}, bf16[4,64,768]{2,1,0:T(8,128)(2,1)}, u32[]{:S(2)}, u32[]{:S(2)}) collective-permute-start(bf16[4,64,768]{2,1,0:T(8,128)(2,1)} %param.10), channel_id=1, source_target_pairs={{0,1},{1,0},{2,3},{3,2},{4,5},{5,4},{6,7},{7,6},{8,9},{9,8},{10,11... | collective-permute-start | bytes 1179656 | tf_op jit(solution)/shard_map/ppermute | solution.py:134
  3.6 1.5 %collective-permute-start.4 = (bf16[4,64,768]{2,1,0:T(8,128)(2,1)}, bf16[4,64,768]{2,1,0:T(8,128)(2,1)}, u32[]{:S(2)}, u32[]{:S(2)}) collective-permute-start(bf16[4,64,768]{2,1,0:T(8,128)(2,1)} %param.10), channel_id=1, source_target_pairs={{0,2},{1,3},{2,0},{3,1},{4,6},{5,7},{6,4},{7,5},{8,10},{9,11},{10,... | collective-permute-start | bytes 1179656 | tf_op jit(solution)/shard_map/ppermute | solution.py:134
  5.8 3.2 %convolution_convert_fusion = bf16[256,2304]{1,0:T(8,128)(2,1)S(1)} fusion(bf16[256,768]{1,0:T(8,128)(2,1)} %bitcast.66, bf16[768,2304]{1,0:T(8,128)(2,1)} %param.14), kind=kOutput, calls=%fused_computation.9 | convolution fusion | flops 906559488 | bytes 5111808 | tf_op jit(solution)/shard_map/dot_general | solution.py:34
  9.1 1.0 %fusion.116 = (bf16[4,64,768]{2,1,0:T(8,128)(2,1)}, bf16[4,64,768]{2,1,0:T(8,128)(2,1)S(1)}, bf16[4,64,768]{2,1,0:T(8,128)(2,1)}) fusion(bf16[4,64,2304]{2,1,0:T(8,128)(2,1)S(1)} %bitcast.56), kind=kLoop, calls=%fused_computation.181 | loop fusion | bytes 2359296 | tf_op jit(solution)/shard_map/slice | solution.py:152
  10.2 2.1 %collective-permute-start.1 = (bf16[64,768]{1,0:T(8,128)(2,1)S(1)}, bf16[64,768]{1,0:T(8,128)(2,1)S(1)}, u32[]{:S(2)}, u32[]{:S(2)}) collective-permute-start(bf16[64,768]{1,0:T(8,128)(2,1)S(1)} %broadcast_select_fusion), channel_id=1, source_target_pairs={{0,8},{4,12},{8,0},{12,4},{16,24},{20,28},{24,16},{28,20},{1,9},{5... | collective-permute-start | bytes 294920 | tf_op jit(solution)/shard_map/ppermute | solution.py:59
  12.3 0.8 fusion.47
  13.1 1.6 %reshape.103 = bf16[4,64,12,64]{3,2,1,0:T(8,128)(2,1)} reshape(bf16[4,64,768]{2,1,0:T(8,128)(2,1)S(1)} %get-tuple-element.75) | data formatting | bytes 786432 | tf_op jit(solution)/shard_map/reshape | solution.py:170
  14.7 1.1 %collective-permute-done.1 = bf16[64,768]{1,0:T(8,128)(2,1)S(1)} collective-permute-done((bf16[64,768]{1,0:T(8,128)(2,1)S(1)}, bf16[64,768]{1,0:T(8,128)(2,1)S(1)}, u32[]{:S(2)}, u32[]{:S(2)}) %collective-permute-start.1) | collective-permute-done | bytes 98336 | tf_op jit(solution)/shard_map/ppermute | solution.py:59
  15.8 2.8 %collective-permute-start.2 = (bf16[64,768]{1,0:T(8,128)(2,1)S(1)}, bf16[64,768]{1,0:T(8,128)(2,1)S(1)}, u32[]{:S(2)}, u32[]{:S(2)}) collective-permute-start(bf16[64,768]{1,0:T(8,128)(2,1)S(1)} %broadcast_select_fusion.1), channel_id=1, source_target_pairs={{0,16},{4,20},{8,24},{12,28},{16,0},{20,4},{24,8},{28,12},{1,17},{... | collective-permute-start | bytes 294920 | tf_op jit(solution)/shard_map/ppermute | solution.py:59
  18.6 5.0 %collective-permute-done.2 = bf16[64,768]{1,0:T(8,128)(2,1)S(1)} collective-permute-done((bf16[64,768]{1,0:T(8,128)(2,1)S(1)}, bf16[64,768]{1,0:T(8,128)(2,1)S(1)}, u32[]{:S(2)}, u32[]{:S(2)}) %collective-permute-start.2) | collective-permute-done | bytes 98336 | tf_op jit(solution)/shard_map/ppermute | solution.py:59
  23.6 0.6 copy-done.10
  24.2 3.5 %convolution_convert_fusion.1 = bf16[64,2304]{0,1:T(8,128)(2,1)S(1)} fusion(bf16[64,768]{1,0:T(8,128)(2,1)S(1)} %broadcast_select_fusion.2, bf16[768,2304]{1,0:T(8,128)(2,1)} %param.14), kind=kOutput, calls=%fused_computation.10 | convolution fusion | flops 226639872 | bytes 3932160 | tf_op jit(solution)/shard_map/dot_general | solution.py:34
  27.7 0.8 fusion.117
  28.7 0.6 fusion.118
  29.3 0.3 fusion.30
  30.0 0.7 copy-done.4
  30.6 2.4 %multiply_bitcast_fusion = f32[4,12,64,64]{2,3,0,1:T(8,128)S(1)} fusion(bf16[64,12,64,1]{0,2,3,1:T(8,128)(2,1)} %bitcast.61, bf16[4,64,12,64]{3,2,1,0:T(8,128)(2,1)} %reshape.103), kind=kOutput, calls=%fused_computation.30 | convolution fusion | flops 25362432 | bytes 1277952 | tf_op jit(solution)/shard_map/rqhd,khd->rhqk/dot_general | solution.py:194
  33.0 1.3 %pad_maximum_fusion.2 = bf16[4,192,768]{2,1,0:T(8,128)(2,1)S(1)} fusion(bf16[4,64,768]{2,1,0:T(8,128)(2,1)} %collective-permute-done.5, bf16[4,64,768]{2,1,0:T(8,128)(2,1)} %collective-permute-done.4, bf16[4,64,768]{2,1,0:T(8,128)(2,1)} %collective-permute-done.3), kind=kLoop, calls=%fused_computation.38 | loop fusion | flops 3538944 | bytes 2359296 | tf_op jit(solution)/shard_map/concatenate | solution.py:175
  34.3 2.0 %convolution_convert_fusion.2 = bf16[768,1536]{1,0:T(8,128)(2,1)S(1)} fusion(bf16[768,768]{1,0:T(8,128)(2,1)S(1)} %bitcast.60, bf16[768,2304]{1,0:T(8,128)(2,1)S(1)} %copy-done.3), kind=kOutput, calls=%fused_computation.11 | convolution fusion | flops 1813118976 | bytes 5898240 | tf_op jit(solution)/shard_map/dot_general | solution.py:34
  36.4 0.2 fusion.115
  36.5 0.8 copy-done.5
  37.5 1.9 %pad_maximum_fusion = (bf16[4,256,768]{2,1,0:T(8,128)(2,1)}, bf16[4,256,768]{2,1,0:T(8,128)(2,1)}) fusion(bf16[4,192,768]{2,1,0:T(8,128)(2,1)S(1)} %get-tuple-element.71, bf16[4,64,768]{2,1,0:T(8,128)(2,1)S(1)} %copy-done.6, bf16[4,192,768]{2,1,0:T(8,128)(2,1)S(1)} %get-tuple-element.70, bf16[4,64,768]{2,1,0:T(8,128)(2,1)S(1)} %copy-done.5), kind=kLoop, calls=%fused_computation.23 | loop fusion | flops 6291456 | bytes 6291456 | tf_op jit(solution)/shard_map/concatenate | solution.py:179
  39.3 2.6 %copy.109 = bf16[4,256,768]{1,2,0:T(8,128)(2,1)} copy(bf16[4,256,768]{2,1,0:T(8,128)(2,1)} %get-tuple-element.95) | data formatting | bytes 3145728 | tf_op jit(solution)/shard_map/concatenate | solution.py:179
  42.0 4.0 %multiply_select_fusion = f32[4,12,64,256]{3,2,1,0:T(8,128)} fusion(bf16[4,256,12,64]{1,3,2,0:T(8,128)(2,1)} %bitcast.55, pred[4,64,256]{2,1,0:T(8,128)(4,1)S(1)} %copy-done.12, bf16[4,64,12,64]{3,2,1,0:T(8,128)(2,1)} %reshape.103), kind=kOutput, calls=%fused_computation.13 | convolution fusion | flops 102236160 | bytes 5177344 | tf_op jit(solution)/shard_map/rqhd,rkhd->rhqk/dot_general | solution.py:190
  46.0 2.6 %copy.114 = bf16[4,256,768]{1,2,0:T(8,128)(2,1)} copy(bf16[4,256,768]{2,1,0:T(8,128)(2,1)} %get-tuple-element.96) | data formatting | bytes 3145728 | tf_op jit(solution)/shard_map/concatenate | solution.py:180
  48.6 1.0 %broadcast_select_fusion.4 = (f32[32,792]{1,0:T(8,128)S(1)}, f32[32,792]{1,0:T(8,128)S(1)}) fusion(f32[32,792]{1,0:T(8,128)} %collective-permute-done.6, pred[]{:T(512)S(6)} %eq.133, f32[64,792]{1,0:T(8,128)} %copy-done.4), kind=kLoop, calls=%fused_computation.93 | loop fusion | flops 76032 | bytes 506881 | tf_op jit(solution)/shard_map/jit(_where)/select_n | solution.py:110
  49.6 0.6 copy-done.8
  50.2 0.7 fusion.77
  51.1 0.4 fusion.60
  51.5 1.5 %fusion.113 = (f32[32,768]{1,0:T(8,128)S(1)}, bf16[32,768]{1,0:T(8,128)(2,1)}) fusion(f32[64,768]{1,0:T(8,128)S(1)} %fusion.60, f32[32,792]{1,0:T(8,128)} %copy-done.8, f32[32,792]{1,0:T(8,128)S(1)} %get-tuple-element.82), kind=kLoop, calls=%fused_computation.179 | loop fusion | flops 122880 | bytes 540672 | tf_op jit(solution)/shard_map/convert_element_type | solution.py:115
  53.0 0.8 pad_maximum_fusion.9
  53.8 2.4 %reduce_max.28 = f32[4,12,64]{2,1,0:T(8,128)S(1)} reduce(f32[4,12,64,256]{3,2,1,0:T(8,128)} %multiply_select_fusion, f32[]{:T(128)} %constant.114.clone.1), dimensions={3}, to_apply=%region_3.4 | reduce | flops 783360 | bytes 3158020 | tf_op jit(solution)/shard_map/reduce_max | solution.py:200
  56.2 0.2 reduce_max.29
  56.5 2.9 %fusion.8 = f32[4,12,64]{2,1,0:T(8,128)S(1)} fusion(f32[4,12,64,256]{3,2,1,0:T(8,128)} %multiply_select_fusion, f32[4,12,64]{2,1,0:T(8,128)S(1)} %copy_maximum_fusion), kind=kLoop, calls=%fused_computation.14 | loop fusion | flops 1569792 | bytes 3170304 | tf_op jit(solution)/shard_map/reduce_sum | solution.py:203
  59.5 1.3 %fusion.25 = (f32[4,12,64]{2,0,1:T(4,128)S(1)}, bf16[4,12,64,64]{2,3,0,1:T(8,128)(2,1)}) fusion(f32[4,12,64,64]{2,3,0,1:T(8,128)S(1)} %multiply_bitcast_fusion, f32[4,12,64]{2,0,1:T(4,128)S(1)} %copy.118), kind=kLoop, calls=%fused_computation.32 | loop fusion | flops 586752 | bytes 1204224 | tf_op jit(solution)/shard_map/reduce_sum | solution.py:203
  60.8 1.4 %fusion.22 = f32[4,64,12,64]{1,3,2,0:T(8,128)S(1)} fusion(bf16[4,256,12,64]{1,3,2,0:T(8,128)(2,1)S(1)} %bitcast.54, f32[4,12,64,256]{3,2,1,0:T(8,128)S(1)} %copy-done.1, f32[4,12,64]{2,1,0:T(8,128)S(1)} %copy_maximum_fusion), kind=kOutput, calls=%fused_computation.31 | convolution fusion | flops 102236160 | bytes 5517312 | tf_op jit(solution)/shard_map/rhqk,rkhd->rqhd/dot_general | solution.py:204
  62.1 0.7 collective-permute-start.7
  62.8 1.4 %collective-permute-start.8 = (f32[32,24]{1,0:T(8,128)S(1)}, f32[32,24]{1,0:T(8,128)S(1)}, u32[]{:S(2)}, u32[]{:S(2)}) collective-permute-start(f32[32,24]{1,0:T(8,128)S(1)} %pad_maximum_fusion.9), channel_id=1, source_target_pairs={{0,8},{4,12},{8,0},{12,4},{16,24},{20,28},{24,16},{28,20},{1,9},{5... | collective-permute-start | bytes 9224 | tf_op jit(solution)/shard_map/ppermute | solution.py:59
  64.2 0.6 copy_add_fusion
  64.8 1.9 %collective-permute-done.8 = f32[32,24]{1,0:T(8,128)S(1)} collective-permute-done((f32[32,24]{1,0:T(8,128)S(1)}, f32[32,24]{1,0:T(8,128)S(1)}, u32[]{:S(2)}, u32[]{:S(2)}) %collective-permute-start.8) | collective-permute-done | bytes 3104 | tf_op jit(solution)/shard_map/ppermute | solution.py:59
  66.8 0.6 copy-done.7
  67.5 0.7 fusion.76
  68.3 1.1 %fusion.59 = f32[64,768]{1,0:T(8,128)S(1)} fusion(s32[768]{0:T(1024)} %copy-done.13, f32[32,12]{0,1:T(8,128)S(1)} %copy.121, f32[32,12]{0,1:T(8,128)S(1)} %copy.120), kind=kOutput, calls=%fused_computation.97 | convolution fusion | flops 7087872 | bytes 202752 | tf_op jit(solution)/shard_map/dot_general | solution.py:53
  69.4 1.5 %fusion.111 = (f32[32,768]{1,0:T(8,128)S(1)}, bf16[32,768]{1,0:T(8,128)(2,1)}) fusion(f32[64,768]{1,0:T(8,128)S(1)} %fusion.59, f32[32,792]{1,0:T(8,128)} %copy-done.7, f32[32,792]{1,0:T(8,128)S(1)} %get-tuple-element.86), kind=kLoop, calls=%fused_computation.178 | loop fusion | flops 122880 | bytes 540672 | tf_op jit(solution)/shard_map/convert_element_type | solution.py:115
  70.9 1.4 %pad_maximum_fusion.10 = f32[32,24]{1,0:T(8,128)} fusion(f32[32,12]{1,0:T(8,128)} %get-tuple-element.63, f32[32,12]{1,0:T(8,128)} %get-tuple-element.60), kind=kLoop, calls=%fused_computation.123 | loop fusion | flops 768 | bytes 6144 | tf_op jit(solution)/shard_map/concatenate | solution.py:80
  72.3 3.3 %collective-permute-start.9 = (bf16[32,768]{1,0:T(8,128)(2,1)}, bf16[32,768]{1,0:T(8,128)(2,1)S(1)}, u32[]{:S(2)}, u32[]{:S(2)}) collective-permute-start(bf16[32,768]{1,0:T(8,128)(2,1)} %get-tuple-element.46), channel_id=1, source_target_pairs={{0,16},{4,20},{8,24},{12,28},{16,0},{20,4},{24,8},{28,12},{1,17},{... | collective-permute-start | bytes 147464 | tf_op jit(solution)/shard_map/ppermute | solution.py:59
  75.6 1.5 %fusion.20 = bf16[4,64,12,64]{1,3,2,0:T(8,128)(2,1)S(1)} fusion(f32[4,64,12,64]{1,3,2,0:T(8,128)S(1)} %fusion.22, bf16[64,12,64,1]{0,2,1,3:T(8,128)(2,1)} %bitcast.63, bf16[4,12,64,64]{2,3,0,1:T(8,128)(2,1)} %get-tuple-element.49, f32[4,64,12]{1,2,0:T(8,128)} %bitcast.65), kind=kOutput, calls=%fused_computation.27 | convolution fusion | flops 25755648 | bytes 1683456 | tf_op jit(solution)/shard_map/rhqk,khd->rqhd/dot_general | solution.py:211
  77.2 0.6 copy.125
  77.8 1.2 %convert_element_type.105 = bf16[256,768]{0,1:T(8,128)(2,1)} reshape(bf16[4,64,12,64]{1,0,3,2:T(4,128)(2,1)S(1)} %copy.125) | data formatting | bytes 786432 | tf_op jit(solution)/shard_map/convert_element_type | solution.py:215
  79.0 1.4 %collective-permute-done.10 = f32[32,24]{1,0:T(8,128)S(1)} collective-permute-done((f32[32,24]{1,0:T(8,128)}, f32[32,24]{1,0:T(8,128)S(1)}, u32[]{:S(2)}, u32[]{:S(2)}) %collective-permute-start.10) | collective-permute-done | bytes 3104 | tf_op jit(solution)/shard_map/ppermute | solution.py:59
  80.8 0.4 fusion.58
  81.3 0.2 copy.129
  81.6 1.7 %collective-permute-done.11 = f32[32,792]{0,1:T(8,128)S(1)} collective-permute-done((f32[32,792]{0,1:T(8,128)S(1)}, f32[32,792]{0,1:T(8,128)S(1)}, u32[]{:S(2)}, u32[]{:S(2)}) %collective-permute-start.11) | collective-permute-done | bytes 101408 | tf_op jit(solution)/shard_map/ppermute | solution.py:59
  83.3 0.3 maximum_select_fusion
  83.6 0.3 fusion.79
  83.9 0.5 fusion.57
  84.4 0.6 fusion.31
  85.0 0.7 fusion.119
  85.7 0.3 multiply_reduce_fusion.1
  86.0 7.4 %fusion.120 = (f32[320]{0:T(512)S(1)}, f32[320,768]{1,0:T(8,128)S(1)}) fusion(bf16[3072,768]{1,0:T(8,128)(2,1)} %param.18, bf16[768,3072]{1,0:T(8,128)(2,1)} %param.17, f32[320,768]{1,0:T(8,128)S(1)} %get-tuple-element.92, f32[768]{0:T(1024)S(1)} %copy-done.24, f32[320]{0:T(512)S(1)} %add_rsqrt_fusion.1, f32[320]{0:T(512)S(1)} %broadcast_multiply_fusion.1), kind=kOutput, calls=%fused_computation.185 | convolution fusion | flops 3031449344 | bytes 11410176 | tf_op jit(solution)/shard_map/dot_general | solution.py:29
  93.5 0.3 multiply_reduce_fusion
  93.7 0.2 multiply_convert_fusion
  93.9 0.8 slice.216
  94.7 0.6 slice.217
  (92 shorter events, 1.9 us)
Async XLA Ops:
  0.6 84.4 %copy-start = (bf16[768,768]{1,0:T(8,128)(2,1)S(1)}, bf16[768,768]{1,0:T(8,128)(2,1)}, u32[]{:S(2)}) copy-start(bf16[768,768]{1,0:T(8,128)(2,1)} %param.15) | copy-start | bytes 3538948
  0.6 32.3 %collective-permute-start.3 = (bf16[4,64,768]{2,1,0:T(8,128)(2,1)}, bf16[4,64,768]{2,1,0:T(8,128)(2,1)}, u32[]{:S(2)}, u32[]{:S(2)}) collective-permute-start(bf16[4,64,768]{2,1,0:T(8,128)(2,1)} %param.10), channel_id=1, source_target_pairs={{0,1},{1,0},{2,3},{3,2},{4,5},{5,4},{6,7},{7,6},{8,9},{9,8},{10,11... | collective-permute-start | bytes 1179656 | tf_op jit(solution)/shard_map/ppermute | solution.py:134
  3.6 29.3 %collective-permute-start.4 = (bf16[4,64,768]{2,1,0:T(8,128)(2,1)}, bf16[4,64,768]{2,1,0:T(8,128)(2,1)}, u32[]{:S(2)}, u32[]{:S(2)}) collective-permute-start(bf16[4,64,768]{2,1,0:T(8,128)(2,1)} %param.10), channel_id=1, source_target_pairs={{0,2},{1,3},{2,0},{3,1},{4,6},{5,7},{6,4},{7,5},{8,10},{9,11},{10,... | collective-permute-start | bytes 1179656 | tf_op jit(solution)/shard_map/ppermute | solution.py:134
  5.2 27.8 %collective-permute-start.5 = (bf16[4,64,768]{2,1,0:T(8,128)(2,1)}, bf16[4,64,768]{2,1,0:T(8,128)(2,1)}, u32[]{:S(2)}, u32[]{:S(2)}) collective-permute-start(bf16[4,64,768]{2,1,0:T(8,128)(2,1)} %param.10), channel_id=1, source_target_pairs={{0,3},{1,2},{2,1},{3,0},{4,7},{5,6},{6,5},{7,4},{8,11},{9,10},{10,... | collective-permute-start | bytes 1179656 | tf_op jit(solution)/shard_map/ppermute | solution.py:134
  5.2 5.0 %collective-permute-start = (bf16[64,768]{1,0:T(8,128)(2,1)}, bf16[64,768]{1,0:T(8,128)(2,1)S(1)}, u32[]{:S(2)}, u32[]{:S(2)}) collective-permute-start(bf16[64,768]{1,0:T(8,128)(2,1)} %bitcast.64), channel_id=1, source_target_pairs={{0,4},{4,0},{8,12},{12,8},{16,20},{20,16},{24,28},{28,24},{1,5},{5... | collective-permute-start | bytes 294920 | tf_op jit(solution)/shard_map/ppermute | solution.py:59
  9.1 1.1 %copy-start.19 = (bf16[1,64,768]{2,1,0:T(8,128)(2,1)S(1)}, bf16[1,64,768]{2,1,0:T(8,128)(2,1)}, u32[]{:S(2)}) copy-start(bf16[1,64,768]{2,1,0:T(8,128)(2,1)} %param.11) | copy-start | bytes 294916
  9.1 3.2 %copy-start.22 = (s32[4,64]{1,0:T(4,128)S(1)}, s32[4,64]{1,0:T(4,128)}, u32[]{:S(2)}) copy-start(s32[4,64]{1,0:T(4,128)} %param.13) | copy-start | bytes 3076
  10.2 5.6 %collective-permute-start.1 = (bf16[64,768]{1,0:T(8,128)(2,1)S(1)}, bf16[64,768]{1,0:T(8,128)(2,1)S(1)}, u32[]{:S(2)}, u32[]{:S(2)}) collective-permute-start(bf16[64,768]{1,0:T(8,128)(2,1)S(1)} %broadcast_select_fusion), channel_id=1, source_target_pairs={{0,8},{4,12},{8,0},{12,4},{16,24},{20,28},{24,16},{28,20},{1,9},{5... | collective-permute-start | bytes 294920 | tf_op jit(solution)/shard_map/ppermute | solution.py:59
  15.8 7.8 %collective-permute-start.2 = (bf16[64,768]{1,0:T(8,128)(2,1)S(1)}, bf16[64,768]{1,0:T(8,128)(2,1)S(1)}, u32[]{:S(2)}, u32[]{:S(2)}) collective-permute-start(bf16[64,768]{1,0:T(8,128)(2,1)S(1)} %broadcast_select_fusion.1), channel_id=1, source_target_pairs={{0,16},{4,20},{8,24},{12,28},{16,0},{20,4},{24,8},{28,12},{1,17},{... | collective-permute-start | bytes 294920 | tf_op jit(solution)/shard_map/ppermute | solution.py:59
  18.6 32.5 %copy-start.13 = (s32[768]{0:T(1024)}, s32[768]{0:T(1024)S(1)}, u32[]{:S(2)}) copy-start(s32[768]{0:T(1024)S(1)} %add_select_fusion) | copy-start | bytes 9220
  23.6 0.6 copy-start.10
  29.9 0.7 copy-start.4
  30.6 3.7 %copy-start.3 = (bf16[768,2304]{1,0:T(8,128)(2,1)S(1)}, bf16[768,2304]{1,0:T(8,128)(2,1)}, u32[]{:S(2)}) copy-start(bf16[768,2304]{1,0:T(8,128)(2,1)} %param.14) | copy-start | bytes 10616836
  36.3 1.0 %copy-start.5 = (bf16[4,64,768]{2,1,0:T(8,128)(2,1)S(1)}, bf16[4,64,768]{2,1,0:T(8,128)(2,1)}, u32[]{:S(2)}) copy-start(bf16[4,64,768]{2,1,0:T(8,128)(2,1)} %get-tuple-element.74) | copy-start | bytes 1179652
  36.4 1.1 %copy-start.6 = (bf16[4,64,768]{2,1,0:T(8,128)(2,1)S(1)}, bf16[4,64,768]{2,1,0:T(8,128)(2,1)}, u32[]{:S(2)}) copy-start(bf16[4,64,768]{2,1,0:T(8,128)(2,1)} %get-tuple-element.76) | copy-start | bytes 1179652
  39.3 2.6 %copy-start.12 = (pred[4,64,256]{2,1,0:T(8,128)(4,1)S(1)}, pred[4,64,256]{2,1,0:T(8,128)(4,1)}, u32[]{:S(2)}) copy-start(pred[4,64,256]{2,1,0:T(8,128)(4,1)} %fusion.47) | copy-start | bytes 196612
  42.0 6.6 %collective-permute-start.6 = (f32[32,792]{1,0:T(8,128)S(1)}, f32[32,792]{1,0:T(8,128)}, u32[]{:S(2)}, u32[]{:S(2)}) collective-permute-start(f32[32,792]{1,0:T(8,128)S(1)} %slice_select_fusion), channel_id=1, source_target_pairs={{0,4},{4,0},{8,12},{12,8},{16,20},{20,16},{24,28},{28,24},{1,5},{5... | collective-permute-start | bytes 304136 | tf_op jit(solution)/shard_map/ppermute | solution.py:59
  49.6 0.6 copy-start.8
  56.5 4.2 %copy-start.1 = (f32[4,12,64,256]{3,2,1,0:T(8,128)S(1)}, f32[4,12,64,256]{3,2,1,0:T(8,128)}, u32[]{:S(2)}) copy-start(f32[4,12,64,256]{3,2,1,0:T(8,128)} %multiply_select_fusion) | copy-start | bytes 9437188
  56.5 4.2 %copy-start.2 = (bf16[4,256,768]{1,2,0:T(8,128)(2,1)S(1)}, bf16[4,256,768]{1,2,0:T(8,128)(2,1)}, u32[]{:S(2)}) copy-start(bf16[4,256,768]{1,2,0:T(8,128)(2,1)} %copy.114) | copy-start | bytes 4718596
  60.7 1.4 %copy-start.20 = (bf16[32,768]{1,0:T(8,128)(2,1)S(1)}, bf16[32,768]{1,0:T(8,128)(2,1)}, u32[]{:S(2)}) copy-start(bf16[32,768]{1,0:T(8,128)(2,1)} %get-tuple-element.36) | copy-start | bytes 147460
  60.7 6.0 %copy-start.15 = (f32[32,12]{1,0:T(8,128)S(1)}, f32[32,12]{1,0:T(8,128)}, u32[]{:S(2)}) copy-start(f32[32,12]{1,0:T(8,128)} %get-tuple-element.66) | copy-start | bytes 4612
  60.7 6.0 %copy-start.16 = (f32[32,12]{1,0:T(8,128)S(1)}, f32[32,12]{1,0:T(8,128)}, u32[]{:S(2)}) copy-start(f32[32,12]{1,0:T(8,128)} %get-tuple-element.69) | copy-start | bytes 4612
  62.1 4.6 %collective-permute-start.7 = (bf16[32,768]{1,0:T(8,128)(2,1)S(1)}, bf16[32,768]{1,0:T(8,128)(2,1)S(1)}, u32[]{:S(2)}, u32[]{:S(2)}) collective-permute-start(bf16[32,768]{1,0:T(8,128)(2,1)S(1)} %copy-done.20), channel_id=1, source_target_pairs={{0,8},{4,12},{8,0},{12,4},{16,24},{20,28},{24,16},{28,20},{1,9},{5... | collective-permute-start | bytes 147464 | tf_op jit(solution)/shard_map/ppermute | solution.py:59
  62.8 3.9 %collective-permute-start.8 = (f32[32,24]{1,0:T(8,128)S(1)}, f32[32,24]{1,0:T(8,128)S(1)}, u32[]{:S(2)}, u32[]{:S(2)}) collective-permute-start(f32[32,24]{1,0:T(8,128)S(1)} %pad_maximum_fusion.9), channel_id=1, source_target_pairs={{0,8},{4,12},{8,0},{12,4},{16,24},{20,28},{24,16},{28,20},{1,9},{5... | collective-permute-start | bytes 9224 | tf_op jit(solution)/shard_map/ppermute | solution.py:59
  66.8 0.6 copy-start.7
  72.3 8.1 %collective-permute-start.9 = (bf16[32,768]{1,0:T(8,128)(2,1)}, bf16[32,768]{1,0:T(8,128)(2,1)S(1)}, u32[]{:S(2)}, u32[]{:S(2)}) collective-permute-start(bf16[32,768]{1,0:T(8,128)(2,1)} %get-tuple-element.46), channel_id=1, source_target_pairs={{0,16},{4,20},{8,24},{12,28},{16,0},{20,4},{24,8},{28,12},{1,17},{... | collective-permute-start | bytes 147464 | tf_op jit(solution)/shard_map/ppermute | solution.py:59
  75.6 4.8 %collective-permute-start.10 = (f32[32,24]{1,0:T(8,128)}, f32[32,24]{1,0:T(8,128)S(1)}, u32[]{:S(2)}, u32[]{:S(2)}) collective-permute-start(f32[32,24]{1,0:T(8,128)} %pad_maximum_fusion.10), channel_id=1, source_target_pairs={{0,16},{4,20},{8,24},{12,28},{16,0},{20,4},{24,8},{28,12},{1,17},{... | collective-permute-start | bytes 9224 | tf_op jit(solution)/shard_map/ppermute | solution.py:59
  77.1 3.3 %copy-start.17 = (f32[32,12]{1,0:T(8,128)S(1)}, f32[32,12]{1,0:T(8,128)}, u32[]{:S(2)}) copy-start(f32[32,12]{1,0:T(8,128)} %get-tuple-element.60) | copy-start | bytes 4612
  77.2 3.3 %copy-start.18 = (f32[32,12]{1,0:T(8,128)S(1)}, f32[32,12]{1,0:T(8,128)}, u32[]{:S(2)}) copy-start(f32[32,12]{1,0:T(8,128)} %get-tuple-element.63) | copy-start | bytes 4612
  77.2 3.6 %copy-start.14 = (s32[768]{0:T(1024)S(1)}, s32[768]{0:T(1024)}, u32[]{:S(2)}) copy-start(s32[768]{0:T(1024)} %copy-done.13) | copy-start | bytes 9220
  81.3 3.7 %copy-start.11 = (bf16[64,768]{1,0:T(8,128)(2,1)S(1)}, bf16[64,768]{1,0:T(8,128)(2,1)}, u32[]{:S(2)}) copy-start(bf16[64,768]{1,0:T(8,128)(2,1)} %copy-done.10) | copy-start | bytes 294916
  81.5 3.5 %copy-start.9 = (bf16[256,768]{0,1:T(8,128)(2,1)S(1)}, bf16[256,768]{0,1:T(8,128)(2,1)}, u32[]{:S(2)}) copy-start(bf16[256,768]{0,1:T(8,128)(2,1)} %convert_element_type.105) | copy-start | bytes 1179652
  81.5 3.5 %copy-start.23 = (bf16[4,64,768]{2,1,0:T(8,128)(2,1)S(1)}, bf16[4,64,768]{2,1,0:T(8,128)(2,1)}, u32[]{:S(2)}) copy-start(bf16[4,64,768]{2,1,0:T(8,128)(2,1)} %param.10) | copy-start | bytes 1179652
  81.5 1.8 %collective-permute-start.11 = (f32[32,792]{0,1:T(8,128)S(1)}, f32[32,792]{0,1:T(8,128)S(1)}, u32[]{:S(2)}, u32[]{:S(2)}) collective-permute-start(f32[32,792]{0,1:T(8,128)S(1)} %copy.129), channel_id=1, source_target_pairs={{0,4},{4,0},{8,12},{12,8},{16,20},{20,16},{24,28},{28,24},{1,5},{5... | collective-permute-start | bytes 304136 | tf_op jit(solution)/shard_map/ppermute | solution.py:59
  85.0 1.0 %copy-start.24 = (f32[768]{0:T(1024)S(1)}, f32[768]{0:T(1024)}, u32[]{:S(2)}) copy-start(f32[768]{0:T(1024)} %param.16) | copy-start | bytes 9220
  86.0 7.7 %copy-start.21 = (f32[768]{0:T(1024)S(1)}, f32[768]{0:T(1024)}, u32[]{:S(2)}) copy-start(f32[768]{0:T(1024)} %param.19) | copy-start | bytes 9220

commit v6 on v3

--- a/solution.py
+++ b/solution.py
@@ -69,28 +69,46 @@
     return value
 
 
-def merge(lo, hi, width):
-    top = jnp.maximum(lo[:, width + HEADS :], hi[:, width + HEADS :])
-    fade_lo = jnp.exp(lo[:, width + HEADS :] - top)
-    fade_hi = jnp.exp(hi[:, width + HEADS :] - top)
-    total = lo[:, width : width + HEADS] * fade_lo + hi[:, width : width + HEADS] * fade_hi
-    fades = head_spread(jnp.concatenate([fade_lo, fade_hi], axis=0))
-    rows = lo.shape[0]
-    mixed = lo[:, :width] * fades[:rows] + hi[:, :width] * fades[rows:]
-    return jnp.concatenate([mixed, total, top], axis=-1)
-
-
-def all_merge(value, axis, count, width):
+def merge(lo, hi):
+    top = jnp.maximum(lo[2], hi[2])
+    fade_lo = jnp.exp(lo[2] - top)
+    fade_hi = jnp.exp(hi[2] - top)
+    total = lo[1] * fade_lo + hi[1] * fade_hi
+    mixed = lo[0] * head_spread(fade_lo) + hi[0] * head_spread(fade_hi)
+    return mixed, total, top
+
+
+def pick(flag, a, b):
+    return tuple(jnp.where(flag, x, y) for x, y in zip(a, b))
+
+
+def all_merge(value, axis, count):
     here = lax.axis_index(axis)
-    step = 1
+    half = value[0].shape[0] // 2
+    first = (here & 1) == 0
+    top_half = tuple(v[:half] for v in value)
+    low_half = tuple(v[half:] for v in value)
+    mine = pick(first, top_half, low_half)
+    sent = pick(first, low_half, top_half)
+    got = tuple(partner(v, axis, 1, count) for v in sent)
+    value = merge(pick(first, mine, got), pick(first, got, mine))
+    step = 2
     while step < count:
-        got = partner(value, axis, step, count)
+        mixed = value[0].astype(jnp.bfloat16)
+        got = (
+            partner(mixed, axis, step, count).astype(jnp.float32),
+            partner(value[1], axis, step, count),
+            partner(value[2], axis, step, count),
+        )
+        mine = (mixed.astype(jnp.float32), value[1], value[2])
         low_side = (here & step) == 0
-        lo = jnp.where(low_side, value, got)
-        hi = jnp.where(low_side, got, value)
-        value = merge(lo, hi, width)
+        value = merge(pick(low_side, mine, got), pick(low_side, got, mine))
         step *= 2
-    return value
+    got = tuple(partner(v, axis, 1, count) for v in value)
+    return tuple(
+        jnp.where(first, jnp.concatenate([v, g]), jnp.concatenate([g, v]))
+        for v, g in zip(value, got)
+    )
 
 
 def fan_out(value, axis, count):
@@ -136,14 +154,14 @@
     col_weights = head_spread(col_exp.astype(jnp.bfloat16).astype(jnp.float32))
     part_mixed = (col_weights * own_vals.astype(jnp.float32)).sum(0)
     part_total = col_exp.sum(0)
-    packed = jnp.concatenate([part_mixed, part_total, part_top], axis=-1)
-    packed = all_merge(packed, "band", n_band, model_width)
-    col_top = jnp.maximum(packed[:, model_width + HEADS :], self_scores)
-    fade = jnp.exp(packed[:, model_width + HEADS :] - col_top)
+    merged = all_merge((part_mixed, part_total, part_top), "band", n_band)
+    col_top = jnp.maximum(merged[2], self_scores)
+    fade = jnp.exp(merged[2] - col_top)
     self_exp = jnp.exp(self_scores - col_top)
-    col_total = packed[:, model_width : model_width + HEADS] * fade + self_exp
-    spreads = head_spread(jnp.concatenate([fade, self_exp.astype(jnp.bfloat16).astype(jnp.float32)], axis=0))
-    col_mixed = packed[:, :model_width] * spreads[:cols_dev] + spreads[cols_dev:] * sum_vals.astype(jnp.float32)
+    col_total = merged[1] * fade + self_exp
+    col_mixed = merged[0] * head_spread(fade) + head_spread(
+        self_exp.astype(jnp.bfloat16).astype(jnp.float32)
+    ) * sum_vals.astype(jnp.float32)
     summary_att = (col_mixed / head_spread(col_total)).astype(jnp.bfloat16)
 
     sources = [own_group] + [s for s, _ in row_parts]

time: 105 us -> 89.6 us (0.85)
  waiting for transfers between devices: 34 us -> 18.1 us
  starting transfers between devices: 12.5 us -> 16.9 us
  other arithmetic: 10.5 us -> 9.2 us
  local copies, waits for them, and re-layouts: 16.3 us -> 15 us
  matrix products: 29.4 us -> 28.1 us
    ppermute x6 -> x15, waiting for transfers between devices: 34 us -> 18.1 us  [partner(): return lax.ppermute(value, axis, [(i, i ^ step) for i in range(count)])]
    ppermute x6 -> x15, starting transfers between devices: 7.9 us -> 12.3 us  [partner(): return lax.ppermute(value, axis, [(i, i ^ step) for i in range(count)])]
    reshape x0 -> x2, local copies, waits for them, and re-layouts: none -> 2.29 us  [the longest x1 1.15 us: local(): sk = sum_keys.reshape(cols_dev, HEADS, HEAD_DIM)]
    convert_element_type x1, local copies, waits for them, and re-layouts: 1.83 us -> 0.16 us  [local(): summary_att = (col_mixed / head_spread(col_total)).astype(jnp.bfloat16)]
    concatenate x3 -> x0, other arithmetic: 1.61 us -> none  [the longest x2 0.81 us: merge(): return jnp.concatenate([mixed, total, top], axis=-1)]
    dot_general x1, matrix products: 0.69 us -> 1.84 us  [finish(): mixed_out = jnp.dot(attended, w_out, preferred_element_type=jnp.float32)]
    reduce_sum x1 -> x0, local copies, waits for them, and re-layouts: 1.09 us -> none  [local(): part_mixed = (col_weights * own_vals.astype(jnp.float32)).sum(0)]
    dot_general x1, matrix products: 3.13 us -> 2.07 us  [local(): jnp.einsum('rqhd,khd->rhqk', q4, sk, preferred_element_type=jnp.float32)]
  transfers between devices with their start and end apart: 9 -> 18, of which waited for: 4 -> 8; matrix products, arithmetic and copies ran while one was open for 38% -> 44% of each run, Pallas kernels for 0% -> 0%
where the time goes in v6:
time: 89.6 us; the launch traced here: 89.1 us
  matrix products  28.1 us (31%)
  waiting for transfers between devices  18.1 us (20%)
  starting transfers between devices  16.9 us (19%)
  local copies, waits for them, and re-layouts  15 us (17%)
  other arithmetic  9.2 us (10%)
  between operations  1.84 us (2%)
    ppermute x15, waiting for transfers between devices, partner(): return lax.ppermute(value, axis, [(i, i ^ step) for i in range(count)])  18.1 us
    ppermute x15, starting transfers between devices, partner(): return lax.ppermute(value, axis, [(i, i ^ step) for i in range(count)])  12.3 us
    dot_general x3, matrix products, project(): jnp.dot(values, weight, preferred_element_type=jnp.float32)  7.99 us
    dot_general x1, matrix products, finish(): outer_out = jnp.dot(inner_act, w_down, preferred_element_type=jnp.float32)  7.54 us
    ppermute x3, starting transfers between devices, fan_out(): got.append((source, lax.ppermute(value, axis, pairs)))  4.6 us
    dot_general x10, matrix products, head_spread(): jnp.dot(flat, head_matrix(), precision=lax.Precision.HIGHEST, preferred_e...  4.09 us
    concatenate x1, local copies, waits for them, and re-layouts, local(): row_keys = jnp.concatenate([own_keys, other_kv[:, :, :model_width]], axis=1)  2.6 us
    concatenate x1, local copies, waits for them, and re-layouts, local(): row_vals = jnp.concatenate([own_vals, other_kv[:, :, model_width:]], axis=1)  2.57 us
  transfers between devices with their start and end apart: 18, of which 8 were waited for; matrix products, arithmetic and copies ran while one was open for 44% of the time, Pallas kernels for 0%

profile of v6, /device:TPU:0, one launch (start us, length us, event | category | flops | bytes accessed | tf_op | source)
XLA Modules:
  0.0 89.1 jit_solution(18243144136708342951)
XLA Ops:
  0.6 4.0 %collective-permute-start.5 = (bf16[4,64,768]{2,1,0:T(8,128)(2,1)}, bf16[4,64,768]{2,1,0:T(8,128)(2,1)}, u32[]{:S(2)}, u32[]{:S(2)}) collective-permute-start(bf16[4,64,768]{2,1,0:T(8,128)(2,1)} %param.10), channel_id=1, source_target_pairs={{0,3},{1,2},{2,1},{3,0},{4,7},{5,6},{6,5},{7,4},{8,11},{9,10},{10,... | collective-permute-start | bytes 1179656 | tf_op jit(solution)/shard_map/ppermute | solution.py:124
  4.6 0.5 collective-permute-start.4
  5.9 3.2 %convolution_convert_fusion = bf16[256,2304]{1,0:T(8,128)(2,1)S(1)} fusion(bf16[256,768]{1,0:T(8,128)(2,1)} %bitcast.66, bf16[768,2304]{1,0:T(8,128)(2,1)} %param.14), kind=kOutput, calls=%fused_computation.9 | convolution fusion | flops 906559488 | bytes 5111808 | tf_op jit(solution)/shard_map/dot_general | solution.py:34
  9.2 1.0 %fusion.124 = (bf16[4,64,768]{2,1,0:T(8,128)(2,1)}, bf16[4,64,768]{2,1,0:T(8,128)(2,1)}, bf16[4,64,768]{2,1,0:T(8,128)(2,1)}) fusion(bf16[4,64,2304]{2,1,0:T(8,128)(2,1)S(1)} %bitcast.59), kind=kLoop, calls=%fused_computation.179 | loop fusion | bytes 2359296 | tf_op jit(solution)/shard_map/slice | solution.py:140
  10.3 0.7 broadcast_select_fusion
  11.0 2.0 %collective-permute-start.1 = (bf16[64,768]{1,0:T(8,128)(2,1)}, bf16[64,768]{1,0:T(8,128)(2,1)}, u32[]{:S(2)}, u32[]{:S(2)}) collective-permute-start(bf16[64,768]{1,0:T(8,128)(2,1)} %broadcast_select_fusion), channel_id=1, source_target_pairs={{0,8},{4,12},{8,0},{12,4},{16,24},{20,28},{24,16},{28,20},{1,9},{5... | collective-permute-start | bytes 294920 | tf_op jit(solution)/shard_map/ppermute | solution.py:59
  13.1 1.7 %reshape.106 = bf16[4,64,12,64]{3,2,1,0:T(8,128)(2,1)S(1)} reshape(bf16[4,64,768]{2,1,0:T(8,128)(2,1)} %get-tuple-element.11) | data formatting | bytes 786432 | tf_op jit(solution)/shard_map/reshape | solution.py:175
  14.8 1.9 %collective-permute-done.1 = bf16[64,768]{1,0:T(8,128)(2,1)} collective-permute-done((bf16[64,768]{1,0:T(8,128)(2,1)}, bf16[64,768]{1,0:T(8,128)(2,1)}, u32[]{:S(2)}, u32[]{:S(2)}) %collective-permute-start.1) | collective-permute-done | bytes 98336 | tf_op jit(solution)/shard_map/ppermute | solution.py:59
  16.7 0.9 %broadcast_select_fusion.1 = bf16[64,768]{1,0:T(8,128)(2,1)S(1)} fusion(bf16[64,768]{1,0:T(8,128)(2,1)} %broadcast_select_fusion, bf16[64,768]{1,0:T(8,128)(2,1)} %collective-permute-done.1, pred[]{:T(512)S(6)} %eq.182), kind=kLoop, calls=%fused_computation.85 | loop fusion | flops 49152 | bytes 294913 | tf_op jit(solution)/shard_map/jit(_where)/select_n | solution.py:67
  17.6 2.8 %collective-permute-start.2 = (bf16[64,768]{1,0:T(8,128)(2,1)S(1)}, bf16[64,768]{1,0:T(8,128)(2,1)S(1)}, u32[]{:S(2)}, u32[]{:S(2)}) collective-permute-start(bf16[64,768]{1,0:T(8,128)(2,1)S(1)} %broadcast_select_fusion.1), channel_id=1, source_target_pairs={{0,16},{4,20},{8,24},{12,28},{16,0},{20,4},{24,8},{28,12},{1,17},{... | collective-permute-start | bytes 294920 | tf_op jit(solution)/shard_map/ppermute | solution.py:59
  20.5 4.8 %collective-permute-done.2 = bf16[64,768]{1,0:T(8,128)(2,1)S(1)} collective-permute-done((bf16[64,768]{1,0:T(8,128)(2,1)S(1)}, bf16[64,768]{1,0:T(8,128)(2,1)S(1)}, u32[]{:S(2)}, u32[]{:S(2)}) %collective-permute-start.2) | collective-permute-done | bytes 98336 | tf_op jit(solution)/shard_map/ppermute | solution.py:59
  25.3 2.8 %convolution_convert_fusion.1 = bf16[64,2304]{1,0:T(8,128)(2,1)S(1)} fusion(bf16[64,768]{1,0:T(8,128)(2,1)S(1)} %broadcast_select_fusion.2, bf16[768,2304]{1,0:T(8,128)(2,1)} %param.14), kind=kOutput, calls=%fused_computation.10 | convolution fusion | flops 226639872 | bytes 3932160 | tf_op jit(solution)/shard_map/dot_general | solution.py:34
  28.1 0.8 fusion.125
  28.9 0.6 fusion.126
  29.5 0.3 fusion.32
  30.0 0.5 collective-permute-start.7
  30.5 0.7 slice_select_fusion
  31.2 1.1 %reshape.108 = bf16[64,12,64]{2,1,0:T(8,128)(2,1)S(1)} reshape(bf16[64,768]{1,0:T(8,128)(2,1)} %get-tuple-element.16) | data formatting | bytes 196608 | tf_op jit(solution)/shard_map/reshape | solution.py:178
  32.3 2.1 %bitcast_reduce_fusion = (f32[4,12,64]{2,0,1:T(4,128)S(1)}, f32[12,64,4,64]{3,1,2,0:T(8,128)}) fusion(bf16[4,64,12,64]{3,2,1,0:T(8,128)(2,1)S(1)} %reshape.106, bf16[64,12,64,1]{2,1,0,3:T(8,128)(2,1)S(1)} %bitcast.64), kind=kOutput, calls=%fused_computation.30 | convolution fusion | flops 25555968 | bytes 1290240 | tf_op jit(solution)/shard_map/rqhd,khd->rhqk/dot_general | solution.py:192
  34.4 0.2 convolution_multiply_fusion.3
  34.6 1.1 %copy.58 = bf16[64,768]{0,1:T(8,128)(2,1)S(1)} copy(bf16[64,768]{1,0:T(8,128)(2,1)} %get-tuple-element.14) | data formatting | bytes 196608 | tf_op jit(solution)/shard_map/reshape | solution.py:179
  35.8 0.8 collective-permute-start.15
  36.6 1.3 %collective-permute-start.9 = (f32[32,12]{0,1:T(8,128)S(1)}, f32[32,12]{0,1:T(8,128)S(1)}, u32[]{:S(2)}, u32[]{:S(2)}) collective-permute-start(f32[32,12]{0,1:T(8,128)S(1)} %get-tuple-element.5), channel_id=1, source_target_pairs={{0,8},{4,12},{8,0},{12,4},{16,24},{20,28},{24,16},{28,20},{1,9},{5... | collective-permute-start | bytes 4616 | tf_op jit(solution)/shard_map/ppermute | solution.py:59
  37.9 0.3 fusion.66
  38.2 1.4 %collective-permute-done.15 = f32[32,12]{0,1:T(8,128)S(1)} collective-permute-done((f32[32,12]{0,1:T(8,128)S(1)}, f32[32,12]{0,1:T(8,128)S(1)}, u32[]{:S(2)}, u32[]{:S(2)}) %collective-permute-start.15) | collective-permute-done | bytes 1568 | tf_op jit(solution)/shard_map/ppermute | solution.py:59
  39.5 0.7 collective-permute-done.9
  40.2 3.4 %collective-permute-start.16 = (f32[32,12]{0,1:T(8,128)S(1)}, f32[32,12]{0,1:T(8,128)S(1)}, u32[]{:S(2)}, u32[]{:S(2)}) collective-permute-start(f32[32,12]{0,1:T(8,128)S(1)} %get-tuple-element.2), channel_id=1, source_target_pairs={{0,16},{4,20},{8,24},{12,28},{16,0},{20,4},{24,8},{28,12},{1,17},{... | collective-permute-start | bytes 4616 | tf_op jit(solution)/shard_map/ppermute | solution.py:59
  43.8 0.3 fusion.63
  44.0 1.3 %collective-permute-done.16 = f32[32,12]{0,1:T(8,128)S(1)} collective-permute-done((f32[32,12]{0,1:T(8,128)S(1)}, f32[32,12]{0,1:T(8,128)S(1)}, u32[]{:S(2)}, u32[]{:S(2)}) %collective-permute-start.16) | collective-permute-done | bytes 1568 | tf_op jit(solution)/shard_map/ppermute | solution.py:59
  45.3 2.9 %collective-permute-done.11 = f32[32,12]{0,1:T(8,128)S(1)} collective-permute-done((f32[32,12]{0,1:T(8,128)S(1)}, f32[32,12]{0,1:T(8,128)S(1)}, u32[]{:S(2)}, u32[]{:S(2)}) %collective-permute-start.11) | collective-permute-done | bytes 1568 | tf_op jit(solution)/shard_map/ppermute | solution.py:59
  48.3 0.3 fusion.61
  48.6 0.9 %collective-permute-done.13 = f32[32,12]{0,1:T(8,128)S(1)} collective-permute-done((f32[32,12]{0,1:T(8,128)S(1)}, f32[32,12]{0,1:T(8,128)S(1)}, u32[]{:S(2)}, u32[]{:S(2)}) %collective-permute-start.13) | collective-permute-done | bytes 1568 | tf_op jit(solution)/shard_map/ppermute | solution.py:59
  49.5 0.2 collective-permute-start.17
  49.7 0.9 %fusion.59 = f32[64,768]{1,0:T(8,128)} fusion(s32[768]{0:T(1024)S(1)} %add_select_fusion, f32[64,12]{0,1:T(8,128)S(1)} %convolution_multiply_fusion.3, f32[64,12]{0,1:T(8,128)S(1)} %maximum_select_fusion.1), kind=kOutput, calls=%fused_computation.89 | convolution fusion | flops 1191168 | bytes 205824 | tf_op jit(solution)/shard_map/dot_general | solution.py:53
  50.6 1.0 %fusion.60 = f32[64,768]{1,0:T(8,128)} fusion(s32[768]{0:T(1024)S(1)} %add_select_fusion, f32[64,12]{0,1:T(8,128)S(1)} %maximum_select_fusion.1, f32[64,12]{0,1:T(8,128)S(1)} %convolution_multiply_fusion.3), kind=kOutput, calls=%fused_computation.90 | convolution fusion | flops 7088640 | bytes 205824 | tf_op jit(solution)/shard_map/dot_general | solution.py:53
  51.6 0.3 add_convert_fusion
  51.9 0.2 collective-permute-start.8
  52.0 1.3 %pad_maximum_fusion.2 = bf16[4,192,768]{2,1,0:T(8,128)(2,1)S(1)} fusion(bf16[4,64,768]{2,1,0:T(8,128)(2,1)} %collective-permute-done.5, bf16[4,64,768]{2,1,0:T(8,128)(2,1)} %collective-permute-done.4, bf16[4,64,768]{2,1,0:T(8,128)(2,1)} %collective-permute-done.3), kind=kLoop, calls=%fused_computation.42 | loop fusion | flops 3538944 | bytes 2359296 | tf_op jit(solution)/shard_map/concatenate | solution.py:168
  53.4 2.0 %convolution_convert_fusion.2 = bf16[768,1536]{1,0:T(8,128)(2,1)S(1)} fusion(bf16[768,768]{1,0:T(8,128)(2,1)S(1)} %bitcast.63, bf16[768,2304]{1,0:T(8,128)(2,1)S(1)} %copy-done.3), kind=kOutput, calls=%fused_computation.11 | convolution fusion | flops 1813118976 | bytes 5898240 | tf_op jit(solution)/shard_map/dot_general | solution.py:34
  55.4 0.2 fusion.123
  55.6 0.8 copy-done.4
  56.5 1.9 %pad_maximum_fusion = (bf16[4,256,768]{2,1,0:T(8,128)(2,1)}, bf16[4,256,768]{2,1,0:T(8,128)(2,1)}) fusion(bf16[4,192,768]{2,1,0:T(8,128)(2,1)S(1)} %get-tuple-element.8, bf16[4,64,768]{2,1,0:T(8,128)(2,1)S(1)} %copy-done.5, bf16[4,192,768]{2,1,0:T(8,128)(2,1)S(1)} %get-tuple-element.7, bf16[4,64,768]{2,1,0:T(8,128)(2,1)S(1)} %copy-done.4), kind=kLoop, calls=%fused_computation.24 | loop fusion | flops 6291456 | bytes 6291456 | tf_op jit(solution)/shard_map/concatenate | solution.py:173
  58.4 2.6 %copy.42 = bf16[4,256,768]{1,2,0:T(8,128)(2,1)} copy(bf16[4,256,768]{2,1,0:T(8,128)(2,1)} %get-tuple-element.29) | data formatting | bytes 3145728 | tf_op jit(solution)/shard_map/concatenate | solution.py:173
  60.9 2.6 %copy.43 = bf16[4,256,768]{1,2,0:T(8,128)(2,1)} copy(bf16[4,256,768]{2,1,0:T(8,128)(2,1)} %get-tuple-element.30) | data formatting | bytes 3145728 | tf_op jit(solution)/shard_map/concatenate | solution.py:172
  63.5 2.1 %fusion.8 = (f32[4,12,64]{2,1,0:T(8,128)S(1)}, f32[4,12,64,256]{3,2,1,0:T(8,128)S(1)}) fusion(pred[4,64,256]{2,1,0:T(8,128)(4,1)S(1)} %fusion.44, bf16[4,256,12,64]{1,3,2,0:T(8,128)(2,1)} %bitcast.58, bf16[4,64,12,64]{3,2,1,0:T(8,128)(2,1)S(1)} %reshape.106), kind=kOutput, calls=%fused_computation.14 | convolution fusion | flops 103019520 | bytes 5189632 | tf_op jit(solution)/shard_map/rqhd,rkhd->rhqk/dot_general | solution.py:188
  65.7 1.2 %fusion.9 = f32[4,12,64]{2,1,0:T(8,128)S(1)} fusion(f32[4,12,64,256]{3,2,1,0:T(8,128)S(1)} %get-tuple-element.22, f32[4,12,64]{2,1,0:T(8,128)S(1)} %copy_maximum_fusion, pred[4,64,256]{2,1,0:T(8,128)(4,1)S(1)} %fusion.44), kind=kLoop, calls=%fused_computation.15 | loop fusion | flops 3142656 | bytes 3235840 | tf_op jit(solution)/shard_map/reduce_sum | solution.py:197
  67.1 1.3 %fusion.18 = f32[4,12,64,64]{3,2,1,0:T(8,128)S(1)} fusion(bf16[4,256,12,64]{1,3,2,0:T(8,128)(2,1)S(1)} %bitcast.57, f32[4,12,64,256]{3,2,1,0:T(8,128)S(1)} %get-tuple-element.22, f32[4,12,64]{2,1,0:T(8,128)S(1)} %copy_maximum_fusion, pred[4,64,256]{2,1,0:T(8,128)(4,1)S(1)} %fusion.44), kind=kOutput, calls=%fused_computation.23 | convolution fusion | flops 103809024 | bytes 5582848 | tf_op jit(solution)/shard_map/rhqk,rkhd->rqhd/dot_general | solution.py:198
  68.5 0.4 fusion.27
  68.9 0.3 fusion.54
  69.2 0.9 collective-permute-start.10
  70.1 4.2 %collective-permute-done.10 = bf16[32,768]{1,0:T(8,128)(2,1)S(1)} collective-permute-done((bf16[32,768]{1,0:T(8,128)(2,1)S(1)}, bf16[32,768]{1,0:T(8,128)(2,1)S(1)}, u32[]{:S(2)}, u32[]{:S(2)}) %collective-permute-start.10) | collective-permute-done | bytes 49184 | tf_op jit(solution)/shard_map/ppermute | solution.py:59
  74.3 0.3 fusion.57
  74.6 0.4 fusion.21
  75.0 0.6 copy.52
  75.6 1.2 %convert_element_type.99 = bf16[256,768]{0,1:T(8,128)(2,1)} reshape(bf16[4,64,12,64]{1,0,3,2:T(4,128)(2,1)S(1)} %copy.52) | data formatting | bytes 786432 | tf_op jit(solution)/shard_map/convert_element_type | solution.py:205
  76.9 0.4 fusion.51
  77.3 0.2 copy.53
  77.5 1.8 %fusion.74 = (f32[320]{0:T(512)S(1)}, f32[320,768]{1,0:T(8,128)S(1)}) fusion(bf16[64,768]{1,0:T(8,128)(2,1)S(1)} %copy-done.11, bf16[256,768]{1,0:T(8,128)(2,1)} %bitcast.67, bf16[768,768]{1,0:T(8,128)(2,1)S(1)} %copy-done, bf16[64,768]{0,1:T(8,128)(2,1)S(1)} %copy.53, bf16[256,768]{0,1:T(8,128)(2,1)} %convert_element_type.99), kind=kOutput, calls=%fused_computation.105 | convolution fusion | flops 379944640 | bytes 3147008 | tf_op jit(solution)/shard_map/dot_general | solution.py:24
  79.3 0.3 multiply_reduce_fusion.1
  79.7 7.5 %fusion.127 = (f32[320]{0:T(512)S(1)}, f32[320,768]{1,0:T(8,128)S(1)}) fusion(bf16[3072,768]{1,0:T(8,128)(2,1)} %param.18, bf16[768,3072]{1,0:T(8,128)(2,1)} %param.17, f32[768]{0:T(1024)S(1)} %copy-done.18, f32[320]{0:T(512)S(1)} %add_rsqrt_fusion.1, f32[320]{0:T(512)S(1)} %broadcast_multiply_fusion.1, f32[320,768]{1,0:T(8,128)S(1)} %get-tuple-element.26, ...), kind=kOutput, calls=%fused_computation.182 | convolution fusion | flops 3033906944 | bytes 11901696 | tf_op jit(solution)/shard_map/dot_general | solution.py:29
  87.2 0.3 multiply_reduce_fusion
  87.5 0.2 multiply_convert_fusion
  87.7 0.8 slice.82
  88.5 0.6 slice.83
  (77 shorter events, 1.5 us)
Async XLA Ops:
  0.6 76.8 %copy-start = (bf16[768,768]{1,0:T(8,128)(2,1)S(1)}, bf16[768,768]{1,0:T(8,128)(2,1)}, u32[]{:S(2)}) copy-start(bf16[768,768]{1,0:T(8,128)(2,1)} %param.15) | copy-start | bytes 3538948
  0.6 51.4 %collective-permute-start.5 = (bf16[4,64,768]{2,1,0:T(8,128)(2,1)}, bf16[4,64,768]{2,1,0:T(8,128)(2,1)}, u32[]{:S(2)}, u32[]{:S(2)}) collective-permute-start(bf16[4,64,768]{2,1,0:T(8,128)(2,1)} %param.10), channel_id=1, source_target_pairs={{0,3},{1,2},{2,1},{3,0},{4,7},{5,6},{6,5},{7,4},{8,11},{9,10},{10,... | collective-permute-start | bytes 1179656 | tf_op jit(solution)/shard_map/ppermute | solution.py:124
  4.6 47.4 %collective-permute-start.4 = (bf16[4,64,768]{2,1,0:T(8,128)(2,1)}, bf16[4,64,768]{2,1,0:T(8,128)(2,1)}, u32[]{:S(2)}, u32[]{:S(2)}) collective-permute-start(bf16[4,64,768]{2,1,0:T(8,128)(2,1)} %param.10), channel_id=1, source_target_pairs={{0,2},{1,3},{2,0},{3,1},{4,6},{5,7},{6,4},{7,5},{8,10},{9,11},{10,... | collective-permute-start | bytes 1179656 | tf_op jit(solution)/shard_map/ppermute | solution.py:124
  5.1 46.9 %collective-permute-start.3 = (bf16[4,64,768]{2,1,0:T(8,128)(2,1)}, bf16[4,64,768]{2,1,0:T(8,128)(2,1)}, u32[]{:S(2)}, u32[]{:S(2)}) collective-permute-start(bf16[4,64,768]{2,1,0:T(8,128)(2,1)} %param.10), channel_id=1, source_target_pairs={{0,1},{1,0},{2,3},{3,2},{4,5},{5,4},{6,7},{7,6},{8,9},{9,8},{10,11... | collective-permute-start | bytes 1179656 | tf_op jit(solution)/shard_map/ppermute | solution.py:124
  5.3 5.1 %collective-permute-start = (bf16[64,768]{1,0:T(8,128)(2,1)}, bf16[64,768]{1,0:T(8,128)(2,1)S(1)}, u32[]{:S(2)}, u32[]{:S(2)}) collective-permute-start(bf16[64,768]{1,0:T(8,128)(2,1)} %bitcast.71), channel_id=1, source_target_pairs={{0,4},{4,0},{8,12},{12,8},{16,20},{20,16},{24,28},{28,24},{1,5},{5... | collective-permute-start | bytes 294920 | tf_op jit(solution)/shard_map/ppermute | solution.py:59
  9.1 1.2 %copy-start.15 = (bf16[1,64,768]{2,1,0:T(8,128)(2,1)S(1)}, bf16[1,64,768]{2,1,0:T(8,128)(2,1)}, u32[]{:S(2)}) copy-start(bf16[1,64,768]{2,1,0:T(8,128)(2,1)} %param.11) | copy-start | bytes 294916
  9.2 3.8 %copy-start.17 = (s32[4,64]{1,0:T(4,128)S(1)}, s32[4,64]{1,0:T(4,128)}, u32[]{:S(2)}) copy-start(s32[4,64]{1,0:T(4,128)} %param.13) | copy-start | bytes 3076
  11.0 5.7 %collective-permute-start.1 = (bf16[64,768]{1,0:T(8,128)(2,1)}, bf16[64,768]{1,0:T(8,128)(2,1)}, u32[]{:S(2)}, u32[]{:S(2)}) collective-permute-start(bf16[64,768]{1,0:T(8,128)(2,1)} %broadcast_select_fusion), channel_id=1, source_target_pairs={{0,8},{4,12},{8,0},{12,4},{16,24},{20,28},{24,16},{28,20},{1,9},{5... | collective-permute-start | bytes 294920 | tf_op jit(solution)/shard_map/ppermute | solution.py:59
  17.6 7.6 %collective-permute-start.2 = (bf16[64,768]{1,0:T(8,128)(2,1)S(1)}, bf16[64,768]{1,0:T(8,128)(2,1)S(1)}, u32[]{:S(2)}, u32[]{:S(2)}) collective-permute-start(bf16[64,768]{1,0:T(8,128)(2,1)S(1)} %broadcast_select_fusion.1), channel_id=1, source_target_pairs={{0,16},{4,20},{8,24},{12,28},{16,0},{20,4},{24,8},{28,12},{1,17},{... | collective-permute-start | bytes 294920 | tf_op jit(solution)/shard_map/ppermute | solution.py:59
  25.3 4.2 %copy-start.10 = (bf16[64,768]{1,0:T(8,128)(2,1)}, bf16[64,768]{1,0:T(8,128)(2,1)S(1)}, u32[]{:S(2)}) copy-start(bf16[64,768]{1,0:T(8,128)(2,1)S(1)} %broadcast_select_fusion.2) | copy-start | bytes 294916
  28.1 3.1 %copy-start.8 = (bf16[64,2304]{1,0:T(8,128)(2,1)}, bf16[64,2304]{1,0:T(8,128)(2,1)S(1)}, u32[]{:S(2)}) copy-start(bf16[64,2304]{1,0:T(8,128)(2,1)S(1)} %convolution_convert_fusion.1) | copy-start | bytes 884740
  29.8 0.7 copy-start.6
  30.0 5.7 %collective-permute-start.14 = (f32[32,12]{0,1:T(8,128)S(1)}, f32[32,12]{0,1:T(8,128)S(1)}, u32[]{:S(2)}, u32[]{:S(2)}) collective-permute-start(f32[32,12]{0,1:T(8,128)S(1)} %slice_select_fusion.1), channel_id=1, source_target_pairs={{0,4},{4,0},{8,12},{12,8},{16,20},{20,16},{24,28},{28,24},{1,5},{5... | collective-permute-start | bytes 4616 | tf_op jit(solution)/shard_map/ppermute | solution.py:59
  30.0 5.7 %collective-permute-start.7 = (f32[32,12]{0,1:T(8,128)S(1)}, f32[32,12]{0,1:T(8,128)S(1)}, u32[]{:S(2)}, u32[]{:S(2)}) collective-permute-start(f32[32,12]{0,1:T(8,128)S(1)} %slice_select_fusion.2), channel_id=1, source_target_pairs={{0,4},{4,0},{8,12},{12,8},{16,20},{20,16},{24,28},{28,24},{1,5},{5... | collective-permute-start | bytes 4616 | tf_op jit(solution)/shard_map/ppermute | solution.py:59
  31.2 20.5 %copy-start.7 = (f32[64,768]{1,0:T(8,128)S(1)}, f32[64,768]{1,0:T(8,128)}, u32[]{:S(2)}) copy-start(f32[64,768]{1,0:T(8,128)} %copy-done.6) | copy-start | bytes 589828
  31.2 3.2 %copy-start.9 = (bf16[64,2304]{1,0:T(8,128)(2,1)S(1)}, bf16[64,2304]{1,0:T(8,128)(2,1)}, u32[]{:S(2)}) copy-start(bf16[64,2304]{1,0:T(8,128)(2,1)} %copy-done.8) | copy-start | bytes 884740
  35.7 17.7 %copy-start.3 = (bf16[768,2304]{1,0:T(8,128)(2,1)S(1)}, bf16[768,2304]{1,0:T(8,128)(2,1)}, u32[]{:S(2)}) copy-start(bf16[768,2304]{1,0:T(8,128)(2,1)} %param.14) | copy-start | bytes 10616836
  35.8 3.7 %collective-permute-start.15 = (f32[32,12]{0,1:T(8,128)S(1)}, f32[32,12]{0,1:T(8,128)S(1)}, u32[]{:S(2)}, u32[]{:S(2)}) collective-permute-start(f32[32,12]{0,1:T(8,128)S(1)} %get-tuple-element.4), channel_id=1, source_target_pairs={{0,8},{4,12},{8,0},{12,4},{16,24},{20,28},{24,16},{28,20},{1,9},{5... | collective-permute-start | bytes 4616 | tf_op jit(solution)/shard_map/ppermute | solution.py:59
  36.6 3.7 %collective-permute-start.9 = (f32[32,12]{0,1:T(8,128)S(1)}, f32[32,12]{0,1:T(8,128)S(1)}, u32[]{:S(2)}, u32[]{:S(2)}) collective-permute-start(f32[32,12]{0,1:T(8,128)S(1)} %get-tuple-element.5), channel_id=1, source_target_pairs={{0,8},{4,12},{8,0},{12,4},{16,24},{20,28},{24,16},{28,20},{1,9},{5... | collective-permute-start | bytes 4616 | tf_op jit(solution)/shard_map/ppermute | solution.py:59
  40.2 5.1 %collective-permute-start.16 = (f32[32,12]{0,1:T(8,128)S(1)}, f32[32,12]{0,1:T(8,128)S(1)}, u32[]{:S(2)}, u32[]{:S(2)}) collective-permute-start(f32[32,12]{0,1:T(8,128)S(1)} %get-tuple-element.2), channel_id=1, source_target_pairs={{0,16},{4,20},{8,24},{12,28},{16,0},{20,4},{24,8},{28,12},{1,17},{... | collective-permute-start | bytes 4616 | tf_op jit(solution)/shard_map/ppermute | solution.py:59
  43.7 4.5 %collective-permute-start.11 = (f32[32,12]{0,1:T(8,128)S(1)}, f32[32,12]{0,1:T(8,128)S(1)}, u32[]{:S(2)}, u32[]{:S(2)}) collective-permute-start(f32[32,12]{0,1:T(8,128)S(1)} %get-tuple-element.3), channel_id=1, source_target_pairs={{0,16},{4,20},{8,24},{12,28},{16,0},{20,4},{24,8},{28,12},{1,17},{... | collective-permute-start | bytes 4616 | tf_op jit(solution)/shard_map/ppermute | solution.py:59
  45.3 6.3 %collective-permute-start.6 = (f32[32,768]{1,0:T(8,128)}, f32[32,768]{1,0:T(8,128)S(1)}, u32[]{:S(2)}, u32[]{:S(2)}) collective-permute-start(f32[32,768]{1,0:T(8,128)} %slice_select_fusion), channel_id=1, source_target_pairs={{0,4},{4,0},{8,12},{12,8},{16,20},{20,16},{24,28},{28,24},{1,5},{5... | collective-permute-start | bytes 294920 | tf_op jit(solution)/shard_map/ppermute | solution.py:59
  48.3 1.2 %collective-permute-start.13 = (f32[32,12]{0,1:T(8,128)S(1)}, f32[32,12]{0,1:T(8,128)S(1)}, u32[]{:S(2)}, u32[]{:S(2)}) collective-permute-start(f32[32,12]{0,1:T(8,128)S(1)} %get-tuple-element.18), channel_id=1, source_target_pairs={{0,4},{4,0},{8,12},{12,8},{16,20},{20,16},{24,28},{28,24},{1,5},{5... | collective-permute-start | bytes 4616 | tf_op jit(solution)/shard_map/ppermute | solution.py:59
  49.5 27.4 %collective-permute-start.17 = (f32[32,12]{0,1:T(8,128)S(1)}, f32[32,12]{0,1:T(8,128)S(1)}, u32[]{:S(2)}, u32[]{:S(2)}) collective-permute-start(f32[32,12]{0,1:T(8,128)S(1)} %get-tuple-element.17), channel_id=1, source_target_pairs={{0,4},{4,0},{8,12},{12,8},{16,20},{20,16},{24,28},{28,24},{1,5},{5... | collective-permute-start | bytes 4616 | tf_op jit(solution)/shard_map/ppermute | solution.py:59
  51.9 17.1 %collective-permute-start.8 = (bf16[32,768]{1,0:T(8,128)(2,1)S(1)}, bf16[32,768]{1,0:T(8,128)(2,1)S(1)}, u32[]{:S(2)}, u32[]{:S(2)}) collective-permute-start(bf16[32,768]{1,0:T(8,128)(2,1)S(1)} %add_convert_fusion), channel_id=1, source_target_pairs={{0,8},{4,12},{8,0},{12,4},{16,24},{20,28},{24,16},{28,20},{1,9},{5... | collective-permute-start | bytes 147464 | tf_op jit(solution)/shard_map/ppermute | solution.py:59
  55.4 1.0 %copy-start.4 = (bf16[4,64,768]{2,1,0:T(8,128)(2,1)S(1)}, bf16[4,64,768]{2,1,0:T(8,128)(2,1)}, u32[]{:S(2)}) copy-start(bf16[4,64,768]{2,1,0:T(8,128)(2,1)} %get-tuple-element.12) | copy-start | bytes 1179652
  55.4 1.1 %copy-start.5 = (bf16[4,64,768]{2,1,0:T(8,128)(2,1)S(1)}, bf16[4,64,768]{2,1,0:T(8,128)(2,1)}, u32[]{:S(2)}) copy-start(bf16[4,64,768]{2,1,0:T(8,128)(2,1)} %get-tuple-element.13) | copy-start | bytes 1179652
  65.7 1.4 %copy-start.2 = (bf16[4,256,768]{1,2,0:T(8,128)(2,1)S(1)}, bf16[4,256,768]{1,2,0:T(8,128)(2,1)}, u32[]{:S(2)}) copy-start(bf16[4,256,768]{1,2,0:T(8,128)(2,1)} %copy.42) | copy-start | bytes 4718596
  67.1 1.4 %copy-start.1 = (f32[12,64,4,64]{3,1,2,0:T(8,128)S(1)}, f32[12,64,4,64]{3,1,2,0:T(8,128)}, u32[]{:S(2)}) copy-start(f32[12,64,4,64]{3,1,2,0:T(8,128)} %get-tuple-element.24) | copy-start | bytes 2359300
  69.2 5.1 %collective-permute-start.10 = (bf16[32,768]{1,0:T(8,128)(2,1)S(1)}, bf16[32,768]{1,0:T(8,128)(2,1)S(1)}, u32[]{:S(2)}, u32[]{:S(2)}) collective-permute-start(bf16[32,768]{1,0:T(8,128)(2,1)S(1)} %fusion.54), channel_id=1, source_target_pairs={{0,16},{4,20},{8,24},{12,28},{16,0},{20,4},{24,8},{28,12},{1,17},{... | collective-permute-start | bytes 147464 | tf_op jit(solution)/shard_map/ppermute | solution.py:59
  74.5 2.3 %collective-permute-start.12 = (f32[32,768]{1,0:T(8,128)S(1)}, f32[32,768]{1,0:T(8,128)S(1)}, u32[]{:S(2)}, u32[]{:S(2)}) collective-permute-start(f32[32,768]{1,0:T(8,128)S(1)} %fusion.57), channel_id=1, source_target_pairs={{0,4},{4,0},{8,12},{12,8},{16,20},{20,16},{24,28},{28,24},{1,5},{5... | collective-permute-start | bytes 294920 | tf_op jit(solution)/shard_map/ppermute | solution.py:59
  75.0 1.9 %copy-start.13 = (f32[64,768]{1,0:T(8,128)S(1)}, f32[64,768]{1,0:T(8,128)}, u32[]{:S(2)}) copy-start(f32[64,768]{1,0:T(8,128)} %fusion.59) | copy-start | bytes 589828
  75.0 1.9 %copy-start.14 = (f32[64,768]{1,0:T(8,128)S(1)}, f32[64,768]{1,0:T(8,128)}, u32[]{:S(2)}) copy-start(f32[64,768]{1,0:T(8,128)} %fusion.60) | copy-start | bytes 589828
  75.0 2.5 %copy-start.11 = (bf16[64,768]{1,0:T(8,128)(2,1)S(1)}, bf16[64,768]{1,0:T(8,128)(2,1)}, u32[]{:S(2)}) copy-start(bf16[64,768]{1,0:T(8,128)(2,1)} %copy-done.10) | copy-start | bytes 294916
  77.5 1.9 %copy-start.12 = (bf16[4,64,768]{2,1,0:T(8,128)(2,1)S(1)}, bf16[4,64,768]{2,1,0:T(8,128)(2,1)}, u32[]{:S(2)}) copy-start(bf16[4,64,768]{2,1,0:T(8,128)(2,1)} %param.10) | copy-start | bytes 1179652
  77.5 2.2 %copy-start.18 = (f32[768]{0:T(1024)S(1)}, f32[768]{0:T(1024)}, u32[]{:S(2)}) copy-start(f32[768]{0:T(1024)} %param.16) | copy-start | bytes 9220
  79.7 7.8 %copy-start.16 = (f32[768]{0:T(1024)S(1)}, f32[768]{0:T(1024)}, u32[]{:S(2)}) copy-start(f32[768]{0:T(1024)} %param.19) | copy-start | bytes 9220

commit v7 on v5

--- a/solution.py
+++ b/solution.py
@@ -69,55 +69,56 @@
     return value
 
 
-def merge(lo, hi, width):
-    top = jnp.maximum(lo[:, width + HEADS :], hi[:, width + HEADS :])
-    fade_lo = jnp.exp(lo[:, width + HEADS :] - top)
-    fade_hi = jnp.exp(hi[:, width + HEADS :] - top)
-    total = lo[:, width : width + HEADS] * fade_lo + hi[:, width : width + HEADS] * fade_hi
-    fades = head_spread(jnp.concatenate([fade_lo, fade_hi], axis=0))
-    rows = lo.shape[0]
-    mixed = lo[:, :width] * fades[:rows] + hi[:, :width] * fades[rows:]
-    return jnp.concatenate([mixed, total, top], axis=-1)
-
-
-def all_merge(value, axis, count, width, fillers, state):
+def merge(lo, hi):
+    top = jnp.maximum(lo[2], hi[2])
+    fade_lo = jnp.exp(lo[2] - top)
+    fade_hi = jnp.exp(hi[2] - top)
+    total = lo[1] * fade_lo + hi[1] * fade_hi
+    mixed = lo[0] * head_spread(fade_lo) + hi[0] * head_spread(fade_hi)
+    return mixed, total, top
+
+
+def pick(flag, a, b):
+    return tuple(jnp.where(flag, x, y) for x, y in zip(a, b))
+
+
+def all_merge(value, axis, count, fillers, state):
     here = lax.axis_index(axis)
-    rounds = [0]
-
-    def exchange(sent, state):
-        k = rounds[0]
-        rounds[0] += 1
-        if k < len(fillers):
+    rounds = []
+
+    def exchange(sent, step, state):
+        filler = fillers[len(rounds)] if len(rounds) < len(fillers) else None
+        rounds.append(step)
+        if filler is not None:
             sent, state = lax.optimization_barrier((sent, state))
-        got = [partner(s, axis, step_of[k], count) for s in sent]
-        if k < len(fillers):
-            state = fillers[k](state)
+        got = tuple(partner(v, axis, step, count) for v in sent)
+        if filler is not None:
+            state = filler(state)
             got, state = lax.optimization_barrier((got, state))
         return got, state
 
-    steps = []
+    half = value[0].shape[0] // 2
+    first = (here & 1) == 0
+    top_half = tuple(v[:half] for v in value)
+    low_half = tuple(v[half:] for v in value)
+    mine = pick(first, top_half, low_half)
+    sent = pick(first, low_half, top_half)
+    got, state = exchange(sent, 1, state)
+    value = merge(pick(first, mine, got), pick(first, got, mine))
     step = 2
     while step < count:
-        steps.append(step)
+        mixed = value[0].astype(jnp.bfloat16)
+        got, state = exchange((mixed, value[1], value[2]), step, state)
+        got = (got[0].astype(jnp.float32), got[1], got[2])
+        mine = (mixed.astype(jnp.float32), value[1], value[2])
+        low_side = (here & step) == 0
+        value = merge(pick(low_side, mine, got), pick(low_side, got, mine))
         step *= 2
-    step_of = [1] + steps + [1]
-
-    half = value.shape[0] // 2
-    first = (here & 1) == 0
-    mine = jnp.where(first, value[:half], value[half:])
-    sent = jnp.where(first, value[half:], value[:half])
-    (got,), state = exchange([sent], state)
-    value = merge(jnp.where(first, mine, got), jnp.where(first, got, mine), width)
-    for step in steps:
-        mixed = value[:, :width].astype(jnp.bfloat16)
-        stats = value[:, width:]
-        (got_mixed, got_stats), state = exchange([mixed, stats], state)
-        mine = jnp.concatenate([mixed.astype(jnp.float32), stats], axis=-1)
-        got = jnp.concatenate([got_mixed.astype(jnp.float32), got_stats], axis=-1)
-        low_side = (here & step) == 0
-        value = merge(jnp.where(low_side, mine, got), jnp.where(low_side, got, mine), width)
-    (got,), state = exchange([value], state)
-    value = jnp.where(first, jnp.concatenate([value, got]), jnp.concatenate([got, value]))
+    got, state = exchange(value, 1, state)
+    value = tuple(
+        jnp.where(first, jnp.concatenate([v, g]), jnp.concatenate([g, v]))
+        for v, g in zip(value, got)
+    )
     return value, state
 
 
@@ -164,7 +165,6 @@
     col_weights = head_spread(col_exp.astype(jnp.bfloat16).astype(jnp.float32))
     part_mixed = (col_weights * own_vals.astype(jnp.float32)).sum(0)
     part_total = col_exp.sum(0)
-    packed = jnp.concatenate([part_mixed, part_total, part_top], axis=-1)
 
     sources = [own_group] + [s for s, _ in row_parts]
     q4 = queries.reshape(row_count, cols_dev, HEADS, HEAD_DIM)
@@ -214,17 +214,18 @@
         attended = mixed / row_total.transpose(0, 2, 1)[..., None]
         return attended.reshape(row_count * cols_dev, model_width).astype(jnp.bfloat16)
 
-    packed, attended = all_merge(
-        packed, "band", n_band, model_width,
-        [scores_stage, weights_stage, output_stage],
+    merged, attended = all_merge(
+        (part_mixed, part_total, part_top), "band", n_band,
+        [None, scores_stage, weights_stage, output_stage],
         [got for _, got in row_parts],
     )
-    col_top = jnp.maximum(packed[:, model_width + HEADS :], self_scores)
-    fade = jnp.exp(packed[:, model_width + HEADS :] - col_top)
+    col_top = jnp.maximum(merged[2], self_scores)
+    fade = jnp.exp(merged[2] - col_top)
     self_exp = jnp.exp(self_scores - col_top)
-    col_total = packed[:, model_width : model_width + HEADS] * fade + self_exp
-    spreads = head_spread(jnp.concatenate([fade, self_exp.astype(jnp.bfloat16).astype(jnp.float32)], axis=0))
-    col_mixed = packed[:, :model_width] * spreads[:cols_dev] + spreads[cols_dev:] * sum_vals.astype(jnp.float32)
+    col_total = merged[1] * fade + self_exp
+    col_mixed = merged[0] * head_spread(fade) + head_spread(
+        self_exp.astype(jnp.bfloat16).astype(jnp.float32)
+    ) * sum_vals.astype(jnp.float32)
     summary_att = (col_mixed / head_spread(col_total)).astype(jnp.bfloat16)
 
     all_in = jnp.concatenate([flat_cells, tokens], axis=0)

time: 96 us -> 90.2 us (0.940)
  other arithmetic: 21.5 us -> 13.7 us
  starting transfers between devices: 14.9 us -> 19.6 us
  waiting for transfers between devices: 11.1 us -> 8.2 us
  matrix products: 30.1 us -> 31.9 us
  local copies, waits for them, and re-layouts: 15.8 us -> 14.5 us
    ppermute x9 -> x15, starting transfers between devices: 10.4 us -> 15.1 us  [partner(): return lax.ppermute(value, axis, [(i, i ^ step) for i in range(count)])]
    convert_element_type x4 -> x0, other arithmetic: 3.09 us -> none  [the longest x2 3.08 us: all_merge(): mine = jnp.concatenate([mixed.astype(jnp.float32), stats], axis=-1)]
    ppermute x9 -> x15, waiting for transfers between devices: 11.1 us -> 8.19 us  [partner(): return lax.ppermute(value, axis, [(i, i ^ step) for i in range(count)])]
    concatenate x4 -> x0, other arithmetic: 2.37 us -> none  [the longest x3 2.29 us: merge(): return jnp.concatenate([mixed, total, top], axis=-1)]
    unnamed x50 -> x34, local copies, waits for them, and re-layouts: 3.62 us -> 1.52 us
    reshape x0 -> x2, local copies, waits for them, and re-layouts: none -> 1.68 us  [the longest x1 0.87 us: local(): sk = sum_keys.reshape(cols_dev, HEADS, HEAD_DIM)]
    dot_general x1, matrix products: 1.52 us -> 0.35 us  [output_stage(): jnp.einsum('rhqk,khd->rqhd', tok_weights, sv, preferred_element_type=jnp....]
    dot_general x1, matrix products: 0.68 us -> 1.8 us  [finish(): mixed_out = jnp.dot(attended, w_out, preferred_element_type=jnp.float32)]
  transfers between devices with their start and end apart: 12 -> 18, of which waited for: 5 -> 5; matrix products, arithmetic and copies ran while one was open for 27% -> 31% of each run, Pallas kernels for 0% -> 0%
where the time goes in v7:
time: 90.2 us; the launch traced here: 89.7 us
  matrix products  31.9 us (35%)
  starting transfers between devices  19.6 us (22%)
  local copies, waits for them, and re-layouts  14.5 us (16%)
  other arithmetic  13.7 us (15%)
  waiting for transfers between devices  8.2 us (9%)
  between operations  1.74 us (2%)
    ppermute x15, starting transfers between devices, partner(): return lax.ppermute(value, axis, [(i, i ^ step) for i in range(count)])  15.1 us
    dot_general x3, matrix products, project(): jnp.dot(values, weight, preferred_element_type=jnp.float32)  9.61 us
    ppermute x15, waiting for transfers between devices, partner(): return lax.ppermute(value, axis, [(i, i ^ step) for i in range(count)])  8.19 us
    dot_general x1, matrix products, finish(): outer_out = jnp.dot(inner_act, w_down, preferred_element_type=jnp.float32)  7.43 us
    ppermute x3, starting transfers between devices, fan_out(): got.append((source, lax.ppermute(value, axis, pairs)))  4.55 us
    dot_general x1, matrix products, scores_stage(): jnp.einsum('rqhd,rkhd->rhqk', q4, k4, preferred_element_type=jnp.float32)  3.99 us
    dot_general x10, matrix products, head_spread(): jnp.dot(flat, head_matrix(), precision=lax.Precision.HIGHEST, preferred_e...  3.89 us
    reduce_sum x2, other arithmetic, weights_stage(): row_total = cell_exp.sum(-1) + tok_exp.sum(-1)  3.36 us
  transfers between devices with their start and end apart: 18, of which 5 were waited for; matrix products, arithmetic and copies ran while one was open for 31% of the time, Pallas kernels for 0%

profile of v7, /device:TPU:0, one launch (start us, length us, event | category | flops | bytes accessed | tf_op | source)
XLA Modules:
  0.0 89.7 jit_solution(11407067902298544024)
XLA Ops:
  0.6 3.0 %collective-permute-start.6 = (bf16[4,64,768]{2,1,0:T(8,128)(2,1)}, bf16[4,64,768]{2,1,0:T(8,128)(2,1)}, u32[]{:S(2)}, u32[]{:S(2)}) collective-permute-start(bf16[4,64,768]{2,1,0:T(8,128)(2,1)} %param.10), channel_id=1, source_target_pairs={{0,1},{1,0},{2,3},{3,2},{4,5},{5,4},{6,7},{7,6},{8,9},{9,8},{10,11... | collective-permute-start | bytes 1179656 | tf_op jit(solution)/shard_map/ppermute | solution.py:135
  3.6 1.5 %collective-permute-start.7 = (bf16[4,64,768]{2,1,0:T(8,128)(2,1)}, bf16[4,64,768]{2,1,0:T(8,128)(2,1)}, u32[]{:S(2)}, u32[]{:S(2)}) collective-permute-start(bf16[4,64,768]{2,1,0:T(8,128)(2,1)} %param.10), channel_id=1, source_target_pairs={{0,2},{1,3},{2,0},{3,1},{4,6},{5,7},{6,4},{7,5},{8,10},{9,11},{10,... | collective-permute-start | bytes 1179656 | tf_op jit(solution)/shard_map/ppermute | solution.py:135
  5.8 3.2 %convolution_convert_fusion = bf16[256,2304]{1,0:T(8,128)(2,1)S(1)} fusion(bf16[256,768]{1,0:T(8,128)(2,1)} %bitcast.61, bf16[768,2304]{1,0:T(8,128)(2,1)} %param.14), kind=kOutput, calls=%fused_computation.9 | convolution fusion | flops 906559488 | bytes 5111808 | tf_op jit(solution)/shard_map/dot_general | solution.py:34
  9.1 0.9 fusion.116
  10.1 2.1 %collective-permute-start.1 = (bf16[64,768]{1,0:T(8,128)(2,1)S(1)}, bf16[64,768]{1,0:T(8,128)(2,1)S(1)}, u32[]{:S(2)}, u32[]{:S(2)}) collective-permute-start(bf16[64,768]{1,0:T(8,128)(2,1)S(1)} %broadcast_select_fusion), channel_id=1, source_target_pairs={{0,8},{4,12},{8,0},{12,4},{16,24},{20,28},{24,16},{28,20},{1,9},{5... | collective-permute-start | bytes 294920 | tf_op jit(solution)/shard_map/ppermute | solution.py:59
  12.2 0.7 fusion.45
  12.9 1.6 %reshape.103 = bf16[4,64,12,64]{3,2,1,0:T(8,128)(2,1)} reshape(bf16[4,64,768]{2,1,0:T(8,128)(2,1)S(1)} %get-tuple-element.80) | data formatting | bytes 786432 | tf_op jit(solution)/shard_map/reshape | solution.py:170
  14.5 1.1 %collective-permute-done.1 = bf16[64,768]{1,0:T(8,128)(2,1)S(1)} collective-permute-done((bf16[64,768]{1,0:T(8,128)(2,1)S(1)}, bf16[64,768]{1,0:T(8,128)(2,1)S(1)}, u32[]{:S(2)}, u32[]{:S(2)}) %collective-permute-start.1) | collective-permute-done | bytes 98336 | tf_op jit(solution)/shard_map/ppermute | solution.py:59
  15.7 2.8 %collective-permute-start.2 = (bf16[64,768]{1,0:T(8,128)(2,1)S(1)}, bf16[64,768]{1,0:T(8,128)(2,1)S(1)}, u32[]{:S(2)}, u32[]{:S(2)}) collective-permute-start(bf16[64,768]{1,0:T(8,128)(2,1)S(1)} %broadcast_select_fusion.1), channel_id=1, source_target_pairs={{0,16},{4,20},{8,24},{12,28},{16,0},{20,4},{24,8},{28,12},{1,17},{... | collective-permute-start | bytes 294920 | tf_op jit(solution)/shard_map/ppermute | solution.py:59
  18.5 5.0 %collective-permute-done.2 = bf16[64,768]{1,0:T(8,128)(2,1)S(1)} collective-permute-done((bf16[64,768]{1,0:T(8,128)(2,1)S(1)}, bf16[64,768]{1,0:T(8,128)(2,1)S(1)}, u32[]{:S(2)}, u32[]{:S(2)}) %collective-permute-start.2) | collective-permute-done | bytes 98336 | tf_op jit(solution)/shard_map/ppermute | solution.py:59
  23.5 0.6 copy-done.5
  24.1 2.7 %convolution_convert_fusion.1 = bf16[64,2304]{1,0:T(8,128)(2,1)S(1)} fusion(bf16[64,768]{1,0:T(8,128)(2,1)S(1)} %broadcast_select_fusion.2, bf16[768,2304]{1,0:T(8,128)(2,1)} %param.14), kind=kOutput, calls=%fused_computation.10 | convolution fusion | flops 226639872 | bytes 3932160 | tf_op jit(solution)/shard_map/dot_general | solution.py:34
  26.9 0.6 fusion.118
  27.6 0.3 fusion.30
  27.9 0.7 slice_select_fusion.2
  28.6 0.7 slice_select_fusion.1
  29.2 0.5 collective-permute-start.4
  29.7 0.7 slice_select_fusion
  30.4 0.9 reshape.107
  31.3 2.2 %multiply_bitcast_fusion = f32[4,12,64,64]{2,3,0,1:T(8,128)S(1)} fusion(bf16[4,64,12,64]{3,2,1,0:T(8,128)(2,1)} %reshape.103, bf16[64,12,64,1]{2,1,0,3:T(8,128)(2,1)} %bitcast.56), kind=kOutput, calls=%fused_computation.30 | convolution fusion | flops 25362432 | bytes 1277952 | tf_op jit(solution)/shard_map/rqhd,khd->rhqk/dot_general | solution.py:194
  33.5 0.8 convolution_multiply_fusion.3
  34.3 0.8 copy.59
  35.1 0.9 multiply_add_fusion.2
  36.0 0.3 fusion.62
  36.3 0.4 collective-permute-done.3
  36.6 1.2 %add_convert_fusion = bf16[32,768]{1,0:T(8,128)(2,1)S(1)} fusion(f32[32,768]{1,0:T(8,128)S(1)} %collective-permute-done.3, f32[32,768]{1,0:T(8,128)S(1)} %fusion.62, f32[64,768]{1,0:T(8,128)} %copy-done.4, pred[]{:T(512)S(6)} %eq.186, s32[768]{0:T(1024)S(1)} %add_select_fusion, f32[32,12]{0,1:T(8,128)S(1)} %get-tuple-element.38, ...), kind=kOutput, calls=%fused_computation.77 | convolution fusion | flops 3720960 | bytes 451072 | tf_op jit(solution)/shard_map/dot_general | solution.py:53
  37.9 1.3 %pad_maximum_fusion.2 = bf16[4,192,768]{2,1,0:T(8,128)(2,1)S(1)} fusion(bf16[4,64,768]{2,1,0:T(8,128)(2,1)} %collective-permute-done.8, bf16[4,64,768]{2,1,0:T(8,128)(2,1)} %collective-permute-done.7, bf16[4,64,768]{2,1,0:T(8,128)(2,1)} %collective-permute-done.6), kind=kLoop, calls=%fused_computation.37 | loop fusion | flops 3538944 | bytes 2359296 | tf_op jit(solution)/shard_map/concatenate | solution.py:175
  39.2 3.7 %convolution_convert_fusion.2 = bf16[768,1536]{1,0:T(8,128)(2,1)S(1)} fusion(bf16[768,768]{1,0:T(8,128)(2,1)S(1)} %bitcast.55, bf16[768,2304]{1,0:T(8,128)(2,1)} %param.14), kind=kOutput, calls=%fused_computation.11 | convolution fusion | flops 1813118976 | bytes 5898240 | tf_op jit(solution)/shard_map/dot_general | solution.py:34
  42.9 0.2 fusion.115
  43.0 0.8 copy-done.3
  43.9 1.9 %pad_maximum_fusion = (bf16[4,256,768]{2,1,0:T(8,128)(2,1)}, bf16[4,256,768]{2,1,0:T(8,128)(2,1)}) fusion(bf16[4,192,768]{2,1,0:T(8,128)(2,1)S(1)} %get-tuple-element.76, bf16[4,64,768]{2,1,0:T(8,128)(2,1)S(1)} %copy-done.3, bf16[4,192,768]{2,1,0:T(8,128)(2,1)S(1)} %get-tuple-element.75, bf16[4,64,768]{2,1,0:T(8,128)(2,1)S(1)} %get-tuple-element.79), kind=kLoop, calls=%fused_computation.23 | loop fusion | flops 6291456 | bytes 6291456 | tf_op jit(solution)/shard_map/concatenate | solution.py:179
  45.7 2.6 %copy.43 = bf16[4,256,768]{1,2,0:T(8,128)(2,1)} copy(bf16[4,256,768]{2,1,0:T(8,128)(2,1)} %get-tuple-element.93) | data formatting | bytes 3145728 | tf_op jit(solution)/shard_map/concatenate | solution.py:179
  48.4 0.6 collective-permute-start.9
  49.0 1.4 %collective-permute-start.10 = (f32[32,12]{0,1:T(8,128)S(1)}, f32[32,12]{0,1:T(8,128)S(1)}, u32[]{:S(2)}, u32[]{:S(2)}) collective-permute-start(f32[32,12]{0,1:T(8,128)S(1)} %get-tuple-element.37), channel_id=1, source_target_pairs={{0,8},{4,12},{8,0},{12,4},{16,24},{20,28},{24,16},{28,20},{1,9},{5... | collective-permute-start | bytes 4616 | tf_op jit(solution)/shard_map/ppermute | solution.py:59
  50.4 0.6 collective-permute-start.11
  51.0 4.0 %multiply_select_fusion = f32[4,12,64,256]{3,2,1,0:T(8,128)} fusion(bf16[4,256,12,64]{1,3,2,0:T(8,128)(2,1)} %bitcast.50, pred[4,64,256]{2,1,0:T(8,128)(4,1)S(1)} %copy-done.7, bf16[4,64,12,64]{3,2,1,0:T(8,128)(2,1)} %reshape.103), kind=kOutput, calls=%fused_computation.13 | convolution fusion | flops 102236160 | bytes 5177344 | tf_op jit(solution)/shard_map/rqhd,rkhd->rhqk/dot_general | solution.py:190
  55.0 2.6 %copy.47 = bf16[4,256,768]{1,2,0:T(8,128)(2,1)} copy(bf16[4,256,768]{2,1,0:T(8,128)(2,1)} %get-tuple-element.94) | data formatting | bytes 3145728 | tf_op jit(solution)/shard_map/concatenate | solution.py:180
  57.6 0.3 fusion.59
  57.9 0.3 fusion.51
  58.2 2.4 %reduce_max.28 = f32[4,12,64]{2,1,0:T(8,128)S(1)} reduce(f32[4,12,64,256]{3,2,1,0:T(8,128)} %multiply_select_fusion, f32[]{:T(128)} %constant.123.clone.1), dimensions={3}, to_apply=%region_3.4 | reduce | flops 783360 | bytes 3158020 | tf_op jit(solution)/shard_map/reduce_max | solution.py:200
  60.6 0.2 reduce_max.29
  60.8 2.9 %fusion.8 = f32[4,12,64]{2,1,0:T(8,128)S(1)} fusion(f32[4,12,64,256]{3,2,1,0:T(8,128)} %multiply_select_fusion, f32[4,12,64]{2,1,0:T(8,128)S(1)} %copy_maximum_fusion), kind=kLoop, calls=%fused_computation.14 | loop fusion | flops 1569792 | bytes 3170304 | tf_op jit(solution)/shard_map/reduce_sum | solution.py:203
  63.8 0.4 fusion.25
  64.2 1.2 %fusion.22 = f32[4,64,12,64]{1,3,2,0:T(8,128)S(1)} fusion(bf16[4,256,12,64]{1,3,2,0:T(8,128)(2,1)S(1)} %bitcast.49, f32[4,12,64,256]{3,2,1,0:T(8,128)S(1)} %copy-done.1, f32[4,12,64]{2,1,0:T(8,128)S(1)} %copy_maximum_fusion), kind=kOutput, calls=%fused_computation.31 | convolution fusion | flops 102236160 | bytes 5517312 | tf_op jit(solution)/shard_map/rhqk,rkhd->rqhd/dot_general | solution.py:204
  65.4 3.4 %collective-permute-start.12 = (bf16[32,768]{1,0:T(8,128)(2,1)S(1)}, bf16[32,768]{1,0:T(8,128)(2,1)S(1)}, u32[]{:S(2)}, u32[]{:S(2)}) collective-permute-start(bf16[32,768]{1,0:T(8,128)(2,1)S(1)} %fusion.51), channel_id=1, source_target_pairs={{0,16},{4,20},{8,24},{12,28},{16,0},{20,4},{24,8},{28,12},{1,17},{... | collective-permute-start | bytes 147464 | tf_op jit(solution)/shard_map/ppermute | solution.py:59
  68.9 2.8 %collective-permute-start.14 = (f32[32,12]{0,1:T(8,128)S(1)}, f32[32,12]{0,1:T(8,128)S(1)}, u32[]{:S(2)}, u32[]{:S(2)}) collective-permute-start(f32[32,12]{0,1:T(8,128)S(1)} %get-tuple-element.50), channel_id=1, source_target_pairs={{0,16},{4,20},{8,24},{12,28},{16,0},{20,4},{24,8},{28,12},{1,17},{... | collective-permute-start | bytes 4616 | tf_op jit(solution)/shard_map/ppermute | solution.py:59
  71.8 1.6 %collective-permute-done.13 = f32[32,12]{0,1:T(8,128)S(1)} collective-permute-done((f32[32,12]{0,1:T(8,128)S(1)}, f32[32,12]{0,1:T(8,128)S(1)}, u32[]{:S(2)}, u32[]{:S(2)}) %collective-permute-start.13) | collective-permute-done | bytes 1568 | tf_op jit(solution)/shard_map/ppermute | solution.py:59
  73.5 0.3 fusion.57
  73.8 0.3 fusion.54
  74.1 0.5 collective-permute-start.16
  74.7 0.4 fusion.20
  75.1 0.6 copy.53
  75.7 1.2 %convert_element_type.109 = bf16[256,768]{0,1:T(8,128)(2,1)} reshape(bf16[4,64,12,64]{1,0,3,2:T(4,128)(2,1)S(1)} %copy.53) | data formatting | bytes 786432 | tf_op jit(solution)/shard_map/convert_element_type | solution.py:215
  77.0 0.3 fusion.56
  77.3 0.4 fusion.31
  77.7 0.4 fusion.32
  78.1 0.2 copy.54
  78.3 1.8 %fusion.119 = (f32[320]{0:T(512)S(1)}, f32[320,768]{1,0:T(8,128)S(1)}) fusion(bf16[768,768]{1,0:T(8,128)(2,1)S(1)} %copy-done, bf16[64,768]{0,1:T(8,128)(2,1)S(1)} %copy.54, bf16[256,768]{0,1:T(8,128)(2,1)} %convert_element_type.109, bf16[64,768]{1,0:T(8,128)(2,1)S(1)} %copy-done.6, bf16[256,768]{1,0:T(8,128)(2,1)} %bitcast.62), kind=kOutput, calls=%fused_computation.171 | convolution fusion | flops 379944640 | bytes 3147008 | tf_op jit(solution)/shard_map/dot_general | solution.py:24
  80.1 0.3 multiply_reduce_fusion.1
  80.4 7.4 %fusion.120 = (f32[320]{0:T(512)S(1)}, f32[320,768]{1,0:T(8,128)S(1)}) fusion(bf16[3072,768]{1,0:T(8,128)(2,1)} %param.18, bf16[768,3072]{1,0:T(8,128)(2,1)} %param.17, f32[320,768]{1,0:T(8,128)S(1)} %get-tuple-element.90, f32[768]{0:T(1024)S(1)} %copy-done.16, f32[320]{0:T(512)S(1)} %add_rsqrt_fusion.1, f32[320]{0:T(512)S(1)} %broadcast_multiply_fusion.1), kind=kOutput, calls=%fused_computation.172 | convolution fusion | flops 3031449344 | bytes 11410176 | tf_op jit(solution)/shard_map/dot_general | solution.py:29
  87.8 0.3 multiply_reduce_fusion
  88.1 0.2 multiply_convert_fusion
  88.3 0.8 slice.82
  89.1 0.6 slice.83
  (74 shorter events, 0.7 us)
Async XLA Ops:
  0.6 77.6 %copy-start = (bf16[768,768]{1,0:T(8,128)(2,1)S(1)}, bf16[768,768]{1,0:T(8,128)(2,1)}, u32[]{:S(2)}) copy-start(bf16[768,768]{1,0:T(8,128)(2,1)} %param.15) | copy-start | bytes 3538948
  0.6 37.2 %collective-permute-start.6 = (bf16[4,64,768]{2,1,0:T(8,128)(2,1)}, bf16[4,64,768]{2,1,0:T(8,128)(2,1)}, u32[]{:S(2)}, u32[]{:S(2)}) collective-permute-start(bf16[4,64,768]{2,1,0:T(8,128)(2,1)} %param.10), channel_id=1, source_target_pairs={{0,1},{1,0},{2,3},{3,2},{4,5},{5,4},{6,7},{7,6},{8,9},{9,8},{10,11... | collective-permute-start | bytes 1179656 | tf_op jit(solution)/shard_map/ppermute | solution.py:135
  3.6 34.2 %collective-permute-start.7 = (bf16[4,64,768]{2,1,0:T(8,128)(2,1)}, bf16[4,64,768]{2,1,0:T(8,128)(2,1)}, u32[]{:S(2)}, u32[]{:S(2)}) collective-permute-start(bf16[4,64,768]{2,1,0:T(8,128)(2,1)} %param.10), channel_id=1, source_target_pairs={{0,2},{1,3},{2,0},{3,1},{4,6},{5,7},{6,4},{7,5},{8,10},{9,11},{10,... | collective-permute-start | bytes 1179656 | tf_op jit(solution)/shard_map/ppermute | solution.py:135
  5.2 32.7 %collective-permute-start.8 = (bf16[4,64,768]{2,1,0:T(8,128)(2,1)}, bf16[4,64,768]{2,1,0:T(8,128)(2,1)}, u32[]{:S(2)}, u32[]{:S(2)}) collective-permute-start(bf16[4,64,768]{2,1,0:T(8,128)(2,1)} %param.10), channel_id=1, source_target_pairs={{0,3},{1,2},{2,1},{3,0},{4,7},{5,6},{6,5},{7,4},{8,11},{9,10},{10,... | collective-permute-start | bytes 1179656 | tf_op jit(solution)/shard_map/ppermute | solution.py:135
  5.2 4.9 %collective-permute-start = (bf16[64,768]{1,0:T(8,128)(2,1)}, bf16[64,768]{1,0:T(8,128)(2,1)S(1)}, u32[]{:S(2)}, u32[]{:S(2)}) collective-permute-start(bf16[64,768]{1,0:T(8,128)(2,1)} %bitcast.59), channel_id=1, source_target_pairs={{0,4},{4,0},{8,12},{12,8},{16,20},{20,16},{24,28},{28,24},{1,5},{5... | collective-permute-start | bytes 294920 | tf_op jit(solution)/shard_map/ppermute | solution.py:59
  9.1 1.0 %copy-start.12 = (bf16[1,64,768]{2,1,0:T(8,128)(2,1)S(1)}, bf16[1,64,768]{2,1,0:T(8,128)(2,1)}, u32[]{:S(2)}) copy-start(bf16[1,64,768]{2,1,0:T(8,128)(2,1)} %param.11) | copy-start | bytes 294916
  9.1 3.1 %copy-start.15 = (s32[4,64]{1,0:T(4,128)S(1)}, s32[4,64]{1,0:T(4,128)}, u32[]{:S(2)}) copy-start(s32[4,64]{1,0:T(4,128)} %param.13) | copy-start | bytes 3076
  10.1 5.6 %collective-permute-start.1 = (bf16[64,768]{1,0:T(8,128)(2,1)S(1)}, bf16[64,768]{1,0:T(8,128)(2,1)S(1)}, u32[]{:S(2)}, u32[]{:S(2)}) collective-permute-start(bf16[64,768]{1,0:T(8,128)(2,1)S(1)} %broadcast_select_fusion), channel_id=1, source_target_pairs={{0,8},{4,12},{8,0},{12,4},{16,24},{20,28},{24,16},{28,20},{1,9},{5... | collective-permute-start | bytes 294920 | tf_op jit(solution)/shard_map/ppermute | solution.py:59
  15.7 7.8 %collective-permute-start.2 = (bf16[64,768]{1,0:T(8,128)(2,1)S(1)}, bf16[64,768]{1,0:T(8,128)(2,1)S(1)}, u32[]{:S(2)}, u32[]{:S(2)}) collective-permute-start(bf16[64,768]{1,0:T(8,128)(2,1)S(1)} %broadcast_select_fusion.1), channel_id=1, source_target_pairs={{0,16},{4,20},{8,24},{12,28},{16,0},{20,4},{24,8},{28,12},{1,17},{... | collective-permute-start | bytes 294920 | tf_op jit(solution)/shard_map/ppermute | solution.py:59
  23.5 0.6 copy-start.5
  27.6 3.7 %copy-start.8 = (f32[64,12]{0,1:T(8,128)}, f32[64,12]{0,1:T(8,128)S(1)}, u32[]{:S(2)}) copy-start(f32[64,12]{0,1:T(8,128)S(1)} %fusion.66) | copy-start | bytes 9220
  27.9 3.4 %copy-start.4 = (f32[64,768]{1,0:T(8,128)}, f32[64,768]{1,0:T(8,128)S(1)}, u32[]{:S(2)}) copy-start(f32[64,768]{1,0:T(8,128)S(1)} %fusion.30) | copy-start | bytes 589828
  29.2 5.9 %collective-permute-start.5 = (f32[32,12]{0,1:T(8,128)}, f32[32,12]{0,1:T(8,128)}, u32[]{:S(2)}, u32[]{:S(2)}) collective-permute-start(f32[32,12]{0,1:T(8,128)} %slice_select_fusion.1), channel_id=1, source_target_pairs={{0,4},{4,0},{8,12},{12,8},{16,20},{20,16},{24,28},{28,24},{1,5},{5... | collective-permute-start | bytes 4616 | tf_op jit(solution)/shard_map/ppermute | solution.py:59
  29.2 5.9 %collective-permute-start.4 = (f32[32,12]{0,1:T(8,128)}, f32[32,12]{0,1:T(8,128)}, u32[]{:S(2)}, u32[]{:S(2)}) collective-permute-start(f32[32,12]{0,1:T(8,128)} %slice_select_fusion.2), channel_id=1, source_target_pairs={{0,4},{4,0},{8,12},{12,8},{16,20},{20,16},{24,28},{28,24},{1,5},{5... | collective-permute-start | bytes 4616 | tf_op jit(solution)/shard_map/ppermute | solution.py:59
  35.1 1.5 %collective-permute-start.3 = (f32[32,768]{1,0:T(8,128)}, f32[32,768]{1,0:T(8,128)S(1)}, u32[]{:S(2)}, u32[]{:S(2)}) collective-permute-start(f32[32,768]{1,0:T(8,128)} %slice_select_fusion), channel_id=1, source_target_pairs={{0,4},{4,0},{8,12},{12,8},{16,20},{20,16},{24,28},{28,24},{1,5},{5... | collective-permute-start | bytes 294920 | tf_op jit(solution)/shard_map/ppermute | solution.py:59
  37.8 10.5 %copy-start.10 = (bf16[32,768]{1,0:T(8,128)(2,1)}, bf16[32,768]{1,0:T(8,128)(2,1)S(1)}, u32[]{:S(2)}) copy-start(bf16[32,768]{1,0:T(8,128)(2,1)S(1)} %add_convert_fusion) | copy-start | bytes 147460
  42.9 1.0 %copy-start.3 = (bf16[4,64,768]{2,1,0:T(8,128)(2,1)S(1)}, bf16[4,64,768]{2,1,0:T(8,128)(2,1)}, u32[]{:S(2)}) copy-start(bf16[4,64,768]{2,1,0:T(8,128)(2,1)} %get-tuple-element.81) | copy-start | bytes 1179652
  45.7 5.3 %copy-start.7 = (pred[4,64,256]{2,1,0:T(8,128)(4,1)S(1)}, pred[4,64,256]{2,1,0:T(8,128)(4,1)}, u32[]{:S(2)}) copy-start(pred[4,64,256]{2,1,0:T(8,128)(4,1)} %fusion.45) | copy-start | bytes 196612
  48.4 9.3 %collective-permute-start.9 = (bf16[32,768]{1,0:T(8,128)(2,1)S(1)}, bf16[32,768]{1,0:T(8,128)(2,1)S(1)}, u32[]{:S(2)}, u32[]{:S(2)}) collective-permute-start(bf16[32,768]{1,0:T(8,128)(2,1)S(1)} %add_convert_fusion), channel_id=1, source_target_pairs={{0,8},{4,12},{8,0},{12,4},{16,24},{20,28},{24,16},{28,20},{1,9},{5... | collective-permute-start | bytes 147464 | tf_op jit(solution)/shard_map/ppermute | solution.py:59
  49.0 8.6 %collective-permute-start.10 = (f32[32,12]{0,1:T(8,128)S(1)}, f32[32,12]{0,1:T(8,128)S(1)}, u32[]{:S(2)}, u32[]{:S(2)}) collective-permute-start(f32[32,12]{0,1:T(8,128)S(1)} %get-tuple-element.37), channel_id=1, source_target_pairs={{0,8},{4,12},{8,0},{12,4},{16,24},{20,28},{24,16},{28,20},{1,9},{5... | collective-permute-start | bytes 4616 | tf_op jit(solution)/shard_map/ppermute | solution.py:59
  50.4 7.2 %collective-permute-start.11 = (f32[32,12]{0,1:T(8,128)S(1)}, f32[32,12]{0,1:T(8,128)S(1)}, u32[]{:S(2)}, u32[]{:S(2)}) collective-permute-start(f32[32,12]{0,1:T(8,128)S(1)} %get-tuple-element.38), channel_id=1, source_target_pairs={{0,8},{4,12},{8,0},{12,4},{16,24},{20,28},{24,16},{28,20},{1,9},{5... | collective-permute-start | bytes 4616 | tf_op jit(solution)/shard_map/ppermute | solution.py:59
  55.0 2.9 %copy-start.11 = (bf16[32,768]{1,0:T(8,128)(2,1)S(1)}, bf16[32,768]{1,0:T(8,128)(2,1)}, u32[]{:S(2)}) copy-start(bf16[32,768]{1,0:T(8,128)(2,1)} %copy-done.10) | copy-start | bytes 147460
  60.8 3.4 %copy-start.1 = (f32[4,12,64,256]{3,2,1,0:T(8,128)S(1)}, f32[4,12,64,256]{3,2,1,0:T(8,128)}, u32[]{:S(2)}) copy-start(f32[4,12,64,256]{3,2,1,0:T(8,128)} %multiply_select_fusion) | copy-start | bytes 9437188
  60.8 3.4 %copy-start.2 = (bf16[4,256,768]{1,2,0:T(8,128)(2,1)S(1)}, bf16[4,256,768]{1,2,0:T(8,128)(2,1)}, u32[]{:S(2)}) copy-start(bf16[4,256,768]{1,2,0:T(8,128)(2,1)} %copy.47) | copy-start | bytes 4718596
  64.2 10.5 %copy-start.9 = (bf16[64,768]{0,1:T(8,128)(2,1)S(1)}, bf16[64,768]{0,1:T(8,128)(2,1)}, u32[]{:S(2)}) copy-start(bf16[64,768]{0,1:T(8,128)(2,1)} %copy.59) | copy-start | bytes 294916
  65.4 8.1 %collective-permute-start.12 = (bf16[32,768]{1,0:T(8,128)(2,1)S(1)}, bf16[32,768]{1,0:T(8,128)(2,1)S(1)}, u32[]{:S(2)}, u32[]{:S(2)}) collective-permute-start(bf16[32,768]{1,0:T(8,128)(2,1)S(1)} %fusion.51), channel_id=1, source_target_pairs={{0,16},{4,20},{8,24},{12,28},{16,0},{20,4},{24,8},{28,12},{1,17},{... | collective-permute-start | bytes 147464 | tf_op jit(solution)/shard_map/ppermute | solution.py:59
  68.9 4.5 %collective-permute-start.13 = (f32[32,12]{0,1:T(8,128)S(1)}, f32[32,12]{0,1:T(8,128)S(1)}, u32[]{:S(2)}, u32[]{:S(2)}) collective-permute-start(f32[32,12]{0,1:T(8,128)S(1)} %get-tuple-element.49), channel_id=1, source_target_pairs={{0,16},{4,20},{8,24},{12,28},{16,0},{20,4},{24,8},{28,12},{1,17},{... | collective-permute-start | bytes 4616 | tf_op jit(solution)/shard_map/ppermute | solution.py:59
  68.9 4.6 %collective-permute-start.14 = (f32[32,12]{0,1:T(8,128)S(1)}, f32[32,12]{0,1:T(8,128)S(1)}, u32[]{:S(2)}, u32[]{:S(2)}) collective-permute-start(f32[32,12]{0,1:T(8,128)S(1)} %get-tuple-element.50), channel_id=1, source_target_pairs={{0,16},{4,20},{8,24},{12,28},{16,0},{20,4},{24,8},{28,12},{1,17},{... | collective-permute-start | bytes 4616 | tf_op jit(solution)/shard_map/ppermute | solution.py:59
  74.1 2.9 %collective-permute-start.15 = (f32[32,768]{1,0:T(8,128)S(1)}, f32[32,768]{1,0:T(8,128)S(1)}, u32[]{:S(2)}, u32[]{:S(2)}) collective-permute-start(f32[32,768]{1,0:T(8,128)S(1)} %fusion.54), channel_id=1, source_target_pairs={{0,4},{4,0},{8,12},{12,8},{16,20},{20,16},{24,28},{28,24},{1,5},{5... | collective-permute-start | bytes 294920 | tf_op jit(solution)/shard_map/ppermute | solution.py:59
  74.1 2.8 %collective-permute-start.16 = (f32[32,12]{0,1:T(8,128)S(1)}, f32[32,12]{0,1:T(8,128)S(1)}, u32[]{:S(2)}, u32[]{:S(2)}) collective-permute-start(f32[32,12]{0,1:T(8,128)S(1)} %get-tuple-element.61), channel_id=1, source_target_pairs={{0,4},{4,0},{8,12},{12,8},{16,20},{20,16},{24,28},{28,24},{1,5},{5... | collective-permute-start | bytes 4616 | tf_op jit(solution)/shard_map/ppermute | solution.py:59
  74.6 2.3 %collective-permute-start.17 = (f32[32,12]{0,1:T(8,128)S(1)}, f32[32,12]{0,1:T(8,128)S(1)}, u32[]{:S(2)}, u32[]{:S(2)}) collective-permute-start(f32[32,12]{0,1:T(8,128)S(1)} %get-tuple-element.62), channel_id=1, source_target_pairs={{0,4},{4,0},{8,12},{12,8},{16,20},{20,16},{24,28},{28,24},{1,5},{5... | collective-permute-start | bytes 4616 | tf_op jit(solution)/shard_map/ppermute | solution.py:59
  75.1 1.9 %copy-start.13 = (f32[64,12]{0,1:T(8,128)S(1)}, f32[64,12]{0,1:T(8,128)}, u32[]{:S(2)}) copy-start(f32[64,12]{0,1:T(8,128)} %convolution_multiply_fusion.3) | copy-start | bytes 9220
  75.1 3.2 %copy-start.6 = (bf16[64,768]{1,0:T(8,128)(2,1)S(1)}, bf16[64,768]{1,0:T(8,128)(2,1)}, u32[]{:S(2)}) copy-start(bf16[64,768]{1,0:T(8,128)(2,1)} %copy-done.5) | copy-start | bytes 294916
  78.2 2.1 %copy-start.16 = (f32[768]{0:T(1024)S(1)}, f32[768]{0:T(1024)}, u32[]{:S(2)}) copy-start(f32[768]{0:T(1024)} %param.16) | copy-start | bytes 9220
  80.3 7.7 %copy-start.14 = (f32[768]{0:T(1024)S(1)}, f32[768]{0:T(1024)}, u32[]{:S(2)}) copy-start(f32[768]{0:T(1024)} %param.19) | copy-start | bytes 9220

commit v8 on v6

--- a/solution.py
+++ b/solution.py
@@ -70,19 +70,19 @@
 
 
 def merge(lo, hi):
-    top = jnp.maximum(lo[2], hi[2])
-    fade_lo = jnp.exp(lo[2] - top)
-    fade_hi = jnp.exp(hi[2] - top)
-    total = lo[1] * fade_lo + hi[1] * fade_hi
+    top = jnp.maximum(lo[1][:, HEADS:], hi[1][:, HEADS:])
+    fade_lo = jnp.exp(lo[1][:, HEADS:] - top)
+    fade_hi = jnp.exp(hi[1][:, HEADS:] - top)
+    total = lo[1][:, :HEADS] * fade_lo + hi[1][:, :HEADS] * fade_hi
     mixed = lo[0] * head_spread(fade_lo) + hi[0] * head_spread(fade_hi)
-    return mixed, total, top
+    return mixed, jnp.concatenate([total, top], axis=-1)
 
 
 def pick(flag, a, b):
     return tuple(jnp.where(flag, x, y) for x, y in zip(a, b))
 
 
-def all_merge(value, axis, count):
+def half_merge(value, axis, count):
     here = lax.axis_index(axis)
     half = value[0].shape[0] // 2
     first = (here & 1) == 0
@@ -98,17 +98,18 @@
         got = (
             partner(mixed, axis, step, count).astype(jnp.float32),
             partner(value[1], axis, step, count),
-            partner(value[2], axis, step, count),
         )
-        mine = (mixed.astype(jnp.float32), value[1], value[2])
+        mine = (mixed.astype(jnp.float32), value[1])
         low_side = (here & step) == 0
         value = merge(pick(low_side, mine, got), pick(low_side, got, mine))
         step *= 2
-    got = tuple(partner(v, axis, 1, count) for v in value)
-    return tuple(
-        jnp.where(first, jnp.concatenate([v, g]), jnp.concatenate([g, v]))
-        for v, g in zip(value, got)
-    )
+    return value
+
+
+def join_halves(value, axis, count):
+    first = (lax.axis_index(axis) & 1) == 0
+    got = partner(value, axis, 1, count)
+    return jnp.where(first, jnp.concatenate([value, got]), jnp.concatenate([got, value]))
 
 
 def fan_out(value, axis, count):
@@ -154,15 +155,22 @@
     col_weights = head_spread(col_exp.astype(jnp.bfloat16).astype(jnp.float32))
     part_mixed = (col_weights * own_vals.astype(jnp.float32)).sum(0)
     part_total = col_exp.sum(0)
-    merged = all_merge((part_mixed, part_total, part_top), "band", n_band)
-    col_top = jnp.maximum(merged[2], self_scores)
-    fade = jnp.exp(merged[2] - col_top)
-    self_exp = jnp.exp(self_scores - col_top)
-    col_total = merged[1] * fade + self_exp
+    merged = half_merge(
+        (part_mixed, jnp.concatenate([part_total, part_top], axis=-1)), "band", n_band
+    )
+    half = cols_dev // 2
+    first = (own_band & 1) == 0
+    half_self = jnp.where(first, self_scores[:half], self_scores[half:])
+    half_vals = jnp.where(first, sum_vals[:half], sum_vals[half:]).astype(jnp.float32)
+    col_top = jnp.maximum(merged[1][:, HEADS:], half_self)
+    fade = jnp.exp(merged[1][:, HEADS:] - col_top)
+    self_exp = jnp.exp(half_self - col_top)
+    col_total = merged[1][:, :HEADS] * fade + self_exp
     col_mixed = merged[0] * head_spread(fade) + head_spread(
         self_exp.astype(jnp.bfloat16).astype(jnp.float32)
-    ) * sum_vals.astype(jnp.float32)
+    ) * half_vals
     summary_att = (col_mixed / head_spread(col_total)).astype(jnp.bfloat16)
+    summary_att = join_halves(summary_att, "band", n_band)
 
     sources = [own_group] + [s for s, _ in row_parts]
     other_cells = jnp.concatenate([got for _, got in row_parts], axis=1)

time: 89.6 us -> 85.3 us (0.952)
  waiting for transfers between devices: 18.1 us -> 14.4 us
    ppermute x15 -> x10, waiting for transfers between devices: 18.1 us -> 14.4 us  [partner(): return lax.ppermute(value, axis, [(i, i ^ step) for i in range(count)])]
    ppermute x15 -> x10, starting transfers between devices: 12.3 us -> 11.9 us  [partner(): return lax.ppermute(value, axis, [(i, i ^ step) for i in range(count)])]
  transfers between devices with their start and end apart: 18 -> 13, of which waited for: 8 -> 5; matrix products, arithmetic and copies ran while one was open for 44% -> 44% of each run, Pallas kernels for 0% -> 0%
where the time goes in v8:
time: 85.3 us; the launch traced here: 84.7 us
  matrix products  28 us (33%)
  starting transfers between devices  16.6 us (19%)
  local copies, waits for them, and re-layouts  14.7 us (17%)
  waiting for transfers between devices  14.4 us (17%)
  other arithmetic  9.19 us (11%)
  between operations  1.85 us (2%)
    ppermute x10, waiting for transfers between devices, partner(): return lax.ppermute(value, axis, [(i, i ^ step) for i in range(count)])  14.4 us
    ppermute x10, starting transfers between devices, partner(): return lax.ppermute(value, axis, [(i, i ^ step) for i in range(count)])  11.9 us
    dot_general x3, matrix products, project(): jnp.dot(values, weight, preferred_element_type=jnp.float32)  7.99 us
    dot_general x1, matrix products, finish(): outer_out = jnp.dot(inner_act, w_down, preferred_element_type=jnp.float32)  7.43 us
    ppermute x3, starting transfers between devices, fan_out(): got.append((source, lax.ppermute(value, axis, pairs)))  4.6 us
    dot_general x10, matrix products, head_spread(): jnp.dot(flat, head_matrix(), precision=lax.Precision.HIGHEST, preferred_e...  4.29 us
    concatenate x1, local copies, waits for them, and re-layouts, local(): row_vals = jnp.concatenate([own_vals, other_kv[:, :, model_width:]], axis=1)  2.58 us
    concatenate x1, local copies, waits for them, and re-layouts, local(): row_keys = jnp.concatenate([own_keys, other_kv[:, :, :model_width]], axis=1)  2.58 us
  transfers between devices with their start and end apart: 13, of which 5 were waited for; matrix products, arithmetic and copies ran while one was open for 44% of the time, Pallas kernels for 0%

profile of v8, /device:TPU:0, one launch (start us, length us, event | category | flops | bytes accessed | tf_op | source)
XLA Modules:
  0.0 84.7 jit_solution(8532198635074983111)
XLA Ops:
  0.6 4.0 %collective-permute-start.5 = (bf16[4,64,768]{2,1,0:T(8,128)(2,1)}, bf16[4,64,768]{2,1,0:T(8,128)(2,1)}, u32[]{:S(2)}, u32[]{:S(2)}) collective-permute-start(bf16[4,64,768]{2,1,0:T(8,128)(2,1)} %param.10), channel_id=1, source_target_pairs={{0,3},{1,2},{2,1},{3,0},{4,7},{5,6},{6,5},{7,4},{8,11},{9,10},{10,... | collective-permute-start | bytes 1179656 | tf_op jit(solution)/shard_map/ppermute | solution.py:125
  4.6 0.5 collective-permute-start.4
  5.1 0.1 collective-permute-start.3
  5.9 3.2 %convolution_convert_fusion = bf16[256,2304]{1,0:T(8,128)(2,1)S(1)} fusion(bf16[256,768]{1,0:T(8,128)(2,1)} %bitcast.68, bf16[768,2304]{1,0:T(8,128)(2,1)} %param.14), kind=kOutput, calls=%fused_computation.9 | convolution fusion | flops 906559488 | bytes 5111808 | tf_op jit(solution)/shard_map/dot_general | solution.py:34
  9.2 1.0 %fusion.118 = (bf16[4,64,768]{2,1,0:T(8,128)(2,1)}, bf16[4,64,768]{2,1,0:T(8,128)(2,1)}, bf16[4,64,768]{2,1,0:T(8,128)(2,1)}) fusion(bf16[4,64,2304]{2,1,0:T(8,128)(2,1)S(1)} %bitcast.59), kind=kLoop, calls=%fused_computation.180 | loop fusion | bytes 2359296 | tf_op jit(solution)/shard_map/slice | solution.py:141
  10.3 0.7 broadcast_select_fusion
  11.0 2.0 %collective-permute-start.1 = (bf16[64,768]{1,0:T(8,128)(2,1)}, bf16[64,768]{1,0:T(8,128)(2,1)}, u32[]{:S(2)}, u32[]{:S(2)}) collective-permute-start(bf16[64,768]{1,0:T(8,128)(2,1)} %broadcast_select_fusion), channel_id=1, source_target_pairs={{0,8},{4,12},{8,0},{12,4},{16,24},{20,28},{24,16},{28,20},{1,9},{5... | collective-permute-start | bytes 294920 | tf_op jit(solution)/shard_map/ppermute | solution.py:59
  12.9 0.1 fusion.47
  13.1 1.7 %reshape.106 = bf16[4,64,12,64]{3,2,1,0:T(8,128)(2,1)S(1)} reshape(bf16[4,64,768]{2,1,0:T(8,128)(2,1)} %get-tuple-element.12) | data formatting | bytes 786432 | tf_op jit(solution)/shard_map/reshape | solution.py:183
  14.8 1.9 %collective-permute-done.1 = bf16[64,768]{1,0:T(8,128)(2,1)} collective-permute-done((bf16[64,768]{1,0:T(8,128)(2,1)}, bf16[64,768]{1,0:T(8,128)(2,1)}, u32[]{:S(2)}, u32[]{:S(2)}) %collective-permute-start.1) | collective-permute-done | bytes 98336 | tf_op jit(solution)/shard_map/ppermute | solution.py:59
  16.7 0.9 %broadcast_select_fusion.1 = bf16[64,768]{1,0:T(8,128)(2,1)S(1)} fusion(bf16[64,768]{1,0:T(8,128)(2,1)} %broadcast_select_fusion, bf16[64,768]{1,0:T(8,128)(2,1)} %collective-permute-done.1, pred[]{:T(512)S(6)} %eq.91), kind=kLoop, calls=%fused_computation.85 | loop fusion | flops 49152 | bytes 294913 | tf_op jit(solution)/shard_map/jit(_where)/select_n | solution.py:67
  17.6 2.8 %collective-permute-start.2 = (bf16[64,768]{1,0:T(8,128)(2,1)S(1)}, bf16[64,768]{1,0:T(8,128)(2,1)S(1)}, u32[]{:S(2)}, u32[]{:S(2)}) collective-permute-start(bf16[64,768]{1,0:T(8,128)(2,1)S(1)} %broadcast_select_fusion.1), channel_id=1, source_target_pairs={{0,16},{4,20},{8,24},{12,28},{16,0},{20,4},{24,8},{28,12},{1,17},{... | collective-permute-start | bytes 294920 | tf_op jit(solution)/shard_map/ppermute | solution.py:59
  20.5 4.8 %collective-permute-done.2 = bf16[64,768]{1,0:T(8,128)(2,1)S(1)} collective-permute-done((bf16[64,768]{1,0:T(8,128)(2,1)S(1)}, bf16[64,768]{1,0:T(8,128)(2,1)S(1)}, u32[]{:S(2)}, u32[]{:S(2)}) %collective-permute-start.2) | collective-permute-done | bytes 98336 | tf_op jit(solution)/shard_map/ppermute | solution.py:59
  25.3 2.8 %convolution_convert_fusion.1 = bf16[64,2304]{1,0:T(8,128)(2,1)S(1)} fusion(bf16[64,768]{1,0:T(8,128)(2,1)S(1)} %broadcast_select_fusion.2, bf16[768,2304]{1,0:T(8,128)(2,1)} %param.14), kind=kOutput, calls=%fused_computation.10 | convolution fusion | flops 226639872 | bytes 3932160 | tf_op jit(solution)/shard_map/dot_general | solution.py:34
  28.1 0.8 fusion.119
  28.9 0.2 convolution_multiply_fusion.3
  29.1 0.6 fusion.120
  29.8 0.3 fusion.32
  30.3 0.5 copy-done.6
  30.8 0.7 slice_select_fusion
  31.4 1.1 %reshape.108 = bf16[64,12,64]{2,1,0:T(8,128)(2,1)S(1)} reshape(bf16[64,768]{1,0:T(8,128)(2,1)} %get-tuple-element.17) | data formatting | bytes 196608 | tf_op jit(solution)/shard_map/reshape | solution.py:186
  32.6 2.0 %bitcast_reduce_fusion = (f32[4,12,64]{2,0,1:T(4,128)S(1)}, f32[12,64,4,64]{3,1,2,0:T(8,128)}) fusion(bf16[4,64,12,64]{3,2,1,0:T(8,128)(2,1)S(1)} %reshape.106, bf16[64,12,64,1]{2,1,0,3:T(8,128)(2,1)S(1)} %bitcast.64), kind=kOutput, calls=%fused_computation.30 | convolution fusion | flops 25555968 | bytes 1290240 | tf_op jit(solution)/shard_map/rqhd,khd->rhqk/dot_general | solution.py:200
  34.6 1.1 %copy.58 = bf16[64,768]{0,1:T(8,128)(2,1)S(1)} copy(bf16[64,768]{1,0:T(8,128)(2,1)} %get-tuple-element.15) | data formatting | bytes 196608 | tf_op jit(solution)/shard_map/reshape | solution.py:187
  35.8 0.8 collective-permute-start.9
  36.6 0.3 fusion.67
  36.8 2.7 %collective-permute-done.9 = f32[32,24]{0,1:T(8,128)S(1)} collective-permute-done((f32[32,24]{0,1:T(8,128)S(1)}, f32[32,24]{0,1:T(8,128)S(1)}, u32[]{:S(2)}, u32[]{:S(2)}) %collective-permute-start.9) | collective-permute-done | bytes 3104 | tf_op jit(solution)/shard_map/ppermute | solution.py:59
  39.6 2.1 %collective-permute-start.11 = (f32[32,24]{0,1:T(8,128)S(1)}, f32[32,24]{0,1:T(8,128)S(1)}, u32[]{:S(2)}, u32[]{:S(2)}) collective-permute-start(f32[32,24]{0,1:T(8,128)S(1)} %pad_maximum_fusion.5), channel_id=1, source_target_pairs={{0,16},{4,20},{8,24},{12,28},{16,0},{20,4},{24,8},{28,12},{1,17},{... | collective-permute-start | bytes 9224 | tf_op jit(solution)/shard_map/ppermute | solution.py:59
  41.7 0.3 fusion.64
  42.0 2.3 %collective-permute-done.11 = f32[32,24]{0,1:T(8,128)S(1)} collective-permute-done((f32[32,24]{0,1:T(8,128)S(1)}, f32[32,24]{0,1:T(8,128)S(1)}, u32[]{:S(2)}, u32[]{:S(2)}) %collective-permute-start.11) | collective-permute-done | bytes 3104 | tf_op jit(solution)/shard_map/ppermute | solution.py:59
  44.3 0.2 fusion.63
  44.6 0.3 fusion.62
  44.8 0.3 fusion.61
  45.1 0.2 fusion.60
  45.3 1.2 %add_convert_fusion = bf16[32,768]{1,0:T(8,128)(2,1)S(1)} fusion(f32[32,768]{1,0:T(8,128)} %collective-permute-done.6, f32[32,768]{1,0:T(8,128)S(1)} %fusion.67, f32[64,768]{1,0:T(8,128)S(1)} %copy-done.7, pred[]{:T(512)S(6)} %eq.187, s32[768]{0:T(1024)S(1)} %add_select_fusion, f32[32,12]{0,1:T(8,128)S(1)} %get-tuple-element.5, ...), kind=kOutput, calls=%fused_computation.83 | convolution fusion | flops 3720576 | bytes 462849 | tf_op jit(solution)/shard_map/dot_general | solution.py:53
  46.5 1.2 %collective-permute-start.8 = (bf16[32,768]{1,0:T(8,128)(2,1)S(1)}, bf16[32,768]{1,0:T(8,128)(2,1)S(1)}, u32[]{:S(2)}, u32[]{:S(2)}) collective-permute-start(bf16[32,768]{1,0:T(8,128)(2,1)S(1)} %add_convert_fusion), channel_id=1, source_target_pairs={{0,8},{4,12},{8,0},{12,4},{16,24},{20,28},{24,16},{28,20},{1,9},{5... | collective-permute-start | bytes 147464 | tf_op jit(solution)/shard_map/ppermute | solution.py:59
  47.7 1.3 %pad_maximum_fusion.2 = bf16[4,192,768]{2,1,0:T(8,128)(2,1)S(1)} fusion(bf16[4,64,768]{2,1,0:T(8,128)(2,1)} %collective-permute-done.5, bf16[4,64,768]{2,1,0:T(8,128)(2,1)} %collective-permute-done.4, bf16[4,64,768]{2,1,0:T(8,128)(2,1)} %collective-permute-done.3), kind=kLoop, calls=%fused_computation.42 | loop fusion | flops 3538944 | bytes 2359296 | tf_op jit(solution)/shard_map/concatenate | solution.py:176
  49.0 2.0 %convolution_convert_fusion.2 = bf16[768,1536]{1,0:T(8,128)(2,1)S(1)} fusion(bf16[768,768]{1,0:T(8,128)(2,1)S(1)} %bitcast.63, bf16[768,2304]{1,0:T(8,128)(2,1)S(1)} %copy-done.3), kind=kOutput, calls=%fused_computation.11 | convolution fusion | flops 1813118976 | bytes 5898240 | tf_op jit(solution)/shard_map/dot_general | solution.py:34
  51.0 0.2 fusion.117
  51.2 0.8 copy-done.4
  52.0 0.1 copy-done.5
  52.1 1.9 %pad_maximum_fusion = (bf16[4,256,768]{2,1,0:T(8,128)(2,1)}, bf16[4,256,768]{2,1,0:T(8,128)(2,1)}) fusion(bf16[4,192,768]{2,1,0:T(8,128)(2,1)S(1)} %get-tuple-element.9, bf16[4,64,768]{2,1,0:T(8,128)(2,1)S(1)} %copy-done.5, bf16[4,192,768]{2,1,0:T(8,128)(2,1)S(1)} %get-tuple-element.8, bf16[4,64,768]{2,1,0:T(8,128)(2,1)S(1)} %copy-done.4), kind=kLoop, calls=%fused_computation.24 | loop fusion | flops 6291456 | bytes 6291456 | tf_op jit(solution)/shard_map/concatenate | solution.py:181
  54.0 2.6 %copy.42 = bf16[4,256,768]{1,2,0:T(8,128)(2,1)} copy(bf16[4,256,768]{2,1,0:T(8,128)(2,1)} %get-tuple-element.32) | data formatting | bytes 3145728 | tf_op jit(solution)/shard_map/concatenate | solution.py:181
  56.6 2.6 %copy.43 = bf16[4,256,768]{1,2,0:T(8,128)(2,1)} copy(bf16[4,256,768]{2,1,0:T(8,128)(2,1)} %get-tuple-element.33) | data formatting | bytes 3145728 | tf_op jit(solution)/shard_map/concatenate | solution.py:180
  59.2 2.1 %fusion.8 = (f32[4,12,64]{2,1,0:T(8,128)S(1)}, f32[4,12,64,256]{3,2,1,0:T(8,128)S(1)}) fusion(pred[4,64,256]{2,1,0:T(8,128)(4,1)S(1)} %fusion.47, bf16[4,256,12,64]{1,3,2,0:T(8,128)(2,1)} %bitcast.58, bf16[4,64,12,64]{3,2,1,0:T(8,128)(2,1)S(1)} %reshape.106), kind=kOutput, calls=%fused_computation.14 | convolution fusion | flops 103019520 | bytes 5189632 | tf_op jit(solution)/shard_map/rqhd,rkhd->rhqk/dot_general | solution.py:196
  61.4 1.2 %fusion.9 = f32[4,12,64]{2,1,0:T(8,128)S(1)} fusion(f32[4,12,64,256]{3,2,1,0:T(8,128)S(1)} %get-tuple-element.25, f32[4,12,64]{2,1,0:T(8,128)S(1)} %copy_maximum_fusion, pred[4,64,256]{2,1,0:T(8,128)(4,1)S(1)} %fusion.47), kind=kLoop, calls=%fused_computation.15 | loop fusion | flops 3142656 | bytes 3235840 | tf_op jit(solution)/shard_map/reduce_sum | solution.py:205
  62.6 0.1 copy-done.2
  62.7 1.3 %fusion.18 = f32[4,12,64,64]{3,2,1,0:T(8,128)S(1)} fusion(bf16[4,256,12,64]{1,3,2,0:T(8,128)(2,1)S(1)} %bitcast.57, f32[4,12,64,256]{3,2,1,0:T(8,128)S(1)} %get-tuple-element.25, f32[4,12,64]{2,1,0:T(8,128)S(1)} %copy_maximum_fusion, pred[4,64,256]{2,1,0:T(8,128)(4,1)S(1)} %fusion.47), kind=kOutput, calls=%fused_computation.23 | convolution fusion | flops 103809024 | bytes 5582848 | tf_op jit(solution)/shard_map/rhqk,rkhd->rqhd/dot_general | solution.py:206
  64.0 0.1 copy-done.1
  64.2 0.4 fusion.27
  64.6 0.3 fusion.53
  64.9 3.0 %collective-permute-start.10 = (bf16[32,768]{1,0:T(8,128)(2,1)S(1)}, bf16[32,768]{1,0:T(8,128)(2,1)S(1)}, u32[]{:S(2)}, u32[]{:S(2)}) collective-permute-start(bf16[32,768]{1,0:T(8,128)(2,1)S(1)} %fusion.53), channel_id=1, source_target_pairs={{0,16},{4,20},{8,24},{12,28},{16,0},{20,4},{24,8},{28,12},{1,17},{... | collective-permute-start | bytes 147464 | tf_op jit(solution)/shard_map/ppermute | solution.py:59
  67.8 2.6 %collective-permute-done.10 = bf16[32,768]{1,0:T(8,128)(2,1)S(1)} collective-permute-done((bf16[32,768]{1,0:T(8,128)(2,1)S(1)}, bf16[32,768]{1,0:T(8,128)(2,1)S(1)}, u32[]{:S(2)}, u32[]{:S(2)}) %collective-permute-start.10) | collective-permute-done | bytes 49184 | tf_op jit(solution)/shard_map/ppermute | solution.py:59
  70.4 1.1 %fusion.33 = bf16[32,768]{1,0:T(8,128)(2,1)S(1)} fusion(f32[32,768]{1,0:T(8,128)S(1)} %fusion.61, f32[32,768]{1,0:T(8,128)S(1)} %fusion.63, bf16[32,768]{1,0:T(8,128)(2,1)S(1)} %collective-permute-done.10, bf16[32,768]{1,0:T(8,128)(2,1)S(1)} %fusion.53, f32[32,768]{1,0:T(8,128)S(1)} %fusion.62, f32[32,768]{1,0:T(8,128)S(1)} %fusion.60, ...), kind=kOutput, calls=%fused_computation.44 | convolution fusion | flops 3896064 | bytes 692226 | tf_op jit(solution)/shard_map/dot_general | solution.py:53
  71.6 0.4 fusion.21
  72.0 0.6 copy.52
  72.6 0.5 convert_element_type.99
  73.1 0.2 copy.53
  73.3 1.7 %fusion.121 = (f32[320]{0:T(512)S(1)}, f32[320,768]{1,0:T(8,128)S(1)}) fusion(bf16[768,768]{1,0:T(8,128)(2,1)S(1)} %copy-done, bf16[64,768]{0,1:T(8,128)(2,1)S(1)} %copy.53, bf16[256,768]{0,1:T(8,128)(2,1)S(1)} %convert_element_type.99, bf16[64,768]{1,0:T(8,128)(2,1)S(1)} %copy-done.10, bf16[256,768]{1,0:T(8,128)(2,1)} %bitcast.69), kind=kOutput, calls=%fused_computation.183 | convolution fusion | flops 379944640 | bytes 3147008 | tf_op jit(solution)/shard_map/dot_general | solution.py:24
  75.0 0.3 multiply_reduce_fusion.1
  75.3 7.4 %fusion.122 = (f32[320]{0:T(512)S(1)}, f32[320,768]{1,0:T(8,128)S(1)}) fusion(bf16[3072,768]{1,0:T(8,128)(2,1)} %param.18, bf16[768,3072]{1,0:T(8,128)(2,1)} %param.17, f32[320,768]{1,0:T(8,128)S(1)} %get-tuple-element.29, f32[768]{0:T(1024)S(1)} %copy-done.14, f32[320]{0:T(512)S(1)} %add_rsqrt_fusion.1, f32[320]{0:T(512)S(1)} %broadcast_multiply_fusion.1), kind=kOutput, calls=%fused_computation.184 | convolution fusion | flops 3031449344 | bytes 11410176 | tf_op jit(solution)/shard_map/dot_general | solution.py:29
  82.8 0.3 multiply_reduce_fusion
  83.0 0.2 multiply_convert_fusion
  83.2 0.8 slice.160
  84.0 0.6 slice.161
  (65 shorter events, 0.8 us)
Async XLA Ops:
  0.6 72.7 %copy-start = (bf16[768,768]{1,0:T(8,128)(2,1)S(1)}, bf16[768,768]{1,0:T(8,128)(2,1)}, u32[]{:S(2)}) copy-start(bf16[768,768]{1,0:T(8,128)(2,1)} %param.15) | copy-start | bytes 3538948
  0.6 47.0 %collective-permute-start.5 = (bf16[4,64,768]{2,1,0:T(8,128)(2,1)}, bf16[4,64,768]{2,1,0:T(8,128)(2,1)}, u32[]{:S(2)}, u32[]{:S(2)}) collective-permute-start(bf16[4,64,768]{2,1,0:T(8,128)(2,1)} %param.10), channel_id=1, source_target_pairs={{0,3},{1,2},{2,1},{3,0},{4,7},{5,6},{6,5},{7,4},{8,11},{9,10},{10,... | collective-permute-start | bytes 1179656 | tf_op jit(solution)/shard_map/ppermute | solution.py:125
  4.6 43.1 %collective-permute-start.4 = (bf16[4,64,768]{2,1,0:T(8,128)(2,1)}, bf16[4,64,768]{2,1,0:T(8,128)(2,1)}, u32[]{:S(2)}, u32[]{:S(2)}) collective-permute-start(bf16[4,64,768]{2,1,0:T(8,128)(2,1)} %param.10), channel_id=1, source_target_pairs={{0,2},{1,3},{2,0},{3,1},{4,6},{5,7},{6,4},{7,5},{8,10},{9,11},{10,... | collective-permute-start | bytes 1179656 | tf_op jit(solution)/shard_map/ppermute | solution.py:125
  5.1 42.6 %collective-permute-start.3 = (bf16[4,64,768]{2,1,0:T(8,128)(2,1)}, bf16[4,64,768]{2,1,0:T(8,128)(2,1)}, u32[]{:S(2)}, u32[]{:S(2)}) collective-permute-start(bf16[4,64,768]{2,1,0:T(8,128)(2,1)} %param.10), channel_id=1, source_target_pairs={{0,1},{1,0},{2,3},{3,2},{4,5},{5,4},{6,7},{7,6},{8,9},{9,8},{10,11... | collective-permute-start | bytes 1179656 | tf_op jit(solution)/shard_map/ppermute | solution.py:125
  5.3 5.0 %collective-permute-start = (bf16[64,768]{1,0:T(8,128)(2,1)}, bf16[64,768]{1,0:T(8,128)(2,1)S(1)}, u32[]{:S(2)}, u32[]{:S(2)}) collective-permute-start(bf16[64,768]{1,0:T(8,128)(2,1)} %bitcast.67), channel_id=1, source_target_pairs={{0,4},{4,0},{8,12},{12,8},{16,20},{20,16},{24,28},{28,24},{1,5},{5... | collective-permute-start | bytes 294920 | tf_op jit(solution)/shard_map/ppermute | solution.py:59
  9.1 1.2 %copy-start.11 = (bf16[1,64,768]{2,1,0:T(8,128)(2,1)S(1)}, bf16[1,64,768]{2,1,0:T(8,128)(2,1)}, u32[]{:S(2)}) copy-start(bf16[1,64,768]{2,1,0:T(8,128)(2,1)} %param.11) | copy-start | bytes 294916
  9.2 3.8 %copy-start.13 = (s32[4,64]{1,0:T(4,128)S(1)}, s32[4,64]{1,0:T(4,128)}, u32[]{:S(2)}) copy-start(s32[4,64]{1,0:T(4,128)} %param.13) | copy-start | bytes 3076
  11.0 5.7 %collective-permute-start.1 = (bf16[64,768]{1,0:T(8,128)(2,1)}, bf16[64,768]{1,0:T(8,128)(2,1)}, u32[]{:S(2)}, u32[]{:S(2)}) collective-permute-start(bf16[64,768]{1,0:T(8,128)(2,1)} %broadcast_select_fusion), channel_id=1, source_target_pairs={{0,8},{4,12},{8,0},{12,4},{16,24},{20,28},{24,16},{28,20},{1,9},{5... | collective-permute-start | bytes 294920 | tf_op jit(solution)/shard_map/ppermute | solution.py:59
  17.6 7.6 %collective-permute-start.2 = (bf16[64,768]{1,0:T(8,128)(2,1)S(1)}, bf16[64,768]{1,0:T(8,128)(2,1)S(1)}, u32[]{:S(2)}, u32[]{:S(2)}) collective-permute-start(bf16[64,768]{1,0:T(8,128)(2,1)S(1)} %broadcast_select_fusion.1), channel_id=1, source_target_pairs={{0,16},{4,20},{8,24},{12,28},{16,0},{20,4},{24,8},{28,12},{1,17},{... | collective-permute-start | bytes 294920 | tf_op jit(solution)/shard_map/ppermute | solution.py:59
  25.3 3.8 %copy-start.9 = (bf16[64,768]{1,0:T(8,128)(2,1)}, bf16[64,768]{1,0:T(8,128)(2,1)S(1)}, u32[]{:S(2)}) copy-start(bf16[64,768]{1,0:T(8,128)(2,1)S(1)} %broadcast_select_fusion.2) | copy-start | bytes 294916
  28.1 3.4 %copy-start.8 = (bf16[64,2304]{1,0:T(8,128)(2,1)}, bf16[64,2304]{1,0:T(8,128)(2,1)S(1)}, u32[]{:S(2)}) copy-start(bf16[64,2304]{1,0:T(8,128)(2,1)S(1)} %convolution_convert_fusion.1) | copy-start | bytes 884740
  30.1 0.7 copy-start.6
  30.2 5.5 %collective-permute-start.7 = (f32[32,24]{0,1:T(8,128)S(1)}, f32[32,24]{0,1:T(8,128)S(1)}, u32[]{:S(2)}, u32[]{:S(2)}) collective-permute-start(f32[32,24]{0,1:T(8,128)S(1)} %fusion.97), channel_id=1, source_target_pairs={{0,4},{4,0},{8,12},{12,8},{16,20},{20,16},{24,28},{28,24},{1,5},{5... | collective-permute-start | bytes 9224 | tf_op jit(solution)/shard_map/ppermute | solution.py:59
  31.4 13.9 %copy-start.7 = (f32[64,768]{1,0:T(8,128)S(1)}, f32[64,768]{1,0:T(8,128)}, u32[]{:S(2)}) copy-start(f32[64,768]{1,0:T(8,128)} %copy-done.6) | copy-start | bytes 589828
  31.4 13.9 %collective-permute-start.6 = (f32[32,768]{1,0:T(8,128)}, f32[32,768]{1,0:T(8,128)}, u32[]{:S(2)}, u32[]{:S(2)}) collective-permute-start(f32[32,768]{1,0:T(8,128)} %slice_select_fusion), channel_id=1, source_target_pairs={{0,4},{4,0},{8,12},{12,8},{16,20},{20,16},{24,28},{28,24},{1,5},{5... | collective-permute-start | bytes 294920 | tf_op jit(solution)/shard_map/ppermute | solution.py:59
  35.7 13.3 %copy-start.3 = (bf16[768,2304]{1,0:T(8,128)(2,1)S(1)}, bf16[768,2304]{1,0:T(8,128)(2,1)}, u32[]{:S(2)}) copy-start(bf16[768,2304]{1,0:T(8,128)(2,1)} %param.14) | copy-start | bytes 10616836
  35.8 3.8 %collective-permute-start.9 = (f32[32,24]{0,1:T(8,128)S(1)}, f32[32,24]{0,1:T(8,128)S(1)}, u32[]{:S(2)}, u32[]{:S(2)}) collective-permute-start(f32[32,24]{0,1:T(8,128)S(1)} %pad_maximum_fusion.4), channel_id=1, source_target_pairs={{0,8},{4,12},{8,0},{12,4},{16,24},{20,28},{24,16},{28,20},{1,9},{5... | collective-permute-start | bytes 9224 | tf_op jit(solution)/shard_map/ppermute | solution.py:59
  39.6 4.7 %collective-permute-start.11 = (f32[32,24]{0,1:T(8,128)S(1)}, f32[32,24]{0,1:T(8,128)S(1)}, u32[]{:S(2)}, u32[]{:S(2)}) collective-permute-start(f32[32,24]{0,1:T(8,128)S(1)} %pad_maximum_fusion.5), channel_id=1, source_target_pairs={{0,16},{4,20},{8,24},{12,28},{16,0},{20,4},{24,8},{28,12},{1,17},{... | collective-permute-start | bytes 9224 | tf_op jit(solution)/shard_map/ppermute | solution.py:59
  46.5 18.1 %collective-permute-start.8 = (bf16[32,768]{1,0:T(8,128)(2,1)S(1)}, bf16[32,768]{1,0:T(8,128)(2,1)S(1)}, u32[]{:S(2)}, u32[]{:S(2)}) collective-permute-start(bf16[32,768]{1,0:T(8,128)(2,1)S(1)} %add_convert_fusion), channel_id=1, source_target_pairs={{0,8},{4,12},{8,0},{12,4},{16,24},{20,28},{24,16},{28,20},{1,9},{5... | collective-permute-start | bytes 147464 | tf_op jit(solution)/shard_map/ppermute | solution.py:59
  51.0 1.0 %copy-start.4 = (bf16[4,64,768]{2,1,0:T(8,128)(2,1)S(1)}, bf16[4,64,768]{2,1,0:T(8,128)(2,1)}, u32[]{:S(2)}) copy-start(bf16[4,64,768]{2,1,0:T(8,128)(2,1)} %get-tuple-element.13) | copy-start | bytes 1179652
  51.0 1.1 %copy-start.5 = (bf16[4,64,768]{2,1,0:T(8,128)(2,1)S(1)}, bf16[4,64,768]{2,1,0:T(8,128)(2,1)}, u32[]{:S(2)}) copy-start(bf16[4,64,768]{2,1,0:T(8,128)(2,1)} %get-tuple-element.14) | copy-start | bytes 1179652
  61.3 1.4 %copy-start.2 = (bf16[4,256,768]{1,2,0:T(8,128)(2,1)S(1)}, bf16[4,256,768]{1,2,0:T(8,128)(2,1)}, u32[]{:S(2)}) copy-start(bf16[4,256,768]{1,2,0:T(8,128)(2,1)} %copy.42) | copy-start | bytes 4718596
  62.7 1.4 %copy-start.1 = (f32[12,64,4,64]{3,1,2,0:T(8,128)S(1)}, f32[12,64,4,64]{3,1,2,0:T(8,128)}, u32[]{:S(2)}) copy-start(f32[12,64,4,64]{3,1,2,0:T(8,128)} %get-tuple-element.27) | copy-start | bytes 2359300
  64.9 5.6 %collective-permute-start.10 = (bf16[32,768]{1,0:T(8,128)(2,1)S(1)}, bf16[32,768]{1,0:T(8,128)(2,1)S(1)}, u32[]{:S(2)}, u32[]{:S(2)}) collective-permute-start(bf16[32,768]{1,0:T(8,128)(2,1)S(1)} %fusion.53), channel_id=1, source_target_pairs={{0,16},{4,20},{8,24},{12,28},{16,0},{20,4},{24,8},{28,12},{1,17},{... | collective-permute-start | bytes 147464 | tf_op jit(solution)/shard_map/ppermute | solution.py:59
  71.5 1.6 %collective-permute-start.12 = (bf16[32,768]{1,0:T(8,128)(2,1)S(1)}, bf16[32,768]{1,0:T(8,128)(2,1)S(1)}, u32[]{:S(2)}, u32[]{:S(2)}) collective-permute-start(bf16[32,768]{1,0:T(8,128)(2,1)S(1)} %fusion.33), channel_id=1, source_target_pairs={{0,4},{4,0},{8,12},{12,8},{16,20},{20,16},{24,28},{28,24},{1,5},{5... | collective-permute-start | bytes 147464 | tf_op jit(solution)/shard_map/ppermute | solution.py:59
  72.0 1.3 %copy-start.10 = (bf16[64,768]{1,0:T(8,128)(2,1)S(1)}, bf16[64,768]{1,0:T(8,128)(2,1)}, u32[]{:S(2)}) copy-start(bf16[64,768]{1,0:T(8,128)(2,1)} %copy-done.9) | copy-start | bytes 294916
  73.3 2.0 %copy-start.14 = (f32[768]{0:T(1024)S(1)}, f32[768]{0:T(1024)}, u32[]{:S(2)}) copy-start(f32[768]{0:T(1024)} %param.16) | copy-start | bytes 9220
  75.3 7.7 %copy-start.12 = (f32[768]{0:T(1024)S(1)}, f32[768]{0:T(1024)}, u32[]{:S(2)}) copy-start(f32[768]{0:T(1024)} %param.19) | copy-start | bytes 9220

commit v9 on v8

--- a/solution.py
+++ b/solution.py
@@ -59,14 +59,16 @@
     return lax.ppermute(value, axis, [(i, i ^ step) for i in range(count)])
 
 
-def broadcast_from(value, axis, count, source):
+def broadcast_from(value, axis, count, source, held):
     here = lax.axis_index(axis)
     step = 1
     while step < count:
         got = partner(value, axis, step, count)
+        if step == 1:
+            got, held = lax.optimization_barrier((got, held))
         value = jnp.where(here // step == source // step, value, got)
         step *= 2
-    return value
+    return value, held
 
 
 def merge(lo, hi):
@@ -134,18 +136,19 @@
     flat_cells = cells.reshape(row_count * cols_dev, model_width)
     w_kv = w_qkv[:, model_width:]
 
-    tokens = broadcast_from(summary[0], "band", n_band, owner[0])
-    row_parts = fan_out(cells, "col", n_col)
+    tokens = broadcast_from(summary[0], "band", n_band, owner[0], cells)
+    row_parts = fan_out(tokens[1], "col", n_col)
+    tokens = tokens[0]
 
     qkv_cells = project(flat_cells, w_qkv).reshape(row_count, cols_dev, 3 * model_width)
     queries = qkv_cells[:, :, :model_width]
     own_keys = qkv_cells[:, :, model_width : 2 * model_width]
     own_vals = qkv_cells[:, :, 2 * model_width :]
 
-    summary_qkv = project(tokens, w_qkv)
-    sum_queries = summary_qkv[:, :model_width]
-    sum_keys = summary_qkv[:, model_width : 2 * model_width]
-    sum_vals = summary_qkv[:, 2 * model_width :]
+    sum_queries = project(tokens, w_qkv[:, :model_width])
+    summary_kv = project(tokens, w_kv)
+    sum_keys = summary_kv[:, :model_width]
+    sum_vals = summary_kv[:, model_width:]
 
     sq = sum_queries.astype(jnp.float32)
     col_scores = head_sum(sq[None] * own_keys.astype(jnp.float32)) * score_scale

time: 85.3 us -> 80.6 us (0.945)
  local copies, waits for them, and re-layouts: 14.7 us -> 12.7 us
  other arithmetic: 9.19 us -> 7.76 us
    ppermute x3, starting transfers between devices: 4.6 us -> 3.49 us  [fan_out(): got.append((source, lax.ppermute(value, axis, pairs)))]
    dot_general x3 -> x4, matrix products: 7.99 us -> 9.06 us  [project(): jnp.dot(values, weight, preferred_element_type=jnp.float32)]
    reshape x1, local copies, waits for them, and re-layouts: 1.13 us -> 0.17 us  [local(): sk = sum_keys.reshape(cols_dev, HEADS, HEAD_DIM)]
    dot_general x10, matrix products: 4.29 us -> 3.36 us  [head_spread(): jnp.dot(flat, head_matrix(), precision=lax.Precision.HIGHEST, preferred_e...]
    reshape x1, local copies, waits for them, and re-layouts: 1.05 us -> 0.16 us  [local(): sv = sum_vals.reshape(cols_dev, HEADS, HEAD_DIM)]
  transfers between devices with their start and end apart: 13 -> 13, of which waited for: 5 -> 6; matrix products, arithmetic and copies ran while one was open for 44% -> 43% of each run, Pallas kernels for 0% -> 0%
where the time goes in v9:
time: 80.6 us; the launch traced here: 80 us
  matrix products  28.1 us (35%)
  starting transfers between devices  15.8 us (20%)
  waiting for transfers between devices  13.7 us (17%)
  local copies, waits for them, and re-layouts  12.7 us (16%)
  other arithmetic  7.76 us (10%)
  between operations  1.91 us (2%)
    ppermute x10, waiting for transfers between devices, partner(): return lax.ppermute(value, axis, [(i, i ^ step) for i in range(count)])  13.7 us
    ppermute x10, starting transfers between devices, partner(): return lax.ppermute(value, axis, [(i, i ^ step) for i in range(count)])  12.4 us
    dot_general x4, matrix products, project(): jnp.dot(values, weight, preferred_element_type=jnp.float32)  9.06 us
    dot_general x1, matrix products, finish(): outer_out = jnp.dot(inner_act, w_down, preferred_element_type=jnp.float32)  7.43 us
    ppermute x3, starting transfers between devices, fan_out(): got.append((source, lax.ppermute(value, axis, pairs)))  3.49 us
    dot_general x10, matrix products, head_spread(): jnp.dot(flat, head_matrix(), precision=lax.Precision.HIGHEST, preferred_e...  3.36 us
    concatenate x1, local copies, waits for them, and re-layouts, local(): row_vals = jnp.concatenate([own_vals, other_kv[:, :, model_width:]], axis=1)  2.58 us
    concatenate x1, local copies, waits for them, and re-layouts, local(): row_keys = jnp.concatenate([own_keys, other_kv[:, :, :model_width]], axis=1)  2.58 us
  transfers between devices with their start and end apart: 13, of which 6 were waited for; matrix products, arithmetic and copies ran while one was open for 43% of the time, Pallas kernels for 0%

profile of v9, /device:TPU:0, one launch (start us, length us, event | category | flops | bytes accessed | tf_op | source)
XLA Modules:
  0.0 80.0 jit_solution(10253137013881320170)
XLA Ops:
  0.6 0.5 collective-permute-start
  1.8 3.2 %convolution_convert_fusion = bf16[256,2304]{1,0:T(8,128)(2,1)S(1)} fusion(bf16[256,768]{1,0:T(8,128)(2,1)} %bitcast.68, bf16[768,2304]{1,0:T(8,128)(2,1)} %param.14), kind=kOutput, calls=%fused_computation.9 | convolution fusion | flops 906559488 | bytes 5111808 | tf_op jit(solution)/shard_map/dot_general | solution.py:34
  5.1 1.0 %fusion.127 = (bf16[4,64,768]{2,1,0:T(8,128)(2,1)}, bf16[4,64,768]{2,1,0:T(8,128)(2,1)}, bf16[4,64,768]{2,1,0:T(8,128)(2,1)}) fusion(bf16[4,64,2304]{2,1,0:T(8,128)(2,1)S(1)} %bitcast.59), kind=kLoop, calls=%fused_computation.184 | loop fusion | bytes 2359296 | tf_op jit(solution)/shard_map/slice | solution.py:144
  6.2 0.7 broadcast_select_fusion
  6.9 2.7 %collective-permute-start.1 = (bf16[64,768]{1,0:T(8,128)(2,1)}, bf16[64,768]{1,0:T(8,128)(2,1)}, u32[]{:S(2)}, u32[]{:S(2)}) collective-permute-start(bf16[64,768]{1,0:T(8,128)(2,1)} %broadcast_select_fusion), channel_id=1, source_target_pairs={{0,8},{4,12},{8,0},{12,4},{16,24},{20,28},{24,16},{28,20},{1,9},{5... | collective-permute-start | bytes 294920 | tf_op jit(solution)/shard_map/ppermute | solution.py:59
  9.5 0.1 fusion.56
  9.7 1.7 %reshape.106 = bf16[4,64,12,64]{3,2,1,0:T(8,128)(2,1)S(1)} reshape(bf16[4,64,768]{2,1,0:T(8,128)(2,1)} %get-tuple-element.16) | data formatting | bytes 786432 | tf_op jit(solution)/shard_map/reshape | solution.py:186
  11.4 1.8 %collective-permute-done.1 = bf16[64,768]{1,0:T(8,128)(2,1)} collective-permute-done((bf16[64,768]{1,0:T(8,128)(2,1)}, bf16[64,768]{1,0:T(8,128)(2,1)}, u32[]{:S(2)}, u32[]{:S(2)}) %collective-permute-start.1) | collective-permute-done | bytes 98336 | tf_op jit(solution)/shard_map/ppermute | solution.py:59
  13.2 0.9 %broadcast_select_fusion.1 = bf16[64,768]{1,0:T(8,128)(2,1)S(1)} fusion(bf16[64,768]{1,0:T(8,128)(2,1)} %broadcast_select_fusion, bf16[64,768]{1,0:T(8,128)(2,1)} %collective-permute-done.1, pred[]{:T(512)S(6)} %eq.91), kind=kLoop, calls=%fused_computation.89 | loop fusion | flops 49152 | bytes 294913 | tf_op jit(solution)/shard_map/jit(_where)/select_n | solution.py:69
  14.1 2.8 %collective-permute-start.2 = (bf16[64,768]{1,0:T(8,128)(2,1)S(1)}, bf16[64,768]{1,0:T(8,128)(2,1)S(1)}, u32[]{:S(2)}, u32[]{:S(2)}) collective-permute-start(bf16[64,768]{1,0:T(8,128)(2,1)S(1)} %broadcast_select_fusion.1), channel_id=1, source_target_pairs={{0,16},{4,20},{8,24},{12,28},{16,0},{20,4},{24,8},{28,12},{1,17},{... | collective-permute-start | bytes 294920 | tf_op jit(solution)/shard_map/ppermute | solution.py:59
  17.0 2.4 %collective-permute-start.5 = (bf16[4,64,768]{2,1,0:T(8,128)(2,1)}, bf16[4,64,768]{2,1,0:T(8,128)(2,1)}, u32[]{:S(2)}, u32[]{:S(2)}) collective-permute-start(bf16[4,64,768]{2,1,0:T(8,128)(2,1)} %param.10), channel_id=1, source_target_pairs={{0,3},{1,2},{2,1},{3,0},{4,7},{5,6},{6,5},{7,4},{8,11},{9,10},{10,... | collective-permute-start | bytes 1179656 | tf_op jit(solution)/shard_map/ppermute | solution.py:127
  19.4 0.5 collective-permute-start.4
  19.9 0.5 collective-permute-start.3
  20.5 1.3 %collective-permute-done.2 = bf16[64,768]{1,0:T(8,128)(2,1)S(1)} collective-permute-done((bf16[64,768]{1,0:T(8,128)(2,1)S(1)}, bf16[64,768]{1,0:T(8,128)(2,1)S(1)}, u32[]{:S(2)}, u32[]{:S(2)}) %collective-permute-start.2) | collective-permute-done | bytes 98336 | tf_op jit(solution)/shard_map/ppermute | solution.py:59
  21.8 1.6 %fusion.39 = f32[64,768]{1,0:T(8,128)S(1)} fusion(bf16[64,768]{1,0:T(8,128)(2,1)S(1)} %broadcast_select_fusion.2, bf16[768,2304]{1,0:T(8,128)(2,1)} %param.14), kind=kOutput, calls=%fused_computation.47 | convolution fusion | flops 75595776 | bytes 1474560 | tf_op jit(solution)/shard_map/dot_general | solution.py:34
  23.4 2.2 %convolution_convert_fusion.2 = bf16[64,1536]{1,0:T(8,128)(2,1)S(1)} fusion(bf16[64,768]{1,0:T(8,128)(2,1)S(1)} %broadcast_select_fusion.2, bf16[768,2304]{1,0:T(8,128)(2,1)} %param.14), kind=kOutput, calls=%fused_computation.16 | convolution fusion | flops 151093248 | bytes 2654208 | tf_op jit(solution)/shard_map/dot_general | solution.py:34
  25.6 0.6 fusion.129
  26.3 0.3 fusion.33
  26.6 0.2 convolution_multiply_fusion.3
  27.0 0.3 copy-done.5
  27.3 0.2 reshape.108
  27.5 2.0 %bitcast_reduce_fusion = (f32[4,12,64]{2,0,1:T(4,128)S(1)}, f32[12,64,4,64]{3,1,2,0:T(8,128)}) fusion(bf16[4,64,12,64]{3,2,1,0:T(8,128)(2,1)S(1)} %reshape.106, bf16[64,12,64,1]{2,1,0,3:T(8,128)(2,1)S(1)} %bitcast.64), kind=kOutput, calls=%fused_computation.31 | convolution fusion | flops 25555968 | bytes 1290240 | tf_op jit(solution)/shard_map/rqhd,khd->rhqk/dot_general | solution.py:203
  29.6 0.2 collective-permute-start.6
  29.8 0.2 copy.58
  30.1 0.7 collective-permute-start.9
  30.8 0.2 fusion.76
  31.1 2.8 %collective-permute-done.9 = f32[32,24]{0,1:T(8,128)S(1)} collective-permute-done((f32[32,24]{0,1:T(8,128)S(1)}, f32[32,24]{0,1:T(8,128)S(1)}, u32[]{:S(2)}, u32[]{:S(2)}) %collective-permute-start.9) | collective-permute-done | bytes 3104 | tf_op jit(solution)/shard_map/ppermute | solution.py:59
  33.9 2.1 %collective-permute-start.11 = (f32[32,24]{0,1:T(8,128)S(1)}, f32[32,24]{0,1:T(8,128)S(1)}, u32[]{:S(2)}, u32[]{:S(2)}) collective-permute-start(f32[32,24]{0,1:T(8,128)S(1)} %pad_maximum_fusion.5), channel_id=1, source_target_pairs={{0,16},{4,20},{8,24},{12,28},{16,0},{20,4},{24,8},{28,12},{1,17},{... | collective-permute-start | bytes 9224 | tf_op jit(solution)/shard_map/ppermute | solution.py:59
  36.0 0.3 fusion.73
  36.3 2.3 %collective-permute-done.11 = f32[32,24]{0,1:T(8,128)S(1)} collective-permute-done((f32[32,24]{0,1:T(8,128)S(1)}, f32[32,24]{0,1:T(8,128)S(1)}, u32[]{:S(2)}, u32[]{:S(2)}) %collective-permute-start.11) | collective-permute-done | bytes 3104 | tf_op jit(solution)/shard_map/ppermute | solution.py:59
  38.6 0.2 fusion.72
  38.9 0.3 fusion.71
  39.1 0.3 add_convert_fusion
  39.4 1.2 %collective-permute-start.8 = (bf16[32,768]{1,0:T(8,128)(2,1)S(1)}, bf16[32,768]{1,0:T(8,128)(2,1)S(1)}, u32[]{:S(2)}, u32[]{:S(2)}) collective-permute-start(bf16[32,768]{1,0:T(8,128)(2,1)S(1)} %add_convert_fusion), channel_id=1, source_target_pairs={{0,8},{4,12},{8,0},{12,4},{16,24},{20,28},{24,16},{28,20},{1,9},{5... | collective-permute-start | bytes 147464 | tf_op jit(solution)/shard_map/ppermute | solution.py:59
  40.6 0.3 fusion.70
  40.8 2.7 %collective-permute-done.8 = bf16[32,768]{1,0:T(8,128)(2,1)S(1)} collective-permute-done((bf16[32,768]{1,0:T(8,128)(2,1)S(1)}, bf16[32,768]{1,0:T(8,128)(2,1)S(1)}, u32[]{:S(2)}, u32[]{:S(2)}) %collective-permute-start.8) | collective-permute-done | bytes 49184 | tf_op jit(solution)/shard_map/ppermute | solution.py:59
  43.6 0.3 fusion.62
  43.8 2.1 %collective-permute-start.10 = (bf16[32,768]{1,0:T(8,128)(2,1)S(1)}, bf16[32,768]{1,0:T(8,128)(2,1)S(1)}, u32[]{:S(2)}, u32[]{:S(2)}) collective-permute-start(bf16[32,768]{1,0:T(8,128)(2,1)S(1)} %fusion.62), channel_id=1, source_target_pairs={{0,16},{4,20},{8,24},{12,28},{16,0},{20,4},{24,8},{28,12},{1,17},{... | collective-permute-start | bytes 147464 | tf_op jit(solution)/shard_map/ppermute | solution.py:59
  45.9 0.2 fusion.69
  46.1 2.8 %collective-permute-done.10 = bf16[32,768]{1,0:T(8,128)(2,1)S(1)} collective-permute-done((bf16[32,768]{1,0:T(8,128)(2,1)S(1)}, bf16[32,768]{1,0:T(8,128)(2,1)S(1)}, u32[]{:S(2)}, u32[]{:S(2)}) %collective-permute-start.10) | collective-permute-done | bytes 49184 | tf_op jit(solution)/shard_map/ppermute | solution.py:59
  48.9 1.1 %fusion.42 = bf16[32,768]{1,0:T(8,128)(2,1)S(1)} fusion(f32[32,768]{1,0:T(8,128)S(1)} %fusion.70, f32[32,768]{1,0:T(8,128)S(1)} %fusion.72, bf16[32,768]{1,0:T(8,128)(2,1)S(1)} %collective-permute-done.10, bf16[32,768]{1,0:T(8,128)(2,1)S(1)} %fusion.62, f32[32,768]{1,0:T(8,128)S(1)} %fusion.71, f32[32,768]{1,0:T(8,128)S(1)} %fusion.69, ...), kind=kOutput, calls=%fused_computation.49 | convolution fusion | flops 3896064 | bytes 692226 | tf_op jit(solution)/shard_map/dot_general | solution.py:53
  50.1 1.3 %pad_maximum_fusion.2 = bf16[4,192,768]{2,1,0:T(8,128)(2,1)S(1)} fusion(bf16[4,64,768]{2,1,0:T(8,128)(2,1)} %collective-permute-done.5, bf16[4,64,768]{2,1,0:T(8,128)(2,1)} %collective-permute-done.4, bf16[4,64,768]{2,1,0:T(8,128)(2,1)} %collective-permute-done.3), kind=kLoop, calls=%fused_computation.43 | loop fusion | flops 3538944 | bytes 2359296 | tf_op jit(solution)/shard_map/concatenate | solution.py:179
  51.4 2.0 %convolution_convert_fusion.1 = bf16[768,1536]{1,0:T(8,128)(2,1)S(1)} fusion(bf16[768,768]{1,0:T(8,128)(2,1)S(1)} %bitcast.63, bf16[768,2304]{1,0:T(8,128)(2,1)S(1)} %copy-done.10), kind=kOutput, calls=%fused_computation.10 | convolution fusion | flops 1813118976 | bytes 5898240 | tf_op jit(solution)/shard_map/dot_general | solution.py:34
  53.4 0.2 fusion.126
  53.6 0.8 %copy-done.3 = bf16[4,64,768]{2,1,0:T(8,128)(2,1)S(1)} copy-done((bf16[4,64,768]{2,1,0:T(8,128)(2,1)S(1)}, bf16[4,64,768]{2,1,0:T(8,128)(2,1)}, u32[]{:S(2)}) %copy-start.3) | copy-done | bytes 393240
  54.5 1.9 %pad_maximum_fusion = (bf16[4,256,768]{2,1,0:T(8,128)(2,1)}, bf16[4,256,768]{2,1,0:T(8,128)(2,1)}) fusion(bf16[4,192,768]{2,1,0:T(8,128)(2,1)S(1)} %get-tuple-element.13, bf16[4,64,768]{2,1,0:T(8,128)(2,1)S(1)} %copy-done.4, bf16[4,192,768]{2,1,0:T(8,128)(2,1)S(1)} %get-tuple-element.12, bf16[4,64,768]{2,1,0:T(8,128)(2,1)S(1)} %copy-done.3), kind=kLoop, calls=%fused_computation.25 | loop fusion | flops 6291456 | bytes 6291456 | tf_op jit(solution)/shard_map/concatenate | solution.py:184
  56.4 2.6 %copy.42 = bf16[4,256,768]{1,2,0:T(8,128)(2,1)} copy(bf16[4,256,768]{2,1,0:T(8,128)(2,1)} %get-tuple-element.35) | data formatting | bytes 3145728 | tf_op jit(solution)/shard_map/concatenate | solution.py:184
  59.0 2.6 %copy.43 = bf16[4,256,768]{1,2,0:T(8,128)(2,1)} copy(bf16[4,256,768]{2,1,0:T(8,128)(2,1)} %get-tuple-element.36) | data formatting | bytes 3145728 | tf_op jit(solution)/shard_map/concatenate | solution.py:183
  61.6 2.1 %fusion.8 = (f32[4,12,64]{2,1,0:T(8,128)S(1)}, f32[4,12,64,256]{3,2,1,0:T(8,128)S(1)}) fusion(pred[4,64,256]{2,1,0:T(8,128)(4,1)S(1)} %fusion.56, bf16[4,256,12,64]{1,3,2,0:T(8,128)(2,1)} %bitcast.58, bf16[4,64,12,64]{3,2,1,0:T(8,128)(2,1)S(1)} %reshape.106), kind=kOutput, calls=%fused_computation.13 | convolution fusion | flops 103019520 | bytes 5189632 | tf_op jit(solution)/shard_map/rqhd,rkhd->rhqk/dot_general | solution.py:199
  63.8 1.2 %fusion.9 = f32[4,12,64]{2,1,0:T(8,128)S(1)} fusion(f32[4,12,64,256]{3,2,1,0:T(8,128)S(1)} %get-tuple-element.28, f32[4,12,64]{2,1,0:T(8,128)S(1)} %copy_maximum_fusion, pred[4,64,256]{2,1,0:T(8,128)(4,1)S(1)} %fusion.56), kind=kLoop, calls=%fused_computation.14 | loop fusion | flops 3142656 | bytes 3235840 | tf_op jit(solution)/shard_map/reduce_sum | solution.py:208
  65.0 0.1 copy-done.2
  65.1 1.3 %fusion.19 = f32[4,12,64,64]{3,2,1,0:T(8,128)S(1)} fusion(bf16[4,256,12,64]{1,3,2,0:T(8,128)(2,1)S(1)} %bitcast.57, f32[4,12,64,256]{3,2,1,0:T(8,128)S(1)} %get-tuple-element.28, f32[4,12,64]{2,1,0:T(8,128)S(1)} %copy_maximum_fusion, pred[4,64,256]{2,1,0:T(8,128)(4,1)S(1)} %fusion.56), kind=kOutput, calls=%fused_computation.24 | convolution fusion | flops 103809024 | bytes 5582848 | tf_op jit(solution)/shard_map/rhqk,rkhd->rqhd/dot_general | solution.py:209
  66.5 0.4 fusion.28
  67.0 0.4 fusion.22
  67.4 0.6 copy.52
  68.0 0.5 convert_element_type.102
  68.5 0.2 copy.53
  68.7 1.7 %fusion.130 = (f32[320]{0:T(512)S(1)}, f32[320,768]{1,0:T(8,128)S(1)}) fusion(bf16[768,768]{1,0:T(8,128)(2,1)S(1)} %copy-done, bf16[64,768]{0,1:T(8,128)(2,1)S(1)} %copy.53, bf16[256,768]{0,1:T(8,128)(2,1)S(1)} %convert_element_type.102, bf16[64,768]{1,0:T(8,128)(2,1)S(1)} %copy-done.9, bf16[256,768]{1,0:T(8,128)(2,1)} %bitcast.69), kind=kOutput, calls=%fused_computation.187 | convolution fusion | flops 379944640 | bytes 3147008 | tf_op jit(solution)/shard_map/dot_general | solution.py:24
  70.4 0.3 multiply_reduce_fusion.1
  70.7 7.4 %fusion.131 = (f32[320]{0:T(512)S(1)}, f32[320,768]{1,0:T(8,128)S(1)}) fusion(bf16[3072,768]{1,0:T(8,128)(2,1)} %param.18, bf16[768,3072]{1,0:T(8,128)(2,1)} %param.17, f32[320,768]{1,0:T(8,128)S(1)} %get-tuple-element.32, f32[768]{0:T(1024)S(1)} %copy-done.14, f32[320]{0:T(512)S(1)} %add_rsqrt_fusion.1, f32[320]{0:T(512)S(1)} %broadcast_multiply_fusion.1), kind=kOutput, calls=%fused_computation.188 | convolution fusion | flops 3031449344 | bytes 11410176 | tf_op jit(solution)/shard_map/dot_general | solution.py:29
  78.1 0.3 multiply_reduce_fusion
  78.4 0.2 multiply_convert_fusion
  78.6 0.8 slice.159
  79.4 0.6 slice.160
  (66 shorter events, 1.0 us)
Async XLA Ops:
  0.6 68.1 %copy-start = (bf16[768,768]{1,0:T(8,128)(2,1)S(1)}, bf16[768,768]{1,0:T(8,128)(2,1)}, u32[]{:S(2)}) copy-start(bf16[768,768]{1,0:T(8,128)(2,1)} %param.15) | copy-start | bytes 3538948
  0.6 5.6 %collective-permute-start = (bf16[64,768]{1,0:T(8,128)(2,1)}, bf16[64,768]{1,0:T(8,128)(2,1)S(1)}, u32[]{:S(2)}, u32[]{:S(2)}) collective-permute-start(bf16[64,768]{1,0:T(8,128)(2,1)} %bitcast.67), channel_id=1, source_target_pairs={{0,4},{4,0},{8,12},{12,8},{16,20},{20,16},{24,28},{28,24},{1,5},{5... | collective-permute-start | bytes 294920 | tf_op jit(solution)/shard_map/ppermute | solution.py:59
  5.0 1.2 %copy-start.11 = (bf16[1,64,768]{2,1,0:T(8,128)(2,1)S(1)}, bf16[1,64,768]{2,1,0:T(8,128)(2,1)}, u32[]{:S(2)}) copy-start(bf16[1,64,768]{2,1,0:T(8,128)(2,1)} %param.11) | copy-start | bytes 294916
  5.1 4.5 %copy-start.13 = (s32[4,64]{1,0:T(4,128)S(1)}, s32[4,64]{1,0:T(4,128)}, u32[]{:S(2)}) copy-start(s32[4,64]{1,0:T(4,128)} %param.13) | copy-start | bytes 3076
  6.9 6.4 %collective-permute-start.1 = (bf16[64,768]{1,0:T(8,128)(2,1)}, bf16[64,768]{1,0:T(8,128)(2,1)}, u32[]{:S(2)}, u32[]{:S(2)}) collective-permute-start(bf16[64,768]{1,0:T(8,128)(2,1)} %broadcast_select_fusion), channel_id=1, source_target_pairs={{0,8},{4,12},{8,0},{12,4},{16,24},{20,28},{24,16},{28,20},{1,9},{5... | collective-permute-start | bytes 294920 | tf_op jit(solution)/shard_map/ppermute | solution.py:59
  14.1 7.6 %collective-permute-start.2 = (bf16[64,768]{1,0:T(8,128)(2,1)S(1)}, bf16[64,768]{1,0:T(8,128)(2,1)S(1)}, u32[]{:S(2)}, u32[]{:S(2)}) collective-permute-start(bf16[64,768]{1,0:T(8,128)(2,1)S(1)} %broadcast_select_fusion.1), channel_id=1, source_target_pairs={{0,16},{4,20},{8,24},{12,28},{16,0},{20,4},{24,8},{28,12},{1,17},{... | collective-permute-start | bytes 294920 | tf_op jit(solution)/shard_map/ppermute | solution.py:59
  17.0 33.1 %collective-permute-start.5 = (bf16[4,64,768]{2,1,0:T(8,128)(2,1)}, bf16[4,64,768]{2,1,0:T(8,128)(2,1)}, u32[]{:S(2)}, u32[]{:S(2)}) collective-permute-start(bf16[4,64,768]{2,1,0:T(8,128)(2,1)} %param.10), channel_id=1, source_target_pairs={{0,3},{1,2},{2,1},{3,0},{4,7},{5,6},{6,5},{7,4},{8,11},{9,10},{10,... | collective-permute-start | bytes 1179656 | tf_op jit(solution)/shard_map/ppermute | solution.py:127
  19.4 30.7 %collective-permute-start.4 = (bf16[4,64,768]{2,1,0:T(8,128)(2,1)}, bf16[4,64,768]{2,1,0:T(8,128)(2,1)}, u32[]{:S(2)}, u32[]{:S(2)}) collective-permute-start(bf16[4,64,768]{2,1,0:T(8,128)(2,1)} %param.10), channel_id=1, source_target_pairs={{0,2},{1,3},{2,0},{3,1},{4,6},{5,7},{6,4},{7,5},{8,10},{9,11},{10,... | collective-permute-start | bytes 1179656 | tf_op jit(solution)/shard_map/ppermute | solution.py:127
  19.9 30.2 %collective-permute-start.3 = (bf16[4,64,768]{2,1,0:T(8,128)(2,1)}, bf16[4,64,768]{2,1,0:T(8,128)(2,1)}, u32[]{:S(2)}, u32[]{:S(2)}) collective-permute-start(bf16[4,64,768]{2,1,0:T(8,128)(2,1)} %param.10), channel_id=1, source_target_pairs={{0,1},{1,0},{2,3},{3,2},{4,5},{5,4},{6,7},{7,6},{8,9},{9,8},{10,11... | collective-permute-start | bytes 1179656 | tf_op jit(solution)/shard_map/ppermute | solution.py:127
  21.8 4.5 %copy-start.8 = (bf16[64,768]{1,0:T(8,128)(2,1)}, bf16[64,768]{1,0:T(8,128)(2,1)S(1)}, u32[]{:S(2)}) copy-start(bf16[64,768]{1,0:T(8,128)(2,1)S(1)} %broadcast_select_fusion.2) | copy-start | bytes 294916
  25.6 1.7 %copy-start.7 = (bf16[64,1536]{1,0:T(8,128)(2,1)}, bf16[64,1536]{1,0:T(8,128)(2,1)S(1)}, u32[]{:S(2)}) copy-start(bf16[64,1536]{1,0:T(8,128)(2,1)S(1)} %convolution_convert_fusion.2) | copy-start | bytes 589828
  26.6 0.7 copy-start.5
  27.0 3.0 %collective-permute-start.7 = (f32[32,24]{0,1:T(8,128)S(1)}, f32[32,24]{0,1:T(8,128)S(1)}, u32[]{:S(2)}, u32[]{:S(2)}) collective-permute-start(f32[32,24]{0,1:T(8,128)S(1)} %fusion.106), channel_id=1, source_target_pairs={{0,4},{4,0},{8,12},{12,8},{16,20},{20,16},{24,28},{28,24},{1,5},{5... | collective-permute-start | bytes 9224 | tf_op jit(solution)/shard_map/ppermute | solution.py:59
  27.3 11.8 %copy-start.6 = (f32[64,768]{1,0:T(8,128)S(1)}, f32[64,768]{1,0:T(8,128)}, u32[]{:S(2)}) copy-start(f32[64,768]{1,0:T(8,128)} %copy-done.5) | copy-start | bytes 589828
  29.6 9.5 %collective-permute-start.6 = (f32[32,768]{1,0:T(8,128)S(1)}, f32[32,768]{1,0:T(8,128)S(1)}, u32[]{:S(2)}, u32[]{:S(2)}) collective-permute-start(f32[32,768]{1,0:T(8,128)S(1)} %slice_select_fusion), channel_id=1, source_target_pairs={{0,4},{4,0},{8,12},{12,8},{16,20},{20,16},{24,28},{28,24},{1,5},{5... | collective-permute-start | bytes 294920 | tf_op jit(solution)/shard_map/ppermute | solution.py:59
  30.1 21.3 %copy-start.10 = (bf16[768,2304]{1,0:T(8,128)(2,1)S(1)}, bf16[768,2304]{1,0:T(8,128)(2,1)}, u32[]{:S(2)}) copy-start(bf16[768,2304]{1,0:T(8,128)(2,1)} %param.14) | copy-start | bytes 10616836
  30.1 3.8 %collective-permute-start.9 = (f32[32,24]{0,1:T(8,128)S(1)}, f32[32,24]{0,1:T(8,128)S(1)}, u32[]{:S(2)}, u32[]{:S(2)}) collective-permute-start(f32[32,24]{0,1:T(8,128)S(1)} %pad_maximum_fusion.4), channel_id=1, source_target_pairs={{0,8},{4,12},{8,0},{12,4},{16,24},{20,28},{24,16},{28,20},{1,9},{5... | collective-permute-start | bytes 9224 | tf_op jit(solution)/shard_map/ppermute | solution.py:59
  33.9 4.7 %collective-permute-start.11 = (f32[32,24]{0,1:T(8,128)S(1)}, f32[32,24]{0,1:T(8,128)S(1)}, u32[]{:S(2)}, u32[]{:S(2)}) collective-permute-start(f32[32,24]{0,1:T(8,128)S(1)} %pad_maximum_fusion.5), channel_id=1, source_target_pairs={{0,16},{4,20},{8,24},{12,28},{16,0},{20,4},{24,8},{28,12},{1,17},{... | collective-permute-start | bytes 9224 | tf_op jit(solution)/shard_map/ppermute | solution.py:59
  39.4 4.2 %collective-permute-start.8 = (bf16[32,768]{1,0:T(8,128)(2,1)S(1)}, bf16[32,768]{1,0:T(8,128)(2,1)S(1)}, u32[]{:S(2)}, u32[]{:S(2)}) collective-permute-start(bf16[32,768]{1,0:T(8,128)(2,1)S(1)} %add_convert_fusion), channel_id=1, source_target_pairs={{0,8},{4,12},{8,0},{12,4},{16,24},{20,28},{24,16},{28,20},{1,9},{5... | collective-permute-start | bytes 147464 | tf_op jit(solution)/shard_map/ppermute | solution.py:59
  43.8 5.1 %collective-permute-start.10 = (bf16[32,768]{1,0:T(8,128)(2,1)S(1)}, bf16[32,768]{1,0:T(8,128)(2,1)S(1)}, u32[]{:S(2)}, u32[]{:S(2)}) collective-permute-start(bf16[32,768]{1,0:T(8,128)(2,1)S(1)} %fusion.62), channel_id=1, source_target_pairs={{0,16},{4,20},{8,24},{12,28},{16,0},{20,4},{24,8},{28,12},{1,17},{... | collective-permute-start | bytes 147464 | tf_op jit(solution)/shard_map/ppermute | solution.py:59
  50.0 18.5 %collective-permute-start.12 = (bf16[32,768]{1,0:T(8,128)(2,1)S(1)}, bf16[32,768]{1,0:T(8,128)(2,1)S(1)}, u32[]{:S(2)}, u32[]{:S(2)}) collective-permute-start(bf16[32,768]{1,0:T(8,128)(2,1)S(1)} %fusion.42), channel_id=1, source_target_pairs={{0,4},{4,0},{8,12},{12,8},{16,20},{20,16},{24,28},{28,24},{1,5},{5... | collective-permute-start | bytes 147464 | tf_op jit(solution)/shard_map/ppermute | solution.py:59
  53.4 1.0 %copy-start.3 = (bf16[4,64,768]{2,1,0:T(8,128)(2,1)S(1)}, bf16[4,64,768]{2,1,0:T(8,128)(2,1)}, u32[]{:S(2)}) copy-start(bf16[4,64,768]{2,1,0:T(8,128)(2,1)} %get-tuple-element.17) | copy-start | bytes 1179652
  53.4 1.1 %copy-start.4 = (bf16[4,64,768]{2,1,0:T(8,128)(2,1)S(1)}, bf16[4,64,768]{2,1,0:T(8,128)(2,1)}, u32[]{:S(2)}) copy-start(bf16[4,64,768]{2,1,0:T(8,128)(2,1)} %get-tuple-element.18) | copy-start | bytes 1179652
  63.7 1.4 %copy-start.2 = (bf16[4,256,768]{1,2,0:T(8,128)(2,1)S(1)}, bf16[4,256,768]{1,2,0:T(8,128)(2,1)}, u32[]{:S(2)}) copy-start(bf16[4,256,768]{1,2,0:T(8,128)(2,1)} %copy.42) | copy-start | bytes 4718596
  65.1 1.4 %copy-start.1 = (f32[12,64,4,64]{3,1,2,0:T(8,128)S(1)}, f32[12,64,4,64]{3,1,2,0:T(8,128)}, u32[]{:S(2)}) copy-start(f32[12,64,4,64]{3,1,2,0:T(8,128)} %get-tuple-element.30) | copy-start | bytes 2359300
  67.4 1.3 %copy-start.9 = (bf16[64,768]{1,0:T(8,128)(2,1)S(1)}, bf16[64,768]{1,0:T(8,128)(2,1)}, u32[]{:S(2)}) copy-start(bf16[64,768]{1,0:T(8,128)(2,1)} %copy-done.8) | copy-start | bytes 294916
  68.7 2.0 %copy-start.14 = (f32[768]{0:T(1024)S(1)}, f32[768]{0:T(1024)}, u32[]{:S(2)}) copy-start(f32[768]{0:T(1024)} %param.16) | copy-start | bytes 9220
  70.7 7.7 %copy-start.12 = (f32[768]{0:T(1024)S(1)}, f32[768]{0:T(1024)}, u32[]{:S(2)}) copy-start(f32[768]{0:T(1024)} %param.19) | copy-start | bytes 9220

commit v10 on v9

--- a/solution.py
+++ b/solution.py
@@ -176,16 +176,19 @@
     summary_att = join_halves(summary_att, "band", n_band)
 
     sources = [own_group] + [s for s, _ in row_parts]
-    other_cells = jnp.concatenate([got for _, got in row_parts], axis=1)
-    width_other = other_cells.shape[1]
-    other_kv = project(other_cells.reshape(row_count * width_other, model_width), w_kv)
-    other_kv = other_kv.reshape(row_count, width_other, 2 * model_width)
-    row_keys = jnp.concatenate([own_keys, other_kv[:, :, :model_width]], axis=1)
-    row_vals = jnp.concatenate([own_vals, other_kv[:, :, model_width:]], axis=1)
-    width_now = row_keys.shape[1]
+    row_cells = jnp.concatenate([cells] + [got for _, got in row_parts], axis=1)
+    width_now = row_cells.shape[1]
+    keys_t = jnp.einsum(
+        "ic,rki->rck", w_qkv[:, model_width : 2 * model_width], row_cells,
+        preferred_element_type=jnp.float32,
+    ).astype(jnp.bfloat16)
+    vals_t = jnp.einsum(
+        "ic,rki->rck", w_qkv[:, 2 * model_width :], row_cells,
+        preferred_element_type=jnp.float32,
+    ).astype(jnp.bfloat16)
     q4 = queries.reshape(row_count, cols_dev, HEADS, HEAD_DIM)
-    k4 = row_keys.reshape(row_count, width_now, HEADS, HEAD_DIM)
-    v4 = row_vals.reshape(row_count, width_now, HEADS, HEAD_DIM)
+    k4 = keys_t.reshape(row_count, HEADS, HEAD_DIM, width_now)
+    v4 = vals_t.reshape(row_count, HEADS, HEAD_DIM, width_now)
     sk = sum_keys.reshape(cols_dev, HEADS, HEAD_DIM)
     sv = sum_vals.reshape(cols_dev, HEADS, HEAD_DIM)
     key_groups = jnp.concatenate(
@@ -196,7 +199,7 @@
         None, None, :
     ]
     cell_scores = (
-        jnp.einsum("rqhd,rkhd->rhqk", q4, k4, preferred_element_type=jnp.float32) * score_scale
+        jnp.einsum("rqhd,rhdk->rhqk", q4, k4, preferred_element_type=jnp.float32) * score_scale
     )
     cell_scores = jnp.where(allowed[:, None], cell_scores, -1e30)
     tok_scores = (
@@ -207,7 +210,7 @@
     tok_exp = jnp.exp(tok_scores - row_top[..., None])
     row_total = cell_exp.sum(-1) + tok_exp.sum(-1)
     mixed = jnp.einsum(
-        "rhqk,rkhd->rqhd", cell_exp.astype(jnp.bfloat16), v4, preferred_element_type=jnp.float32
+        "rhqk,rhdk->rqhd", cell_exp.astype(jnp.bfloat16), v4, preferred_element_type=jnp.float32
     )
     mixed = mixed + jnp.einsum(
         "rhqk,khd->rqhd", tok_exp.astype(jnp.bfloat16), sv, preferred_element_type=jnp.float32

time: 80.6 us -> 87.6 us (1.087)
  local copies, waits for them, and re-layouts: 12.7 us -> 19.9 us
  matrix products: 28.1 us -> 33.5 us
  other arithmetic: 7.76 us -> 3.67 us
  waiting for transfers between devices: 13.7 us -> 11.8 us
    dot_general x2 -> x4, matrix products: 3.4 us -> 9.88 us  [the longest x1 4.07 us: local(): jnp.einsum('ic,rki->rck', w_qkv[:, 2 * model_width:], row_cells, preferre...]
    convert_element_type x0 -> x2, local copies, waits for them, and re-layouts: none -> 5.35 us  [the longest x1 2.76 us: local(): vals_t = jnp.einsum('ic,rki->rck', w_qkv[:, 2 * model_width:], row_cells,...]
    unnamed x30 -> x33, local copies, waits for them, and re-layouts: 1.56 us -> 5.05 us
    concatenate x2 -> x1, local copies, waits for them, and re-layouts: 5.16 us -> 1.78 us  [local(): row_cells = jnp.concatenate([cells] + [got for _, got in row_parts], axis=1)]
    concatenate x2 -> x0, other arithmetic: 3.2 us -> none  [the longest x1 1.88 us: local(): row_vals = jnp.concatenate([own_vals, other_kv[:, :, model_width:]], axis=1)]
    ppermute x10, waiting for transfers between devices: 13.7 us -> 11.8 us  [partner(): return lax.ppermute(value, axis, [(i, i ^ step) for i in range(count)])]
    select_n x3, other arithmetic: 1.57 us -> 0.04 us  [broadcast_from(): value = jnp.where(here // step == source // step, value, got)]
    reshape x1, local copies, waits for them, and re-layouts: 1.66 us -> 0.61 us  [local(): q4 = queries.reshape(row_count, cols_dev, HEADS, HEAD_DIM)]
  transfers between devices with their start and end apart: 13 -> 13, of which waited for: 6 -> 5; matrix products, arithmetic and copies ran while one was open for 43% -> 51% of each run, Pallas kernels for 0% -> 0%
where the time goes in v10:
time: 87.6 us; the launch traced here: 87.1 us
  matrix products  33.5 us (38%)
  local copies, waits for them, and re-layouts  19.9 us (23%)
  starting transfers between devices  16.4 us (19%)
  waiting for transfers between devices  11.8 us (13%)
  other arithmetic  3.67 us (4%)
  between operations  1.79 us (2%)
    ppermute x10, starting transfers between devices, partner(): return lax.ppermute(value, axis, [(i, i ^ step) for i in range(count)])  13 us
    ppermute x10, waiting for transfers between devices, partner(): return lax.ppermute(value, axis, [(i, i ^ step) for i in range(count)])  11.8 us
    dot_general x3, matrix products, project(): jnp.dot(values, weight, preferred_element_type=jnp.float32)  8.15 us
    dot_general x1, matrix products, finish(): outer_out = jnp.dot(inner_act, w_down, preferred_element_type=jnp.float32)  7.43 us
    unnamed x33, local copies, waits for them, and re-layouts  5.05 us
    dot_general x1, matrix products, local(): jnp.einsum('ic,rki->rck', w_qkv[:, 2 * model_width:], row_cells, preferre...  4.07 us
    ppermute x3, starting transfers between devices, fan_out(): got.append((source, lax.ppermute(value, axis, pairs)))  3.49 us
    convert_element_type x1, local copies, waits for them, and re-layouts, local(): vals_t = jnp.einsum('ic,rki->rck', w_qkv[:, 2 * model_width:], row_cells,...  2.76 us
  transfers between devices with their start and end apart: 13, of which 5 were waited for; matrix products, arithmetic and copies ran while one was open for 51% of the time, Pallas kernels for 0%

profile of v10, /device:TPU:0, one launch (start us, length us, event | category | flops | bytes accessed | tf_op | source)
XLA Modules:
  0.0 87.1 jit_solution(18424937358119033848)
XLA Ops:
  0.6 0.5 collective-permute-start
  1.2 4.3 %convolution_convert_fusion = bf16[256,2304]{1,0:T(8,128)(2,1)} fusion(bf16[256,768]{1,0:T(8,128)(2,1)} %bitcast.72, bf16[768,2304]{1,0:T(8,128)(2,1)} %param.14), kind=kOutput, calls=%fused_computation.9 | convolution fusion | flops 906559488 | bytes 5111808 | tf_op jit(solution)/shard_map/dot_general | solution.py:34
  5.5 0.1 fusion.66
  6.4 1.0 %slice.132 = bf16[4,64,768]{2,1,0:T(8,128)(2,1)S(1)} slice(bf16[4,64,2304]{2,1,0:T(8,128)(2,1)} %bitcast.68), slice={[0:4], [0:64], [0:768]} | slice | bytes 786432 | tf_op jit(solution)/shard_map/slice | solution.py:144
  7.4 0.6 reshape.98
  8.1 2.7 %collective-permute-start.1 = (bf16[64,768]{1,0:T(8,128)(2,1)S(1)}, bf16[64,768]{1,0:T(8,128)(2,1)S(1)}, u32[]{:S(2)}, u32[]{:S(2)}) collective-permute-start(bf16[64,768]{1,0:T(8,128)(2,1)S(1)} %broadcast_select_fusion), channel_id=1, source_target_pairs={{0,8},{4,12},{8,0},{12,4},{16,24},{20,28},{24,16},{28,20},{1,9},{5... | collective-permute-start | bytes 294920 | tf_op jit(solution)/shard_map/ppermute | solution.py:59
  10.8 0.8 constant_dynamic-update-slice_fusion.3
  11.6 2.6 %collective-permute-done.1 = bf16[64,768]{1,0:T(8,128)(2,1)S(1)} collective-permute-done((bf16[64,768]{1,0:T(8,128)(2,1)S(1)}, bf16[64,768]{1,0:T(8,128)(2,1)S(1)}, u32[]{:S(2)}, u32[]{:S(2)}) %collective-permute-start.1) | collective-permute-done | bytes 98336 | tf_op jit(solution)/shard_map/ppermute | solution.py:59
  14.2 2.8 %collective-permute-start.2 = (bf16[64,768]{1,0:T(8,128)(2,1)S(1)}, bf16[64,768]{1,0:T(8,128)(2,1)S(1)}, u32[]{:S(2)}, u32[]{:S(2)}) collective-permute-start(bf16[64,768]{1,0:T(8,128)(2,1)S(1)} %broadcast_select_fusion.1), channel_id=1, source_target_pairs={{0,16},{4,20},{8,24},{12,28},{16,0},{20,4},{24,8},{28,12},{1,17},{... | collective-permute-start | bytes 294920 | tf_op jit(solution)/shard_map/ppermute | solution.py:59
  17.1 1.5 %collective-permute-start.3 = (bf16[4,64,768]{2,1,0:T(8,128)(2,1)S(1)}, bf16[4,64,768]{2,1,0:T(8,128)(2,1)}, u32[]{:S(2)}, u32[]{:S(2)}) collective-permute-start(bf16[4,64,768]{2,1,0:T(8,128)(2,1)S(1)} %copy-done.4), channel_id=1, source_target_pairs={{0,1},{1,0},{2,3},{3,2},{4,5},{5,4},{6,7},{7,6},{8,9},{9,8},{10,11... | collective-permute-start | bytes 1179656 | tf_op jit(solution)/shard_map/ppermute | solution.py:127
  18.5 1.5 %collective-permute-start.4 = (bf16[4,64,768]{2,1,0:T(8,128)(2,1)S(1)}, bf16[4,64,768]{2,1,0:T(8,128)(2,1)}, u32[]{:S(2)}, u32[]{:S(2)}) collective-permute-start(bf16[4,64,768]{2,1,0:T(8,128)(2,1)S(1)} %copy-done.4), channel_id=1, source_target_pairs={{0,2},{1,3},{2,0},{3,1},{4,6},{5,7},{6,4},{7,5},{8,10},{9,11},{10,... | collective-permute-start | bytes 1179656 | tf_op jit(solution)/shard_map/ppermute | solution.py:127
  20.1 0.5 collective-permute-start.5
  20.5 1.3 %collective-permute-done.2 = bf16[64,768]{1,0:T(8,128)(2,1)S(1)} collective-permute-done((bf16[64,768]{1,0:T(8,128)(2,1)S(1)}, bf16[64,768]{1,0:T(8,128)(2,1)S(1)}, u32[]{:S(2)}, u32[]{:S(2)}) %collective-permute-start.2) | collective-permute-done | bytes 98336 | tf_op jit(solution)/shard_map/ppermute | solution.py:59
  21.9 1.7 %fusion.48 = f32[64,768]{1,0:T(8,128)S(1)} fusion(bf16[64,768]{1,0:T(8,128)(2,1)S(1)} %broadcast_select_fusion.2, bf16[768,2304]{1,0:T(8,128)(2,1)} %param.14), kind=kOutput, calls=%fused_computation.51 | convolution fusion | flops 75595776 | bytes 1474560 | tf_op jit(solution)/shard_map/dot_general | solution.py:34
  23.5 2.2 %fusion.13 = bf16[64,1536]{1,0:T(8,128)(2,1)S(1)} fusion(bf16[64,768]{1,0:T(8,128)(2,1)S(1)} %broadcast_select_fusion.2, bf16[768,2304]{1,0:T(8,128)(2,1)} %param.14), kind=kOutput, calls=%fused_computation.17 | convolution fusion | flops 151093248 | bytes 2654208 | tf_op jit(solution)/shard_map/dot_general | solution.py:34
  25.8 0.6 fusion.136
  26.4 0.3 fusion.38
  26.7 0.2 convolution_multiply_fusion.3
  26.9 0.7 fusion.135
  27.7 0.7 slice_select_fusion
  28.4 1.1 %reshape.100 = bf16[64,12,64]{2,1,0:T(8,128)(2,1)S(1)} reshape(bf16[64,768]{1,0:T(8,128)(2,1)} %get-tuple-element.15) | data formatting | bytes 196608 | tf_op jit(solution)/shard_map/reshape | solution.py:192
  29.5 2.6 %bitcast_reduce_fusion = (f32[4,12,64]{2,0,1:T(4,128)}, f32[12,64,4,64]{3,1,2,0:T(8,128)}) fusion(bf16[4,64,12,64]{3,2,1,0:T(8,128)(2,1)S(1)} %reshape.98, bf16[64,12,64,1]{2,1,0,3:T(8,128)(2,1)S(1)} %bitcast.71), kind=kOutput, calls=%fused_computation.30 | convolution fusion | flops 25555968 | bytes 1290240 | tf_op jit(solution)/shard_map/rqhd,khd->rhqk/dot_general | solution.py:206
  32.2 0.5 collective-permute-start.6
  32.7 0.8 copy.58
  33.6 0.7 collective-permute-start.9
  34.4 0.3 fusion.86
  34.6 2.8 %collective-permute-done.9 = f32[32,24]{0,1:T(8,128)S(1)} collective-permute-done((f32[32,24]{0,1:T(8,128)S(1)}, f32[32,24]{0,1:T(8,128)S(1)}, u32[]{:S(2)}, u32[]{:S(2)}) %collective-permute-start.9) | collective-permute-done | bytes 3104 | tf_op jit(solution)/shard_map/ppermute | solution.py:59
  37.5 2.1 %collective-permute-start.11 = (f32[32,24]{0,1:T(8,128)S(1)}, f32[32,24]{0,1:T(8,128)S(1)}, u32[]{:S(2)}, u32[]{:S(2)}) collective-permute-start(f32[32,24]{0,1:T(8,128)S(1)} %pad_maximum_fusion.2), channel_id=1, source_target_pairs={{0,16},{4,20},{8,24},{12,28},{16,0},{20,4},{24,8},{28,12},{1,17},{... | collective-permute-start | bytes 9224 | tf_op jit(solution)/shard_map/ppermute | solution.py:59
  39.5 0.3 fusion.83
  39.8 2.3 %collective-permute-done.11 = f32[32,24]{0,1:T(8,128)S(1)} collective-permute-done((f32[32,24]{0,1:T(8,128)S(1)}, f32[32,24]{0,1:T(8,128)S(1)}, u32[]{:S(2)}, u32[]{:S(2)}) %collective-permute-start.11) | collective-permute-done | bytes 3104 | tf_op jit(solution)/shard_map/ppermute | solution.py:59
  42.1 0.2 fusion.82
  42.4 0.3 fusion.81
  42.7 0.3 fusion.80
  42.9 0.3 add_convert_fusion
  43.2 1.2 %collective-permute-start.8 = (bf16[32,768]{1,0:T(8,128)(2,1)S(1)}, bf16[32,768]{1,0:T(8,128)(2,1)S(1)}, u32[]{:S(2)}, u32[]{:S(2)}) collective-permute-start(bf16[32,768]{1,0:T(8,128)(2,1)S(1)} %add_convert_fusion), channel_id=1, source_target_pairs={{0,8},{4,12},{8,0},{12,4},{16,24},{20,28},{24,16},{28,20},{1,9},{5... | collective-permute-start | bytes 147464 | tf_op jit(solution)/shard_map/ppermute | solution.py:59
  44.4 0.2 fusion.79
  44.6 2.8 %collective-permute-done.8 = bf16[32,768]{1,0:T(8,128)(2,1)S(1)} collective-permute-done((bf16[32,768]{1,0:T(8,128)(2,1)S(1)}, bf16[32,768]{1,0:T(8,128)(2,1)S(1)}, u32[]{:S(2)}, u32[]{:S(2)}) %collective-permute-start.8) | collective-permute-done | bytes 49184 | tf_op jit(solution)/shard_map/ppermute | solution.py:59
  47.3 0.3 fusion.72
  47.6 2.3 %collective-permute-start.10 = (bf16[32,768]{1,0:T(8,128)(2,1)S(1)}, bf16[32,768]{1,0:T(8,128)(2,1)S(1)}, u32[]{:S(2)}, u32[]{:S(2)}) collective-permute-start(bf16[32,768]{1,0:T(8,128)(2,1)S(1)} %fusion.72), channel_id=1, source_target_pairs={{0,16},{4,20},{8,24},{12,28},{16,0},{20,4},{24,8},{28,12},{1,17},{... | collective-permute-start | bytes 147464 | tf_op jit(solution)/shard_map/ppermute | solution.py:59
  49.9 1.8 %constant_dynamic-update-slice_fusion.2 = bf16[4,256,768]{2,1,0:T(8,128)(2,1)} fusion(bf16[4,256,768]{2,1,0:T(8,128)(2,1)} %constant_dynamic-update-slice_fusion.3, bf16[4,64,768]{2,1,0:T(8,128)(2,1)} %collective-permute-done.3), kind=kLoop, calls=%fused_computation.135 | loop fusion | bytes 786432
  51.7 1.8 %constant_dynamic-update-slice_fusion.1 = bf16[4,256,768]{2,1,0:T(8,128)(2,1)} fusion(bf16[4,256,768]{2,1,0:T(8,128)(2,1)} %constant_dynamic-update-slice_fusion.2, bf16[4,64,768]{2,1,0:T(8,128)(2,1)} %collective-permute-done.4), kind=kLoop, calls=%fused_computation.134 | loop fusion | bytes 786432
  53.5 1.8 %constant_dynamic-update-slice_fusion = bf16[4,256,768]{2,1,0:T(8,128)(2,1)} fusion(bf16[4,256,768]{2,1,0:T(8,128)(2,1)} %constant_dynamic-update-slice_fusion.1, bf16[4,64,768]{2,1,0:T(8,128)(2,1)} %collective-permute-done.5), kind=kLoop, calls=%fused_computation.133 | loop fusion | bytes 786432 | tf_op jit(solution)/shard_map/concatenate | solution.py:179
  55.3 4.1 %fusion.31 = bf16[4,768,256]{1,2,0:T(8,128)(2,1)} fusion(bf16[4,256,768]{2,1,0:T(8,128)(2,1)} %constant_dynamic-update-slice_fusion, bf16[768,2304]{1,0:T(8,128)(2,1)S(1)} %copy-done.7), kind=kOutput, calls=%fused_computation.36 | convolution fusion | flops 1208745984 | bytes 4325376 | tf_op jit(solution)/shard_map/ic,rki->rck/dot_general | solution.py:185
  59.3 2.6 %fusion.32 = bf16[4,768,256]{1,2,0:T(8,128)(2,1)} fusion(bf16[4,256,768]{2,1,0:T(8,128)(2,1)S(1)} %copy-done.10, bf16[768,2304]{1,0:T(8,128)(2,1)S(1)} %copy-done.7), kind=kOutput, calls=%fused_computation.37 | convolution fusion | flops 1208745984 | bytes 4325376 | tf_op jit(solution)/shard_map/ic,rki->rck/dot_general | solution.py:181
  61.9 0.3 fusion.51
  62.3 2.8 %copy.42 = bf16[4,768,256]{2,1,0:T(8,128)(2,1)} copy(bf16[4,768,256]{1,2,0:T(8,128)(2,1)} %fusion.31) | data formatting | bytes 3145728 | tf_op jit(solution)/shard_map/convert_element_type | solution.py:188
  65.0 2.6 %copy.43 = bf16[4,768,256]{2,1,0:T(8,128)(2,1)} copy(bf16[4,768,256]{1,2,0:T(8,128)(2,1)} %fusion.32) | data formatting | bytes 3145728 | tf_op jit(solution)/shard_map/convert_element_type | solution.py:184
  67.6 2.1 %fusion.8 = (f32[4,12,64]{2,1,0:T(8,128)S(1)}, f32[4,12,64,256]{3,2,1,0:T(8,128)S(1)}) fusion(pred[4,64,256]{2,1,0:T(8,128)(4,1)S(1)} %fusion.66, bf16[4,12,64,256]{3,2,1,0:T(8,128)(2,1)} %bitcast.67, bf16[4,64,12,64]{3,2,1,0:T(8,128)(2,1)S(1)} %reshape.98), kind=kOutput, calls=%fused_computation.12 | convolution fusion | flops 103019520 | bytes 5189632 | tf_op jit(solution)/shard_map/rqhd,rhdk->rhqk/dot_general | solution.py:202
  69.8 1.2 %fusion.9 = f32[4,12,64]{2,1,0:T(8,128)S(1)} fusion(f32[4,12,64,256]{3,2,1,0:T(8,128)S(1)} %get-tuple-element.23, f32[4,12,64]{2,1,0:T(8,128)S(1)} %copy_maximum_fusion, pred[4,64,256]{2,1,0:T(8,128)(4,1)S(1)} %fusion.66), kind=kLoop, calls=%fused_computation.13 | loop fusion | flops 3142656 | bytes 3235840 | tf_op jit(solution)/shard_map/reduce_sum | solution.py:211
  71.2 1.1 %fusion.22 = f32[4,12,64,64]{3,2,1,0:T(8,128)S(1)} fusion(bf16[4,12,64,256]{3,2,1,0:T(8,128)(2,1)S(1)} %bitcast.66, f32[4,12,64,256]{3,2,1,0:T(8,128)S(1)} %get-tuple-element.23, f32[4,12,64]{2,1,0:T(8,128)S(1)} %copy_maximum_fusion, pred[4,64,256]{2,1,0:T(8,128)(4,1)S(1)} %fusion.66), kind=kOutput, calls=%fused_computation.25 | convolution fusion | flops 103809024 | bytes 5582848 | tf_op jit(solution)/shard_map/rhqk,rhdk->rqhd/dot_general | solution.py:212
  72.3 0.3 copy-done.1
  72.6 0.4 fusion.33
  73.0 0.2 copy-done.8
  73.3 0.3 fusion.25
  73.6 0.6 copy.52
  74.3 1.2 %convert_element_type.114 = bf16[256,768]{0,1:T(8,128)(2,1)} reshape(bf16[4,64,12,64]{1,0,3,2:T(4,128)(2,1)S(1)} %copy.52) | data formatting | bytes 786432 | tf_op jit(solution)/shard_map/convert_element_type | solution.py:219
  75.5 0.2 copy.53
  75.7 1.7 %fusion.137 = (f32[320]{0:T(512)S(1)}, f32[320,768]{1,0:T(8,128)S(1)}) fusion(bf16[768,768]{1,0:T(8,128)(2,1)S(1)} %copy-done, bf16[64,768]{0,1:T(8,128)(2,1)S(1)} %copy.53, bf16[256,768]{0,1:T(8,128)(2,1)} %convert_element_type.114, bf16[64,768]{1,0:T(8,128)(2,1)S(1)} %copy-done.6, bf16[256,768]{1,0:T(8,128)(2,1)S(1)} %bitcast.73), kind=kOutput, calls=%fused_computation.193 | convolution fusion | flops 379944640 | bytes 3147008 | tf_op jit(solution)/shard_map/dot_general | solution.py:24
  77.4 0.3 multiply_reduce_fusion.1
  77.7 7.4 %fusion.138 = (f32[320]{0:T(512)S(1)}, f32[320,768]{1,0:T(8,128)S(1)}) fusion(bf16[3072,768]{1,0:T(8,128)(2,1)} %param.18, bf16[768,3072]{1,0:T(8,128)(2,1)} %param.17, f32[320,768]{1,0:T(8,128)S(1)} %get-tuple-element.27, f32[768]{0:T(1024)S(1)} %copy-done.14, f32[320]{0:T(512)S(1)} %add_rsqrt_fusion.1, f32[320]{0:T(512)S(1)} %broadcast_multiply_fusion.1), kind=kOutput, calls=%fused_computation.194 | convolution fusion | flops 3031449344 | bytes 11410176 | tf_op jit(solution)/shard_map/dot_general | solution.py:29
  85.2 0.3 multiply_reduce_fusion
  85.4 0.2 multiply_convert_fusion
  85.6 0.8 slice.157
  86.4 0.6 slice.158
  (68 shorter events, 0.8 us)
Async XLA Ops:
  0.6 75.1 %copy-start = (bf16[768,768]{1,0:T(8,128)(2,1)S(1)}, bf16[768,768]{1,0:T(8,128)(2,1)}, u32[]{:S(2)}) copy-start(bf16[768,768]{1,0:T(8,128)(2,1)} %param.15) | copy-start | bytes 3538948
  0.6 7.4 %collective-permute-start = (bf16[64,768]{1,0:T(8,128)(2,1)}, bf16[64,768]{1,0:T(8,128)(2,1)S(1)}, u32[]{:S(2)}, u32[]{:S(2)}) collective-permute-start(bf16[64,768]{1,0:T(8,128)(2,1)} %bitcast.76), channel_id=1, source_target_pairs={{0,4},{4,0},{8,12},{12,8},{16,20},{20,16},{24,28},{28,24},{1,5},{5... | collective-permute-start | bytes 294920 | tf_op jit(solution)/shard_map/ppermute | solution.py:59
  1.2 4.4 %copy-start.13 = (s32[4,64]{1,0:T(4,128)S(1)}, s32[4,64]{1,0:T(4,128)}, u32[]{:S(2)}) copy-start(s32[4,64]{1,0:T(4,128)} %param.13) | copy-start | bytes 3076
  5.4 2.6 %copy-start.11 = (bf16[1,64,768]{2,1,0:T(8,128)(2,1)S(1)}, bf16[1,64,768]{2,1,0:T(8,128)(2,1)}, u32[]{:S(2)}) copy-start(bf16[1,64,768]{2,1,0:T(8,128)(2,1)} %param.11) | copy-start | bytes 294916
  5.4 5.4 %copy-start.4 = (bf16[4,64,768]{2,1,0:T(8,128)(2,1)S(1)}, bf16[4,64,768]{2,1,0:T(8,128)(2,1)}, u32[]{:S(2)}) copy-start(bf16[4,64,768]{2,1,0:T(8,128)(2,1)} %param.10) | copy-start | bytes 1179652
  8.1 6.1 %collective-permute-start.1 = (bf16[64,768]{1,0:T(8,128)(2,1)S(1)}, bf16[64,768]{1,0:T(8,128)(2,1)S(1)}, u32[]{:S(2)}, u32[]{:S(2)}) collective-permute-start(bf16[64,768]{1,0:T(8,128)(2,1)S(1)} %broadcast_select_fusion), channel_id=1, source_target_pairs={{0,8},{4,12},{8,0},{12,4},{16,24},{20,28},{24,16},{28,20},{1,9},{5... | collective-permute-start | bytes 294920 | tf_op jit(solution)/shard_map/ppermute | solution.py:59
  14.2 7.6 %collective-permute-start.2 = (bf16[64,768]{1,0:T(8,128)(2,1)S(1)}, bf16[64,768]{1,0:T(8,128)(2,1)S(1)}, u32[]{:S(2)}, u32[]{:S(2)}) collective-permute-start(bf16[64,768]{1,0:T(8,128)(2,1)S(1)} %broadcast_select_fusion.1), channel_id=1, source_target_pairs={{0,16},{4,20},{8,24},{12,28},{16,0},{20,4},{24,8},{28,12},{1,17},{... | collective-permute-start | bytes 294920 | tf_op jit(solution)/shard_map/ppermute | solution.py:59
  17.1 32.9 %collective-permute-start.3 = (bf16[4,64,768]{2,1,0:T(8,128)(2,1)S(1)}, bf16[4,64,768]{2,1,0:T(8,128)(2,1)}, u32[]{:S(2)}, u32[]{:S(2)}) collective-permute-start(bf16[4,64,768]{2,1,0:T(8,128)(2,1)S(1)} %copy-done.4), channel_id=1, source_target_pairs={{0,1},{1,0},{2,3},{3,2},{4,5},{5,4},{6,7},{7,6},{8,9},{9,8},{10,11... | collective-permute-start | bytes 1179656 | tf_op jit(solution)/shard_map/ppermute | solution.py:127
  18.5 33.1 %collective-permute-start.4 = (bf16[4,64,768]{2,1,0:T(8,128)(2,1)S(1)}, bf16[4,64,768]{2,1,0:T(8,128)(2,1)}, u32[]{:S(2)}, u32[]{:S(2)}) collective-permute-start(bf16[4,64,768]{2,1,0:T(8,128)(2,1)S(1)} %copy-done.4), channel_id=1, source_target_pairs={{0,2},{1,3},{2,0},{3,1},{4,6},{5,7},{6,4},{7,5},{8,10},{9,11},{10,... | collective-permute-start | bytes 1179656 | tf_op jit(solution)/shard_map/ppermute | solution.py:127
  20.1 33.4 %collective-permute-start.5 = (bf16[4,64,768]{2,1,0:T(8,128)(2,1)S(1)}, bf16[4,64,768]{2,1,0:T(8,128)(2,1)}, u32[]{:S(2)}, u32[]{:S(2)}) collective-permute-start(bf16[4,64,768]{2,1,0:T(8,128)(2,1)S(1)} %copy-done.4), channel_id=1, source_target_pairs={{0,3},{1,2},{2,1},{3,0},{4,7},{5,6},{6,5},{7,4},{8,11},{9,10},{10,... | collective-permute-start | bytes 1179656 | tf_op jit(solution)/shard_map/ppermute | solution.py:127
  21.8 3.9 %copy-start.5 = (bf16[64,768]{1,0:T(8,128)(2,1)}, bf16[64,768]{1,0:T(8,128)(2,1)S(1)}, u32[]{:S(2)}) copy-start(bf16[64,768]{1,0:T(8,128)(2,1)S(1)} %broadcast_select_fusion.2) | copy-start | bytes 294916
  21.8 3.9 %copy-start.3 = (bf16[256,2304]{1,0:T(8,128)(2,1)S(1)}, bf16[256,2304]{1,0:T(8,128)(2,1)}, u32[]{:S(2)}) copy-start(bf16[256,2304]{1,0:T(8,128)(2,1)} %convolution_convert_fusion) | copy-start | bytes 3538948
  27.7 5.8 %collective-permute-start.7 = (f32[32,24]{0,1:T(8,128)S(1)}, f32[32,24]{0,1:T(8,128)S(1)}, u32[]{:S(2)}, u32[]{:S(2)}) collective-permute-start(f32[32,24]{0,1:T(8,128)S(1)} %fusion.116), channel_id=1, source_target_pairs={{0,4},{4,0},{8,12},{12,8},{16,20},{20,16},{24,28},{28,24},{1,5},{5... | collective-permute-start | bytes 9224 | tf_op jit(solution)/shard_map/ppermute | solution.py:59
  32.2 10.7 %collective-permute-start.6 = (f32[32,768]{1,0:T(8,128)}, f32[32,768]{1,0:T(8,128)S(1)}, u32[]{:S(2)}, u32[]{:S(2)}) collective-permute-start(f32[32,768]{1,0:T(8,128)} %slice_select_fusion), channel_id=1, source_target_pairs={{0,4},{4,0},{8,12},{12,8},{16,20},{20,16},{24,28},{28,24},{1,5},{5... | collective-permute-start | bytes 294920 | tf_op jit(solution)/shard_map/ppermute | solution.py:59
  33.6 21.6 %copy-start.7 = (bf16[768,2304]{1,0:T(8,128)(2,1)S(1)}, bf16[768,2304]{1,0:T(8,128)(2,1)}, u32[]{:S(2)}) copy-start(bf16[768,2304]{1,0:T(8,128)(2,1)} %param.14) | copy-start | bytes 10616836
  33.6 3.8 %collective-permute-start.9 = (f32[32,24]{0,1:T(8,128)S(1)}, f32[32,24]{0,1:T(8,128)S(1)}, u32[]{:S(2)}, u32[]{:S(2)}) collective-permute-start(f32[32,24]{0,1:T(8,128)S(1)} %pad_maximum_fusion.1), channel_id=1, source_target_pairs={{0,8},{4,12},{8,0},{12,4},{16,24},{20,28},{24,16},{28,20},{1,9},{5... | collective-permute-start | bytes 9224 | tf_op jit(solution)/shard_map/ppermute | solution.py:59
  37.5 4.7 %collective-permute-start.11 = (f32[32,24]{0,1:T(8,128)S(1)}, f32[32,24]{0,1:T(8,128)S(1)}, u32[]{:S(2)}, u32[]{:S(2)}) collective-permute-start(f32[32,24]{0,1:T(8,128)S(1)} %pad_maximum_fusion.2), channel_id=1, source_target_pairs={{0,16},{4,20},{8,24},{12,28},{16,0},{20,4},{24,8},{28,12},{1,17},{... | collective-permute-start | bytes 9224 | tf_op jit(solution)/shard_map/ppermute | solution.py:59
  43.2 4.2 %collective-permute-start.8 = (bf16[32,768]{1,0:T(8,128)(2,1)S(1)}, bf16[32,768]{1,0:T(8,128)(2,1)S(1)}, u32[]{:S(2)}, u32[]{:S(2)}) collective-permute-start(bf16[32,768]{1,0:T(8,128)(2,1)S(1)} %add_convert_fusion), channel_id=1, source_target_pairs={{0,8},{4,12},{8,0},{12,4},{16,24},{20,28},{24,16},{28,20},{1,9},{5... | collective-permute-start | bytes 147464 | tf_op jit(solution)/shard_map/ppermute | solution.py:59
  47.6 14.3 %collective-permute-start.10 = (bf16[32,768]{1,0:T(8,128)(2,1)S(1)}, bf16[32,768]{1,0:T(8,128)(2,1)S(1)}, u32[]{:S(2)}, u32[]{:S(2)}) collective-permute-start(bf16[32,768]{1,0:T(8,128)(2,1)S(1)} %fusion.72), channel_id=1, source_target_pairs={{0,16},{4,20},{8,24},{12,28},{16,0},{20,4},{24,8},{28,12},{1,17},{... | collective-permute-start | bytes 147464 | tf_op jit(solution)/shard_map/ppermute | solution.py:59
  55.3 4.1 %copy-start.10 = (bf16[4,256,768]{2,1,0:T(8,128)(2,1)S(1)}, bf16[4,256,768]{2,1,0:T(8,128)(2,1)}, u32[]{:S(2)}) copy-start(bf16[4,256,768]{2,1,0:T(8,128)(2,1)} %constant_dynamic-update-slice_fusion) | copy-start | bytes 4718596
  62.2 13.3 %collective-permute-start.12 = (bf16[32,768]{1,0:T(8,128)(2,1)S(1)}, bf16[32,768]{1,0:T(8,128)(2,1)S(1)}, u32[]{:S(2)}, u32[]{:S(2)}) collective-permute-start(bf16[32,768]{1,0:T(8,128)(2,1)S(1)} %fusion.51), channel_id=1, source_target_pairs={{0,4},{4,0},{8,12},{12,8},{16,20},{20,16},{24,28},{28,24},{1,5},{5... | collective-permute-start | bytes 147464 | tf_op jit(solution)/shard_map/ppermute | solution.py:59
  67.6 2.2 %copy-start.9 = (f32[4,12,64]{2,0,1:T(4,128)S(1)}, f32[4,12,64]{2,0,1:T(4,128)}, u32[]{:S(2)}) copy-start(f32[4,12,64]{2,0,1:T(4,128)} %get-tuple-element.24) | copy-start | bytes 36868
  69.8 1.4 %copy-start.2 = (bf16[4,768,256]{2,1,0:T(8,128)(2,1)S(1)}, bf16[4,768,256]{2,1,0:T(8,128)(2,1)}, u32[]{:S(2)}) copy-start(bf16[4,768,256]{2,1,0:T(8,128)(2,1)} %copy.42) | copy-start | bytes 4718596
  71.2 1.4 %copy-start.1 = (f32[12,64,4,64]{3,1,2,0:T(8,128)S(1)}, f32[12,64,4,64]{3,1,2,0:T(8,128)}, u32[]{:S(2)}) copy-start(f32[12,64,4,64]{3,1,2,0:T(8,128)} %get-tuple-element.25) | copy-start | bytes 2359300
  72.3 1.0 %copy-start.8 = (bf16[64,768]{0,1:T(8,128)(2,1)S(1)}, bf16[64,768]{0,1:T(8,128)(2,1)}, u32[]{:S(2)}) copy-start(bf16[64,768]{0,1:T(8,128)(2,1)} %copy.58) | copy-start | bytes 294916
  73.6 2.1 %copy-start.6 = (bf16[64,768]{1,0:T(8,128)(2,1)S(1)}, bf16[64,768]{1,0:T(8,128)(2,1)}, u32[]{:S(2)}) copy-start(bf16[64,768]{1,0:T(8,128)(2,1)} %copy-done.5) | copy-start | bytes 294916
  75.7 2.0 %copy-start.14 = (f32[768]{0:T(1024)S(1)}, f32[768]{0:T(1024)}, u32[]{:S(2)}) copy-start(f32[768]{0:T(1024)} %param.16) | copy-start | bytes 9220
  77.7 7.7 %copy-start.12 = (f32[768]{0:T(1024)S(1)}, f32[768]{0:T(1024)}, u32[]{:S(2)}) copy-start(f32[768]{0:T(1024)} %param.19) | copy-start | bytes 9220

commit v11 on v9

--- a/solution.py
+++ b/solution.py
@@ -61,14 +61,15 @@
 
 def broadcast_from(value, axis, count, source, held):
     here = lax.axis_index(axis)
-    step = 1
-    while step < count:
-        got = partner(value, axis, step, count)
-        if step == 1:
-            got, held = lax.optimization_barrier((got, held))
-        value = jnp.where(here // step == source // step, value, got)
-        step *= 2
-    return value, held
+    got = partner(value, axis, 1, count)
+    got, held = lax.optimization_barrier((got, held))
+    value = jnp.where(here == source, value, got)
+    chip = here // 2
+    result = value
+    for step in range(1, count // 2):
+        got = partner(value, axis, 2 * step, count)
+        result = jnp.where((chip ^ step) == source // 2, got, result)
+    return result, held
 
 
 def merge(lo, hi):
@@ -94,18 +95,23 @@
     sent = pick(first, low_half, top_half)
     got = tuple(partner(v, axis, 1, count) for v in sent)
     value = merge(pick(first, mine, got), pick(first, got, mine))
-    step = 2
-    while step < count:
-        mixed = value[0].astype(jnp.bfloat16)
-        got = (
-            partner(mixed, axis, step, count).astype(jnp.float32),
-            partner(value[1], axis, step, count),
-        )
-        mine = (mixed.astype(jnp.float32), value[1])
-        low_side = (here & step) == 0
-        value = merge(pick(low_side, mine, got), pick(low_side, got, mine))
-        step *= 2
-    return value
+    chip = here // 2
+    mine = (value[0].astype(jnp.bfloat16).astype(jnp.float32), value[1])
+    got = []
+    for step in range(1, count // 2):
+        got.append((
+            partner(value[0].astype(jnp.bfloat16), axis, 2 * step, count).astype(jnp.float32),
+            partner(value[1], axis, 2 * step, count),
+        ))
+    parts = []
+    for c in range(count // 2):
+        part = mine
+        for step in range(1, count // 2):
+            part = pick((chip ^ step) == c, got[step - 1], part)
+        parts.append(part)
+    while len(parts) > 1:
+        parts = [merge(parts[i], parts[i + 1]) for i in range(0, len(parts), 2)]
+    return parts[0]
 
 
 def join_halves(value, axis, count):

time: 80.6 us -> 84.4 us (1.047)
  starting transfers between devices: 15.8 us -> 19.5 us
    ppermute x10 -> x13, waiting for transfers between devices: 13.7 us -> 9.83 us  [partner(): return lax.ppermute(value, axis, [(i, i ^ step) for i in range(count)])]
    ppermute x3, waiting for transfers between devices: 0.01 us -> 3.65 us  [fan_out(): got.append((source, lax.ppermute(value, axis, pairs)))]
    ppermute x10 -> x13, starting transfers between devices: 12.4 us -> 14.9 us  [partner(): return lax.ppermute(value, axis, [(i, i ^ step) for i in range(count)])]
    ppermute x3, starting transfers between devices: 3.49 us -> 4.6 us  [fan_out(): got.append((source, lax.ppermute(value, axis, pairs)))]
    dot_general x10 -> x12, matrix products: 3.36 us -> 4.07 us  [head_spread(): jnp.dot(flat, head_matrix(), precision=lax.Precision.HIGHEST, preferred_e...]
  transfers between devices with their start and end apart: 13 -> 16, of which waited for: 6 -> 6; matrix products, arithmetic and copies ran while one was open for 43% -> 20% of each run, Pallas kernels for 0% -> 0%
where the time goes in v11:
time: 84.4 us; the launch traced here: 83.9 us
  matrix products  28.9 us (34%)
  starting transfers between devices  19.5 us (23%)
  waiting for transfers between devices  13.5 us (16%)
  local copies, waits for them, and re-layouts  13 us (15%)
  other arithmetic  7.17 us (8%)
  between operations  1.81 us (2%)
    ppermute x13, starting transfers between devices, partner(): return lax.ppermute(value, axis, [(i, i ^ step) for i in range(count)])  14.9 us
    ppermute x13, waiting for transfers between devices, partner(): return lax.ppermute(value, axis, [(i, i ^ step) for i in range(count)])  9.83 us
    dot_general x4, matrix products, project(): jnp.dot(values, weight, preferred_element_type=jnp.float32)  9.04 us
    dot_general x1, matrix products, finish(): outer_out = jnp.dot(inner_act, w_down, preferred_element_type=jnp.float32)  7.43 us
    ppermute x3, starting transfers between devices, fan_out(): got.append((source, lax.ppermute(value, axis, pairs)))  4.6 us
    dot_general x12, matrix products, head_spread(): jnp.dot(flat, head_matrix(), precision=lax.Precision.HIGHEST, preferred_e...  4.07 us
    ppermute x3, waiting for transfers between devices, fan_out(): got.append((source, lax.ppermute(value, axis, pairs)))  3.65 us
    concatenate x1, local copies, waits for them, and re-layouts, local(): row_keys = jnp.concatenate([own_keys, other_kv[:, :, :model_width]], axis=1)  2.58 us
  transfers between devices with their start and end apart: 16, of which 6 were waited for; matrix products, arithmetic and copies ran while one was open for 20% of the time, Pallas kernels for 0%

profile of v11, /device:TPU:0, one launch (start us, length us, event | category | flops | bytes accessed | tf_op | source)
XLA Modules:
  0.0 83.9 jit_solution(17568897215288274737)
XLA Ops:
  0.6 0.5 collective-permute-start
  1.2 3.2 %convolution_convert_fusion = bf16[256,2304]{1,0:T(8,128)(2,1)S(1)} fusion(bf16[256,768]{1,0:T(8,128)(2,1)} %bitcast.68, bf16[768,2304]{1,0:T(8,128)(2,1)} %param.14), kind=kOutput, calls=%fused_computation.9 | convolution fusion | flops 906559488 | bytes 5111808 | tf_op jit(solution)/shard_map/dot_general | solution.py:34
  4.4 1.0 %fusion.140 = (bf16[4,64,768]{2,1,0:T(8,128)(2,1)}, bf16[4,64,768]{2,1,0:T(8,128)(2,1)}, bf16[4,64,768]{2,1,0:T(8,128)(2,1)}) fusion(bf16[4,64,2304]{2,1,0:T(8,128)(2,1)S(1)} %bitcast.59), kind=kLoop, calls=%fused_computation.205 | loop fusion | bytes 2359296 | tf_op jit(solution)/shard_map/slice | solution.py:150
  5.5 0.1 fusion.57
  6.4 1.7 %reshape.106 = bf16[4,64,12,64]{3,2,1,0:T(8,128)(2,1)S(1)} reshape(bf16[4,64,768]{2,1,0:T(8,128)(2,1)} %get-tuple-element.14) | data formatting | bytes 786432 | tf_op jit(solution)/shard_map/reshape | solution.py:192
  8.1 1.1 %broadcast_select_fusion = bf16[64,768]{1,0:T(8,128)(2,1)S(1)} fusion(bf16[64,768]{1,0:T(8,128)(2,1)} %collective-permute-done, pred[]{:T(512)S(6)} %eq.243, bf16[1,64,768]{2,1,0:T(8,128)(2,1)} %param.11), kind=kLoop, calls=%fused_computation.99 | loop fusion | flops 49152 | bytes 294913 | tf_op jit(solution)/shard_map/jit(_where)/select_n | solution.py:66
  9.2 4.7 %collective-permute-start.1 = (bf16[64,768]{1,0:T(8,128)(2,1)S(1)}, bf16[64,768]{1,0:T(8,128)(2,1)S(1)}, u32[]{:S(2)}, u32[]{:S(2)}) collective-permute-start(bf16[64,768]{1,0:T(8,128)(2,1)S(1)} %broadcast_select_fusion), channel_id=1, source_target_pairs={{0,24},{4,28},{8,16},{12,20},{16,8},{20,12},{24,0},{28,4},{1,25},{... | collective-permute-start | bytes 294920 | tf_op jit(solution)/shard_map/ppermute | solution.py:59
  14.0 0.6 collective-permute-start.3
  14.6 2.6 %collective-permute-start.6 = (bf16[4,64,768]{2,1,0:T(8,128)(2,1)}, bf16[4,64,768]{2,1,0:T(8,128)(2,1)}, u32[]{:S(2)}, u32[]{:S(2)}) collective-permute-start(bf16[4,64,768]{2,1,0:T(8,128)(2,1)} %param.10), channel_id=1, source_target_pairs={{0,3},{1,2},{2,1},{3,0},{4,7},{5,6},{6,5},{7,4},{8,11},{9,10},{10,... | collective-permute-start | bytes 1179656 | tf_op jit(solution)/shard_map/ppermute | solution.py:133
  17.2 0.5 collective-permute-start.5
  17.7 5.1 %collective-permute-done.2 = bf16[64,768]{1,0:T(8,128)(2,1)S(1)} collective-permute-done((bf16[64,768]{1,0:T(8,128)(2,1)S(1)}, bf16[64,768]{1,0:T(8,128)(2,1)S(1)}, u32[]{:S(2)}, u32[]{:S(2)}) %collective-permute-start.2) | collective-permute-done | bytes 98336 | tf_op jit(solution)/shard_map/ppermute | solution.py:59
  22.9 1.6 %fusion.39 = f32[64,768]{1,0:T(8,128)S(1)} fusion(bf16[64,768]{1,0:T(8,128)(2,1)S(1)} %select_select_fusion, bf16[768,2304]{1,0:T(8,128)(2,1)} %param.14), kind=kOutput, calls=%fused_computation.47 | convolution fusion | flops 75595776 | bytes 1474560 | tf_op jit(solution)/shard_map/dot_general | solution.py:34
  24.5 0.6 fusion.142
  25.2 0.3 fusion.33
  25.5 0.5 convolution_convert_fusion.2
  26.0 0.2 convolution_multiply_fusion.4
  26.5 0.2 reshape.108
  26.7 0.9 %collective-permute-done.8 = f32[32,24]{0,1:T(8,128)S(1)} collective-permute-done((f32[32,24]{0,1:T(8,128)S(1)}, f32[32,24]{0,1:T(8,128)S(1)}, u32[]{:S(2)}, u32[]{:S(2)}) %collective-permute-start.8) | collective-permute-done | bytes 3104 | tf_op jit(solution)/shard_map/ppermute | solution.py:59
  27.7 2.5 %collective-permute-start.12 = (f32[32,24]{0,1:T(8,128)S(1)}, f32[32,24]{0,1:T(8,128)S(1)}, u32[]{:S(2)}, u32[]{:S(2)}) collective-permute-start(f32[32,24]{0,1:T(8,128)S(1)} %pad_maximum_fusion.4), channel_id=1, source_target_pairs={{0,24},{4,28},{8,16},{12,20},{16,8},{20,12},{24,0},{28,4},{1,25},{... | collective-permute-start | bytes 9224 | tf_op jit(solution)/shard_map/ppermute | solution.py:59
  30.2 1.9 %collective-permute-start.14 = (f32[32,24]{0,1:T(8,128)S(1)}, f32[32,24]{0,1:T(8,128)S(1)}, u32[]{:S(2)}, u32[]{:S(2)}) collective-permute-start(f32[32,24]{0,1:T(8,128)S(1)} %pad_maximum_fusion.4), channel_id=1, source_target_pairs={{0,8},{4,12},{8,0},{12,4},{16,24},{20,28},{24,16},{28,20},{1,9},{5... | collective-permute-start | bytes 9224 | tf_op jit(solution)/shard_map/ppermute | solution.py:59
  32.1 0.2 fusion.78
  32.4 0.8 %collective-permute-done.12 = f32[32,24]{0,1:T(8,128)S(1)} collective-permute-done((f32[32,24]{0,1:T(8,128)S(1)}, f32[32,24]{0,1:T(8,128)S(1)}, u32[]{:S(2)}, u32[]{:S(2)}) %collective-permute-start.12) | collective-permute-done | bytes 3104 | tf_op jit(solution)/shard_map/ppermute | solution.py:59
  33.2 1.6 %collective-permute-done.13 = f32[32,24]{0,1:T(8,128)S(1)} collective-permute-done((f32[32,24]{0,1:T(8,128)S(1)}, f32[32,24]{0,1:T(8,128)S(1)}, u32[]{:S(2)}, u32[]{:S(2)}) %collective-permute-start.13) | collective-permute-done | bytes 3104 | tf_op jit(solution)/shard_map/ppermute | solution.py:59
  34.8 0.3 fusion.76
  35.1 0.3 fusion.75
  35.4 0.3 fusion.74
  35.6 0.3 fusion.71
  35.9 0.2 fusion.70
  36.1 0.3 fusion.73
  36.4 1.2 %add_convert_fusion = bf16[32,768]{1,0:T(8,128)(2,1)S(1)} fusion(f32[32,768]{1,0:T(8,128)S(1)} %collective-permute-done.7, f32[32,768]{1,0:T(8,128)S(1)} %fusion.78, f32[64,768]{1,0:T(8,128)} %copy-done.5, pred[]{:T(512)S(6)} %eq.247, s32[768]{0:T(1024)S(1)} %add_select_fusion, f32[32,12]{0,1:T(8,128)S(1)} %get-tuple-element.7, ...), kind=kOutput, calls=%fused_computation.97 | convolution fusion | flops 3720576 | bytes 462849 | tf_op jit(solution)/shard_map/dot_general | solution.py:53
  37.6 1.6 %collective-permute-start.9 = (bf16[32,768]{1,0:T(8,128)(2,1)S(1)}, bf16[32,768]{1,0:T(8,128)(2,1)S(1)}, u32[]{:S(2)}, u32[]{:S(2)}) collective-permute-start(bf16[32,768]{1,0:T(8,128)(2,1)S(1)} %add_convert_fusion), channel_id=1, source_target_pairs={{0,24},{4,28},{8,16},{12,20},{16,8},{20,12},{24,0},{28,4},{1,25},{... | collective-permute-start | bytes 147464 | tf_op jit(solution)/shard_map/ppermute | solution.py:59
  39.1 1.0 %collective-permute-start.10 = (bf16[32,768]{1,0:T(8,128)(2,1)S(1)}, bf16[32,768]{1,0:T(8,128)(2,1)S(1)}, u32[]{:S(2)}, u32[]{:S(2)}) collective-permute-start(bf16[32,768]{1,0:T(8,128)(2,1)S(1)} %add_convert_fusion), channel_id=1, source_target_pairs={{0,16},{4,20},{8,24},{12,28},{16,0},{20,4},{24,8},{28,12},{1,17},{... | collective-permute-start | bytes 147464 | tf_op jit(solution)/shard_map/ppermute | solution.py:59
  40.1 1.9 %collective-permute-start.11 = (bf16[32,768]{1,0:T(8,128)(2,1)S(1)}, bf16[32,768]{1,0:T(8,128)(2,1)S(1)}, u32[]{:S(2)}, u32[]{:S(2)}) collective-permute-start(bf16[32,768]{1,0:T(8,128)(2,1)S(1)} %add_convert_fusion), channel_id=1, source_target_pairs={{0,8},{4,12},{8,0},{12,4},{16,24},{20,28},{24,16},{28,20},{1,9},{5... | collective-permute-start | bytes 147464 | tf_op jit(solution)/shard_map/ppermute | solution.py:59
  42.0 0.3 fusion.72
  42.3 1.4 %collective-permute-done.9 = bf16[32,768]{1,0:T(8,128)(2,1)S(1)} collective-permute-done((bf16[32,768]{1,0:T(8,128)(2,1)S(1)}, bf16[32,768]{1,0:T(8,128)(2,1)S(1)}, u32[]{:S(2)}, u32[]{:S(2)}) %collective-permute-start.9) | collective-permute-done | bytes 49184 | tf_op jit(solution)/shard_map/ppermute | solution.py:59
  43.7 1.5 %collective-permute-start.4 = (bf16[4,64,768]{2,1,0:T(8,128)(2,1)}, bf16[4,64,768]{2,1,0:T(8,128)(2,1)S(1)}, u32[]{:S(2)}, u32[]{:S(2)}) collective-permute-start(bf16[4,64,768]{2,1,0:T(8,128)(2,1)} %param.10), channel_id=1, source_target_pairs={{0,1},{1,0},{2,3},{3,2},{4,5},{5,4},{6,7},{7,6},{8,9},{9,8},{10,11... | collective-permute-start | bytes 1179656 | tf_op jit(solution)/shard_map/ppermute | solution.py:133
  45.2 0.3 fusion.42
  45.5 0.3 fusion.43
  45.8 2.0 %bitcast_reduce_fusion = (f32[4,12,64]{2,0,1:T(4,128)S(1)}, f32[12,64,4,64]{3,1,2,0:T(8,128)}) fusion(bf16[4,64,12,64]{3,2,1,0:T(8,128)(2,1)S(1)} %reshape.106, bf16[64,12,64,1]{2,1,0,3:T(8,128)(2,1)S(1)} %bitcast.64), kind=kOutput, calls=%fused_computation.31 | convolution fusion | flops 25555968 | bytes 1290240 | tf_op jit(solution)/shard_map/rqhd,khd->rhqk/dot_general | solution.py:209
  47.9 0.2 copy.58
  48.1 0.8 copy.53
  48.9 3.6 %collective-permute-done.4 = bf16[4,64,768]{2,1,0:T(8,128)(2,1)S(1)} collective-permute-done((bf16[4,64,768]{2,1,0:T(8,128)(2,1)}, bf16[4,64,768]{2,1,0:T(8,128)(2,1)S(1)}, u32[]{:S(2)}, u32[]{:S(2)}) %collective-permute-start.4) | collective-permute-done | bytes 393248 | tf_op jit(solution)/shard_map/ppermute | solution.py:133
  52.6 1.2 %pad_maximum_fusion.2 = bf16[4,192,768]{2,1,0:T(8,128)(2,1)S(1)} fusion(bf16[4,64,768]{2,1,0:T(8,128)(2,1)} %collective-permute-done.6, bf16[4,64,768]{2,1,0:T(8,128)(2,1)} %collective-permute-done.5, bf16[4,64,768]{2,1,0:T(8,128)(2,1)S(1)} %collective-permute-done.4), kind=kLoop, calls=%fused_computation.43 | loop fusion | flops 3538944 | bytes 2359296 | tf_op jit(solution)/shard_map/concatenate | solution.py:185
  53.8 3.6 %convolution_convert_fusion.1 = bf16[768,1536]{1,0:T(8,128)(2,1)S(1)} fusion(bf16[768,768]{1,0:T(8,128)(2,1)S(1)} %bitcast.63, bf16[768,2304]{1,0:T(8,128)(2,1)} %param.14), kind=kOutput, calls=%fused_computation.10 | convolution fusion | flops 1813118976 | bytes 5898240 | tf_op jit(solution)/shard_map/dot_general | solution.py:34
  57.4 0.2 fusion.139
  57.6 0.8 copy-done.3
  58.5 1.9 %pad_maximum_fusion = (bf16[4,256,768]{2,1,0:T(8,128)(2,1)}, bf16[4,256,768]{2,1,0:T(8,128)(2,1)}) fusion(bf16[4,192,768]{2,1,0:T(8,128)(2,1)S(1)} %get-tuple-element.11, bf16[4,64,768]{2,1,0:T(8,128)(2,1)S(1)} %copy-done.4, bf16[4,192,768]{2,1,0:T(8,128)(2,1)S(1)} %get-tuple-element.10, bf16[4,64,768]{2,1,0:T(8,128)(2,1)S(1)} %copy-done.3), kind=kLoop, calls=%fused_computation.25 | loop fusion | flops 6291456 | bytes 6291456 | tf_op jit(solution)/shard_map/concatenate | solution.py:190
  60.4 2.6 %copy.42 = bf16[4,256,768]{1,2,0:T(8,128)(2,1)} copy(bf16[4,256,768]{2,1,0:T(8,128)(2,1)} %get-tuple-element.35) | data formatting | bytes 3145728 | tf_op jit(solution)/shard_map/concatenate | solution.py:190
  63.0 2.6 %copy.43 = bf16[4,256,768]{1,2,0:T(8,128)(2,1)} copy(bf16[4,256,768]{2,1,0:T(8,128)(2,1)} %get-tuple-element.36) | data formatting | bytes 3145728 | tf_op jit(solution)/shard_map/concatenate | solution.py:189
  65.6 2.1 %fusion.8 = (f32[4,12,64]{2,1,0:T(8,128)S(1)}, f32[4,12,64,256]{3,2,1,0:T(8,128)S(1)}) fusion(pred[4,64,256]{2,1,0:T(8,128)(4,1)S(1)} %fusion.57, bf16[4,256,12,64]{1,3,2,0:T(8,128)(2,1)} %bitcast.58, bf16[4,64,12,64]{3,2,1,0:T(8,128)(2,1)S(1)} %reshape.106), kind=kOutput, calls=%fused_computation.13 | convolution fusion | flops 103019520 | bytes 5189632 | tf_op jit(solution)/shard_map/rqhd,rkhd->rhqk/dot_general | solution.py:205
  67.7 1.2 %fusion.9 = f32[4,12,64]{2,1,0:T(8,128)S(1)} fusion(f32[4,12,64,256]{3,2,1,0:T(8,128)S(1)} %get-tuple-element.26, f32[4,12,64]{2,1,0:T(8,128)S(1)} %copy_maximum_fusion, pred[4,64,256]{2,1,0:T(8,128)(4,1)S(1)} %fusion.57), kind=kLoop, calls=%fused_computation.14 | loop fusion | flops 3142656 | bytes 3235840 | tf_op jit(solution)/shard_map/reduce_sum | solution.py:214
  69.0 0.1 copy-done.2
  69.1 1.3 %fusion.19 = f32[4,12,64,64]{3,2,1,0:T(8,128)S(1)} fusion(bf16[4,256,12,64]{1,3,2,0:T(8,128)(2,1)S(1)} %bitcast.57, f32[4,12,64,256]{3,2,1,0:T(8,128)S(1)} %get-tuple-element.26, f32[4,12,64]{2,1,0:T(8,128)S(1)} %copy_maximum_fusion, pred[4,64,256]{2,1,0:T(8,128)(4,1)S(1)} %fusion.57), kind=kOutput, calls=%fused_computation.24 | convolution fusion | flops 103809024 | bytes 5582848 | tf_op jit(solution)/shard_map/rhqk,rkhd->rqhd/dot_general | solution.py:215
  70.5 0.4 fusion.28
  71.0 0.4 fusion.22
  71.3 0.6 copy.52
  72.0 0.5 convert_element_type.104
  72.5 1.8 %fusion.143 = (f32[320]{0:T(512)S(1)}, f32[320,768]{1,0:T(8,128)S(1)}) fusion(bf16[768,768]{1,0:T(8,128)(2,1)S(1)} %copy-done, bf16[64,768]{0,1:T(8,128)(2,1)} %copy.53, bf16[256,768]{0,1:T(8,128)(2,1)S(1)} %convert_element_type.104, bf16[64,768]{1,0:T(8,128)(2,1)S(1)} %copy-done.7, bf16[256,768]{1,0:T(8,128)(2,1)} %bitcast.69), kind=kOutput, calls=%fused_computation.208 | convolution fusion | flops 379944640 | bytes 3147008 | tf_op jit(solution)/shard_map/dot_general | solution.py:24
  74.3 0.3 multiply_reduce_fusion.1
  74.6 7.4 %fusion.144 = (f32[320]{0:T(512)S(1)}, f32[320,768]{1,0:T(8,128)S(1)}) fusion(bf16[3072,768]{1,0:T(8,128)(2,1)} %param.18, bf16[768,3072]{1,0:T(8,128)(2,1)} %param.17, f32[320,768]{1,0:T(8,128)S(1)} %get-tuple-element.30, f32[768]{0:T(1024)S(1)} %copy-done.11, f32[320]{0:T(512)S(1)} %add_rsqrt_fusion.1, f32[320]{0:T(512)S(1)} %broadcast_multiply_fusion.1), kind=kOutput, calls=%fused_computation.209 | convolution fusion | flops 3031449344 | bytes 11410176 | tf_op jit(solution)/shard_map/dot_general | solution.py:29
  82.0 0.3 multiply_reduce_fusion
  82.3 0.2 multiply_convert_fusion
  82.5 0.8 slice.159
  83.3 0.6 slice.160
  (64 shorter events, 1.0 us)
Async XLA Ops:
  0.6 71.8 %copy-start = (bf16[768,768]{1,0:T(8,128)(2,1)S(1)}, bf16[768,768]{1,0:T(8,128)(2,1)}, u32[]{:S(2)}) copy-start(bf16[768,768]{1,0:T(8,128)(2,1)} %param.15) | copy-start | bytes 3538948
  0.6 7.4 %collective-permute-start = (bf16[64,768]{1,0:T(8,128)(2,1)}, bf16[64,768]{1,0:T(8,128)(2,1)}, u32[]{:S(2)}, u32[]{:S(2)}) collective-permute-start(bf16[64,768]{1,0:T(8,128)(2,1)} %bitcast.67), channel_id=1, source_target_pairs={{0,4},{4,0},{8,12},{12,8},{16,20},{20,16},{24,28},{28,24},{1,5},{5... | collective-permute-start | bytes 294920 | tf_op jit(solution)/shard_map/ppermute | solution.py:59
  4.4 1.1 %copy-start.10 = (s32[4,64]{1,0:T(4,128)S(1)}, s32[4,64]{1,0:T(4,128)}, u32[]{:S(2)}) copy-start(s32[4,64]{1,0:T(4,128)} %param.13) | copy-start | bytes 3076
  8.1 17.4 %copy-start.8 = (bf16[768,2304]{1,0:T(8,128)(2,1)S(1)}, bf16[768,2304]{1,0:T(8,128)(2,1)}, u32[]{:S(2)}) copy-start(bf16[768,2304]{1,0:T(8,128)(2,1)} %param.14) | copy-start | bytes 10616836
  9.2 8.5 %collective-permute-start.1 = (bf16[64,768]{1,0:T(8,128)(2,1)S(1)}, bf16[64,768]{1,0:T(8,128)(2,1)S(1)}, u32[]{:S(2)}, u32[]{:S(2)}) collective-permute-start(bf16[64,768]{1,0:T(8,128)(2,1)S(1)} %broadcast_select_fusion), channel_id=1, source_target_pairs={{0,24},{4,28},{8,16},{12,20},{16,8},{20,12},{24,0},{28,4},{1,25},{... | collective-permute-start | bytes 294920 | tf_op jit(solution)/shard_map/ppermute | solution.py:59
  14.0 8.9 %collective-permute-start.2 = (bf16[64,768]{1,0:T(8,128)(2,1)S(1)}, bf16[64,768]{1,0:T(8,128)(2,1)S(1)}, u32[]{:S(2)}, u32[]{:S(2)}) collective-permute-start(bf16[64,768]{1,0:T(8,128)(2,1)S(1)} %broadcast_select_fusion), channel_id=1, source_target_pairs={{0,16},{4,20},{8,24},{12,28},{16,0},{20,4},{24,8},{28,12},{1,17},{... | collective-permute-start | bytes 294920 | tf_op jit(solution)/shard_map/ppermute | solution.py:59
  14.0 8.9 %collective-permute-start.3 = (bf16[64,768]{1,0:T(8,128)(2,1)S(1)}, bf16[64,768]{1,0:T(8,128)(2,1)S(1)}, u32[]{:S(2)}, u32[]{:S(2)}) collective-permute-start(bf16[64,768]{1,0:T(8,128)(2,1)S(1)} %broadcast_select_fusion), channel_id=1, source_target_pairs={{0,8},{4,12},{8,0},{12,4},{16,24},{20,28},{24,16},{28,20},{1,9},{5... | collective-permute-start | bytes 294920 | tf_op jit(solution)/shard_map/ppermute | solution.py:59
  14.6 34.3 %collective-permute-start.6 = (bf16[4,64,768]{2,1,0:T(8,128)(2,1)}, bf16[4,64,768]{2,1,0:T(8,128)(2,1)}, u32[]{:S(2)}, u32[]{:S(2)}) collective-permute-start(bf16[4,64,768]{2,1,0:T(8,128)(2,1)} %param.10), channel_id=1, source_target_pairs={{0,3},{1,2},{2,1},{3,0},{4,7},{5,6},{6,5},{7,4},{8,11},{9,10},{10,... | collective-permute-start | bytes 1179656 | tf_op jit(solution)/shard_map/ppermute | solution.py:133
  17.2 31.7 %collective-permute-start.5 = (bf16[4,64,768]{2,1,0:T(8,128)(2,1)}, bf16[4,64,768]{2,1,0:T(8,128)(2,1)}, u32[]{:S(2)}, u32[]{:S(2)}) collective-permute-start(bf16[4,64,768]{2,1,0:T(8,128)(2,1)} %param.10), channel_id=1, source_target_pairs={{0,2},{1,3},{2,0},{3,1},{4,6},{5,7},{6,4},{7,5},{8,10},{9,11},{10,... | collective-permute-start | bytes 1179656 | tf_op jit(solution)/shard_map/ppermute | solution.py:133
  22.8 3.2 %copy-start.6 = (bf16[64,768]{1,0:T(8,128)(2,1)}, bf16[64,768]{1,0:T(8,128)(2,1)S(1)}, u32[]{:S(2)}) copy-start(bf16[64,768]{1,0:T(8,128)(2,1)S(1)} %select_select_fusion) | copy-start | bytes 294916
  25.5 0.9 %copy-start.5 = (f32[64,768]{1,0:T(8,128)}, f32[64,768]{1,0:T(8,128)S(1)}, u32[]{:S(2)}) copy-start(f32[64,768]{1,0:T(8,128)S(1)} %fusion.33) | copy-start | bytes 589828
  26.4 1.2 %collective-permute-start.8 = (f32[32,24]{0,1:T(8,128)S(1)}, f32[32,24]{0,1:T(8,128)S(1)}, u32[]{:S(2)}, u32[]{:S(2)}) collective-permute-start(f32[32,24]{0,1:T(8,128)S(1)} %fusion.114), channel_id=1, source_target_pairs={{0,4},{4,0},{8,12},{12,8},{16,20},{20,16},{24,28},{28,24},{1,5},{5... | collective-permute-start | bytes 9224 | tf_op jit(solution)/shard_map/ppermute | solution.py:59
  27.7 5.6 %collective-permute-start.12 = (f32[32,24]{0,1:T(8,128)S(1)}, f32[32,24]{0,1:T(8,128)S(1)}, u32[]{:S(2)}, u32[]{:S(2)}) collective-permute-start(f32[32,24]{0,1:T(8,128)S(1)} %pad_maximum_fusion.4), channel_id=1, source_target_pairs={{0,24},{4,28},{8,16},{12,20},{16,8},{20,12},{24,0},{28,4},{1,25},{... | collective-permute-start | bytes 9224 | tf_op jit(solution)/shard_map/ppermute | solution.py:59
  30.2 4.6 %collective-permute-start.13 = (f32[32,24]{0,1:T(8,128)S(1)}, f32[32,24]{0,1:T(8,128)S(1)}, u32[]{:S(2)}, u32[]{:S(2)}) collective-permute-start(f32[32,24]{0,1:T(8,128)S(1)} %pad_maximum_fusion.4), channel_id=1, source_target_pairs={{0,16},{4,20},{8,24},{12,28},{16,0},{20,4},{24,8},{28,12},{1,17},{... | collective-permute-start | bytes 9224 | tf_op jit(solution)/shard_map/ppermute | solution.py:59
  30.2 4.6 %collective-permute-start.14 = (f32[32,24]{0,1:T(8,128)S(1)}, f32[32,24]{0,1:T(8,128)S(1)}, u32[]{:S(2)}, u32[]{:S(2)}) collective-permute-start(f32[32,24]{0,1:T(8,128)S(1)} %pad_maximum_fusion.4), channel_id=1, source_target_pairs={{0,8},{4,12},{8,0},{12,4},{16,24},{20,28},{24,16},{28,20},{1,9},{5... | collective-permute-start | bytes 9224 | tf_op jit(solution)/shard_map/ppermute | solution.py:59
  33.2 3.1 %collective-permute-start.7 = (f32[32,768]{1,0:T(8,128)S(1)}, f32[32,768]{1,0:T(8,128)S(1)}, u32[]{:S(2)}, u32[]{:S(2)}) collective-permute-start(f32[32,768]{1,0:T(8,128)S(1)} %slice_select_fusion), channel_id=1, source_target_pairs={{0,4},{4,0},{8,12},{12,8},{16,20},{20,16},{24,28},{28,24},{1,5},{5... | collective-permute-start | bytes 294920 | tf_op jit(solution)/shard_map/ppermute | solution.py:59
  37.6 6.1 %collective-permute-start.9 = (bf16[32,768]{1,0:T(8,128)(2,1)S(1)}, bf16[32,768]{1,0:T(8,128)(2,1)S(1)}, u32[]{:S(2)}, u32[]{:S(2)}) collective-permute-start(bf16[32,768]{1,0:T(8,128)(2,1)S(1)} %add_convert_fusion), channel_id=1, source_target_pairs={{0,24},{4,28},{8,16},{12,20},{16,8},{20,12},{24,0},{28,4},{1,25},{... | collective-permute-start | bytes 147464 | tf_op jit(solution)/shard_map/ppermute | solution.py:59
  39.1 6.1 %collective-permute-start.10 = (bf16[32,768]{1,0:T(8,128)(2,1)S(1)}, bf16[32,768]{1,0:T(8,128)(2,1)S(1)}, u32[]{:S(2)}, u32[]{:S(2)}) collective-permute-start(bf16[32,768]{1,0:T(8,128)(2,1)S(1)} %add_convert_fusion), channel_id=1, source_target_pairs={{0,16},{4,20},{8,24},{12,28},{16,0},{20,4},{24,8},{28,12},{1,17},{... | collective-permute-start | bytes 147464 | tf_op jit(solution)/shard_map/ppermute | solution.py:59
  40.1 5.1 %collective-permute-start.11 = (bf16[32,768]{1,0:T(8,128)(2,1)S(1)}, bf16[32,768]{1,0:T(8,128)(2,1)S(1)}, u32[]{:S(2)}, u32[]{:S(2)}) collective-permute-start(bf16[32,768]{1,0:T(8,128)(2,1)S(1)} %add_convert_fusion), channel_id=1, source_target_pairs={{0,8},{4,12},{8,0},{12,4},{16,24},{20,28},{24,16},{28,20},{1,9},{5... | collective-permute-start | bytes 147464 | tf_op jit(solution)/shard_map/ppermute | solution.py:59
  43.7 8.9 %collective-permute-start.4 = (bf16[4,64,768]{2,1,0:T(8,128)(2,1)}, bf16[4,64,768]{2,1,0:T(8,128)(2,1)S(1)}, u32[]{:S(2)}, u32[]{:S(2)}) collective-permute-start(bf16[4,64,768]{2,1,0:T(8,128)(2,1)} %param.10), channel_id=1, source_target_pairs={{0,1},{1,0},{2,3},{3,2},{4,5},{5,4},{6,7},{7,6},{8,9},{9,8},{10,11... | collective-permute-start | bytes 1179656 | tf_op jit(solution)/shard_map/ppermute | solution.py:133
  45.8 2.3 %collective-permute-start.15 = (bf16[32,768]{1,0:T(8,128)(2,1)S(1)}, bf16[32,768]{1,0:T(8,128)(2,1)S(1)}, u32[]{:S(2)}, u32[]{:S(2)}) collective-permute-start(bf16[32,768]{1,0:T(8,128)(2,1)S(1)} %fusion.43), channel_id=1, source_target_pairs={{0,4},{4,0},{8,12},{12,8},{16,20},{20,16},{24,28},{28,24},{1,5},{5... | collective-permute-start | bytes 147464 | tf_op jit(solution)/shard_map/ppermute | solution.py:59
  57.4 1.0 %copy-start.3 = (bf16[4,64,768]{2,1,0:T(8,128)(2,1)S(1)}, bf16[4,64,768]{2,1,0:T(8,128)(2,1)}, u32[]{:S(2)}) copy-start(bf16[4,64,768]{2,1,0:T(8,128)(2,1)} %get-tuple-element.15) | copy-start | bytes 1179652
  57.4 1.1 %copy-start.4 = (bf16[4,64,768]{2,1,0:T(8,128)(2,1)S(1)}, bf16[4,64,768]{2,1,0:T(8,128)(2,1)}, u32[]{:S(2)}) copy-start(bf16[4,64,768]{2,1,0:T(8,128)(2,1)} %get-tuple-element.16) | copy-start | bytes 1179652
  67.7 1.4 %copy-start.2 = (bf16[4,256,768]{1,2,0:T(8,128)(2,1)S(1)}, bf16[4,256,768]{1,2,0:T(8,128)(2,1)}, u32[]{:S(2)}) copy-start(bf16[4,256,768]{1,2,0:T(8,128)(2,1)} %copy.42) | copy-start | bytes 4718596
  69.1 1.4 %copy-start.1 = (f32[12,64,4,64]{3,1,2,0:T(8,128)S(1)}, f32[12,64,4,64]{3,1,2,0:T(8,128)}, u32[]{:S(2)}) copy-start(f32[12,64,4,64]{3,1,2,0:T(8,128)} %get-tuple-element.28) | copy-start | bytes 2359300
  71.3 1.1 %copy-start.7 = (bf16[64,768]{1,0:T(8,128)(2,1)S(1)}, bf16[64,768]{1,0:T(8,128)(2,1)}, u32[]{:S(2)}) copy-start(bf16[64,768]{1,0:T(8,128)(2,1)} %copy-done.6) | copy-start | bytes 294916
  72.5 2.1 %copy-start.11 = (f32[768]{0:T(1024)S(1)}, f32[768]{0:T(1024)}, u32[]{:S(2)}) copy-start(f32[768]{0:T(1024)} %param.16) | copy-start | bytes 9220
  74.6 7.7 %copy-start.9 = (f32[768]{0:T(1024)S(1)}, f32[768]{0:T(1024)}, u32[]{:S(2)}) copy-start(f32[768]{0:T(1024)} %param.19) | copy-start | bytes 9220

commit v12 on v9

--- a/solution.py
+++ b/solution.py
@@ -3,6 +3,7 @@
 import jax
 import jax.numpy as jnp
 from jax import lax
+from jax.experimental import pallas as pl
 from jax.sharding import PartitionSpec as P
 
 HEADS = 12
@@ -128,6 +129,54 @@
     return got
 
 
+def row_kernel(q_ref, k_ref, v_ref, sk_ref, sv_ref, allow_ref, o_ref, *, scale):
+    allow = allow_ref[0] > 0.5
+    lane = lax.broadcasted_iota(jnp.int32, (1, 2 * HEAD_DIM), 1)
+    low = lane < HEAD_DIM
+    nt = (((1,), (1,)), ((), ()))
+    for pair in range(HEADS // 2):
+        cols = slice(pair * 2 * HEAD_DIM, (pair + 1) * 2 * HEAD_DIM)
+        q = q_ref[0, :, cols]
+        k = k_ref[0, :, cols]
+        v = v_ref[0, :, cols]
+        sk = sk_ref[:, cols]
+        sv = sv_ref[:, cols]
+        outs = []
+        for side in (low, jnp.logical_not(low)):
+            qh = jnp.where(side, q, jnp.zeros_like(q))
+            s = lax.dot_general(qh, k, nt, preferred_element_type=jnp.float32) * scale
+            s = jnp.where(allow, s, -1e30)
+            ts = lax.dot_general(qh, sk, nt, preferred_element_type=jnp.float32) * scale
+            top = jnp.maximum(s.max(-1, keepdims=True), ts.max(-1, keepdims=True))
+            e = jnp.exp(s - top)
+            te = jnp.exp(ts - top)
+            tot = e.sum(-1, keepdims=True) + te.sum(-1, keepdims=True)
+            acc = jnp.dot(e.astype(jnp.bfloat16), v, preferred_element_type=jnp.float32)
+            acc = acc + jnp.dot(te.astype(jnp.bfloat16), sv, preferred_element_type=jnp.float32)
+            outs.append(acc / tot)
+        o_ref[0, :, cols] = jnp.where(low, outs[0], outs[1]).astype(o_ref.dtype)
+
+
+def row_attention(q, k, v, sk, sv, allow):
+    rows, nq, width = q.shape
+    nk = k.shape[1]
+    kern = functools.partial(row_kernel, scale=HEAD_DIM ** (-0.5))
+    return pl.pallas_call(
+        kern,
+        grid=(rows,),
+        in_specs=[
+            pl.BlockSpec((1, nq, width), lambda r: (r, 0, 0)),
+            pl.BlockSpec((1, nk, width), lambda r: (r, 0, 0)),
+            pl.BlockSpec((1, nk, width), lambda r: (r, 0, 0)),
+            pl.BlockSpec((sk.shape[0], width), lambda r: (0, 0)),
+            pl.BlockSpec((sv.shape[0], width), lambda r: (0, 0)),
+            pl.BlockSpec((1, nq, nk), lambda r: (r, 0, 0)),
+        ],
+        out_specs=pl.BlockSpec((1, nq, width), lambda r: (r, 0, 0)),
+        out_shape=jax.ShapeDtypeStruct(q.shape, jnp.bfloat16),
+    )(q, k, v, sk, sv, allow)
+
+
 def local(cells, summary, owner, schema, w_qkv, w_out, gain_attn, w_up, w_down, gain_ffn, *, n_band, n_col):
     row_count, cols_dev, model_width = cells.shape
     own_group = lax.axis_index("col")
@@ -183,11 +232,6 @@
     row_keys = jnp.concatenate([own_keys, other_kv[:, :, :model_width]], axis=1)
     row_vals = jnp.concatenate([own_vals, other_kv[:, :, model_width:]], axis=1)
     width_now = row_keys.shape[1]
-    q4 = queries.reshape(row_count, cols_dev, HEADS, HEAD_DIM)
-    k4 = row_keys.reshape(row_count, width_now, HEADS, HEAD_DIM)
-    v4 = row_vals.reshape(row_count, width_now, HEADS, HEAD_DIM)
-    sk = sum_keys.reshape(cols_dev, HEADS, HEAD_DIM)
-    sv = sum_vals.reshape(cols_dev, HEADS, HEAD_DIM)
     key_groups = jnp.concatenate(
         [jnp.full((cols_dev,), s, jnp.int32) for s in sources]
     )
@@ -195,25 +239,10 @@
     allowed = (jnp.right_shift(schema[:, :, None], key_groups[None, None, :]) & 1 == 1) | own_block[
         None, None, :
     ]
-    cell_scores = (
-        jnp.einsum("rqhd,rkhd->rhqk", q4, k4, preferred_element_type=jnp.float32) * score_scale
-    )
-    cell_scores = jnp.where(allowed[:, None], cell_scores, -1e30)
-    tok_scores = (
-        jnp.einsum("rqhd,khd->rhqk", q4, sk, preferred_element_type=jnp.float32) * score_scale
-    )
-    row_top = jnp.maximum(cell_scores.max(-1), tok_scores.max(-1))
-    cell_exp = jnp.exp(cell_scores - row_top[..., None])
-    tok_exp = jnp.exp(tok_scores - row_top[..., None])
-    row_total = cell_exp.sum(-1) + tok_exp.sum(-1)
-    mixed = jnp.einsum(
-        "rhqk,rkhd->rqhd", cell_exp.astype(jnp.bfloat16), v4, preferred_element_type=jnp.float32
-    )
-    mixed = mixed + jnp.einsum(
-        "rhqk,khd->rqhd", tok_exp.astype(jnp.bfloat16), sv, preferred_element_type=jnp.float32
-    )
-    attended = mixed / row_total.transpose(0, 2, 1)[..., None]
-    attended = attended.reshape(row_count * cols_dev, model_width).astype(jnp.bfloat16)
+    attended = row_attention(
+        queries, row_keys, row_vals, sum_keys, sum_vals, allowed.astype(jnp.float32)
+    )
+    attended = attended.reshape(row_count * cols_dev, model_width)
 
     all_in = jnp.concatenate([flat_cells, tokens], axis=0)
     all_att = jnp.concatenate([attended, summary_att], axis=0)

time: 80.6 us -> 76.8 us (0.953)
  Pallas kernels: 0 us -> 15 us
  local copies, waits for them, and re-layouts: 12.7 us -> 3.26 us
  matrix products: 28.1 us -> 21.5 us
  other arithmetic: 7.76 us -> 3.96 us
  waiting for transfers between devices: 13.7 us -> 15.1 us
    pallas_call x0 -> x1, Pallas kernels: none -> 15 us  [row_attention(): pl.pallas_call(kern, grid=(rows,), in_specs=[pl.BlockSpec((1, nq, width),...]
    dot_general x4 -> x0, matrix products: 5.81 us -> none  [the longest x1 2.13 us: local(): jnp.einsum('rqhd,rkhd->rhqk', q4, k4, preferred_element_type=jnp.float32)]
    concatenate x2 -> x0, local copies, waits for them, and re-layouts: 5.16 us -> none  [the longest x1 2.58 us: local(): row_vals = jnp.concatenate([own_vals, other_kv[:, :, model_width:]], axis=1)]
    reshape x3 -> x0, local copies, waits for them, and re-layouts: 1.99 us -> none  [the longest x1 1.66 us: local(): q4 = queries.reshape(row_count, cols_dev, HEADS, HEAD_DIM)]
    reduce_sum x2 -> x0, other arithmetic: 1.66 us -> none  [local(): row_total = cell_exp.sum(-1) + tok_exp.sum(-1)]
    select_n x3, other arithmetic: 1.57 us -> 0.04 us  [broadcast_from(): value = jnp.where(here // step == source // step, value, got)]
    unnamed x30 -> x14, local copies, waits for them, and re-layouts: 1.56 us -> 0.04 us
    ppermute x10, waiting for transfers between devices: 13.7 us -> 15 us  [partner(): return lax.ppermute(value, axis, [(i, i ^ step) for i in range(count)])]
  transfers between devices with their start and end apart: 13 -> 13, of which waited for: 6 -> 7; matrix products, arithmetic and copies ran while one was open for 43% -> 23% of each run, Pallas kernels for 0% -> 20%
where the time goes in v12:
time: 76.8 us; the launch traced here: 76.5 us
  matrix products  21.5 us (28%)
  starting transfers between devices  16.2 us (21%)
  waiting for transfers between devices  15.1 us (20%)
  Pallas kernels  15 us (20%)
  other arithmetic  3.96 us (5%)
  local copies, waits for them, and re-layouts  3.26 us (4%)
  between operations  1.61 us (2%)
    ppermute x10, waiting for transfers between devices, partner(): return lax.ppermute(value, axis, [(i, i ^ step) for i in range(count)])  15 us
    pallas_call x1, Pallas kernels, row_attention(): pl.pallas_call(kern, grid=(rows,), in_specs=[pl.BlockSpec((1, nq, width),...  15 us
    ppermute x10, starting transfers between devices, partner(): return lax.ppermute(value, axis, [(i, i ^ step) for i in range(count)])  12.7 us
    dot_general x4, matrix products, project(): jnp.dot(values, weight, preferred_element_type=jnp.float32)  9.03 us
    dot_general x1, matrix products, finish(): outer_out = jnp.dot(inner_act, w_down, preferred_element_type=jnp.float32)  7.43 us
    ppermute x3, starting transfers between devices, fan_out(): got.append((source, lax.ppermute(value, axis, pairs)))  3.49 us
    dot_general x10, matrix products, head_spread(): jnp.dot(flat, head_matrix(), precision=lax.Precision.HIGHEST, preferred_e...  2.56 us
    concatenate x1, other arithmetic, local(): row_keys = jnp.concatenate([own_keys, other_kv[:, :, :model_width]], axis=1)  1.84 us
  transfers between devices with their start and end apart: 13, of which 7 were waited for; matrix products, arithmetic and copies ran while one was open for 23% of the time, Pallas kernels for 20%

profile of v12, /device:TPU:0, one launch (start us, length us, event | category | flops | bytes accessed | tf_op | source)
XLA Modules:
  0.0 76.5 jit_solution(16558632503700021332)
XLA Ops:
  0.6 0.0 copy-start
  0.6 0.5 collective-permute-start
  1.8 3.2 %convolution_convert_fusion = bf16[256,2304]{1,0:T(8,128)(2,1)S(1)} fusion(bf16[256,768]{1,0:T(8,128)(2,1)} %bitcast.36, bf16[768,2304]{1,0:T(8,128)(2,1)} %param.14), kind=kOutput, calls=%fused_computation.9 | convolution fusion | flops 906559488 | bytes 5111808 | tf_op jit(solution)/shard_map/dot_general | solution.py:35
  5.0 0.0 copy-start.2
  5.1 0.0 copy-start.4
  5.1 0.9 %fusion.106 = (bf16[4,64,768]{2,1,0:T(8,128)(2,1)S(1)}, bf16[4,64,768]{2,1,0:T(8,128)(2,1)S(1)}, bf16[4,64,768]{2,1,0:T(8,128)(2,1)}) fusion(bf16[4,64,2304]{2,1,0:T(8,128)(2,1)S(1)} %bitcast.28), kind=kLoop, calls=%fused_computation.156 | loop fusion | bytes 2359296 | tf_op jit(solution)/shard_map/slice | solution.py:195
  5.9 0.1 pad_add_fusion
  6.0 0.0 collective-permute-done
  6.1 2.7 %collective-permute-start.1 = (bf16[64,768]{1,0:T(8,128)(2,1)S(1)}, bf16[64,768]{1,0:T(8,128)(2,1)S(1)}, u32[]{:S(2)}, u32[]{:S(2)}) collective-permute-start(bf16[64,768]{1,0:T(8,128)(2,1)S(1)} %broadcast_select_fusion), channel_id=1, source_target_pairs={{0,8},{4,12},{8,0},{12,4},{16,24},{20,28},{24,16},{28,20},{1,9},{5... | collective-permute-start | bytes 294920 | tf_op jit(solution)/shard_map/ppermute | solution.py:60
  8.8 0.8 %fusion.39.allow_ref = f32[4,64,256]{2,1,0:T(8,128)} fusion(s32[256]{0:T(256)S(1)} %pad_add_fusion, s32[4,64]{1,0:T(4,128)S(1)} %copy-done.4, pred[256]{0:T(512)(128)(4,1)S(1)} %iota_compare_fusion.15), kind=kLoop, calls=%fused_computation.47 | loop fusion | flops 327680 | bytes 264448 | tf_op jit(solution)/shard_map/convert_element_type | solution.py:243
  9.6 2.6 %collective-permute-done.1 = bf16[64,768]{1,0:T(8,128)(2,1)S(1)} collective-permute-done((bf16[64,768]{1,0:T(8,128)(2,1)S(1)}, bf16[64,768]{1,0:T(8,128)(2,1)S(1)}, u32[]{:S(2)}, u32[]{:S(2)}) %collective-permute-start.1) | collective-permute-done | bytes 98336 | tf_op jit(solution)/shard_map/ppermute | solution.py:60
  12.2 2.8 %collective-permute-start.2 = (bf16[64,768]{1,0:T(8,128)(2,1)S(1)}, bf16[64,768]{1,0:T(8,128)(2,1)S(1)}, u32[]{:S(2)}, u32[]{:S(2)}) collective-permute-start(bf16[64,768]{1,0:T(8,128)(2,1)S(1)} %broadcast_select_fusion.1), channel_id=1, source_target_pairs={{0,16},{4,20},{8,24},{12,28},{16,0},{20,4},{24,8},{28,12},{1,17},{... | collective-permute-start | bytes 294920 | tf_op jit(solution)/shard_map/ppermute | solution.py:60
  15.0 2.4 %collective-permute-start.5 = (bf16[4,64,768]{2,1,0:T(8,128)(2,1)}, bf16[4,64,768]{2,1,0:T(8,128)(2,1)S(1)}, u32[]{:S(2)}, u32[]{:S(2)}) collective-permute-start(bf16[4,64,768]{2,1,0:T(8,128)(2,1)} %param.10), channel_id=1, source_target_pairs={{0,3},{1,2},{2,1},{3,0},{4,7},{5,6},{6,5},{7,4},{8,11},{9,10},{10,... | collective-permute-start | bytes 1179656 | tf_op jit(solution)/shard_map/ppermute | solution.py:128
  17.5 0.5 collective-permute-start.4
  18.0 0.5 collective-permute-start.3
  18.5 1.3 %collective-permute-done.2 = bf16[64,768]{1,0:T(8,128)(2,1)S(1)} collective-permute-done((bf16[64,768]{1,0:T(8,128)(2,1)S(1)}, bf16[64,768]{1,0:T(8,128)(2,1)S(1)}, u32[]{:S(2)}, u32[]{:S(2)}) %collective-permute-start.2) | collective-permute-done | bytes 98336 | tf_op jit(solution)/shard_map/ppermute | solution.py:60
  19.8 1.6 %fusion.25 = f32[64,768]{1,0:T(8,128)S(1)} fusion(bf16[64,768]{1,0:T(8,128)(2,1)S(1)} %broadcast_select_fusion.2, bf16[768,2304]{1,0:T(8,128)(2,1)} %param.14), kind=kOutput, calls=%fused_computation.28 | convolution fusion | flops 75595776 | bytes 1474560 | tf_op jit(solution)/shard_map/dot_general | solution.py:35
  21.4 2.2 %convolution_convert_fusion.2 = bf16[64,1536]{1,0:T(8,128)(2,1)S(1)} fusion(bf16[64,768]{1,0:T(8,128)(2,1)S(1)} %broadcast_select_fusion.2, bf16[768,2304]{1,0:T(8,128)(2,1)} %param.14), kind=kOutput, calls=%fused_computation.11 | convolution fusion | flops 151093248 | bytes 2654208 | tf_op jit(solution)/shard_map/dot_general | solution.py:35
  23.6 0.6 fusion.108
  24.3 0.3 fusion.19
  24.6 0.2 convolution_multiply_fusion.2
  24.8 0.8 fusion.107
  25.5 0.1 fusion.87
  25.6 0.0 collective-permute-start.7
  25.6 0.1 slice_select_fusion.2
  25.7 0.5 collective-permute-start.6
  26.2 0.6 collective-permute-done.7
  26.8 0.1 broadcast_select_fusion.8
  26.9 0.0 copy-start.1
  26.9 0.7 collective-permute-start.9
  27.6 0.3 fusion.58
  27.9 2.8 %collective-permute-done.9 = f32[32,24]{0,1:T(8,128)S(1)} collective-permute-done((f32[32,24]{0,1:T(8,128)S(1)}, f32[32,24]{0,1:T(8,128)S(1)}, u32[]{:S(2)}, u32[]{:S(2)}) %collective-permute-start.9) | collective-permute-done | bytes 3104 | tf_op jit(solution)/shard_map/ppermute | solution.py:60
  30.7 2.1 %collective-permute-start.11 = (f32[32,24]{0,1:T(8,128)S(1)}, f32[32,24]{0,1:T(8,128)S(1)}, u32[]{:S(2)}, u32[]{:S(2)}) collective-permute-start(f32[32,24]{0,1:T(8,128)S(1)} %pad_maximum_fusion.5), channel_id=1, source_target_pairs={{0,16},{4,20},{8,24},{12,28},{16,0},{20,4},{24,8},{28,12},{1,17},{... | collective-permute-start | bytes 9224 | tf_op jit(solution)/shard_map/ppermute | solution.py:60
  32.8 0.3 fusion.55
  33.0 2.3 %collective-permute-done.11 = f32[32,24]{0,1:T(8,128)S(1)} collective-permute-done((f32[32,24]{0,1:T(8,128)S(1)}, f32[32,24]{0,1:T(8,128)S(1)}, u32[]{:S(2)}, u32[]{:S(2)}) %collective-permute-start.11) | collective-permute-done | bytes 3104 | tf_op jit(solution)/shard_map/ppermute | solution.py:60
  35.4 0.2 fusion.54
  35.7 0.3 fusion.53
  35.9 0.0 collective-permute-done.6
  35.9 0.3 add_convert_fusion
  36.2 1.2 %collective-permute-start.8 = (bf16[32,768]{1,0:T(8,128)(2,1)S(1)}, bf16[32,768]{1,0:T(8,128)(2,1)S(1)}, u32[]{:S(2)}, u32[]{:S(2)}) collective-permute-start(bf16[32,768]{1,0:T(8,128)(2,1)S(1)} %add_convert_fusion), channel_id=1, source_target_pairs={{0,8},{4,12},{8,0},{12,4},{16,24},{20,28},{24,16},{28,20},{1,9},{5... | collective-permute-start | bytes 147464 | tf_op jit(solution)/shard_map/ppermute | solution.py:60
  37.4 0.3 fusion.52
  37.6 2.7 %collective-permute-done.8 = bf16[32,768]{1,0:T(8,128)(2,1)S(1)} collective-permute-done((bf16[32,768]{1,0:T(8,128)(2,1)S(1)}, bf16[32,768]{1,0:T(8,128)(2,1)S(1)}, u32[]{:S(2)}, u32[]{:S(2)}) %collective-permute-start.8) | collective-permute-done | bytes 49184 | tf_op jit(solution)/shard_map/ppermute | solution.py:60
  40.4 0.3 fusion.44
  40.6 2.1 %collective-permute-start.10 = (bf16[32,768]{1,0:T(8,128)(2,1)S(1)}, bf16[32,768]{1,0:T(8,128)(2,1)S(1)}, u32[]{:S(2)}, u32[]{:S(2)}) collective-permute-start(bf16[32,768]{1,0:T(8,128)(2,1)S(1)} %fusion.44), channel_id=1, source_target_pairs={{0,16},{4,20},{8,24},{12,28},{16,0},{20,4},{24,8},{28,12},{1,17},{... | collective-permute-start | bytes 147464 | tf_op jit(solution)/shard_map/ppermute | solution.py:60
  42.7 0.2 fusion.51
  42.9 2.8 %collective-permute-done.10 = bf16[32,768]{1,0:T(8,128)(2,1)S(1)} collective-permute-done((bf16[32,768]{1,0:T(8,128)(2,1)S(1)}, bf16[32,768]{1,0:T(8,128)(2,1)S(1)}, u32[]{:S(2)}, u32[]{:S(2)}) %collective-permute-start.10) | collective-permute-done | bytes 49184 | tf_op jit(solution)/shard_map/ppermute | solution.py:60
  45.7 0.3 fusion.28
  45.9 0.1 collective-permute-start.12
  46.0 0.0 collective-permute-done.5
  46.0 0.0 collective-permute-done.4
  46.0 0.1 pad_maximum_fusion.2
  46.1 2.0 %convolution_convert_fusion.1 = bf16[768,1536]{1,0:T(8,128)(2,1)S(1)} fusion(bf16[768,768]{1,0:T(8,128)(2,1)S(1)} %bitcast.32, bf16[768,2304]{1,0:T(8,128)(2,1)S(1)} %copy-done.1), kind=kOutput, calls=%fused_computation.10 | convolution fusion | flops 1813118976 | bytes 5898240 | tf_op jit(solution)/shard_map/dot_general | solution.py:35
  48.2 0.2 fusion.105
  48.3 1.8 %pad_maximum_fusion = (bf16[4,256,768]{2,1,0:T(8,128)(2,1)}, bf16[4,256,768]{2,1,0:T(8,128)(2,1)}) fusion(bf16[4,192,768]{2,1,0:T(8,128)(2,1)S(1)} %get-tuple-element.13, bf16[4,64,768]{2,1,0:T(8,128)(2,1)S(1)} %get-tuple-element.15, bf16[4,192,768]{2,1,0:T(8,128)(2,1)S(1)} %get-tuple-element.12, bf16[4,64,768]{2,1,0:T(8,128)(2,1)S(1)} %get-tuple-element.14), kind=kLoop, calls=%fused_computation.19 | loop fusion | flops 6291456 | bytes 6291456 | tf_op jit(solution)/shard_map/concatenate | solution.py:232
  50.2 15.0 %shard_map.113 = bf16[4,64,768]{2,1,0:T(8,128)(2,1)} custom-call(bf16[4,64,768]{2,1,0:T(8,128)(2,1)} %get-tuple-element.16.q_ref, bf16[4,256,768]{2,1,0:T(8,128)(2,1)} %get-tuple-element.29.k_ref, bf16[4,256,768]{2,1,0:T(8,128)(2,1)} %get-tuple-element.30.v_ref, bf16[64,768]{1,0:T(8,128)(2,1)} %get-tuple-element.18.sk_ref, ...), custom_call_target="tpu_custom_call" | custom-call | tf_op jit(solution)/shard_map/pallas_call | solution.py:164
  65.2 0.0 copy-start.6
  65.2 1.7 %fusion.109 = (f32[320]{0:T(512)S(1)}, f32[320,768]{1,0:T(8,128)S(1)}) fusion(bf16[768,768]{1,0:T(8,128)(2,1)S(1)} %copy-done, bf16[64,768]{1,0:T(8,128)(2,1)S(1)} %maximum_select_fusion, bf16[256,768]{1,0:T(8,128)(2,1)} %bitcast.33, bf16[64,768]{1,0:T(8,128)(2,1)S(1)} %broadcast_select_fusion.2, bf16[256,768]{1,0:T(8,128)(2,1)S(1)} %bitcast.37), kind=kOutput, calls=%fused_computation.159 | convolution fusion | flops 379944640 | bytes 3147008 | tf_op jit(solution)/shard_map/dot_general | solution.py:25
  66.9 0.3 multiply_reduce_fusion.1
  67.2 0.0 copy-start.3
  67.2 7.4 %fusion.110 = (f32[320]{0:T(512)S(1)}, f32[320,768]{1,0:T(8,128)S(1)}) fusion(bf16[3072,768]{1,0:T(8,128)(2,1)} %param.18, bf16[768,3072]{1,0:T(8,128)(2,1)} %param.17, f32[320,768]{1,0:T(8,128)S(1)} %get-tuple-element.26, f32[768]{0:T(1024)S(1)} %copy-done.6, f32[320]{0:T(512)S(1)} %add_rsqrt_fusion.1, f32[320]{0:T(512)S(1)} %broadcast_multiply_fusion.1), kind=kOutput, calls=%fused_computation.160 | convolution fusion | flops 3031449344 | bytes 11410176 | tf_op jit(solution)/shard_map/dot_general | solution.py:30
  74.6 0.3 multiply_reduce_fusion
  74.9 0.2 multiply_convert_fusion
  75.1 0.8 %slice.159 = bf16[256,768]{1,0:T(8,128)(2,1)} slice(bf16[320,768]{1,0:T(8,128)(2,1)S(1)} %multiply_convert_fusion), slice={[0:256], [0:768]} | slice | bytes 786432 | tf_op jit(solution)/shard_map/slice | solution.py:250
  75.9 0.6 slice.160
  (34 shorter events, 0.2 us)
Async XLA Ops:
  0.6 64.6 %copy-start = (bf16[768,768]{1,0:T(8,128)(2,1)S(1)}, bf16[768,768]{1,0:T(8,128)(2,1)}, u32[]{:S(2)}) copy-start(bf16[768,768]{1,0:T(8,128)(2,1)} %param.15) | copy-start | bytes 3538948
  0.6 5.4 %collective-permute-start = (bf16[64,768]{1,0:T(8,128)(2,1)}, bf16[64,768]{1,0:T(8,128)(2,1)S(1)}, u32[]{:S(2)}, u32[]{:S(2)}) collective-permute-start(bf16[64,768]{1,0:T(8,128)(2,1)} %bitcast.35), channel_id=1, source_target_pairs={{0,4},{4,0},{8,12},{12,8},{16,20},{20,16},{24,28},{28,24},{1,5},{5... | collective-permute-start | bytes 294920 | tf_op jit(solution)/shard_map/ppermute | solution.py:60
  5.0 1.0 %copy-start.2 = (bf16[1,64,768]{2,1,0:T(8,128)(2,1)S(1)}, bf16[1,64,768]{2,1,0:T(8,128)(2,1)}, u32[]{:S(2)}) copy-start(bf16[1,64,768]{2,1,0:T(8,128)(2,1)} %param.11) | copy-start | bytes 294916
  5.1 3.7 %copy-start.4 = (s32[4,64]{1,0:T(4,128)S(1)}, s32[4,64]{1,0:T(4,128)}, u32[]{:S(2)}) copy-start(s32[4,64]{1,0:T(4,128)} %param.13) | copy-start | bytes 3076
  6.1 6.1 %collective-permute-start.1 = (bf16[64,768]{1,0:T(8,128)(2,1)S(1)}, bf16[64,768]{1,0:T(8,128)(2,1)S(1)}, u32[]{:S(2)}, u32[]{:S(2)}) collective-permute-start(bf16[64,768]{1,0:T(8,128)(2,1)S(1)} %broadcast_select_fusion), channel_id=1, source_target_pairs={{0,8},{4,12},{8,0},{12,4},{16,24},{20,28},{24,16},{28,20},{1,9},{5... | collective-permute-start | bytes 294920 | tf_op jit(solution)/shard_map/ppermute | solution.py:60
  12.2 7.6 %collective-permute-start.2 = (bf16[64,768]{1,0:T(8,128)(2,1)S(1)}, bf16[64,768]{1,0:T(8,128)(2,1)S(1)}, u32[]{:S(2)}, u32[]{:S(2)}) collective-permute-start(bf16[64,768]{1,0:T(8,128)(2,1)S(1)} %broadcast_select_fusion.1), channel_id=1, source_target_pairs={{0,16},{4,20},{8,24},{12,28},{16,0},{20,4},{24,8},{28,12},{1,17},{... | collective-permute-start | bytes 294920 | tf_op jit(solution)/shard_map/ppermute | solution.py:60
  15.0 31.0 %collective-permute-start.5 = (bf16[4,64,768]{2,1,0:T(8,128)(2,1)}, bf16[4,64,768]{2,1,0:T(8,128)(2,1)S(1)}, u32[]{:S(2)}, u32[]{:S(2)}) collective-permute-start(bf16[4,64,768]{2,1,0:T(8,128)(2,1)} %param.10), channel_id=1, source_target_pairs={{0,3},{1,2},{2,1},{3,0},{4,7},{5,6},{6,5},{7,4},{8,11},{9,10},{10,... | collective-permute-start | bytes 1179656 | tf_op jit(solution)/shard_map/ppermute | solution.py:128
  17.5 28.6 %collective-permute-start.4 = (bf16[4,64,768]{2,1,0:T(8,128)(2,1)}, bf16[4,64,768]{2,1,0:T(8,128)(2,1)S(1)}, u32[]{:S(2)}, u32[]{:S(2)}) collective-permute-start(bf16[4,64,768]{2,1,0:T(8,128)(2,1)} %param.10), channel_id=1, source_target_pairs={{0,2},{1,3},{2,0},{3,1},{4,6},{5,7},{6,4},{7,5},{8,10},{9,11},{10,... | collective-permute-start | bytes 1179656 | tf_op jit(solution)/shard_map/ppermute | solution.py:128
  18.0 28.1 %collective-permute-start.3 = (bf16[4,64,768]{2,1,0:T(8,128)(2,1)}, bf16[4,64,768]{2,1,0:T(8,128)(2,1)S(1)}, u32[]{:S(2)}, u32[]{:S(2)}) collective-permute-start(bf16[4,64,768]{2,1,0:T(8,128)(2,1)} %param.10), channel_id=1, source_target_pairs={{0,1},{1,0},{2,3},{3,2},{4,5},{5,4},{6,7},{7,6},{8,9},{9,8},{10,11... | collective-permute-start | bytes 1179656 | tf_op jit(solution)/shard_map/ppermute | solution.py:128
  25.6 1.2 %collective-permute-start.7 = (f32[32,24]{0,1:T(8,128)S(1)}, f32[32,24]{0,1:T(8,128)S(1)}, u32[]{:S(2)}, u32[]{:S(2)}) collective-permute-start(f32[32,24]{0,1:T(8,128)S(1)} %fusion.87), channel_id=1, source_target_pairs={{0,4},{4,0},{8,12},{12,8},{16,20},{20,16},{24,28},{28,24},{1,5},{5... | collective-permute-start | bytes 9224 | tf_op jit(solution)/shard_map/ppermute | solution.py:60
  25.7 10.2 %collective-permute-start.6 = (f32[32,768]{1,0:T(8,128)S(1)}, f32[32,768]{1,0:T(8,128)S(1)}, u32[]{:S(2)}, u32[]{:S(2)}) collective-permute-start(f32[32,768]{1,0:T(8,128)S(1)} %slice_select_fusion), channel_id=1, source_target_pairs={{0,4},{4,0},{8,12},{12,8},{16,20},{20,16},{24,28},{28,24},{1,5},{5... | collective-permute-start | bytes 294920 | tf_op jit(solution)/shard_map/ppermute | solution.py:60
  26.9 19.3 %copy-start.1 = (bf16[768,2304]{1,0:T(8,128)(2,1)S(1)}, bf16[768,2304]{1,0:T(8,128)(2,1)}, u32[]{:S(2)}) copy-start(bf16[768,2304]{1,0:T(8,128)(2,1)} %param.14) | copy-start | bytes 10616836
  26.9 3.8 %collective-permute-start.9 = (f32[32,24]{0,1:T(8,128)S(1)}, f32[32,24]{0,1:T(8,128)S(1)}, u32[]{:S(2)}, u32[]{:S(2)}) collective-permute-start(f32[32,24]{0,1:T(8,128)S(1)} %pad_maximum_fusion.4), channel_id=1, source_target_pairs={{0,8},{4,12},{8,0},{12,4},{16,24},{20,28},{24,16},{28,20},{1,9},{5... | collective-permute-start | bytes 9224 | tf_op jit(solution)/shard_map/ppermute | solution.py:60
  30.7 4.7 %collective-permute-start.11 = (f32[32,24]{0,1:T(8,128)S(1)}, f32[32,24]{0,1:T(8,128)S(1)}, u32[]{:S(2)}, u32[]{:S(2)}) collective-permute-start(f32[32,24]{0,1:T(8,128)S(1)} %pad_maximum_fusion.5), channel_id=1, source_target_pairs={{0,16},{4,20},{8,24},{12,28},{16,0},{20,4},{24,8},{28,12},{1,17},{... | collective-permute-start | bytes 9224 | tf_op jit(solution)/shard_map/ppermute | solution.py:60
  36.2 4.2 %collective-permute-start.8 = (bf16[32,768]{1,0:T(8,128)(2,1)S(1)}, bf16[32,768]{1,0:T(8,128)(2,1)S(1)}, u32[]{:S(2)}, u32[]{:S(2)}) collective-permute-start(bf16[32,768]{1,0:T(8,128)(2,1)S(1)} %add_convert_fusion), channel_id=1, source_target_pairs={{0,8},{4,12},{8,0},{12,4},{16,24},{20,28},{24,16},{28,20},{1,9},{5... | collective-permute-start | bytes 147464 | tf_op jit(solution)/shard_map/ppermute | solution.py:60
  40.6 5.1 %collective-permute-start.10 = (bf16[32,768]{1,0:T(8,128)(2,1)S(1)}, bf16[32,768]{1,0:T(8,128)(2,1)S(1)}, u32[]{:S(2)}, u32[]{:S(2)}) collective-permute-start(bf16[32,768]{1,0:T(8,128)(2,1)S(1)} %fusion.44), channel_id=1, source_target_pairs={{0,16},{4,20},{8,24},{12,28},{16,0},{20,4},{24,8},{28,12},{1,17},{... | collective-permute-start | bytes 147464 | tf_op jit(solution)/shard_map/ppermute | solution.py:60
  45.9 19.2 %collective-permute-start.12 = (bf16[32,768]{1,0:T(8,128)(2,1)S(1)}, bf16[32,768]{1,0:T(8,128)(2,1)S(1)}, u32[]{:S(2)}, u32[]{:S(2)}) collective-permute-start(bf16[32,768]{1,0:T(8,128)(2,1)S(1)} %fusion.28), channel_id=1, source_target_pairs={{0,4},{4,0},{8,12},{12,8},{16,20},{20,16},{24,28},{28,24},{1,5},{5... | collective-permute-start | bytes 147464 | tf_op jit(solution)/shard_map/ppermute | solution.py:60
  50.2 15.0 %copy-start.5 = (bf16[4,64,768]{2,1,0:T(8,128)(2,1)S(1)}, bf16[4,64,768]{2,1,0:T(8,128)(2,1)}, u32[]{:S(2)}) copy-start(bf16[4,64,768]{2,1,0:T(8,128)(2,1)} %param.10) | copy-start | bytes 1179652
  65.2 2.0 %copy-start.6 = (f32[768]{0:T(1024)S(1)}, f32[768]{0:T(1024)}, u32[]{:S(2)}) copy-start(f32[768]{0:T(1024)} %param.16) | copy-start | bytes 9220
  67.2 7.7 %copy-start.3 = (f32[768]{0:T(1024)S(1)}, f32[768]{0:T(1024)}, u32[]{:S(2)}) copy-start(f32[768]{0:T(1024)} %param.19) | copy-start | bytes 9220

commit v13 on v12

--- a/solution.py
+++ b/solution.py
@@ -129,24 +129,23 @@
     return got
 
 
-def row_kernel(q_ref, k_ref, v_ref, sk_ref, sv_ref, allow_ref, o_ref, *, scale):
+def row_kernel(q_ref, kt_ref, v_ref, skt_ref, sv_ref, allow_ref, o_ref, *, scale):
     allow = allow_ref[0] > 0.5
     lane = lax.broadcasted_iota(jnp.int32, (1, 2 * HEAD_DIM), 1)
     low = lane < HEAD_DIM
-    nt = (((1,), (1,)), ((), ()))
     for pair in range(HEADS // 2):
         cols = slice(pair * 2 * HEAD_DIM, (pair + 1) * 2 * HEAD_DIM)
         q = q_ref[0, :, cols]
-        k = k_ref[0, :, cols]
+        kt = kt_ref[0, cols, :]
         v = v_ref[0, :, cols]
-        sk = sk_ref[:, cols]
+        skt = skt_ref[cols, :]
         sv = sv_ref[:, cols]
         outs = []
         for side in (low, jnp.logical_not(low)):
             qh = jnp.where(side, q, jnp.zeros_like(q))
-            s = lax.dot_general(qh, k, nt, preferred_element_type=jnp.float32) * scale
+            s = jnp.dot(qh, kt, preferred_element_type=jnp.float32) * scale
             s = jnp.where(allow, s, -1e30)
-            ts = lax.dot_general(qh, sk, nt, preferred_element_type=jnp.float32) * scale
+            ts = jnp.dot(qh, skt, preferred_element_type=jnp.float32) * scale
             top = jnp.maximum(s.max(-1, keepdims=True), ts.max(-1, keepdims=True))
             e = jnp.exp(s - top)
             te = jnp.exp(ts - top)
@@ -157,24 +156,24 @@
         o_ref[0, :, cols] = jnp.where(low, outs[0], outs[1]).astype(o_ref.dtype)
 
 
-def row_attention(q, k, v, sk, sv, allow):
+def row_attention(q, kt, v, skt, sv, allow):
     rows, nq, width = q.shape
-    nk = k.shape[1]
+    nk = v.shape[1]
     kern = functools.partial(row_kernel, scale=HEAD_DIM ** (-0.5))
     return pl.pallas_call(
         kern,
         grid=(rows,),
         in_specs=[
             pl.BlockSpec((1, nq, width), lambda r: (r, 0, 0)),
+            pl.BlockSpec((1, width, nk), lambda r: (r, 0, 0)),
             pl.BlockSpec((1, nk, width), lambda r: (r, 0, 0)),
-            pl.BlockSpec((1, nk, width), lambda r: (r, 0, 0)),
-            pl.BlockSpec((sk.shape[0], width), lambda r: (0, 0)),
+            pl.BlockSpec((width, skt.shape[1]), lambda r: (0, 0)),
             pl.BlockSpec((sv.shape[0], width), lambda r: (0, 0)),
             pl.BlockSpec((1, nq, nk), lambda r: (r, 0, 0)),
         ],
         out_specs=pl.BlockSpec((1, nq, width), lambda r: (r, 0, 0)),
         out_shape=jax.ShapeDtypeStruct(q.shape, jnp.bfloat16),
-    )(q, k, v, sk, sv, allow)
+    )(q, kt, v, skt, sv, allow)
 
 
 def local(cells, summary, owner, schema, w_qkv, w_out, gain_attn, w_up, w_down, gain_ffn, *, n_band, n_col):
@@ -240,7 +239,8 @@
         None, None, :
     ]
     attended = row_attention(
-        queries, row_keys, row_vals, sum_keys, sum_vals, allowed.astype(jnp.float32)
+        queries, jnp.swapaxes(row_keys, 1, 2), row_vals, sum_keys.T, sum_vals,
+        allowed.astype(jnp.float32),
     )
     attended = attended.reshape(row_count * cols_dev, model_width)
 

time: 76.8 us -> 81 us (1.055)
  local copies, waits for them, and re-layouts: 3.26 us -> 5.62 us
  other arithmetic: 3.96 us -> 5.64 us
  matrix products: 21.5 us -> 23 us
    transpose x0 -> x2, local copies, waits for them, and re-layouts: none -> 2.38 us  [the longest x1 1.57 us: local(): jnp.swapaxes(row_keys, 1, 2)]
    concatenate x1 -> x0, other arithmetic: 1.84 us -> none  [local(): row_keys = jnp.concatenate([own_keys, other_kv[:, :, :model_width]], axis=1)]
    dot_general x10, matrix products: 2.56 us -> 4.02 us  [head_spread(): jnp.dot(flat, head_matrix(), precision=lax.Precision.HIGHEST, preferred_e...]
    transpose x0 -> x1, other arithmetic: none -> 1.39 us  [local(): jnp.swapaxes(row_keys, 1, 2)]
    concatenate x1, other arithmetic: 0.08 us -> 1.32 us  [local(): other_cells = jnp.concatenate([got for _, got in row_parts], axis=1)]
    select_n x1, other arithmetic: 0.02 us -> 0.9 us  [join_halves(): jnp.where(first, jnp.concatenate([value, got]), jnp.concatenate([got, val...]
    pallas_call x1, Pallas kernels: 15 us -> 14.2 us  [row_attention(): pl.pallas_call(kern, grid=(rows,), in_specs=[pl.BlockSpec((1, nq, width),...]
  transfers between devices with their start and end apart: 13 -> 13, of which waited for: 7 -> 6; matrix products, arithmetic and copies ran while one was open for 23% -> 27% of each run, Pallas kernels for 20% -> 18%
where the time goes in v13:
time: 81 us; the launch traced here: 80.6 us
  matrix products  23 us (28%)
  starting transfers between devices  16.1 us (20%)
  waiting for transfers between devices  14.5 us (18%)
  Pallas kernels  14.2 us (18%)
  other arithmetic  5.64 us (7%)
  local copies, waits for them, and re-layouts  5.62 us (7%)
  between operations  1.62 us (2%)
    ppermute x10, waiting for transfers between devices, partner(): return lax.ppermute(value, axis, [(i, i ^ step) for i in range(count)])  14.5 us
    pallas_call x1, Pallas kernels, row_attention(): pl.pallas_call(kern, grid=(rows,), in_specs=[pl.BlockSpec((1, nq, width),...  14.2 us
    ppermute x10, starting transfers between devices, partner(): return lax.ppermute(value, axis, [(i, i ^ step) for i in range(count)])  12.6 us
    dot_general x4, matrix products, project(): jnp.dot(values, weight, preferred_element_type=jnp.float32)  9.07 us
    dot_general x1, matrix products, finish(): outer_out = jnp.dot(inner_act, w_down, preferred_element_type=jnp.float32)  7.43 us
    dot_general x10, matrix products, head_spread(): jnp.dot(flat, head_matrix(), precision=lax.Precision.HIGHEST, preferred_e...  4.02 us
    ppermute x3, starting transfers between devices, fan_out(): got.append((source, lax.ppermute(value, axis, pairs)))  3.49 us
    dot_general x1, matrix products, finish(): mixed_out = jnp.dot(attended, w_out, preferred_element_type=jnp.float32)  1.65 us
  transfers between devices with their start and end apart: 13, of which 6 were waited for; matrix products, arithmetic and copies ran while one was open for 27% of the time, Pallas kernels for 18%

profile of v13, /device:TPU:0, one launch (start us, length us, event | category | flops | bytes accessed | tf_op | source)
XLA Modules:
  0.0 80.6 jit_solution(3819005472682311084)
XLA Ops:
  0.6 0.0 copy-start
  0.6 0.5 collective-permute-start
  1.8 3.2 %convolution_convert_fusion = bf16[256,2304]{1,0:T(8,128)(2,1)S(1)} fusion(bf16[256,768]{1,0:T(8,128)(2,1)} %bitcast.40, bf16[768,2304]{1,0:T(8,128)(2,1)} %param.14), kind=kOutput, calls=%fused_computation.9 | convolution fusion | flops 906559488 | bytes 5111808 | tf_op jit(solution)/shard_map/dot_general | solution.py:35
  5.0 0.0 copy-start.5
  5.1 0.0 copy-start.7
  5.1 0.9 %fusion.106 = (bf16[4,64,768]{2,1,0:T(8,128)(2,1)S(1)}, bf16[4,64,768]{2,1,0:T(8,128)(2,1)S(1)}, bf16[4,64,768]{2,1,0:T(8,128)(2,1)}) fusion(bf16[4,64,2304]{2,1,0:T(8,128)(2,1)S(1)} %bitcast.32), kind=kLoop, calls=%fused_computation.157 | loop fusion | bytes 2359296 | tf_op jit(solution)/shard_map/slice | solution.py:194
  5.9 0.1 pad_add_fusion
  6.1 2.7 %collective-permute-start.1 = (bf16[64,768]{1,0:T(8,128)(2,1)S(1)}, bf16[64,768]{1,0:T(8,128)(2,1)S(1)}, u32[]{:S(2)}, u32[]{:S(2)}) collective-permute-start(bf16[64,768]{1,0:T(8,128)(2,1)S(1)} %broadcast_select_fusion), channel_id=1, source_target_pairs={{0,8},{4,12},{8,0},{12,4},{16,24},{20,28},{24,16},{28,20},{1,9},{5... | collective-permute-start | bytes 294920 | tf_op jit(solution)/shard_map/ppermute | solution.py:60
  8.8 0.8 %fusion.39.allow_ref = f32[4,64,256]{2,1,0:T(8,128)} fusion(s32[256]{0:T(256)S(1)} %pad_add_fusion, s32[4,64]{1,0:T(4,128)S(1)} %copy-done.7, pred[256]{0:T(512)(128)(4,1)S(1)} %iota_compare_fusion.15), kind=kLoop, calls=%fused_computation.47 | loop fusion | flops 327680 | bytes 264448 | tf_op jit(solution)/shard_map/convert_element_type | solution.py:243
  9.6 2.5 %collective-permute-done.1 = bf16[64,768]{1,0:T(8,128)(2,1)S(1)} collective-permute-done((bf16[64,768]{1,0:T(8,128)(2,1)S(1)}, bf16[64,768]{1,0:T(8,128)(2,1)S(1)}, u32[]{:S(2)}, u32[]{:S(2)}) %collective-permute-start.1) | collective-permute-done | bytes 98336 | tf_op jit(solution)/shard_map/ppermute | solution.py:60
  12.2 2.8 %collective-permute-start.2 = (bf16[64,768]{1,0:T(8,128)(2,1)S(1)}, bf16[64,768]{1,0:T(8,128)(2,1)S(1)}, u32[]{:S(2)}, u32[]{:S(2)}) collective-permute-start(bf16[64,768]{1,0:T(8,128)(2,1)S(1)} %broadcast_select_fusion.1), channel_id=1, source_target_pairs={{0,16},{4,20},{8,24},{12,28},{16,0},{20,4},{24,8},{28,12},{1,17},{... | collective-permute-start | bytes 294920 | tf_op jit(solution)/shard_map/ppermute | solution.py:60
  15.0 2.4 %collective-permute-start.5 = (bf16[4,64,768]{2,1,0:T(8,128)(2,1)}, bf16[4,64,768]{2,1,0:T(8,128)(2,1)}, u32[]{:S(2)}, u32[]{:S(2)}) collective-permute-start(bf16[4,64,768]{2,1,0:T(8,128)(2,1)} %param.10), channel_id=1, source_target_pairs={{0,3},{1,2},{2,1},{3,0},{4,7},{5,6},{6,5},{7,4},{8,11},{9,10},{10,... | collective-permute-start | bytes 1179656 | tf_op jit(solution)/shard_map/ppermute | solution.py:128
  17.5 0.5 collective-permute-start.4
  18.0 0.5 collective-permute-start.3
  18.5 1.3 %collective-permute-done.2 = bf16[64,768]{1,0:T(8,128)(2,1)S(1)} collective-permute-done((bf16[64,768]{1,0:T(8,128)(2,1)S(1)}, bf16[64,768]{1,0:T(8,128)(2,1)S(1)}, u32[]{:S(2)}, u32[]{:S(2)}) %collective-permute-start.2) | collective-permute-done | bytes 98336 | tf_op jit(solution)/shard_map/ppermute | solution.py:60
  19.8 1.6 %fusion.25 = f32[64,768]{1,0:T(8,128)S(1)} fusion(bf16[64,768]{1,0:T(8,128)(2,1)S(1)} %broadcast_select_fusion.2, bf16[768,2304]{1,0:T(8,128)(2,1)} %param.14), kind=kOutput, calls=%fused_computation.28 | convolution fusion | flops 75595776 | bytes 1474560 | tf_op jit(solution)/shard_map/dot_general | solution.py:35
  21.5 2.2 %convolution_convert_fusion.2 = bf16[64,1536]{1,0:T(8,128)(2,1)S(1)} fusion(bf16[64,768]{1,0:T(8,128)(2,1)S(1)} %broadcast_select_fusion.2, bf16[768,2304]{1,0:T(8,128)(2,1)} %param.14), kind=kOutput, calls=%fused_computation.11 | convolution fusion | flops 151093248 | bytes 2654208 | tf_op jit(solution)/shard_map/dot_general | solution.py:35
  23.7 0.6 fusion.108
  24.3 0.3 fusion.19
  24.7 0.2 convolution_multiply_fusion.2
  24.8 0.1 copy-done.1
  24.9 0.7 fusion.107
  25.6 0.1 fusion.88
  25.6 0.0 collective-permute-start.7
  25.7 0.1 slice_select_fusion.2
  25.7 0.5 collective-permute-start.6
  26.2 0.8 %copy.13.skt_ref = bf16[768,64]{1,0:T(8,128)(2,1)} copy(bf16[768,64]{0,1:T(8,128)(2,1)S(1)} %get-tuple-element.18) | data formatting | bytes 196608 | tf_op jit(solution)/shard_map/transpose | solution.py:242
  27.1 0.0 collective-permute-done.7
  27.1 0.1 broadcast_select_fusion.8
  27.2 0.0 copy-start.4
  27.2 0.7 collective-permute-start.9
  27.9 0.3 fusion.59
  28.2 2.8 %collective-permute-done.9 = f32[32,24]{0,1:T(8,128)S(1)} collective-permute-done((f32[32,24]{0,1:T(8,128)S(1)}, f32[32,24]{0,1:T(8,128)S(1)}, u32[]{:S(2)}, u32[]{:S(2)}) %collective-permute-start.9) | collective-permute-done | bytes 3104 | tf_op jit(solution)/shard_map/ppermute | solution.py:60
  31.0 2.1 %collective-permute-start.11 = (f32[32,24]{0,1:T(8,128)S(1)}, f32[32,24]{0,1:T(8,128)S(1)}, u32[]{:S(2)}, u32[]{:S(2)}) collective-permute-start(f32[32,24]{0,1:T(8,128)S(1)} %pad_maximum_fusion.4), channel_id=1, source_target_pairs={{0,16},{4,20},{8,24},{12,28},{16,0},{20,4},{24,8},{28,12},{1,17},{... | collective-permute-start | bytes 9224 | tf_op jit(solution)/shard_map/ppermute | solution.py:60
  33.1 0.3 fusion.56
  33.3 2.3 %collective-permute-done.11 = f32[32,24]{0,1:T(8,128)S(1)} collective-permute-done((f32[32,24]{0,1:T(8,128)S(1)}, f32[32,24]{0,1:T(8,128)S(1)}, u32[]{:S(2)}, u32[]{:S(2)}) %collective-permute-start.11) | collective-permute-done | bytes 3104 | tf_op jit(solution)/shard_map/ppermute | solution.py:60
  35.7 0.3 fusion.55
  36.0 0.3 fusion.54
  36.2 0.0 collective-permute-done.6
  36.2 0.3 add_convert_fusion
  36.5 1.2 %collective-permute-start.8 = (bf16[32,768]{1,0:T(8,128)(2,1)S(1)}, bf16[32,768]{1,0:T(8,128)(2,1)S(1)}, u32[]{:S(2)}, u32[]{:S(2)}) collective-permute-start(bf16[32,768]{1,0:T(8,128)(2,1)S(1)} %add_convert_fusion), channel_id=1, source_target_pairs={{0,8},{4,12},{8,0},{12,4},{16,24},{20,28},{24,16},{28,20},{1,9},{5... | collective-permute-start | bytes 147464 | tf_op jit(solution)/shard_map/ppermute | solution.py:60
  37.7 0.3 fusion.53
  37.9 2.7 %collective-permute-done.8 = bf16[32,768]{1,0:T(8,128)(2,1)S(1)} collective-permute-done((bf16[32,768]{1,0:T(8,128)(2,1)S(1)}, bf16[32,768]{1,0:T(8,128)(2,1)S(1)}, u32[]{:S(2)}, u32[]{:S(2)}) %collective-permute-start.8) | collective-permute-done | bytes 49184 | tf_op jit(solution)/shard_map/ppermute | solution.py:60
  40.6 0.3 fusion.44
  40.9 2.1 %collective-permute-start.10 = (bf16[32,768]{1,0:T(8,128)(2,1)S(1)}, bf16[32,768]{1,0:T(8,128)(2,1)S(1)}, u32[]{:S(2)}, u32[]{:S(2)}) collective-permute-start(bf16[32,768]{1,0:T(8,128)(2,1)S(1)} %fusion.44), channel_id=1, source_target_pairs={{0,16},{4,20},{8,24},{12,28},{16,0},{20,4},{24,8},{28,12},{1,17},{... | collective-permute-start | bytes 147464 | tf_op jit(solution)/shard_map/ppermute | solution.py:60
  43.0 0.2 fusion.52
  43.2 2.8 %collective-permute-done.10 = bf16[32,768]{1,0:T(8,128)(2,1)S(1)} collective-permute-done((bf16[32,768]{1,0:T(8,128)(2,1)S(1)}, bf16[32,768]{1,0:T(8,128)(2,1)S(1)}, u32[]{:S(2)}, u32[]{:S(2)}) %collective-permute-start.10) | collective-permute-done | bytes 49184 | tf_op jit(solution)/shard_map/ppermute | solution.py:60
  46.0 1.7 %fusion.28 = bf16[32,768]{1,0:T(8,128)(2,1)} fusion(f32[32,768]{1,0:T(8,128)S(1)} %fusion.53, f32[32,768]{1,0:T(8,128)S(1)} %fusion.55, bf16[32,768]{1,0:T(8,128)(2,1)S(1)} %collective-permute-done.10, bf16[32,768]{1,0:T(8,128)(2,1)S(1)} %fusion.44, f32[32,768]{1,0:T(8,128)S(1)} %fusion.54, f32[32,768]{1,0:T(8,128)S(1)} %fusion.52, ...), kind=kOutput, calls=%fused_computation.30 | convolution fusion | flops 3896064 | bytes 692226 | tf_op jit(solution)/shard_map/dot_general | solution.py:54
  47.7 1.3 %pad_maximum_fusion.1 = bf16[4,192,768]{2,1,0:T(8,128)(2,1)S(1)} fusion(bf16[4,64,768]{2,1,0:T(8,128)(2,1)} %collective-permute-done.5, bf16[4,64,768]{2,1,0:T(8,128)(2,1)} %collective-permute-done.4, bf16[4,64,768]{2,1,0:T(8,128)(2,1)} %collective-permute-done.3), kind=kLoop, calls=%fused_computation.24 | loop fusion | flops 3538944 | bytes 2359296 | tf_op jit(solution)/shard_map/concatenate | solution.py:227
  49.0 2.0 %convolution_convert_fusion.1 = bf16[768,1536]{1,0:T(8,128)(2,1)S(1)} fusion(bf16[768,768]{1,0:T(8,128)(2,1)S(1)} %bitcast.36, bf16[768,2304]{1,0:T(8,128)(2,1)S(1)} %copy-done.4), kind=kOutput, calls=%fused_computation.10 | convolution fusion | flops 1813118976 | bytes 5898240 | tf_op jit(solution)/shard_map/dot_general | solution.py:35
  51.0 0.2 fusion.105
  51.2 1.4 %maximum_bitcast_fusion = (bf16[4,768,256]{1,2,0:T(8,128)(2,1)S(1)}, bf16[4,256,768]{2,1,0:T(8,128)(2,1)}) fusion(bf16[4,192,768]{2,1,0:T(8,128)(2,1)S(1)} %get-tuple-element.13, bf16[4,64,768]{2,1,0:T(8,128)(2,1)S(1)} %get-tuple-element.15, bf16[4,192,768]{2,1,0:T(8,128)(2,1)S(1)} %get-tuple-element.12, bf16[4,64,768]{2,1,0:T(8,128)(2,1)S(1)} %get-tuple-element.14), kind=kLoop, calls=%fused_computation.19 | loop fusion | flops 6291456 | bytes 6291456 | tf_op jit(solution)/shard_map/transpose | solution.py:242
  52.6 1.6 %copy.12.kt_ref = bf16[4,768,256]{2,1,0:T(8,128)(2,1)} copy(bf16[4,768,256]{1,2,0:T(8,128)(2,1)S(1)} %get-tuple-element.29) | data formatting | bytes 3145728 | tf_op jit(solution)/shard_map/transpose | solution.py:242
  54.2 14.2 %shard_map.113 = bf16[4,64,768]{2,1,0:T(8,128)(2,1)} custom-call(bf16[4,64,768]{2,1,0:T(8,128)(2,1)} %get-tuple-element.16.q_ref, bf16[4,768,256]{2,1,0:T(8,128)(2,1)} %copy.12.kt_ref, bf16[4,256,768]{2,1,0:T(8,128)(2,1)} %get-tuple-element.30.v_ref, bf16[768,64]{1,0:T(8,128)(2,1)} %copy.13.skt_ref, bf16[64,768]{1,0:T(8,128)(2,1)} %get-tuple-element.17.sv_ref, ...), custom_call_target="tpu_custom_call" | custom-call | tf_op jit(solution)/shard_map/pallas_call | solution.py:163
  68.3 0.9 %maximum_select_fusion = bf16[64,768]{1,0:T(8,128)(2,1)S(1)} fusion(bf16[32,768]{1,0:T(8,128)(2,1)} %collective-permute-done.12, bf16[32,768]{1,0:T(8,128)(2,1)} %fusion.28, pred[]{:T(512)S(6)} %eq.90), kind=kLoop, calls=%fused_computation.63 | loop fusion | flops 442368 | bytes 196609 | tf_op jit(solution)/shard_map/jit(_where)/select_n | solution.py:115
  69.2 0.0 copy-start.9
  69.3 1.7 %fusion.109 = (f32[320]{0:T(512)S(1)}, f32[320,768]{1,0:T(8,128)S(1)}) fusion(bf16[768,768]{1,0:T(8,128)(2,1)S(1)} %copy-done, bf16[64,768]{1,0:T(8,128)(2,1)S(1)} %maximum_select_fusion, bf16[256,768]{1,0:T(8,128)(2,1)} %bitcast.37, bf16[64,768]{1,0:T(8,128)(2,1)S(1)} %copy-done.3, bf16[256,768]{1,0:T(8,128)(2,1)S(1)} %bitcast.41), kind=kOutput, calls=%fused_computation.160 | convolution fusion | flops 379944640 | bytes 3147008 | tf_op jit(solution)/shard_map/dot_general | solution.py:25
  70.9 0.3 multiply_reduce_fusion.1
  71.2 0.0 copy-start.6
  71.2 7.4 %fusion.110 = (f32[320]{0:T(512)S(1)}, f32[320,768]{1,0:T(8,128)S(1)}) fusion(bf16[3072,768]{1,0:T(8,128)(2,1)} %param.18, bf16[768,3072]{1,0:T(8,128)(2,1)} %param.17, f32[320,768]{1,0:T(8,128)S(1)} %get-tuple-element.26, f32[768]{0:T(1024)S(1)} %copy-done.9, f32[320]{0:T(512)S(1)} %add_rsqrt_fusion.1, f32[320]{0:T(512)S(1)} %broadcast_multiply_fusion.1), kind=kOutput, calls=%fused_computation.161 | convolution fusion | flops 3031449344 | bytes 11410176 | tf_op jit(solution)/shard_map/dot_general | solution.py:30
  78.7 0.3 multiply_reduce_fusion
  79.0 0.2 multiply_convert_fusion
  79.2 0.8 slice.159
  79.9 0.6 slice.160
  (42 shorter events, 0.2 us)
Async XLA Ops:
  0.6 68.6 %copy-start = (bf16[768,768]{1,0:T(8,128)(2,1)S(1)}, bf16[768,768]{1,0:T(8,128)(2,1)}, u32[]{:S(2)}) copy-start(bf16[768,768]{1,0:T(8,128)(2,1)} %param.15) | copy-start | bytes 3538948
  0.6 5.4 %collective-permute-start = (bf16[64,768]{1,0:T(8,128)(2,1)}, bf16[64,768]{1,0:T(8,128)(2,1)S(1)}, u32[]{:S(2)}, u32[]{:S(2)}) collective-permute-start(bf16[64,768]{1,0:T(8,128)(2,1)} %bitcast.39), channel_id=1, source_target_pairs={{0,4},{4,0},{8,12},{12,8},{16,20},{20,16},{24,28},{28,24},{1,5},{5... | collective-permute-start | bytes 294920 | tf_op jit(solution)/shard_map/ppermute | solution.py:60
  5.0 1.0 %copy-start.5 = (bf16[1,64,768]{2,1,0:T(8,128)(2,1)S(1)}, bf16[1,64,768]{2,1,0:T(8,128)(2,1)}, u32[]{:S(2)}) copy-start(bf16[1,64,768]{2,1,0:T(8,128)(2,1)} %param.11) | copy-start | bytes 294916
  5.1 3.7 %copy-start.7 = (s32[4,64]{1,0:T(4,128)S(1)}, s32[4,64]{1,0:T(4,128)}, u32[]{:S(2)}) copy-start(s32[4,64]{1,0:T(4,128)} %param.13) | copy-start | bytes 3076
  6.1 6.1 %collective-permute-start.1 = (bf16[64,768]{1,0:T(8,128)(2,1)S(1)}, bf16[64,768]{1,0:T(8,128)(2,1)S(1)}, u32[]{:S(2)}, u32[]{:S(2)}) collective-permute-start(bf16[64,768]{1,0:T(8,128)(2,1)S(1)} %broadcast_select_fusion), channel_id=1, source_target_pairs={{0,8},{4,12},{8,0},{12,4},{16,24},{20,28},{24,16},{28,20},{1,9},{5... | collective-permute-start | bytes 294920 | tf_op jit(solution)/shard_map/ppermute | solution.py:60
  12.2 7.6 %collective-permute-start.2 = (bf16[64,768]{1,0:T(8,128)(2,1)S(1)}, bf16[64,768]{1,0:T(8,128)(2,1)S(1)}, u32[]{:S(2)}, u32[]{:S(2)}) collective-permute-start(bf16[64,768]{1,0:T(8,128)(2,1)S(1)} %broadcast_select_fusion.1), channel_id=1, source_target_pairs={{0,16},{4,20},{8,24},{12,28},{16,0},{20,4},{24,8},{28,12},{1,17},{... | collective-permute-start | bytes 294920 | tf_op jit(solution)/shard_map/ppermute | solution.py:60
  15.0 32.7 %collective-permute-start.5 = (bf16[4,64,768]{2,1,0:T(8,128)(2,1)}, bf16[4,64,768]{2,1,0:T(8,128)(2,1)}, u32[]{:S(2)}, u32[]{:S(2)}) collective-permute-start(bf16[4,64,768]{2,1,0:T(8,128)(2,1)} %param.10), channel_id=1, source_target_pairs={{0,3},{1,2},{2,1},{3,0},{4,7},{5,6},{6,5},{7,4},{8,11},{9,10},{10,... | collective-permute-start | bytes 1179656 | tf_op jit(solution)/shard_map/ppermute | solution.py:128
  17.5 30.2 %collective-permute-start.4 = (bf16[4,64,768]{2,1,0:T(8,128)(2,1)}, bf16[4,64,768]{2,1,0:T(8,128)(2,1)}, u32[]{:S(2)}, u32[]{:S(2)}) collective-permute-start(bf16[4,64,768]{2,1,0:T(8,128)(2,1)} %param.10), channel_id=1, source_target_pairs={{0,2},{1,3},{2,0},{3,1},{4,6},{5,7},{6,4},{7,5},{8,10},{9,11},{10,... | collective-permute-start | bytes 1179656 | tf_op jit(solution)/shard_map/ppermute | solution.py:128
  18.0 29.7 %collective-permute-start.3 = (bf16[4,64,768]{2,1,0:T(8,128)(2,1)}, bf16[4,64,768]{2,1,0:T(8,128)(2,1)}, u32[]{:S(2)}, u32[]{:S(2)}) collective-permute-start(bf16[4,64,768]{2,1,0:T(8,128)(2,1)} %param.10), channel_id=1, source_target_pairs={{0,1},{1,0},{2,3},{3,2},{4,5},{5,4},{6,7},{7,6},{8,9},{9,8},{10,11... | collective-permute-start | bytes 1179656 | tf_op jit(solution)/shard_map/ppermute | solution.py:128
  19.8 4.5 %copy-start.2 = (bf16[64,768]{1,0:T(8,128)(2,1)}, bf16[64,768]{1,0:T(8,128)(2,1)S(1)}, u32[]{:S(2)}) copy-start(bf16[64,768]{1,0:T(8,128)(2,1)S(1)} %broadcast_select_fusion.2) | copy-start | bytes 294916
  23.7 1.2 %copy-start.1 = (bf16[64,1536]{1,0:T(8,128)(2,1)}, bf16[64,1536]{1,0:T(8,128)(2,1)S(1)}, u32[]{:S(2)}) copy-start(bf16[64,1536]{1,0:T(8,128)(2,1)S(1)} %convolution_convert_fusion.2) | copy-start | bytes 589828
  25.6 1.4 %collective-permute-start.7 = (f32[32,24]{0,1:T(8,128)S(1)}, f32[32,24]{0,1:T(8,128)S(1)}, u32[]{:S(2)}, u32[]{:S(2)}) collective-permute-start(f32[32,24]{0,1:T(8,128)S(1)} %fusion.88), channel_id=1, source_target_pairs={{0,4},{4,0},{8,12},{12,8},{16,20},{20,16},{24,28},{28,24},{1,5},{5... | collective-permute-start | bytes 9224 | tf_op jit(solution)/shard_map/ppermute | solution.py:60
  25.7 10.5 %collective-permute-start.6 = (f32[32,768]{1,0:T(8,128)S(1)}, f32[32,768]{1,0:T(8,128)S(1)}, u32[]{:S(2)}, u32[]{:S(2)}) collective-permute-start(f32[32,768]{1,0:T(8,128)S(1)} %slice_select_fusion), channel_id=1, source_target_pairs={{0,4},{4,0},{8,12},{12,8},{16,20},{20,16},{24,28},{28,24},{1,5},{5... | collective-permute-start | bytes 294920 | tf_op jit(solution)/shard_map/ppermute | solution.py:60
  27.2 21.8 %copy-start.4 = (bf16[768,2304]{1,0:T(8,128)(2,1)S(1)}, bf16[768,2304]{1,0:T(8,128)(2,1)}, u32[]{:S(2)}) copy-start(bf16[768,2304]{1,0:T(8,128)(2,1)} %param.14) | copy-start | bytes 10616836
  27.2 3.8 %collective-permute-start.9 = (f32[32,24]{0,1:T(8,128)S(1)}, f32[32,24]{0,1:T(8,128)S(1)}, u32[]{:S(2)}, u32[]{:S(2)}) collective-permute-start(f32[32,24]{0,1:T(8,128)S(1)} %pad_maximum_fusion.3), channel_id=1, source_target_pairs={{0,8},{4,12},{8,0},{12,4},{16,24},{20,28},{24,16},{28,20},{1,9},{5... | collective-permute-start | bytes 9224 | tf_op jit(solution)/shard_map/ppermute | solution.py:60
  31.0 4.7 %collective-permute-start.11 = (f32[32,24]{0,1:T(8,128)S(1)}, f32[32,24]{0,1:T(8,128)S(1)}, u32[]{:S(2)}, u32[]{:S(2)}) collective-permute-start(f32[32,24]{0,1:T(8,128)S(1)} %pad_maximum_fusion.4), channel_id=1, source_target_pairs={{0,16},{4,20},{8,24},{12,28},{16,0},{20,4},{24,8},{28,12},{1,17},{... | collective-permute-start | bytes 9224 | tf_op jit(solution)/shard_map/ppermute | solution.py:60
  36.5 4.2 %collective-permute-start.8 = (bf16[32,768]{1,0:T(8,128)(2,1)S(1)}, bf16[32,768]{1,0:T(8,128)(2,1)S(1)}, u32[]{:S(2)}, u32[]{:S(2)}) collective-permute-start(bf16[32,768]{1,0:T(8,128)(2,1)S(1)} %add_convert_fusion), channel_id=1, source_target_pairs={{0,8},{4,12},{8,0},{12,4},{16,24},{20,28},{24,16},{28,20},{1,9},{5... | collective-permute-start | bytes 147464 | tf_op jit(solution)/shard_map/ppermute | solution.py:60
  40.9 5.1 %collective-permute-start.10 = (bf16[32,768]{1,0:T(8,128)(2,1)S(1)}, bf16[32,768]{1,0:T(8,128)(2,1)S(1)}, u32[]{:S(2)}, u32[]{:S(2)}) collective-permute-start(bf16[32,768]{1,0:T(8,128)(2,1)S(1)} %fusion.44), channel_id=1, source_target_pairs={{0,16},{4,20},{8,24},{12,28},{16,0},{20,4},{24,8},{28,12},{1,17},{... | collective-permute-start | bytes 147464 | tf_op jit(solution)/shard_map/ppermute | solution.py:60
  47.7 20.7 %collective-permute-start.12 = (bf16[32,768]{1,0:T(8,128)(2,1)}, bf16[32,768]{1,0:T(8,128)(2,1)}, u32[]{:S(2)}, u32[]{:S(2)}) collective-permute-start(bf16[32,768]{1,0:T(8,128)(2,1)} %fusion.28), channel_id=1, source_target_pairs={{0,4},{4,0},{8,12},{12,8},{16,20},{20,16},{24,28},{28,24},{1,5},{5... | collective-permute-start | bytes 147464 | tf_op jit(solution)/shard_map/ppermute | solution.py:60
  54.2 15.1 %copy-start.3 = (bf16[64,768]{1,0:T(8,128)(2,1)S(1)}, bf16[64,768]{1,0:T(8,128)(2,1)}, u32[]{:S(2)}) copy-start(bf16[64,768]{1,0:T(8,128)(2,1)} %copy-done.2) | copy-start | bytes 294916
  54.2 15.1 %copy-start.8 = (bf16[4,64,768]{2,1,0:T(8,128)(2,1)S(1)}, bf16[4,64,768]{2,1,0:T(8,128)(2,1)}, u32[]{:S(2)}) copy-start(bf16[4,64,768]{2,1,0:T(8,128)(2,1)} %param.10) | copy-start | bytes 1179652
  69.2 2.0 %copy-start.9 = (f32[768]{0:T(1024)S(1)}, f32[768]{0:T(1024)}, u32[]{:S(2)}) copy-start(f32[768]{0:T(1024)} %param.16) | copy-start | bytes 9220
  71.2 7.7 %copy-start.6 = (f32[768]{0:T(1024)S(1)}, f32[768]{0:T(1024)}, u32[]{:S(2)}) copy-start(f32[768]{0:T(1024)} %param.19) | copy-start | bytes 9220

commit v14 on v12

--- a/solution.py
+++ b/solution.py
@@ -130,31 +130,32 @@
 
 
 def row_kernel(q_ref, k_ref, v_ref, sk_ref, sv_ref, allow_ref, o_ref, *, scale):
+    rows = q_ref.shape[1]
     allow = allow_ref[0] > 0.5
+    allow = jnp.concatenate([allow, allow], axis=0)
     lane = lax.broadcasted_iota(jnp.int32, (1, 2 * HEAD_DIM), 1)
     low = lane < HEAD_DIM
     nt = (((1,), (1,)), ((), ()))
     for pair in range(HEADS // 2):
         cols = slice(pair * 2 * HEAD_DIM, (pair + 1) * 2 * HEAD_DIM)
-        q = q_ref[0, :, cols]
+        q = q_ref[0, :, cols] * scale
+        zero = jnp.zeros_like(q)
+        qh = jnp.concatenate([jnp.where(low, q, zero), jnp.where(low, zero, q)], axis=0)
         k = k_ref[0, :, cols]
         v = v_ref[0, :, cols]
         sk = sk_ref[:, cols]
         sv = sv_ref[:, cols]
-        outs = []
-        for side in (low, jnp.logical_not(low)):
-            qh = jnp.where(side, q, jnp.zeros_like(q))
-            s = lax.dot_general(qh, k, nt, preferred_element_type=jnp.float32) * scale
-            s = jnp.where(allow, s, -1e30)
-            ts = lax.dot_general(qh, sk, nt, preferred_element_type=jnp.float32) * scale
-            top = jnp.maximum(s.max(-1, keepdims=True), ts.max(-1, keepdims=True))
-            e = jnp.exp(s - top)
-            te = jnp.exp(ts - top)
-            tot = e.sum(-1, keepdims=True) + te.sum(-1, keepdims=True)
-            acc = jnp.dot(e.astype(jnp.bfloat16), v, preferred_element_type=jnp.float32)
-            acc = acc + jnp.dot(te.astype(jnp.bfloat16), sv, preferred_element_type=jnp.float32)
-            outs.append(acc / tot)
-        o_ref[0, :, cols] = jnp.where(low, outs[0], outs[1]).astype(o_ref.dtype)
+        s = lax.dot_general(qh, k, nt, preferred_element_type=jnp.float32)
+        s = jnp.where(allow, s, -1e30)
+        ts = lax.dot_general(qh, sk, nt, preferred_element_type=jnp.float32)
+        top = jnp.maximum(s.max(-1, keepdims=True), ts.max(-1, keepdims=True))
+        e = jnp.exp(s - top)
+        te = jnp.exp(ts - top)
+        tot = e.sum(-1, keepdims=True) + te.sum(-1, keepdims=True)
+        acc = jnp.dot(e.astype(jnp.bfloat16), v, preferred_element_type=jnp.float32)
+        acc = acc + jnp.dot(te.astype(jnp.bfloat16), sv, preferred_element_type=jnp.float32)
+        out = jnp.where(low, acc[:rows] / tot[:rows], acc[rows:] / tot[rows:])
+        o_ref[0, :, cols] = out.astype(o_ref.dtype)
 
 
 def row_attention(q, k, v, sk, sv, allow):

time: 76.8 us -> 70.7 us (0.921)
  Pallas kernels: 15 us -> 8.88 us
    pallas_call x1, Pallas kernels: 15 us -> 8.88 us  [row_attention(): pl.pallas_call(kern, grid=(rows,), in_specs=[pl.BlockSpec((1, nq, width),...]
  transfers between devices with their start and end apart: 13 -> 13, of which waited for: 7 -> 7; matrix products, arithmetic and copies ran while one was open for 23% -> 25% of each run, Pallas kernels for 20% -> 13%
where the time goes in v14:
time: 70.7 us; the launch traced here: 70.4 us
  matrix products  21.5 us (30%)
  starting transfers between devices  16.2 us (23%)
  waiting for transfers between devices  15 us (21%)
  Pallas kernels  8.88 us (13%)
  other arithmetic  3.96 us (6%)
  local copies, waits for them, and re-layouts  3.26 us (5%)
  between operations  1.61 us (2%)
    ppermute x10, waiting for transfers between devices, partner(): return lax.ppermute(value, axis, [(i, i ^ step) for i in range(count)])  15 us
    ppermute x10, starting transfers between devices, partner(): return lax.ppermute(value, axis, [(i, i ^ step) for i in range(count)])  12.7 us
    dot_general x4, matrix products, project(): jnp.dot(values, weight, preferred_element_type=jnp.float32)  9.03 us
    pallas_call x1, Pallas kernels, row_attention(): pl.pallas_call(kern, grid=(rows,), in_specs=[pl.BlockSpec((1, nq, width),...  8.88 us
    dot_general x1, matrix products, finish(): outer_out = jnp.dot(inner_act, w_down, preferred_element_type=jnp.float32)  7.43 us
    ppermute x3, starting transfers between devices, fan_out(): got.append((source, lax.ppermute(value, axis, pairs)))  3.49 us
    dot_general x10, matrix products, head_spread(): jnp.dot(flat, head_matrix(), precision=lax.Precision.HIGHEST, preferred_e...  2.56 us
    concatenate x1, other arithmetic, local(): row_keys = jnp.concatenate([own_keys, other_kv[:, :, :model_width]], axis=1)  1.84 us
  transfers between devices with their start and end apart: 13, of which 7 were waited for; matrix products, arithmetic and copies ran while one was open for 25% of the time, Pallas kernels for 13%

profile of v14, /device:TPU:0, one launch (start us, length us, event | category | flops | bytes accessed | tf_op | source)
XLA Modules:
  0.0 70.4 jit_solution(18028723681725082800)
XLA Ops:
  0.6 0.0 copy-start
  0.6 0.5 collective-permute-start
  1.8 3.2 %convolution_convert_fusion = bf16[256,2304]{1,0:T(8,128)(2,1)S(1)} fusion(bf16[256,768]{1,0:T(8,128)(2,1)} %bitcast.36, bf16[768,2304]{1,0:T(8,128)(2,1)} %param.14), kind=kOutput, calls=%fused_computation.9 | convolution fusion | flops 906559488 | bytes 5111808 | tf_op jit(solution)/shard_map/dot_general | solution.py:35
  5.0 0.0 copy-start.2
  5.1 0.0 copy-start.4
  5.1 0.9 %fusion.106 = (bf16[4,64,768]{2,1,0:T(8,128)(2,1)S(1)}, bf16[4,64,768]{2,1,0:T(8,128)(2,1)S(1)}, bf16[4,64,768]{2,1,0:T(8,128)(2,1)}) fusion(bf16[4,64,2304]{2,1,0:T(8,128)(2,1)S(1)} %bitcast.28), kind=kLoop, calls=%fused_computation.156 | loop fusion | bytes 2359296 | tf_op jit(solution)/shard_map/slice | solution.py:196
  5.9 0.1 pad_add_fusion
  6.0 0.0 collective-permute-done
  6.1 2.7 %collective-permute-start.1 = (bf16[64,768]{1,0:T(8,128)(2,1)S(1)}, bf16[64,768]{1,0:T(8,128)(2,1)S(1)}, u32[]{:S(2)}, u32[]{:S(2)}) collective-permute-start(bf16[64,768]{1,0:T(8,128)(2,1)S(1)} %broadcast_select_fusion), channel_id=1, source_target_pairs={{0,8},{4,12},{8,0},{12,4},{16,24},{20,28},{24,16},{28,20},{1,9},{5... | collective-permute-start | bytes 294920 | tf_op jit(solution)/shard_map/ppermute | solution.py:60
  8.8 0.8 %fusion.39.allow_ref = f32[4,64,256]{2,1,0:T(8,128)} fusion(s32[256]{0:T(256)S(1)} %pad_add_fusion, s32[4,64]{1,0:T(4,128)S(1)} %copy-done.4, pred[256]{0:T(512)(128)(4,1)S(1)} %iota_compare_fusion.15), kind=kLoop, calls=%fused_computation.47 | loop fusion | flops 327680 | bytes 264448 | tf_op jit(solution)/shard_map/convert_element_type | solution.py:244
  9.6 2.6 %collective-permute-done.1 = bf16[64,768]{1,0:T(8,128)(2,1)S(1)} collective-permute-done((bf16[64,768]{1,0:T(8,128)(2,1)S(1)}, bf16[64,768]{1,0:T(8,128)(2,1)S(1)}, u32[]{:S(2)}, u32[]{:S(2)}) %collective-permute-start.1) | collective-permute-done | bytes 98336 | tf_op jit(solution)/shard_map/ppermute | solution.py:60
  12.2 2.8 %collective-permute-start.2 = (bf16[64,768]{1,0:T(8,128)(2,1)S(1)}, bf16[64,768]{1,0:T(8,128)(2,1)S(1)}, u32[]{:S(2)}, u32[]{:S(2)}) collective-permute-start(bf16[64,768]{1,0:T(8,128)(2,1)S(1)} %broadcast_select_fusion.1), channel_id=1, source_target_pairs={{0,16},{4,20},{8,24},{12,28},{16,0},{20,4},{24,8},{28,12},{1,17},{... | collective-permute-start | bytes 294920 | tf_op jit(solution)/shard_map/ppermute | solution.py:60
  15.0 2.4 %collective-permute-start.5 = (bf16[4,64,768]{2,1,0:T(8,128)(2,1)}, bf16[4,64,768]{2,1,0:T(8,128)(2,1)S(1)}, u32[]{:S(2)}, u32[]{:S(2)}) collective-permute-start(bf16[4,64,768]{2,1,0:T(8,128)(2,1)} %param.10), channel_id=1, source_target_pairs={{0,3},{1,2},{2,1},{3,0},{4,7},{5,6},{6,5},{7,4},{8,11},{9,10},{10,... | collective-permute-start | bytes 1179656 | tf_op jit(solution)/shard_map/ppermute | solution.py:128
  17.5 0.5 collective-permute-start.4
  18.0 0.5 collective-permute-start.3
  18.5 1.3 %collective-permute-done.2 = bf16[64,768]{1,0:T(8,128)(2,1)S(1)} collective-permute-done((bf16[64,768]{1,0:T(8,128)(2,1)S(1)}, bf16[64,768]{1,0:T(8,128)(2,1)S(1)}, u32[]{:S(2)}, u32[]{:S(2)}) %collective-permute-start.2) | collective-permute-done | bytes 98336 | tf_op jit(solution)/shard_map/ppermute | solution.py:60
  19.8 1.6 %fusion.25 = f32[64,768]{1,0:T(8,128)S(1)} fusion(bf16[64,768]{1,0:T(8,128)(2,1)S(1)} %broadcast_select_fusion.2, bf16[768,2304]{1,0:T(8,128)(2,1)} %param.14), kind=kOutput, calls=%fused_computation.28 | convolution fusion | flops 75595776 | bytes 1474560 | tf_op jit(solution)/shard_map/dot_general | solution.py:35
  21.4 2.2 %convolution_convert_fusion.2 = bf16[64,1536]{1,0:T(8,128)(2,1)S(1)} fusion(bf16[64,768]{1,0:T(8,128)(2,1)S(1)} %broadcast_select_fusion.2, bf16[768,2304]{1,0:T(8,128)(2,1)} %param.14), kind=kOutput, calls=%fused_computation.11 | convolution fusion | flops 151093248 | bytes 2654208 | tf_op jit(solution)/shard_map/dot_general | solution.py:35
  23.6 0.6 fusion.108
  24.3 0.3 fusion.19
  24.6 0.2 convolution_multiply_fusion.2
  24.7 0.8 %fusion.107 = (bf16[64,768]{1,0:T(8,128)(2,1)}, bf16[64,768]{1,0:T(8,128)(2,1)}) fusion(bf16[64,1536]{1,0:T(8,128)(2,1)S(1)} %convolution_convert_fusion.2), kind=kLoop, calls=%fused_computation.157 | loop fusion | bytes 393216 | tf_op jit(solution)/shard_map/slice | solution.py:201
  25.5 0.1 fusion.87
  25.6 0.0 collective-permute-start.7
  25.6 0.1 slice_select_fusion.2
  25.7 0.5 collective-permute-start.6
  26.2 0.6 collective-permute-done.7
  26.8 0.1 broadcast_select_fusion.8
  26.9 0.0 copy-start.1
  26.9 0.7 %collective-permute-start.9 = (f32[32,24]{0,1:T(8,128)S(1)}, f32[32,24]{0,1:T(8,128)S(1)}, u32[]{:S(2)}, u32[]{:S(2)}) collective-permute-start(f32[32,24]{0,1:T(8,128)S(1)} %pad_maximum_fusion.4), channel_id=1, source_target_pairs={{0,8},{4,12},{8,0},{12,4},{16,24},{20,28},{24,16},{28,20},{1,9},{5... | collective-permute-start | bytes 9224 | tf_op jit(solution)/shard_map/ppermute | solution.py:60
  27.6 0.3 fusion.58
  27.9 2.8 %collective-permute-done.9 = f32[32,24]{0,1:T(8,128)S(1)} collective-permute-done((f32[32,24]{0,1:T(8,128)S(1)}, f32[32,24]{0,1:T(8,128)S(1)}, u32[]{:S(2)}, u32[]{:S(2)}) %collective-permute-start.9) | collective-permute-done | bytes 3104 | tf_op jit(solution)/shard_map/ppermute | solution.py:60
  30.7 2.1 %collective-permute-start.11 = (f32[32,24]{0,1:T(8,128)S(1)}, f32[32,24]{0,1:T(8,128)S(1)}, u32[]{:S(2)}, u32[]{:S(2)}) collective-permute-start(f32[32,24]{0,1:T(8,128)S(1)} %pad_maximum_fusion.5), channel_id=1, source_target_pairs={{0,16},{4,20},{8,24},{12,28},{16,0},{20,4},{24,8},{28,12},{1,17},{... | collective-permute-start | bytes 9224 | tf_op jit(solution)/shard_map/ppermute | solution.py:60
  32.8 0.3 fusion.55
  33.1 2.3 %collective-permute-done.11 = f32[32,24]{0,1:T(8,128)S(1)} collective-permute-done((f32[32,24]{0,1:T(8,128)S(1)}, f32[32,24]{0,1:T(8,128)S(1)}, u32[]{:S(2)}, u32[]{:S(2)}) %collective-permute-start.11) | collective-permute-done | bytes 3104 | tf_op jit(solution)/shard_map/ppermute | solution.py:60
  35.4 0.2 fusion.54
  35.7 0.3 fusion.53
  35.9 0.0 collective-permute-done.6
  35.9 0.3 add_convert_fusion
  36.2 1.2 %collective-permute-start.8 = (bf16[32,768]{1,0:T(8,128)(2,1)S(1)}, bf16[32,768]{1,0:T(8,128)(2,1)S(1)}, u32[]{:S(2)}, u32[]{:S(2)}) collective-permute-start(bf16[32,768]{1,0:T(8,128)(2,1)S(1)} %add_convert_fusion), channel_id=1, source_target_pairs={{0,8},{4,12},{8,0},{12,4},{16,24},{20,28},{24,16},{28,20},{1,9},{5... | collective-permute-start | bytes 147464 | tf_op jit(solution)/shard_map/ppermute | solution.py:60
  37.4 0.3 fusion.52
  37.6 2.7 %collective-permute-done.8 = bf16[32,768]{1,0:T(8,128)(2,1)S(1)} collective-permute-done((bf16[32,768]{1,0:T(8,128)(2,1)S(1)}, bf16[32,768]{1,0:T(8,128)(2,1)S(1)}, u32[]{:S(2)}, u32[]{:S(2)}) %collective-permute-start.8) | collective-permute-done | bytes 49184 | tf_op jit(solution)/shard_map/ppermute | solution.py:60
  40.3 0.3 fusion.44
  40.6 2.1 %collective-permute-start.10 = (bf16[32,768]{1,0:T(8,128)(2,1)S(1)}, bf16[32,768]{1,0:T(8,128)(2,1)S(1)}, u32[]{:S(2)}, u32[]{:S(2)}) collective-permute-start(bf16[32,768]{1,0:T(8,128)(2,1)S(1)} %fusion.44), channel_id=1, source_target_pairs={{0,16},{4,20},{8,24},{12,28},{16,0},{20,4},{24,8},{28,12},{1,17},{... | collective-permute-start | bytes 147464 | tf_op jit(solution)/shard_map/ppermute | solution.py:60
  42.7 0.2 fusion.51
  42.9 2.8 %collective-permute-done.10 = bf16[32,768]{1,0:T(8,128)(2,1)S(1)} collective-permute-done((bf16[32,768]{1,0:T(8,128)(2,1)S(1)}, bf16[32,768]{1,0:T(8,128)(2,1)S(1)}, u32[]{:S(2)}, u32[]{:S(2)}) %collective-permute-start.10) | collective-permute-done | bytes 49184 | tf_op jit(solution)/shard_map/ppermute | solution.py:60
  45.7 0.3 fusion.28
  45.9 0.1 collective-permute-start.12
  46.0 0.0 collective-permute-done.4
  46.0 0.0 collective-permute-done.3
  46.0 0.1 pad_maximum_fusion.2
  46.1 2.0 %convolution_convert_fusion.1 = bf16[768,1536]{1,0:T(8,128)(2,1)S(1)} fusion(bf16[768,768]{1,0:T(8,128)(2,1)S(1)} %bitcast.32, bf16[768,2304]{1,0:T(8,128)(2,1)S(1)} %copy-done.1), kind=kOutput, calls=%fused_computation.10 | convolution fusion | flops 1813118976 | bytes 5898240 | tf_op jit(solution)/shard_map/dot_general | solution.py:35
  48.2 0.2 fusion.105
  48.3 1.8 %pad_maximum_fusion = (bf16[4,256,768]{2,1,0:T(8,128)(2,1)}, bf16[4,256,768]{2,1,0:T(8,128)(2,1)}) fusion(bf16[4,192,768]{2,1,0:T(8,128)(2,1)S(1)} %get-tuple-element.13, bf16[4,64,768]{2,1,0:T(8,128)(2,1)S(1)} %get-tuple-element.15, bf16[4,192,768]{2,1,0:T(8,128)(2,1)S(1)} %get-tuple-element.12, bf16[4,64,768]{2,1,0:T(8,128)(2,1)S(1)} %get-tuple-element.14), kind=kLoop, calls=%fused_computation.19 | loop fusion | flops 6291456 | bytes 6291456 | tf_op jit(solution)/shard_map/concatenate | solution.py:233
  50.2 8.9 %shard_map.113 = bf16[4,64,768]{2,1,0:T(8,128)(2,1)} custom-call(bf16[4,64,768]{2,1,0:T(8,128)(2,1)} %get-tuple-element.16.q_ref, bf16[4,256,768]{2,1,0:T(8,128)(2,1)} %get-tuple-element.29.k_ref, bf16[4,256,768]{2,1,0:T(8,128)(2,1)} %get-tuple-element.30.v_ref, bf16[64,768]{1,0:T(8,128)(2,1)} %get-tuple-element.18.sk_ref, ...), custom_call_target="tpu_custom_call" | custom-call | tf_op jit(solution)/shard_map/pallas_call | solution.py:165
  59.1 0.0 copy-start.6
  59.1 1.6 %fusion.109 = (f32[320]{0:T(512)S(1)}, f32[320,768]{1,0:T(8,128)S(1)}) fusion(bf16[768,768]{1,0:T(8,128)(2,1)S(1)} %copy-done, bf16[64,768]{1,0:T(8,128)(2,1)S(1)} %maximum_select_fusion, bf16[256,768]{1,0:T(8,128)(2,1)} %bitcast.33, bf16[64,768]{1,0:T(8,128)(2,1)S(1)} %broadcast_select_fusion.2, bf16[256,768]{1,0:T(8,128)(2,1)S(1)} %bitcast.37), kind=kOutput, calls=%fused_computation.159 | convolution fusion | flops 379944640 | bytes 3147008 | tf_op jit(solution)/shard_map/dot_general | solution.py:25
  60.8 0.3 multiply_reduce_fusion.1
  61.0 0.0 copy-start.3
  61.1 7.4 %fusion.110 = (f32[320]{0:T(512)S(1)}, f32[320,768]{1,0:T(8,128)S(1)}) fusion(bf16[3072,768]{1,0:T(8,128)(2,1)} %param.18, bf16[768,3072]{1,0:T(8,128)(2,1)} %param.17, f32[320,768]{1,0:T(8,128)S(1)} %get-tuple-element.26, f32[768]{0:T(1024)S(1)} %copy-done.6, f32[320]{0:T(512)S(1)} %add_rsqrt_fusion.1, f32[320]{0:T(512)S(1)} %broadcast_multiply_fusion.1), kind=kOutput, calls=%fused_computation.160 | convolution fusion | flops 3031449344 | bytes 11410176 | tf_op jit(solution)/shard_map/dot_general | solution.py:30
  68.5 0.3 multiply_reduce_fusion
  68.8 0.2 multiply_convert_fusion
  69.0 0.8 %slice.159 = bf16[256,768]{1,0:T(8,128)(2,1)} slice(bf16[320,768]{1,0:T(8,128)(2,1)S(1)} %multiply_convert_fusion), slice={[0:256], [0:768]} | slice | bytes 786432 | tf_op jit(solution)/shard_map/slice | solution.py:251
  69.7 0.6 slice.160
  (34 shorter events, 0.2 us)
Async XLA Ops:
  0.6 58.5 %copy-start = (bf16[768,768]{1,0:T(8,128)(2,1)S(1)}, bf16[768,768]{1,0:T(8,128)(2,1)}, u32[]{:S(2)}) copy-start(bf16[768,768]{1,0:T(8,128)(2,1)} %param.15) | copy-start | bytes 3538948
  0.6 5.4 %collective-permute-start = (bf16[64,768]{1,0:T(8,128)(2,1)}, bf16[64,768]{1,0:T(8,128)(2,1)S(1)}, u32[]{:S(2)}, u32[]{:S(2)}) collective-permute-start(bf16[64,768]{1,0:T(8,128)(2,1)} %bitcast.35), channel_id=1, source_target_pairs={{0,4},{4,0},{8,12},{12,8},{16,20},{20,16},{24,28},{28,24},{1,5},{5... | collective-permute-start | bytes 294920 | tf_op jit(solution)/shard_map/ppermute | solution.py:60
  5.0 1.0 %copy-start.2 = (bf16[1,64,768]{2,1,0:T(8,128)(2,1)S(1)}, bf16[1,64,768]{2,1,0:T(8,128)(2,1)}, u32[]{:S(2)}) copy-start(bf16[1,64,768]{2,1,0:T(8,128)(2,1)} %param.11) | copy-start | bytes 294916
  5.1 3.7 %copy-start.4 = (s32[4,64]{1,0:T(4,128)S(1)}, s32[4,64]{1,0:T(4,128)}, u32[]{:S(2)}) copy-start(s32[4,64]{1,0:T(4,128)} %param.13) | copy-start | bytes 3076
  6.1 6.1 %collective-permute-start.1 = (bf16[64,768]{1,0:T(8,128)(2,1)S(1)}, bf16[64,768]{1,0:T(8,128)(2,1)S(1)}, u32[]{:S(2)}, u32[]{:S(2)}) collective-permute-start(bf16[64,768]{1,0:T(8,128)(2,1)S(1)} %broadcast_select_fusion), channel_id=1, source_target_pairs={{0,8},{4,12},{8,0},{12,4},{16,24},{20,28},{24,16},{28,20},{1,9},{5... | collective-permute-start | bytes 294920 | tf_op jit(solution)/shard_map/ppermute | solution.py:60
  12.2 7.6 %collective-permute-start.2 = (bf16[64,768]{1,0:T(8,128)(2,1)S(1)}, bf16[64,768]{1,0:T(8,128)(2,1)S(1)}, u32[]{:S(2)}, u32[]{:S(2)}) collective-permute-start(bf16[64,768]{1,0:T(8,128)(2,1)S(1)} %broadcast_select_fusion.1), channel_id=1, source_target_pairs={{0,16},{4,20},{8,24},{12,28},{16,0},{20,4},{24,8},{28,12},{1,17},{... | collective-permute-start | bytes 294920 | tf_op jit(solution)/shard_map/ppermute | solution.py:60
  15.0 31.0 %collective-permute-start.5 = (bf16[4,64,768]{2,1,0:T(8,128)(2,1)}, bf16[4,64,768]{2,1,0:T(8,128)(2,1)S(1)}, u32[]{:S(2)}, u32[]{:S(2)}) collective-permute-start(bf16[4,64,768]{2,1,0:T(8,128)(2,1)} %param.10), channel_id=1, source_target_pairs={{0,3},{1,2},{2,1},{3,0},{4,7},{5,6},{6,5},{7,4},{8,11},{9,10},{10,... | collective-permute-start | bytes 1179656 | tf_op jit(solution)/shard_map/ppermute | solution.py:128
  17.5 28.6 %collective-permute-start.4 = (bf16[4,64,768]{2,1,0:T(8,128)(2,1)}, bf16[4,64,768]{2,1,0:T(8,128)(2,1)S(1)}, u32[]{:S(2)}, u32[]{:S(2)}) collective-permute-start(bf16[4,64,768]{2,1,0:T(8,128)(2,1)} %param.10), channel_id=1, source_target_pairs={{0,2},{1,3},{2,0},{3,1},{4,6},{5,7},{6,4},{7,5},{8,10},{9,11},{10,... | collective-permute-start | bytes 1179656 | tf_op jit(solution)/shard_map/ppermute | solution.py:128
  18.0 28.1 %collective-permute-start.3 = (bf16[4,64,768]{2,1,0:T(8,128)(2,1)}, bf16[4,64,768]{2,1,0:T(8,128)(2,1)S(1)}, u32[]{:S(2)}, u32[]{:S(2)}) collective-permute-start(bf16[4,64,768]{2,1,0:T(8,128)(2,1)} %param.10), channel_id=1, source_target_pairs={{0,1},{1,0},{2,3},{3,2},{4,5},{5,4},{6,7},{7,6},{8,9},{9,8},{10,11... | collective-permute-start | bytes 1179656 | tf_op jit(solution)/shard_map/ppermute | solution.py:128
  25.6 1.2 %collective-permute-start.7 = (f32[32,24]{0,1:T(8,128)S(1)}, f32[32,24]{0,1:T(8,128)S(1)}, u32[]{:S(2)}, u32[]{:S(2)}) collective-permute-start(f32[32,24]{0,1:T(8,128)S(1)} %fusion.87), channel_id=1, source_target_pairs={{0,4},{4,0},{8,12},{12,8},{16,20},{20,16},{24,28},{28,24},{1,5},{5... | collective-permute-start | bytes 9224 | tf_op jit(solution)/shard_map/ppermute | solution.py:60
  25.7 10.2 %collective-permute-start.6 = (f32[32,768]{1,0:T(8,128)S(1)}, f32[32,768]{1,0:T(8,128)S(1)}, u32[]{:S(2)}, u32[]{:S(2)}) collective-permute-start(f32[32,768]{1,0:T(8,128)S(1)} %slice_select_fusion), channel_id=1, source_target_pairs={{0,4},{4,0},{8,12},{12,8},{16,20},{20,16},{24,28},{28,24},{1,5},{5... | collective-permute-start | bytes 294920 | tf_op jit(solution)/shard_map/ppermute | solution.py:60
  26.9 19.3 %copy-start.1 = (bf16[768,2304]{1,0:T(8,128)(2,1)S(1)}, bf16[768,2304]{1,0:T(8,128)(2,1)}, u32[]{:S(2)}) copy-start(bf16[768,2304]{1,0:T(8,128)(2,1)} %param.14) | copy-start | bytes 10616836
  26.9 3.8 %collective-permute-start.9 = (f32[32,24]{0,1:T(8,128)S(1)}, f32[32,24]{0,1:T(8,128)S(1)}, u32[]{:S(2)}, u32[]{:S(2)}) collective-permute-start(f32[32,24]{0,1:T(8,128)S(1)} %pad_maximum_fusion.4), channel_id=1, source_target_pairs={{0,8},{4,12},{8,0},{12,4},{16,24},{20,28},{24,16},{28,20},{1,9},{5... | collective-permute-start | bytes 9224 | tf_op jit(solution)/shard_map/ppermute | solution.py:60
  30.7 4.7 %collective-permute-start.11 = (f32[32,24]{0,1:T(8,128)S(1)}, f32[32,24]{0,1:T(8,128)S(1)}, u32[]{:S(2)}, u32[]{:S(2)}) collective-permute-start(f32[32,24]{0,1:T(8,128)S(1)} %pad_maximum_fusion.5), channel_id=1, source_target_pairs={{0,16},{4,20},{8,24},{12,28},{16,0},{20,4},{24,8},{28,12},{1,17},{... | collective-permute-start | bytes 9224 | tf_op jit(solution)/shard_map/ppermute | solution.py:60
  36.2 4.2 %collective-permute-start.8 = (bf16[32,768]{1,0:T(8,128)(2,1)S(1)}, bf16[32,768]{1,0:T(8,128)(2,1)S(1)}, u32[]{:S(2)}, u32[]{:S(2)}) collective-permute-start(bf16[32,768]{1,0:T(8,128)(2,1)S(1)} %add_convert_fusion), channel_id=1, source_target_pairs={{0,8},{4,12},{8,0},{12,4},{16,24},{20,28},{24,16},{28,20},{1,9},{5... | collective-permute-start | bytes 147464 | tf_op jit(solution)/shard_map/ppermute | solution.py:60
  40.6 5.1 %collective-permute-start.10 = (bf16[32,768]{1,0:T(8,128)(2,1)S(1)}, bf16[32,768]{1,0:T(8,128)(2,1)S(1)}, u32[]{:S(2)}, u32[]{:S(2)}) collective-permute-start(bf16[32,768]{1,0:T(8,128)(2,1)S(1)} %fusion.44), channel_id=1, source_target_pairs={{0,16},{4,20},{8,24},{12,28},{16,0},{20,4},{24,8},{28,12},{1,17},{... | collective-permute-start | bytes 147464 | tf_op jit(solution)/shard_map/ppermute | solution.py:60
  45.9 13.1 %collective-permute-start.12 = (bf16[32,768]{1,0:T(8,128)(2,1)S(1)}, bf16[32,768]{1,0:T(8,128)(2,1)S(1)}, u32[]{:S(2)}, u32[]{:S(2)}) collective-permute-start(bf16[32,768]{1,0:T(8,128)(2,1)S(1)} %fusion.28), channel_id=1, source_target_pairs={{0,4},{4,0},{8,12},{12,8},{16,20},{20,16},{24,28},{28,24},{1,5},{5... | collective-permute-start | bytes 147464 | tf_op jit(solution)/shard_map/ppermute | solution.py:60
  50.2 8.9 %copy-start.5 = (bf16[4,64,768]{2,1,0:T(8,128)(2,1)S(1)}, bf16[4,64,768]{2,1,0:T(8,128)(2,1)}, u32[]{:S(2)}) copy-start(bf16[4,64,768]{2,1,0:T(8,128)(2,1)} %param.10) | copy-start | bytes 1179652
  59.1 2.0 %copy-start.6 = (f32[768]{0:T(1024)S(1)}, f32[768]{0:T(1024)}, u32[]{:S(2)}) copy-start(f32[768]{0:T(1024)} %param.16) | copy-start | bytes 9220
  61.0 7.7 %copy-start.3 = (f32[768]{0:T(1024)S(1)}, f32[768]{0:T(1024)}, u32[]{:S(2)}) copy-start(f32[768]{0:T(1024)} %param.19) | copy-start | bytes 9220

commit v15 on v14

--- a/solution.py
+++ b/solution.py
@@ -158,9 +158,11 @@
         o_ref[0, :, cols] = out.astype(o_ref.dtype)
 
 
-def row_attention(q, k, v, sk, sv, allow):
-    rows, nq, width = q.shape
-    nk = k.shape[1]
+def row_attention(qkv, kv, summary_kv, allow):
+    rows, nq, triple = qkv.shape
+    width = triple // 3
+    nk = kv.shape[1]
+    ns = summary_kv.shape[0]
     kern = functools.partial(row_kernel, scale=HEAD_DIM ** (-0.5))
     return pl.pallas_call(
         kern,
@@ -168,14 +170,14 @@
         in_specs=[
             pl.BlockSpec((1, nq, width), lambda r: (r, 0, 0)),
             pl.BlockSpec((1, nk, width), lambda r: (r, 0, 0)),
-            pl.BlockSpec((1, nk, width), lambda r: (r, 0, 0)),
-            pl.BlockSpec((sk.shape[0], width), lambda r: (0, 0)),
-            pl.BlockSpec((sv.shape[0], width), lambda r: (0, 0)),
+            pl.BlockSpec((1, nk, width), lambda r: (r, 0, 1)),
+            pl.BlockSpec((ns, width), lambda r: (0, 0)),
+            pl.BlockSpec((ns, width), lambda r: (0, 1)),
             pl.BlockSpec((1, nq, nk), lambda r: (r, 0, 0)),
         ],
         out_specs=pl.BlockSpec((1, nq, width), lambda r: (r, 0, 0)),
-        out_shape=jax.ShapeDtypeStruct(q.shape, jnp.bfloat16),
-    )(q, k, v, sk, sv, allow)
+        out_shape=jax.ShapeDtypeStruct((rows, nq, width), jnp.bfloat16),
+    )(qkv, kv, kv, summary_kv, summary_kv, allow)
 
 
 def local(cells, summary, owner, schema, w_qkv, w_out, gain_attn, w_up, w_down, gain_ffn, *, n_band, n_col):
@@ -226,13 +228,10 @@
     summary_att = join_halves(summary_att, "band", n_band)
 
     sources = [own_group] + [s for s, _ in row_parts]
-    other_cells = jnp.concatenate([got for _, got in row_parts], axis=1)
-    width_other = other_cells.shape[1]
-    other_kv = project(other_cells.reshape(row_count * width_other, model_width), w_kv)
-    other_kv = other_kv.reshape(row_count, width_other, 2 * model_width)
-    row_keys = jnp.concatenate([own_keys, other_kv[:, :, :model_width]], axis=1)
-    row_vals = jnp.concatenate([own_vals, other_kv[:, :, model_width:]], axis=1)
-    width_now = row_keys.shape[1]
+    row_cells = jnp.concatenate([cells] + [got for _, got in row_parts], axis=1)
+    width_now = row_cells.shape[1]
+    row_kv = project(row_cells.reshape(row_count * width_now, model_width), w_kv)
+    row_kv = row_kv.reshape(row_count, width_now, 2 * model_width)
     key_groups = jnp.concatenate(
         [jnp.full((cols_dev,), s, jnp.int32) for s in sources]
     )
@@ -240,9 +239,7 @@
     allowed = (jnp.right_shift(schema[:, :, None], key_groups[None, None, :]) & 1 == 1) | own_block[
         None, None, :
     ]
-    attended = row_attention(
-        queries, row_keys, row_vals, sum_keys, sum_vals, allowed.astype(jnp.float32)
-    )
+    attended = row_attention(qkv_cells, row_kv, summary_kv, allowed.astype(jnp.float32))
     attended = attended.reshape(row_count * cols_dev, model_width)
 
     all_in = jnp.concatenate([flat_cells, tokens], axis=0)

time: 70.7 us -> 69.4 us (0.982)
  matrix products: 21.5 us -> 23.6 us
  local copies, waits for them, and re-layouts: 3.26 us -> 1.5 us
  other arithmetic: 3.96 us -> 2.24 us
    dot_general x4, matrix products: 9.03 us -> 11.2 us  [project(): jnp.dot(values, weight, preferred_element_type=jnp.float32)]
    concatenate x2 -> x1, other arithmetic: 1.91 us -> 0.11 us  [local(): row_cells = jnp.concatenate([cells] + [got for _, got in row_parts], axis=1)]
    slice x3 -> x0, local copies, waits for them, and re-layouts: 1.79 us -> none  [the longest x1 0.86 us: local(): own_vals = qkv_cells[:, :, 2 * model_width:]]
  transfers between devices with their start and end apart: 13 -> 13, of which waited for: 7 -> 7; matrix products, arithmetic and copies ran while one was open for 25% -> 23% of each run, Pallas kernels for 13% -> 13%
where the time goes in v15:
time: 69.4 us; the launch traced here: 69.1 us
  matrix products  23.6 us (34%)
  starting transfers between devices  16.2 us (23%)
  waiting for transfers between devices  15.1 us (22%)
  Pallas kernels  8.88 us (13%)
  other arithmetic  2.24 us (3%)
  between operations  1.68 us (2%)
  local copies, waits for them, and re-layouts  1.5 us (2%)
    ppermute x10, waiting for transfers between devices, partner(): return lax.ppermute(value, axis, [(i, i ^ step) for i in range(count)])  15 us
    ppermute x10, starting transfers between devices, partner(): return lax.ppermute(value, axis, [(i, i ^ step) for i in range(count)])  12.7 us
    dot_general x4, matrix products, project(): jnp.dot(values, weight, preferred_element_type=jnp.float32)  11.2 us
    pallas_call x1, Pallas kernels, row_attention(): pl.pallas_call(kern, grid=(rows,), in_specs=[pl.BlockSpec((1, nq, width),...  8.88 us
    dot_general x1, matrix products, finish(): outer_out = jnp.dot(inner_act, w_down, preferred_element_type=jnp.float32)  7.43 us
    ppermute x3, starting transfers between devices, fan_out(): got.append((source, lax.ppermute(value, axis, pairs)))  3.49 us
    dot_general x10, matrix products, head_spread(): jnp.dot(flat, head_matrix(), precision=lax.Precision.HIGHEST, preferred_e...  2.55 us
    dot_general x1, matrix products, finish(): mixed_out = jnp.dot(attended, w_out, preferred_element_type=jnp.float32)  1.65 us
  transfers between devices with their start and end apart: 13, of which 7 were waited for; matrix products, arithmetic and copies ran while one was open for 23% of the time, Pallas kernels for 13%

profile of v15, /device:TPU:0, one launch (start us, length us, event | category | flops | bytes accessed | tf_op | source)
XLA Modules:
  0.0 69.1 jit_solution(18198517399887454582)
XLA Ops:
  0.6 0.0 copy-start
  0.6 0.0 copy-start.7
  0.7 0.0 copy-start.9
  0.7 0.5 collective-permute-start
  1.8 3.3 %convolution_convert_fusion = bf16[256,2304]{1,0:T(8,128)(2,1)S(1)} fusion(bf16[256,768]{1,0:T(8,128)(2,1)} %bitcast.35, bf16[768,2304]{1,0:T(8,128)(2,1)} %param.14), kind=kOutput, calls=%fused_computation.9 | convolution fusion | flops 906559488 | bytes 5111808 | tf_op jit(solution)/shard_map/dot_general | solution.py:35
  5.2 0.1 pad_add_fusion
  5.3 0.0 collective-permute-done
  5.3 2.7 %collective-permute-start.1 = (bf16[64,768]{1,0:T(8,128)(2,1)S(1)}, bf16[64,768]{1,0:T(8,128)(2,1)S(1)}, u32[]{:S(2)}, u32[]{:S(2)}) collective-permute-start(bf16[64,768]{1,0:T(8,128)(2,1)S(1)} %broadcast_select_fusion), channel_id=1, source_target_pairs={{0,8},{4,12},{8,0},{12,4},{16,24},{20,28},{24,16},{28,20},{1,9},{5... | collective-permute-start | bytes 294920 | tf_op jit(solution)/shard_map/ppermute | solution.py:60
  8.0 0.0 copy-done.9
  8.0 0.8 %fusion.40.allow_ref = f32[4,64,256]{2,1,0:T(8,128)} fusion(s32[256]{0:T(256)S(1)} %pad_add_fusion, s32[4,64]{1,0:T(4,128)S(1)} %copy-done.9, pred[256]{0:T(512)(128)(4,1)S(1)} %iota_compare_fusion.15), kind=kLoop, calls=%fused_computation.46 | loop fusion | flops 327680 | bytes 264448 | tf_op jit(solution)/shard_map/convert_element_type | solution.py:242
  8.9 2.5 %collective-permute-done.1 = bf16[64,768]{1,0:T(8,128)(2,1)S(1)} collective-permute-done((bf16[64,768]{1,0:T(8,128)(2,1)S(1)}, bf16[64,768]{1,0:T(8,128)(2,1)S(1)}, u32[]{:S(2)}, u32[]{:S(2)}) %collective-permute-start.1) | collective-permute-done | bytes 98336 | tf_op jit(solution)/shard_map/ppermute | solution.py:60
  11.4 2.8 %collective-permute-start.2 = (bf16[64,768]{1,0:T(8,128)(2,1)S(1)}, bf16[64,768]{1,0:T(8,128)(2,1)S(1)}, u32[]{:S(2)}, u32[]{:S(2)}) collective-permute-start(bf16[64,768]{1,0:T(8,128)(2,1)S(1)} %broadcast_select_fusion.1), channel_id=1, source_target_pairs={{0,16},{4,20},{8,24},{12,28},{16,0},{20,4},{24,8},{28,12},{1,17},{... | collective-permute-start | bytes 294920 | tf_op jit(solution)/shard_map/ppermute | solution.py:60
  14.3 1.5 %collective-permute-start.3 = (bf16[4,64,768]{2,1,0:T(8,128)(2,1)S(1)}, bf16[4,64,768]{2,1,0:T(8,128)(2,1)S(1)}, u32[]{:S(2)}, u32[]{:S(2)}) collective-permute-start(bf16[4,64,768]{2,1,0:T(8,128)(2,1)S(1)} %copy-done.3), channel_id=1, source_target_pairs={{0,1},{1,0},{2,3},{3,2},{4,5},{5,4},{6,7},{7,6},{8,9},{9,8},{10,11... | collective-permute-start | bytes 1179656 | tf_op jit(solution)/shard_map/ppermute | solution.py:128
  15.7 1.5 %collective-permute-start.4 = (bf16[4,64,768]{2,1,0:T(8,128)(2,1)S(1)}, bf16[4,64,768]{2,1,0:T(8,128)(2,1)S(1)}, u32[]{:S(2)}, u32[]{:S(2)}) collective-permute-start(bf16[4,64,768]{2,1,0:T(8,128)(2,1)S(1)} %copy-done.3), channel_id=1, source_target_pairs={{0,2},{1,3},{2,0},{3,1},{4,6},{5,7},{6,4},{7,5},{8,10},{9,11},{10,... | collective-permute-start | bytes 1179656 | tf_op jit(solution)/shard_map/ppermute | solution.py:128
  17.3 0.5 collective-permute-start.5
  17.7 1.3 %collective-permute-done.2 = bf16[64,768]{1,0:T(8,128)(2,1)S(1)} collective-permute-done((bf16[64,768]{1,0:T(8,128)(2,1)S(1)}, bf16[64,768]{1,0:T(8,128)(2,1)S(1)}, u32[]{:S(2)}, u32[]{:S(2)}) %collective-permute-start.2) | collective-permute-done | bytes 98336 | tf_op jit(solution)/shard_map/ppermute | solution.py:60
  19.0 0.0 copy-start.4
  19.1 2.2 %convolution_convert_fusion.2.sk_ref.sv_ref = bf16[64,1536]{1,0:T(8,128)(2,1)S(1)} fusion(bf16[64,768]{1,0:T(8,128)(2,1)S(1)} %broadcast_select_fusion.2, bf16[768,2304]{1,0:T(8,128)(2,1)} %param.14), kind=kOutput, calls=%fused_computation.11 | convolution fusion | flops 151093248 | bytes 2654208 | tf_op jit(solution)/shard_map/dot_general | solution.py:35
  21.3 1.7 %fusion.25 = f32[64,768]{1,0:T(8,128)S(1)} fusion(bf16[64,768]{1,0:T(8,128)(2,1)S(1)} %broadcast_select_fusion.2, bf16[768,2304]{1,0:T(8,128)(2,1)} %param.14), kind=kOutput, calls=%fused_computation.26 | convolution fusion | flops 75595776 | bytes 1474560 | tf_op jit(solution)/shard_map/dot_general | solution.py:35
  23.0 0.6 fusion.105
  23.6 0.3 fusion.19
  24.0 0.0 copy-start.6
  24.0 0.2 convolution_multiply_fusion.2
  24.1 0.2 fusion.89
  24.3 0.0 collective-permute-start.7
  24.3 0.1 slice_select_fusion.2
  24.4 0.5 collective-permute-start.6
  24.9 0.6 collective-permute-done.7
  25.5 0.1 broadcast_select_fusion.8
  25.6 0.7 %collective-permute-start.9 = (f32[32,24]{0,1:T(8,128)S(1)}, f32[32,24]{0,1:T(8,128)S(1)}, u32[]{:S(2)}, u32[]{:S(2)}) collective-permute-start(f32[32,24]{0,1:T(8,128)S(1)} %pad_maximum_fusion.2), channel_id=1, source_target_pairs={{0,8},{4,12},{8,0},{12,4},{16,24},{20,28},{24,16},{28,20},{1,9},{5... | collective-permute-start | bytes 9224 | tf_op jit(solution)/shard_map/ppermute | solution.py:60
  26.3 0.3 fusion.60
  26.6 2.8 %collective-permute-done.9 = f32[32,24]{0,1:T(8,128)S(1)} collective-permute-done((f32[32,24]{0,1:T(8,128)S(1)}, f32[32,24]{0,1:T(8,128)S(1)}, u32[]{:S(2)}, u32[]{:S(2)}) %collective-permute-start.9) | collective-permute-done | bytes 3104 | tf_op jit(solution)/shard_map/ppermute | solution.py:60
  29.4 2.1 %collective-permute-start.11 = (f32[32,24]{0,1:T(8,128)S(1)}, f32[32,24]{0,1:T(8,128)S(1)}, u32[]{:S(2)}, u32[]{:S(2)}) collective-permute-start(f32[32,24]{0,1:T(8,128)S(1)} %pad_maximum_fusion.3), channel_id=1, source_target_pairs={{0,16},{4,20},{8,24},{12,28},{16,0},{20,4},{24,8},{28,12},{1,17},{... | collective-permute-start | bytes 9224 | tf_op jit(solution)/shard_map/ppermute | solution.py:60
  31.5 0.2 fusion.57
  31.7 2.3 %collective-permute-done.11 = f32[32,24]{0,1:T(8,128)S(1)} collective-permute-done((f32[32,24]{0,1:T(8,128)S(1)}, f32[32,24]{0,1:T(8,128)S(1)}, u32[]{:S(2)}, u32[]{:S(2)}) %collective-permute-start.11) | collective-permute-done | bytes 3104 | tf_op jit(solution)/shard_map/ppermute | solution.py:60
  34.1 0.3 fusion.55
  34.4 0.3 fusion.56
  34.6 0.0 collective-permute-done.6
  34.6 0.3 add_convert_fusion
  34.9 1.2 %collective-permute-start.8 = (bf16[32,768]{1,0:T(8,128)(2,1)S(1)}, bf16[32,768]{1,0:T(8,128)(2,1)S(1)}, u32[]{:S(2)}, u32[]{:S(2)}) collective-permute-start(bf16[32,768]{1,0:T(8,128)(2,1)S(1)} %add_convert_fusion), channel_id=1, source_target_pairs={{0,8},{4,12},{8,0},{12,4},{16,24},{20,28},{24,16},{28,20},{1,9},{5... | collective-permute-start | bytes 147464 | tf_op jit(solution)/shard_map/ppermute | solution.py:60
  36.1 0.2 fusion.53
  36.3 2.8 %collective-permute-done.8 = bf16[32,768]{1,0:T(8,128)(2,1)S(1)} collective-permute-done((bf16[32,768]{1,0:T(8,128)(2,1)S(1)}, bf16[32,768]{1,0:T(8,128)(2,1)S(1)}, u32[]{:S(2)}, u32[]{:S(2)}) %collective-permute-start.8) | collective-permute-done | bytes 49184 | tf_op jit(solution)/shard_map/ppermute | solution.py:60
  39.0 0.3 fusion.45
  39.3 2.1 %collective-permute-start.10 = (bf16[32,768]{1,0:T(8,128)(2,1)S(1)}, bf16[32,768]{1,0:T(8,128)(2,1)S(1)}, u32[]{:S(2)}, u32[]{:S(2)}) collective-permute-start(bf16[32,768]{1,0:T(8,128)(2,1)S(1)} %fusion.45), channel_id=1, source_target_pairs={{0,16},{4,20},{8,24},{12,28},{16,0},{20,4},{24,8},{28,12},{1,17},{... | collective-permute-start | bytes 147464 | tf_op jit(solution)/shard_map/ppermute | solution.py:60
  41.4 0.3 fusion.54
  41.6 2.7 %collective-permute-done.10 = bf16[32,768]{1,0:T(8,128)(2,1)S(1)} collective-permute-done((bf16[32,768]{1,0:T(8,128)(2,1)S(1)}, bf16[32,768]{1,0:T(8,128)(2,1)S(1)}, u32[]{:S(2)}, u32[]{:S(2)}) %collective-permute-start.10) | collective-permute-done | bytes 49184 | tf_op jit(solution)/shard_map/ppermute | solution.py:60
  44.4 0.3 fusion.28
  44.6 0.1 collective-permute-start.12
  44.7 0.0 collective-permute-done.3
  44.7 0.0 collective-permute-done.4
  44.7 0.0 collective-permute-done.5
  44.7 0.1 pad_maximum_fusion
  44.9 4.0 %convolution_convert_fusion.1 = bf16[1024,1536]{1,0:T(8,128)(2,1)} fusion(bf16[1024,768]{1,0:T(8,128)(2,1)S(1)} %bitcast.33, bf16[768,2304]{1,0:T(8,128)(2,1)S(1)} %copy-done.6), kind=kOutput, calls=%fused_computation.10 | convolution fusion | flops 2417491968 | bytes 7077888 | tf_op jit(solution)/shard_map/dot_general | solution.py:35
  48.9 8.9 %shard_map.113 = bf16[4,64,768]{2,1,0:T(8,128)(2,1)} custom-call(bf16[4,64,2304]{2,1,0:T(8,128)(2,1)} %bitcast.32, bf16[4,256,1536]{2,1,0:T(8,128)(2,1)} %bitcast.28, bf16[4,256,1536]{2,1,0:T(8,128)(2,1)} %bitcast.29, bf16[64,1536]{1,0:T(8,128)(2,1)} %copy-done.2, bf16[64,1536]{1,0:T(8,128)(2,1)} %copy-done.2, f32[4,64,256]{2,1,0:T(8,128)} %fusion.40.allow_ref), custom_call_target="tpu_custom_call" | custom-call | tf_op jit(solution)/shard_map/pallas_call | solution.py:167
  57.8 0.0 collective-permute-done.12
  57.8 1.7 %fusion.106 = (f32[320]{0:T(512)S(1)}, f32[320,768]{1,0:T(8,128)S(1)}) fusion(bf16[768,768]{1,0:T(8,128)(2,1)S(1)} %copy-done, bf16[64,768]{1,0:T(8,128)(2,1)S(1)} %maximum_select_fusion, bf16[256,768]{1,0:T(8,128)(2,1)} %bitcast.34, bf16[64,768]{1,0:T(8,128)(2,1)S(1)} %copy-done.5, bf16[256,768]{1,0:T(8,128)(2,1)S(1)} %bitcast.36), kind=kOutput, calls=%fused_computation.154 | convolution fusion | flops 379944640 | bytes 3147008 | tf_op jit(solution)/shard_map/dot_general | solution.py:25
  59.5 0.3 multiply_reduce_fusion.1
  59.8 0.0 copy-start.8
  59.8 7.4 %fusion.107 = (f32[320]{0:T(512)S(1)}, f32[320,768]{1,0:T(8,128)S(1)}) fusion(bf16[3072,768]{1,0:T(8,128)(2,1)} %param.18, bf16[768,3072]{1,0:T(8,128)(2,1)} %param.17, f32[320,768]{1,0:T(8,128)S(1)} %get-tuple-element.19, f32[768]{0:T(1024)S(1)} %copy-done.10, f32[320]{0:T(512)S(1)} %add_rsqrt_fusion.1, f32[320]{0:T(512)S(1)} %broadcast_multiply_fusion.1), kind=kOutput, calls=%fused_computation.155 | convolution fusion | flops 3031449344 | bytes 11410176 | tf_op jit(solution)/shard_map/dot_general | solution.py:30
  67.2 0.3 multiply_reduce_fusion
  67.5 0.0 copy-done.8
  67.5 0.2 multiply_convert_fusion
  67.7 0.8 %slice.140 = bf16[256,768]{1,0:T(8,128)(2,1)} slice(bf16[320,768]{1,0:T(8,128)(2,1)S(1)} %multiply_convert_fusion), slice={[0:256], [0:768]} | slice | bytes 786432 | tf_op jit(solution)/shard_map/slice | solution.py:248
  68.5 0.6 slice.141
  (38 shorter events, 0.3 us)
Async XLA Ops:
  0.6 57.2 %copy-start = (bf16[768,768]{1,0:T(8,128)(2,1)S(1)}, bf16[768,768]{1,0:T(8,128)(2,1)}, u32[]{:S(2)}) copy-start(bf16[768,768]{1,0:T(8,128)(2,1)} %param.15) | copy-start | bytes 3538948
  0.6 4.6 %copy-start.7 = (bf16[1,64,768]{2,1,0:T(8,128)(2,1)S(1)}, bf16[1,64,768]{2,1,0:T(8,128)(2,1)}, u32[]{:S(2)}) copy-start(bf16[1,64,768]{2,1,0:T(8,128)(2,1)} %param.11) | copy-start | bytes 294916
  0.7 7.4 %copy-start.9 = (s32[4,64]{1,0:T(4,128)S(1)}, s32[4,64]{1,0:T(4,128)}, u32[]{:S(2)}) copy-start(s32[4,64]{1,0:T(4,128)} %param.13) | copy-start | bytes 3076
  0.7 4.6 %collective-permute-start = (bf16[64,768]{1,0:T(8,128)(2,1)}, bf16[64,768]{1,0:T(8,128)(2,1)S(1)}, u32[]{:S(2)}, u32[]{:S(2)}) collective-permute-start(bf16[64,768]{1,0:T(8,128)(2,1)} %bitcast.38), channel_id=1, source_target_pairs={{0,4},{4,0},{8,12},{12,8},{16,20},{20,16},{24,28},{28,24},{1,5},{5... | collective-permute-start | bytes 294920 | tf_op jit(solution)/shard_map/ppermute | solution.py:60
  1.8 12.4 %copy-start.3 = (bf16[4,64,768]{2,1,0:T(8,128)(2,1)S(1)}, bf16[4,64,768]{2,1,0:T(8,128)(2,1)}, u32[]{:S(2)}) copy-start(bf16[4,64,768]{2,1,0:T(8,128)(2,1)} %param.10) | copy-start | bytes 1179652
  5.1 18.8 %copy-start.1 = (bf16[256,2304]{1,0:T(8,128)(2,1)}, bf16[256,2304]{1,0:T(8,128)(2,1)S(1)}, u32[]{:S(2)}) copy-start(bf16[256,2304]{1,0:T(8,128)(2,1)S(1)} %convolution_convert_fusion) | copy-start | bytes 3538948
  5.3 6.1 %collective-permute-start.1 = (bf16[64,768]{1,0:T(8,128)(2,1)S(1)}, bf16[64,768]{1,0:T(8,128)(2,1)S(1)}, u32[]{:S(2)}, u32[]{:S(2)}) collective-permute-start(bf16[64,768]{1,0:T(8,128)(2,1)S(1)} %broadcast_select_fusion), channel_id=1, source_target_pairs={{0,8},{4,12},{8,0},{12,4},{16,24},{20,28},{24,16},{28,20},{1,9},{5... | collective-permute-start | bytes 294920 | tf_op jit(solution)/shard_map/ppermute | solution.py:60
  11.4 7.6 %collective-permute-start.2 = (bf16[64,768]{1,0:T(8,128)(2,1)S(1)}, bf16[64,768]{1,0:T(8,128)(2,1)S(1)}, u32[]{:S(2)}, u32[]{:S(2)}) collective-permute-start(bf16[64,768]{1,0:T(8,128)(2,1)S(1)} %broadcast_select_fusion.1), channel_id=1, source_target_pairs={{0,16},{4,20},{8,24},{12,28},{16,0},{20,4},{24,8},{28,12},{1,17},{... | collective-permute-start | bytes 294920 | tf_op jit(solution)/shard_map/ppermute | solution.py:60
  14.3 30.5 %collective-permute-start.3 = (bf16[4,64,768]{2,1,0:T(8,128)(2,1)S(1)}, bf16[4,64,768]{2,1,0:T(8,128)(2,1)S(1)}, u32[]{:S(2)}, u32[]{:S(2)}) collective-permute-start(bf16[4,64,768]{2,1,0:T(8,128)(2,1)S(1)} %copy-done.3), channel_id=1, source_target_pairs={{0,1},{1,0},{2,3},{3,2},{4,5},{5,4},{6,7},{7,6},{8,9},{9,8},{10,11... | collective-permute-start | bytes 1179656 | tf_op jit(solution)/shard_map/ppermute | solution.py:128
  15.7 29.0 %collective-permute-start.4 = (bf16[4,64,768]{2,1,0:T(8,128)(2,1)S(1)}, bf16[4,64,768]{2,1,0:T(8,128)(2,1)S(1)}, u32[]{:S(2)}, u32[]{:S(2)}) collective-permute-start(bf16[4,64,768]{2,1,0:T(8,128)(2,1)S(1)} %copy-done.3), channel_id=1, source_target_pairs={{0,2},{1,3},{2,0},{3,1},{4,6},{5,7},{6,4},{7,5},{8,10},{9,11},{10,... | collective-permute-start | bytes 1179656 | tf_op jit(solution)/shard_map/ppermute | solution.py:128
  17.3 27.5 %collective-permute-start.5 = (bf16[4,64,768]{2,1,0:T(8,128)(2,1)S(1)}, bf16[4,64,768]{2,1,0:T(8,128)(2,1)S(1)}, u32[]{:S(2)}, u32[]{:S(2)}) collective-permute-start(bf16[4,64,768]{2,1,0:T(8,128)(2,1)S(1)} %copy-done.3), channel_id=1, source_target_pairs={{0,3},{1,2},{2,1},{3,0},{4,7},{5,6},{6,5},{7,4},{8,11},{9,10},{10,... | collective-permute-start | bytes 1179656 | tf_op jit(solution)/shard_map/ppermute | solution.py:128
  19.0 6.5 %copy-start.4 = (bf16[64,768]{1,0:T(8,128)(2,1)}, bf16[64,768]{1,0:T(8,128)(2,1)S(1)}, u32[]{:S(2)}) copy-start(bf16[64,768]{1,0:T(8,128)(2,1)S(1)} %broadcast_select_fusion.2) | copy-start | bytes 294916
  21.3 23.6 %copy-start.2 = (bf16[64,1536]{1,0:T(8,128)(2,1)}, bf16[64,1536]{1,0:T(8,128)(2,1)S(1)}, u32[]{:S(2)}) copy-start(bf16[64,1536]{1,0:T(8,128)(2,1)S(1)} %convolution_convert_fusion.2.sk_ref.sv_ref) | copy-start | bytes 589828
  24.0 20.9 %copy-start.6 = (bf16[768,2304]{1,0:T(8,128)(2,1)S(1)}, bf16[768,2304]{1,0:T(8,128)(2,1)}, u32[]{:S(2)}) copy-start(bf16[768,2304]{1,0:T(8,128)(2,1)} %param.14) | copy-start | bytes 10616836
  24.3 1.2 %collective-permute-start.7 = (f32[32,24]{0,1:T(8,128)S(1)}, f32[32,24]{0,1:T(8,128)S(1)}, u32[]{:S(2)}, u32[]{:S(2)}) collective-permute-start(f32[32,24]{0,1:T(8,128)S(1)} %fusion.89), channel_id=1, source_target_pairs={{0,4},{4,0},{8,12},{12,8},{16,20},{20,16},{24,28},{28,24},{1,5},{5... | collective-permute-start | bytes 9224 | tf_op jit(solution)/shard_map/ppermute | solution.py:60
  24.4 10.2 %collective-permute-start.6 = (f32[32,768]{1,0:T(8,128)S(1)}, f32[32,768]{1,0:T(8,128)S(1)}, u32[]{:S(2)}, u32[]{:S(2)}) collective-permute-start(f32[32,768]{1,0:T(8,128)S(1)} %slice_select_fusion), channel_id=1, source_target_pairs={{0,4},{4,0},{8,12},{12,8},{16,20},{20,16},{24,28},{28,24},{1,5},{5... | collective-permute-start | bytes 294920 | tf_op jit(solution)/shard_map/ppermute | solution.py:60
  25.6 3.8 %collective-permute-start.9 = (f32[32,24]{0,1:T(8,128)S(1)}, f32[32,24]{0,1:T(8,128)S(1)}, u32[]{:S(2)}, u32[]{:S(2)}) collective-permute-start(f32[32,24]{0,1:T(8,128)S(1)} %pad_maximum_fusion.2), channel_id=1, source_target_pairs={{0,8},{4,12},{8,0},{12,4},{16,24},{20,28},{24,16},{28,20},{1,9},{5... | collective-permute-start | bytes 9224 | tf_op jit(solution)/shard_map/ppermute | solution.py:60
  29.4 4.7 %collective-permute-start.11 = (f32[32,24]{0,1:T(8,128)S(1)}, f32[32,24]{0,1:T(8,128)S(1)}, u32[]{:S(2)}, u32[]{:S(2)}) collective-permute-start(f32[32,24]{0,1:T(8,128)S(1)} %pad_maximum_fusion.3), channel_id=1, source_target_pairs={{0,16},{4,20},{8,24},{12,28},{16,0},{20,4},{24,8},{28,12},{1,17},{... | collective-permute-start | bytes 9224 | tf_op jit(solution)/shard_map/ppermute | solution.py:60
  34.9 4.2 %collective-permute-start.8 = (bf16[32,768]{1,0:T(8,128)(2,1)S(1)}, bf16[32,768]{1,0:T(8,128)(2,1)S(1)}, u32[]{:S(2)}, u32[]{:S(2)}) collective-permute-start(bf16[32,768]{1,0:T(8,128)(2,1)S(1)} %add_convert_fusion), channel_id=1, source_target_pairs={{0,8},{4,12},{8,0},{12,4},{16,24},{20,28},{24,16},{28,20},{1,9},{5... | collective-permute-start | bytes 147464 | tf_op jit(solution)/shard_map/ppermute | solution.py:60
  39.3 5.1 %collective-permute-start.10 = (bf16[32,768]{1,0:T(8,128)(2,1)S(1)}, bf16[32,768]{1,0:T(8,128)(2,1)S(1)}, u32[]{:S(2)}, u32[]{:S(2)}) collective-permute-start(bf16[32,768]{1,0:T(8,128)(2,1)S(1)} %fusion.45), channel_id=1, source_target_pairs={{0,16},{4,20},{8,24},{12,28},{16,0},{20,4},{24,8},{28,12},{1,17},{... | collective-permute-start | bytes 147464 | tf_op jit(solution)/shard_map/ppermute | solution.py:60
  44.6 13.2 %collective-permute-start.12 = (bf16[32,768]{1,0:T(8,128)(2,1)S(1)}, bf16[32,768]{1,0:T(8,128)(2,1)S(1)}, u32[]{:S(2)}, u32[]{:S(2)}) collective-permute-start(bf16[32,768]{1,0:T(8,128)(2,1)S(1)} %fusion.28), channel_id=1, source_target_pairs={{0,4},{4,0},{8,12},{12,8},{16,20},{20,16},{24,28},{28,24},{1,5},{5... | collective-permute-start | bytes 147464 | tf_op jit(solution)/shard_map/ppermute | solution.py:60
  48.9 8.9 %copy-start.5 = (bf16[64,768]{1,0:T(8,128)(2,1)S(1)}, bf16[64,768]{1,0:T(8,128)(2,1)}, u32[]{:S(2)}) copy-start(bf16[64,768]{1,0:T(8,128)(2,1)} %copy-done.4) | copy-start | bytes 294916
  57.8 2.0 %copy-start.10 = (f32[768]{0:T(1024)S(1)}, f32[768]{0:T(1024)}, u32[]{:S(2)}) copy-start(f32[768]{0:T(1024)} %param.16) | copy-start | bytes 9220
  59.8 7.7 %copy-start.8 = (f32[768]{0:T(1024)S(1)}, f32[768]{0:T(1024)}, u32[]{:S(2)}) copy-start(f32[768]{0:T(1024)} %param.19) | copy-start | bytes 9220

commit v16 on v15

--- a/solution.py
+++ b/solution.py
@@ -83,6 +83,22 @@
 
 def pick(flag, a, b):
     return tuple(jnp.where(flag, x, y) for x, y in zip(a, b))
+
+
+def pack_partial(value):
+    stats = value[1]
+    high = stats.astype(jnp.bfloat16)
+    rest = stats - high.astype(jnp.float32)
+    middle = rest.astype(jnp.bfloat16)
+    low = (rest - middle.astype(jnp.float32)).astype(jnp.bfloat16)
+    return jnp.concatenate([value[0].astype(jnp.bfloat16), high, middle, low], axis=-1)
+
+
+def unpack_partial(packed, width):
+    part = packed.astype(jnp.float32)
+    n = (packed.shape[1] - width) // 3
+    stats = (part[:, width : width + n] + part[:, width + n : width + 2 * n]) + part[:, width + 2 * n :]
+    return part[:, :width], stats
 
 
 def half_merge(value, axis, count):
@@ -97,12 +113,9 @@
     value = merge(pick(first, mine, got), pick(first, got, mine))
     step = 2
     while step < count:
-        mixed = value[0].astype(jnp.bfloat16)
-        got = (
-            partner(mixed, axis, step, count).astype(jnp.float32),
-            partner(value[1], axis, step, count),
-        )
-        mine = (mixed.astype(jnp.float32), value[1])
+        packed = pack_partial(value)
+        got = unpack_partial(partner(packed, axis, step, count), value[0].shape[1])
+        mine = unpack_partial(packed, value[0].shape[1])
         low_side = (here & step) == 0
         value = merge(pick(low_side, mine, got), pick(low_side, got, mine))
         step *= 2

time: 69.4 us -> 62.6 us (0.902)
  waiting for transfers between devices: 15.1 us -> 9.34 us
  starting transfers between devices: 16.2 us -> 13.1 us
  other arithmetic: 2.24 us -> 4.11 us
    ppermute x10 -> x8, waiting for transfers between devices: 15 us -> 8.58 us  [partner(): return lax.ppermute(value, axis, [(i, i ^ step) for i in range(count)])]
    ppermute x10 -> x8, starting transfers between devices: 12.7 us -> 9.59 us  [partner(): return lax.ppermute(value, axis, [(i, i ^ step) for i in range(count)])]
    concatenate x1, other arithmetic: 0.11 us -> 1.34 us  [local(): row_cells = jnp.concatenate([cells] + [got for _, got in row_parts], axis=1)]
    ppermute x3, waiting for transfers between devices: 0.01 us -> 0.77 us  [fan_out(): got.append((source, lax.ppermute(value, axis, pairs)))]
  transfers between devices with their start and end apart: 13 -> 11, of which waited for: 7 -> 6; matrix products, arithmetic and copies ran while one was open for 23% -> 27% of each run, Pallas kernels for 13% -> 14%
where the time goes in v16:
time: 62.6 us; the launch traced here: 62.3 us
  matrix products  23.6 us (38%)
  starting transfers between devices  13.1 us (21%)
  waiting for transfers between devices  9.34 us (15%)
  Pallas kernels  8.88 us (14%)
  other arithmetic  4.11 us (7%)
  between operations  1.65 us (3%)
  local copies, waits for them, and re-layouts  1.64 us (3%)
    dot_general x4, matrix products, project(): jnp.dot(values, weight, preferred_element_type=jnp.float32)  11.2 us
    ppermute x8, starting transfers between devices, partner(): return lax.ppermute(value, axis, [(i, i ^ step) for i in range(count)])  9.59 us
    pallas_call x1, Pallas kernels, row_attention(): pl.pallas_call(kern, grid=(rows,), in_specs=[pl.BlockSpec((1, nq, width),...  8.88 us
    ppermute x8, waiting for transfers between devices, partner(): return lax.ppermute(value, axis, [(i, i ^ step) for i in range(count)])  8.58 us
    dot_general x1, matrix products, finish(): outer_out = jnp.dot(inner_act, w_down, preferred_element_type=jnp.float32)  7.43 us
    ppermute x3, starting transfers between devices, fan_out(): got.append((source, lax.ppermute(value, axis, pairs)))  3.49 us
    dot_general x10, matrix products, head_spread(): jnp.dot(flat, head_matrix(), precision=lax.Precision.HIGHEST, preferred_e...  2.43 us
    dot_general x1, matrix products, finish(): mixed_out = jnp.dot(attended, w_out, preferred_element_type=jnp.float32)  1.65 us
  transfers between devices with their start and end apart: 11, of which 6 were waited for; matrix products, arithmetic and copies ran while one was open for 27% of the time, Pallas kernels for 14%

profile of v16, /device:TPU:0, one launch (start us, length us, event | category | flops | bytes accessed | tf_op | source)
XLA Modules:
  0.0 62.3 jit_solution(4446874658540249416)
XLA Ops:
  0.6 0.0 copy-start
  0.7 0.5 collective-permute-start
  1.8 3.3 %convolution_convert_fusion = bf16[256,2304]{1,0:T(8,128)(2,1)S(1)} fusion(bf16[256,768]{1,0:T(8,128)(2,1)} %bitcast.35, bf16[768,2304]{1,0:T(8,128)(2,1)} %param.14), kind=kOutput, calls=%fused_computation.9 | convolution fusion | flops 906559488 | bytes 5111808 | tf_op jit(solution)/shard_map/dot_general | solution.py:35
  5.2 0.1 pad_add_fusion
  5.3 0.0 collective-permute-done
  5.3 2.7 %collective-permute-start.1 = (bf16[64,768]{1,0:T(8,128)(2,1)S(1)}, bf16[64,768]{1,0:T(8,128)(2,1)S(1)}, u32[]{:S(2)}, u32[]{:S(2)}) collective-permute-start(bf16[64,768]{1,0:T(8,128)(2,1)S(1)} %broadcast_select_fusion), channel_id=1, source_target_pairs={{0,8},{4,12},{8,0},{12,4},{16,24},{20,28},{24,16},{28,20},{1,9},{5... | collective-permute-start | bytes 294920 | tf_op jit(solution)/shard_map/ppermute | solution.py:60
  8.0 0.8 %fusion.40.allow_ref = f32[4,64,256]{2,1,0:T(8,128)} fusion(s32[256]{0:T(256)S(1)} %pad_add_fusion, s32[4,64]{1,0:T(4,128)S(1)} %copy-done.9, pred[256]{0:T(512)(128)(4,1)S(1)} %iota_compare_fusion.15), kind=kLoop, calls=%fused_computation.46 | loop fusion | flops 327680 | bytes 264448 | tf_op jit(solution)/shard_map/convert_element_type | solution.py:255
  8.9 2.5 %collective-permute-done.1 = bf16[64,768]{1,0:T(8,128)(2,1)S(1)} collective-permute-done((bf16[64,768]{1,0:T(8,128)(2,1)S(1)}, bf16[64,768]{1,0:T(8,128)(2,1)S(1)}, u32[]{:S(2)}, u32[]{:S(2)}) %collective-permute-start.1) | collective-permute-done | bytes 98336 | tf_op jit(solution)/shard_map/ppermute | solution.py:60
  11.4 2.8 %collective-permute-start.2 = (bf16[64,768]{1,0:T(8,128)(2,1)S(1)}, bf16[64,768]{1,0:T(8,128)(2,1)S(1)}, u32[]{:S(2)}, u32[]{:S(2)}) collective-permute-start(bf16[64,768]{1,0:T(8,128)(2,1)S(1)} %broadcast_select_fusion.1), channel_id=1, source_target_pairs={{0,16},{4,20},{8,24},{12,28},{16,0},{20,4},{24,8},{28,12},{1,17},{... | collective-permute-start | bytes 294920 | tf_op jit(solution)/shard_map/ppermute | solution.py:60
  14.3 1.5 %collective-permute-start.3 = (bf16[4,64,768]{2,1,0:T(8,128)(2,1)S(1)}, bf16[4,64,768]{2,1,0:T(8,128)(2,1)}, u32[]{:S(2)}, u32[]{:S(2)}) collective-permute-start(bf16[4,64,768]{2,1,0:T(8,128)(2,1)S(1)} %copy-done.3), channel_id=1, source_target_pairs={{0,1},{1,0},{2,3},{3,2},{4,5},{5,4},{6,7},{7,6},{8,9},{9,8},{10,11... | collective-permute-start | bytes 1179656 | tf_op jit(solution)/shard_map/ppermute | solution.py:141
  15.7 1.5 %collective-permute-start.4 = (bf16[4,64,768]{2,1,0:T(8,128)(2,1)S(1)}, bf16[4,64,768]{2,1,0:T(8,128)(2,1)}, u32[]{:S(2)}, u32[]{:S(2)}) collective-permute-start(bf16[4,64,768]{2,1,0:T(8,128)(2,1)S(1)} %copy-done.3), channel_id=1, source_target_pairs={{0,2},{1,3},{2,0},{3,1},{4,6},{5,7},{6,4},{7,5},{8,10},{9,11},{10,... | collective-permute-start | bytes 1179656 | tf_op jit(solution)/shard_map/ppermute | solution.py:141
  17.3 0.5 collective-permute-start.5
  17.7 1.3 %collective-permute-done.2 = bf16[64,768]{1,0:T(8,128)(2,1)S(1)} collective-permute-done((bf16[64,768]{1,0:T(8,128)(2,1)S(1)}, bf16[64,768]{1,0:T(8,128)(2,1)S(1)}, u32[]{:S(2)}, u32[]{:S(2)}) %collective-permute-start.2) | collective-permute-done | bytes 98336 | tf_op jit(solution)/shard_map/ppermute | solution.py:60
  19.0 0.0 copy-start.4
  19.1 2.2 %convolution_convert_fusion.2.sk_ref.sv_ref = bf16[64,1536]{1,0:T(8,128)(2,1)S(1)} fusion(bf16[64,768]{1,0:T(8,128)(2,1)S(1)} %broadcast_select_fusion.2, bf16[768,2304]{1,0:T(8,128)(2,1)} %param.14), kind=kOutput, calls=%fused_computation.11 | convolution fusion | flops 151093248 | bytes 2654208 | tf_op jit(solution)/shard_map/dot_general | solution.py:35
  21.3 1.7 %fusion.25 = f32[64,768]{1,0:T(8,128)S(1)} fusion(bf16[64,768]{1,0:T(8,128)(2,1)S(1)} %broadcast_select_fusion.2, bf16[768,2304]{1,0:T(8,128)(2,1)} %param.14), kind=kOutput, calls=%fused_computation.26 | convolution fusion | flops 75595776 | bytes 1474560 | tf_op jit(solution)/shard_map/dot_general | solution.py:35
  23.0 0.6 %fusion.99 = (f32[64,12]{0,1:T(8,128)S(1)}, f32[4,64,12]{1,2,0:T(8,128)S(1)}) fusion(s32[768]{0:T(1024)S(1)} %add_select_fusion, bf16[4,64,2304]{2,1,0:T(8,128)(2,1)S(1)} %bitcast.30, f32[64,768]{1,0:T(8,128)S(1)} %fusion.25), kind=kOutput, calls=%fused_computation.161 | convolution fusion | flops 28719360 | bytes 609280 | tf_op jit(solution)/shard_map/dot_general | solution.py:46
  23.6 0.3 fusion.19
  24.0 0.1 slice_maximum_fusion.3
  24.0 0.1 copy.18
  24.1 0.1 copy.19
  24.2 0.1 collective-permute-start.7
  24.3 0.6 collective-permute-start.6
  24.8 0.2 convolution_multiply_fusion.1
  25.1 0.4 collective-permute-done.7
  25.4 0.1 fusion.77
  25.5 0.3 fusion.51
  25.8 0.1 fusion.79
  25.9 0.1 fusion.95
  25.9 0.0 collective-permute-done.6
  25.9 0.3 add_convert_fusion.1
  26.2 0.1 fusion.98
  26.3 0.7 %collective-permute-start.8 = (bf16[32,840]{1,0:T(8,128)(2,1)S(1)}, bf16[32,840]{1,0:T(8,128)(2,1)S(1)}, u32[]{:S(2)}, u32[]{:S(2)}) collective-permute-start(bf16[32,840]{1,0:T(8,128)(2,1)S(1)} %get-tuple-element.11), channel_id=1, source_target_pairs={{0,8},{4,12},{8,0},{12,4},{16,24},{20,28},{24,16},{28,20},{1,9},{5... | collective-permute-start | bytes 161288 | tf_op jit(solution)/shard_map/ppermute | solution.py:60
  27.0 3.5 %collective-permute-done.8 = bf16[32,840]{1,0:T(8,128)(2,1)S(1)} collective-permute-done((bf16[32,840]{1,0:T(8,128)(2,1)S(1)}, bf16[32,840]{1,0:T(8,128)(2,1)S(1)}, u32[]{:S(2)}, u32[]{:S(2)}) %collective-permute-start.8) | collective-permute-done | bytes 53792 | tf_op jit(solution)/shard_map/ppermute | solution.py:60
  30.5 0.1 broadcast_select_fusion.6
  30.6 0.1 fusion.76
  30.7 0.3 fusion.48
  31.0 0.1 fusion.80
  31.1 0.1 fusion.94
  31.1 0.3 add_convert_fusion
  31.4 0.1 fusion.97
  31.5 2.1 %collective-permute-start.9 = (bf16[32,840]{1,0:T(8,128)(2,1)S(1)}, bf16[32,840]{1,0:T(8,128)(2,1)S(1)}, u32[]{:S(2)}, u32[]{:S(2)}) collective-permute-start(bf16[32,840]{1,0:T(8,128)(2,1)S(1)} %get-tuple-element.7), channel_id=1, source_target_pairs={{0,16},{4,20},{8,24},{12,28},{16,0},{20,4},{24,8},{28,12},{1,17},{... | collective-permute-start | bytes 161288 | tf_op jit(solution)/shard_map/ppermute | solution.py:60
  33.6 0.0 collective-permute-done.3
  33.6 0.8 %collective-permute-done.4 = bf16[4,64,768]{2,1,0:T(8,128)(2,1)} collective-permute-done((bf16[4,64,768]{2,1,0:T(8,128)(2,1)S(1)}, bf16[4,64,768]{2,1,0:T(8,128)(2,1)}, u32[]{:S(2)}, u32[]{:S(2)}) %collective-permute-start.4) | collective-permute-done | bytes 393248 | tf_op jit(solution)/shard_map/ppermute | solution.py:141
  34.4 1.3 %pad_maximum_fusion = bf16[4,256,768]{2,1,0:T(8,128)(2,1)S(1)} fusion(bf16[4,64,768]{2,1,0:T(8,128)(2,1)} %collective-permute-done.5, bf16[4,64,768]{2,1,0:T(8,128)(2,1)} %collective-permute-done.4, bf16[4,64,768]{2,1,0:T(8,128)(2,1)} %collective-permute-done.3, bf16[4,64,768]{2,1,0:T(8,128)(2,1)S(1)} %copy-done.3), kind=kLoop, calls=%fused_computation.19 | loop fusion | flops 6291456 | bytes 3145728 | tf_op jit(solution)/shard_map/concatenate | solution.py:244
  35.7 0.9 %collective-permute-done.9 = bf16[32,840]{1,0:T(8,128)(2,1)S(1)} collective-permute-done((bf16[32,840]{1,0:T(8,128)(2,1)S(1)}, bf16[32,840]{1,0:T(8,128)(2,1)S(1)}, u32[]{:S(2)}, u32[]{:S(2)}) %collective-permute-start.9) | collective-permute-done | bytes 53792 | tf_op jit(solution)/shard_map/ppermute | solution.py:60
  36.6 0.1 broadcast_select_fusion.4
  36.7 0.1 slice_maximum_fusion
  36.8 0.3 fusion.47
  37.0 0.2 fusion.46
  37.3 0.2 fusion.45
  37.5 0.1 fusion.44
  37.6 0.3 fusion.28
  37.9 0.1 collective-permute-start.10
  38.0 4.0 %convolution_convert_fusion.1 = bf16[1024,1536]{1,0:T(8,128)(2,1)} fusion(bf16[1024,768]{1,0:T(8,128)(2,1)S(1)} %bitcast.33, bf16[768,2304]{1,0:T(8,128)(2,1)S(1)} %copy-done.6), kind=kOutput, calls=%fused_computation.10 | convolution fusion | flops 2417491968 | bytes 7077888 | tf_op jit(solution)/shard_map/dot_general | solution.py:35
  42.0 8.9 %shard_map.113 = bf16[4,64,768]{2,1,0:T(8,128)(2,1)} custom-call(bf16[4,64,2304]{2,1,0:T(8,128)(2,1)} %bitcast.32, bf16[4,256,1536]{2,1,0:T(8,128)(2,1)} %bitcast.28, bf16[4,256,1536]{2,1,0:T(8,128)(2,1)} %bitcast.29, bf16[64,1536]{1,0:T(8,128)(2,1)} %copy-done.2, bf16[64,1536]{1,0:T(8,128)(2,1)} %copy-done.2, f32[4,64,256]{2,1,0:T(8,128)} %fusion.40.allow_ref), custom_call_target="tpu_custom_call" | custom-call | tf_op jit(solution)/shard_map/pallas_call | solution.py:180
  51.0 1.7 %fusion.100 = (f32[320]{0:T(512)S(1)}, f32[320,768]{1,0:T(8,128)S(1)}) fusion(bf16[768,768]{1,0:T(8,128)(2,1)S(1)} %copy-done, bf16[64,768]{1,0:T(8,128)(2,1)S(1)} %maximum_select_fusion, bf16[256,768]{1,0:T(8,128)(2,1)} %bitcast.34, bf16[64,768]{1,0:T(8,128)(2,1)S(1)} %copy-done.5, bf16[256,768]{1,0:T(8,128)(2,1)S(1)} %bitcast.36), kind=kOutput, calls=%fused_computation.162 | convolution fusion | flops 379944640 | bytes 3147008 | tf_op jit(solution)/shard_map/dot_general | solution.py:25
  52.6 0.3 multiply_reduce_fusion.1
  52.9 0.0 copy-start.8
  52.9 7.4 %fusion.101 = (f32[320]{0:T(512)S(1)}, f32[320,768]{1,0:T(8,128)S(1)}) fusion(bf16[3072,768]{1,0:T(8,128)(2,1)} %param.18, bf16[768,3072]{1,0:T(8,128)(2,1)} %param.17, f32[320,768]{1,0:T(8,128)S(1)} %get-tuple-element.29, f32[768]{0:T(1024)S(1)} %copy-done.10, f32[320]{0:T(512)S(1)} %add_rsqrt_fusion.1, f32[320]{0:T(512)S(1)} %broadcast_multiply_fusion.1), kind=kOutput, calls=%fused_computation.163 | convolution fusion | flops 3031449344 | bytes 11410176 | tf_op jit(solution)/shard_map/dot_general | solution.py:30
  60.4 0.3 multiply_reduce_fusion
  60.6 0.2 multiply_convert_fusion
  60.8 0.8 %slice.220 = bf16[256,768]{1,0:T(8,128)(2,1)} slice(bf16[320,768]{1,0:T(8,128)(2,1)S(1)} %multiply_convert_fusion), slice={[0:256], [0:768]} | slice | bytes 786432 | tf_op jit(solution)/shard_map/slice | solution.py:261
  61.6 0.6 %slice.221 = bf16[64,768]{1,0:T(8,128)(2,1)} slice(bf16[320,768]{1,0:T(8,128)(2,1)S(1)} %multiply_convert_fusion), slice={[256:320], [0:768]} | slice | bytes 196608 | tf_op jit(solution)/shard_map/slice | solution.py:262
  (42 shorter events, 0.2 us)
Async XLA Ops:
  0.6 50.3 %copy-start = (bf16[768,768]{1,0:T(8,128)(2,1)S(1)}, bf16[768,768]{1,0:T(8,128)(2,1)}, u32[]{:S(2)}) copy-start(bf16[768,768]{1,0:T(8,128)(2,1)} %param.15) | copy-start | bytes 3538948
  0.6 4.6 %copy-start.7 = (bf16[1,64,768]{2,1,0:T(8,128)(2,1)S(1)}, bf16[1,64,768]{2,1,0:T(8,128)(2,1)}, u32[]{:S(2)}) copy-start(bf16[1,64,768]{2,1,0:T(8,128)(2,1)} %param.11) | copy-start | bytes 294916
  0.7 7.4 %copy-start.9 = (s32[4,64]{1,0:T(4,128)S(1)}, s32[4,64]{1,0:T(4,128)}, u32[]{:S(2)}) copy-start(s32[4,64]{1,0:T(4,128)} %param.13) | copy-start | bytes 3076
  0.7 4.6 %collective-permute-start = (bf16[64,768]{1,0:T(8,128)(2,1)}, bf16[64,768]{1,0:T(8,128)(2,1)S(1)}, u32[]{:S(2)}, u32[]{:S(2)}) collective-permute-start(bf16[64,768]{1,0:T(8,128)(2,1)} %bitcast.38), channel_id=1, source_target_pairs={{0,4},{4,0},{8,12},{12,8},{16,20},{20,16},{24,28},{28,24},{1,5},{5... | collective-permute-start | bytes 294920 | tf_op jit(solution)/shard_map/ppermute | solution.py:60
  1.8 12.4 %copy-start.3 = (bf16[4,64,768]{2,1,0:T(8,128)(2,1)S(1)}, bf16[4,64,768]{2,1,0:T(8,128)(2,1)}, u32[]{:S(2)}) copy-start(bf16[4,64,768]{2,1,0:T(8,128)(2,1)} %param.10) | copy-start | bytes 1179652
  5.1 18.8 %copy-start.1 = (bf16[256,2304]{1,0:T(8,128)(2,1)}, bf16[256,2304]{1,0:T(8,128)(2,1)S(1)}, u32[]{:S(2)}) copy-start(bf16[256,2304]{1,0:T(8,128)(2,1)S(1)} %convolution_convert_fusion) | copy-start | bytes 3538948
  5.3 6.1 %collective-permute-start.1 = (bf16[64,768]{1,0:T(8,128)(2,1)S(1)}, bf16[64,768]{1,0:T(8,128)(2,1)S(1)}, u32[]{:S(2)}, u32[]{:S(2)}) collective-permute-start(bf16[64,768]{1,0:T(8,128)(2,1)S(1)} %broadcast_select_fusion), channel_id=1, source_target_pairs={{0,8},{4,12},{8,0},{12,4},{16,24},{20,28},{24,16},{28,20},{1,9},{5... | collective-permute-start | bytes 294920 | tf_op jit(solution)/shard_map/ppermute | solution.py:60
  11.4 7.6 %collective-permute-start.2 = (bf16[64,768]{1,0:T(8,128)(2,1)S(1)}, bf16[64,768]{1,0:T(8,128)(2,1)S(1)}, u32[]{:S(2)}, u32[]{:S(2)}) collective-permute-start(bf16[64,768]{1,0:T(8,128)(2,1)S(1)} %broadcast_select_fusion.1), channel_id=1, source_target_pairs={{0,16},{4,20},{8,24},{12,28},{16,0},{20,4},{24,8},{28,12},{1,17},{... | collective-permute-start | bytes 294920 | tf_op jit(solution)/shard_map/ppermute | solution.py:60
  14.3 19.4 %collective-permute-start.3 = (bf16[4,64,768]{2,1,0:T(8,128)(2,1)S(1)}, bf16[4,64,768]{2,1,0:T(8,128)(2,1)}, u32[]{:S(2)}, u32[]{:S(2)}) collective-permute-start(bf16[4,64,768]{2,1,0:T(8,128)(2,1)S(1)} %copy-done.3), channel_id=1, source_target_pairs={{0,1},{1,0},{2,3},{3,2},{4,5},{5,4},{6,7},{7,6},{8,9},{9,8},{10,11... | collective-permute-start | bytes 1179656 | tf_op jit(solution)/shard_map/ppermute | solution.py:141
  15.7 18.6 %collective-permute-start.4 = (bf16[4,64,768]{2,1,0:T(8,128)(2,1)S(1)}, bf16[4,64,768]{2,1,0:T(8,128)(2,1)}, u32[]{:S(2)}, u32[]{:S(2)}) collective-permute-start(bf16[4,64,768]{2,1,0:T(8,128)(2,1)S(1)} %copy-done.3), channel_id=1, source_target_pairs={{0,2},{1,3},{2,0},{3,1},{4,6},{5,7},{6,4},{7,5},{8,10},{9,11},{10,... | collective-permute-start | bytes 1179656 | tf_op jit(solution)/shard_map/ppermute | solution.py:141
  17.3 17.1 %collective-permute-start.5 = (bf16[4,64,768]{2,1,0:T(8,128)(2,1)S(1)}, bf16[4,64,768]{2,1,0:T(8,128)(2,1)}, u32[]{:S(2)}, u32[]{:S(2)}) collective-permute-start(bf16[4,64,768]{2,1,0:T(8,128)(2,1)S(1)} %copy-done.3), channel_id=1, source_target_pairs={{0,3},{1,2},{2,1},{3,0},{4,7},{5,6},{6,5},{7,4},{8,11},{9,10},{10,... | collective-permute-start | bytes 1179656 | tf_op jit(solution)/shard_map/ppermute | solution.py:141
  19.0 6.0 %copy-start.4 = (bf16[64,768]{1,0:T(8,128)(2,1)}, bf16[64,768]{1,0:T(8,128)(2,1)S(1)}, u32[]{:S(2)}) copy-start(bf16[64,768]{1,0:T(8,128)(2,1)S(1)} %broadcast_select_fusion.2) | copy-start | bytes 294916
  21.3 16.3 %copy-start.2 = (bf16[64,1536]{1,0:T(8,128)(2,1)}, bf16[64,1536]{1,0:T(8,128)(2,1)S(1)}, u32[]{:S(2)}) copy-start(bf16[64,1536]{1,0:T(8,128)(2,1)S(1)} %convolution_convert_fusion.2.sk_ref.sv_ref) | copy-start | bytes 589828
  24.2 1.2 %collective-permute-start.7 = (f32[32,24]{1,0:T(8,128)S(1)}, f32[32,24]{1,0:T(8,128)S(1)}, u32[]{:S(2)}, u32[]{:S(2)}) collective-permute-start(f32[32,24]{1,0:T(8,128)S(1)} %broadcast_select_fusion.9), channel_id=1, source_target_pairs={{0,4},{4,0},{8,12},{12,8},{16,20},{20,16},{24,28},{28,24},{1,5},{5... | collective-permute-start | bytes 9224 | tf_op jit(solution)/shard_map/ppermute | solution.py:60
  24.3 1.7 %collective-permute-start.6 = (f32[32,768]{1,0:T(8,128)S(1)}, f32[32,768]{1,0:T(8,128)S(1)}, u32[]{:S(2)}, u32[]{:S(2)}) collective-permute-start(f32[32,768]{1,0:T(8,128)S(1)} %slice_select_fusion), channel_id=1, source_target_pairs={{0,4},{4,0},{8,12},{12,8},{16,20},{20,16},{24,28},{28,24},{1,5},{5... | collective-permute-start | bytes 294920 | tf_op jit(solution)/shard_map/ppermute | solution.py:60
  26.3 11.7 %copy-start.6 = (bf16[768,2304]{1,0:T(8,128)(2,1)S(1)}, bf16[768,2304]{1,0:T(8,128)(2,1)}, u32[]{:S(2)}) copy-start(bf16[768,2304]{1,0:T(8,128)(2,1)} %param.14) | copy-start | bytes 10616836
  26.3 4.2 %collective-permute-start.8 = (bf16[32,840]{1,0:T(8,128)(2,1)S(1)}, bf16[32,840]{1,0:T(8,128)(2,1)S(1)}, u32[]{:S(2)}, u32[]{:S(2)}) collective-permute-start(bf16[32,840]{1,0:T(8,128)(2,1)S(1)} %get-tuple-element.11), channel_id=1, source_target_pairs={{0,8},{4,12},{8,0},{12,4},{16,24},{20,28},{24,16},{28,20},{1,9},{5... | collective-permute-start | bytes 161288 | tf_op jit(solution)/shard_map/ppermute | solution.py:60
  31.5 5.1 %collective-permute-start.9 = (bf16[32,840]{1,0:T(8,128)(2,1)S(1)}, bf16[32,840]{1,0:T(8,128)(2,1)S(1)}, u32[]{:S(2)}, u32[]{:S(2)}) collective-permute-start(bf16[32,840]{1,0:T(8,128)(2,1)S(1)} %get-tuple-element.7), channel_id=1, source_target_pairs={{0,16},{4,20},{8,24},{12,28},{16,0},{20,4},{24,8},{28,12},{1,17},{... | collective-permute-start | bytes 161288 | tf_op jit(solution)/shard_map/ppermute | solution.py:60
  37.9 13.0 %collective-permute-start.10 = (bf16[32,768]{1,0:T(8,128)(2,1)S(1)}, bf16[32,768]{1,0:T(8,128)(2,1)S(1)}, u32[]{:S(2)}, u32[]{:S(2)}) collective-permute-start(bf16[32,768]{1,0:T(8,128)(2,1)S(1)} %fusion.28), channel_id=1, source_target_pairs={{0,4},{4,0},{8,12},{12,8},{16,20},{20,16},{24,28},{28,24},{1,5},{5... | collective-permute-start | bytes 147464 | tf_op jit(solution)/shard_map/ppermute | solution.py:60
  42.0 8.9 %copy-start.5 = (bf16[64,768]{1,0:T(8,128)(2,1)S(1)}, bf16[64,768]{1,0:T(8,128)(2,1)}, u32[]{:S(2)}) copy-start(bf16[64,768]{1,0:T(8,128)(2,1)} %copy-done.4) | copy-start | bytes 294916
  50.9 2.0 %copy-start.10 = (f32[768]{0:T(1024)S(1)}, f32[768]{0:T(1024)}, u32[]{:S(2)}) copy-start(f32[768]{0:T(1024)} %param.16) | copy-start | bytes 9220
  52.9 7.7 %copy-start.8 = (f32[768]{0:T(1024)S(1)}, f32[768]{0:T(1024)}, u32[]{:S(2)}) copy-start(f32[768]{0:T(1024)} %param.19) | copy-start | bytes 9220

commit v17 on v16

--- a/solution.py
+++ b/solution.py
@@ -87,11 +87,12 @@
 
 def pack_partial(value):
     stats = value[1]
-    high = stats.astype(jnp.bfloat16)
+    high = lax.optimization_barrier(stats.astype(jnp.bfloat16))
     rest = stats - high.astype(jnp.float32)
-    middle = rest.astype(jnp.bfloat16)
+    middle = lax.optimization_barrier(rest.astype(jnp.bfloat16))
     low = (rest - middle.astype(jnp.float32)).astype(jnp.bfloat16)
-    return jnp.concatenate([value[0].astype(jnp.bfloat16), high, middle, low], axis=-1)
+    packed = jnp.concatenate([value[0].astype(jnp.bfloat16), high, middle, low], axis=-1)
+    return lax.optimization_barrier(packed)
 
 
 def unpack_partial(packed, width):
@@ -220,7 +221,7 @@
     self_scores = head_sum(sq * sum_keys.astype(jnp.float32)) * score_scale
     part_top = col_scores.max(0)
     col_exp = jnp.exp(col_scores - part_top[None])
-    col_weights = head_spread(col_exp.astype(jnp.bfloat16).astype(jnp.float32))
+    col_weights = head_spread(lax.optimization_barrier(col_exp.astype(jnp.bfloat16)).astype(jnp.float32))
     part_mixed = (col_weights * own_vals.astype(jnp.float32)).sum(0)
     part_total = col_exp.sum(0)
     merged = half_merge(
@@ -235,7 +236,7 @@
     self_exp = jnp.exp(half_self - col_top)
     col_total = merged[1][:, :HEADS] * fade + self_exp
     col_mixed = merged[0] * head_spread(fade) + head_spread(
-        self_exp.astype(jnp.bfloat16).astype(jnp.float32)
+        lax.optimization_barrier(self_exp.astype(jnp.bfloat16)).astype(jnp.float32)
     ) * half_vals
     summary_att = (col_mixed / head_spread(col_total)).astype(jnp.bfloat16)
     summary_att = join_halves(summary_att, "band", n_band)

time: 62.6 us -> 63.1 us (level)
  transfers between devices with their start and end apart: 11 -> 11, of which waited for: 6 -> 7; matrix products, arithmetic and copies ran while one was open for 27% -> 27% of each run, Pallas kernels for 14% -> 14%
where the time goes in v17:
time: 63.1 us; the launch traced here: 62.8 us
  matrix products  23.6 us (37%)
  starting transfers between devices  13.2 us (21%)
  waiting for transfers between devices  9.55 us (15%)
  Pallas kernels  8.88 us (14%)
  other arithmetic  4.3 us (7%)
  between operations  1.68 us (3%)
  local copies, waits for them, and re-layouts  1.64 us (3%)
    dot_general x4, matrix products, project(): jnp.dot(values, weight, preferred_element_type=jnp.float32)  11.2 us
    ppermute x8, starting transfers between devices, partner(): return lax.ppermute(value, axis, [(i, i ^ step) for i in range(count)])  9.69 us
    pallas_call x1, Pallas kernels, row_attention(): pl.pallas_call(kern, grid=(rows,), in_specs=[pl.BlockSpec((1, nq, width),...  8.88 us
    ppermute x8, waiting for transfers between devices, partner(): return lax.ppermute(value, axis, [(i, i ^ step) for i in range(count)])  8.81 us
    dot_general x1, matrix products, finish(): outer_out = jnp.dot(inner_act, w_down, preferred_element_type=jnp.float32)  7.43 us
    ppermute x3, starting transfers between devices, fan_out(): got.append((source, lax.ppermute(value, axis, pairs)))  3.49 us
    dot_general x10, matrix products, head_spread(): jnp.dot(flat, head_matrix(), precision=lax.Precision.HIGHEST, preferred_e...  2.39 us
    dot_general x1, matrix products, finish(): mixed_out = jnp.dot(attended, w_out, preferred_element_type=jnp.float32)  1.65 us
  transfers between devices with their start and end apart: 11, of which 7 were waited for; matrix products, arithmetic and copies ran while one was open for 27% of the time, Pallas kernels for 14%

profile of v17, /device:TPU:0, one launch (start us, length us, event | category | flops | bytes accessed | tf_op | source)
XLA Modules:
  0.0 62.8 jit_solution(1909247015487435891)
XLA Ops:
  0.6 0.0 copy-start
  0.7 0.5 collective-permute-start
  1.8 3.3 %convolution_convert_fusion = bf16[256,2304]{1,0:T(8,128)(2,1)S(1)} fusion(bf16[256,768]{1,0:T(8,128)(2,1)} %bitcast.37, bf16[768,2304]{1,0:T(8,128)(2,1)} %param.14), kind=kOutput, calls=%fused_computation.9 | convolution fusion | flops 906559488 | bytes 5111808 | tf_op jit(solution)/shard_map/dot_general | solution.py:35
  5.2 0.1 pad_add_fusion
  5.3 2.7 %collective-permute-start.1 = (bf16[64,768]{1,0:T(8,128)(2,1)S(1)}, bf16[64,768]{1,0:T(8,128)(2,1)S(1)}, u32[]{:S(2)}, u32[]{:S(2)}) collective-permute-start(bf16[64,768]{1,0:T(8,128)(2,1)S(1)} %broadcast_select_fusion), channel_id=1, source_target_pairs={{0,8},{4,12},{8,0},{12,4},{16,24},{20,28},{24,16},{28,20},{1,9},{5... | collective-permute-start | bytes 294920 | tf_op jit(solution)/shard_map/ppermute | solution.py:60
  8.0 0.9 %fusion.40.allow_ref = f32[4,64,256]{2,1,0:T(8,128)} fusion(s32[256]{0:T(256)S(1)} %pad_add_fusion, s32[4,64]{1,0:T(4,128)S(1)} %copy-done.9, pred[256]{0:T(512)(128)(4,1)S(1)} %iota_compare_fusion.15), kind=kLoop, calls=%fused_computation.46 | loop fusion | flops 327680 | bytes 264448 | tf_op jit(solution)/shard_map/convert_element_type | solution.py:256
  8.9 2.5 %collective-permute-done.1 = bf16[64,768]{1,0:T(8,128)(2,1)S(1)} collective-permute-done((bf16[64,768]{1,0:T(8,128)(2,1)S(1)}, bf16[64,768]{1,0:T(8,128)(2,1)S(1)}, u32[]{:S(2)}, u32[]{:S(2)}) %collective-permute-start.1) | collective-permute-done | bytes 98336 | tf_op jit(solution)/shard_map/ppermute | solution.py:60
  11.4 2.8 %collective-permute-start.2 = (bf16[64,768]{1,0:T(8,128)(2,1)S(1)}, bf16[64,768]{1,0:T(8,128)(2,1)S(1)}, u32[]{:S(2)}, u32[]{:S(2)}) collective-permute-start(bf16[64,768]{1,0:T(8,128)(2,1)S(1)} %broadcast_select_fusion.1), channel_id=1, source_target_pairs={{0,16},{4,20},{8,24},{12,28},{16,0},{20,4},{24,8},{28,12},{1,17},{... | collective-permute-start | bytes 294920 | tf_op jit(solution)/shard_map/ppermute | solution.py:60
  14.3 1.5 %collective-permute-start.3 = (bf16[4,64,768]{2,1,0:T(8,128)(2,1)S(1)}, bf16[4,64,768]{2,1,0:T(8,128)(2,1)}, u32[]{:S(2)}, u32[]{:S(2)}) collective-permute-start(bf16[4,64,768]{2,1,0:T(8,128)(2,1)S(1)} %copy-done.3), channel_id=1, source_target_pairs={{0,1},{1,0},{2,3},{3,2},{4,5},{5,4},{6,7},{7,6},{8,9},{9,8},{10,11... | collective-permute-start | bytes 1179656 | tf_op jit(solution)/shard_map/ppermute | solution.py:142
  15.7 1.5 %collective-permute-start.4 = (bf16[4,64,768]{2,1,0:T(8,128)(2,1)S(1)}, bf16[4,64,768]{2,1,0:T(8,128)(2,1)}, u32[]{:S(2)}, u32[]{:S(2)}) collective-permute-start(bf16[4,64,768]{2,1,0:T(8,128)(2,1)S(1)} %copy-done.3), channel_id=1, source_target_pairs={{0,2},{1,3},{2,0},{3,1},{4,6},{5,7},{6,4},{7,5},{8,10},{9,11},{10,... | collective-permute-start | bytes 1179656 | tf_op jit(solution)/shard_map/ppermute | solution.py:142
  17.3 0.5 collective-permute-start.5
  17.7 1.3 %collective-permute-done.2 = bf16[64,768]{1,0:T(8,128)(2,1)S(1)} collective-permute-done((bf16[64,768]{1,0:T(8,128)(2,1)S(1)}, bf16[64,768]{1,0:T(8,128)(2,1)S(1)}, u32[]{:S(2)}, u32[]{:S(2)}) %collective-permute-start.2) | collective-permute-done | bytes 98336 | tf_op jit(solution)/shard_map/ppermute | solution.py:60
  19.0 0.0 copy-start.4
  19.1 2.2 %convolution_convert_fusion.2.sk_ref.sv_ref = bf16[64,1536]{1,0:T(8,128)(2,1)S(1)} fusion(bf16[64,768]{1,0:T(8,128)(2,1)S(1)} %broadcast_select_fusion.2, bf16[768,2304]{1,0:T(8,128)(2,1)} %param.14), kind=kOutput, calls=%fused_computation.11 | convolution fusion | flops 151093248 | bytes 2654208 | tf_op jit(solution)/shard_map/dot_general | solution.py:35
  21.3 1.7 %fusion.25 = f32[64,768]{1,0:T(8,128)S(1)} fusion(bf16[64,768]{1,0:T(8,128)(2,1)S(1)} %broadcast_select_fusion.2, bf16[768,2304]{1,0:T(8,128)(2,1)} %param.14), kind=kOutput, calls=%fused_computation.26 | convolution fusion | flops 75595776 | bytes 1474560 | tf_op jit(solution)/shard_map/dot_general | solution.py:35
  23.0 0.6 %fusion.94 = (f32[64,12]{0,1:T(8,128)S(1)}, f32[4,64,12]{1,2,0:T(8,128)S(1)}) fusion(s32[768]{0:T(1024)S(1)} %add_select_fusion, bf16[4,64,2304]{2,1,0:T(8,128)(2,1)S(1)} %bitcast.32, f32[64,768]{1,0:T(8,128)S(1)} %fusion.25), kind=kOutput, calls=%fused_computation.158 | convolution fusion | flops 28719360 | bytes 609280 | tf_op jit(solution)/shard_map/dot_general | solution.py:46
  23.6 0.1 slice_maximum_fusion.3
  23.7 0.1 copy.18
  23.8 0.1 copy.19
  23.9 0.1 collective-permute-start.7
  23.9 0.3 fusion.19
  24.3 0.5 collective-permute-start.6
  24.8 0.3 collective-permute-done.7
  25.1 0.1 fusion.76
  25.2 0.2 fusion.51
  25.5 0.1 fusion.92
  25.6 0.1 fusion.77
  25.6 0.1 subtract_convert_fusion.1
  25.7 0.1 collective-permute-done.6
  25.8 0.3 add_convert_fusion.1
  26.0 0.1 pad_maximum_fusion.1
  26.1 0.7 %collective-permute-start.8 = (bf16[32,840]{1,0:T(8,128)(2,1)S(1)}, bf16[32,840]{1,0:T(8,128)(2,1)S(1)}, u32[]{:S(2)}, u32[]{:S(2)}) collective-permute-start(bf16[32,840]{1,0:T(8,128)(2,1)S(1)} %pad_maximum_fusion.1), channel_id=1, source_target_pairs={{0,8},{4,12},{8,0},{12,4},{16,24},{20,28},{24,16},{28,20},{1,9},{5... | collective-permute-start | bytes 161288 | tf_op jit(solution)/shard_map/ppermute | solution.py:60
  26.8 0.2 convolution_multiply_fusion.1
  27.0 0.0 copy-start.6
  27.0 3.3 %collective-permute-done.8 = bf16[32,840]{1,0:T(8,128)(2,1)S(1)} collective-permute-done((bf16[32,840]{1,0:T(8,128)(2,1)S(1)}, bf16[32,840]{1,0:T(8,128)(2,1)S(1)}, u32[]{:S(2)}, u32[]{:S(2)}) %collective-permute-start.8) | collective-permute-done | bytes 53792 | tf_op jit(solution)/shard_map/ppermute | solution.py:60
  30.3 0.1 broadcast_select_fusion.6
  30.4 0.1 fusion.75
  30.5 0.2 fusion.48
  30.8 0.1 fusion.91
  30.8 0.1 fusion.78
  30.9 0.1 subtract_convert_fusion
  31.0 0.3 add_convert_fusion
  31.3 0.1 pad_maximum_fusion.2
  31.3 2.3 %collective-permute-start.9 = (bf16[32,840]{1,0:T(8,128)(2,1)S(1)}, bf16[32,840]{1,0:T(8,128)(2,1)S(1)}, u32[]{:S(2)}, u32[]{:S(2)}) collective-permute-start(bf16[32,840]{1,0:T(8,128)(2,1)S(1)} %pad_maximum_fusion.2), channel_id=1, source_target_pairs={{0,16},{4,20},{8,24},{12,28},{16,0},{20,4},{24,8},{28,12},{1,17},{... | collective-permute-start | bytes 161288 | tf_op jit(solution)/shard_map/ppermute | solution.py:60
  33.6 0.7 %collective-permute-done.4 = bf16[4,64,768]{2,1,0:T(8,128)(2,1)} collective-permute-done((bf16[4,64,768]{2,1,0:T(8,128)(2,1)S(1)}, bf16[4,64,768]{2,1,0:T(8,128)(2,1)}, u32[]{:S(2)}, u32[]{:S(2)}) %collective-permute-start.4) | collective-permute-done | bytes 393248 | tf_op jit(solution)/shard_map/ppermute | solution.py:142
  34.4 1.3 %pad_maximum_fusion = bf16[4,256,768]{2,1,0:T(8,128)(2,1)S(1)} fusion(bf16[4,64,768]{2,1,0:T(8,128)(2,1)} %collective-permute-done.5, bf16[4,64,768]{2,1,0:T(8,128)(2,1)} %collective-permute-done.4, bf16[4,64,768]{2,1,0:T(8,128)(2,1)} %collective-permute-done.3, bf16[4,64,768]{2,1,0:T(8,128)(2,1)S(1)} %copy-done.3), kind=kLoop, calls=%fused_computation.19 | loop fusion | flops 6291456 | bytes 3145728 | tf_op jit(solution)/shard_map/concatenate | solution.py:245
  35.7 1.4 %collective-permute-done.9 = bf16[32,840]{1,0:T(8,128)(2,1)S(1)} collective-permute-done((bf16[32,840]{1,0:T(8,128)(2,1)S(1)}, bf16[32,840]{1,0:T(8,128)(2,1)S(1)}, u32[]{:S(2)}, u32[]{:S(2)}) %collective-permute-start.9) | collective-permute-done | bytes 53792 | tf_op jit(solution)/shard_map/ppermute | solution.py:60
  37.1 0.1 broadcast_select_fusion.4
  37.2 0.1 fusion.80
  37.3 0.2 fusion.47
  37.5 0.2 fusion.46
  37.8 0.2 fusion.45
  38.0 0.1 fusion.44
  38.1 0.3 fusion.28
  38.4 0.1 collective-permute-start.10
  38.5 4.1 %convolution_convert_fusion.1 = bf16[1024,1536]{1,0:T(8,128)(2,1)} fusion(bf16[1024,768]{1,0:T(8,128)(2,1)S(1)} %bitcast.35, bf16[768,2304]{1,0:T(8,128)(2,1)S(1)} %copy-done.6), kind=kOutput, calls=%fused_computation.10 | convolution fusion | flops 2417491968 | bytes 7077888 | tf_op jit(solution)/shard_map/dot_general | solution.py:35
  42.6 8.9 %shard_map.113 = bf16[4,64,768]{2,1,0:T(8,128)(2,1)} custom-call(bf16[4,64,2304]{2,1,0:T(8,128)(2,1)} %bitcast.34, bf16[4,256,1536]{2,1,0:T(8,128)(2,1)} %bitcast.30, bf16[4,256,1536]{2,1,0:T(8,128)(2,1)} %bitcast.31, bf16[64,1536]{1,0:T(8,128)(2,1)} %copy-done.2, bf16[64,1536]{1,0:T(8,128)(2,1)} %copy-done.2, f32[4,64,256]{2,1,0:T(8,128)} %fusion.40.allow_ref), custom_call_target="tpu_custom_call" | custom-call | tf_op jit(solution)/shard_map/pallas_call | solution.py:181
  51.5 1.6 %fusion.95 = (f32[320]{0:T(512)S(1)}, f32[320,768]{1,0:T(8,128)S(1)}) fusion(bf16[768,768]{1,0:T(8,128)(2,1)S(1)} %copy-done, bf16[64,768]{1,0:T(8,128)(2,1)S(1)} %maximum_select_fusion, bf16[256,768]{1,0:T(8,128)(2,1)} %bitcast.36, bf16[64,768]{1,0:T(8,128)(2,1)S(1)} %copy-done.5, bf16[256,768]{1,0:T(8,128)(2,1)S(1)} %bitcast.38), kind=kOutput, calls=%fused_computation.159 | convolution fusion | flops 379944640 | bytes 3147008 | tf_op jit(solution)/shard_map/dot_general | solution.py:25
  53.2 0.3 multiply_reduce_fusion.1
  53.5 7.4 %fusion.96 = (f32[320]{0:T(512)S(1)}, f32[320,768]{1,0:T(8,128)S(1)}) fusion(bf16[3072,768]{1,0:T(8,128)(2,1)} %param.18, bf16[768,3072]{1,0:T(8,128)(2,1)} %param.17, f32[320,768]{1,0:T(8,128)S(1)} %get-tuple-element.26, f32[768]{0:T(1024)S(1)} %copy-done.10, f32[320]{0:T(512)S(1)} %add_rsqrt_fusion.1, f32[320]{0:T(512)S(1)} %broadcast_multiply_fusion.1), kind=kOutput, calls=%fused_computation.160 | convolution fusion | flops 3031449344 | bytes 11410176 | tf_op jit(solution)/shard_map/dot_general | solution.py:30
  60.9 0.3 multiply_reduce_fusion
  61.2 0.2 multiply_convert_fusion
  61.4 0.8 %slice.220 = bf16[256,768]{1,0:T(8,128)(2,1)} slice(bf16[320,768]{1,0:T(8,128)(2,1)S(1)} %multiply_convert_fusion), slice={[0:256], [0:768]} | slice | bytes 786432 | tf_op jit(solution)/shard_map/slice | solution.py:262
  62.2 0.6 %slice.221 = bf16[64,768]{1,0:T(8,128)(2,1)} slice(bf16[320,768]{1,0:T(8,128)(2,1)S(1)} %multiply_convert_fusion), slice={[256:320], [0:768]} | slice | bytes 196608 | tf_op jit(solution)/shard_map/slice | solution.py:263
  (45 shorter events, 0.3 us)
Async XLA Ops:
  0.6 50.9 %copy-start = (bf16[768,768]{1,0:T(8,128)(2,1)S(1)}, bf16[768,768]{1,0:T(8,128)(2,1)}, u32[]{:S(2)}) copy-start(bf16[768,768]{1,0:T(8,128)(2,1)} %param.15) | copy-start | bytes 3538948
  0.6 4.6 %copy-start.7 = (bf16[1,64,768]{2,1,0:T(8,128)(2,1)S(1)}, bf16[1,64,768]{2,1,0:T(8,128)(2,1)}, u32[]{:S(2)}) copy-start(bf16[1,64,768]{2,1,0:T(8,128)(2,1)} %param.11) | copy-start | bytes 294916
  0.7 7.4 %copy-start.9 = (s32[4,64]{1,0:T(4,128)S(1)}, s32[4,64]{1,0:T(4,128)}, u32[]{:S(2)}) copy-start(s32[4,64]{1,0:T(4,128)} %param.13) | copy-start | bytes 3076
  0.7 4.6 %collective-permute-start = (bf16[64,768]{1,0:T(8,128)(2,1)}, bf16[64,768]{1,0:T(8,128)(2,1)S(1)}, u32[]{:S(2)}, u32[]{:S(2)}) collective-permute-start(bf16[64,768]{1,0:T(8,128)(2,1)} %bitcast.40), channel_id=1, source_target_pairs={{0,4},{4,0},{8,12},{12,8},{16,20},{20,16},{24,28},{28,24},{1,5},{5... | collective-permute-start | bytes 294920 | tf_op jit(solution)/shard_map/ppermute | solution.py:60
  1.8 12.4 %copy-start.3 = (bf16[4,64,768]{2,1,0:T(8,128)(2,1)S(1)}, bf16[4,64,768]{2,1,0:T(8,128)(2,1)}, u32[]{:S(2)}) copy-start(bf16[4,64,768]{2,1,0:T(8,128)(2,1)} %param.10) | copy-start | bytes 1179652
  5.1 18.8 %copy-start.1 = (bf16[256,2304]{1,0:T(8,128)(2,1)}, bf16[256,2304]{1,0:T(8,128)(2,1)S(1)}, u32[]{:S(2)}) copy-start(bf16[256,2304]{1,0:T(8,128)(2,1)S(1)} %convolution_convert_fusion) | copy-start | bytes 3538948
  5.3 6.1 %collective-permute-start.1 = (bf16[64,768]{1,0:T(8,128)(2,1)S(1)}, bf16[64,768]{1,0:T(8,128)(2,1)S(1)}, u32[]{:S(2)}, u32[]{:S(2)}) collective-permute-start(bf16[64,768]{1,0:T(8,128)(2,1)S(1)} %broadcast_select_fusion), channel_id=1, source_target_pairs={{0,8},{4,12},{8,0},{12,4},{16,24},{20,28},{24,16},{28,20},{1,9},{5... | collective-permute-start | bytes 294920 | tf_op jit(solution)/shard_map/ppermute | solution.py:60
  11.4 7.6 %collective-permute-start.2 = (bf16[64,768]{1,0:T(8,128)(2,1)S(1)}, bf16[64,768]{1,0:T(8,128)(2,1)S(1)}, u32[]{:S(2)}, u32[]{:S(2)}) collective-permute-start(bf16[64,768]{1,0:T(8,128)(2,1)S(1)} %broadcast_select_fusion.1), channel_id=1, source_target_pairs={{0,16},{4,20},{8,24},{12,28},{16,0},{20,4},{24,8},{28,12},{1,17},{... | collective-permute-start | bytes 294920 | tf_op jit(solution)/shard_map/ppermute | solution.py:60
  14.3 19.4 %collective-permute-start.3 = (bf16[4,64,768]{2,1,0:T(8,128)(2,1)S(1)}, bf16[4,64,768]{2,1,0:T(8,128)(2,1)}, u32[]{:S(2)}, u32[]{:S(2)}) collective-permute-start(bf16[4,64,768]{2,1,0:T(8,128)(2,1)S(1)} %copy-done.3), channel_id=1, source_target_pairs={{0,1},{1,0},{2,3},{3,2},{4,5},{5,4},{6,7},{7,6},{8,9},{9,8},{10,11... | collective-permute-start | bytes 1179656 | tf_op jit(solution)/shard_map/ppermute | solution.py:142
  15.7 18.6 %collective-permute-start.4 = (bf16[4,64,768]{2,1,0:T(8,128)(2,1)S(1)}, bf16[4,64,768]{2,1,0:T(8,128)(2,1)}, u32[]{:S(2)}, u32[]{:S(2)}) collective-permute-start(bf16[4,64,768]{2,1,0:T(8,128)(2,1)S(1)} %copy-done.3), channel_id=1, source_target_pairs={{0,2},{1,3},{2,0},{3,1},{4,6},{5,7},{6,4},{7,5},{8,10},{9,11},{10,... | collective-permute-start | bytes 1179656 | tf_op jit(solution)/shard_map/ppermute | solution.py:142
  17.3 17.1 %collective-permute-start.5 = (bf16[4,64,768]{2,1,0:T(8,128)(2,1)S(1)}, bf16[4,64,768]{2,1,0:T(8,128)(2,1)}, u32[]{:S(2)}, u32[]{:S(2)}) collective-permute-start(bf16[4,64,768]{2,1,0:T(8,128)(2,1)S(1)} %copy-done.3), channel_id=1, source_target_pairs={{0,3},{1,2},{2,1},{3,0},{4,7},{5,6},{6,5},{7,4},{8,11},{9,10},{10,... | collective-permute-start | bytes 1179656 | tf_op jit(solution)/shard_map/ppermute | solution.py:142
  19.0 6.4 %copy-start.4 = (bf16[64,768]{1,0:T(8,128)(2,1)}, bf16[64,768]{1,0:T(8,128)(2,1)S(1)}, u32[]{:S(2)}) copy-start(bf16[64,768]{1,0:T(8,128)(2,1)S(1)} %broadcast_select_fusion.2) | copy-start | bytes 294916
  21.3 16.8 %copy-start.2 = (bf16[64,1536]{1,0:T(8,128)(2,1)}, bf16[64,1536]{1,0:T(8,128)(2,1)S(1)}, u32[]{:S(2)}) copy-start(bf16[64,1536]{1,0:T(8,128)(2,1)S(1)} %convolution_convert_fusion.2.sk_ref.sv_ref) | copy-start | bytes 589828
  23.9 1.2 %collective-permute-start.7 = (f32[32,24]{1,0:T(8,128)S(1)}, f32[32,24]{1,0:T(8,128)S(1)}, u32[]{:S(2)}, u32[]{:S(2)}) collective-permute-start(f32[32,24]{1,0:T(8,128)S(1)} %broadcast_select_fusion.9), channel_id=1, source_target_pairs={{0,4},{4,0},{8,12},{12,8},{16,20},{20,16},{24,28},{28,24},{1,5},{5... | collective-permute-start | bytes 9224 | tf_op jit(solution)/shard_map/ppermute | solution.py:60
  24.3 1.5 %collective-permute-start.6 = (f32[32,768]{1,0:T(8,128)S(1)}, f32[32,768]{1,0:T(8,128)S(1)}, u32[]{:S(2)}, u32[]{:S(2)}) collective-permute-start(f32[32,768]{1,0:T(8,128)S(1)} %slice_select_fusion), channel_id=1, source_target_pairs={{0,4},{4,0},{8,12},{12,8},{16,20},{20,16},{24,28},{28,24},{1,5},{5... | collective-permute-start | bytes 294920 | tf_op jit(solution)/shard_map/ppermute | solution.py:60
  26.1 4.2 %collective-permute-start.8 = (bf16[32,840]{1,0:T(8,128)(2,1)S(1)}, bf16[32,840]{1,0:T(8,128)(2,1)S(1)}, u32[]{:S(2)}, u32[]{:S(2)}) collective-permute-start(bf16[32,840]{1,0:T(8,128)(2,1)S(1)} %pad_maximum_fusion.1), channel_id=1, source_target_pairs={{0,8},{4,12},{8,0},{12,4},{16,24},{20,28},{24,16},{28,20},{1,9},{5... | collective-permute-start | bytes 161288 | tf_op jit(solution)/shard_map/ppermute | solution.py:60
  27.0 11.5 %copy-start.6 = (bf16[768,2304]{1,0:T(8,128)(2,1)S(1)}, bf16[768,2304]{1,0:T(8,128)(2,1)}, u32[]{:S(2)}) copy-start(bf16[768,2304]{1,0:T(8,128)(2,1)} %param.14) | copy-start | bytes 10616836
  31.3 5.8 %collective-permute-start.9 = (bf16[32,840]{1,0:T(8,128)(2,1)S(1)}, bf16[32,840]{1,0:T(8,128)(2,1)S(1)}, u32[]{:S(2)}, u32[]{:S(2)}) collective-permute-start(bf16[32,840]{1,0:T(8,128)(2,1)S(1)} %pad_maximum_fusion.2), channel_id=1, source_target_pairs={{0,16},{4,20},{8,24},{12,28},{16,0},{20,4},{24,8},{28,12},{1,17},{... | collective-permute-start | bytes 161288 | tf_op jit(solution)/shard_map/ppermute | solution.py:60
  38.4 13.1 %collective-permute-start.10 = (bf16[32,768]{1,0:T(8,128)(2,1)S(1)}, bf16[32,768]{1,0:T(8,128)(2,1)S(1)}, u32[]{:S(2)}, u32[]{:S(2)}) collective-permute-start(bf16[32,768]{1,0:T(8,128)(2,1)S(1)} %fusion.28), channel_id=1, source_target_pairs={{0,4},{4,0},{8,12},{12,8},{16,20},{20,16},{24,28},{28,24},{1,5},{5... | collective-permute-start | bytes 147464 | tf_op jit(solution)/shard_map/ppermute | solution.py:60
  42.6 8.9 %copy-start.5 = (bf16[64,768]{1,0:T(8,128)(2,1)S(1)}, bf16[64,768]{1,0:T(8,128)(2,1)}, u32[]{:S(2)}) copy-start(bf16[64,768]{1,0:T(8,128)(2,1)} %copy-done.4) | copy-start | bytes 294916
  51.5 2.0 %copy-start.10 = (f32[768]{0:T(1024)S(1)}, f32[768]{0:T(1024)}, u32[]{:S(2)}) copy-start(f32[768]{0:T(1024)} %param.16) | copy-start | bytes 9220
  53.5 7.7 %copy-start.8 = (f32[768]{0:T(1024)S(1)}, f32[768]{0:T(1024)}, u32[]{:S(2)}) copy-start(f32[768]{0:T(1024)} %param.19) | copy-start | bytes 9220

commit v18 on v17

--- a/solution.py
+++ b/solution.py
@@ -28,7 +28,7 @@
         jnp.bfloat16
     )
     outer_out = jnp.dot(inner_act, w_down, preferred_element_type=jnp.float32)
-    return layer_norm(hidden.astype(jnp.float32) + outer_out, gain_ffn).astype(jnp.bfloat16)
+    return hidden.astype(jnp.float32) + outer_out
 
 
 def project(values, weight):
@@ -259,8 +259,9 @@
     all_in = jnp.concatenate([flat_cells, tokens], axis=0)
     all_att = jnp.concatenate([attended, summary_att], axis=0)
     all_out = finish(all_in, all_att, w_out, gain_attn, w_up, w_down, gain_ffn)
-    cells_out = all_out[: row_count * cols_dev].reshape(row_count, cols_dev, model_width)
-    summary_out = all_out[row_count * cols_dev :]
+    cells_out = layer_norm(all_out[: row_count * cols_dev], gain_ffn).astype(jnp.bfloat16)
+    cells_out = cells_out.reshape(row_count, cols_dev, model_width)
+    summary_out = layer_norm(all_out[row_count * cols_dev :], gain_ffn).astype(jnp.bfloat16)
     return (cells_out, summary_out)
 
 

time: 63.1 us -> 63.4 us (level)
  other arithmetic: 4.3 us -> 6.12 us
  local copies, waits for them, and re-layouts: 1.64 us -> 0.22 us
    convert_element_type x1 -> x2, other arithmetic: 0.19 us -> 1.65 us  [the longest x1 0.92 us: local(): layer_norm(all_out[:row_count * cols_dev], gain_ffn).astype(jnp.bfloat16)]
    slice x2 -> x0, local copies, waits for them, and re-layouts: 1.42 us -> none  [the longest x1 0.77 us: local(): all_out[:row_count * cols_dev].reshape(row_count, cols_dev, model_width)]
where the time goes in v18:
time: 63.4 us; the launch traced here: 63.1 us
  matrix products  23.4 us (37%)
  starting transfers between devices  13.2 us (21%)
  waiting for transfers between devices  9.58 us (15%)
  Pallas kernels  8.88 us (14%)
  other arithmetic  6.12 us (10%)
  between operations  1.7 us (3%)
    dot_general x4, matrix products, project(): jnp.dot(values, weight, preferred_element_type=jnp.float32)  11.2 us
    ppermute x8, starting transfers between devices, partner(): return lax.ppermute(value, axis, [(i, i ^ step) for i in range(count)])  9.69 us
    pallas_call x1, Pallas kernels, row_attention(): pl.pallas_call(kern, grid=(rows,), in_specs=[pl.BlockSpec((1, nq, width),...  8.88 us
    ppermute x8, waiting for transfers between devices, partner(): return lax.ppermute(value, axis, [(i, i ^ step) for i in range(count)])  8.84 us
    dot_general x1, matrix products, finish(): outer_out = jnp.dot(inner_act, w_down, preferred_element_type=jnp.float32)  7.34 us
    ppermute x3, starting transfers between devices, fan_out(): got.append((source, lax.ppermute(value, axis, pairs)))  3.49 us
    dot_general x10, matrix products, head_spread(): jnp.dot(flat, head_matrix(), precision=lax.Precision.HIGHEST, preferred_e...  2.39 us
    dot_general x1, matrix products, finish(): mixed_out = jnp.dot(attended, w_out, preferred_element_type=jnp.float32)  1.65 us
  transfers between devices with their start and end apart: 11, of which 7 were waited for; matrix products, arithmetic and copies ran while one was open for 27% of the time, Pallas kernels for 14%

profile of v18, /device:TPU:0, one launch (start us, length us, event | category | flops | bytes accessed | tf_op | source)
XLA Modules:
  0.0 63.1 jit_solution(231981428063076414)
XLA Ops:
  0.6 0.0 copy-start
  0.7 0.5 collective-permute-start
  1.8 3.3 %convolution_convert_fusion = bf16[256,2304]{1,0:T(8,128)(2,1)S(1)} fusion(bf16[256,768]{1,0:T(8,128)(2,1)} %bitcast.37, bf16[768,2304]{1,0:T(8,128)(2,1)} %param.14), kind=kOutput, calls=%fused_computation.9 | convolution fusion | flops 906559488 | bytes 5111808 | tf_op jit(solution)/shard_map/dot_general | solution.py:35
  5.2 0.1 pad_add_fusion
  5.3 2.7 %collective-permute-start.1 = (bf16[64,768]{1,0:T(8,128)(2,1)S(1)}, bf16[64,768]{1,0:T(8,128)(2,1)S(1)}, u32[]{:S(2)}, u32[]{:S(2)}) collective-permute-start(bf16[64,768]{1,0:T(8,128)(2,1)S(1)} %broadcast_select_fusion), channel_id=1, source_target_pairs={{0,8},{4,12},{8,0},{12,4},{16,24},{20,28},{24,16},{28,20},{1,9},{5... | collective-permute-start | bytes 294920 | tf_op jit(solution)/shard_map/ppermute | solution.py:60
  8.0 0.8 %fusion.40.allow_ref = f32[4,64,256]{2,1,0:T(8,128)} fusion(s32[256]{0:T(256)S(1)} %pad_add_fusion, s32[4,64]{1,0:T(4,128)S(1)} %copy-done.9, pred[256]{0:T(512)(128)(4,1)S(1)} %iota_compare_fusion.15), kind=kLoop, calls=%fused_computation.48 | loop fusion | flops 327680 | bytes 264448 | tf_op jit(solution)/shard_map/convert_element_type | solution.py:256
  8.8 2.6 %collective-permute-done.1 = bf16[64,768]{1,0:T(8,128)(2,1)S(1)} collective-permute-done((bf16[64,768]{1,0:T(8,128)(2,1)S(1)}, bf16[64,768]{1,0:T(8,128)(2,1)S(1)}, u32[]{:S(2)}, u32[]{:S(2)}) %collective-permute-start.1) | collective-permute-done | bytes 98336 | tf_op jit(solution)/shard_map/ppermute | solution.py:60
  11.4 2.8 %collective-permute-start.2 = (bf16[64,768]{1,0:T(8,128)(2,1)S(1)}, bf16[64,768]{1,0:T(8,128)(2,1)S(1)}, u32[]{:S(2)}, u32[]{:S(2)}) collective-permute-start(bf16[64,768]{1,0:T(8,128)(2,1)S(1)} %broadcast_select_fusion.1), channel_id=1, source_target_pairs={{0,16},{4,20},{8,24},{12,28},{16,0},{20,4},{24,8},{28,12},{1,17},{... | collective-permute-start | bytes 294920 | tf_op jit(solution)/shard_map/ppermute | solution.py:60
  14.3 1.5 %collective-permute-start.3 = (bf16[4,64,768]{2,1,0:T(8,128)(2,1)S(1)}, bf16[4,64,768]{2,1,0:T(8,128)(2,1)}, u32[]{:S(2)}, u32[]{:S(2)}) collective-permute-start(bf16[4,64,768]{2,1,0:T(8,128)(2,1)S(1)} %copy-done.3), channel_id=1, source_target_pairs={{0,1},{1,0},{2,3},{3,2},{4,5},{5,4},{6,7},{7,6},{8,9},{9,8},{10,11... | collective-permute-start | bytes 1179656 | tf_op jit(solution)/shard_map/ppermute | solution.py:142
  15.7 1.5 %collective-permute-start.4 = (bf16[4,64,768]{2,1,0:T(8,128)(2,1)S(1)}, bf16[4,64,768]{2,1,0:T(8,128)(2,1)}, u32[]{:S(2)}, u32[]{:S(2)}) collective-permute-start(bf16[4,64,768]{2,1,0:T(8,128)(2,1)S(1)} %copy-done.3), channel_id=1, source_target_pairs={{0,2},{1,3},{2,0},{3,1},{4,6},{5,7},{6,4},{7,5},{8,10},{9,11},{10,... | collective-permute-start | bytes 1179656 | tf_op jit(solution)/shard_map/ppermute | solution.py:142
  17.3 0.5 collective-permute-start.5
  17.7 1.3 %collective-permute-done.2 = bf16[64,768]{1,0:T(8,128)(2,1)S(1)} collective-permute-done((bf16[64,768]{1,0:T(8,128)(2,1)S(1)}, bf16[64,768]{1,0:T(8,128)(2,1)S(1)}, u32[]{:S(2)}, u32[]{:S(2)}) %collective-permute-start.2) | collective-permute-done | bytes 98336 | tf_op jit(solution)/shard_map/ppermute | solution.py:60
  19.1 2.2 %convolution_convert_fusion.2.sk_ref.sv_ref = bf16[64,1536]{1,0:T(8,128)(2,1)S(1)} fusion(bf16[64,768]{1,0:T(8,128)(2,1)S(1)} %broadcast_select_fusion.2, bf16[768,2304]{1,0:T(8,128)(2,1)} %param.14), kind=kOutput, calls=%fused_computation.11 | convolution fusion | flops 151093248 | bytes 2654208 | tf_op jit(solution)/shard_map/dot_general | solution.py:35
  21.3 1.7 %fusion.25 = f32[64,768]{1,0:T(8,128)S(1)} fusion(bf16[64,768]{1,0:T(8,128)(2,1)S(1)} %broadcast_select_fusion.2, bf16[768,2304]{1,0:T(8,128)(2,1)} %param.14), kind=kOutput, calls=%fused_computation.26 | convolution fusion | flops 75595776 | bytes 1474560 | tf_op jit(solution)/shard_map/dot_general | solution.py:35
  23.0 0.6 %fusion.94 = (f32[64,12]{0,1:T(8,128)S(1)}, f32[4,64,12]{1,2,0:T(8,128)S(1)}) fusion(s32[768]{0:T(1024)S(1)} %add_select_fusion, bf16[4,64,2304]{2,1,0:T(8,128)(2,1)S(1)} %bitcast.32, f32[64,768]{1,0:T(8,128)S(1)} %fusion.25), kind=kOutput, calls=%fused_computation.166 | convolution fusion | flops 28719360 | bytes 609280 | tf_op jit(solution)/shard_map/dot_general | solution.py:46
  23.6 0.1 slice_maximum_fusion.3
  23.7 0.1 copy.18
  23.8 0.1 copy.19
  23.9 0.1 collective-permute-start.7
  23.9 0.3 fusion.19
  24.3 0.5 collective-permute-start.6
  24.8 0.3 collective-permute-done.7
  25.1 0.1 fusion.76
  25.2 0.2 fusion.51
  25.5 0.1 fusion.92
  25.6 0.1 fusion.77
  25.6 0.1 subtract_convert_fusion.1
  25.7 0.1 collective-permute-done.6
  25.8 0.3 add_convert_fusion.1
  26.0 0.1 pad_maximum_fusion.1
  26.1 0.7 %collective-permute-start.8 = (bf16[32,840]{1,0:T(8,128)(2,1)S(1)}, bf16[32,840]{1,0:T(8,128)(2,1)S(1)}, u32[]{:S(2)}, u32[]{:S(2)}) collective-permute-start(bf16[32,840]{1,0:T(8,128)(2,1)S(1)} %pad_maximum_fusion.1), channel_id=1, source_target_pairs={{0,8},{4,12},{8,0},{12,4},{16,24},{20,28},{24,16},{28,20},{1,9},{5... | collective-permute-start | bytes 161288 | tf_op jit(solution)/shard_map/ppermute | solution.py:60
  26.8 0.2 convolution_multiply_fusion.1
  27.0 3.3 %collective-permute-done.8 = bf16[32,840]{1,0:T(8,128)(2,1)S(1)} collective-permute-done((bf16[32,840]{1,0:T(8,128)(2,1)S(1)}, bf16[32,840]{1,0:T(8,128)(2,1)S(1)}, u32[]{:S(2)}, u32[]{:S(2)}) %collective-permute-start.8) | collective-permute-done | bytes 53792 | tf_op jit(solution)/shard_map/ppermute | solution.py:60
  30.3 0.1 broadcast_select_fusion.6
  30.4 0.1 fusion.75
  30.5 0.2 fusion.48
  30.8 0.1 fusion.91
  30.8 0.1 fusion.78
  30.9 0.1 subtract_convert_fusion
  31.0 0.3 add_convert_fusion
  31.3 0.1 pad_maximum_fusion.2
  31.3 2.3 %collective-permute-start.9 = (bf16[32,840]{1,0:T(8,128)(2,1)S(1)}, bf16[32,840]{1,0:T(8,128)(2,1)S(1)}, u32[]{:S(2)}, u32[]{:S(2)}) collective-permute-start(bf16[32,840]{1,0:T(8,128)(2,1)S(1)} %pad_maximum_fusion.2), channel_id=1, source_target_pairs={{0,16},{4,20},{8,24},{12,28},{16,0},{20,4},{24,8},{28,12},{1,17},{... | collective-permute-start | bytes 161288 | tf_op jit(solution)/shard_map/ppermute | solution.py:60
  33.6 0.7 %collective-permute-done.4 = bf16[4,64,768]{2,1,0:T(8,128)(2,1)} collective-permute-done((bf16[4,64,768]{2,1,0:T(8,128)(2,1)S(1)}, bf16[4,64,768]{2,1,0:T(8,128)(2,1)}, u32[]{:S(2)}, u32[]{:S(2)}) %collective-permute-start.4) | collective-permute-done | bytes 393248 | tf_op jit(solution)/shard_map/ppermute | solution.py:142
  34.4 1.3 %pad_maximum_fusion = bf16[4,256,768]{2,1,0:T(8,128)(2,1)S(1)} fusion(bf16[4,64,768]{2,1,0:T(8,128)(2,1)} %collective-permute-done.5, bf16[4,64,768]{2,1,0:T(8,128)(2,1)} %collective-permute-done.4, bf16[4,64,768]{2,1,0:T(8,128)(2,1)} %collective-permute-done.3, bf16[4,64,768]{2,1,0:T(8,128)(2,1)S(1)} %copy-done.3), kind=kLoop, calls=%fused_computation.19 | loop fusion | flops 6291456 | bytes 3145728 | tf_op jit(solution)/shard_map/concatenate | solution.py:245
  35.7 1.4 %collective-permute-done.9 = bf16[32,840]{1,0:T(8,128)(2,1)S(1)} collective-permute-done((bf16[32,840]{1,0:T(8,128)(2,1)S(1)}, bf16[32,840]{1,0:T(8,128)(2,1)S(1)}, u32[]{:S(2)}, u32[]{:S(2)}) %collective-permute-start.9) | collective-permute-done | bytes 53792 | tf_op jit(solution)/shard_map/ppermute | solution.py:60
  37.1 0.1 broadcast_select_fusion.4
  37.2 0.1 fusion.80
  37.3 0.2 fusion.47
  37.5 0.2 fusion.46
  37.8 0.2 fusion.45
  38.0 0.1 fusion.44
  38.1 0.3 fusion.28
  38.4 0.1 collective-permute-start.10
  38.5 4.0 %convolution_convert_fusion.1 = bf16[1024,1536]{1,0:T(8,128)(2,1)} fusion(bf16[1024,768]{1,0:T(8,128)(2,1)S(1)} %bitcast.35, bf16[768,2304]{1,0:T(8,128)(2,1)S(1)} %copy-done.6), kind=kOutput, calls=%fused_computation.10 | convolution fusion | flops 2417491968 | bytes 7077888 | tf_op jit(solution)/shard_map/dot_general | solution.py:35
  42.5 8.9 %shard_map.113 = bf16[4,64,768]{2,1,0:T(8,128)(2,1)} custom-call(bf16[4,64,2304]{2,1,0:T(8,128)(2,1)} %bitcast.34, bf16[4,256,1536]{2,1,0:T(8,128)(2,1)} %bitcast.30, bf16[4,256,1536]{2,1,0:T(8,128)(2,1)} %bitcast.31, bf16[64,1536]{1,0:T(8,128)(2,1)} %copy-done.2, bf16[64,1536]{1,0:T(8,128)(2,1)} %copy-done.2, f32[4,64,256]{2,1,0:T(8,128)} %fusion.40.allow_ref), custom_call_target="tpu_custom_call" | custom-call | tf_op jit(solution)/shard_map/pallas_call | solution.py:181
  51.5 1.6 %fusion.95 = (f32[320]{0:T(512)S(1)}, f32[320,768]{1,0:T(8,128)S(1)}) fusion(bf16[768,768]{1,0:T(8,128)(2,1)S(1)} %copy-done, bf16[64,768]{1,0:T(8,128)(2,1)S(1)} %maximum_select_fusion, bf16[256,768]{1,0:T(8,128)(2,1)} %bitcast.36, bf16[64,768]{1,0:T(8,128)(2,1)S(1)} %copy-done.5, bf16[256,768]{1,0:T(8,128)(2,1)S(1)} %bitcast.38), kind=kOutput, calls=%fused_computation.167 | convolution fusion | flops 379944640 | bytes 3147008 | tf_op jit(solution)/shard_map/dot_general | solution.py:25
  53.1 0.3 multiply_reduce_fusion
  53.4 7.3 %fusion.16 = f32[320,768]{1,0:T(8,128)S(1)} fusion(bf16[3072,768]{1,0:T(8,128)(2,1)} %param.18, f32[768]{0:T(1024)S(1)} %copy-done.10, f32[320]{0:T(512)S(1)} %add_rsqrt_fusion, f32[320,768]{1,0:T(8,128)S(1)} %get-tuple-element.26, f32[320]{0:T(512)S(1)} %broadcast_multiply_fusion, bf16[768,3072]{1,0:T(8,128)(2,1)} %param.17), kind=kOutput, calls=%fused_computation.21 | convolution fusion | flops 3031203840 | bytes 11408896 | tf_op jit(solution)/shard_map/dot_general | solution.py:30
  60.8 0.1 slice_reduce_fusion.1
  60.9 0.1 slice_reduce_fusion
  61.0 0.2 multiply_reduce_fusion.2
  61.2 0.2 multiply_reduce_fusion.1
  61.5 0.7 %multiply_convert_fusion.2 = bf16[64,768]{1,0:T(8,128)(2,1)} fusion(f32[320,768]{1,0:T(8,128)S(1)} %fusion.16, f32[768]{0:T(1024)S(1)} %copy-done.8, f32[64]{0:T(128)S(1)} %add_rsqrt_fusion.2, f32[64]{0:T(128)S(1)} %broadcast_multiply_fusion.2), kind=kLoop, calls=%fused_computation.49 | loop fusion | flops 196608 | bytes 298496 | tf_op jit(solution)/shard_map/convert_element_type | solution.py:264
  62.2 0.9 %multiply_convert_fusion.1 = bf16[256,768]{1,0:T(8,128)(2,1)} fusion(f32[320,768]{1,0:T(8,128)S(1)} %fusion.16, f32[768]{0:T(1024)S(1)} %copy-done.8, f32[256]{0:T(256)S(1)} %add_rsqrt_fusion.1, f32[256]{0:T(256)S(1)} %broadcast_multiply_fusion.1), kind=kLoop, calls=%fused_computation.34 | loop fusion | flops 786432 | bytes 1184768 | tf_op jit(solution)/shard_map/convert_element_type | solution.py:262
  (49 shorter events, 0.3 us)
Async XLA Ops:
  0.6 50.8 %copy-start = (bf16[768,768]{1,0:T(8,128)(2,1)S(1)}, bf16[768,768]{1,0:T(8,128)(2,1)}, u32[]{:S(2)}) copy-start(bf16[768,768]{1,0:T(8,128)(2,1)} %param.15) | copy-start | bytes 3538948
  0.6 4.6 %copy-start.7 = (bf16[1,64,768]{2,1,0:T(8,128)(2,1)S(1)}, bf16[1,64,768]{2,1,0:T(8,128)(2,1)}, u32[]{:S(2)}) copy-start(bf16[1,64,768]{2,1,0:T(8,128)(2,1)} %param.11) | copy-start | bytes 294916
  0.7 7.4 %copy-start.9 = (s32[4,64]{1,0:T(4,128)S(1)}, s32[4,64]{1,0:T(4,128)}, u32[]{:S(2)}) copy-start(s32[4,64]{1,0:T(4,128)} %param.13) | copy-start | bytes 3076
  0.7 4.6 %collective-permute-start = (bf16[64,768]{1,0:T(8,128)(2,1)}, bf16[64,768]{1,0:T(8,128)(2,1)S(1)}, u32[]{:S(2)}, u32[]{:S(2)}) collective-permute-start(bf16[64,768]{1,0:T(8,128)(2,1)} %bitcast.40), channel_id=1, source_target_pairs={{0,4},{4,0},{8,12},{12,8},{16,20},{20,16},{24,28},{28,24},{1,5},{5... | collective-permute-start | bytes 294920 | tf_op jit(solution)/shard_map/ppermute | solution.py:60
  1.8 12.4 %copy-start.3 = (bf16[4,64,768]{2,1,0:T(8,128)(2,1)S(1)}, bf16[4,64,768]{2,1,0:T(8,128)(2,1)}, u32[]{:S(2)}) copy-start(bf16[4,64,768]{2,1,0:T(8,128)(2,1)} %param.10) | copy-start | bytes 1179652
  5.1 18.8 %copy-start.1 = (bf16[256,2304]{1,0:T(8,128)(2,1)}, bf16[256,2304]{1,0:T(8,128)(2,1)S(1)}, u32[]{:S(2)}) copy-start(bf16[256,2304]{1,0:T(8,128)(2,1)S(1)} %convolution_convert_fusion) | copy-start | bytes 3538948
  5.3 6.1 %collective-permute-start.1 = (bf16[64,768]{1,0:T(8,128)(2,1)S(1)}, bf16[64,768]{1,0:T(8,128)(2,1)S(1)}, u32[]{:S(2)}, u32[]{:S(2)}) collective-permute-start(bf16[64,768]{1,0:T(8,128)(2,1)S(1)} %broadcast_select_fusion), channel_id=1, source_target_pairs={{0,8},{4,12},{8,0},{12,4},{16,24},{20,28},{24,16},{28,20},{1,9},{5... | collective-permute-start | bytes 294920 | tf_op jit(solution)/shard_map/ppermute | solution.py:60
  11.4 7.6 %collective-permute-start.2 = (bf16[64,768]{1,0:T(8,128)(2,1)S(1)}, bf16[64,768]{1,0:T(8,128)(2,1)S(1)}, u32[]{:S(2)}, u32[]{:S(2)}) collective-permute-start(bf16[64,768]{1,0:T(8,128)(2,1)S(1)} %broadcast_select_fusion.1), channel_id=1, source_target_pairs={{0,16},{4,20},{8,24},{12,28},{16,0},{20,4},{24,8},{28,12},{1,17},{... | collective-permute-start | bytes 294920 | tf_op jit(solution)/shard_map/ppermute | solution.py:60
  14.3 19.4 %collective-permute-start.3 = (bf16[4,64,768]{2,1,0:T(8,128)(2,1)S(1)}, bf16[4,64,768]{2,1,0:T(8,128)(2,1)}, u32[]{:S(2)}, u32[]{:S(2)}) collective-permute-start(bf16[4,64,768]{2,1,0:T(8,128)(2,1)S(1)} %copy-done.3), channel_id=1, source_target_pairs={{0,1},{1,0},{2,3},{3,2},{4,5},{5,4},{6,7},{7,6},{8,9},{9,8},{10,11... | collective-permute-start | bytes 1179656 | tf_op jit(solution)/shard_map/ppermute | solution.py:142
  15.7 18.6 %collective-permute-start.4 = (bf16[4,64,768]{2,1,0:T(8,128)(2,1)S(1)}, bf16[4,64,768]{2,1,0:T(8,128)(2,1)}, u32[]{:S(2)}, u32[]{:S(2)}) collective-permute-start(bf16[4,64,768]{2,1,0:T(8,128)(2,1)S(1)} %copy-done.3), channel_id=1, source_target_pairs={{0,2},{1,3},{2,0},{3,1},{4,6},{5,7},{6,4},{7,5},{8,10},{9,11},{10,... | collective-permute-start | bytes 1179656 | tf_op jit(solution)/shard_map/ppermute | solution.py:142
  17.3 17.1 %collective-permute-start.5 = (bf16[4,64,768]{2,1,0:T(8,128)(2,1)S(1)}, bf16[4,64,768]{2,1,0:T(8,128)(2,1)}, u32[]{:S(2)}, u32[]{:S(2)}) collective-permute-start(bf16[4,64,768]{2,1,0:T(8,128)(2,1)S(1)} %copy-done.3), channel_id=1, source_target_pairs={{0,3},{1,2},{2,1},{3,0},{4,7},{5,6},{6,5},{7,4},{8,11},{9,10},{10,... | collective-permute-start | bytes 1179656 | tf_op jit(solution)/shard_map/ppermute | solution.py:142
  19.0 6.4 %copy-start.4 = (bf16[64,768]{1,0:T(8,128)(2,1)}, bf16[64,768]{1,0:T(8,128)(2,1)S(1)}, u32[]{:S(2)}) copy-start(bf16[64,768]{1,0:T(8,128)(2,1)S(1)} %broadcast_select_fusion.2) | copy-start | bytes 294916
  21.3 16.8 %copy-start.2 = (bf16[64,1536]{1,0:T(8,128)(2,1)}, bf16[64,1536]{1,0:T(8,128)(2,1)S(1)}, u32[]{:S(2)}) copy-start(bf16[64,1536]{1,0:T(8,128)(2,1)S(1)} %convolution_convert_fusion.2.sk_ref.sv_ref) | copy-start | bytes 589828
  23.9 1.2 %collective-permute-start.7 = (f32[32,24]{1,0:T(8,128)S(1)}, f32[32,24]{1,0:T(8,128)S(1)}, u32[]{:S(2)}, u32[]{:S(2)}) collective-permute-start(f32[32,24]{1,0:T(8,128)S(1)} %broadcast_select_fusion.9), channel_id=1, source_target_pairs={{0,4},{4,0},{8,12},{12,8},{16,20},{20,16},{24,28},{28,24},{1,5},{5... | collective-permute-start | bytes 9224 | tf_op jit(solution)/shard_map/ppermute | solution.py:60
  24.3 1.5 %collective-permute-start.6 = (f32[32,768]{1,0:T(8,128)S(1)}, f32[32,768]{1,0:T(8,128)S(1)}, u32[]{:S(2)}, u32[]{:S(2)}) collective-permute-start(f32[32,768]{1,0:T(8,128)S(1)} %slice_select_fusion), channel_id=1, source_target_pairs={{0,4},{4,0},{8,12},{12,8},{16,20},{20,16},{24,28},{28,24},{1,5},{5... | collective-permute-start | bytes 294920 | tf_op jit(solution)/shard_map/ppermute | solution.py:60
  26.1 4.2 %collective-permute-start.8 = (bf16[32,840]{1,0:T(8,128)(2,1)S(1)}, bf16[32,840]{1,0:T(8,128)(2,1)S(1)}, u32[]{:S(2)}, u32[]{:S(2)}) collective-permute-start(bf16[32,840]{1,0:T(8,128)(2,1)S(1)} %pad_maximum_fusion.1), channel_id=1, source_target_pairs={{0,8},{4,12},{8,0},{12,4},{16,24},{20,28},{24,16},{28,20},{1,9},{5... | collective-permute-start | bytes 161288 | tf_op jit(solution)/shard_map/ppermute | solution.py:60
  27.0 11.5 %copy-start.6 = (bf16[768,2304]{1,0:T(8,128)(2,1)S(1)}, bf16[768,2304]{1,0:T(8,128)(2,1)}, u32[]{:S(2)}) copy-start(bf16[768,2304]{1,0:T(8,128)(2,1)} %param.14) | copy-start | bytes 10616836
  31.3 5.8 %collective-permute-start.9 = (bf16[32,840]{1,0:T(8,128)(2,1)S(1)}, bf16[32,840]{1,0:T(8,128)(2,1)S(1)}, u32[]{:S(2)}, u32[]{:S(2)}) collective-permute-start(bf16[32,840]{1,0:T(8,128)(2,1)S(1)} %pad_maximum_fusion.2), channel_id=1, source_target_pairs={{0,16},{4,20},{8,24},{12,28},{16,0},{20,4},{24,8},{28,12},{1,17},{... | collective-permute-start | bytes 161288 | tf_op jit(solution)/shard_map/ppermute | solution.py:60
  38.4 13.0 %collective-permute-start.10 = (bf16[32,768]{1,0:T(8,128)(2,1)S(1)}, bf16[32,768]{1,0:T(8,128)(2,1)S(1)}, u32[]{:S(2)}, u32[]{:S(2)}) collective-permute-start(bf16[32,768]{1,0:T(8,128)(2,1)S(1)} %fusion.28), channel_id=1, source_target_pairs={{0,4},{4,0},{8,12},{12,8},{16,20},{20,16},{24,28},{28,24},{1,5},{5... | collective-permute-start | bytes 147464 | tf_op jit(solution)/shard_map/ppermute | solution.py:60
  42.5 8.9 %copy-start.5 = (bf16[64,768]{1,0:T(8,128)(2,1)S(1)}, bf16[64,768]{1,0:T(8,128)(2,1)}, u32[]{:S(2)}) copy-start(bf16[64,768]{1,0:T(8,128)(2,1)} %copy-done.4) | copy-start | bytes 294916
  51.4 2.0 %copy-start.10 = (f32[768]{0:T(1024)S(1)}, f32[768]{0:T(1024)}, u32[]{:S(2)}) copy-start(f32[768]{0:T(1024)} %param.16) | copy-start | bytes 9220
  53.4 8.1 %copy-start.8 = (f32[768]{0:T(1024)S(1)}, f32[768]{0:T(1024)}, u32[]{:S(2)}) copy-start(f32[768]{0:T(1024)} %param.19) | copy-start | bytes 9220

commit v19 on v17

--- a/solution.py
+++ b/solution.py
@@ -102,7 +102,7 @@
     return part[:, :width], stats
 
 
-def half_merge(value, axis, count):
+def half_merge(value, axis, count, rider):
     here = lax.axis_index(axis)
     half = value[0].shape[0] // 2
     first = (here & 1) == 0
@@ -115,12 +115,15 @@
     step = 2
     while step < count:
         packed = pack_partial(value)
-        got = unpack_partial(partner(packed, axis, step, count), value[0].shape[1])
+        got = partner(packed, axis, step, count)
+        if step * 2 >= count:
+            got, rider = lax.optimization_barrier((got, rider))
+        got = unpack_partial(got, value[0].shape[1])
         mine = unpack_partial(packed, value[0].shape[1])
         low_side = (here & step) == 0
         value = merge(pick(low_side, mine, got), pick(low_side, got, mine))
         step *= 2
-    return value
+    return value, rider
 
 
 def join_halves(value, axis, count):
@@ -224,8 +227,12 @@
     col_weights = head_spread(lax.optimization_barrier(col_exp.astype(jnp.bfloat16)).astype(jnp.float32))
     part_mixed = (col_weights * own_vals.astype(jnp.float32)).sum(0)
     part_total = col_exp.sum(0)
-    merged = half_merge(
-        (part_mixed, jnp.concatenate([part_total, part_top], axis=-1)), "band", n_band
+    row_cells = jnp.concatenate([cells] + [got for _, got in row_parts], axis=1)
+    width_now = row_cells.shape[1]
+    row_kv = project(row_cells.reshape(row_count * width_now, model_width), w_kv)
+    row_kv = row_kv.reshape(row_count, width_now, 2 * model_width)
+    merged, row_kv = half_merge(
+        (part_mixed, jnp.concatenate([part_total, part_top], axis=-1)), "band", n_band, row_kv
     )
     half = cols_dev // 2
     first = (own_band & 1) == 0
@@ -242,10 +249,6 @@
     summary_att = join_halves(summary_att, "band", n_band)
 
     sources = [own_group] + [s for s, _ in row_parts]
-    row_cells = jnp.concatenate([cells] + [got for _, got in row_parts], axis=1)
-    width_now = row_cells.shape[1]
-    row_kv = project(row_cells.reshape(row_count * width_now, model_width), w_kv)
-    row_kv = row_kv.reshape(row_count, width_now, 2 * model_width)
     key_groups = jnp.concatenate(
         [jnp.full((cols_dev,), s, jnp.int32) for s in sources]
     )

time: 63.1 us -> 62.6 us (level)
  matrix products: 23.6 us -> 20.6 us
  waiting for transfers between devices: 9.55 us -> 11.9 us
    ppermute x3, waiting for transfers between devices: 0.74 us -> 3.75 us  [fan_out(): got.append((source, lax.ppermute(value, axis, pairs)))]
    dot_general x4, matrix products: 11.2 us -> 8.28 us  [project(): jnp.dot(values, weight, preferred_element_type=jnp.float32)]
  transfers between devices with their start and end apart: 11 -> 11, of which waited for: 7 -> 6; matrix products, arithmetic and copies ran while one was open for 27% -> 22% of each run, Pallas kernels for 14% -> 14%
where the time goes in v19:
time: 62.6 us; the launch traced here: 62.3 us
  matrix products  20.6 us (33%)
  starting transfers between devices  13.2 us (21%)
  waiting for transfers between devices  11.9 us (19%)
  Pallas kernels  8.88 us (14%)
  other arithmetic  4.29 us (7%)
  between operations  1.75 us (3%)
  local copies, waits for them, and re-layouts  1.63 us (3%)
    ppermute x8, starting transfers between devices, partner(): return lax.ppermute(value, axis, [(i, i ^ step) for i in range(count)])  9.73 us
    pallas_call x1, Pallas kernels, row_attention(): pl.pallas_call(kern, grid=(rows,), in_specs=[pl.BlockSpec((1, nq, width),...  8.88 us
    dot_general x4, matrix products, project(): jnp.dot(values, weight, preferred_element_type=jnp.float32)  8.28 us
    ppermute x8, waiting for transfers between devices, partner(): return lax.ppermute(value, axis, [(i, i ^ step) for i in range(count)])  8.19 us
    dot_general x1, matrix products, finish(): outer_out = jnp.dot(inner_act, w_down, preferred_element_type=jnp.float32)  7.43 us
    ppermute x3, waiting for transfers between devices, fan_out(): got.append((source, lax.ppermute(value, axis, pairs)))  3.75 us
    ppermute x3, starting transfers between devices, fan_out(): got.append((source, lax.ppermute(value, axis, pairs)))  3.49 us
    dot_general x10, matrix products, head_spread(): jnp.dot(flat, head_matrix(), precision=lax.Precision.HIGHEST, preferred_e...  2.39 us
  transfers between devices with their start and end apart: 11, of which 6 were waited for; matrix products, arithmetic and copies ran while one was open for 22% of the time, Pallas kernels for 14%

profile of v19, /device:TPU:0, one launch (start us, length us, event | category | flops | bytes accessed | tf_op | source)
XLA Modules:
  0.0 62.3 jit_solution(4853724529555243734)
XLA Ops:
  0.6 0.0 copy-start
  0.7 0.5 collective-permute-start
  1.9 0.0 copy-start.6
  1.9 3.4 %convolution_convert_fusion = bf16[256,2304]{1,0:T(8,128)(2,1)S(1)} fusion(bf16[256,768]{1,0:T(8,128)(2,1)} %bitcast.37, bf16[768,2304]{1,0:T(8,128)(2,1)} %param.14), kind=kOutput, calls=%fused_computation.9 | convolution fusion | flops 906559488 | bytes 5111808 | tf_op jit(solution)/shard_map/dot_general | solution.py:35
  5.3 2.7 %collective-permute-start.1 = (bf16[64,768]{1,0:T(8,128)(2,1)S(1)}, bf16[64,768]{1,0:T(8,128)(2,1)S(1)}, u32[]{:S(2)}, u32[]{:S(2)}) collective-permute-start(bf16[64,768]{1,0:T(8,128)(2,1)S(1)} %broadcast_select_fusion), channel_id=1, source_target_pairs={{0,8},{4,12},{8,0},{12,4},{16,24},{20,28},{24,16},{28,20},{1,9},{5... | collective-permute-start | bytes 294920 | tf_op jit(solution)/shard_map/ppermute | solution.py:60
  8.1 0.1 pad_add_fusion
  8.2 3.3 %collective-permute-done.1 = bf16[64,768]{1,0:T(8,128)(2,1)S(1)} collective-permute-done((bf16[64,768]{1,0:T(8,128)(2,1)S(1)}, bf16[64,768]{1,0:T(8,128)(2,1)S(1)}, u32[]{:S(2)}, u32[]{:S(2)}) %collective-permute-start.1) | collective-permute-done | bytes 98336 | tf_op jit(solution)/shard_map/ppermute | solution.py:60
  11.5 2.8 %collective-permute-start.2 = (bf16[64,768]{1,0:T(8,128)(2,1)S(1)}, bf16[64,768]{1,0:T(8,128)(2,1)S(1)}, u32[]{:S(2)}, u32[]{:S(2)}) collective-permute-start(bf16[64,768]{1,0:T(8,128)(2,1)S(1)} %broadcast_select_fusion.1), channel_id=1, source_target_pairs={{0,16},{4,20},{8,24},{12,28},{16,0},{20,4},{24,8},{28,12},{1,17},{... | collective-permute-start | bytes 294920 | tf_op jit(solution)/shard_map/ppermute | solution.py:60
  14.3 1.5 %collective-permute-start.7 = (bf16[4,64,768]{2,1,0:T(8,128)(2,1)S(1)}, bf16[4,64,768]{2,1,0:T(8,128)(2,1)}, u32[]{:S(2)}, u32[]{:S(2)}) collective-permute-start(bf16[4,64,768]{2,1,0:T(8,128)(2,1)S(1)} %copy-done.3), channel_id=1, source_target_pairs={{0,1},{1,0},{2,3},{3,2},{4,5},{5,4},{6,7},{7,6},{8,9},{9,8},{10,11... | collective-permute-start | bytes 1179656 | tf_op jit(solution)/shard_map/ppermute | solution.py:145
  15.8 1.5 %collective-permute-start.8 = (bf16[4,64,768]{2,1,0:T(8,128)(2,1)S(1)}, bf16[4,64,768]{2,1,0:T(8,128)(2,1)}, u32[]{:S(2)}, u32[]{:S(2)}) collective-permute-start(bf16[4,64,768]{2,1,0:T(8,128)(2,1)S(1)} %copy-done.3), channel_id=1, source_target_pairs={{0,2},{1,3},{2,0},{3,1},{4,6},{5,7},{6,4},{7,5},{8,10},{9,11},{10,... | collective-permute-start | bytes 1179656 | tf_op jit(solution)/shard_map/ppermute | solution.py:145
  17.3 0.5 collective-permute-start.9
  17.8 1.3 %collective-permute-done.2 = bf16[64,768]{1,0:T(8,128)(2,1)S(1)} collective-permute-done((bf16[64,768]{1,0:T(8,128)(2,1)S(1)}, bf16[64,768]{1,0:T(8,128)(2,1)S(1)}, u32[]{:S(2)}, u32[]{:S(2)}) %collective-permute-start.2) | collective-permute-done | bytes 98336 | tf_op jit(solution)/shard_map/ppermute | solution.py:60
  19.1 0.0 copy-start.4
  19.1 0.3 fusion.25
  19.4 0.5 convolution_convert_fusion.2.sk_ref.sv_ref
  20.0 0.6 %fusion.93 = (f32[64,12]{0,1:T(8,128)S(1)}, f32[4,64,12]{1,2,0:T(8,128)S(1)}) fusion(s32[768]{0:T(1024)S(1)} %add_select_fusion, bf16[4,64,2304]{2,1,0:T(8,128)(2,1)S(1)} %bitcast.32, f32[64,768]{1,0:T(8,128)S(1)} %fusion.25), kind=kOutput, calls=%fused_computation.160 | convolution fusion | flops 28719360 | bytes 609280 | tf_op jit(solution)/shard_map/dot_general | solution.py:46
  20.6 0.1 slice_maximum_fusion.3
  20.7 0.1 copy.18
  20.8 0.1 copy.19
  20.9 0.1 collective-permute-start.4
  20.9 0.3 fusion.19
  21.2 0.0 copy-start.7
  21.3 0.6 collective-permute-start.3
  21.8 0.3 collective-permute-done.4
  22.1 0.1 fusion.75
  22.2 0.2 fusion.50
  22.5 0.1 fusion.91
  22.5 0.1 fusion.76
  22.6 0.1 subtract_convert_fusion.1
  22.7 0.1 collective-permute-done.3
  22.8 0.2 add_convert_fusion.1
  23.0 0.1 pad_maximum_fusion.1
  23.1 0.7 %collective-permute-start.5 = (bf16[32,840]{1,0:T(8,128)(2,1)S(1)}, bf16[32,840]{1,0:T(8,128)(2,1)S(1)}, u32[]{:S(2)}, u32[]{:S(2)}) collective-permute-start(bf16[32,840]{1,0:T(8,128)(2,1)S(1)} %pad_maximum_fusion.1), channel_id=1, source_target_pairs={{0,8},{4,12},{8,0},{12,4},{16,24},{20,28},{24,16},{28,20},{1,9},{5... | collective-permute-start | bytes 161288 | tf_op jit(solution)/shard_map/ppermute | solution.py:60
  23.8 0.2 convolution_multiply_fusion.4
  24.0 3.3 %collective-permute-done.5 = bf16[32,840]{1,0:T(8,128)(2,1)S(1)} collective-permute-done((bf16[32,840]{1,0:T(8,128)(2,1)S(1)}, bf16[32,840]{1,0:T(8,128)(2,1)S(1)}, u32[]{:S(2)}, u32[]{:S(2)}) %collective-permute-start.5) | collective-permute-done | bytes 53792 | tf_op jit(solution)/shard_map/ppermute | solution.py:60
  27.3 0.1 broadcast_select_fusion.6
  27.4 0.1 fusion.74
  27.5 0.2 fusion.47
  27.8 0.1 fusion.90
  27.9 0.1 fusion.77
  27.9 0.1 subtract_convert_fusion
  28.0 0.3 add_convert_fusion
  28.3 0.1 pad_maximum_fusion.2
  28.4 2.3 %collective-permute-start.6 = (bf16[32,840]{1,0:T(8,128)(2,1)S(1)}, bf16[32,840]{1,0:T(8,128)(2,1)S(1)}, u32[]{:S(2)}, u32[]{:S(2)}) collective-permute-start(bf16[32,840]{1,0:T(8,128)(2,1)S(1)} %pad_maximum_fusion.2), channel_id=1, source_target_pairs={{0,16},{4,20},{8,24},{12,28},{16,0},{20,4},{24,8},{28,12},{1,17},{... | collective-permute-start | bytes 161288 | tf_op jit(solution)/shard_map/ppermute | solution.py:60
  30.7 3.7 %collective-permute-done.8 = bf16[4,64,768]{2,1,0:T(8,128)(2,1)} collective-permute-done((bf16[4,64,768]{2,1,0:T(8,128)(2,1)S(1)}, bf16[4,64,768]{2,1,0:T(8,128)(2,1)}, u32[]{:S(2)}, u32[]{:S(2)}) %collective-permute-start.8) | collective-permute-done | bytes 393248 | tf_op jit(solution)/shard_map/ppermute | solution.py:145
  34.4 1.3 %pad_maximum_fusion = bf16[4,256,768]{2,1,0:T(8,128)(2,1)S(1)} fusion(bf16[4,64,768]{2,1,0:T(8,128)(2,1)} %collective-permute-done.9, bf16[4,64,768]{2,1,0:T(8,128)(2,1)} %collective-permute-done.8, bf16[4,64,768]{2,1,0:T(8,128)(2,1)} %collective-permute-done.7, bf16[4,64,768]{2,1,0:T(8,128)(2,1)S(1)} %copy-done.3), kind=kLoop, calls=%fused_computation.19 | loop fusion | flops 6291456 | bytes 3145728 | tf_op jit(solution)/shard_map/concatenate | solution.py:230
  35.8 4.1 %convolution_convert_fusion.1 = bf16[1024,1536]{1,0:T(8,128)(2,1)} fusion(bf16[1024,768]{1,0:T(8,128)(2,1)S(1)} %bitcast.35, bf16[768,2304]{1,0:T(8,128)(2,1)S(1)} %copy-done.7), kind=kOutput, calls=%fused_computation.10 | convolution fusion | flops 2417491968 | bytes 7077888 | tf_op jit(solution)/shard_map/dot_general | solution.py:35
  39.9 0.1 broadcast_select_fusion.4
  39.9 0.1 fusion.79
  40.0 0.3 convolution_multiply_fusion.3
  40.3 0.3 fusion.29
  40.5 0.1 fusion.46
  40.7 0.2 fusion.28
  40.9 0.3 fusion.30
  41.2 0.1 collective-permute-start.10
  41.2 0.8 %fusion.42.allow_ref = f32[4,64,256]{2,1,0:T(8,128)} fusion(s32[256]{0:T(256)S(1)} %pad_add_fusion, s32[4,64]{1,0:T(4,128)S(1)} %copy-done.10, pred[256]{0:T(512)(128)(4,1)S(1)} %iota_compare_fusion.15), kind=kLoop, calls=%fused_computation.51 | loop fusion | flops 327680 | bytes 264448 | tf_op jit(solution)/shard_map/convert_element_type | solution.py:259
  42.1 8.9 %shard_map.113 = bf16[4,64,768]{2,1,0:T(8,128)(2,1)} custom-call(bf16[4,64,2304]{2,1,0:T(8,128)(2,1)} %bitcast.34, bf16[4,256,1536]{2,1,0:T(8,128)(2,1)} %bitcast.30, bf16[4,256,1536]{2,1,0:T(8,128)(2,1)} %bitcast.31, bf16[64,1536]{1,0:T(8,128)(2,1)} %copy-done.2, bf16[64,1536]{1,0:T(8,128)(2,1)} %copy-done.2, f32[4,64,256]{2,1,0:T(8,128)} %fusion.42.allow_ref), custom_call_target="tpu_custom_call" | custom-call | tf_op jit(solution)/shard_map/pallas_call | solution.py:184
  51.0 1.7 %fusion.94 = (f32[320]{0:T(512)S(1)}, f32[320,768]{1,0:T(8,128)S(1)}) fusion(bf16[768,768]{1,0:T(8,128)(2,1)S(1)} %copy-done, bf16[64,768]{1,0:T(8,128)(2,1)S(1)} %maximum_select_fusion, bf16[256,768]{1,0:T(8,128)(2,1)} %bitcast.36, bf16[64,768]{1,0:T(8,128)(2,1)S(1)} %copy-done.5, bf16[256,768]{1,0:T(8,128)(2,1)S(1)} %bitcast.38), kind=kOutput, calls=%fused_computation.161 | convolution fusion | flops 379944640 | bytes 3147008 | tf_op jit(solution)/shard_map/dot_general | solution.py:25
  52.7 0.3 multiply_reduce_fusion.1
  53.0 7.4 %fusion.95 = (f32[320]{0:T(512)S(1)}, f32[320,768]{1,0:T(8,128)S(1)}) fusion(bf16[3072,768]{1,0:T(8,128)(2,1)} %param.18, bf16[768,3072]{1,0:T(8,128)(2,1)} %param.17, f32[320,768]{1,0:T(8,128)S(1)} %get-tuple-element.30, f32[768]{0:T(1024)S(1)} %copy-done.11, f32[320]{0:T(512)S(1)} %add_rsqrt_fusion.1, f32[320]{0:T(512)S(1)} %broadcast_multiply_fusion.1), kind=kOutput, calls=%fused_computation.162 | convolution fusion | flops 3031449344 | bytes 11410176 | tf_op jit(solution)/shard_map/dot_general | solution.py:30
  60.4 0.3 multiply_reduce_fusion
  60.7 0.2 multiply_convert_fusion
  60.9 0.8 %slice.220 = bf16[256,768]{1,0:T(8,128)(2,1)} slice(bf16[320,768]{1,0:T(8,128)(2,1)S(1)} %multiply_convert_fusion), slice={[0:256], [0:768]} | slice | bytes 786432 | tf_op jit(solution)/shard_map/slice | solution.py:265
  61.7 0.6 %slice.221 = bf16[64,768]{1,0:T(8,128)(2,1)} slice(bf16[320,768]{1,0:T(8,128)(2,1)S(1)} %multiply_convert_fusion), slice={[256:320], [0:768]} | slice | bytes 196608 | tf_op jit(solution)/shard_map/slice | solution.py:266
  (47 shorter events, 0.2 us)
Async XLA Ops:
  0.6 50.4 %copy-start = (bf16[768,768]{1,0:T(8,128)(2,1)S(1)}, bf16[768,768]{1,0:T(8,128)(2,1)}, u32[]{:S(2)}) copy-start(bf16[768,768]{1,0:T(8,128)(2,1)} %param.15) | copy-start | bytes 3538948
  0.6 4.7 %copy-start.8 = (bf16[1,64,768]{2,1,0:T(8,128)(2,1)S(1)}, bf16[1,64,768]{2,1,0:T(8,128)(2,1)}, u32[]{:S(2)}) copy-start(bf16[1,64,768]{2,1,0:T(8,128)(2,1)} %param.11) | copy-start | bytes 294916
  0.7 4.6 %collective-permute-start = (bf16[64,768]{1,0:T(8,128)(2,1)}, bf16[64,768]{1,0:T(8,128)(2,1)S(1)}, u32[]{:S(2)}, u32[]{:S(2)}) collective-permute-start(bf16[64,768]{1,0:T(8,128)(2,1)} %bitcast.40), channel_id=1, source_target_pairs={{0,4},{4,0},{8,12},{12,8},{16,20},{20,16},{24,28},{28,24},{1,5},{5... | collective-permute-start | bytes 294920 | tf_op jit(solution)/shard_map/ppermute | solution.py:60
  1.8 12.5 %copy-start.3 = (bf16[4,64,768]{2,1,0:T(8,128)(2,1)S(1)}, bf16[4,64,768]{2,1,0:T(8,128)(2,1)}, u32[]{:S(2)}) copy-start(bf16[4,64,768]{2,1,0:T(8,128)(2,1)} %param.10) | copy-start | bytes 1179652
  1.9 17.2 %copy-start.6 = (bf16[768,2304]{1,0:T(8,128)(2,1)S(1)}, bf16[768,2304]{1,0:T(8,128)(2,1)}, u32[]{:S(2)}) copy-start(bf16[768,2304]{1,0:T(8,128)(2,1)} %param.14) | copy-start | bytes 10616836
  5.3 16.0 %copy-start.1 = (bf16[256,2304]{1,0:T(8,128)(2,1)}, bf16[256,2304]{1,0:T(8,128)(2,1)S(1)}, u32[]{:S(2)}) copy-start(bf16[256,2304]{1,0:T(8,128)(2,1)S(1)} %convolution_convert_fusion) | copy-start | bytes 3538948
  5.3 6.1 %collective-permute-start.1 = (bf16[64,768]{1,0:T(8,128)(2,1)S(1)}, bf16[64,768]{1,0:T(8,128)(2,1)S(1)}, u32[]{:S(2)}, u32[]{:S(2)}) collective-permute-start(bf16[64,768]{1,0:T(8,128)(2,1)S(1)} %broadcast_select_fusion), channel_id=1, source_target_pairs={{0,8},{4,12},{8,0},{12,4},{16,24},{20,28},{24,16},{28,20},{1,9},{5... | collective-permute-start | bytes 294920 | tf_op jit(solution)/shard_map/ppermute | solution.py:60
  11.5 7.6 %collective-permute-start.2 = (bf16[64,768]{1,0:T(8,128)(2,1)S(1)}, bf16[64,768]{1,0:T(8,128)(2,1)S(1)}, u32[]{:S(2)}, u32[]{:S(2)}) collective-permute-start(bf16[64,768]{1,0:T(8,128)(2,1)S(1)} %broadcast_select_fusion.1), channel_id=1, source_target_pairs={{0,16},{4,20},{8,24},{12,28},{16,0},{20,4},{24,8},{28,12},{1,17},{... | collective-permute-start | bytes 294920 | tf_op jit(solution)/shard_map/ppermute | solution.py:60
  14.3 16.4 %collective-permute-start.7 = (bf16[4,64,768]{2,1,0:T(8,128)(2,1)S(1)}, bf16[4,64,768]{2,1,0:T(8,128)(2,1)}, u32[]{:S(2)}, u32[]{:S(2)}) collective-permute-start(bf16[4,64,768]{2,1,0:T(8,128)(2,1)S(1)} %copy-done.3), channel_id=1, source_target_pairs={{0,1},{1,0},{2,3},{3,2},{4,5},{5,4},{6,7},{7,6},{8,9},{9,8},{10,11... | collective-permute-start | bytes 1179656 | tf_op jit(solution)/shard_map/ppermute | solution.py:145
  15.8 18.6 %collective-permute-start.8 = (bf16[4,64,768]{2,1,0:T(8,128)(2,1)S(1)}, bf16[4,64,768]{2,1,0:T(8,128)(2,1)}, u32[]{:S(2)}, u32[]{:S(2)}) collective-permute-start(bf16[4,64,768]{2,1,0:T(8,128)(2,1)S(1)} %copy-done.3), channel_id=1, source_target_pairs={{0,2},{1,3},{2,0},{3,1},{4,6},{5,7},{6,4},{7,5},{8,10},{9,11},{10,... | collective-permute-start | bytes 1179656 | tf_op jit(solution)/shard_map/ppermute | solution.py:145
  17.3 17.1 %collective-permute-start.9 = (bf16[4,64,768]{2,1,0:T(8,128)(2,1)S(1)}, bf16[4,64,768]{2,1,0:T(8,128)(2,1)}, u32[]{:S(2)}, u32[]{:S(2)}) collective-permute-start(bf16[4,64,768]{2,1,0:T(8,128)(2,1)S(1)} %copy-done.3), channel_id=1, source_target_pairs={{0,3},{1,2},{2,1},{3,0},{4,7},{5,6},{6,5},{7,4},{8,11},{9,10},{10,... | collective-permute-start | bytes 1179656 | tf_op jit(solution)/shard_map/ppermute | solution.py:145
  19.1 3.4 %copy-start.4 = (bf16[64,768]{1,0:T(8,128)(2,1)}, bf16[64,768]{1,0:T(8,128)(2,1)S(1)}, u32[]{:S(2)}) copy-start(bf16[64,768]{1,0:T(8,128)(2,1)S(1)} %broadcast_select_fusion.2) | copy-start | bytes 294916
  20.0 20.7 %copy-start.2 = (bf16[64,1536]{1,0:T(8,128)(2,1)}, bf16[64,1536]{1,0:T(8,128)(2,1)S(1)}, u32[]{:S(2)}) copy-start(bf16[64,1536]{1,0:T(8,128)(2,1)S(1)} %convolution_convert_fusion.2.sk_ref.sv_ref) | copy-start | bytes 589828
  20.9 1.2 %collective-permute-start.4 = (f32[32,24]{1,0:T(8,128)S(1)}, f32[32,24]{1,0:T(8,128)S(1)}, u32[]{:S(2)}, u32[]{:S(2)}) collective-permute-start(f32[32,24]{1,0:T(8,128)S(1)} %broadcast_select_fusion.9), channel_id=1, source_target_pairs={{0,4},{4,0},{8,12},{12,8},{16,20},{20,16},{24,28},{28,24},{1,5},{5... | collective-permute-start | bytes 9224 | tf_op jit(solution)/shard_map/ppermute | solution.py:60
  21.2 14.5 %copy-start.7 = (bf16[768,2304]{1,0:T(8,128)(2,1)S(1)}, bf16[768,2304]{1,0:T(8,128)(2,1)}, u32[]{:S(2)}) copy-start(bf16[768,2304]{1,0:T(8,128)(2,1)} %param.14) | copy-start | bytes 10616836
  21.3 1.5 %collective-permute-start.3 = (f32[32,768]{1,0:T(8,128)S(1)}, f32[32,768]{1,0:T(8,128)S(1)}, u32[]{:S(2)}, u32[]{:S(2)}) collective-permute-start(f32[32,768]{1,0:T(8,128)S(1)} %slice_select_fusion), channel_id=1, source_target_pairs={{0,4},{4,0},{8,12},{12,8},{16,20},{20,16},{24,28},{28,24},{1,5},{5... | collective-permute-start | bytes 294920 | tf_op jit(solution)/shard_map/ppermute | solution.py:60
  23.1 4.2 %collective-permute-start.5 = (bf16[32,840]{1,0:T(8,128)(2,1)S(1)}, bf16[32,840]{1,0:T(8,128)(2,1)S(1)}, u32[]{:S(2)}, u32[]{:S(2)}) collective-permute-start(bf16[32,840]{1,0:T(8,128)(2,1)S(1)} %pad_maximum_fusion.1), channel_id=1, source_target_pairs={{0,8},{4,12},{8,0},{12,4},{16,24},{20,28},{24,16},{28,20},{1,9},{5... | collective-permute-start | bytes 161288 | tf_op jit(solution)/shard_map/ppermute | solution.py:60
  28.4 11.5 %collective-permute-start.6 = (bf16[32,840]{1,0:T(8,128)(2,1)S(1)}, bf16[32,840]{1,0:T(8,128)(2,1)S(1)}, u32[]{:S(2)}, u32[]{:S(2)}) collective-permute-start(bf16[32,840]{1,0:T(8,128)(2,1)S(1)} %pad_maximum_fusion.2), channel_id=1, source_target_pairs={{0,16},{4,20},{8,24},{12,28},{16,0},{20,4},{24,8},{28,12},{1,17},{... | collective-permute-start | bytes 161288 | tf_op jit(solution)/shard_map/ppermute | solution.py:60
  35.8 5.5 %copy-start.10 = (s32[4,64]{1,0:T(4,128)S(1)}, s32[4,64]{1,0:T(4,128)}, u32[]{:S(2)}) copy-start(s32[4,64]{1,0:T(4,128)} %param.13) | copy-start | bytes 3076
  41.2 9.8 %collective-permute-start.10 = (bf16[32,768]{1,0:T(8,128)(2,1)S(1)}, bf16[32,768]{1,0:T(8,128)(2,1)S(1)}, u32[]{:S(2)}, u32[]{:S(2)}) collective-permute-start(bf16[32,768]{1,0:T(8,128)(2,1)S(1)} %fusion.30), channel_id=1, source_target_pairs={{0,4},{4,0},{8,12},{12,8},{16,20},{20,16},{24,28},{28,24},{1,5},{5... | collective-permute-start | bytes 147464 | tf_op jit(solution)/shard_map/ppermute | solution.py:60
  42.1 8.9 %copy-start.5 = (bf16[64,768]{1,0:T(8,128)(2,1)S(1)}, bf16[64,768]{1,0:T(8,128)(2,1)}, u32[]{:S(2)}) copy-start(bf16[64,768]{1,0:T(8,128)(2,1)} %copy-done.4) | copy-start | bytes 294916
  51.0 2.0 %copy-start.11 = (f32[768]{0:T(1024)S(1)}, f32[768]{0:T(1024)}, u32[]{:S(2)}) copy-start(f32[768]{0:T(1024)} %param.16) | copy-start | bytes 9220
  53.0 7.7 %copy-start.9 = (f32[768]{0:T(1024)S(1)}, f32[768]{0:T(1024)}, u32[]{:S(2)}) copy-start(f32[768]{0:T(1024)} %param.19) | copy-start | bytes 9220

commit v20 on v19

--- a/solution.py
+++ b/solution.py
@@ -205,8 +205,18 @@
     flat_cells = cells.reshape(row_count * cols_dev, model_width)
     w_kv = w_qkv[:, model_width:]
 
-    tokens = broadcast_from(summary[0], "band", n_band, owner[0], cells)
-    row_parts = fan_out(tokens[1], "col", n_col)
+    key_sources = [own_group] + [own_group ^ step for step in range(1, n_col)]
+    key_groups = jnp.concatenate(
+        [jnp.full((cols_dev,), s, jnp.int32) for s in key_sources]
+    )
+    own_block = jnp.arange(n_col * cols_dev, dtype=jnp.int32) < cols_dev
+    allowed = (jnp.right_shift(schema[:, :, None], key_groups[None, None, :]) & 1 == 1) | own_block[
+        None, None, :
+    ]
+    allowed = allowed.astype(jnp.float32)
+    tokens = broadcast_from(summary[0], "band", n_band, owner[0], (cells, allowed))
+    held_cells, allowed = tokens[1]
+    row_parts = fan_out(held_cells, "col", n_col)
     tokens = tokens[0]
 
     qkv_cells = project(flat_cells, w_qkv).reshape(row_count, cols_dev, 3 * model_width)
@@ -249,14 +259,7 @@
     summary_att = join_halves(summary_att, "band", n_band)
 
     sources = [own_group] + [s for s, _ in row_parts]
-    key_groups = jnp.concatenate(
-        [jnp.full((cols_dev,), s, jnp.int32) for s in sources]
-    )
-    own_block = jnp.arange(width_now, dtype=jnp.int32) < cols_dev
-    allowed = (jnp.right_shift(schema[:, :, None], key_groups[None, None, :]) & 1 == 1) | own_block[
-        None, None, :
-    ]
-    attended = row_attention(qkv_cells, row_kv, summary_kv, allowed.astype(jnp.float32))
+    attended = row_attention(qkv_cells, row_kv, summary_kv, allowed)
     attended = attended.reshape(row_count * cols_dev, model_width)
 
     all_in = jnp.concatenate([flat_cells, tokens], axis=0)

time: 62.6 us -> 61.1 us (0.976)
  waiting for transfers between devices: 11.9 us -> 6.45 us
  matrix products: 20.6 us -> 23.4 us
  other arithmetic: 4.29 us -> 5.9 us
    dot_general x4, matrix products: 8.28 us -> 11.1 us  [project(): jnp.dot(values, weight, preferred_element_type=jnp.float32)]
    ppermute x8, waiting for transfers between devices: 8.19 us -> 5.4 us  [partner(): return lax.ppermute(value, axis, [(i, i ^ step) for i in range(count)])]
    ppermute x3, waiting for transfers between devices: 3.75 us -> 1.04 us  [fan_out(): got.append((source, lax.ppermute(value, axis, pairs)))]
    select_n x3, other arithmetic: 0.04 us -> 0.98 us  [broadcast_from(): value = jnp.where(here // step == source // step, value, got)]
    convert_element_type x1, other arithmetic: 0.85 us -> 1.51 us  [local(): allowed = allowed.astype(jnp.float32)]
  transfers between devices with their start and end apart: 11 -> 11, of which waited for: 6 -> 5; matrix products, arithmetic and copies ran while one was open for 22% -> 29% of each run, Pallas kernels for 14% -> 15%
where the time goes in v20:
time: 61.1 us; the launch traced here: 60.8 us
  matrix products  23.4 us (38%)
  starting transfers between devices  12.8 us (21%)
  Pallas kernels  8.86 us (15%)
  waiting for transfers between devices  6.45 us (11%)
  other arithmetic  5.9 us (10%)
  between operations  1.72 us (3%)
  local copies, waits for them, and re-layouts  1.63 us (3%)
    dot_general x4, matrix products, project(): jnp.dot(values, weight, preferred_element_type=jnp.float32)  11.1 us
    ppermute x8, starting transfers between devices, partner(): return lax.ppermute(value, axis, [(i, i ^ step) for i in range(count)])  9.3 us
    pallas_call x1, Pallas kernels, row_attention(): pl.pallas_call(kern, grid=(rows,), in_specs=[pl.BlockSpec((1, nq, width),...  8.86 us
    dot_general x1, matrix products, finish(): outer_out = jnp.dot(inner_act, w_down, preferred_element_type=jnp.float32)  7.43 us
    ppermute x8, waiting for transfers between devices, partner(): return lax.ppermute(value, axis, [(i, i ^ step) for i in range(count)])  5.4 us
    ppermute x3, starting transfers between devices, fan_out(): got.append((source, lax.ppermute(value, axis, pairs)))  3.49 us
    dot_general x10, matrix products, head_spread(): jnp.dot(flat, head_matrix(), precision=lax.Precision.HIGHEST, preferred_e...  2.4 us
    dot_general x1, matrix products, finish(): mixed_out = jnp.dot(attended, w_out, preferred_element_type=jnp.float32)  1.65 us
  transfers between devices with their start and end apart: 11, of which 5 were waited for; matrix products, arithmetic and copies ran while one was open for 29% of the time, Pallas kernels for 15%

profile of v20, /device:TPU:0, one launch (start us, length us, event | category | flops | bytes accessed | tf_op | source)
XLA Modules:
  0.0 60.8 jit_solution(18060615914099105299)
XLA Ops:
  0.6 0.0 copy-start
  0.6 0.5 collective-permute-start
  1.2 0.1 pad_add_fusion
  1.3 1.5 %fusion.42.allow_ref = f32[4,64,256]{2,1,0:T(8,128)} fusion(s32[256]{0:T(256)S(1)} %pad_add_fusion, s32[4,64]{1,0:T(4,128)} %param.13, pred[256]{0:T(512)(128)(4,1)S(1)} %iota_compare_fusion.15), kind=kLoop, calls=%fused_computation.51 | loop fusion | flops 327680 | bytes 264448 | tf_op jit(solution)/shard_map/convert_element_type | solution.py:216
  3.4 0.0 copy-start.3
  3.5 1.0 %broadcast_select_fusion = bf16[64,768]{1,0:T(8,128)(2,1)S(1)} fusion(bf16[64,768]{1,0:T(8,128)(2,1)S(1)} %collective-permute-done, pred[]{:T(512)S(6)} %eq.88, bf16[1,64,768]{2,1,0:T(8,128)(2,1)} %param.11), kind=kLoop, calls=%fused_computation.58 | loop fusion | flops 49152 | bytes 294913 | tf_op jit(solution)/shard_map/jit(_where)/select_n | solution.py:70
  4.4 2.8 %collective-permute-start.1 = (bf16[64,768]{1,0:T(8,128)(2,1)S(1)}, bf16[64,768]{1,0:T(8,128)(2,1)S(1)}, u32[]{:S(2)}, u32[]{:S(2)}) collective-permute-start(bf16[64,768]{1,0:T(8,128)(2,1)S(1)} %broadcast_select_fusion), channel_id=1, source_target_pairs={{0,8},{4,12},{8,0},{12,4},{16,24},{20,28},{24,16},{28,20},{1,9},{5... | collective-permute-start | bytes 294920 | tf_op jit(solution)/shard_map/ppermute | solution.py:60
  7.2 3.2 %convolution_convert_fusion = bf16[256,2304]{1,0:T(8,128)(2,1)S(1)} fusion(bf16[256,768]{1,0:T(8,128)(2,1)} %bitcast.37, bf16[768,2304]{1,0:T(8,128)(2,1)} %param.14), kind=kOutput, calls=%fused_computation.9 | convolution fusion | flops 906559488 | bytes 5111808 | tf_op jit(solution)/shard_map/dot_general | solution.py:35
  10.6 2.8 %collective-permute-start.2 = (bf16[64,768]{1,0:T(8,128)(2,1)S(1)}, bf16[64,768]{1,0:T(8,128)(2,1)S(1)}, u32[]{:S(2)}, u32[]{:S(2)}) collective-permute-start(bf16[64,768]{1,0:T(8,128)(2,1)S(1)} %broadcast_select_fusion.1), channel_id=1, source_target_pairs={{0,16},{4,20},{8,24},{12,28},{16,0},{20,4},{24,8},{28,12},{1,17},{... | collective-permute-start | bytes 294920 | tf_op jit(solution)/shard_map/ppermute | solution.py:60
  13.4 1.5 %collective-permute-start.7 = (bf16[4,64,768]{2,1,0:T(8,128)(2,1)S(1)}, bf16[4,64,768]{2,1,0:T(8,128)(2,1)}, u32[]{:S(2)}, u32[]{:S(2)}) collective-permute-start(bf16[4,64,768]{2,1,0:T(8,128)(2,1)S(1)} %copy-done.3), channel_id=1, source_target_pairs={{0,1},{1,0},{2,3},{3,2},{4,5},{5,4},{6,7},{7,6},{8,9},{9,8},{10,11... | collective-permute-start | bytes 1179656 | tf_op jit(solution)/shard_map/ppermute | solution.py:145
  14.9 1.5 %collective-permute-start.8 = (bf16[4,64,768]{2,1,0:T(8,128)(2,1)S(1)}, bf16[4,64,768]{2,1,0:T(8,128)(2,1)}, u32[]{:S(2)}, u32[]{:S(2)}) collective-permute-start(bf16[4,64,768]{2,1,0:T(8,128)(2,1)S(1)} %copy-done.3), channel_id=1, source_target_pairs={{0,2},{1,3},{2,0},{3,1},{4,6},{5,7},{6,4},{7,5},{8,10},{9,11},{10,... | collective-permute-start | bytes 1179656 | tf_op jit(solution)/shard_map/ppermute | solution.py:145
  16.4 0.5 collective-permute-start.9
  16.9 1.5 %collective-permute-done.2 = bf16[64,768]{1,0:T(8,128)(2,1)S(1)} collective-permute-done((bf16[64,768]{1,0:T(8,128)(2,1)S(1)}, bf16[64,768]{1,0:T(8,128)(2,1)S(1)}, u32[]{:S(2)}, u32[]{:S(2)}) %collective-permute-start.2) | collective-permute-done | bytes 98336 | tf_op jit(solution)/shard_map/ppermute | solution.py:60
  18.4 0.0 copy-start.4
  18.4 1.6 %fusion.25 = f32[64,768]{1,0:T(8,128)S(1)} fusion(bf16[64,768]{1,0:T(8,128)(2,1)S(1)} %broadcast_select_fusion.2, bf16[768,2304]{1,0:T(8,128)(2,1)} %param.14), kind=kOutput, calls=%fused_computation.26 | convolution fusion | flops 75595776 | bytes 1474560 | tf_op jit(solution)/shard_map/dot_general | solution.py:35
  20.1 2.2 %convolution_convert_fusion.2.sk_ref.sv_ref = bf16[64,1536]{1,0:T(8,128)(2,1)S(1)} fusion(bf16[64,768]{1,0:T(8,128)(2,1)S(1)} %broadcast_select_fusion.2, bf16[768,2304]{1,0:T(8,128)(2,1)} %param.14), kind=kOutput, calls=%fused_computation.11 | convolution fusion | flops 151093248 | bytes 2654208 | tf_op jit(solution)/shard_map/dot_general | solution.py:35
  22.3 0.6 %fusion.93 = (f32[64,12]{0,1:T(8,128)S(1)}, f32[4,64,12]{1,2,0:T(8,128)S(1)}) fusion(s32[768]{0:T(1024)S(1)} %add_select_fusion, bf16[4,64,2304]{2,1,0:T(8,128)(2,1)S(1)} %bitcast.32, f32[64,768]{1,0:T(8,128)S(1)} %fusion.25), kind=kOutput, calls=%fused_computation.160 | convolution fusion | flops 28719360 | bytes 609280 | tf_op jit(solution)/shard_map/dot_general | solution.py:46
  22.9 0.1 slice_maximum_fusion.3
  23.0 0.1 copy.18
  23.1 0.1 copy.19
  23.2 0.1 collective-permute-start.4
  23.2 0.3 fusion.19
  23.5 0.0 copy-start.6
  23.6 0.6 collective-permute-start.3
  24.1 0.3 collective-permute-done.4
  24.4 0.1 fusion.75
  24.5 0.3 fusion.50
  24.8 0.1 fusion.91
  24.8 0.1 fusion.76
  24.9 0.1 subtract_convert_fusion.1
  25.0 0.1 collective-permute-done.3
  25.1 0.2 add_convert_fusion.1
  25.3 0.1 pad_maximum_fusion.1
  25.4 0.4 collective-permute-start.5
  25.9 0.2 convolution_multiply_fusion.4
  26.1 3.5 %collective-permute-done.5 = bf16[32,840]{1,0:T(8,128)(2,1)S(1)} collective-permute-done((bf16[32,840]{1,0:T(8,128)(2,1)S(1)}, bf16[32,840]{1,0:T(8,128)(2,1)S(1)}, u32[]{:S(2)}, u32[]{:S(2)}) %collective-permute-start.5) | collective-permute-done | bytes 53792 | tf_op jit(solution)/shard_map/ppermute | solution.py:60
  29.6 0.1 broadcast_select_fusion.6
  29.7 0.1 fusion.74
  29.8 0.3 fusion.47
  30.1 0.1 fusion.90
  30.1 0.1 fusion.77
  30.2 0.1 subtract_convert_fusion
  30.3 0.3 add_convert_fusion
  30.6 0.1 pad_maximum_fusion.2
  30.7 2.1 %collective-permute-start.6 = (bf16[32,840]{1,0:T(8,128)(2,1)S(1)}, bf16[32,840]{1,0:T(8,128)(2,1)S(1)}, u32[]{:S(2)}, u32[]{:S(2)}) collective-permute-start(bf16[32,840]{1,0:T(8,128)(2,1)S(1)} %pad_maximum_fusion.2), channel_id=1, source_target_pairs={{0,16},{4,20},{8,24},{12,28},{16,0},{20,4},{24,8},{28,12},{1,17},{... | collective-permute-start | bytes 161288 | tf_op jit(solution)/shard_map/ppermute | solution.py:60
  32.7 1.0 %collective-permute-done.8 = bf16[4,64,768]{2,1,0:T(8,128)(2,1)} collective-permute-done((bf16[4,64,768]{2,1,0:T(8,128)(2,1)S(1)}, bf16[4,64,768]{2,1,0:T(8,128)(2,1)}, u32[]{:S(2)}, u32[]{:S(2)}) %collective-permute-start.8) | collective-permute-done | bytes 393248 | tf_op jit(solution)/shard_map/ppermute | solution.py:145
  33.8 1.3 %pad_maximum_fusion = bf16[4,256,768]{2,1,0:T(8,128)(2,1)S(1)} fusion(bf16[4,64,768]{2,1,0:T(8,128)(2,1)} %collective-permute-done.9, bf16[4,64,768]{2,1,0:T(8,128)(2,1)} %collective-permute-done.8, bf16[4,64,768]{2,1,0:T(8,128)(2,1)} %collective-permute-done.7, bf16[4,64,768]{2,1,0:T(8,128)(2,1)S(1)} %copy-done.3), kind=kLoop, calls=%fused_computation.19 | loop fusion | flops 6291456 | bytes 3145728 | tf_op jit(solution)/shard_map/concatenate | solution.py:240
  35.1 4.0 %convolution_convert_fusion.1 = bf16[1024,1536]{1,0:T(8,128)(2,1)} fusion(bf16[1024,768]{1,0:T(8,128)(2,1)S(1)} %bitcast.35, bf16[768,2304]{1,0:T(8,128)(2,1)S(1)} %copy-done.6), kind=kOutput, calls=%fused_computation.10 | convolution fusion | flops 2417491968 | bytes 7077888 | tf_op jit(solution)/shard_map/dot_general | solution.py:35
  39.2 0.1 broadcast_select_fusion.4
  39.3 0.1 fusion.79
  39.4 0.3 convolution_multiply_fusion.3
  39.6 0.3 fusion.29
  39.9 0.1 fusion.46
  40.0 0.2 fusion.28
  40.2 0.3 fusion.30
  40.5 0.1 collective-permute-start.10
  40.6 8.9 %shard_map.113 = bf16[4,64,768]{2,1,0:T(8,128)(2,1)} custom-call(bf16[4,64,2304]{2,1,0:T(8,128)(2,1)} %bitcast.34, bf16[4,256,1536]{2,1,0:T(8,128)(2,1)} %bitcast.30, bf16[4,256,1536]{2,1,0:T(8,128)(2,1)} %bitcast.31, bf16[64,1536]{1,0:T(8,128)(2,1)} %copy-done.2, bf16[64,1536]{1,0:T(8,128)(2,1)} %copy-done.2, f32[4,64,256]{2,1,0:T(8,128)} %fusion.42.allow_ref), custom_call_target="tpu_custom_call" | custom-call | tf_op jit(solution)/shard_map/pallas_call | solution.py:184
  49.5 1.6 %fusion.94 = (f32[320]{0:T(512)S(1)}, f32[320,768]{1,0:T(8,128)S(1)}) fusion(bf16[768,768]{1,0:T(8,128)(2,1)S(1)} %copy-done, bf16[64,768]{1,0:T(8,128)(2,1)S(1)} %maximum_select_fusion, bf16[256,768]{1,0:T(8,128)(2,1)} %bitcast.36, bf16[64,768]{1,0:T(8,128)(2,1)S(1)} %copy-done.5, bf16[256,768]{1,0:T(8,128)(2,1)S(1)} %bitcast.38), kind=kOutput, calls=%fused_computation.161 | convolution fusion | flops 379944640 | bytes 3147008 | tf_op jit(solution)/shard_map/dot_general | solution.py:25
  51.1 0.3 multiply_reduce_fusion.1
  51.4 7.4 %fusion.95 = (f32[320]{0:T(512)S(1)}, f32[320,768]{1,0:T(8,128)S(1)}) fusion(bf16[3072,768]{1,0:T(8,128)(2,1)} %param.18, bf16[768,3072]{1,0:T(8,128)(2,1)} %param.17, f32[320,768]{1,0:T(8,128)S(1)} %get-tuple-element.32, f32[768]{0:T(1024)S(1)} %copy-done.8, f32[320]{0:T(512)S(1)} %add_rsqrt_fusion.1, f32[320]{0:T(512)S(1)} %broadcast_multiply_fusion.1), kind=kOutput, calls=%fused_computation.162 | convolution fusion | flops 3031449344 | bytes 11410176 | tf_op jit(solution)/shard_map/dot_general | solution.py:30
  58.9 0.3 multiply_reduce_fusion
  59.2 0.2 multiply_convert_fusion
  59.4 0.8 %slice.220 = bf16[256,768]{1,0:T(8,128)(2,1)} slice(bf16[320,768]{1,0:T(8,128)(2,1)S(1)} %multiply_convert_fusion), slice={[0:256], [0:768]} | slice | bytes 786432 | tf_op jit(solution)/shard_map/slice | solution.py:268
  60.1 0.6 %slice.221 = bf16[64,768]{1,0:T(8,128)(2,1)} slice(bf16[320,768]{1,0:T(8,128)(2,1)S(1)} %multiply_convert_fusion), slice={[256:320], [0:768]} | slice | bytes 196608 | tf_op jit(solution)/shard_map/slice | solution.py:269
  (41 shorter events, 0.2 us)
Async XLA Ops:
  0.6 48.8 %copy-start = (bf16[768,768]{1,0:T(8,128)(2,1)S(1)}, bf16[768,768]{1,0:T(8,128)(2,1)}, u32[]{:S(2)}) copy-start(bf16[768,768]{1,0:T(8,128)(2,1)} %param.15) | copy-start | bytes 3538948
  0.6 2.8 %collective-permute-start = (bf16[64,768]{1,0:T(8,128)(2,1)}, bf16[64,768]{1,0:T(8,128)(2,1)S(1)}, u32[]{:S(2)}, u32[]{:S(2)}) collective-permute-start(bf16[64,768]{1,0:T(8,128)(2,1)} %bitcast.40), channel_id=1, source_target_pairs={{0,4},{4,0},{8,12},{12,8},{16,20},{20,16},{24,28},{28,24},{1,5},{5... | collective-permute-start | bytes 294920 | tf_op jit(solution)/shard_map/ppermute | solution.py:60
  3.4 9.9 %copy-start.3 = (bf16[4,64,768]{2,1,0:T(8,128)(2,1)S(1)}, bf16[4,64,768]{2,1,0:T(8,128)(2,1)}, u32[]{:S(2)}) copy-start(bf16[4,64,768]{2,1,0:T(8,128)(2,1)} %param.10) | copy-start | bytes 1179652
  4.4 6.1 %collective-permute-start.1 = (bf16[64,768]{1,0:T(8,128)(2,1)S(1)}, bf16[64,768]{1,0:T(8,128)(2,1)S(1)}, u32[]{:S(2)}, u32[]{:S(2)}) collective-permute-start(bf16[64,768]{1,0:T(8,128)(2,1)S(1)} %broadcast_select_fusion), channel_id=1, source_target_pairs={{0,8},{4,12},{8,0},{12,4},{16,24},{20,28},{24,16},{28,20},{1,9},{5... | collective-permute-start | bytes 294920 | tf_op jit(solution)/shard_map/ppermute | solution.py:60
  10.4 13.1 %copy-start.1 = (bf16[256,2304]{1,0:T(8,128)(2,1)}, bf16[256,2304]{1,0:T(8,128)(2,1)S(1)}, u32[]{:S(2)}) copy-start(bf16[256,2304]{1,0:T(8,128)(2,1)S(1)} %convolution_convert_fusion) | copy-start | bytes 3538948
  10.6 7.8 %collective-permute-start.2 = (bf16[64,768]{1,0:T(8,128)(2,1)S(1)}, bf16[64,768]{1,0:T(8,128)(2,1)S(1)}, u32[]{:S(2)}, u32[]{:S(2)}) collective-permute-start(bf16[64,768]{1,0:T(8,128)(2,1)S(1)} %broadcast_select_fusion.1), channel_id=1, source_target_pairs={{0,16},{4,20},{8,24},{12,28},{16,0},{20,4},{24,8},{28,12},{1,17},{... | collective-permute-start | bytes 294920 | tf_op jit(solution)/shard_map/ppermute | solution.py:60
  13.4 19.4 %collective-permute-start.7 = (bf16[4,64,768]{2,1,0:T(8,128)(2,1)S(1)}, bf16[4,64,768]{2,1,0:T(8,128)(2,1)}, u32[]{:S(2)}, u32[]{:S(2)}) collective-permute-start(bf16[4,64,768]{2,1,0:T(8,128)(2,1)S(1)} %copy-done.3), channel_id=1, source_target_pairs={{0,1},{1,0},{2,3},{3,2},{4,5},{5,4},{6,7},{7,6},{8,9},{9,8},{10,11... | collective-permute-start | bytes 1179656 | tf_op jit(solution)/shard_map/ppermute | solution.py:145
  14.9 18.9 %collective-permute-start.8 = (bf16[4,64,768]{2,1,0:T(8,128)(2,1)S(1)}, bf16[4,64,768]{2,1,0:T(8,128)(2,1)}, u32[]{:S(2)}, u32[]{:S(2)}) collective-permute-start(bf16[4,64,768]{2,1,0:T(8,128)(2,1)S(1)} %copy-done.3), channel_id=1, source_target_pairs={{0,2},{1,3},{2,0},{3,1},{4,6},{5,7},{6,4},{7,5},{8,10},{9,11},{10,... | collective-permute-start | bytes 1179656 | tf_op jit(solution)/shard_map/ppermute | solution.py:145
  16.4 17.4 %collective-permute-start.9 = (bf16[4,64,768]{2,1,0:T(8,128)(2,1)S(1)}, bf16[4,64,768]{2,1,0:T(8,128)(2,1)}, u32[]{:S(2)}, u32[]{:S(2)}) collective-permute-start(bf16[4,64,768]{2,1,0:T(8,128)(2,1)S(1)} %copy-done.3), channel_id=1, source_target_pairs={{0,3},{1,2},{2,1},{3,0},{4,7},{5,6},{6,5},{7,4},{8,11},{9,10},{10,... | collective-permute-start | bytes 1179656 | tf_op jit(solution)/shard_map/ppermute | solution.py:145
  18.4 6.3 %copy-start.4 = (bf16[64,768]{1,0:T(8,128)(2,1)}, bf16[64,768]{1,0:T(8,128)(2,1)S(1)}, u32[]{:S(2)}) copy-start(bf16[64,768]{1,0:T(8,128)(2,1)S(1)} %broadcast_select_fusion.2) | copy-start | bytes 294916
  22.3 17.7 %copy-start.2 = (bf16[64,1536]{1,0:T(8,128)(2,1)}, bf16[64,1536]{1,0:T(8,128)(2,1)S(1)}, u32[]{:S(2)}) copy-start(bf16[64,1536]{1,0:T(8,128)(2,1)S(1)} %convolution_convert_fusion.2.sk_ref.sv_ref) | copy-start | bytes 589828
  23.2 1.2 %collective-permute-start.4 = (f32[32,24]{1,0:T(8,128)S(1)}, f32[32,24]{1,0:T(8,128)S(1)}, u32[]{:S(2)}, u32[]{:S(2)}) collective-permute-start(f32[32,24]{1,0:T(8,128)S(1)} %broadcast_select_fusion.9), channel_id=1, source_target_pairs={{0,4},{4,0},{8,12},{12,8},{16,20},{20,16},{24,28},{28,24},{1,5},{5... | collective-permute-start | bytes 9224 | tf_op jit(solution)/shard_map/ppermute | solution.py:60
  23.5 11.6 %copy-start.6 = (bf16[768,2304]{1,0:T(8,128)(2,1)S(1)}, bf16[768,2304]{1,0:T(8,128)(2,1)}, u32[]{:S(2)}) copy-start(bf16[768,2304]{1,0:T(8,128)(2,1)} %param.14) | copy-start | bytes 10616836
  23.6 1.5 %collective-permute-start.3 = (f32[32,768]{1,0:T(8,128)S(1)}, f32[32,768]{1,0:T(8,128)S(1)}, u32[]{:S(2)}, u32[]{:S(2)}) collective-permute-start(f32[32,768]{1,0:T(8,128)S(1)} %slice_select_fusion), channel_id=1, source_target_pairs={{0,4},{4,0},{8,12},{12,8},{16,20},{20,16},{24,28},{28,24},{1,5},{5... | collective-permute-start | bytes 294920 | tf_op jit(solution)/shard_map/ppermute | solution.py:60
  25.4 4.2 %collective-permute-start.5 = (bf16[32,840]{1,0:T(8,128)(2,1)S(1)}, bf16[32,840]{1,0:T(8,128)(2,1)S(1)}, u32[]{:S(2)}, u32[]{:S(2)}) collective-permute-start(bf16[32,840]{1,0:T(8,128)(2,1)S(1)} %pad_maximum_fusion.1), channel_id=1, source_target_pairs={{0,8},{4,12},{8,0},{12,4},{16,24},{20,28},{24,16},{28,20},{1,9},{5... | collective-permute-start | bytes 161288 | tf_op jit(solution)/shard_map/ppermute | solution.py:60
  30.7 8.5 %collective-permute-start.6 = (bf16[32,840]{1,0:T(8,128)(2,1)S(1)}, bf16[32,840]{1,0:T(8,128)(2,1)S(1)}, u32[]{:S(2)}, u32[]{:S(2)}) collective-permute-start(bf16[32,840]{1,0:T(8,128)(2,1)S(1)} %pad_maximum_fusion.2), channel_id=1, source_target_pairs={{0,16},{4,20},{8,24},{12,28},{16,0},{20,4},{24,8},{28,12},{1,17},{... | collective-permute-start | bytes 161288 | tf_op jit(solution)/shard_map/ppermute | solution.py:60
  40.5 9.0 %copy-start.5 = (bf16[64,768]{1,0:T(8,128)(2,1)S(1)}, bf16[64,768]{1,0:T(8,128)(2,1)}, u32[]{:S(2)}) copy-start(bf16[64,768]{1,0:T(8,128)(2,1)} %copy-done.4) | copy-start | bytes 294916
  40.5 8.9 %collective-permute-start.10 = (bf16[32,768]{1,0:T(8,128)(2,1)S(1)}, bf16[32,768]{1,0:T(8,128)(2,1)S(1)}, u32[]{:S(2)}, u32[]{:S(2)}) collective-permute-start(bf16[32,768]{1,0:T(8,128)(2,1)S(1)} %fusion.30), channel_id=1, source_target_pairs={{0,4},{4,0},{8,12},{12,8},{16,20},{20,16},{24,28},{28,24},{1,5},{5... | collective-permute-start | bytes 147464 | tf_op jit(solution)/shard_map/ppermute | solution.py:60
  49.4 2.0 %copy-start.8 = (f32[768]{0:T(1024)S(1)}, f32[768]{0:T(1024)}, u32[]{:S(2)}) copy-start(f32[768]{0:T(1024)} %param.16) | copy-start | bytes 9220
  51.4 7.7 %copy-start.7 = (f32[768]{0:T(1024)S(1)}, f32[768]{0:T(1024)}, u32[]{:S(2)}) copy-start(f32[768]{0:T(1024)} %param.19) | copy-start | bytes 9220

commit v21 on v20

--- a/solution.py
+++ b/solution.py
@@ -214,9 +214,9 @@
         None, None, :
     ]
     allowed = allowed.astype(jnp.float32)
-    tokens = broadcast_from(summary[0], "band", n_band, owner[0], (cells, allowed))
-    held_cells, allowed = tokens[1]
-    row_parts = fan_out(held_cells, "col", n_col)
+    row_parts = fan_out(cells, "col", n_col)
+    tokens = broadcast_from(summary[0], "band", n_band, owner[0], allowed)
+    allowed = tokens[1]
     tokens = tokens[0]
 
     qkv_cells = project(flat_cells, w_qkv).reshape(row_count, cols_dev, 3 * model_width)

time: 61.1 us -> 62.5 us (1.023)
  waiting for transfers between devices: 6.45 us -> 7.42 us
    ppermute x8, waiting for transfers between devices: 5.4 us -> 7.41 us  [partner(): return lax.ppermute(value, axis, [(i, i ^ step) for i in range(count)])]
    ppermute x3, starting transfers between devices: 3.49 us -> 4.55 us  [fan_out(): got.append((source, lax.ppermute(value, axis, pairs)))]
    ppermute x3, waiting for transfers between devices: 1.04 us -> 0.01 us  [fan_out(): got.append((source, lax.ppermute(value, axis, pairs)))]
    ppermute x8, starting transfers between devices: 9.3 us -> 8.6 us  [partner(): return lax.ppermute(value, axis, [(i, i ^ step) for i in range(count)])]
  transfers between devices with their start and end apart: 11 -> 11, of which waited for: 5 -> 4; matrix products, arithmetic and copies ran while one was open for 29% -> 28% of each run, Pallas kernels for 15% -> 14%
where the time goes in v21:
time: 62.5 us; the launch traced here: 62.1 us
  matrix products  23.4 us (37%)
  starting transfers between devices  13.1 us (21%)
  Pallas kernels  8.86 us (14%)
  waiting for transfers between devices  7.42 us (12%)
  other arithmetic  5.86 us (9%)
  between operations  1.73 us (3%)
  local copies, waits for them, and re-layouts  1.63 us (3%)
    dot_general x4, matrix products, project(): jnp.dot(values, weight, preferred_element_type=jnp.float32)  11.1 us
    pallas_call x1, Pallas kernels, row_attention(): pl.pallas_call(kern, grid=(rows,), in_specs=[pl.BlockSpec((1, nq, width),...  8.86 us
    ppermute x8, starting transfers between devices, partner(): return lax.ppermute(value, axis, [(i, i ^ step) for i in range(count)])  8.6 us
    dot_general x1, matrix products, finish(): outer_out = jnp.dot(inner_act, w_down, preferred_element_type=jnp.float32)  7.43 us
    ppermute x8, waiting for transfers between devices, partner(): return lax.ppermute(value, axis, [(i, i ^ step) for i in range(count)])  7.41 us
    ppermute x3, starting transfers between devices, fan_out(): got.append((source, lax.ppermute(value, axis, pairs)))  4.55 us
    dot_general x10, matrix products, head_spread(): jnp.dot(flat, head_matrix(), precision=lax.Precision.HIGHEST, preferred_e...  2.39 us
    dot_general x1, matrix products, finish(): mixed_out = jnp.dot(attended, w_out, preferred_element_type=jnp.float32)  1.65 us
  transfers between devices with their start and end apart: 11, of which 4 were waited for; matrix products, arithmetic and copies ran while one was open for 28% of the time, Pallas kernels for 14%

profile of v21, /device:TPU:0, one launch (start us, length us, event | category | flops | bytes accessed | tf_op | source)
XLA Modules:
  0.0 62.1 jit_solution(6613145499364886296)
XLA Ops:
  0.6 0.0 copy-start
  0.6 3.0 %collective-permute-start.7 = (bf16[4,64,768]{2,1,0:T(8,128)(2,1)}, bf16[4,64,768]{2,1,0:T(8,128)(2,1)}, u32[]{:S(2)}, u32[]{:S(2)}) collective-permute-start(bf16[4,64,768]{2,1,0:T(8,128)(2,1)} %param.10), channel_id=1, source_target_pairs={{0,1},{1,0},{2,3},{3,2},{4,5},{5,4},{6,7},{7,6},{8,9},{9,8},{10,11... | collective-permute-start | bytes 1179656 | tf_op jit(solution)/shard_map/ppermute | solution.py:145
  3.6 1.5 %collective-permute-start.8 = (bf16[4,64,768]{2,1,0:T(8,128)(2,1)}, bf16[4,64,768]{2,1,0:T(8,128)(2,1)}, u32[]{:S(2)}, u32[]{:S(2)}) collective-permute-start(bf16[4,64,768]{2,1,0:T(8,128)(2,1)} %param.10), channel_id=1, source_target_pairs={{0,2},{1,3},{2,0},{3,1},{4,6},{5,7},{6,4},{7,5},{8,10},{9,11},{10,... | collective-permute-start | bytes 1179656 | tf_op jit(solution)/shard_map/ppermute | solution.py:145
  5.2 0.0 collective-permute-start.9
  5.2 0.1 pad_add_fusion
  5.3 1.5 %fusion.42.allow_ref = f32[4,64,256]{2,1,0:T(8,128)} fusion(s32[256]{0:T(256)S(1)} %pad_add_fusion, s32[4,64]{1,0:T(4,128)} %param.13, pred[256]{0:T(512)(128)(4,1)S(1)} %iota_compare_fusion.15), kind=kLoop, calls=%fused_computation.51 | loop fusion | flops 327680 | bytes 264448 | tf_op jit(solution)/shard_map/convert_element_type | solution.py:216
  7.5 0.9 %broadcast_select_fusion = bf16[64,768]{1,0:T(8,128)(2,1)S(1)} fusion(bf16[64,768]{1,0:T(8,128)(2,1)S(1)} %collective-permute-done, pred[]{:T(512)S(6)} %eq.88, bf16[1,64,768]{2,1,0:T(8,128)(2,1)} %param.11), kind=kLoop, calls=%fused_computation.58 | loop fusion | flops 49152 | bytes 294913 | tf_op jit(solution)/shard_map/jit(_where)/select_n | solution.py:70
  8.4 2.1 %collective-permute-start.1 = (bf16[64,768]{1,0:T(8,128)(2,1)S(1)}, bf16[64,768]{1,0:T(8,128)(2,1)S(1)}, u32[]{:S(2)}, u32[]{:S(2)}) collective-permute-start(bf16[64,768]{1,0:T(8,128)(2,1)S(1)} %broadcast_select_fusion), channel_id=1, source_target_pairs={{0,8},{4,12},{8,0},{12,4},{16,24},{20,28},{24,16},{28,20},{1,9},{5... | collective-permute-start | bytes 294920 | tf_op jit(solution)/shard_map/ppermute | solution.py:60
  10.5 3.2 %convolution_convert_fusion = bf16[256,2304]{1,0:T(8,128)(2,1)S(1)} fusion(bf16[256,768]{1,0:T(8,128)(2,1)} %bitcast.37, bf16[768,2304]{1,0:T(8,128)(2,1)} %param.14), kind=kOutput, calls=%fused_computation.9 | convolution fusion | flops 906559488 | bytes 5111808 | tf_op jit(solution)/shard_map/dot_general | solution.py:35
  13.8 0.2 collective-permute-done.1
  14.0 2.8 %collective-permute-start.2 = (bf16[64,768]{1,0:T(8,128)(2,1)S(1)}, bf16[64,768]{1,0:T(8,128)(2,1)S(1)}, u32[]{:S(2)}, u32[]{:S(2)}) collective-permute-start(bf16[64,768]{1,0:T(8,128)(2,1)S(1)} %broadcast_select_fusion.1), channel_id=1, source_target_pairs={{0,16},{4,20},{8,24},{12,28},{16,0},{20,4},{24,8},{28,12},{1,17},{... | collective-permute-start | bytes 294920 | tf_op jit(solution)/shard_map/ppermute | solution.py:60
  16.8 5.0 %collective-permute-done.2 = bf16[64,768]{1,0:T(8,128)(2,1)S(1)} collective-permute-done((bf16[64,768]{1,0:T(8,128)(2,1)S(1)}, bf16[64,768]{1,0:T(8,128)(2,1)S(1)}, u32[]{:S(2)}, u32[]{:S(2)}) %collective-permute-start.2) | collective-permute-done | bytes 98336 | tf_op jit(solution)/shard_map/ppermute | solution.py:60
  21.8 0.0 copy-start.4
  21.9 1.6 %fusion.25 = f32[64,768]{1,0:T(8,128)S(1)} fusion(bf16[64,768]{1,0:T(8,128)(2,1)S(1)} %broadcast_select_fusion.2, bf16[768,2304]{1,0:T(8,128)(2,1)} %param.14), kind=kOutput, calls=%fused_computation.26 | convolution fusion | flops 75595776 | bytes 1474560 | tf_op jit(solution)/shard_map/dot_general | solution.py:35
  23.5 0.0 copy-start.3
  23.5 2.3 %convolution_convert_fusion.2.sk_ref.sv_ref = bf16[64,1536]{1,0:T(8,128)(2,1)S(1)} fusion(bf16[64,768]{1,0:T(8,128)(2,1)S(1)} %broadcast_select_fusion.2, bf16[768,2304]{1,0:T(8,128)(2,1)} %param.14), kind=kOutput, calls=%fused_computation.11 | convolution fusion | flops 151093248 | bytes 2654208 | tf_op jit(solution)/shard_map/dot_general | solution.py:35
  25.8 0.6 %fusion.93 = (f32[64,12]{0,1:T(8,128)S(1)}, f32[4,64,12]{1,2,0:T(8,128)S(1)}) fusion(s32[768]{0:T(1024)S(1)} %add_select_fusion, bf16[4,64,2304]{2,1,0:T(8,128)(2,1)S(1)} %bitcast.32, f32[64,768]{1,0:T(8,128)S(1)} %fusion.25), kind=kOutput, calls=%fused_computation.160 | convolution fusion | flops 28719360 | bytes 609280 | tf_op jit(solution)/shard_map/dot_general | solution.py:46
  26.4 0.1 slice_maximum_fusion.3
  26.5 0.1 copy.18
  26.6 0.1 copy.19
  26.7 0.1 collective-permute-start.4
  26.7 0.3 fusion.19
  27.0 0.0 copy-start.6
  27.1 0.6 collective-permute-start.3
  27.6 0.2 convolution_multiply_fusion.4
  27.9 0.0 collective-permute-done.4
  27.9 0.1 fusion.75
  28.0 0.3 fusion.50
  28.2 0.1 fusion.91
  28.3 0.1 fusion.76
  28.4 0.1 subtract_convert_fusion.1
  28.5 0.1 collective-permute-done.3
  28.6 0.2 add_convert_fusion.1
  28.8 0.1 pad_maximum_fusion.1
  28.9 0.7 %collective-permute-start.5 = (bf16[32,840]{1,0:T(8,128)(2,1)S(1)}, bf16[32,840]{1,0:T(8,128)(2,1)S(1)}, u32[]{:S(2)}, u32[]{:S(2)}) collective-permute-start(bf16[32,840]{1,0:T(8,128)(2,1)S(1)} %pad_maximum_fusion.1), channel_id=1, source_target_pairs={{0,8},{4,12},{8,0},{12,4},{16,24},{20,28},{24,16},{28,20},{1,9},{5... | collective-permute-start | bytes 161288 | tf_op jit(solution)/shard_map/ppermute | solution.py:60
  29.6 1.3 %pad_maximum_fusion = bf16[4,256,768]{2,1,0:T(8,128)(2,1)S(1)} fusion(bf16[4,64,768]{2,1,0:T(8,128)(2,1)} %collective-permute-done.9, bf16[4,64,768]{2,1,0:T(8,128)(2,1)} %collective-permute-done.8, bf16[4,64,768]{2,1,0:T(8,128)(2,1)} %collective-permute-done.7, bf16[4,64,768]{2,1,0:T(8,128)(2,1)S(1)} %copy-done.3), kind=kLoop, calls=%fused_computation.19 | loop fusion | flops 6291456 | bytes 3145728 | tf_op jit(solution)/shard_map/concatenate | solution.py:240
  31.0 2.1 %collective-permute-done.5 = bf16[32,840]{1,0:T(8,128)(2,1)S(1)} collective-permute-done((bf16[32,840]{1,0:T(8,128)(2,1)S(1)}, bf16[32,840]{1,0:T(8,128)(2,1)S(1)}, u32[]{:S(2)}, u32[]{:S(2)}) %collective-permute-start.5) | collective-permute-done | bytes 53792 | tf_op jit(solution)/shard_map/ppermute | solution.py:60
  33.1 0.1 broadcast_select_fusion.6
  33.2 0.1 fusion.74
  33.3 0.3 fusion.47
  33.5 0.3 add_convert_fusion
  33.8 0.1 fusion.90
  33.9 0.1 fusion.77
  34.0 0.1 subtract_convert_fusion
  34.0 0.1 pad_maximum_fusion.2
  34.1 2.3 %collective-permute-start.6 = (bf16[32,840]{1,0:T(8,128)(2,1)S(1)}, bf16[32,840]{1,0:T(8,128)(2,1)S(1)}, u32[]{:S(2)}, u32[]{:S(2)}) collective-permute-start(bf16[32,840]{1,0:T(8,128)(2,1)S(1)} %pad_maximum_fusion.2), channel_id=1, source_target_pairs={{0,16},{4,20},{8,24},{12,28},{16,0},{20,4},{24,8},{28,12},{1,17},{... | collective-permute-start | bytes 161288 | tf_op jit(solution)/shard_map/ppermute | solution.py:60
  36.4 4.0 %convolution_convert_fusion.1 = bf16[1024,1536]{1,0:T(8,128)(2,1)} fusion(bf16[1024,768]{1,0:T(8,128)(2,1)S(1)} %bitcast.35, bf16[768,2304]{1,0:T(8,128)(2,1)S(1)} %copy-done.6), kind=kOutput, calls=%fused_computation.10 | convolution fusion | flops 2417491968 | bytes 7077888 | tf_op jit(solution)/shard_map/dot_general | solution.py:35
  40.5 0.1 broadcast_select_fusion.4
  40.6 0.1 fusion.79
  40.7 0.3 convolution_multiply_fusion.3
  40.9 0.2 fusion.29
  41.2 0.1 fusion.46
  41.3 0.2 fusion.28
  41.5 0.3 fusion.30
  41.8 0.0 copy-start.5
  41.8 0.1 collective-permute-start.10
  41.9 8.9 %shard_map.113 = bf16[4,64,768]{2,1,0:T(8,128)(2,1)} custom-call(bf16[4,64,2304]{2,1,0:T(8,128)(2,1)} %bitcast.34, bf16[4,256,1536]{2,1,0:T(8,128)(2,1)} %bitcast.30, bf16[4,256,1536]{2,1,0:T(8,128)(2,1)} %bitcast.31, bf16[64,1536]{1,0:T(8,128)(2,1)} %copy-done.2, bf16[64,1536]{1,0:T(8,128)(2,1)} %copy-done.2, f32[4,64,256]{2,1,0:T(8,128)} %fusion.42.allow_ref), custom_call_target="tpu_custom_call" | custom-call | tf_op jit(solution)/shard_map/pallas_call | solution.py:184
  50.8 1.6 %fusion.94 = (f32[320]{0:T(512)S(1)}, f32[320,768]{1,0:T(8,128)S(1)}) fusion(bf16[768,768]{1,0:T(8,128)(2,1)S(1)} %copy-done, bf16[64,768]{1,0:T(8,128)(2,1)S(1)} %maximum_select_fusion, bf16[256,768]{1,0:T(8,128)(2,1)} %bitcast.36, bf16[64,768]{1,0:T(8,128)(2,1)S(1)} %copy-done.5, bf16[256,768]{1,0:T(8,128)(2,1)S(1)} %bitcast.38), kind=kOutput, calls=%fused_computation.161 | convolution fusion | flops 379944640 | bytes 3147008 | tf_op jit(solution)/shard_map/dot_general | solution.py:25
  52.5 0.3 multiply_reduce_fusion.1
  52.8 7.4 %fusion.95 = (f32[320]{0:T(512)S(1)}, f32[320,768]{1,0:T(8,128)S(1)}) fusion(bf16[3072,768]{1,0:T(8,128)(2,1)} %param.18, bf16[768,3072]{1,0:T(8,128)(2,1)} %param.17, f32[320,768]{1,0:T(8,128)S(1)} %get-tuple-element.30, f32[768]{0:T(1024)S(1)} %copy-done.8, f32[320]{0:T(512)S(1)} %add_rsqrt_fusion.1, f32[320]{0:T(512)S(1)} %broadcast_multiply_fusion.1), kind=kOutput, calls=%fused_computation.162 | convolution fusion | flops 3031449344 | bytes 11410176 | tf_op jit(solution)/shard_map/dot_general | solution.py:30
  60.2 0.3 multiply_reduce_fusion
  60.5 0.2 multiply_convert_fusion
  60.7 0.8 %slice.220 = bf16[256,768]{1,0:T(8,128)(2,1)} slice(bf16[320,768]{1,0:T(8,128)(2,1)S(1)} %multiply_convert_fusion), slice={[0:256], [0:768]} | slice | bytes 786432 | tf_op jit(solution)/shard_map/slice | solution.py:268
  61.5 0.6 %slice.221 = bf16[64,768]{1,0:T(8,128)(2,1)} slice(bf16[320,768]{1,0:T(8,128)(2,1)S(1)} %multiply_convert_fusion), slice={[256:320], [0:768]} | slice | bytes 196608 | tf_op jit(solution)/shard_map/slice | solution.py:269
  (41 shorter events, 0.2 us)
Async XLA Ops:
  0.6 50.2 %copy-start = (bf16[768,768]{1,0:T(8,128)(2,1)S(1)}, bf16[768,768]{1,0:T(8,128)(2,1)}, u32[]{:S(2)}) copy-start(bf16[768,768]{1,0:T(8,128)(2,1)} %param.15) | copy-start | bytes 3538948
  0.6 28.9 %collective-permute-start.7 = (bf16[4,64,768]{2,1,0:T(8,128)(2,1)}, bf16[4,64,768]{2,1,0:T(8,128)(2,1)}, u32[]{:S(2)}, u32[]{:S(2)}) collective-permute-start(bf16[4,64,768]{2,1,0:T(8,128)(2,1)} %param.10), channel_id=1, source_target_pairs={{0,1},{1,0},{2,3},{3,2},{4,5},{5,4},{6,7},{7,6},{8,9},{9,8},{10,11... | collective-permute-start | bytes 1179656 | tf_op jit(solution)/shard_map/ppermute | solution.py:145
  3.6 25.9 %collective-permute-start.8 = (bf16[4,64,768]{2,1,0:T(8,128)(2,1)}, bf16[4,64,768]{2,1,0:T(8,128)(2,1)}, u32[]{:S(2)}, u32[]{:S(2)}) collective-permute-start(bf16[4,64,768]{2,1,0:T(8,128)(2,1)} %param.10), channel_id=1, source_target_pairs={{0,2},{1,3},{2,0},{3,1},{4,6},{5,7},{6,4},{7,5},{8,10},{9,11},{10,... | collective-permute-start | bytes 1179656 | tf_op jit(solution)/shard_map/ppermute | solution.py:145
  5.2 24.4 %collective-permute-start.9 = (bf16[4,64,768]{2,1,0:T(8,128)(2,1)}, bf16[4,64,768]{2,1,0:T(8,128)(2,1)}, u32[]{:S(2)}, u32[]{:S(2)}) collective-permute-start(bf16[4,64,768]{2,1,0:T(8,128)(2,1)} %param.10), channel_id=1, source_target_pairs={{0,3},{1,2},{2,1},{3,0},{4,7},{5,6},{6,5},{7,4},{8,11},{9,10},{10,... | collective-permute-start | bytes 1179656 | tf_op jit(solution)/shard_map/ppermute | solution.py:145
  5.2 2.3 %collective-permute-start = (bf16[64,768]{1,0:T(8,128)(2,1)}, bf16[64,768]{1,0:T(8,128)(2,1)S(1)}, u32[]{:S(2)}, u32[]{:S(2)}) collective-permute-start(bf16[64,768]{1,0:T(8,128)(2,1)} %bitcast.40), channel_id=1, source_target_pairs={{0,4},{4,0},{8,12},{12,8},{16,20},{20,16},{24,28},{28,24},{1,5},{5... | collective-permute-start | bytes 294920 | tf_op jit(solution)/shard_map/ppermute | solution.py:60
  8.4 5.5 %collective-permute-start.1 = (bf16[64,768]{1,0:T(8,128)(2,1)S(1)}, bf16[64,768]{1,0:T(8,128)(2,1)S(1)}, u32[]{:S(2)}, u32[]{:S(2)}) collective-permute-start(bf16[64,768]{1,0:T(8,128)(2,1)S(1)} %broadcast_select_fusion), channel_id=1, source_target_pairs={{0,8},{4,12},{8,0},{12,4},{16,24},{20,28},{24,16},{28,20},{1,9},{5... | collective-permute-start | bytes 294920 | tf_op jit(solution)/shard_map/ppermute | solution.py:60
  13.7 13.3 %copy-start.1 = (bf16[256,2304]{1,0:T(8,128)(2,1)}, bf16[256,2304]{1,0:T(8,128)(2,1)S(1)}, u32[]{:S(2)}) copy-start(bf16[256,2304]{1,0:T(8,128)(2,1)S(1)} %convolution_convert_fusion) | copy-start | bytes 3538948
  14.0 7.8 %collective-permute-start.2 = (bf16[64,768]{1,0:T(8,128)(2,1)S(1)}, bf16[64,768]{1,0:T(8,128)(2,1)S(1)}, u32[]{:S(2)}, u32[]{:S(2)}) collective-permute-start(bf16[64,768]{1,0:T(8,128)(2,1)S(1)} %broadcast_select_fusion.1), channel_id=1, source_target_pairs={{0,16},{4,20},{8,24},{12,28},{16,0},{20,4},{24,8},{28,12},{1,17},{... | collective-permute-start | bytes 294920 | tf_op jit(solution)/shard_map/ppermute | solution.py:60
  21.8 6.0 %copy-start.4 = (bf16[64,768]{1,0:T(8,128)(2,1)}, bf16[64,768]{1,0:T(8,128)(2,1)S(1)}, u32[]{:S(2)}) copy-start(bf16[64,768]{1,0:T(8,128)(2,1)S(1)} %broadcast_select_fusion.2) | copy-start | bytes 294916
  23.5 6.1 %copy-start.3 = (bf16[4,64,768]{2,1,0:T(8,128)(2,1)S(1)}, bf16[4,64,768]{2,1,0:T(8,128)(2,1)}, u32[]{:S(2)}) copy-start(bf16[4,64,768]{2,1,0:T(8,128)(2,1)} %param.10) | copy-start | bytes 1179652
  25.8 15.6 %copy-start.2 = (bf16[64,1536]{1,0:T(8,128)(2,1)}, bf16[64,1536]{1,0:T(8,128)(2,1)S(1)}, u32[]{:S(2)}) copy-start(bf16[64,1536]{1,0:T(8,128)(2,1)S(1)} %convolution_convert_fusion.2.sk_ref.sv_ref) | copy-start | bytes 589828
  26.7 1.2 %collective-permute-start.4 = (f32[32,24]{1,0:T(8,128)S(1)}, f32[32,24]{1,0:T(8,128)S(1)}, u32[]{:S(2)}, u32[]{:S(2)}) collective-permute-start(f32[32,24]{1,0:T(8,128)S(1)} %broadcast_select_fusion.9), channel_id=1, source_target_pairs={{0,4},{4,0},{8,12},{12,8},{16,20},{20,16},{24,28},{28,24},{1,5},{5... | collective-permute-start | bytes 9224 | tf_op jit(solution)/shard_map/ppermute | solution.py:60
  27.0 9.4 %copy-start.6 = (bf16[768,2304]{1,0:T(8,128)(2,1)S(1)}, bf16[768,2304]{1,0:T(8,128)(2,1)}, u32[]{:S(2)}) copy-start(bf16[768,2304]{1,0:T(8,128)(2,1)} %param.14) | copy-start | bytes 10616836
  27.1 1.5 %collective-permute-start.3 = (f32[32,768]{1,0:T(8,128)S(1)}, f32[32,768]{1,0:T(8,128)S(1)}, u32[]{:S(2)}, u32[]{:S(2)}) collective-permute-start(f32[32,768]{1,0:T(8,128)S(1)} %slice_select_fusion), channel_id=1, source_target_pairs={{0,4},{4,0},{8,12},{12,8},{16,20},{20,16},{24,28},{28,24},{1,5},{5... | collective-permute-start | bytes 294920 | tf_op jit(solution)/shard_map/ppermute | solution.py:60
  28.9 4.2 %collective-permute-start.5 = (bf16[32,840]{1,0:T(8,128)(2,1)S(1)}, bf16[32,840]{1,0:T(8,128)(2,1)S(1)}, u32[]{:S(2)}, u32[]{:S(2)}) collective-permute-start(bf16[32,840]{1,0:T(8,128)(2,1)S(1)} %pad_maximum_fusion.1), channel_id=1, source_target_pairs={{0,8},{4,12},{8,0},{12,4},{16,24},{20,28},{24,16},{28,20},{1,9},{5... | collective-permute-start | bytes 161288 | tf_op jit(solution)/shard_map/ppermute | solution.py:60
  34.1 6.3 %collective-permute-start.6 = (bf16[32,840]{1,0:T(8,128)(2,1)S(1)}, bf16[32,840]{1,0:T(8,128)(2,1)S(1)}, u32[]{:S(2)}, u32[]{:S(2)}) collective-permute-start(bf16[32,840]{1,0:T(8,128)(2,1)S(1)} %pad_maximum_fusion.2), channel_id=1, source_target_pairs={{0,16},{4,20},{8,24},{12,28},{16,0},{20,4},{24,8},{28,12},{1,17},{... | collective-permute-start | bytes 161288 | tf_op jit(solution)/shard_map/ppermute | solution.py:60
  41.8 9.0 %copy-start.5 = (bf16[64,768]{1,0:T(8,128)(2,1)S(1)}, bf16[64,768]{1,0:T(8,128)(2,1)}, u32[]{:S(2)}) copy-start(bf16[64,768]{1,0:T(8,128)(2,1)} %copy-done.4) | copy-start | bytes 294916
  41.8 8.9 %collective-permute-start.10 = (bf16[32,768]{1,0:T(8,128)(2,1)S(1)}, bf16[32,768]{1,0:T(8,128)(2,1)S(1)}, u32[]{:S(2)}, u32[]{:S(2)}) collective-permute-start(bf16[32,768]{1,0:T(8,128)(2,1)S(1)} %fusion.30), channel_id=1, source_target_pairs={{0,4},{4,0},{8,12},{12,8},{16,20},{20,16},{24,28},{28,24},{1,5},{5... | collective-permute-start | bytes 147464 | tf_op jit(solution)/shard_map/ppermute | solution.py:60
  50.7 2.0 %copy-start.8 = (f32[768]{0:T(1024)S(1)}, f32[768]{0:T(1024)}, u32[]{:S(2)}) copy-start(f32[768]{0:T(1024)} %param.16) | copy-start | bytes 9220
  52.7 7.7 %copy-start.7 = (f32[768]{0:T(1024)S(1)}, f32[768]{0:T(1024)}, u32[]{:S(2)}) copy-start(f32[768]{0:T(1024)} %param.19) | copy-start | bytes 9220

commit v22 on v20

--- a/solution.py
+++ b/solution.py
@@ -148,18 +148,18 @@
 
 def row_kernel(q_ref, k_ref, v_ref, sk_ref, sv_ref, allow_ref, o_ref, *, scale):
     rows = q_ref.shape[1]
-    allow = allow_ref[0] > 0.5
-    allow = jnp.concatenate([allow, allow], axis=0)
     lane = lax.broadcasted_iota(jnp.int32, (1, 2 * HEAD_DIM), 1)
     low = lane < HEAD_DIM
     nt = (((1,), (1,)), ((), ()))
-    for pair in range(HEADS // 2):
+    for row, pair in [(row, pair) for row in range(q_ref.shape[0]) for pair in range(HEADS // 2)]:
+        allow = allow_ref[row] > 0.5
+        allow = jnp.concatenate([allow, allow], axis=0)
         cols = slice(pair * 2 * HEAD_DIM, (pair + 1) * 2 * HEAD_DIM)
-        q = q_ref[0, :, cols] * scale
+        q = q_ref[row, :, cols] * scale
         zero = jnp.zeros_like(q)
         qh = jnp.concatenate([jnp.where(low, q, zero), jnp.where(low, zero, q)], axis=0)
-        k = k_ref[0, :, cols]
-        v = v_ref[0, :, cols]
+        k = k_ref[row, :, cols]
+        v = v_ref[row, :, cols]
         sk = sk_ref[:, cols]
         sv = sv_ref[:, cols]
         s = lax.dot_general(qh, k, nt, preferred_element_type=jnp.float32)
@@ -172,7 +172,7 @@
         acc = jnp.dot(e.astype(jnp.bfloat16), v, preferred_element_type=jnp.float32)
         acc = acc + jnp.dot(te.astype(jnp.bfloat16), sv, preferred_element_type=jnp.float32)
         out = jnp.where(low, acc[:rows] / tot[:rows], acc[rows:] / tot[rows:])
-        o_ref[0, :, cols] = out.astype(o_ref.dtype)
+        o_ref[row, :, cols] = out.astype(o_ref.dtype)
 
 
 def row_attention(qkv, kv, summary_kv, allow):
@@ -183,16 +183,16 @@
     kern = functools.partial(row_kernel, scale=HEAD_DIM ** (-0.5))
     return pl.pallas_call(
         kern,
-        grid=(rows,),
+        grid=(rows // 2,),
         in_specs=[
-            pl.BlockSpec((1, nq, width), lambda r: (r, 0, 0)),
-            pl.BlockSpec((1, nk, width), lambda r: (r, 0, 0)),
-            pl.BlockSpec((1, nk, width), lambda r: (r, 0, 1)),
+            pl.BlockSpec((2, nq, width), lambda r: (r, 0, 0)),
+            pl.BlockSpec((2, nk, width), lambda r: (r, 0, 0)),
+            pl.BlockSpec((2, nk, width), lambda r: (r, 0, 1)),
             pl.BlockSpec((ns, width), lambda r: (0, 0)),
             pl.BlockSpec((ns, width), lambda r: (0, 1)),
-            pl.BlockSpec((1, nq, nk), lambda r: (r, 0, 0)),
+            pl.BlockSpec((2, nq, nk), lambda r: (r, 0, 0)),
         ],
-        out_specs=pl.BlockSpec((1, nq, width), lambda r: (r, 0, 0)),
+        out_specs=pl.BlockSpec((2, nq, width), lambda r: (r, 0, 0)),
         out_shape=jax.ShapeDtypeStruct((rows, nq, width), jnp.bfloat16),
     )(qkv, kv, kv, summary_kv, summary_kv, allow)
 

time: 61.1 us -> 61.3 us (level)
  no operation moved by 1% of the time
where the time goes in v22:
time: 61.3 us; the launch traced here: 61 us
  matrix products  23.6 us (38%)
  starting transfers between devices  12.8 us (21%)
  Pallas kernels  8.91 us (15%)
  waiting for transfers between devices  6.45 us (11%)
  other arithmetic  5.9 us (10%)
  between operations  1.73 us (3%)
  local copies, waits for them, and re-layouts  1.63 us (3%)
    dot_general x4, matrix products, project(): jnp.dot(values, weight, preferred_element_type=jnp.float32)  11.3 us
    ppermute x8, starting transfers between devices, partner(): return lax.ppermute(value, axis, [(i, i ^ step) for i in range(count)])  9.3 us
    pallas_call x1, Pallas kernels, row_attention(): pl.pallas_call(kern, grid=(rows // 2,), in_specs=[pl.BlockSpec((2, nq, wi...  8.91 us
    dot_general x1, matrix products, finish(): outer_out = jnp.dot(inner_act, w_down, preferred_element_type=jnp.float32)  7.43 us
    ppermute x8, waiting for transfers between devices, partner(): return lax.ppermute(value, axis, [(i, i ^ step) for i in range(count)])  5.4 us
    ppermute x3, starting transfers between devices, fan_out(): got.append((source, lax.ppermute(value, axis, pairs)))  3.49 us
    dot_general x10, matrix products, head_spread(): jnp.dot(flat, head_matrix(), precision=lax.Precision.HIGHEST, preferred_e...  2.4 us
    dot_general x1, matrix products, finish(): mixed_out = jnp.dot(attended, w_out, preferred_element_type=jnp.float32)  1.65 us
  transfers between devices with their start and end apart: 11, of which 5 were waited for; matrix products, arithmetic and copies ran while one was open for 29% of the time, Pallas kernels for 15%

profile of v22, /device:TPU:0, one launch (start us, length us, event | category | flops | bytes accessed | tf_op | source)
XLA Modules:
  0.0 61.0 jit_solution(3720467022304955691)
XLA Ops:
  0.6 0.0 copy-start
  0.6 0.5 collective-permute-start
  1.2 0.1 pad_add_fusion
  1.3 1.5 %fusion.42.allow_ref = f32[4,64,256]{2,1,0:T(8,128)} fusion(s32[256]{0:T(256)S(1)} %pad_add_fusion, s32[4,64]{1,0:T(4,128)} %param.13, pred[256]{0:T(512)(128)(4,1)S(1)} %iota_compare_fusion.15), kind=kLoop, calls=%fused_computation.51 | loop fusion | flops 327680 | bytes 264448 | tf_op jit(solution)/shard_map/convert_element_type | solution.py:216
  3.4 0.0 copy-start.3
  3.5 1.0 %broadcast_select_fusion = bf16[64,768]{1,0:T(8,128)(2,1)S(1)} fusion(bf16[64,768]{1,0:T(8,128)(2,1)S(1)} %collective-permute-done, pred[]{:T(512)S(6)} %eq.88, bf16[1,64,768]{2,1,0:T(8,128)(2,1)} %param.11), kind=kLoop, calls=%fused_computation.58 | loop fusion | flops 49152 | bytes 294913 | tf_op jit(solution)/shard_map/jit(_where)/select_n | solution.py:70
  4.4 2.8 %collective-permute-start.1 = (bf16[64,768]{1,0:T(8,128)(2,1)S(1)}, bf16[64,768]{1,0:T(8,128)(2,1)S(1)}, u32[]{:S(2)}, u32[]{:S(2)}) collective-permute-start(bf16[64,768]{1,0:T(8,128)(2,1)S(1)} %broadcast_select_fusion), channel_id=1, source_target_pairs={{0,8},{4,12},{8,0},{12,4},{16,24},{20,28},{24,16},{28,20},{1,9},{5... | collective-permute-start | bytes 294920 | tf_op jit(solution)/shard_map/ppermute | solution.py:60
  7.2 3.2 %convolution_convert_fusion = bf16[256,2304]{1,0:T(8,128)(2,1)S(1)} fusion(bf16[256,768]{1,0:T(8,128)(2,1)} %bitcast.37, bf16[768,2304]{1,0:T(8,128)(2,1)} %param.14), kind=kOutput, calls=%fused_computation.9 | convolution fusion | flops 906559488 | bytes 5111808 | tf_op jit(solution)/shard_map/dot_general | solution.py:35
  10.6 2.8 %collective-permute-start.2 = (bf16[64,768]{1,0:T(8,128)(2,1)S(1)}, bf16[64,768]{1,0:T(8,128)(2,1)S(1)}, u32[]{:S(2)}, u32[]{:S(2)}) collective-permute-start(bf16[64,768]{1,0:T(8,128)(2,1)S(1)} %broadcast_select_fusion.1), channel_id=1, source_target_pairs={{0,16},{4,20},{8,24},{12,28},{16,0},{20,4},{24,8},{28,12},{1,17},{... | collective-permute-start | bytes 294920 | tf_op jit(solution)/shard_map/ppermute | solution.py:60
  13.4 1.5 %collective-permute-start.7 = (bf16[4,64,768]{2,1,0:T(8,128)(2,1)S(1)}, bf16[4,64,768]{2,1,0:T(8,128)(2,1)}, u32[]{:S(2)}, u32[]{:S(2)}) collective-permute-start(bf16[4,64,768]{2,1,0:T(8,128)(2,1)S(1)} %copy-done.3), channel_id=1, source_target_pairs={{0,1},{1,0},{2,3},{3,2},{4,5},{5,4},{6,7},{7,6},{8,9},{9,8},{10,11... | collective-permute-start | bytes 1179656 | tf_op jit(solution)/shard_map/ppermute | solution.py:145
  14.9 1.5 %collective-permute-start.8 = (bf16[4,64,768]{2,1,0:T(8,128)(2,1)S(1)}, bf16[4,64,768]{2,1,0:T(8,128)(2,1)}, u32[]{:S(2)}, u32[]{:S(2)}) collective-permute-start(bf16[4,64,768]{2,1,0:T(8,128)(2,1)S(1)} %copy-done.3), channel_id=1, source_target_pairs={{0,2},{1,3},{2,0},{3,1},{4,6},{5,7},{6,4},{7,5},{8,10},{9,11},{10,... | collective-permute-start | bytes 1179656 | tf_op jit(solution)/shard_map/ppermute | solution.py:145
  16.4 0.5 collective-permute-start.9
  16.9 1.5 %collective-permute-done.2 = bf16[64,768]{1,0:T(8,128)(2,1)S(1)} collective-permute-done((bf16[64,768]{1,0:T(8,128)(2,1)S(1)}, bf16[64,768]{1,0:T(8,128)(2,1)S(1)}, u32[]{:S(2)}, u32[]{:S(2)}) %collective-permute-start.2) | collective-permute-done | bytes 98336 | tf_op jit(solution)/shard_map/ppermute | solution.py:60
  18.4 1.6 %fusion.25 = f32[64,768]{1,0:T(8,128)S(1)} fusion(bf16[64,768]{1,0:T(8,128)(2,1)S(1)} %broadcast_select_fusion.2, bf16[768,2304]{1,0:T(8,128)(2,1)} %param.14), kind=kOutput, calls=%fused_computation.26 | convolution fusion | flops 75595776 | bytes 1474560 | tf_op jit(solution)/shard_map/dot_general | solution.py:35
  20.1 2.2 %convolution_convert_fusion.2.sk_ref.sv_ref = bf16[64,1536]{1,0:T(8,128)(2,1)S(1)} fusion(bf16[64,768]{1,0:T(8,128)(2,1)S(1)} %broadcast_select_fusion.2, bf16[768,2304]{1,0:T(8,128)(2,1)} %param.14), kind=kOutput, calls=%fused_computation.11 | convolution fusion | flops 151093248 | bytes 2654208 | tf_op jit(solution)/shard_map/dot_general | solution.py:35
  22.3 0.6 %fusion.93 = (f32[64,12]{0,1:T(8,128)S(1)}, f32[4,64,12]{1,2,0:T(8,128)S(1)}) fusion(s32[768]{0:T(1024)S(1)} %add_select_fusion, bf16[4,64,2304]{2,1,0:T(8,128)(2,1)S(1)} %bitcast.32, f32[64,768]{1,0:T(8,128)S(1)} %fusion.25), kind=kOutput, calls=%fused_computation.160 | convolution fusion | flops 28719360 | bytes 609280 | tf_op jit(solution)/shard_map/dot_general | solution.py:46
  22.9 0.1 slice_maximum_fusion.3
  23.0 0.1 copy.18
  23.1 0.1 copy.19
  23.2 0.1 collective-permute-start.4
  23.2 0.3 fusion.19
  23.6 0.6 collective-permute-start.3
  24.1 0.3 collective-permute-done.4
  24.4 0.1 fusion.75
  24.5 0.2 fusion.50
  24.8 0.1 fusion.91
  24.8 0.1 fusion.76
  24.9 0.1 subtract_convert_fusion.1
  25.0 0.1 collective-permute-done.3
  25.1 0.2 add_convert_fusion.1
  25.3 0.1 pad_maximum_fusion.1
  25.4 0.4 collective-permute-start.5
  25.9 0.2 convolution_multiply_fusion.4
  26.1 3.5 %collective-permute-done.5 = bf16[32,840]{1,0:T(8,128)(2,1)S(1)} collective-permute-done((bf16[32,840]{1,0:T(8,128)(2,1)S(1)}, bf16[32,840]{1,0:T(8,128)(2,1)S(1)}, u32[]{:S(2)}, u32[]{:S(2)}) %collective-permute-start.5) | collective-permute-done | bytes 53792 | tf_op jit(solution)/shard_map/ppermute | solution.py:60
  29.6 0.1 broadcast_select_fusion.6
  29.7 0.1 fusion.74
  29.8 0.2 fusion.47
  30.1 0.1 fusion.90
  30.1 0.1 fusion.77
  30.2 0.1 subtract_convert_fusion
  30.3 0.3 add_convert_fusion
  30.6 0.1 pad_maximum_fusion.2
  30.7 2.0 %collective-permute-start.6 = (bf16[32,840]{1,0:T(8,128)(2,1)S(1)}, bf16[32,840]{1,0:T(8,128)(2,1)S(1)}, u32[]{:S(2)}, u32[]{:S(2)}) collective-permute-start(bf16[32,840]{1,0:T(8,128)(2,1)S(1)} %pad_maximum_fusion.2), channel_id=1, source_target_pairs={{0,16},{4,20},{8,24},{12,28},{16,0},{20,4},{24,8},{28,12},{1,17},{... | collective-permute-start | bytes 161288 | tf_op jit(solution)/shard_map/ppermute | solution.py:60
  32.7 1.0 %collective-permute-done.8 = bf16[4,64,768]{2,1,0:T(8,128)(2,1)} collective-permute-done((bf16[4,64,768]{2,1,0:T(8,128)(2,1)S(1)}, bf16[4,64,768]{2,1,0:T(8,128)(2,1)}, u32[]{:S(2)}, u32[]{:S(2)}) %collective-permute-start.8) | collective-permute-done | bytes 393248 | tf_op jit(solution)/shard_map/ppermute | solution.py:145
  33.8 1.3 %pad_maximum_fusion = bf16[4,256,768]{2,1,0:T(8,128)(2,1)S(1)} fusion(bf16[4,64,768]{2,1,0:T(8,128)(2,1)} %collective-permute-done.9, bf16[4,64,768]{2,1,0:T(8,128)(2,1)} %collective-permute-done.8, bf16[4,64,768]{2,1,0:T(8,128)(2,1)} %collective-permute-done.7, bf16[4,64,768]{2,1,0:T(8,128)(2,1)S(1)} %copy-done.3), kind=kLoop, calls=%fused_computation.19 | loop fusion | flops 6291456 | bytes 3145728 | tf_op jit(solution)/shard_map/concatenate | solution.py:240
  35.1 4.2 %convolution_convert_fusion.1 = bf16[1024,1536]{1,0:T(8,128)(2,1)} fusion(bf16[1024,768]{1,0:T(8,128)(2,1)S(1)} %bitcast.35, bf16[768,2304]{1,0:T(8,128)(2,1)S(1)} %copy-done.6), kind=kOutput, calls=%fused_computation.10 | convolution fusion | flops 2417491968 | bytes 7077888 | tf_op jit(solution)/shard_map/dot_general | solution.py:35
  39.4 0.1 broadcast_select_fusion.4
  39.4 0.1 fusion.79
  39.5 0.3 convolution_multiply_fusion.3
  39.8 0.3 fusion.29
  40.1 0.1 fusion.46
  40.2 0.2 fusion.28
  40.4 0.3 fusion.30
  40.7 0.0 copy-start.5
  40.7 0.1 collective-permute-start.10
  40.8 8.9 %shard_map.113 = bf16[4,64,768]{2,1,0:T(8,128)(2,1)} custom-call(bf16[4,64,2304]{2,1,0:T(8,128)(2,1)} %bitcast.34, bf16[4,256,1536]{2,1,0:T(8,128)(2,1)} %bitcast.30, bf16[4,256,1536]{2,1,0:T(8,128)(2,1)} %bitcast.31, bf16[64,1536]{1,0:T(8,128)(2,1)} %copy-done.2, bf16[64,1536]{1,0:T(8,128)(2,1)} %copy-done.2, f32[4,64,256]{2,1,0:T(8,128)} %fusion.42.allow_ref), custom_call_target="tpu_custom_call" | custom-call | tf_op jit(solution)/shard_map/pallas_call | solution.py:184
  49.7 1.7 %fusion.94 = (f32[320]{0:T(512)S(1)}, f32[320,768]{1,0:T(8,128)S(1)}) fusion(bf16[768,768]{1,0:T(8,128)(2,1)S(1)} %copy-done, bf16[64,768]{1,0:T(8,128)(2,1)S(1)} %maximum_select_fusion, bf16[256,768]{1,0:T(8,128)(2,1)} %bitcast.36, bf16[64,768]{1,0:T(8,128)(2,1)S(1)} %copy-done.5, bf16[256,768]{1,0:T(8,128)(2,1)S(1)} %bitcast.38), kind=kOutput, calls=%fused_computation.161 | convolution fusion | flops 379944640 | bytes 3147008 | tf_op jit(solution)/shard_map/dot_general | solution.py:25
  51.4 0.3 multiply_reduce_fusion.1
  51.7 0.0 copy-start.7
  51.7 7.4 %fusion.95 = (f32[320]{0:T(512)S(1)}, f32[320,768]{1,0:T(8,128)S(1)}) fusion(bf16[3072,768]{1,0:T(8,128)(2,1)} %param.18, bf16[768,3072]{1,0:T(8,128)(2,1)} %param.17, f32[320,768]{1,0:T(8,128)S(1)} %get-tuple-element.32, f32[768]{0:T(1024)S(1)} %copy-done.8, f32[320]{0:T(512)S(1)} %add_rsqrt_fusion.1, f32[320]{0:T(512)S(1)} %broadcast_multiply_fusion.1), kind=kOutput, calls=%fused_computation.162 | convolution fusion | flops 3031449344 | bytes 11410176 | tf_op jit(solution)/shard_map/dot_general | solution.py:30
  59.1 0.3 multiply_reduce_fusion
  59.4 0.2 multiply_convert_fusion
  59.6 0.8 %slice.220 = bf16[256,768]{1,0:T(8,128)(2,1)} slice(bf16[320,768]{1,0:T(8,128)(2,1)S(1)} %multiply_convert_fusion), slice={[0:256], [0:768]} | slice | bytes 786432 | tf_op jit(solution)/shard_map/slice | solution.py:268
  60.4 0.6 %slice.221 = bf16[64,768]{1,0:T(8,128)(2,1)} slice(bf16[320,768]{1,0:T(8,128)(2,1)S(1)} %multiply_convert_fusion), slice={[256:320], [0:768]} | slice | bytes 196608 | tf_op jit(solution)/shard_map/slice | solution.py:269
  (41 shorter events, 0.2 us)
Async XLA Ops:
  0.6 49.1 %copy-start = (bf16[768,768]{1,0:T(8,128)(2,1)S(1)}, bf16[768,768]{1,0:T(8,128)(2,1)}, u32[]{:S(2)}) copy-start(bf16[768,768]{1,0:T(8,128)(2,1)} %param.15) | copy-start | bytes 3538948
  0.6 2.8 %collective-permute-start = (bf16[64,768]{1,0:T(8,128)(2,1)}, bf16[64,768]{1,0:T(8,128)(2,1)S(1)}, u32[]{:S(2)}, u32[]{:S(2)}) collective-permute-start(bf16[64,768]{1,0:T(8,128)(2,1)} %bitcast.40), channel_id=1, source_target_pairs={{0,4},{4,0},{8,12},{12,8},{16,20},{20,16},{24,28},{28,24},{1,5},{5... | collective-permute-start | bytes 294920 | tf_op jit(solution)/shard_map/ppermute | solution.py:60
  3.4 9.9 %copy-start.3 = (bf16[4,64,768]{2,1,0:T(8,128)(2,1)S(1)}, bf16[4,64,768]{2,1,0:T(8,128)(2,1)}, u32[]{:S(2)}) copy-start(bf16[4,64,768]{2,1,0:T(8,128)(2,1)} %param.10) | copy-start | bytes 1179652
  4.4 6.1 %collective-permute-start.1 = (bf16[64,768]{1,0:T(8,128)(2,1)S(1)}, bf16[64,768]{1,0:T(8,128)(2,1)S(1)}, u32[]{:S(2)}, u32[]{:S(2)}) collective-permute-start(bf16[64,768]{1,0:T(8,128)(2,1)S(1)} %broadcast_select_fusion), channel_id=1, source_target_pairs={{0,8},{4,12},{8,0},{12,4},{16,24},{20,28},{24,16},{28,20},{1,9},{5... | collective-permute-start | bytes 294920 | tf_op jit(solution)/shard_map/ppermute | solution.py:60
  10.5 13.1 %copy-start.1 = (bf16[256,2304]{1,0:T(8,128)(2,1)}, bf16[256,2304]{1,0:T(8,128)(2,1)S(1)}, u32[]{:S(2)}) copy-start(bf16[256,2304]{1,0:T(8,128)(2,1)S(1)} %convolution_convert_fusion) | copy-start | bytes 3538948
  10.6 7.8 %collective-permute-start.2 = (bf16[64,768]{1,0:T(8,128)(2,1)S(1)}, bf16[64,768]{1,0:T(8,128)(2,1)S(1)}, u32[]{:S(2)}, u32[]{:S(2)}) collective-permute-start(bf16[64,768]{1,0:T(8,128)(2,1)S(1)} %broadcast_select_fusion.1), channel_id=1, source_target_pairs={{0,16},{4,20},{8,24},{12,28},{16,0},{20,4},{24,8},{28,12},{1,17},{... | collective-permute-start | bytes 294920 | tf_op jit(solution)/shard_map/ppermute | solution.py:60
  13.4 19.3 %collective-permute-start.7 = (bf16[4,64,768]{2,1,0:T(8,128)(2,1)S(1)}, bf16[4,64,768]{2,1,0:T(8,128)(2,1)}, u32[]{:S(2)}, u32[]{:S(2)}) collective-permute-start(bf16[4,64,768]{2,1,0:T(8,128)(2,1)S(1)} %copy-done.3), channel_id=1, source_target_pairs={{0,1},{1,0},{2,3},{3,2},{4,5},{5,4},{6,7},{7,6},{8,9},{9,8},{10,11... | collective-permute-start | bytes 1179656 | tf_op jit(solution)/shard_map/ppermute | solution.py:145
  14.9 18.9 %collective-permute-start.8 = (bf16[4,64,768]{2,1,0:T(8,128)(2,1)S(1)}, bf16[4,64,768]{2,1,0:T(8,128)(2,1)}, u32[]{:S(2)}, u32[]{:S(2)}) collective-permute-start(bf16[4,64,768]{2,1,0:T(8,128)(2,1)S(1)} %copy-done.3), channel_id=1, source_target_pairs={{0,2},{1,3},{2,0},{3,1},{4,6},{5,7},{6,4},{7,5},{8,10},{9,11},{10,... | collective-permute-start | bytes 1179656 | tf_op jit(solution)/shard_map/ppermute | solution.py:145
  16.4 17.4 %collective-permute-start.9 = (bf16[4,64,768]{2,1,0:T(8,128)(2,1)S(1)}, bf16[4,64,768]{2,1,0:T(8,128)(2,1)}, u32[]{:S(2)}, u32[]{:S(2)}) collective-permute-start(bf16[4,64,768]{2,1,0:T(8,128)(2,1)S(1)} %copy-done.3), channel_id=1, source_target_pairs={{0,3},{1,2},{2,1},{3,0},{4,7},{5,6},{6,5},{7,4},{8,11},{9,10},{10,... | collective-permute-start | bytes 1179656 | tf_op jit(solution)/shard_map/ppermute | solution.py:145
  18.4 6.3 %copy-start.4 = (bf16[64,768]{1,0:T(8,128)(2,1)}, bf16[64,768]{1,0:T(8,128)(2,1)S(1)}, u32[]{:S(2)}) copy-start(bf16[64,768]{1,0:T(8,128)(2,1)S(1)} %broadcast_select_fusion.2) | copy-start | bytes 294916
  22.3 17.9 %copy-start.2 = (bf16[64,1536]{1,0:T(8,128)(2,1)}, bf16[64,1536]{1,0:T(8,128)(2,1)S(1)}, u32[]{:S(2)}) copy-start(bf16[64,1536]{1,0:T(8,128)(2,1)S(1)} %convolution_convert_fusion.2.sk_ref.sv_ref) | copy-start | bytes 589828
  23.2 1.2 %collective-permute-start.4 = (f32[32,24]{1,0:T(8,128)S(1)}, f32[32,24]{1,0:T(8,128)S(1)}, u32[]{:S(2)}, u32[]{:S(2)}) collective-permute-start(f32[32,24]{1,0:T(8,128)S(1)} %broadcast_select_fusion.9), channel_id=1, source_target_pairs={{0,4},{4,0},{8,12},{12,8},{16,20},{20,16},{24,28},{28,24},{1,5},{5... | collective-permute-start | bytes 9224 | tf_op jit(solution)/shard_map/ppermute | solution.py:60
  23.5 11.6 %copy-start.6 = (bf16[768,2304]{1,0:T(8,128)(2,1)S(1)}, bf16[768,2304]{1,0:T(8,128)(2,1)}, u32[]{:S(2)}) copy-start(bf16[768,2304]{1,0:T(8,128)(2,1)} %param.14) | copy-start | bytes 10616836
  23.6 1.5 %collective-permute-start.3 = (f32[32,768]{1,0:T(8,128)S(1)}, f32[32,768]{1,0:T(8,128)S(1)}, u32[]{:S(2)}, u32[]{:S(2)}) collective-permute-start(f32[32,768]{1,0:T(8,128)S(1)} %slice_select_fusion), channel_id=1, source_target_pairs={{0,4},{4,0},{8,12},{12,8},{16,20},{20,16},{24,28},{28,24},{1,5},{5... | collective-permute-start | bytes 294920 | tf_op jit(solution)/shard_map/ppermute | solution.py:60
  25.4 4.2 %collective-permute-start.5 = (bf16[32,840]{1,0:T(8,128)(2,1)S(1)}, bf16[32,840]{1,0:T(8,128)(2,1)S(1)}, u32[]{:S(2)}, u32[]{:S(2)}) collective-permute-start(bf16[32,840]{1,0:T(8,128)(2,1)S(1)} %pad_maximum_fusion.1), channel_id=1, source_target_pairs={{0,8},{4,12},{8,0},{12,4},{16,24},{20,28},{24,16},{28,20},{1,9},{5... | collective-permute-start | bytes 161288 | tf_op jit(solution)/shard_map/ppermute | solution.py:60
  30.7 8.7 %collective-permute-start.6 = (bf16[32,840]{1,0:T(8,128)(2,1)S(1)}, bf16[32,840]{1,0:T(8,128)(2,1)S(1)}, u32[]{:S(2)}, u32[]{:S(2)}) collective-permute-start(bf16[32,840]{1,0:T(8,128)(2,1)S(1)} %pad_maximum_fusion.2), channel_id=1, source_target_pairs={{0,16},{4,20},{8,24},{12,28},{16,0},{20,4},{24,8},{28,12},{1,17},{... | collective-permute-start | bytes 161288 | tf_op jit(solution)/shard_map/ppermute | solution.py:60
  40.7 9.0 %copy-start.5 = (bf16[64,768]{1,0:T(8,128)(2,1)S(1)}, bf16[64,768]{1,0:T(8,128)(2,1)}, u32[]{:S(2)}) copy-start(bf16[64,768]{1,0:T(8,128)(2,1)} %copy-done.4) | copy-start | bytes 294916
  40.7 9.0 %collective-permute-start.10 = (bf16[32,768]{1,0:T(8,128)(2,1)S(1)}, bf16[32,768]{1,0:T(8,128)(2,1)S(1)}, u32[]{:S(2)}, u32[]{:S(2)}) collective-permute-start(bf16[32,768]{1,0:T(8,128)(2,1)S(1)} %fusion.30), channel_id=1, source_target_pairs={{0,4},{4,0},{8,12},{12,8},{16,20},{20,16},{24,28},{28,24},{1,5},{5... | collective-permute-start | bytes 147464 | tf_op jit(solution)/shard_map/ppermute | solution.py:60
  49.7 2.0 %copy-start.8 = (f32[768]{0:T(1024)S(1)}, f32[768]{0:T(1024)}, u32[]{:S(2)}) copy-start(f32[768]{0:T(1024)} %param.16) | copy-start | bytes 9220
  51.7 7.7 %copy-start.7 = (f32[768]{0:T(1024)S(1)}, f32[768]{0:T(1024)}, u32[]{:S(2)}) copy-start(f32[768]{0:T(1024)} %param.19) | copy-start | bytes 9220

commit v23 on v20

--- a/solution.py
+++ b/solution.py
@@ -256,17 +256,17 @@
         lax.optimization_barrier(self_exp.astype(jnp.bfloat16)).astype(jnp.float32)
     ) * half_vals
     summary_att = (col_mixed / head_spread(col_total)).astype(jnp.bfloat16)
-    summary_att = join_halves(summary_att, "band", n_band)
 
     sources = [own_group] + [s for s, _ in row_parts]
     attended = row_attention(qkv_cells, row_kv, summary_kv, allowed)
     attended = attended.reshape(row_count * cols_dev, model_width)
 
-    all_in = jnp.concatenate([flat_cells, tokens], axis=0)
+    half_tokens = jnp.where(first, tokens[:half], tokens[half:])
+    all_in = jnp.concatenate([flat_cells, half_tokens], axis=0)
     all_att = jnp.concatenate([attended, summary_att], axis=0)
     all_out = finish(all_in, all_att, w_out, gain_attn, w_up, w_down, gain_ffn)
     cells_out = all_out[: row_count * cols_dev].reshape(row_count, cols_dev, model_width)
-    summary_out = all_out[row_count * cols_dev :]
+    summary_out = join_halves(all_out[row_count * cols_dev :], "band", n_band)
     return (cells_out, summary_out)
 
 

time: 61.1 us -> 61.2 us (level)
  local copies, waits for them, and re-layouts: 1.63 us -> 0.97 us
  other arithmetic: 5.9 us -> 6.52 us
    slice x1, local copies, waits for them, and re-layouts: 0.65 us -> 0.01 us  [local(): summary_out = join_halves(all_out[row_count * cols_dev:], 'band', n_band)]
    select_n x1, other arithmetic: 0.02 us -> 0.66 us  [join_halves(): jnp.where(first, jnp.concatenate([value, got]), jnp.concatenate([got, val...]
  transfers between devices with their start and end apart: 11 -> 11, of which waited for: 5 -> 5; matrix products, arithmetic and copies ran while one was open for 29% -> 30% of each run, Pallas kernels for 15% -> 0%
where the time goes in v23:
time: 61.2 us; the launch traced here: 60.9 us
  matrix products  23.1 us (38%)
  starting transfers between devices  12.8 us (21%)
  Pallas kernels  8.86 us (14%)
  waiting for transfers between devices  6.94 us (11%)
  other arithmetic  6.52 us (11%)
  between operations  1.69 us (3%)
  local copies, waits for them, and re-layouts  0.97 us (2%)
    dot_general x4, matrix products, project(): jnp.dot(values, weight, preferred_element_type=jnp.float32)  11.1 us
    ppermute x8, starting transfers between devices, partner(): return lax.ppermute(value, axis, [(i, i ^ step) for i in range(count)])  9.29 us
    pallas_call x1, Pallas kernels, row_attention(): pl.pallas_call(kern, grid=(rows,), in_specs=[pl.BlockSpec((1, nq, width),...  8.86 us
    dot_general x1, matrix products, finish(): outer_out = jnp.dot(inner_act, w_down, preferred_element_type=jnp.float32)  7.16 us
    ppermute x8, waiting for transfers between devices, partner(): return lax.ppermute(value, axis, [(i, i ^ step) for i in range(count)])  5.85 us
    ppermute x3, starting transfers between devices, fan_out(): got.append((source, lax.ppermute(value, axis, pairs)))  3.49 us
    dot_general x10, matrix products, head_spread(): jnp.dot(flat, head_matrix(), precision=lax.Precision.HIGHEST, preferred_e...  2.4 us
    dot_general x1, matrix products, finish(): mixed_out = jnp.dot(attended, w_out, preferred_element_type=jnp.float32)  1.63 us
  transfers between devices with their start and end apart: 11, of which 5 were waited for; matrix products, arithmetic and copies ran while one was open for 30% of the time, Pallas kernels for 0%

profile of v23, /device:TPU:0, one launch (start us, length us, event | category | flops | bytes accessed | tf_op | source)
XLA Modules:
  0.0 60.9 jit_solution(6046506434270906015)
XLA Ops:
  0.6 0.0 copy-start
  0.6 0.5 collective-permute-start
  1.2 0.1 pad_add_fusion
  1.3 1.5 %fusion.39.allow_ref = f32[4,64,256]{2,1,0:T(8,128)} fusion(s32[256]{0:T(256)S(1)} %pad_add_fusion, s32[4,64]{1,0:T(4,128)} %param.13, pred[256]{0:T(512)(128)(4,1)S(1)} %iota_compare_fusion.15), kind=kLoop, calls=%fused_computation.50 | loop fusion | flops 327680 | bytes 264448 | tf_op jit(solution)/shard_map/convert_element_type | solution.py:216
  3.4 0.0 copy-start.3
  3.5 1.0 %broadcast_select_fusion = bf16[64,768]{1,0:T(8,128)(2,1)S(1)} fusion(bf16[64,768]{1,0:T(8,128)(2,1)S(1)} %collective-permute-done, pred[]{:T(512)S(6)} %eq.89, bf16[1,64,768]{2,1,0:T(8,128)(2,1)} %param.11), kind=kLoop, calls=%fused_computation.57 | loop fusion | flops 49152 | bytes 294913 | tf_op jit(solution)/shard_map/jit(_where)/select_n | solution.py:70
  4.4 2.8 %collective-permute-start.1 = (bf16[64,768]{1,0:T(8,128)(2,1)S(1)}, bf16[64,768]{1,0:T(8,128)(2,1)S(1)}, u32[]{:S(2)}, u32[]{:S(2)}) collective-permute-start(bf16[64,768]{1,0:T(8,128)(2,1)S(1)} %broadcast_select_fusion), channel_id=1, source_target_pairs={{0,8},{4,12},{8,0},{12,4},{16,24},{20,28},{24,16},{28,20},{1,9},{5... | collective-permute-start | bytes 294920 | tf_op jit(solution)/shard_map/ppermute | solution.py:60
  7.2 3.2 %convolution_convert_fusion = bf16[256,2304]{1,0:T(8,128)(2,1)S(1)} fusion(bf16[256,768]{1,0:T(8,128)(2,1)} %bitcast.37, bf16[768,2304]{1,0:T(8,128)(2,1)} %param.14), kind=kOutput, calls=%fused_computation.1 | convolution fusion | flops 906559488 | bytes 5111808 | tf_op jit(solution)/shard_map/dot_general | solution.py:35
  10.6 2.8 %collective-permute-start.2 = (bf16[64,768]{1,0:T(8,128)(2,1)S(1)}, bf16[64,768]{1,0:T(8,128)(2,1)S(1)}, u32[]{:S(2)}, u32[]{:S(2)}) collective-permute-start(bf16[64,768]{1,0:T(8,128)(2,1)S(1)} %broadcast_select_fusion.1), channel_id=1, source_target_pairs={{0,16},{4,20},{8,24},{12,28},{16,0},{20,4},{24,8},{28,12},{1,17},{... | collective-permute-start | bytes 294920 | tf_op jit(solution)/shard_map/ppermute | solution.py:60
  13.4 1.5 %collective-permute-start.7 = (bf16[4,64,768]{2,1,0:T(8,128)(2,1)S(1)}, bf16[4,64,768]{2,1,0:T(8,128)(2,1)}, u32[]{:S(2)}, u32[]{:S(2)}) collective-permute-start(bf16[4,64,768]{2,1,0:T(8,128)(2,1)S(1)} %copy-done.3), channel_id=1, source_target_pairs={{0,1},{1,0},{2,3},{3,2},{4,5},{5,4},{6,7},{7,6},{8,9},{9,8},{10,11... | collective-permute-start | bytes 1179656 | tf_op jit(solution)/shard_map/ppermute | solution.py:145
  14.9 1.5 %collective-permute-start.8 = (bf16[4,64,768]{2,1,0:T(8,128)(2,1)S(1)}, bf16[4,64,768]{2,1,0:T(8,128)(2,1)}, u32[]{:S(2)}, u32[]{:S(2)}) collective-permute-start(bf16[4,64,768]{2,1,0:T(8,128)(2,1)S(1)} %copy-done.3), channel_id=1, source_target_pairs={{0,2},{1,3},{2,0},{3,1},{4,6},{5,7},{6,4},{7,5},{8,10},{9,11},{10,... | collective-permute-start | bytes 1179656 | tf_op jit(solution)/shard_map/ppermute | solution.py:145
  16.4 0.5 collective-permute-start.9
  16.9 1.5 %collective-permute-done.2 = bf16[64,768]{1,0:T(8,128)(2,1)S(1)} collective-permute-done((bf16[64,768]{1,0:T(8,128)(2,1)S(1)}, bf16[64,768]{1,0:T(8,128)(2,1)S(1)}, u32[]{:S(2)}, u32[]{:S(2)}) %collective-permute-start.2) | collective-permute-done | bytes 98336 | tf_op jit(solution)/shard_map/ppermute | solution.py:60
  18.4 1.6 %fusion.25 = f32[64,768]{1,0:T(8,128)S(1)} fusion(bf16[64,768]{1,0:T(8,128)(2,1)S(1)} %broadcast_select_fusion.2, bf16[768,2304]{1,0:T(8,128)(2,1)} %param.14), kind=kOutput, calls=%fused_computation.27 | convolution fusion | flops 75595776 | bytes 1474560 | tf_op jit(solution)/shard_map/dot_general | solution.py:35
  20.0 2.2 %convolution_convert_fusion.2.sk_ref.sv_ref = bf16[64,1536]{1,0:T(8,128)(2,1)S(1)} fusion(bf16[64,768]{1,0:T(8,128)(2,1)S(1)} %broadcast_select_fusion.2, bf16[768,2304]{1,0:T(8,128)(2,1)} %param.14), kind=kOutput, calls=%fused_computation.11 | convolution fusion | flops 151093248 | bytes 2654208 | tf_op jit(solution)/shard_map/dot_general | solution.py:35
  22.2 0.6 %fusion.90 = (f32[64,12]{0,1:T(8,128)S(1)}, f32[4,64,12]{1,2,0:T(8,128)S(1)}) fusion(s32[768]{0:T(1024)S(1)} %add_select_fusion, bf16[4,64,2304]{2,1,0:T(8,128)(2,1)S(1)} %bitcast.32, f32[64,768]{1,0:T(8,128)S(1)} %fusion.25), kind=kOutput, calls=%fused_computation.160 | convolution fusion | flops 28719360 | bytes 609280 | tf_op jit(solution)/shard_map/dot_general | solution.py:46
  22.9 0.1 slice_maximum_fusion.3
  23.0 0.1 copy.18
  23.0 0.1 copy.19
  23.1 0.1 collective-permute-start.4
  23.2 0.3 fusion.19
  23.5 0.0 copy-start.4
  23.5 0.6 collective-permute-start.3
  24.1 0.2 convolution_multiply_fusion.4
  24.3 0.0 collective-permute-done.4
  24.4 0.1 fusion.72
  24.4 0.2 fusion.47
  24.7 0.1 fusion.88
  24.8 0.1 fusion.73
  24.9 0.1 subtract_convert_fusion.1
  24.9 0.1 collective-permute-done.3
  25.0 0.3 add_convert_fusion.1
  25.3 0.1 pad_maximum_fusion.1
  25.4 0.4 collective-permute-start.5
  25.8 3.7 %collective-permute-done.5 = bf16[32,840]{1,0:T(8,128)(2,1)S(1)} collective-permute-done((bf16[32,840]{1,0:T(8,128)(2,1)S(1)}, bf16[32,840]{1,0:T(8,128)(2,1)S(1)}, u32[]{:S(2)}, u32[]{:S(2)}) %collective-permute-start.5) | collective-permute-done | bytes 53792 | tf_op jit(solution)/shard_map/ppermute | solution.py:60
  29.6 0.1 broadcast_select_fusion.6
  29.7 0.1 fusion.71
  29.8 0.2 fusion.44
  30.0 0.1 fusion.87
  30.1 0.1 fusion.74
  30.2 0.1 subtract_convert_fusion
  30.3 0.3 add_convert_fusion
  30.5 0.1 pad_maximum_fusion.2
  30.6 2.0 %collective-permute-start.6 = (bf16[32,840]{1,0:T(8,128)(2,1)S(1)}, bf16[32,840]{1,0:T(8,128)(2,1)S(1)}, u32[]{:S(2)}, u32[]{:S(2)}) collective-permute-start(bf16[32,840]{1,0:T(8,128)(2,1)S(1)} %pad_maximum_fusion.2), channel_id=1, source_target_pairs={{0,16},{4,20},{8,24},{12,28},{16,0},{20,4},{24,8},{28,12},{1,17},{... | collective-permute-start | bytes 161288 | tf_op jit(solution)/shard_map/ppermute | solution.py:60
  32.7 1.1 %collective-permute-done.8 = bf16[4,64,768]{2,1,0:T(8,128)(2,1)} collective-permute-done((bf16[4,64,768]{2,1,0:T(8,128)(2,1)S(1)}, bf16[4,64,768]{2,1,0:T(8,128)(2,1)}, u32[]{:S(2)}, u32[]{:S(2)}) %collective-permute-start.8) | collective-permute-done | bytes 393248 | tf_op jit(solution)/shard_map/ppermute | solution.py:145
  33.8 1.3 %pad_maximum_fusion = bf16[4,256,768]{2,1,0:T(8,128)(2,1)S(1)} fusion(bf16[4,64,768]{2,1,0:T(8,128)(2,1)} %collective-permute-done.9, bf16[4,64,768]{2,1,0:T(8,128)(2,1)} %collective-permute-done.8, bf16[4,64,768]{2,1,0:T(8,128)(2,1)} %collective-permute-done.7, bf16[4,64,768]{2,1,0:T(8,128)(2,1)S(1)} %copy-done.3), kind=kLoop, calls=%fused_computation.19 | loop fusion | flops 6291456 | bytes 3145728 | tf_op jit(solution)/shard_map/concatenate | solution.py:240
  35.1 4.0 %convolution_convert_fusion.1 = bf16[1024,1536]{1,0:T(8,128)(2,1)} fusion(bf16[1024,768]{1,0:T(8,128)(2,1)S(1)} %bitcast.35, bf16[768,2304]{1,0:T(8,128)(2,1)S(1)} %copy-done.4), kind=kOutput, calls=%fused_computation.2 | convolution fusion | flops 2417491968 | bytes 7077888 | tf_op jit(solution)/shard_map/dot_general | solution.py:35
  39.2 0.1 broadcast_select_fusion.4
  39.2 0.1 fusion.76
  39.3 0.3 convolution_multiply_fusion.3
  39.6 0.2 fusion.29
  39.9 0.1 fusion.43
  40.0 0.2 fusion.28
  40.2 0.3 fusion.30
  40.5 8.9 %shard_map.113 = bf16[4,64,768]{2,1,0:T(8,128)(2,1)} custom-call(bf16[4,64,2304]{2,1,0:T(8,128)(2,1)} %bitcast.34, bf16[4,256,1536]{2,1,0:T(8,128)(2,1)} %bitcast.30, bf16[4,256,1536]{2,1,0:T(8,128)(2,1)} %bitcast.31, bf16[64,1536]{1,0:T(8,128)(2,1)} %copy-done.2, bf16[64,1536]{1,0:T(8,128)(2,1)} %copy-done.2, f32[4,64,256]{2,1,0:T(8,128)} %fusion.39.allow_ref), custom_call_target="tpu_custom_call" | custom-call | tf_op jit(solution)/shard_map/pallas_call | solution.py:184
  49.3 1.6 %fusion.91 = (f32[288]{0:T(512)S(1)}, f32[288,768]{1,0:T(8,128)S(1)}) fusion(bf16[768,768]{1,0:T(8,128)(2,1)S(1)} %copy-done, bf16[32,768]{1,0:T(8,128)(2,1)S(1)} %fusion.30, bf16[256,768]{1,0:T(8,128)(2,1)} %bitcast.36, bf16[32,768]{1,0:T(8,128)(2,1)S(1)} %slice_select_fusion.2, bf16[256,768]{1,0:T(8,128)(2,1)S(1)} %bitcast.38), kind=kOutput, calls=%fused_computation.161 | convolution fusion | flops 341950176 | bytes 2950272 | tf_op jit(solution)/shard_map/dot_general | solution.py:25
  51.0 0.3 multiply_reduce_fusion.1
  51.3 7.2 %fusion.92 = (f32[288]{0:T(512)S(1)}, f32[288,768]{1,0:T(8,128)S(1)}) fusion(bf16[3072,768]{1,0:T(8,128)(2,1)} %param.18, bf16[768,3072]{1,0:T(8,128)(2,1)} %param.17, f32[288,768]{1,0:T(8,128)S(1)} %get-tuple-element.32, f32[768]{0:T(1024)S(1)} %copy-done.6, f32[288]{0:T(512)S(1)} %add_rsqrt_fusion.1, f32[288]{0:T(512)S(1)} %broadcast_multiply_fusion.1), kind=kOutput, calls=%fused_computation.162 | convolution fusion | flops 2728304384 | bytes 11213184 | tf_op jit(solution)/shard_map/dot_general | solution.py:30
  58.4 0.3 multiply_reduce_fusion
  58.7 0.2 multiply_convert_fusion
  58.9 0.1 collective-permute-start.10
  59.0 0.8 %slice.230 = bf16[256,768]{1,0:T(8,128)(2,1)} slice(bf16[288,768]{1,0:T(8,128)(2,1)S(1)} %multiply_convert_fusion), slice={[0:256], [0:768]} | slice | bytes 786432 | tf_op jit(solution)/shard_map/slice | solution.py:268
  59.8 0.4 collective-permute-done.10
  60.2 0.7 %maximum_select_fusion = bf16[64,768]{1,0:T(8,128)(2,1)} fusion(bf16[32,768]{1,0:T(8,128)(2,1)S(1)} %collective-permute-done.10, bf16[32,768]{1,0:T(8,128)(2,1)S(1)} %slice.231, pred[]{:T(512)S(6)} %eq.86), kind=kLoop, calls=%fused_computation.54 | loop fusion | flops 442368 | bytes 196609 | tf_op jit(solution)/shard_map/jit(_where)/select_n | solution.py:132
  (38 shorter events, 0.2 us)
Async XLA Ops:
  0.6 48.7 %copy-start = (bf16[768,768]{1,0:T(8,128)(2,1)S(1)}, bf16[768,768]{1,0:T(8,128)(2,1)}, u32[]{:S(2)}) copy-start(bf16[768,768]{1,0:T(8,128)(2,1)} %param.15) | copy-start | bytes 3538948
  0.6 2.8 %collective-permute-start = (bf16[64,768]{1,0:T(8,128)(2,1)}, bf16[64,768]{1,0:T(8,128)(2,1)S(1)}, u32[]{:S(2)}, u32[]{:S(2)}) collective-permute-start(bf16[64,768]{1,0:T(8,128)(2,1)} %bitcast.40), channel_id=1, source_target_pairs={{0,4},{4,0},{8,12},{12,8},{16,20},{20,16},{24,28},{28,24},{1,5},{5... | collective-permute-start | bytes 294920 | tf_op jit(solution)/shard_map/ppermute | solution.py:60
  3.4 9.9 %copy-start.3 = (bf16[4,64,768]{2,1,0:T(8,128)(2,1)S(1)}, bf16[4,64,768]{2,1,0:T(8,128)(2,1)}, u32[]{:S(2)}) copy-start(bf16[4,64,768]{2,1,0:T(8,128)(2,1)} %param.10) | copy-start | bytes 1179652
  4.4 6.1 %collective-permute-start.1 = (bf16[64,768]{1,0:T(8,128)(2,1)S(1)}, bf16[64,768]{1,0:T(8,128)(2,1)S(1)}, u32[]{:S(2)}, u32[]{:S(2)}) collective-permute-start(bf16[64,768]{1,0:T(8,128)(2,1)S(1)} %broadcast_select_fusion), channel_id=1, source_target_pairs={{0,8},{4,12},{8,0},{12,4},{16,24},{20,28},{24,16},{28,20},{1,9},{5... | collective-permute-start | bytes 294920 | tf_op jit(solution)/shard_map/ppermute | solution.py:60
  10.4 13.0 %copy-start.1 = (bf16[256,2304]{1,0:T(8,128)(2,1)}, bf16[256,2304]{1,0:T(8,128)(2,1)S(1)}, u32[]{:S(2)}) copy-start(bf16[256,2304]{1,0:T(8,128)(2,1)S(1)} %convolution_convert_fusion) | copy-start | bytes 3538948
  10.6 7.8 %collective-permute-start.2 = (bf16[64,768]{1,0:T(8,128)(2,1)S(1)}, bf16[64,768]{1,0:T(8,128)(2,1)S(1)}, u32[]{:S(2)}, u32[]{:S(2)}) collective-permute-start(bf16[64,768]{1,0:T(8,128)(2,1)S(1)} %broadcast_select_fusion.1), channel_id=1, source_target_pairs={{0,16},{4,20},{8,24},{12,28},{16,0},{20,4},{24,8},{28,12},{1,17},{... | collective-permute-start | bytes 294920 | tf_op jit(solution)/shard_map/ppermute | solution.py:60
  13.4 19.3 %collective-permute-start.7 = (bf16[4,64,768]{2,1,0:T(8,128)(2,1)S(1)}, bf16[4,64,768]{2,1,0:T(8,128)(2,1)}, u32[]{:S(2)}, u32[]{:S(2)}) collective-permute-start(bf16[4,64,768]{2,1,0:T(8,128)(2,1)S(1)} %copy-done.3), channel_id=1, source_target_pairs={{0,1},{1,0},{2,3},{3,2},{4,5},{5,4},{6,7},{7,6},{8,9},{9,8},{10,11... | collective-permute-start | bytes 1179656 | tf_op jit(solution)/shard_map/ppermute | solution.py:145
  14.9 18.9 %collective-permute-start.8 = (bf16[4,64,768]{2,1,0:T(8,128)(2,1)S(1)}, bf16[4,64,768]{2,1,0:T(8,128)(2,1)}, u32[]{:S(2)}, u32[]{:S(2)}) collective-permute-start(bf16[4,64,768]{2,1,0:T(8,128)(2,1)S(1)} %copy-done.3), channel_id=1, source_target_pairs={{0,2},{1,3},{2,0},{3,1},{4,6},{5,7},{6,4},{7,5},{8,10},{9,11},{10,... | collective-permute-start | bytes 1179656 | tf_op jit(solution)/shard_map/ppermute | solution.py:145
  16.4 17.4 %collective-permute-start.9 = (bf16[4,64,768]{2,1,0:T(8,128)(2,1)S(1)}, bf16[4,64,768]{2,1,0:T(8,128)(2,1)}, u32[]{:S(2)}, u32[]{:S(2)}) collective-permute-start(bf16[4,64,768]{2,1,0:T(8,128)(2,1)S(1)} %copy-done.3), channel_id=1, source_target_pairs={{0,3},{1,2},{2,1},{3,0},{4,7},{5,6},{6,5},{7,4},{8,11},{9,10},{10,... | collective-permute-start | bytes 1179656 | tf_op jit(solution)/shard_map/ppermute | solution.py:145
  22.2 17.8 %copy-start.2 = (bf16[64,1536]{1,0:T(8,128)(2,1)}, bf16[64,1536]{1,0:T(8,128)(2,1)S(1)}, u32[]{:S(2)}) copy-start(bf16[64,1536]{1,0:T(8,128)(2,1)S(1)} %convolution_convert_fusion.2.sk_ref.sv_ref) | copy-start | bytes 589828
  23.1 1.2 %collective-permute-start.4 = (f32[32,24]{1,0:T(8,128)S(1)}, f32[32,24]{1,0:T(8,128)S(1)}, u32[]{:S(2)}, u32[]{:S(2)}) collective-permute-start(f32[32,24]{1,0:T(8,128)S(1)} %broadcast_select_fusion.9), channel_id=1, source_target_pairs={{0,4},{4,0},{8,12},{12,8},{16,20},{20,16},{24,28},{28,24},{1,5},{5... | collective-permute-start | bytes 9224 | tf_op jit(solution)/shard_map/ppermute | solution.py:60
  23.5 11.6 %copy-start.4 = (bf16[768,2304]{1,0:T(8,128)(2,1)S(1)}, bf16[768,2304]{1,0:T(8,128)(2,1)}, u32[]{:S(2)}) copy-start(bf16[768,2304]{1,0:T(8,128)(2,1)} %param.14) | copy-start | bytes 10616836
  23.5 1.5 %collective-permute-start.3 = (f32[32,768]{1,0:T(8,128)S(1)}, f32[32,768]{1,0:T(8,128)S(1)}, u32[]{:S(2)}, u32[]{:S(2)}) collective-permute-start(f32[32,768]{1,0:T(8,128)S(1)} %slice_select_fusion), channel_id=1, source_target_pairs={{0,4},{4,0},{8,12},{12,8},{16,20},{20,16},{24,28},{28,24},{1,5},{5... | collective-permute-start | bytes 294920 | tf_op jit(solution)/shard_map/ppermute | solution.py:60
  25.4 4.2 %collective-permute-start.5 = (bf16[32,840]{1,0:T(8,128)(2,1)S(1)}, bf16[32,840]{1,0:T(8,128)(2,1)S(1)}, u32[]{:S(2)}, u32[]{:S(2)}) collective-permute-start(bf16[32,840]{1,0:T(8,128)(2,1)S(1)} %pad_maximum_fusion.1), channel_id=1, source_target_pairs={{0,8},{4,12},{8,0},{12,4},{16,24},{20,28},{24,16},{28,20},{1,9},{5... | collective-permute-start | bytes 161288 | tf_op jit(solution)/shard_map/ppermute | solution.py:60
  30.6 8.5 %collective-permute-start.6 = (bf16[32,840]{1,0:T(8,128)(2,1)S(1)}, bf16[32,840]{1,0:T(8,128)(2,1)S(1)}, u32[]{:S(2)}, u32[]{:S(2)}) collective-permute-start(bf16[32,840]{1,0:T(8,128)(2,1)S(1)} %pad_maximum_fusion.2), channel_id=1, source_target_pairs={{0,16},{4,20},{8,24},{12,28},{16,0},{20,4},{24,8},{28,12},{1,17},{... | collective-permute-start | bytes 161288 | tf_op jit(solution)/shard_map/ppermute | solution.py:60
  49.3 1.9 %copy-start.6 = (f32[768]{0:T(1024)S(1)}, f32[768]{0:T(1024)}, u32[]{:S(2)}) copy-start(f32[768]{0:T(1024)} %param.16) | copy-start | bytes 9220
  51.2 7.5 %copy-start.5 = (f32[768]{0:T(1024)S(1)}, f32[768]{0:T(1024)}, u32[]{:S(2)}) copy-start(f32[768]{0:T(1024)} %param.19) | copy-start | bytes 9220
  58.9 1.3 %collective-permute-start.10 = (bf16[32,768]{1,0:T(8,128)(2,1)S(1)}, bf16[32,768]{1,0:T(8,128)(2,1)S(1)}, u32[]{:S(2)}, u32[]{:S(2)}) collective-permute-start(bf16[32,768]{1,0:T(8,128)(2,1)S(1)} %slice.231), channel_id=1, source_target_pairs={{0,4},{4,0},{8,12},{12,8},{16,20},{20,16},{24,28},{28,24},{1,5},{5... | collective-permute-start | bytes 147464 | tf_op jit(solution)/shard_map/ppermute | solution.py:60

commit v24 on v23

--- a/solution.py
+++ b/solution.py
@@ -213,7 +213,7 @@
     allowed = (jnp.right_shift(schema[:, :, None], key_groups[None, None, :]) & 1 == 1) | own_block[
         None, None, :
     ]
-    allowed = allowed.astype(jnp.float32)
+    allowed = allowed.astype(jnp.bfloat16)
     tokens = broadcast_from(summary[0], "band", n_band, owner[0], (cells, allowed))
     held_cells, allowed = tokens[1]
     row_parts = fan_out(held_cells, "col", n_col)

time: 61.2 us -> 61.1 us (level)
  no operation moved by 1% of the time
where the time goes in v24:
time: 61.1 us; the launch traced here: 60.8 us
  matrix products  23.1 us (38%)
  starting transfers between devices  12.8 us (21%)
  Pallas kernels  8.87 us (15%)
  waiting for transfers between devices  6.94 us (11%)
  other arithmetic  6.48 us (11%)
  between operations  1.69 us (3%)
  local copies, waits for them, and re-layouts  0.97 us (2%)
    dot_general x4, matrix products, project(): jnp.dot(values, weight, preferred_element_type=jnp.float32)  11.1 us
    ppermute x8, starting transfers between devices, partner(): return lax.ppermute(value, axis, [(i, i ^ step) for i in range(count)])  9.3 us
    pallas_call x1, Pallas kernels, row_attention(): pl.pallas_call(kern, grid=(rows,), in_specs=[pl.BlockSpec((1, nq, width),...  8.87 us
    dot_general x1, matrix products, finish(): outer_out = jnp.dot(inner_act, w_down, preferred_element_type=jnp.float32)  7.16 us
    ppermute x8, waiting for transfers between devices, partner(): return lax.ppermute(value, axis, [(i, i ^ step) for i in range(count)])  5.84 us
    ppermute x3, starting transfers between devices, fan_out(): got.append((source, lax.ppermute(value, axis, pairs)))  3.49 us
    dot_general x10, matrix products, head_spread(): jnp.dot(flat, head_matrix(), precision=lax.Precision.HIGHEST, preferred_e...  2.39 us
    dot_general x1, matrix products, finish(): mixed_out = jnp.dot(attended, w_out, preferred_element_type=jnp.float32)  1.63 us
  transfers between devices with their start and end apart: 11, of which 5 were waited for; matrix products, arithmetic and copies ran while one was open for 30% of the time, Pallas kernels for 0%

profile of v24, /device:TPU:0, one launch (start us, length us, event | category | flops | bytes accessed | tf_op | source)
XLA Modules:
  0.0 60.8 jit_solution(11623193772790944690)
XLA Ops:
  0.6 0.0 copy-start
  0.6 0.5 collective-permute-start
  1.2 0.1 pad_add_fusion
  1.3 1.5 %fusion.39.allow_ref = bf16[4,64,256]{2,1,0:T(8,128)(2,1)} fusion(s32[256]{0:T(256)S(1)} %pad_add_fusion, s32[4,64]{1,0:T(4,128)} %param.13, pred[256]{0:T(512)(128)(4,1)S(1)} %iota_compare_fusion.15), kind=kLoop, calls=%fused_computation.50 | loop fusion | flops 327680 | bytes 133376 | tf_op jit(solution)/shard_map/convert_element_type | solution.py:216
  3.4 0.0 copy-start.3
  3.4 1.0 %broadcast_select_fusion = bf16[64,768]{1,0:T(8,128)(2,1)S(1)} fusion(bf16[64,768]{1,0:T(8,128)(2,1)S(1)} %collective-permute-done, pred[]{:T(512)S(6)} %eq.89, bf16[1,64,768]{2,1,0:T(8,128)(2,1)} %param.11), kind=kLoop, calls=%fused_computation.57 | loop fusion | flops 49152 | bytes 294913 | tf_op jit(solution)/shard_map/jit(_where)/select_n | solution.py:70
  4.4 2.8 %collective-permute-start.1 = (bf16[64,768]{1,0:T(8,128)(2,1)S(1)}, bf16[64,768]{1,0:T(8,128)(2,1)S(1)}, u32[]{:S(2)}, u32[]{:S(2)}) collective-permute-start(bf16[64,768]{1,0:T(8,128)(2,1)S(1)} %broadcast_select_fusion), channel_id=1, source_target_pairs={{0,8},{4,12},{8,0},{12,4},{16,24},{20,28},{24,16},{28,20},{1,9},{5... | collective-permute-start | bytes 294920 | tf_op jit(solution)/shard_map/ppermute | solution.py:60
  7.2 3.2 %convolution_convert_fusion = bf16[256,2304]{1,0:T(8,128)(2,1)S(1)} fusion(bf16[256,768]{1,0:T(8,128)(2,1)} %bitcast.37, bf16[768,2304]{1,0:T(8,128)(2,1)} %param.14), kind=kOutput, calls=%fused_computation.1 | convolution fusion | flops 906559488 | bytes 5111808 | tf_op jit(solution)/shard_map/dot_general | solution.py:35
  10.5 2.8 %collective-permute-start.2 = (bf16[64,768]{1,0:T(8,128)(2,1)S(1)}, bf16[64,768]{1,0:T(8,128)(2,1)S(1)}, u32[]{:S(2)}, u32[]{:S(2)}) collective-permute-start(bf16[64,768]{1,0:T(8,128)(2,1)S(1)} %broadcast_select_fusion.1), channel_id=1, source_target_pairs={{0,16},{4,20},{8,24},{12,28},{16,0},{20,4},{24,8},{28,12},{1,17},{... | collective-permute-start | bytes 294920 | tf_op jit(solution)/shard_map/ppermute | solution.py:60
  13.3 1.5 %collective-permute-start.7 = (bf16[4,64,768]{2,1,0:T(8,128)(2,1)S(1)}, bf16[4,64,768]{2,1,0:T(8,128)(2,1)}, u32[]{:S(2)}, u32[]{:S(2)}) collective-permute-start(bf16[4,64,768]{2,1,0:T(8,128)(2,1)S(1)} %copy-done.3), channel_id=1, source_target_pairs={{0,1},{1,0},{2,3},{3,2},{4,5},{5,4},{6,7},{7,6},{8,9},{9,8},{10,11... | collective-permute-start | bytes 1179656 | tf_op jit(solution)/shard_map/ppermute | solution.py:145
  14.8 1.5 %collective-permute-start.8 = (bf16[4,64,768]{2,1,0:T(8,128)(2,1)S(1)}, bf16[4,64,768]{2,1,0:T(8,128)(2,1)}, u32[]{:S(2)}, u32[]{:S(2)}) collective-permute-start(bf16[4,64,768]{2,1,0:T(8,128)(2,1)S(1)} %copy-done.3), channel_id=1, source_target_pairs={{0,2},{1,3},{2,0},{3,1},{4,6},{5,7},{6,4},{7,5},{8,10},{9,11},{10,... | collective-permute-start | bytes 1179656 | tf_op jit(solution)/shard_map/ppermute | solution.py:145
  16.3 0.5 collective-permute-start.9
  16.8 1.5 %collective-permute-done.2 = bf16[64,768]{1,0:T(8,128)(2,1)S(1)} collective-permute-done((bf16[64,768]{1,0:T(8,128)(2,1)S(1)}, bf16[64,768]{1,0:T(8,128)(2,1)S(1)}, u32[]{:S(2)}, u32[]{:S(2)}) %collective-permute-start.2) | collective-permute-done | bytes 98336 | tf_op jit(solution)/shard_map/ppermute | solution.py:60
  18.4 1.6 %fusion.25 = f32[64,768]{1,0:T(8,128)S(1)} fusion(bf16[64,768]{1,0:T(8,128)(2,1)S(1)} %broadcast_select_fusion.2, bf16[768,2304]{1,0:T(8,128)(2,1)} %param.14), kind=kOutput, calls=%fused_computation.27 | convolution fusion | flops 75595776 | bytes 1474560 | tf_op jit(solution)/shard_map/dot_general | solution.py:35
  20.0 2.2 %convolution_convert_fusion.2.sk_ref.sv_ref = bf16[64,1536]{1,0:T(8,128)(2,1)S(1)} fusion(bf16[64,768]{1,0:T(8,128)(2,1)S(1)} %broadcast_select_fusion.2, bf16[768,2304]{1,0:T(8,128)(2,1)} %param.14), kind=kOutput, calls=%fused_computation.11 | convolution fusion | flops 151093248 | bytes 2654208 | tf_op jit(solution)/shard_map/dot_general | solution.py:35
  22.2 0.6 %fusion.90 = (f32[64,12]{0,1:T(8,128)S(1)}, f32[4,64,12]{1,2,0:T(8,128)S(1)}) fusion(s32[768]{0:T(1024)S(1)} %add_select_fusion, bf16[4,64,2304]{2,1,0:T(8,128)(2,1)S(1)} %bitcast.32, f32[64,768]{1,0:T(8,128)S(1)} %fusion.25), kind=kOutput, calls=%fused_computation.160 | convolution fusion | flops 28719360 | bytes 609280 | tf_op jit(solution)/shard_map/dot_general | solution.py:46
  22.8 0.1 slice_maximum_fusion.3
  22.9 0.1 copy.18
  23.0 0.1 copy.19
  23.1 0.1 collective-permute-start.4
  23.1 0.3 fusion.19
  23.5 0.0 copy-start.4
  23.5 0.6 collective-permute-start.3
  24.0 0.2 convolution_multiply_fusion.4
  24.3 0.0 collective-permute-done.4
  24.3 0.1 fusion.72
  24.4 0.2 fusion.47
  24.7 0.1 fusion.88
  24.7 0.1 fusion.73
  24.8 0.1 subtract_convert_fusion.1
  24.9 0.1 collective-permute-done.3
  25.0 0.2 add_convert_fusion.1
  25.2 0.1 pad_maximum_fusion.1
  25.3 0.4 collective-permute-start.5
  25.8 3.7 %collective-permute-done.5 = bf16[32,840]{1,0:T(8,128)(2,1)S(1)} collective-permute-done((bf16[32,840]{1,0:T(8,128)(2,1)S(1)}, bf16[32,840]{1,0:T(8,128)(2,1)S(1)}, u32[]{:S(2)}, u32[]{:S(2)}) %collective-permute-start.5) | collective-permute-done | bytes 53792 | tf_op jit(solution)/shard_map/ppermute | solution.py:60
  29.5 0.1 broadcast_select_fusion.6
  29.6 0.1 fusion.71
  29.7 0.2 fusion.44
  30.0 0.1 fusion.87
  30.1 0.1 fusion.74
  30.1 0.1 subtract_convert_fusion
  30.2 0.3 add_convert_fusion
  30.5 0.1 pad_maximum_fusion.2
  30.6 2.0 %collective-permute-start.6 = (bf16[32,840]{1,0:T(8,128)(2,1)S(1)}, bf16[32,840]{1,0:T(8,128)(2,1)S(1)}, u32[]{:S(2)}, u32[]{:S(2)}) collective-permute-start(bf16[32,840]{1,0:T(8,128)(2,1)S(1)} %pad_maximum_fusion.2), channel_id=1, source_target_pairs={{0,16},{4,20},{8,24},{12,28},{16,0},{20,4},{24,8},{28,12},{1,17},{... | collective-permute-start | bytes 161288 | tf_op jit(solution)/shard_map/ppermute | solution.py:60
  32.6 1.1 %collective-permute-done.8 = bf16[4,64,768]{2,1,0:T(8,128)(2,1)} collective-permute-done((bf16[4,64,768]{2,1,0:T(8,128)(2,1)S(1)}, bf16[4,64,768]{2,1,0:T(8,128)(2,1)}, u32[]{:S(2)}, u32[]{:S(2)}) %collective-permute-start.8) | collective-permute-done | bytes 393248 | tf_op jit(solution)/shard_map/ppermute | solution.py:145
  33.7 1.3 %pad_maximum_fusion = bf16[4,256,768]{2,1,0:T(8,128)(2,1)S(1)} fusion(bf16[4,64,768]{2,1,0:T(8,128)(2,1)} %collective-permute-done.9, bf16[4,64,768]{2,1,0:T(8,128)(2,1)} %collective-permute-done.8, bf16[4,64,768]{2,1,0:T(8,128)(2,1)} %collective-permute-done.7, bf16[4,64,768]{2,1,0:T(8,128)(2,1)S(1)} %copy-done.3), kind=kLoop, calls=%fused_computation.19 | loop fusion | flops 6291456 | bytes 3145728 | tf_op jit(solution)/shard_map/concatenate | solution.py:240
  35.1 4.0 %convolution_convert_fusion.1 = bf16[1024,1536]{1,0:T(8,128)(2,1)} fusion(bf16[1024,768]{1,0:T(8,128)(2,1)S(1)} %bitcast.35, bf16[768,2304]{1,0:T(8,128)(2,1)S(1)} %copy-done.4), kind=kOutput, calls=%fused_computation.2 | convolution fusion | flops 2417491968 | bytes 7077888 | tf_op jit(solution)/shard_map/dot_general | solution.py:35
  39.1 0.1 broadcast_select_fusion.4
  39.2 0.1 fusion.76
  39.3 0.2 convolution_multiply_fusion.3
  39.5 0.3 fusion.29
  39.8 0.1 fusion.43
  39.9 0.2 fusion.28
  40.1 0.3 fusion.30
  40.4 8.9 %shard_map.113 = bf16[4,64,768]{2,1,0:T(8,128)(2,1)} custom-call(bf16[4,64,2304]{2,1,0:T(8,128)(2,1)} %bitcast.34, bf16[4,256,1536]{2,1,0:T(8,128)(2,1)} %bitcast.30, bf16[4,256,1536]{2,1,0:T(8,128)(2,1)} %bitcast.31, bf16[64,1536]{1,0:T(8,128)(2,1)} %copy-done.2, bf16[64,1536]{1,0:T(8,128)(2,1)} %copy-done.2, bf16[4,64,256]{2,1,0:T(8,128)(2,1)} %fusion.39.allow_ref), custom_call_target="tpu_custom_call" | custom-call | tf_op jit(solution)/shard_map/pallas_call | solution.py:184
  49.3 1.6 %fusion.91 = (f32[288]{0:T(512)S(1)}, f32[288,768]{1,0:T(8,128)S(1)}) fusion(bf16[768,768]{1,0:T(8,128)(2,1)S(1)} %copy-done, bf16[32,768]{1,0:T(8,128)(2,1)S(1)} %fusion.30, bf16[256,768]{1,0:T(8,128)(2,1)} %bitcast.36, bf16[32,768]{1,0:T(8,128)(2,1)S(1)} %slice_select_fusion.2, bf16[256,768]{1,0:T(8,128)(2,1)S(1)} %bitcast.38), kind=kOutput, calls=%fused_computation.161 | convolution fusion | flops 341950176 | bytes 2950272 | tf_op jit(solution)/shard_map/dot_general | solution.py:25
  50.9 0.3 multiply_reduce_fusion.1
  51.2 7.2 %fusion.92 = (f32[288]{0:T(512)S(1)}, f32[288,768]{1,0:T(8,128)S(1)}) fusion(bf16[3072,768]{1,0:T(8,128)(2,1)} %param.18, bf16[768,3072]{1,0:T(8,128)(2,1)} %param.17, f32[288,768]{1,0:T(8,128)S(1)} %get-tuple-element.32, f32[768]{0:T(1024)S(1)} %copy-done.6, f32[288]{0:T(512)S(1)} %add_rsqrt_fusion.1, f32[288]{0:T(512)S(1)} %broadcast_multiply_fusion.1), kind=kOutput, calls=%fused_computation.162 | convolution fusion | flops 2728304384 | bytes 11213184 | tf_op jit(solution)/shard_map/dot_general | solution.py:30
  58.4 0.3 multiply_reduce_fusion
  58.7 0.2 multiply_convert_fusion
  58.9 0.1 collective-permute-start.10
  58.9 0.8 %slice.230 = bf16[256,768]{1,0:T(8,128)(2,1)} slice(bf16[288,768]{1,0:T(8,128)(2,1)S(1)} %multiply_convert_fusion), slice={[0:256], [0:768]} | slice | bytes 786432 | tf_op jit(solution)/shard_map/slice | solution.py:268
  59.7 0.4 collective-permute-done.10
  60.2 0.7 %maximum_select_fusion = bf16[64,768]{1,0:T(8,128)(2,1)} fusion(bf16[32,768]{1,0:T(8,128)(2,1)S(1)} %collective-permute-done.10, bf16[32,768]{1,0:T(8,128)(2,1)S(1)} %slice.231, pred[]{:T(512)S(6)} %eq.86), kind=kLoop, calls=%fused_computation.54 | loop fusion | flops 442368 | bytes 196609 | tf_op jit(solution)/shard_map/jit(_where)/select_n | solution.py:132
  (38 shorter events, 0.2 us)
Async XLA Ops:
  0.6 48.7 %copy-start = (bf16[768,768]{1,0:T(8,128)(2,1)S(1)}, bf16[768,768]{1,0:T(8,128)(2,1)}, u32[]{:S(2)}) copy-start(bf16[768,768]{1,0:T(8,128)(2,1)} %param.15) | copy-start | bytes 3538948
  0.6 2.8 %collective-permute-start = (bf16[64,768]{1,0:T(8,128)(2,1)}, bf16[64,768]{1,0:T(8,128)(2,1)S(1)}, u32[]{:S(2)}, u32[]{:S(2)}) collective-permute-start(bf16[64,768]{1,0:T(8,128)(2,1)} %bitcast.40), channel_id=1, source_target_pairs={{0,4},{4,0},{8,12},{12,8},{16,20},{20,16},{24,28},{28,24},{1,5},{5... | collective-permute-start | bytes 294920 | tf_op jit(solution)/shard_map/ppermute | solution.py:60
  3.4 9.9 %copy-start.3 = (bf16[4,64,768]{2,1,0:T(8,128)(2,1)S(1)}, bf16[4,64,768]{2,1,0:T(8,128)(2,1)}, u32[]{:S(2)}) copy-start(bf16[4,64,768]{2,1,0:T(8,128)(2,1)} %param.10) | copy-start | bytes 1179652
  4.4 6.1 %collective-permute-start.1 = (bf16[64,768]{1,0:T(8,128)(2,1)S(1)}, bf16[64,768]{1,0:T(8,128)(2,1)S(1)}, u32[]{:S(2)}, u32[]{:S(2)}) collective-permute-start(bf16[64,768]{1,0:T(8,128)(2,1)S(1)} %broadcast_select_fusion), channel_id=1, source_target_pairs={{0,8},{4,12},{8,0},{12,4},{16,24},{20,28},{24,16},{28,20},{1,9},{5... | collective-permute-start | bytes 294920 | tf_op jit(solution)/shard_map/ppermute | solution.py:60
  10.4 13.0 %copy-start.1 = (bf16[256,2304]{1,0:T(8,128)(2,1)}, bf16[256,2304]{1,0:T(8,128)(2,1)S(1)}, u32[]{:S(2)}) copy-start(bf16[256,2304]{1,0:T(8,128)(2,1)S(1)} %convolution_convert_fusion) | copy-start | bytes 3538948
  10.5 7.8 %collective-permute-start.2 = (bf16[64,768]{1,0:T(8,128)(2,1)S(1)}, bf16[64,768]{1,0:T(8,128)(2,1)S(1)}, u32[]{:S(2)}, u32[]{:S(2)}) collective-permute-start(bf16[64,768]{1,0:T(8,128)(2,1)S(1)} %broadcast_select_fusion.1), channel_id=1, source_target_pairs={{0,16},{4,20},{8,24},{12,28},{16,0},{20,4},{24,8},{28,12},{1,17},{... | collective-permute-start | bytes 294920 | tf_op jit(solution)/shard_map/ppermute | solution.py:60
  13.3 19.3 %collective-permute-start.7 = (bf16[4,64,768]{2,1,0:T(8,128)(2,1)S(1)}, bf16[4,64,768]{2,1,0:T(8,128)(2,1)}, u32[]{:S(2)}, u32[]{:S(2)}) collective-permute-start(bf16[4,64,768]{2,1,0:T(8,128)(2,1)S(1)} %copy-done.3), channel_id=1, source_target_pairs={{0,1},{1,0},{2,3},{3,2},{4,5},{5,4},{6,7},{7,6},{8,9},{9,8},{10,11... | collective-permute-start | bytes 1179656 | tf_op jit(solution)/shard_map/ppermute | solution.py:145
  14.8 18.9 %collective-permute-start.8 = (bf16[4,64,768]{2,1,0:T(8,128)(2,1)S(1)}, bf16[4,64,768]{2,1,0:T(8,128)(2,1)}, u32[]{:S(2)}, u32[]{:S(2)}) collective-permute-start(bf16[4,64,768]{2,1,0:T(8,128)(2,1)S(1)} %copy-done.3), channel_id=1, source_target_pairs={{0,2},{1,3},{2,0},{3,1},{4,6},{5,7},{6,4},{7,5},{8,10},{9,11},{10,... | collective-permute-start | bytes 1179656 | tf_op jit(solution)/shard_map/ppermute | solution.py:145
  16.3 17.4 %collective-permute-start.9 = (bf16[4,64,768]{2,1,0:T(8,128)(2,1)S(1)}, bf16[4,64,768]{2,1,0:T(8,128)(2,1)}, u32[]{:S(2)}, u32[]{:S(2)}) collective-permute-start(bf16[4,64,768]{2,1,0:T(8,128)(2,1)S(1)} %copy-done.3), channel_id=1, source_target_pairs={{0,3},{1,2},{2,1},{3,0},{4,7},{5,6},{6,5},{7,4},{8,11},{9,10},{10,... | collective-permute-start | bytes 1179656 | tf_op jit(solution)/shard_map/ppermute | solution.py:145
  22.2 17.8 %copy-start.2 = (bf16[64,1536]{1,0:T(8,128)(2,1)}, bf16[64,1536]{1,0:T(8,128)(2,1)S(1)}, u32[]{:S(2)}) copy-start(bf16[64,1536]{1,0:T(8,128)(2,1)S(1)} %convolution_convert_fusion.2.sk_ref.sv_ref) | copy-start | bytes 589828
  23.1 1.2 %collective-permute-start.4 = (f32[32,24]{1,0:T(8,128)S(1)}, f32[32,24]{1,0:T(8,128)S(1)}, u32[]{:S(2)}, u32[]{:S(2)}) collective-permute-start(f32[32,24]{1,0:T(8,128)S(1)} %broadcast_select_fusion.9), channel_id=1, source_target_pairs={{0,4},{4,0},{8,12},{12,8},{16,20},{20,16},{24,28},{28,24},{1,5},{5... | collective-permute-start | bytes 9224 | tf_op jit(solution)/shard_map/ppermute | solution.py:60
  23.5 11.6 %copy-start.4 = (bf16[768,2304]{1,0:T(8,128)(2,1)S(1)}, bf16[768,2304]{1,0:T(8,128)(2,1)}, u32[]{:S(2)}) copy-start(bf16[768,2304]{1,0:T(8,128)(2,1)} %param.14) | copy-start | bytes 10616836
  23.5 1.5 %collective-permute-start.3 = (f32[32,768]{1,0:T(8,128)S(1)}, f32[32,768]{1,0:T(8,128)S(1)}, u32[]{:S(2)}, u32[]{:S(2)}) collective-permute-start(f32[32,768]{1,0:T(8,128)S(1)} %slice_select_fusion), channel_id=1, source_target_pairs={{0,4},{4,0},{8,12},{12,8},{16,20},{20,16},{24,28},{28,24},{1,5},{5... | collective-permute-start | bytes 294920 | tf_op jit(solution)/shard_map/ppermute | solution.py:60
  25.3 4.2 %collective-permute-start.5 = (bf16[32,840]{1,0:T(8,128)(2,1)S(1)}, bf16[32,840]{1,0:T(8,128)(2,1)S(1)}, u32[]{:S(2)}, u32[]{:S(2)}) collective-permute-start(bf16[32,840]{1,0:T(8,128)(2,1)S(1)} %pad_maximum_fusion.1), channel_id=1, source_target_pairs={{0,8},{4,12},{8,0},{12,4},{16,24},{20,28},{24,16},{28,20},{1,9},{5... | collective-permute-start | bytes 161288 | tf_op jit(solution)/shard_map/ppermute | solution.py:60
  30.6 8.5 %collective-permute-start.6 = (bf16[32,840]{1,0:T(8,128)(2,1)S(1)}, bf16[32,840]{1,0:T(8,128)(2,1)S(1)}, u32[]{:S(2)}, u32[]{:S(2)}) collective-permute-start(bf16[32,840]{1,0:T(8,128)(2,1)S(1)} %pad_maximum_fusion.2), channel_id=1, source_target_pairs={{0,16},{4,20},{8,24},{12,28},{16,0},{20,4},{24,8},{28,12},{1,17},{... | collective-permute-start | bytes 161288 | tf_op jit(solution)/shard_map/ppermute | solution.py:60
  49.3 1.9 %copy-start.6 = (f32[768]{0:T(1024)S(1)}, f32[768]{0:T(1024)}, u32[]{:S(2)}) copy-start(f32[768]{0:T(1024)} %param.16) | copy-start | bytes 9220
  51.2 7.5 %copy-start.5 = (f32[768]{0:T(1024)S(1)}, f32[768]{0:T(1024)}, u32[]{:S(2)}) copy-start(f32[768]{0:T(1024)} %param.19) | copy-start | bytes 9220
  58.9 1.3 %collective-permute-start.10 = (bf16[32,768]{1,0:T(8,128)(2,1)S(1)}, bf16[32,768]{1,0:T(8,128)(2,1)S(1)}, u32[]{:S(2)}, u32[]{:S(2)}) collective-permute-start(bf16[32,768]{1,0:T(8,128)(2,1)S(1)} %slice.231), channel_id=1, source_target_pairs={{0,4},{4,0},{8,12},{12,8},{16,20},{20,16},{24,28},{28,24},{1,5},{5... | collective-permute-start | bytes 147464 | tf_op jit(solution)/shard_map/ppermute | solution.py:60
